TPU v7x, 32 devices: a whole 2x2x4 slice. The times are simulated.
32 devices in a mesh: dp: 8 (over z, x), tensor: 4 (over y, core).
Axes of the slice: x: 2, y: 2, z: 4, core: 2. Of those that a mesh axis runs over, the one named last changes fastest.
Arguments:
- tokens: bfloat16 [2048, 4096], P('dp', 'tensor'), may hold values from -6 to 6
- norm_gain: float32 [4096], replicated, may hold values from 0.15 to 5.4, as said below
- w_query: bfloat16 [4096, 4096], P(None, 'tensor'), may hold values from -0.09375 to 0.09375
- key_weight: bfloat16 [4096, 1024], P(None, 'tensor'), may hold values from -0.09375 to 0.09375
- value_weight: bfloat16 [4096, 1024], P(None, 'tensor'), may hold values from -0.09375 to 0.09375
- w_out: bfloat16 [4096, 4096], P('tensor'), may hold values from -0.25 to 0.25
- grad_output: bfloat16 [2048, 4096], P('dp', 'tensor'), may hold values from -6 to 6
- doc_lengths: int32 [8, 2], P('dp'), may hold values from 0 to 256, as said below
- block_owner: int32 [8, 8], replicated, may hold values from 0 to 7, as said below
Outputs:
- relaid_output: bfloat16 [2048, 4096], P('dp', 'tensor')
- input_grad: bfloat16 [2048, 4096], P('dp', 'tensor')
Inputs may be any that keep to these rules, and one draw needn't show every extreme that they name: `doc_lengths`: each row lists the lengths of the documents packed on that dp index in order: multiples of 128, the nonzero ones first, summing to 256. In every draw some dp index holds a single document of 256 tokens. `block_owner`: every dp index owns exactly one block of each position j < 8 and exactly one block from each dp index. `norm_gain`: positive gains.
All inputs are finite; a program needn't handle non-finite values.
Results may differ from a plain program's by a relative error of at most 0.015.
Values may be sent and summed in bfloat16 or wider, within the bound.
No kernel may reach another device: no remote copies, remote signals or barrier semaphores. Data moves between devices by JAX's collectives and lax.ppermute only.
A program may use at most 128 MiB of HBM per device.

v0:
```python
import math

import jax
import jax.numpy as jnp
from jax import lax
from jax.sharding import PartitionSpec as P

HEAD_SIZE = 128


ROPE_BASE = 500000.0
NORM_EPSILON = 1e-05


def doc_tables(lengths_row, token_row_count):
    ends = jnp.cumsum(lengths_row)
    token_index = jnp.arange(token_row_count, dtype=jnp.int32)
    passed = (token_index[:, None] >= ends[None, :]).astype(jnp.int32)
    doc_ids = jnp.sum(passed, axis=1)
    starts = jnp.max(jnp.where(passed > 0, ends[None, :], 0), axis=1)
    return (doc_ids, token_index - starts)


def rope_tables(positions, head_size):
    half_dim = head_size // 2
    steps = jnp.arange(half_dim, dtype=jnp.float32)
    inverse_freq = jnp.power(ROPE_BASE, -2.0 * steps / head_size)
    angles = positions.astype(jnp.float32)[:, None] * inverse_freq[None, :]
    return (jnp.cos(angles), jnp.sin(angles))


def rotate(vectors, cosine, sine_table):
    half_dim = vectors.shape[-1] // 2
    former = vectors[..., :half_dim]
    latter = vectors[..., half_dim:]
    cos_part = cosine[:, None, :]
    sin_part = sine_table[:, None, :]
    return jnp.concatenate(
        [former * cos_part - latter * sin_part, latter * cos_part + former * sin_part], axis=-1
    )


def unrotate(vectors, cosine, sine_table):
    half_dim = vectors.shape[-1] // 2
    former = vectors[..., :half_dim]
    latter = vectors[..., half_dim:]
    cos_part = cosine[:, None, :]
    sin_part = sine_table[:, None, :]
    return jnp.concatenate(
        [former * cos_part + latter * sin_part, latter * cos_part - former * sin_part], axis=-1
    )


def per_device(
    tokens,
    norm_gain,
    w_query,
    key_weight,
    value_weight,
    w_out,
    grad_output,
    doc_lengths,
    block_owner,
):
    token_row_count, width_part = tokens.shape
    full_width = norm_gain.shape[0]
    sources = lax.axis_size("dp")
    data_index = lax.axis_index("dp")
    tensor_index = lax.axis_index("tensor")
    query_width = w_query.shape[1]
    key_width = key_weight.shape[1]
    heads_local = query_width // HEAD_SIZE
    kv_local = key_width // HEAD_SIZE
    query_group_width = heads_local // kv_local
    scale_factor = 1.0 / math.sqrt(HEAD_SIZE)
    gain_part = lax.dynamic_slice_in_dim(norm_gain, tensor_index * width_part, width_part)
    w_joined = jnp.concatenate([w_query, key_weight, value_weight], axis=1)
    x_float = tokens.astype(jnp.float32)
    gathered = lax.all_gather(tokens, "tensor", axis=1, tiled=True)
    gathered_float = gathered.astype(jnp.float32)
    inverse = lax.rsqrt(jnp.mean(gathered_float * gathered_float, axis=1) + NORM_EPSILON)
    normed_input = (gathered_float * inverse[:, None] * norm_gain[None, :]).astype(jnp.bfloat16)
    projected = jnp.dot(normed_input, w_joined, preferred_element_type=jnp.float32)
    doc_ids, positions = doc_tables(doc_lengths[0], token_row_count)
    token_index = jnp.arange(token_row_count, dtype=jnp.int32)
    allowed = (doc_ids[:, None] == doc_ids[None, :]) & (
        token_index[None, :] <= token_index[:, None]
    )
    cosine, sine_table = rope_tables(positions, HEAD_SIZE)
    query_rows = rotate(
        projected[:, :query_width].reshape(token_row_count, heads_local, HEAD_SIZE),
        cosine,
        sine_table,
    ).astype(jnp.bfloat16)
    keys = rotate(
        projected[:, query_width : query_width + key_width].reshape(
            token_row_count, kv_local, HEAD_SIZE
        ),
        cosine,
        sine_table,
    ).astype(jnp.bfloat16)
    value_rows = (
        projected[:, query_width + key_width :]
        .astype(jnp.bfloat16)
        .reshape(token_row_count, kv_local, HEAD_SIZE)
    )
    grouped_query = query_rows.reshape(token_row_count, kv_local, query_group_width, HEAD_SIZE)
    scores = (
        jnp.einsum("qkgd,skd->kgqs", grouped_query, keys, preferred_element_type=jnp.float32)
        * scale_factor
    )
    weights = jnp.where(allowed[None, None], jnp.exp(scores), 0.0)
    probs = weights / jnp.sum(weights, axis=-1, keepdims=True)
    probs_low = probs.astype(jnp.bfloat16)
    attended = jnp.einsum(
        "kgqs,skd->qkgd", probs_low, value_rows, preferred_element_type=jnp.float32
    ).astype(jnp.bfloat16)
    attended_flat = attended.reshape(token_row_count, query_width)
    mixed_turned = lax.psum_scatter(
        lax.dot_general(
            w_out, attended_flat, (((0,), (1,)), ((), ())), preferred_element_type=jnp.float32
        ).astype(jnp.bfloat16),
        "tensor",
        scatter_dimension=0,
        tiled=True,
    ).astype(jnp.float32)
    output_home = (x_float + mixed_turned.T).astype(jnp.bfloat16)
    block_count = block_owner.shape[1]
    owner_row = lax.dynamic_slice_in_dim(block_owner, data_index, 1, 0)[0]
    slot_index = jnp.arange(sources, dtype=jnp.int32)
    send_table = (owner_row[None, :] == slot_index[:, None]).astype(jnp.bfloat16)
    owned_flags = jnp.sum((block_owner == data_index).astype(jnp.int32), axis=1)
    owned_rank = jnp.cumsum(owned_flags) - owned_flags
    block_index = jnp.arange(block_count, dtype=jnp.int32)
    keep_table = (
        (owned_rank[None, :] == block_index[:, None]) & (owned_flags[None, :] > 0)
    ).astype(jnp.bfloat16)
    home_blocks = output_home.reshape(block_count, -1)
    outgoing = jnp.dot(send_table, home_blocks, preferred_element_type=jnp.float32).astype(
        jnp.bfloat16
    )
    incoming = lax.all_to_all(outgoing, "dp", split_axis=0, concat_axis=0, tiled=True)
    relaid = (
        jnp.dot(keep_table, incoming, preferred_element_type=jnp.float32)
        .astype(jnp.bfloat16)
        .reshape(token_row_count, width_part)
    )
    owned_blocks = grad_output.reshape(block_count, -1)
    returning = lax.dot_general(
        keep_table, owned_blocks, (((0,), (0,)), ((), ())), preferred_element_type=jnp.float32
    ).astype(jnp.bfloat16)
    arrived = lax.all_to_all(returning, "dp", split_axis=0, concat_axis=0, tiled=True)
    grad_home = (
        lax.dot_general(
            send_table, arrived, (((0,), (0,)), ((), ())), preferred_element_type=jnp.float32
        )
        .astype(jnp.bfloat16)
        .reshape(token_row_count, width_part)
    )
    attended_gradient = lax.dot_general(
        lax.all_gather(grad_home, "tensor", axis=1, tiled=True),
        w_out,
        (((1,), (1,)), ((), ())),
        preferred_element_type=jnp.float32,
    ).astype(jnp.bfloat16)
    grouped_gradient = attended_gradient.reshape(
        token_row_count, kv_local, query_group_width, HEAD_SIZE
    )
    delta = jnp.sum(grouped_gradient.astype(jnp.float32) * attended.astype(jnp.float32), axis=-1)
    grad_probs = jnp.einsum(
        "qkgd,skd->kgqs", grouped_gradient, value_rows, preferred_element_type=jnp.float32
    )
    grad_scores = (probs * (grad_probs - jnp.transpose(delta, (1, 2, 0))[..., None])).astype(
        jnp.bfloat16
    )
    grad_query_rot = (
        jnp.einsum("kgqs,skd->qkgd", grad_scores, keys, preferred_element_type=jnp.float32)
        * scale_factor
    )
    grad_keys_rot = (
        jnp.einsum("kgqs,qkgd->skd", grad_scores, grouped_query, preferred_element_type=jnp.float32)
        * scale_factor
    )
    value_gradient = jnp.einsum(
        "kgqs,qkgd->skd", probs_low, grouped_gradient, preferred_element_type=jnp.float32
    )
    grad_query = unrotate(
        grad_query_rot.reshape(token_row_count, heads_local, HEAD_SIZE), cosine, sine_table
    ).astype(jnp.bfloat16)
    key_gradient = unrotate(grad_keys_rot, cosine, sine_table).astype(jnp.bfloat16)
    joined_grad = jnp.concatenate(
        [
            grad_query.reshape(token_row_count, query_width),
            key_gradient.reshape(token_row_count, key_width),
            value_gradient.astype(jnp.bfloat16).reshape(token_row_count, key_width),
        ],
        axis=1,
    )
    normed_gradient = (
        lax.psum_scatter(
            lax.dot_general(
                w_joined, joined_grad, (((1,), (1,)), ((), ())), preferred_element_type=jnp.float32
            ).astype(jnp.bfloat16),
            "tensor",
            scatter_dimension=0,
            tiled=True,
        )
        .astype(jnp.float32)
        .T
    )
    stat = (
        lax.psum(jnp.sum(normed_gradient * gain_part[None, :] * x_float, axis=1), "tensor")
        / full_width
    )
    cubed = inverse * inverse * inverse
    grad_x = (
        grad_home.astype(jnp.float32)
        + inverse[:, None] * gain_part[None, :] * normed_gradient
        - x_float * cubed[:, None] * stat[:, None]
    )
    return (relaid, grad_x.astype(jnp.bfloat16))


def solution(mesh):
    placed = (
        P("dp", "tensor"),
        P(),
        P(None, "tensor"),
        P(None, "tensor"),
        P(None, "tensor"),
        P("tensor", None),
        P("dp", "tensor"),
        P("dp", None),
        P(),
    )
    return jax.shard_map(
        per_device,
        mesh=mesh,
        in_specs=placed,
        out_specs=(P("dp", "tensor"), P("dp", "tensor")),
        check_vma=False,
    )
```

profile of v0, /device:TPU:0, one launch (start us, length us, event | category | flops | bytes accessed | tf_op | source)
XLA Modules:
  0.0 188.4 jit_solution(454758210394766941)
XLA Ops:
  7.2 0.7 all-gather.3.cloned.1.call-update
  7.9 1.3 reshape.232
  9.2 0.8 convert_reduce_fusion
  10.0 0.2 reduce-window.16
  10.2 0.4 fusion.1
  10.6 0.6 broadcast.110
  11.1 1.1 reduce
  12.2 1.2 reshape.245
  13.4 7.3 %all-to-all-start.1 = ((bf16[8,2,16384]{2,1,0:T(2,128)(2,1)}), bf16[8,2,16384]{2,1,0:T(2,128)(2,1)S(1)}, u32[]{:S(2)}, u32[]{:S(2)}) async-start(bf16[8,2,16384]{2,1,0:T(2,128)(2,1)} %reshape.245), calls=%async_computation.2 | async-start | bytes 1048576 | tf_op jit(solution)/shard_map/all_to_all | solution.py:152
  20.7 0.2 reduce-window.17
  20.9 0.7 dynamic-slice_bitcast_fusion
  21.7 0.1 fusion.34
  21.8 7.9 %constant_dynamic-update-slice_fusion.2 = bf16[4096,1536]{1,0:T(8,128)(2,1)} fusion(bf16[4096,1024]{1,0:T(8,128)(2,1)} %param.11), kind=kLoop, calls=%fused_computation.78 | loop fusion | bytes 16777216
  29.7 1.6 constant_dynamic-update-slice_fusion.1
  31.3 0.8 copy-done.3
  32.1 1.7 constant_dynamic-update-slice_fusion
  33.8 1.4 all-to-all-done.1
  35.1 0.5 reshape.246
  35.7 0.7 convolution_convert_fusion
  36.4 1.0 reshape.233
  37.4 0.2 reduce-scatter.5.cloned.1.call-start
  37.7 0.5 multiply_cosine_fusion
  38.2 2.2 %fusion.3 = f32[256]{0:T(256)S(1)} fusion(bf16[256,4096]{1,0:T(8,128)(2,1)} %all-gather.3.cloned.1.call-done), kind=kLoop, calls=%fused_computation.11 | loop fusion | flops 3145472 | bytes 2098176 | tf_op jit(solution)/shard_map/reduce_sum | solution.py:81
  40.5 6.8 %fusion.6 = f32[256,1536]{1,0:T(8,128)S(1)} fusion(bf16[4096,1536]{1,0:T(8,128)(2,1)} %constant_dynamic-update-slice_fusion, bf16[256,4096]{1,0:T(8,128)(2,1)S(1)} %copy-done.4, f32[4096]{0:T(1024)S(1)} %copy-done.11, f32[256]{0:T(256)S(1)} %get-tuple-element.21), kind=kOutput, calls=%fused_computation.14 | convolution fusion | flops 3225419776 | bytes 16270336 | tf_op jit(solution)/shard_map/dot_general | solution.py:83
  47.5 0.2 copy.146
  47.7 0.9 copy-done.5
  48.6 0.5 subtract_convert_fusion.1
  49.2 0.3 slice-done
  49.5 0.1 reshape.227
  49.7 0.3 fusion.56
  50.1 2.1 %fusion.13 = (f32[2,4,256]{2,1,0:T(4,128)S(1)}, f32[2,256,256,4]{2,1,3,0:T(8,128)}) fusion(pred[256,256]{0,1:T(8,128)(4,1)S(1)} %fusion.34, bf16[256,2,4,64]{3,0,2,1:T(8,128)(2,1)S(1)} %bitcast.116, bf16[256,2,4,64]{3,0,2,1:T(8,128)(2,1)S(1)} %bitcast.118, bf16[256,2,64]{2,0,1:T(8,128)(2,1)S(1)} %get-tuple-element.11, ...), kind=kOutput, calls=%fused_computation.22 | convolution fusion | flops 137099264 | bytes 2826240 | tf_op jit(solution)/shard_map/qkgd,skd->kgqs/dot_general | solution.py:109
  52.2 8.0 %all-gather.5.cloned.1.call-done = bf16[256,4096]{1,0:T(8,128)(2,1)} async-done(((bf16[256,1024]{1,0:T(8,128)(2,1)}), bf16[256,4096]{1,0:T(8,128)(2,1)}) %all-gather.5.cloned.1.call-update) | async-done | bytes 2097168 | tf_op jit(solution)/shard_map/all_gather | solution.py:161
  60.2 6.4 %convolution_convert_fusion.6 = bf16[256,1024]{1,0:T(8,128)(2,1)S(1)} fusion(bf16[256,4096]{1,0:T(8,128)(2,1)} %all-gather.5.cloned.1.call-done, bf16[1024,4096]{1,0:T(8,128)(2,1)} %param.14), kind=kOutput, calls=%fused_computation.27 | convolution fusion | flops 2147745792 | bytes 11010048 | tf_op jit(solution)/shard_map/dot_general | solution.py:160
  66.6 0.2 copy.105
  66.8 2.4 %fusion.16 = bf16[2,128,256]{2,1,0:T(8,128)(2,1)S(1)} fusion(bf16[256,2,4,128]{0,3,2,1:T(8,128)(2,1)S(1)} %bitcast.121, f32[2,256,256,4]{2,1,3,0:T(8,128)} %get-tuple-element.23, f32[2,4,256]{2,1,0:T(4,128)S(1)} %get-tuple-element.22, pred[256,256]{0,1:T(8,128)(4,1)S(1)} %fusion.34), kind=kOutput, calls=%fused_computation.33 | convolution fusion | flops 136380416 | bytes 2826240 | tf_op jit(solution)/shard_map/kgqs,qkgd->skd/dot_general | solution.py:184
  69.3 1.6 multiply_reduce_fusion
  70.8 0.7 fusion.9
  71.6 0.5 fusion.15
  72.1 0.4 convolution_multiply_fusion
  72.6 0.2 add_convert_fusion.2
  72.8 0.1 pad_maximum_fusion.2
  72.9 0.1 copy.115
  73.0 0.8 copy.117
  73.9 0.4 copy.145
  74.3 0.4 copy.144
  74.7 0.3 add_convert_fusion
  75.0 0.3 pad_maximum_fusion.1
  75.4 0.5 copy-done.6
  75.9 13.8 %convolution_convert_fusion.4 = bf16[4096,256]{0,1:T(8,128)(2,1)} fusion(bf16[4096,1536]{1,0:T(8,128)(2,1)} %constant_dynamic-update-slice_fusion, bf16[256,256]{1,0:T(8,128)(2,1)S(1)} %copy.118, bf16[256,256]{1,0:T(8,128)(2,1)S(1)} %copy-done.6, bf16[256,1024]{1,0:T(8,128)(2,1)S(1)} %bitcast.123), kind=kOutput, calls=%fused_computation.8 | convolution fusion | flops 3224633344 | bytes 15466496 | tf_op jit(solution)/shard_map/dot_general | solution.py:201
  89.8 7.1 %fusion.2 = bf16[4096,256]{0,1:T(8,128)(2,1)} fusion(bf16[256,1024]{0,1:T(8,128)(2,1)S(1)} %bitcast.120, bf16[1024,4096]{1,0:T(8,128)(2,1)} %param.14), kind=kOutput, calls=%fused_computation.10 | convolution fusion | flops 2148532224 | bytes 11010048 | tf_op jit(solution)/shard_map/dot_general | solution.py:120
  96.9 0.8 dynamic_slice.7
  97.7 23.6 %reduce-scatter.5.cloned.1.call-done = bf16[1024,256]{0,1:T(8,128)(2,1)} async-done(((bf16[4096,256]{0,1:T(8,128)(2,1)}), bf16[1024,256]{0,1:T(8,128)(2,1)}) %reduce-scatter.5.cloned.1.call-update) | async-done | bytes 524304 | tf_op jit(solution)/shard_map/reduce_scatter | solution.py:200
  121.3 1.3 fusion.21
  122.6 5.8 %psum.7 = f32[256]{0:T(256)S(1)} all-reduce(f32[256]{0:T(256)S(1)} %fusion.21), channel_id=1, replica_groups=mesh['dp'=8,'tensor'=4] {'tensor'}, use_global_device_ids=true, to_apply=%region_11.12 | all-reduce | flops 256 | bytes 2048 | tf_op jit(solution)/shard_map/psum | solution.py:212
  128.4 26.9 %reduce-scatter.3.cloned.1.call-done = bf16[1024,256]{0,1:T(8,128)(2,1)} async-done(((bf16[4096,256]{0,1:T(8,128)(2,1)}), bf16[1024,256]{0,1:T(8,128)(2,1)}) %reduce-scatter.3.cloned.1.call-update) | async-done | bytes 524304 | tf_op jit(solution)/shard_map/reduce_scatter | solution.py:119
  155.3 2.5 %fusion.20 = (bf16[256,1024]{1,0:T(8,128)(2,1)}, bf16[256,1024]{1,0:T(8,128)(2,1)S(1)}) fusion(bf16[256,1024]{1,0:T(8,128)(2,1)S(1)} %copy-done, bf16[1024,256]{0,1:T(8,128)(2,1)} %reduce-scatter.5.cloned.1.call-done, bf16[256,1024]{1,0:T(8,128)(2,1)S(1)} %copy-done.1, f32[256]{0:T(256)S(1)} %broadcast_multiply_fusion, f32[256]{0:T(256)S(1)} %get-tuple-element.20, ...), kind=kLoop, calls=%fused_computation.37 | loop fusion | flops 3407872 | bytes 3152896 | tf_op jit(solution)/shard_map/convert_element_type | solution.py:221
  157.8 0.2 reshape.230
  158.0 0.3 fusion
  158.3 1.1 reduce.1
  159.4 0.4 reshape.243
  159.8 19.9 %all_to_all.24 = bf16[8,2,16384]{2,1,0:T(2,128)(2,1)S(1)} all-to-all(bf16[8,2,16384]{2,1,0:T(2,128)(2,1)S(1)} %reshape.243), channel_id=1, replica_groups=mesh['dp'=8,'tensor'=4] {'dp'}, dimensions={0} | all-to-all | bytes 1048576 | tf_op jit(solution)/shard_map/all_to_all | solution.py:142
  179.6 0.5 reshape.244
  180.2 0.7 convolution_convert_fusion.2
  180.8 1.0 reshape.231
  (49 shorter events, 1.0 us)
Async XLA Ops:
  7.2 31.1 %all-gather.3.cloned.1.call-start = ((), (), s32[]{:S(2)}) async-start(), calls=%async_computation.4 | async-start | bytes 2621440 | tf_op jit(solution)/shard_map/all_gather | solution.py:79
  10.2 10.5 %copy-start.12 = (s32[1,2]{1,0:T(1,128)S(1)}, s32[1,2]{1,0:T(1,128)}, u32[]{:S(2)}) copy-start(s32[1,2]{1,0:T(1,128)} %param.16) | copy-start | bytes 28
  13.4 21.7 %all-to-all-start.1 = ((bf16[8,2,16384]{2,1,0:T(2,128)(2,1)}), bf16[8,2,16384]{2,1,0:T(2,128)(2,1)S(1)}, u32[]{:S(2)}, u32[]{:S(2)}) async-start(bf16[8,2,16384]{2,1,0:T(2,128)(2,1)} %reshape.245), calls=%async_computation.2 | async-start | bytes 1048576 | tf_op jit(solution)/shard_map/all_to_all | solution.py:152
  20.6 39.6 %all-gather.5.cloned.1.call-start = ((), (), s32[]{:S(2)}) async-start(), calls=%async_computation.6 | async-start | bytes 2621440 | tf_op jit(solution)/shard_map/all_gather | solution.py:161
  21.6 14.1 %copy-start.9 = (s32[8]{0:T(128)}, s32[8]{0:T(128)S(1)}, u32[]{:S(2)}) copy-start(s32[8]{0:T(128)S(1)} %dynamic-slice_bitcast_fusion) | copy-start | bytes 100
  21.8 45.1 %copy-start.7 = (pred[256,256]{0,1:T(8,128)(4,1)}, pred[256,256]{0,1:T(8,128)(4,1)S(1)}, u32[]{:S(2)}) copy-start(pred[256,256]{0,1:T(8,128)(4,1)S(1)} %fusion.34) | copy-start | bytes 196612
  21.8 7.9 %copy-start.2 = (bf16[4096,256]{1,0:T(8,128)(2,1)S(1)}, bf16[4096,256]{1,0:T(8,128)(2,1)}, u32[]{:S(2)}) copy-start(bf16[4096,256]{1,0:T(8,128)(2,1)} %param.12) | copy-start | bytes 6291460
  29.7 2.4 %copy-start.3 = (bf16[4096,256]{1,0:T(8,128)(2,1)S(1)}, bf16[4096,256]{1,0:T(8,128)(2,1)}, u32[]{:S(2)}) copy-start(bf16[4096,256]{1,0:T(8,128)(2,1)} %param.13) | copy-start | bytes 6291460
  36.4 4.1 %copy-start.11 = (f32[4096]{0:T(1024)S(1)}, f32[4096]{0:T(1024)}, u32[]{:S(2)}) copy-start(f32[4096]{0:T(1024)} %param.10) | copy-start | bytes 49156
  37.4 83.9 %reduce-scatter.5.cloned.1.call-start = ((), (), s32[]{:S(2)}) async-start(), calls=%async_computation.7 | async-start | bytes 2621440 | tf_op jit(solution)/shard_map/reduce_scatter | solution.py:200
  38.2 2.3 %copy-start.4 = (bf16[256,4096]{1,0:T(8,128)(2,1)S(1)}, bf16[256,4096]{1,0:T(8,128)(2,1)}, u32[]{:S(2)}) copy-start(bf16[256,4096]{1,0:T(8,128)(2,1)} %all-gather.3.cloned.1.call-done) | copy-start | bytes 6291460
  47.4 1.2 copy-start.5
  48.6 0.9 slice-start
  66.8 2.4 %copy-start.13 = (f32[2,256,256,4]{2,1,3,0:T(8,128)S(1)}, f32[2,256,256,4]{2,1,3,0:T(8,128)}, u32[]{:S(2)}) copy-start(f32[2,256,256,4]{2,1,3,0:T(8,128)} %get-tuple-element.23) | copy-start | bytes 6291460
  69.2 1.6 copy-start.8
  75.0 0.9 copy-start.6
  89.7 65.6 %reduce-scatter.3.cloned.1.call-start = ((), (), s32[]{:S(2)}) async-start(), calls=%async_computation.5 | async-start | bytes 2621440 | tf_op jit(solution)/shard_map/reduce_scatter | solution.py:119
  96.9 24.4 %copy-start = (bf16[256,1024]{1,0:T(8,128)(2,1)S(1)}, bf16[256,1024]{1,0:T(8,128)(2,1)}, u32[]{:S(2)}) copy-start(bf16[256,1024]{1,0:T(8,128)(2,1)} %param.9) | copy-start | bytes 1572868
  96.9 58.4 %copy-start.1 = (bf16[256,1024]{1,0:T(8,128)(2,1)S(1)}, bf16[256,1024]{1,0:T(8,128)(2,1)}, u32[]{:S(2)}) copy-start(bf16[256,1024]{1,0:T(8,128)(2,1)} %reshape.233) | copy-start | bytes 1572868
  155.3 2.7 %copy-start.10 = (s32[8]{0:T(128)S(1)}, s32[8]{0:T(128)}, u32[]{:S(2)}) copy-start(s32[8]{0:T(128)} %copy-done.9) | copy-start | bytes 100
Sparse Core Ops, SparseCore 0:
  9.6 25.2 all-gather.2
  37.5 22.6 all-gather.4
  89.9 31.4 reduce-scatter.4
  123.9 31.3 reduce-scatter.2
where the time goes:
time: 189 us; the launch traced here: 188 us
  waiting for transfers between devices  60.6 us (32%)
  matrix products  43.8 us (23%)
  blocking collectives  25.6 us (14%)
  local copies, waits for them, and re-layouts  25.1 us (13%)
  between operations  14.2 us (8%)
  other arithmetic  11.4 us (6%)
  starting transfers between devices  7.59 us (4%)
    reduce_scatter x1, waiting for transfers between devices, per_device(): lax.psum_scatter(lax.dot_general(w_out, attended_flat, (((0,), (1,)), (()...  26.9 us
    reduce_scatter x1, waiting for transfers between devices, per_device(): lax.psum_scatter(lax.dot_general(w_joined, joined_grad, (((1,), (1,)), ((...  23.6 us
    all_to_all x1, blocking collectives, per_device(): lax.all_to_all(outgoing, 'dp', split_axis=0, concat_axis=0, tiled=True)  19.9 us
    unnamed x39, local copies, waits for them, and re-layouts  15.5 us
    dot_general x1, matrix products, per_device(): lax.dot_general(w_joined, joined_grad, (((1,), (1,)), ((), ())), preferre...  13.8 us
    all_gather x1, waiting for transfers between devices, per_device(): lax.all_gather(grad_home, 'tensor', axis=1, tiled=True)  7.99 us
    all_to_all x1, starting transfers between devices, per_device(): lax.all_to_all(returning, 'dp', split_axis=0, concat_axis=0, tiled=True)  7.25 us
    dot_general x1, matrix products, per_device(): lax.dot_general(w_out, attended_flat, (((0,), (1,)), ((), ())), preferred...  7.11 us
  transfers between devices with their start and end apart: 5, of which 4 were waited for; matrix products, arithmetic and copies ran while one was open for 23% of the time, Pallas kernels for 0%

commit v1 on v0

--- a/solution.py
+++ b/solution.py
@@ -49,6 +49,71 @@
     return jnp.concatenate(
         [former * cos_part + latter * sin_part, latter * cos_part - former * sin_part], axis=-1
     )
+
+
+def _is_pow2(n):
+    return n > 1 and (n & (n - 1)) == 0
+
+
+def _xor_pairs(size, bit):
+    return [(i, i ^ bit) for i in range(size)]
+
+
+def _xor_reorder(stack, position, size):
+    bit = 1
+    while bit < size:
+        swapped = stack[:, [m ^ bit for m in range(size)], :]
+        stack = jnp.where((position & bit) != 0, swapped, stack)
+        bit <<= 1
+    return stack
+
+
+def gather_features(shard, axis_name, size, position):
+    if not _is_pow2(size):
+        full = lax.all_gather(shard, axis_name, axis=1, tiled=True)
+        return full.reshape(shard.shape[0], size, shard.shape[1])
+    held = shard[:, None, :]
+    masks = [0]
+    bit = size >> 1
+    while bit:
+        incoming = lax.ppermute(held, axis_name, _xor_pairs(size, bit))
+        held = jnp.concatenate([held, incoming], axis=1)
+        masks = masks + [m ^ bit for m in masks]
+        bit >>= 1
+    held = held[:, [masks.index(m) for m in range(size)], :]
+    return _xor_reorder(held, position, size)
+
+
+def scatter_features(partial, axis_name, size, position):
+    if not _is_pow2(size):
+        summed = lax.psum_scatter(
+            partial.astype(jnp.bfloat16), axis_name, scatter_dimension=1, tiled=True
+        )
+        return summed[:, 0, :].astype(jnp.float32)
+    held = _xor_reorder(partial, position, size)
+    masks = list(range(size))
+    bit = 1
+    while bit < size:
+        keep = [i for i, m in enumerate(masks) if not m & bit]
+        send = [i for i, m in enumerate(masks) if m & bit]
+        outgoing = held[:, send, :].astype(jnp.bfloat16)
+        incoming = lax.ppermute(outgoing, axis_name, _xor_pairs(size, bit))
+        sent_masks = [masks[i] ^ bit for i in send]
+        order = [sent_masks.index(masks[i]) for i in keep]
+        held = held[:, keep, :] + incoming[:, order, :].astype(jnp.float32)
+        masks = [masks[i] for i in keep]
+        bit <<= 1
+    return held[:, 0, :]
+
+
+def sum_over(values, axis_name, size):
+    if not _is_pow2(size):
+        return lax.psum(values, axis_name)
+    bit = 1
+    while bit < size:
+        values = values + lax.ppermute(values, axis_name, _xor_pairs(size, bit))
+        bit <<= 1
+    return values
 
 
 def per_device(
@@ -65,6 +130,7 @@
     token_row_count, width_part = tokens.shape
     full_width = norm_gain.shape[0]
     sources = lax.axis_size("dp")
+    tensor_size = lax.axis_size("tensor")
     data_index = lax.axis_index("dp")
     tensor_index = lax.axis_index("tensor")
     query_width = w_query.shape[1]
@@ -74,13 +140,32 @@
     query_group_width = heads_local // kv_local
     scale_factor = 1.0 / math.sqrt(HEAD_SIZE)
     gain_part = lax.dynamic_slice_in_dim(norm_gain, tensor_index * width_part, width_part)
-    w_joined = jnp.concatenate([w_query, key_weight, value_weight], axis=1)
     x_float = tokens.astype(jnp.float32)
-    gathered = lax.all_gather(tokens, "tensor", axis=1, tiled=True)
+
+    block_count = block_owner.shape[1]
+    owner_row = lax.dynamic_slice_in_dim(block_owner, data_index, 1, 0)[0]
+    slot_index = jnp.arange(sources, dtype=jnp.int32)
+    send_table = (owner_row[None, :] == slot_index[:, None]).astype(jnp.bfloat16)
+
+    owned_blocks = grad_output.reshape(block_count, -1)
+    arrived = lax.all_to_all(owned_blocks, "dp", split_axis=0, concat_axis=0, tiled=True)
+    grad_home = (
+        lax.dot_general(
+            send_table, arrived, (((0,), (0,)), ((), ())), preferred_element_type=jnp.float32
+        )
+        .astype(jnp.bfloat16)
+        .reshape(token_row_count, width_part)
+    )
+
+    gathered = gather_features(tokens, "tensor", tensor_size, tensor_index).reshape(
+        token_row_count, full_width
+    )
     gathered_float = gathered.astype(jnp.float32)
     inverse = lax.rsqrt(jnp.mean(gathered_float * gathered_float, axis=1) + NORM_EPSILON)
     normed_input = (gathered_float * inverse[:, None] * norm_gain[None, :]).astype(jnp.bfloat16)
-    projected = jnp.dot(normed_input, w_joined, preferred_element_type=jnp.float32)
+    query_raw = jnp.dot(normed_input, w_query, preferred_element_type=jnp.float32)
+    key_raw = jnp.dot(normed_input, key_weight, preferred_element_type=jnp.float32)
+    value_raw = jnp.dot(normed_input, value_weight, preferred_element_type=jnp.float32)
     doc_ids, positions = doc_tables(doc_lengths[0], token_row_count)
     token_index = jnp.arange(token_row_count, dtype=jnp.int32)
     allowed = (doc_ids[:, None] == doc_ids[None, :]) & (
@@ -88,22 +173,12 @@
     )
     cosine, sine_table = rope_tables(positions, HEAD_SIZE)
     query_rows = rotate(
-        projected[:, :query_width].reshape(token_row_count, heads_local, HEAD_SIZE),
-        cosine,
-        sine_table,
+        query_raw.reshape(token_row_count, heads_local, HEAD_SIZE), cosine, sine_table
     ).astype(jnp.bfloat16)
     keys = rotate(
-        projected[:, query_width : query_width + key_width].reshape(
-            token_row_count, kv_local, HEAD_SIZE
-        ),
-        cosine,
-        sine_table,
-    ).astype(jnp.bfloat16)
-    value_rows = (
-        projected[:, query_width + key_width :]
-        .astype(jnp.bfloat16)
-        .reshape(token_row_count, kv_local, HEAD_SIZE)
-    )
+        key_raw.reshape(token_row_count, kv_local, HEAD_SIZE), cosine, sine_table
+    ).astype(jnp.bfloat16)
+    value_rows = value_raw.astype(jnp.bfloat16).reshape(token_row_count, kv_local, HEAD_SIZE)
     grouped_query = query_rows.reshape(token_row_count, kv_local, query_group_width, HEAD_SIZE)
     scores = (
         jnp.einsum("qkgd,skd->kgqs", grouped_query, keys, preferred_element_type=jnp.float32)
@@ -116,49 +191,24 @@
         "kgqs,skd->qkgd", probs_low, value_rows, preferred_element_type=jnp.float32
     ).astype(jnp.bfloat16)
     attended_flat = attended.reshape(token_row_count, query_width)
-    mixed_turned = lax.psum_scatter(
-        lax.dot_general(
-            w_out, attended_flat, (((0,), (1,)), ((), ())), preferred_element_type=jnp.float32
-        ).astype(jnp.bfloat16),
-        "tensor",
-        scatter_dimension=0,
-        tiled=True,
-    ).astype(jnp.float32)
-    output_home = (x_float + mixed_turned.T).astype(jnp.bfloat16)
-    block_count = block_owner.shape[1]
-    owner_row = lax.dynamic_slice_in_dim(block_owner, data_index, 1, 0)[0]
-    slot_index = jnp.arange(sources, dtype=jnp.int32)
-    send_table = (owner_row[None, :] == slot_index[:, None]).astype(jnp.bfloat16)
-    owned_flags = jnp.sum((block_owner == data_index).astype(jnp.int32), axis=1)
-    owned_rank = jnp.cumsum(owned_flags) - owned_flags
-    block_index = jnp.arange(block_count, dtype=jnp.int32)
-    keep_table = (
-        (owned_rank[None, :] == block_index[:, None]) & (owned_flags[None, :] > 0)
-    ).astype(jnp.bfloat16)
+    mixed_partial = jnp.dot(attended_flat, w_out, preferred_element_type=jnp.float32).reshape(
+        token_row_count, tensor_size, width_part
+    )
+    mixed = scatter_features(mixed_partial, "tensor", tensor_size, tensor_index)
+    output_home = (x_float + mixed).astype(jnp.bfloat16)
     home_blocks = output_home.reshape(block_count, -1)
     outgoing = jnp.dot(send_table, home_blocks, preferred_element_type=jnp.float32).astype(
         jnp.bfloat16
     )
-    incoming = lax.all_to_all(outgoing, "dp", split_axis=0, concat_axis=0, tiled=True)
-    relaid = (
-        jnp.dot(keep_table, incoming, preferred_element_type=jnp.float32)
-        .astype(jnp.bfloat16)
-        .reshape(token_row_count, width_part)
-    )
-    owned_blocks = grad_output.reshape(block_count, -1)
-    returning = lax.dot_general(
-        keep_table, owned_blocks, (((0,), (0,)), ((), ())), preferred_element_type=jnp.float32
-    ).astype(jnp.bfloat16)
-    arrived = lax.all_to_all(returning, "dp", split_axis=0, concat_axis=0, tiled=True)
-    grad_home = (
-        lax.dot_general(
-            send_table, arrived, (((0,), (0,)), ((), ())), preferred_element_type=jnp.float32
-        )
-        .astype(jnp.bfloat16)
-        .reshape(token_row_count, width_part)
+    relaid = lax.all_to_all(outgoing, "dp", split_axis=0, concat_axis=0, tiled=True).reshape(
+        token_row_count, width_part
+    )
+
+    grad_full = gather_features(grad_home, "tensor", tensor_size, tensor_index).reshape(
+        token_row_count, full_width
     )
     attended_gradient = lax.dot_general(
-        lax.all_gather(grad_home, "tensor", axis=1, tiled=True),
+        grad_full,
         w_out,
         (((1,), (1,)), ((), ())),
         preferred_element_type=jnp.float32,
@@ -188,29 +238,34 @@
         grad_query_rot.reshape(token_row_count, heads_local, HEAD_SIZE), cosine, sine_table
     ).astype(jnp.bfloat16)
     key_gradient = unrotate(grad_keys_rot, cosine, sine_table).astype(jnp.bfloat16)
-    joined_grad = jnp.concatenate(
-        [
+    contract_out = (((1,), (1,)), ((), ()))
+    normed_partial = (
+        lax.dot_general(
             grad_query.reshape(token_row_count, query_width),
+            w_query,
+            contract_out,
+            preferred_element_type=jnp.float32,
+        )
+        + lax.dot_general(
             key_gradient.reshape(token_row_count, key_width),
+            key_weight,
+            contract_out,
+            preferred_element_type=jnp.float32,
+        )
+        + lax.dot_general(
             value_gradient.astype(jnp.bfloat16).reshape(token_row_count, key_width),
-        ],
-        axis=1,
-    )
-    normed_gradient = (
-        lax.psum_scatter(
-            lax.dot_general(
-                w_joined, joined_grad, (((1,), (1,)), ((), ())), preferred_element_type=jnp.float32
-            ).astype(jnp.bfloat16),
-            "tensor",
-            scatter_dimension=0,
-            tiled=True,
-        )
-        .astype(jnp.float32)
-        .T
-    )
-    stat = (
-        lax.psum(jnp.sum(normed_gradient * gain_part[None, :] * x_float, axis=1), "tensor")
-        / full_width
+            value_weight,
+            contract_out,
+            preferred_element_type=jnp.float32,
+        )
+    )
+    stat_partial = jnp.sum(normed_partial * norm_gain[None, :] * gathered_float, axis=1)
+    stat = sum_over(stat_partial, "tensor", tensor_size) / full_width
+    normed_gradient = scatter_features(
+        normed_partial.reshape(token_row_count, tensor_size, width_part),
+        "tensor",
+        tensor_size,
+        tensor_index,
     )
     cubed = inverse * inverse * inverse
     grad_x = (

time: 189 us -> 342 us (1.81); the launches traced: 188 us -> 335 us
  local copies, waits for them, and re-layouts: 25.1 us -> 151 us
  other arithmetic: 11.4 us -> 78.2 us
  waiting for transfers between devices: 60.6 us -> 27.9 us
  between operations: 14.2 us -> 1.42 us
  blocking collectives: 25.6 us -> 19.9 us
  starting transfers between devices: 7.59 us -> 12.1 us
    gather x0 -> x16, local copies, waits for them, and re-layouts: none -> 64.3 us  [the longest x8 35 us: _xor_reorder(): swapped = stack[:, [m ^ bit for m in range(size)], :]]
    reduce_scatter x2 -> x0, waiting for transfers between devices: 50.5 us -> none  [the longest x1 26.9 us: per_device(): lax.psum_scatter(lax.dot_general(w_out, attended_flat, (((0,), (1,)), (()...]
    select_n x0 -> x7, other arithmetic: none -> 37 us  [the longest x6 37 us: _xor_reorder(): stack = jnp.where(position & bit != 0, swapped, stack)]
    ppermute x0 -> x10, waiting for transfers between devices: none -> 27.9 us  [the longest x2 14.9 us: sum_over(): values = values + lax.ppermute(values, axis_name, _xor_pairs(size, bit))]
    dot_general x0 -> x3, local copies, waits for them, and re-layouts: none -> 27.5 us  [the longest x1 12.1 us: per_device(): jnp.dot(attended_flat, w_out, preferred_element_type=jnp.float32)]
    convert_element_type x2 -> x5, local copies, waits for them, and re-layouts: 0.96 us -> 18.4 us  [the longest x2 11.2 us: per_device(): gathered_float = gathered.astype(jnp.float32)]
    concatenate x0 -> x4, other arithmetic: none -> 9.88 us  [gather_features(): held = jnp.concatenate([held, incoming], axis=1)]
    all_gather x2 -> x0, waiting for transfers between devices: 8.01 us -> none  [the longest x1 7.99 us: per_device(): lax.all_gather(grad_home, 'tensor', axis=1, tiled=True)]
  transfers between devices with their start and end apart: 5 -> 11, of which waited for: 4 -> 3; matrix products, arithmetic and copies ran while one was open for 23% -> 43% of each run, Pallas kernels for 0% -> 0%
where the time goes in v1:
time: 342 us; the launch traced here: 335 us
  local copies, waits for them, and re-layouts  151 us (44%)
  other arithmetic  78.2 us (23%)
  matrix products  44.5 us (13%)
  waiting for transfers between devices  27.9 us (8%)
  blocking collectives  19.9 us (6%)
  starting transfers between devices  12.1 us (4%)
    select_n x6, other arithmetic, _xor_reorder(): stack = jnp.where(position & bit != 0, swapped, stack)  37 us
    gather x8, local copies, waits for them, and re-layouts, _xor_reorder(): swapped = stack[:, [m ^ bit for m in range(size)], :]  35 us
    all_to_all x1, blocking collectives, per_device(): lax.all_to_all(outgoing, 'dp', split_axis=0, concat_axis=0, tiled=True)  19.9 us
    ppermute x2, waiting for transfers between devices, sum_over(): values = values + lax.ppermute(values, axis_name, _xor_pairs(size, bit))  14.9 us
    unnamed x82, local copies, waits for them, and re-layouts  14.9 us
    gather x4, local copies, waits for them, and re-layouts, scatter_features(): held = held[:, keep, :] + incoming[:, order, :].astype(jnp.float32)  14.1 us
    ppermute x4, waiting for transfers between devices, gather_features(): incoming = lax.ppermute(held, axis_name, _xor_pairs(size, bit))  12.9 us
    dot_general x1, local copies, waits for them, and re-layouts, per_device(): jnp.dot(attended_flat, w_out, preferred_element_type=jnp.float32)  12.1 us
  transfers between devices with their start and end apart: 11, of which 3 were waited for; matrix products, arithmetic and copies ran while one was open for 43% of the time, Pallas kernels for 0%

profile of v1, /device:TPU:0, one launch (start us, length us, event | category | flops | bytes accessed | tf_op | source)
XLA Modules:
  0.0 335.2 jit_solution(13185570704129343056)
XLA Ops:
  0.6 3.0 collective-permute-start
  3.7 2.1 all_to_all.19
  6.4 4.6 %reduce.2 = bf16[8,32768]{1,0:T(8,128)(2,1)} reduce(bf16[8,1,32768]{2,1,0:T(2,128)(2,1)S(1)} %all_to_all.19, bf16[]{:T(256)} %broadcast.327), dimensions={1}, to_apply=%all_to_all.19.reduce_sub_computation | reduce | bytes 1048578 | tf_op jit(solution)/shard_map/all_to_all | solution.py:151
  11.0 2.2 reshape.594
  13.2 6.0 %all-to-all-start.1 = ((bf16[8,2,16384]{2,1,0:T(2,128)(2,1)}), bf16[8,2,16384]{2,1,0:T(2,128)(2,1)S(1)}, u32[]{:S(2)}, u32[]{:S(2)}) async-start(bf16[8,2,16384]{2,1,0:T(2,128)(2,1)} %reshape.594), calls=%async_computation.1 | async-start | bytes 1048576 | tf_op jit(solution)/shard_map/all_to_all | solution.py:151
  19.3 11.4 %copy.197 = bf16[1024,4096]{1,0:T(8,128)(2,1)} copy(bf16[1024,4096]{0,1:T(8,128)(2,1)} %bitcast.169) | data formatting | bytes 16777216 | tf_op jit(solution)/shard_map/dot_general | solution.py:166
  30.8 4.1 %copy.193 = bf16[256,4096]{1,0:T(8,128)(2,1)} copy(bf16[256,4096]{0,1:T(8,128)(2,1)} %bitcast.177) | data formatting | bytes 4194304 | tf_op jit(solution)/shard_map/dot_general | solution.py:167
  34.9 12.1 %copy.199 = bf16[4096,1024]{1,0:T(8,128)(2,1)} copy(bf16[4096,1024]{0,1:T(8,128)(2,1)} %bitcast.168) | data formatting | bytes 16777216 | tf_op jit(solution)/shard_map/dot_general | solution.py:194
  47.8 2.1 pad_maximum_fusion.2
  57.0 12.9 %collective-permute-done.4 = bf16[256,1,1024]{2,0,1:T(8,128)(2,1)S(1)} collective-permute-done((bf16[256,1,1024]{2,0,1:T(8,128)(2,1)}, bf16[256,1,1024]{2,0,1:T(8,128)(2,1)S(1)}, u32[]{:S(2)}, u32[]{:S(2)}) %collective-permute-start.4) | collective-permute-done | bytes 524320 | tf_op jit(solution)/shard_map/ppermute | solution.py:79
  70.7 2.1 pad_maximum_fusion.3
  72.8 2.9 pad_maximum_fusion
  75.7 3.6 %gather_fusion = bf16[4,256,1024]{2,1,0:T(8,128)(2,1)} fusion(bf16[256,4,1024]{2,0,1:T(8,128)(2,1)} %pad_maximum_fusion, s32[1024]{0:T(1024)S(1)} %pad_clamp_fusion.5), kind=kCustom, calls=%fused_computation | custom fusion | bytes 4194320 | tf_op jit(solution)/shard_map/gather | solution.py:83
  79.3 3.6 %gather_fusion.1 = bf16[4,256,1024]{2,1,0:T(8,128)(2,1)} fusion(bf16[256,4,1024]{2,0,1:T(8,128)(2,1)} %bitcast.165, s32[1024]{0:T(1024)S(1)} %pad_clamp_fusion.4), kind=kCustom, calls=%fused_computation.1 | custom fusion | bytes 4194320 | tf_op jit(solution)/shard_map/gather | solution.py:65
  82.9 3.8 %bitcast_select_fusion.8 = bf16[256,4,1024]{2,0,1:T(8,128)(2,1)} fusion(bf16[4,256,1024]{2,1,0:T(8,128)(2,1)} %gather_fusion.1, pred[]{:T(512)S(6)} %ne.5, bf16[4,256,1024]{2,1,0:T(8,128)(2,1)} %gather_fusion), kind=kLoop, calls=%fused_computation.40 | loop fusion | flops 1048576 | bytes 6291457 | tf_op jit(solution)/shard_map/jit(_where)/select_n | solution.py:66
  86.7 3.6 %gather_fusion.2 = bf16[4,256,1024]{2,1,0:T(8,128)(2,1)} fusion(bf16[256,4,1024]{2,0,1:T(8,128)(2,1)} %bitcast_select_fusion.8, s32[1024]{0:T(1024)S(1)} %pad_clamp_fusion.3), kind=kCustom, calls=%fused_computation.2 | custom fusion | bytes 4194320 | tf_op jit(solution)/shard_map/gather | solution.py:65
  90.3 4.9 %multiply_reduce_fusion.1 = (f32[256]{0:T(256)S(1)}, f32[256,4,1024]{2,0,1:T(8,128)}) fusion(bf16[256,4,1024]{2,0,1:T(8,128)(2,1)} %bitcast_select_fusion.8, bf16[4,256,1024]{2,1,0:T(8,128)(2,1)} %gather_fusion.2, pred[]{:T(512)S(6)} %ne.4), kind=kLoop, calls=%fused_computation.28 | loop fusion | flops 4194048 | bytes 8389633 | tf_op jit(solution)/shard_map/reduce_sum | solution.py:164
  95.8 5.4 %copy.150 = f32[256,4,1024]{0,2,1:T(8,128)} copy(f32[256,4,1024]{2,0,1:T(8,128)} %get-tuple-element.49) | data formatting | bytes 8388608 | tf_op jit(solution)/shard_map/convert_element_type | solution.py:163
  101.2 4.3 %multiply_convert_fusion = bf16[256,4,1024]{2,0,1:T(8,128)(2,1)} fusion(f32[256,4,1024]{2,0,1:T(8,128)} %get-tuple-element.49, f32[4,1024]{1,0:T(4,128)S(1)} %mul.275, f32[256]{0:T(256)S(1)} %get-tuple-element.63), kind=kLoop, calls=%fused_computation.26 | loop fusion | flops 3145728 | bytes 6308864 | tf_op jit(solution)/shard_map/convert_element_type | solution.py:165
  105.5 3.9 %copy.152 = bf16[256,4,1024]{0,2,1:T(8,128)(2,1)} copy(bf16[256,4,1024]{2,0,1:T(8,128)(2,1)} %multiply_convert_fusion) | data formatting | bytes 4194304 | tf_op jit(solution)/shard_map/convert_element_type | solution.py:165
  109.4 6.5 %fusion.38 = f32[256,8,128]{0,2,1:T(8,128)S(1)} fusion(bf16[256,4096,1]{0,1,2:T(8,128)(2,1)} %bitcast.175, bf16[8,128,4096]{2,1,0:T(8,128)(2,1)} %bitcast.173), kind=kOutput, calls=%fused_computation.120 | convolution fusion | flops 2147483648 | bytes 11534336 | tf_op jit(solution)/shard_map/dot_general | solution.py:166
  117.6 2.0 copy.157
  119.5 2.0 copy.158
  121.5 5.8 %copy.151 = f32[256,4096]{1,0:T(8,128)} copy(f32[256,4096]{0,1:T(8,128)} %bitcast.166) | data formatting | bytes 8388608 | tf_op jit(solution)/shard_map/convert_element_type | solution.py:163
  128.0 3.8 %fusion.8 = (f32[2,4,256]{2,1,0:T(4,128)}, f32[2,256,256,4]{2,1,3,0:T(8,128)}) fusion(pred[256,256]{0,1:T(8,128)(4,1)} %fusion.25, bf16[256,2,4,64]{3,0,2,1:T(8,128)(2,1)} %copy.158, bf16[256,2,4,64]{3,0,2,1:T(8,128)(2,1)} %copy.157, bf16[256,2,64]{0,2,1:T(8,128)(2,1)S(1)} %get-tuple-element.59, bf16[256,2,64]{0,2,1:T(8,128)(2,1)S(1)} %get-tuple-element.58), kind=kOutput, calls=%fused_computation.46 | convolution fusion | flops 137099264 | bytes 2826240 | tf_op jit(solution)/shard_map/qkgd,skd->kgqs/dot_general | solution.py:184
  131.9 3.3 fusion.12
  135.3 2.8 pad_maximum_fusion.1
  138.0 3.7 %gather_fusion.8 = bf16[4,256,1024]{2,1,0:T(8,128)(2,1)} fusion(bf16[256,4,1024]{2,0,1:T(8,128)(2,1)} %pad_maximum_fusion.1, s32[1024]{0:T(1024)} %copy-done.25), kind=kCustom, calls=%fused_computation.8 | custom fusion | bytes 4194320 | tf_op jit(solution)/shard_map/gather | solution.py:83
  141.7 3.7 %gather_fusion.9 = bf16[4,256,1024]{2,1,0:T(8,128)(2,1)} fusion(bf16[256,4,1024]{2,0,1:T(8,128)(2,1)} %bitcast.164, s32[1024]{0:T(1024)} %copy-done.24), kind=kCustom, calls=%fused_computation.9 | custom fusion | bytes 4194320 | tf_op jit(solution)/shard_map/gather | solution.py:65
  145.5 3.8 %bitcast_select_fusion.5 = bf16[256,4,1024]{2,0,1:T(8,128)(2,1)} fusion(bf16[4,256,1024]{2,1,0:T(8,128)(2,1)} %gather_fusion.9, pred[]{:T(512)S(6)} %ne.5, bf16[4,256,1024]{2,1,0:T(8,128)(2,1)} %gather_fusion.8), kind=kLoop, calls=%fused_computation.36 | loop fusion | flops 1048576 | bytes 6291457 | tf_op jit(solution)/shard_map/jit(_where)/select_n | solution.py:66
  149.3 3.7 %gather_fusion.10 = bf16[4,256,1024]{2,1,0:T(8,128)(2,1)} fusion(bf16[256,4,1024]{2,0,1:T(8,128)(2,1)} %bitcast_select_fusion.5, s32[1024]{0:T(1024)} %copy-done.23), kind=kCustom, calls=%fused_computation.10 | custom fusion | bytes 4194320 | tf_op jit(solution)/shard_map/gather | solution.py:65
  153.0 3.8 %bitcast_select_fusion.4 = bf16[256,4,1024]{2,0,1:T(8,128)(2,1)} fusion(bf16[256,4,1024]{2,0,1:T(8,128)(2,1)} %bitcast_select_fusion.5, bf16[4,256,1024]{2,1,0:T(8,128)(2,1)} %gather_fusion.10, pred[]{:T(512)S(6)} %ne.4), kind=kLoop, calls=%fused_computation.35 | loop fusion | flops 1048576 | bytes 6291457 | tf_op jit(solution)/shard_map/jit(_where)/select_n | solution.py:66
  156.7 3.9 %copy.165 = bf16[256,4,1024]{0,2,1:T(8,128)(2,1)} copy(bf16[256,4,1024]{2,0,1:T(8,128)(2,1)} %bitcast_select_fusion.4) | data formatting | bytes 4194304 | tf_op jit(solution)/shard_map/jit(_where)/select_n | solution.py:66
  160.7 7.2 %convolution_convert_fusion.2 = bf16[256,1024]{1,0:T(8,128)(2,1)} fusion(bf16[256,4096]{0,1:T(8,128)(2,1)} %bitcast.182, bf16[1024,4096]{1,0:T(8,128)(2,1)} %param.36), kind=kOutput, calls=%fused_computation.50 | convolution fusion | flops 2147745792 | bytes 11010048 | tf_op jit(solution)/shard_map/dot_general | solution.py:210
  167.9 2.0 copy.166
  169.9 2.6 fusion.11
  177.0 2.4 fusion.40
  181.6 3.0 multiply_reduce_fusion
  184.6 5.7 %copy.173 = f32[256,4096]{0,1:T(8,128)} copy(f32[256,4096]{1,0:T(8,128)} %get-tuple-element.69) | data formatting | bytes 8388608 | tf_op jit(solution)/shard_map/add | solution.py:243
  190.3 5.8 %copy.174 = f32[256,4,1024]{2,0,1:T(8,128)} copy(f32[256,4,1024]{0,2,1:T(8,128)} %bitcast.167) | data formatting | bytes 8388608 | tf_op jit(solution)/shard_map/reshape | solution.py:265
  196.1 5.1 %gather_fusion.11 = f32[4,256,1024]{2,1,0:T(8,128)} fusion(f32[256,4,1024]{2,0,1:T(8,128)} %copy.174, s32[1024]{0:T(1024)} %copy-done.24), kind=kCustom, calls=%fused_computation.11 | custom fusion | bytes 8388624 | tf_op jit(solution)/shard_map/gather | solution.py:65
  201.1 8.0 %fusion.39 = f32[256,4,1024]{2,0,1:T(8,128)} fusion(bf16[256,1024,1]{0,1,2:T(8,128)(2,1)} %bitcast.196, bf16[4,1024,1024]{2,1,0:T(8,128)(2,1)} %bitcast.172), kind=kOutput, calls=%fused_computation.121 | convolution fusion | flops 2147483648 | bytes 13107200 | tf_op jit(solution)/shard_map/dot_general | solution.py:194
  209.1 5.1 %gather_fusion.3 = f32[4,256,1024]{2,1,0:T(8,128)} fusion(f32[256,4,1024]{2,0,1:T(8,128)} %fusion.39, s32[1024]{0:T(1024)} %copy-done.24), kind=kCustom, calls=%fused_computation.3 | custom fusion | bytes 8388624 | tf_op jit(solution)/shard_map/gather | solution.py:65
  214.2 12.0 %bitcast_select_fusion.1 = (f32[256,4,1024]{2,0,1:T(8,128)}, f32[256,4,1024]{2,0,1:T(8,128)}) fusion(f32[256,4,1024]{2,0,1:T(8,128)} %copy.174, f32[4,256,1024]{2,1,0:T(8,128)} %gather_fusion.11, pred[]{:T(512)S(6)} %ne.5, f32[256,4,1024]{2,0,1:T(8,128)} %fusion.39, f32[4,256,1024]{2,1,0:T(8,128)} %gather_fusion.3), kind=kLoop, calls=%fused_computation.22 | loop fusion | flops 2097152 | bytes 25165824 | tf_op jit(solution)/shard_map/jit(_where)/select_n | solution.py:66
  226.2 5.1 %gather_fusion.4 = f32[4,256,1024]{2,1,0:T(8,128)} fusion(f32[256,4,1024]{2,0,1:T(8,128)} %get-tuple-element.71, s32[1024]{0:T(1024)} %copy-done.23), kind=kCustom, calls=%fused_computation.4 | custom fusion | bytes 8388624 | tf_op jit(solution)/shard_map/gather | solution.py:65
  231.4 6.9 %bitcast_select_fusion.2 = f32[256,4,1024]{2,0,1:T(8,128)} fusion(f32[256,4,1024]{2,0,1:T(8,128)} %get-tuple-element.71, f32[4,256,1024]{2,1,0:T(8,128)} %gather_fusion.4, pred[]{:T(512)S(6)} %ne.4), kind=kLoop, calls=%fused_computation.23 | loop fusion | flops 1048576 | bytes 12582913 | tf_op jit(solution)/shard_map/jit(_where)/select_n | solution.py:66
  238.2 3.9 %gather_fusion.6 = bf16[2,256,1024]{2,1,0:T(8,128)(2,1)} fusion(f32[256,4,1024]{2,0,1:T(8,128)} %bitcast_select_fusion.2, s32[1024]{0:T(1024)} %pad_clamp_fusion.1), kind=kCustom, calls=%fused_computation.6 | custom fusion | bytes 2097160 | tf_op jit(solution)/shard_map/gather | solution.py:99
  242.2 5.1 %gather_fusion.12 = f32[4,256,1024]{2,1,0:T(8,128)} fusion(f32[256,4,1024]{2,0,1:T(8,128)} %get-tuple-element.70, s32[1024]{0:T(1024)} %copy-done.23), kind=kCustom, calls=%fused_computation.12 | custom fusion | bytes 8388624 | tf_op jit(solution)/shard_map/gather | solution.py:65
  247.2 6.8 %bitcast_select_fusion = f32[256,4,1024]{2,0,1:T(8,128)} fusion(f32[256,4,1024]{2,0,1:T(8,128)} %get-tuple-element.70, f32[4,256,1024]{2,1,0:T(8,128)} %gather_fusion.12, pred[]{:T(512)S(6)} %ne.4), kind=kLoop, calls=%fused_computation.21 | loop fusion | flops 1048576 | bytes 12582913 | tf_op jit(solution)/shard_map/jit(_where)/select_n | solution.py:66
  254.0 4.0 %gather_fusion.14 = bf16[2,256,1024]{2,1,0:T(8,128)(2,1)} fusion(f32[256,4,1024]{2,0,1:T(8,128)} %bitcast_select_fusion, s32[1024]{0:T(1024)} %pad_clamp_fusion.1), kind=kCustom, calls=%fused_computation.14 | custom fusion | bytes 2097160 | tf_op jit(solution)/shard_map/gather | solution.py:99
  258.5 4.2 %gather_fusion.5 = f32[2,256,1024]{2,1,0:T(8,128)} fusion(f32[256,4,1024]{2,0,1:T(8,128)} %bitcast_select_fusion.2, s32[1024]{0:T(1024)S(1)} %pad_clamp_fusion.2), kind=kCustom, calls=%fused_computation.5 | custom fusion | bytes 4194312 | tf_op jit(solution)/shard_map/gather | solution.py:103
  262.8 4.2 %gather_fusion.13 = f32[2,256,1024]{2,1,0:T(8,128)} fusion(f32[256,4,1024]{2,0,1:T(8,128)} %bitcast_select_fusion, s32[1024]{0:T(1024)S(1)} %pad_clamp_fusion.2), kind=kCustom, calls=%fused_computation.13 | custom fusion | bytes 4194312 | tf_op jit(solution)/shard_map/gather | solution.py:103
  267.0 2.8 gather_fusion.7
  269.8 2.2 add_bitcast_fusion.1
  274.2 2.8 gather_fusion.15
  277.0 2.2 add_bitcast_fusion
  281.4 2.0 collective-permute-start.7
  285.8 13.8 %collective-permute-done.9 = f32[256]{0:T(256)S(1)} collective-permute-done((f32[256]{0:T(256)S(1)}, f32[256]{0:T(256)S(1)}, u32[]{:S(2)}, u32[]{:S(2)}) %collective-permute-start.9) | collective-permute-done | bytes 1056 | tf_op jit(solution)/shard_map/ppermute | solution.py:114
  299.6 3.4 %fusion.16 = (bf16[256,1024]{1,0:T(8,128)(2,1)}, bf16[256,1024]{1,0:T(8,128)(2,1)S(1)}) fusion(bf16[256,1024]{1,0:T(8,128)(2,1)S(1)} %copy-done.7, f32[256,1024]{1,0:T(8,128)} %reshape.444, f32[256,2,1024]{2,0,1:T(8,128)} %copy-done.6, bf16[256,1,1024]{2,0,1:T(8,128)(2,1)} %collective-permute-done.7, f32[256]{0:T(256)S(1)} %add_multiply_fusion, ...), kind=kLoop, calls=%fused_computation.61 | loop fusion | flops 3670016 | bytes 5774336 | tf_op jit(solution)/shard_map/convert_element_type | solution.py:276
  304.4 2.0 reduce.3
  306.9 19.9 %all_to_all.22 = bf16[8,2,16384]{2,1,0:T(2,128)(2,1)} all-to-all(bf16[8,2,16384]{2,1,0:T(2,128)(2,1)S(1)} %reshape.592), channel_id=1, replica_groups=mesh['dp'=8,'tensor'=4] {'dp'}, dimensions={0} | all-to-all | bytes 1048576 | tf_op jit(solution)/shard_map/all_to_all | solution.py:203
  326.7 2.2 reshape.593
  329.0 4.0 %reduce.1 = bf16[8,32768]{1,0:T(8,128)(2,1)} reduce(bf16[8,1,32768]{2,1,0:T(2,128)(2,1)S(1)} %reshape.593, bf16[]{:T(256)} %constant.194), dimensions={1}, to_apply=%all_to_all.15.reduce_sub_computation | reduce | bytes 1048578 | tf_op jit(solution)/shard_map/all_to_all | solution.py:203
  332.9 2.1 reshape.339
  (136 shorter events, 27.9 us)
Async XLA Ops:
  0.6 131.3 %copy-start = (bf16[4096,256]{1,0:T(8,128)(2,1)S(1)}, bf16[4096,256]{1,0:T(8,128)(2,1)}, u32[]{:S(2)}) copy-start(bf16[4096,256]{1,0:T(8,128)(2,1)} %param.35) | copy-start | bytes 6291460
  0.6 47.1 %collective-permute-start = (bf16[256,1,1024]{2,0,1:T(8,128)(2,1)}, bf16[256,1,1024]{2,0,1:T(8,128)(2,1)}, u32[]{:S(2)}, u32[]{:S(2)}) collective-permute-start(bf16[256,1,1024]{2,0,1:T(8,128)(2,1)} %bitcast.178), channel_id=1, source_target_pairs={{0,2},{1,3},{2,0},{3,1},{4,6},{5,7},{6,4},{7,5},{8,10},{9,11},{10,... | collective-permute-start | bytes 1572872 | tf_op jit(solution)/shard_map/ppermute | solution.py:79
  5.8 13.4 %copy-start.32 = (s32[4]{0:T(128)S(1)}, s32[4]{0:T(128)}, u32[]{:S(2)}) copy-start(s32[4]{0:T(128)} %constant.182) | copy-start | bytes 52
  5.8 13.4 %copy-start.18 = (f32[4096]{0:T(1024)S(1)}, f32[4096]{0:T(1024)}, u32[]{:S(2)}) copy-start(f32[4096]{0:T(1024)} %param.32) | copy-start | bytes 49156
  13.2 37.4 %all-to-all-start.1 = ((bf16[8,2,16384]{2,1,0:T(2,128)(2,1)}), bf16[8,2,16384]{2,1,0:T(2,128)(2,1)S(1)}, u32[]{:S(2)}, u32[]{:S(2)}) async-start(bf16[8,2,16384]{2,1,0:T(2,128)(2,1)} %reshape.594), calls=%async_computation.1 | async-start | bytes 1048576 | tf_op jit(solution)/shard_map/all_to_all | solution.py:151
  19.2 56.5 %copy-start.25 = (s32[1024]{0:T(1024)}, s32[1024]{0:T(1024)S(1)}, u32[]{:S(2)}) copy-start(s32[1024]{0:T(1024)S(1)} %pad_clamp_fusion.5) | copy-start | bytes 12292
  19.3 11.4 %copy-start.33 = (s32[1,2]{1,0:T(1,128)S(1)}, s32[1,2]{1,0:T(1,128)}, u32[]{:S(2)}) copy-start(s32[1,2]{1,0:T(1,128)} %param.38) | copy-start | bytes 28
  34.9 12.1 %copy-start.31 = (s32[4]{0:T(128)S(1)}, s32[4]{0:T(128)}, u32[]{:S(2)}) copy-start(s32[4]{0:T(128)} %constant.183) | copy-start | bytes 52
  34.9 12.1 %copy-start.30 = (s32[4]{0:T(128)S(1)}, s32[4]{0:T(128)}, u32[]{:S(2)}) copy-start(s32[4]{0:T(128)} %constant.184) | copy-start | bytes 52
  34.9 12.1 %copy-start.29 = (s32[2]{0:T(128)S(1)}, s32[2]{0:T(128)}, u32[]{:S(2)}) copy-start(s32[2]{0:T(128)} %constant.187) | copy-start | bytes 28
  34.9 12.9 %copy-start.7 = (bf16[256,1024]{1,0:T(8,128)(2,1)S(1)}, bf16[256,1024]{1,0:T(8,128)(2,1)}, u32[]{:S(2)}) copy-start(bf16[256,1024]{1,0:T(8,128)(2,1)} %param.31) | copy-start | bytes 1572868
  47.1 32.3 %copy-start.24 = (s32[1024]{0:T(1024)}, s32[1024]{0:T(1024)S(1)}, u32[]{:S(2)}) copy-start(s32[1024]{0:T(1024)S(1)} %pad_clamp_fusion.4) | copy-start | bytes 12292
  47.1 39.6 %copy-start.23 = (s32[1024]{0:T(1024)}, s32[1024]{0:T(1024)S(1)}, u32[]{:S(2)}) copy-start(s32[1024]{0:T(1024)S(1)} %pad_clamp_fusion.3) | copy-start | bytes 12292
  49.9 22.9 %collective-permute-start.1 = (bf16[256,2,1024]{2,0,1:T(8,128)(2,1)}, bf16[256,2,1024]{2,0,1:T(8,128)(2,1)}, u32[]{:S(2)}, u32[]{:S(2)}) collective-permute-start(bf16[256,2,1024]{2,0,1:T(8,128)(2,1)} %pad_maximum_fusion.2), channel_id=1, source_target_pairs={{0,1},{1,0},{2,3},{3,2},{4,5},{5,4},{6,7},{7,6},{8,9},{9,8},{10,11... | collective-permute-start | bytes 3145736 | tf_op jit(solution)/shard_map/ppermute | solution.py:79
  50.6 5.3 %copy-start.27 = (s32[8]{0:T(128)}, s32[8]{0:T(128)S(1)}, u32[]{:S(2)}) copy-start(s32[8]{0:T(128)S(1)} %dynamic-slice_bitcast_fusion) | copy-start | bytes 100
  55.4 14.5 %collective-permute-start.4 = (bf16[256,1,1024]{2,0,1:T(8,128)(2,1)}, bf16[256,1,1024]{2,0,1:T(8,128)(2,1)S(1)}, u32[]{:S(2)}, u32[]{:S(2)}) collective-permute-start(bf16[256,1,1024]{2,0,1:T(8,128)(2,1)} %broadcast_in_dim_reshape.3), channel_id=1, source_target_pairs={{0,2},{1,3},{2,0},{3,1},{4,6},{5,7},{6,4},{7,5},{8,10},{9,11},{10,... | collective-permute-start | bytes 1572872 | tf_op jit(solution)/shard_map/ppermute | solution.py:79
  69.9 0.8 copy-start.11
  72.8 62.4 %collective-permute-start.5 = (bf16[256,2,1024]{2,0,1:T(8,128)(2,1)}, bf16[256,2,1024]{2,0,1:T(8,128)(2,1)}, u32[]{:S(2)}, u32[]{:S(2)}) collective-permute-start(bf16[256,2,1024]{2,0,1:T(8,128)(2,1)} %pad_maximum_fusion.3), channel_id=1, source_target_pairs={{0,1},{1,0},{2,3},{3,2},{4,5},{5,4},{6,7},{7,6},{8,9},{9,8},{10,11... | collective-permute-start | bytes 3145736 | tf_op jit(solution)/shard_map/ppermute | solution.py:79
  95.8 5.4 %copy-start.20 = (f32[256]{0:T(256)}, f32[256]{0:T(256)S(1)}, u32[]{:S(2)}) copy-start(f32[256]{0:T(256)S(1)} %get-tuple-element.63) | copy-start | bytes 3076
  109.4 6.5 %copy-start.2 = (bf16[256,4096]{1,0:T(8,128)(2,1)S(1)}, bf16[256,4096]{1,0:T(8,128)(2,1)}, u32[]{:S(2)}) copy-start(bf16[256,4096]{1,0:T(8,128)(2,1)} %copy.193) | copy-start | bytes 6291460
  109.4 6.5 %copy-start.3 = (bf16[256,4,1024]{0,2,1:T(8,128)(2,1)S(1)}, bf16[256,4,1024]{0,2,1:T(8,128)(2,1)}, u32[]{:S(2)}) copy-start(bf16[256,4,1024]{0,2,1:T(8,128)(2,1)} %copy.152) | copy-start | bytes 6291460
  127.4 4.5 %copy-start.21 = (f32[256]{0:T(256)S(1)}, f32[256]{0:T(256)}, u32[]{:S(2)}) copy-start(f32[256]{0:T(256)} %copy-done.20) | copy-start | bytes 3076
  127.4 0.6 copy-start.14
  127.4 0.6 copy-start.16
  131.9 3.4 %copy-start.8 = (bf16[256,1,1024]{2,0,1:T(8,128)(2,1)S(1)}, bf16[256,1,1024]{2,0,1:T(8,128)(2,1)}, u32[]{:S(2)}) copy-start(bf16[256,1,1024]{2,0,1:T(8,128)(2,1)} %broadcast_in_dim_reshape.3) | copy-start | bytes 1572868
  131.9 3.4 %copy-start.12 = (bf16[256,1,1024]{2,0,1:T(8,128)(2,1)S(1)}, bf16[256,1,1024]{2,0,1:T(8,128)(2,1)}, u32[]{:S(2)}) copy-start(bf16[256,1,1024]{2,0,1:T(8,128)(2,1)} %copy-done.11) | copy-start | bytes 1572868
  169.9 2.6 copy-start.13
  169.9 2.6 copy-start.19
  169.9 2.6 copy-start.34
  169.9 2.6 copy-start.35
  172.5 4.4 %slice-start = ((s8[8388608]{0:T(1024)(128)(4,1)}), s8[4194304]{0:T(1024)(128)(4,1)S(1)}, s32[]{:S(2)}) async-start(s8[8388608]{0:T(1024)(128)(4,1)} %bitcast.170), calls=%async_computation.2 | async-start | bytes 8388608
  174.0 1.0 copy-start.9
  174.0 1.2 copy-start.10
  174.0 2.9 slice-start.1
  175.2 1.1 copy-start.15
  175.2 1.2 copy-start.17
  177.0 2.4 copy-start.4
  179.4 2.2 copy-start.1
  242.2 24.9 %collective-permute-start.2 = (bf16[256,2,1024]{2,0,1:T(8,128)(2,1)}, bf16[256,2,1024]{2,0,1:T(8,128)(2,1)}, u32[]{:S(2)}, u32[]{:S(2)}) collective-permute-start(bf16[256,2,1024]{2,0,1:T(8,128)(2,1)} %bitcast.184), channel_id=1, source_target_pairs={{0,1},{1,0},{2,3},{3,2},{4,5},{5,4},{6,7},{7,6},{8,9},{9,8},{10,11... | collective-permute-start | bytes 3145736 | tf_op jit(solution)/shard_map/ppermute | solution.py:100
  258.0 16.2 %collective-permute-start.6 = (bf16[256,2,1024]{2,0,1:T(8,128)(2,1)}, bf16[256,2,1024]{2,0,1:T(8,128)(2,1)}, u32[]{:S(2)}, u32[]{:S(2)}) collective-permute-start(bf16[256,2,1024]{2,0,1:T(8,128)(2,1)} %bitcast.183), channel_id=1, source_target_pairs={{0,1},{1,0},{2,3},{3,2},{4,5},{5,4},{6,7},{7,6},{8,9},{9,8},{10,11... | collective-permute-start | bytes 3145736 | tf_op jit(solution)/shard_map/ppermute | solution.py:100
  272.0 1.3 copy-start.5
  274.2 25.4 %collective-permute-start.3 = (bf16[256,1,1024]{2,0,1:T(8,128)(2,1)}, bf16[256,1,1024]{2,0,1:T(8,128)(2,1)}, u32[]{:S(2)}, u32[]{:S(2)}) collective-permute-start(bf16[256,1,1024]{2,0,1:T(8,128)(2,1)} %slice.149), channel_id=1, source_target_pairs={{0,2},{1,3},{2,0},{3,1},{4,6},{5,7},{6,4},{7,5},{8,10},{9,11},{10,... | collective-permute-start | bytes 1572872 | tf_op jit(solution)/shard_map/ppermute | solution.py:100
  279.2 1.3 copy-start.6
  280.5 19.1 %copy-start.22 = (f32[256]{0:T(256)S(1)}, f32[256]{0:T(256)}, u32[]{:S(2)}) copy-start(f32[256]{0:T(256)} %copy-done.20) | copy-start | bytes 3076
  280.5 19.1 %copy-start.26 = (f32[256]{0:T(256)S(1)}, f32[256]{0:T(256)}, u32[]{:S(2)}) copy-start(f32[256]{0:T(256)} %get-tuple-element.62) | copy-start | bytes 3076
  281.4 18.2 %collective-permute-start.7 = (bf16[256,1,1024]{2,0,1:T(8,128)(2,1)}, bf16[256,1,1024]{2,0,1:T(8,128)(2,1)}, u32[]{:S(2)}, u32[]{:S(2)}) collective-permute-start(bf16[256,1,1024]{2,0,1:T(8,128)(2,1)} %slice.148), channel_id=1, source_target_pairs={{0,2},{1,3},{2,0},{3,1},{4,6},{5,7},{6,4},{7,5},{8,10},{9,11},{10,... | collective-permute-start | bytes 1572872 | tf_op jit(solution)/shard_map/ppermute | solution.py:100
  283.4 1.1 collective-permute-start.8
  284.6 15.0 %collective-permute-start.9 = (f32[256]{0:T(256)S(1)}, f32[256]{0:T(256)S(1)}, u32[]{:S(2)}, u32[]{:S(2)}) collective-permute-start(f32[256]{0:T(256)S(1)} %add.179), channel_id=1, source_target_pairs={{0,2},{1,3},{2,0},{3,1},{4,6},{5,7},{6,4},{7,5},{8,10},{9,11},{10,... | collective-permute-start | bytes 3080 | tf_op jit(solution)/shard_map/ppermute | solution.py:114
  299.6 3.7 %copy-start.28 = (s32[8]{0:T(128)S(1)}, s32[8]{0:T(128)}, u32[]{:S(2)}) copy-start(s32[8]{0:T(128)} %copy-done.27) | copy-start | bytes 100

commit v2 on v1

--- a/solution.py
+++ b/solution.py
@@ -59,51 +59,50 @@
     return [(i, i ^ bit) for i in range(size)]
 
 
-def _xor_reorder(stack, position, size):
-    bit = 1
-    while bit < size:
-        swapped = stack[:, [m ^ bit for m in range(size)], :]
-        stack = jnp.where((position & bit) != 0, swapped, stack)
-        bit <<= 1
-    return stack
-
-
 def gather_features(shard, axis_name, size, position):
     if not _is_pow2(size):
-        full = lax.all_gather(shard, axis_name, axis=1, tiled=True)
-        return full.reshape(shard.shape[0], size, shard.shape[1])
-    held = shard[:, None, :]
+        return lax.all_gather(shard, axis_name, axis=1, tiled=True)
+    held = shard[None]
     masks = [0]
     bit = size >> 1
     while bit:
         incoming = lax.ppermute(held, axis_name, _xor_pairs(size, bit))
-        held = jnp.concatenate([held, incoming], axis=1)
+        held = jnp.concatenate([held, incoming], axis=0)
         masks = masks + [m ^ bit for m in masks]
         bit >>= 1
-    held = held[:, [masks.index(m) for m in range(size)], :]
-    return _xor_reorder(held, position, size)
+    table = jnp.asarray([masks.index(m) for m in range(size)], jnp.int32)
+    blocks = [
+        lax.dynamic_index_in_dim(held, table[s ^ position], axis=0, keepdims=False)
+        for s in range(size)
+    ]
+    return jnp.concatenate(blocks, axis=1)
 
 
 def scatter_features(partial, axis_name, size, position):
+    width = partial.shape[1] // size
     if not _is_pow2(size):
         summed = lax.psum_scatter(
             partial.astype(jnp.bfloat16), axis_name, scatter_dimension=1, tiled=True
         )
-        return summed[:, 0, :].astype(jnp.float32)
-    held = _xor_reorder(partial, position, size)
+        return summed.astype(jnp.float32)
+    held = [
+        lax.dynamic_slice_in_dim(partial, (position ^ m) * width, width, axis=1)
+        for m in range(size)
+    ]
     masks = list(range(size))
     bit = 1
     while bit < size:
         keep = [i for i, m in enumerate(masks) if not m & bit]
         send = [i for i, m in enumerate(masks) if m & bit]
-        outgoing = held[:, send, :].astype(jnp.bfloat16)
+        outgoing = jnp.stack([held[i] for i in send]).astype(jnp.bfloat16)
         incoming = lax.ppermute(outgoing, axis_name, _xor_pairs(size, bit))
         sent_masks = [masks[i] ^ bit for i in send]
-        order = [sent_masks.index(masks[i]) for i in keep]
-        held = held[:, keep, :] + incoming[:, order, :].astype(jnp.float32)
+        held = [
+            held[i] + incoming[sent_masks.index(masks[i])].astype(jnp.float32) for i in keep
+        ]
         masks = [masks[i] for i in keep]
         bit <<= 1
-    return held[:, 0, :]
+    return held[0]
 
 
 def sum_over(values, axis_name, size):
@@ -157,9 +156,7 @@
         .reshape(token_row_count, width_part)
     )
 
-    gathered = gather_features(tokens, "tensor", tensor_size, tensor_index).reshape(
-        token_row_count, full_width
-    )
+    gathered = gather_features(tokens, "tensor", tensor_size, tensor_index)
     gathered_float = gathered.astype(jnp.float32)
     inverse = lax.rsqrt(jnp.mean(gathered_float * gathered_float, axis=1) + NORM_EPSILON)
     normed_input = (gathered_float * inverse[:, None] * norm_gain[None, :]).astype(jnp.bfloat16)
@@ -191,9 +188,7 @@
         "kgqs,skd->qkgd", probs_low, value_rows, preferred_element_type=jnp.float32
     ).astype(jnp.bfloat16)
     attended_flat = attended.reshape(token_row_count, query_width)
-    mixed_partial = jnp.dot(attended_flat, w_out, preferred_element_type=jnp.float32).reshape(
-        token_row_count, tensor_size, width_part
-    )
+    mixed_partial = jnp.dot(attended_flat, w_out, preferred_element_type=jnp.float32)
     mixed = scatter_features(mixed_partial, "tensor", tensor_size, tensor_index)
     output_home = (x_float + mixed).astype(jnp.bfloat16)
     home_blocks = output_home.reshape(block_count, -1)
@@ -204,9 +199,7 @@
         token_row_count, width_part
     )
 
-    grad_full = gather_features(grad_home, "tensor", tensor_size, tensor_index).reshape(
-        token_row_count, full_width
-    )
+    grad_full = gather_features(grad_home, "tensor", tensor_size, tensor_index)
     attended_gradient = lax.dot_general(
         grad_full,
         w_out,
@@ -262,7 +255,7 @@
     stat_partial = jnp.sum(normed_partial * norm_gain[None, :] * gathered_float, axis=1)
     stat = sum_over(stat_partial, "tensor", tensor_size) / full_width
     normed_gradient = scatter_features(
-        normed_partial.reshape(token_row_count, tensor_size, width_part),
+        normed_partial,
         "tensor",
         tensor_size,
         tensor_index,

time: 342 us -> 180 us (0.53); the launches traced: 335 us -> 179 us
  local copies, waits for them, and re-layouts: 151 us -> 34.8 us
  other arithmetic: 78.2 us -> 32.2 us
  between operations: 1.42 us -> 8.92 us
  matrix products: 44.5 us -> 37.5 us
  waiting for transfers between devices: 27.9 us -> 31.4 us
    gather x16 -> x0, local copies, waits for them, and re-layouts: 64.3 us -> none  [the longest x8 35 us: _xor_reorder(): swapped = stack[:, [m ^ bit for m in range(size)], :]]
    select_n x7 -> x0, other arithmetic: 37 us -> none  [the longest x6 37 us: _xor_reorder(): stack = jnp.where(position & bit != 0, swapped, stack)]
    dot_general x3 -> x0, local copies, waits for them, and re-layouts: 27.5 us -> none  [the longest x1 12.1 us: per_device(): jnp.dot(attended_flat, w_out, preferred_element_type=jnp.float32)]
    convert_element_type x3 -> x0, local copies, waits for them, and re-layouts: 15.1 us -> none  [the longest x2 11.2 us: per_device(): gathered_float = gathered.astype(jnp.float32)]
    all_to_all x1, waiting for transfers between devices: 0.01 us -> 12.2 us  [per_device(): lax.all_to_all(owned_blocks, 'dp', split_axis=0, concat_axis=0, tiled=True)]
    ppermute x4, waiting for transfers between devices: 12.9 us -> 0.87 us  [gather_features(): incoming = lax.ppermute(held, axis_name, _xor_pairs(size, bit))]
    concatenate x4 -> x3, other arithmetic: 9.88 us -> 3.99 us  [gather_features(): held = jnp.concatenate([held, incoming], axis=0)]
    reshape x1 -> x0, local copies, waits for them, and re-layouts: 5.8 us -> none  [per_device(): normed_partial.reshape(token_row_count, tensor_size, width_part)]
  transfers between devices with their start and end apart: 11 -> 11, of which waited for: 3 -> 4; matrix products, arithmetic and copies ran while one was open for 43% -> 12% of each run, Pallas kernels for 0% -> 0%
where the time goes in v2:
time: 180 us; the launch traced here: 179 us
  matrix products  37.5 us (21%)
  local copies, waits for them, and re-layouts  34.8 us (19%)
  other arithmetic  32.2 us (18%)
  waiting for transfers between devices  31.4 us (17%)
  blocking collectives  18.8 us (10%)
  starting transfers between devices  15.1 us (8%)
  between operations  8.92 us (5%)
    unnamed x71, local copies, waits for them, and re-layouts  19.9 us
    all_to_all x1, blocking collectives, per_device(): lax.all_to_all(outgoing, 'dp', split_axis=0, concat_axis=0, tiled=True)  18.8 us
    ppermute x2, waiting for transfers between devices, sum_over(): values = values + lax.ppermute(values, axis_name, _xor_pairs(size, bit))  18.4 us
    all_to_all x1, waiting for transfers between devices, per_device(): lax.all_to_all(owned_blocks, 'dp', split_axis=0, concat_axis=0, tiled=True)  12.2 us
    dot_general x1, matrix products, per_device(): lax.dot_general(grad_query.reshape(token_row_count, query_width), w_query...  7.72 us
    all_to_all x1, starting transfers between devices, per_device(): lax.all_to_all(owned_blocks, 'dp', split_axis=0, concat_axis=0, tiled=True)  7.25 us
    all_to_all x2, other arithmetic, per_device(): lax.all_to_all(outgoing, 'dp', split_axis=0, concat_axis=0, tiled=True)  6.32 us
    dot_general x1, matrix products, per_device(): jnp.dot(normed_input, w_query, preferred_element_type=jnp.float32)  5.79 us
  transfers between devices with their start and end apart: 11, of which 4 were waited for; matrix products, arithmetic and copies ran while one was open for 12% of the time, Pallas kernels for 0%

profile of v2, /device:TPU:0, one launch (start us, length us, event | category | flops | bytes accessed | tf_op | source)
XLA Modules:
  0.0 178.7 jit_solution(4336995020422479660)
XLA Ops:
  0.6 3.6 %all_to_all.19 = bf16[8,1,32768]{2,1,0:T(2,128)(2,1)} reshape(bf16[256,1024]{1,0:T(8,128)(2,1)} %param.17) | data formatting | bytes 1048576 | tf_op jit(solution)/shard_map/all_to_all | solution.py:150
  4.7 4.9 %reduce.1 = bf16[8,32768]{1,0:T(8,128)(2,1)S(1)} reduce(bf16[8,1,32768]{2,1,0:T(2,128)(2,1)} %all_to_all.19, bf16[]{:T(256)} %broadcast.101), dimensions={1}, to_apply=%all_to_all.19.reduce_sub_computation | reduce | bytes 1048578 | tf_op jit(solution)/shard_map/all_to_all | solution.py:150
  9.6 1.2 reshape.230
  10.8 7.3 %all-to-all-start.1 = ((bf16[8,2,16384]{2,1,0:T(2,128)(2,1)}), bf16[8,2,16384]{2,1,0:T(2,128)(2,1)S(1)}, u32[]{:S(2)}, u32[]{:S(2)}) async-start(bf16[8,2,16384]{2,1,0:T(2,128)(2,1)} %reshape.230), calls=%async_computation.1 | async-start | bytes 1048576 | tf_op jit(solution)/shard_map/all_to_all | solution.py:150
  18.1 1.6 collective-permute-start
  19.7 0.7 fusion.50
  20.4 12.2 %all-to-all-done.1 = bf16[8,2,16384]{2,1,0:T(2,128)(2,1)S(1)} async-done(((bf16[8,2,16384]{2,1,0:T(2,128)(2,1)}), bf16[8,2,16384]{2,1,0:T(2,128)(2,1)S(1)}, u32[]{:S(2)}, u32[]{:S(2)}) %all-to-all-start.1) | async-done | bytes 524320 | tf_op jit(solution)/shard_map/all_to_all | solution.py:150
  32.6 1.8 %reshape.231 = bf16[8,1,32768]{2,1,0:T(2,128)(2,1)} reshape(bf16[8,2,16384]{2,1,0:T(2,128)(2,1)S(1)} %all-to-all-done.1) | data formatting | bytes 1048576
  34.4 1.9 %convolution_convert_fusion = bf16[8,32768]{1,0:T(8,128)(2,1)S(1)} fusion(bf16[8,1,32768]{2,1,0:T(2,128)(2,1)} %reshape.231, s32[8]{0:T(128)S(1)} %fusion.50), kind=kOutput, calls=%fused_computation | convolution fusion | flops 4456512 | bytes 1048608 | tf_op jit(solution)/shard_map/dot_general | solution.py:152
  36.5 1.6 collective-permute-start.4
  38.1 0.7 fusion.63
  46.8 1.3 pad_maximum_fusion.2
  48.1 0.9 collective-permute-done.4
  49.0 1.1 pad_maximum_fusion.4
  50.2 0.7 fusion.44
  51.0 0.5 multiply_cosine_fusion
  51.5 1.1 constant_dynamic-update-slice_fusion.1
  52.6 1.6 pad_maximum_fusion
  54.3 0.6 dynamic-slice_bitcast_fusion.3
  55.0 0.8 copy-done.5
  56.3 1.2 slice-done.1
  57.5 3.2 %fusion.17 = bf16[256,1024]{1,0:T(8,128)(2,1)} fusion(bf16[1024,4096]{1,0:T(8,128)(2,1)S(1)} %bitcast.165, bf16[256,1024]{1,0:T(8,128)(2,1)S(1)} %get-tuple-element.11, bf16[256,1024]{1,0:T(8,128)(2,1)S(1)} %get-tuple-element.12, bf16[256,1024]{1,0:T(8,128)(2,1)S(1)} %get-tuple-element.13, bf16[256,1024]{1,0:T(8,128)(2,1)S(1)} %get-tuple-element.10), kind=kOutput, calls=%fused_computation.32 | convolution fusion | flops 2156134400 | bytes 11010048 | tf_op jit(solution)/shard_map/dot_general | solution.py:203
  60.6 2.0 %copy.90 = bf16[256,1024]{0,1:T(8,128)(2,1)} copy(bf16[256,1024]{1,0:T(8,128)(2,1)} %fusion.17) | data formatting | bytes 1048576 | tf_op jit(solution)/shard_map/convert_element_type | solution.py:208
  62.7 3.3 %convolution_convert_fusion.3 = bf16[256,256]{0,1:T(8,128)(2,1)} fusion(bf16[4096,256]{1,0:T(8,128)(2,1)S(1)} %copy-done, f32[4096]{0:T(1024)S(1)} %copy-done.22, f32[256]{0:T(256)S(1)} %get-tuple-element.33, bf16[256,1024]{1,0:T(8,128)(2,1)} %copy-done.8, bf16[256,1024]{1,0:T(8,128)(2,1)} %copy-done.5, bf16[256,1024]{1,0:T(8,128)(2,1)S(1)} %get-tuple-element.44, ...), kind=kOutput, calls=%fused_computation.39 | convolution fusion | flops 548470784 | bytes 4342784 | tf_op jit(solution)/shard_map/dot_general | solution.py:165
  66.0 5.8 %convolution_bitcast_fusion = f32[32,8,8,128]{3,1,2,0:T(8,128)S(1)} fusion(bf16[4096,1024]{1,0:T(8,128)(2,1)} %param.13, f32[4096]{0:T(1024)S(1)} %copy-done.22, f32[256]{0:T(256)S(1)} %get-tuple-element.33, bf16[256,1024]{1,0:T(8,128)(2,1)S(1)} %copy-done.9, bf16[256,1024]{1,0:T(8,128)(2,1)S(1)} %copy-done.6, bf16[256,1024]{1,0:T(8,128)(2,1)S(1)} %get-tuple-element.44, ...), kind=kOutput, calls=%fused_computation.29 | convolution fusion | flops 2159017984 | bytes 11551744 | tf_op jit(solution)/shard_map/dot_general | solution.py:163
  72.5 0.9 copy.86
  73.4 0.9 copy.85
  74.3 1.1 fusion.56
  75.4 0.7 fusion.62
  76.1 1.8 copy.121
  77.9 0.8 copy.120
  78.7 1.2 subtract_convert_fusion.3
  79.9 2.1 %fusion.16 = (f32[2,4,256]{2,1,0:T(4,128)S(1)}, f32[2,256,256,4]{2,1,3,0:T(8,128)S(1)}) fusion(pred[256,256]{0,1:T(8,128)(4,1)} %fusion.44, bf16[256,2,4,64]{3,0,2,1:T(8,128)(2,1)S(1)} %bitcast.170, bf16[256,2,4,64]{3,0,2,1:T(8,128)(2,1)} %bitcast.172, bf16[256,2,64]{2,0,1:T(8,128)(2,1)S(1)} %get-tuple-element.23, bf16[256,2,64]{2,0,1:T(8,128)(2,1)S(1)} %get-tuple-element.22), kind=kOutput, calls=%fused_computation.27 | convolution fusion | flops 137099264 | bytes 2826240 | tf_op jit(solution)/shard_map/qkgd,skd->kgqs/dot_general | solution.py:181
  82.1 1.5 multiply_reduce_fusion
  83.5 0.8 fusion.14
  84.7 0.6 copy-done.15
  86.0 0.7 fusion.22
  86.7 1.1 fusion.61
  87.8 2.4 %copy.123 = f32[256,8,64]{2,1,0:T(8,128)} copy(f32[256,8,64]{0,2,1:T(8,128)} %get-tuple-element.20) | data formatting | bytes 1048576
  90.2 2.4 %copy.122 = f32[256,8,64]{2,1,0:T(8,128)} copy(f32[256,8,64]{0,2,1:T(8,128)} %get-tuple-element.21) | data formatting | bytes 1048576
  92.5 1.8 %add_convert_fusion = (bf16[256,8,64]{2,1,0:T(8,128)(2,1)S(1)}, bf16[256,8,64]{2,1,0:T(8,128)(2,1)S(1)}) fusion(f32[256,8,64]{2,1,0:T(8,128)} %copy.123, f32[256,8,64]{2,1,0:T(8,128)} %copy.122, f32[256,64]{1,0:T(8,128)S(1)} %get-tuple-element.31, f32[256,64]{1,0:T(8,128)S(1)} %get-tuple-element.30), kind=kLoop, calls=%fused_computation.61 | loop fusion | flops 1048576 | bytes 1703936 | tf_op jit(solution)/shard_map/convert.13
  94.7 7.7 %fusion.37 = f32[256,4096]{1,0:T(8,128)} fusion(bf16[4096,1024]{1,0:T(8,128)(2,1)} %param.13, bf16[32,8,8,128]{3,2,1,0:T(8,128)(2,1)S(1)} %bitcast.175), kind=kOutput, calls=%fused_computation.73 | convolution fusion | flops 2147483648 | bytes 13107200 | tf_op jit(solution)/shard_map/dot_general | solution.py:236
  102.8 3.7 %convolution_add_fusion.1 = f32[256,4096]{1,0:T(8,128)S(1)} fusion(f32[256,4096]{1,0:T(8,128)} %fusion.37, bf16[256,256]{0,1:T(8,128)(2,1)S(1)} %bitcast.178, bf16[4096,256]{1,0:T(8,128)(2,1)} %param.14), kind=kOutput, calls=%fused_computation.7 | convolution fusion | flops 537919488 | bytes 10616832 | tf_op jit(solution)/shard_map/dot_general | solution.py:242
  106.6 1.3 fusion.4
  108.1 1.1 pad_maximum_fusion.5
  109.2 1.4 copy-done.2
  111.0 0.9 slice-done.3
  112.1 2.5 %fusion.64 = f32[256,4096]{1,0:T(8,128)S(1)} fusion(bf16[256,1024]{0,1:T(8,128)(2,1)S(1)} %bitcast.174, bf16[1024,4096]{1,0:T(8,128)(2,1)S(1)} %bitcast.167), kind=kOutput, calls=%fused_computation.130 | convolution fusion | flops 2147483648 | bytes 13107200 | tf_op jit(solution)/shard_map/dot_general | solution.py:191
  114.8 1.3 pad_maximum_fusion.3
  116.2 0.8 copy-done.1
  117.5 2.3 %fusion.36 = bf16[1,256,1024]{2,1,0:T(8,128)(2,1)} fusion(f32[256,4096]{1,0:T(8,128)} %copy-done.2, s32[]{:T(128)S(6)} %select_n.83, bf16[2,256,1024]{2,1,0:T(8,128)(2,1)} %collective-permute-done.6), kind=kLoop, calls=%fused_computation.72 | loop fusion | flops 786432 | bytes 2097156 | tf_op jit(solution)/shard_map/convert_element_type | solution.py:97
  119.8 1.5 collective-permute-start.7
  121.3 2.3 %fusion.35 = bf16[1,256,1024]{2,1,0:T(8,128)(2,1)} fusion(f32[256,4096]{1,0:T(8,128)} %copy-done.1, s32[]{:T(128)S(6)} %select_n.83, bf16[2,256,1024]{2,1,0:T(8,128)(2,1)} %collective-permute-done.2), kind=kLoop, calls=%fused_computation.71 | loop fusion | flops 786432 | bytes 2097156 | tf_op jit(solution)/shard_map/convert_element_type | solution.py:97
  124.1 1.1 collective-permute-done.8
  125.2 1.5 collective-permute-start.9
  126.8 1.2 reshape.217
  128.0 17.2 %collective-permute-done.9 = f32[256]{0:T(256)S(1)} collective-permute-done((f32[256]{0:T(256)S(1)}, f32[256]{0:T(256)S(1)}, u32[]{:S(2)}, u32[]{:S(2)}) %collective-permute-start.9) | collective-permute-done | bytes 1056 | tf_op jit(solution)/shard_map/ppermute | solution.py:113
  145.2 3.9 %fusion.26 = (bf16[256,1024]{1,0:T(8,128)(2,1)}, bf16[256,1024]{1,0:T(8,128)(2,1)S(1)}) fusion(bf16[256,1024]{1,0:T(8,128)(2,1)} %param.11, f32[256,1024]{1,0:T(8,128)} %reshape.217, f32[256,4096]{1,0:T(8,128)} %copy-done.2, s32[]{:T(128)S(6)} %select_n.80, bf16[2,256,1024]{2,1,0:T(8,128)(2,1)} %collective-permute-done.6, ...), kind=kLoop, calls=%fused_computation.43 | loop fusion | flops 4718592 | bytes 6822916 | tf_op jit(solution)/shard_map/convert_element_type | solution.py:269
  149.3 1.1 fusion
  150.4 2.0 %reduce.2 = bf16[8,32768]{1,0:T(8,128)(2,1)S(1)} reduce(bf16[8,1,32768]{2,0,1:T(8,128)(2,1)} %fusion, bf16[]{:T(256)} %broadcast.101), dimensions={1}, to_apply=%copy.88.reduce_sub_computation | reduce | bytes 1048578 | tf_op jit(solution)/shard_map/all_to_all | solution.py:198
  152.8 18.8 %all_to_all.22 = bf16[8,2,16384]{2,1,0:T(2,128)(2,1)S(1)} all-to-all(bf16[8,2,16384]{2,1,0:T(2,128)(2,1)S(1)} %reshape.228), channel_id=1, replica_groups=mesh['dp'=8,'tensor'=4] {'dp'}, dimensions={0} | all-to-all | bytes 1048576 | tf_op jit(solution)/shard_map/all_to_all | solution.py:198
  171.6 1.8 %reshape.229 = bf16[8,1,32768]{2,1,0:T(2,128)(2,1)} reshape(bf16[8,2,16384]{2,1,0:T(2,128)(2,1)S(1)} %all_to_all.22) | data formatting | bytes 1048576
  173.4 4.3 %reduce = bf16[8,32768]{1,0:T(8,128)(2,1)S(1)} reduce(bf16[8,1,32768]{2,1,0:T(2,128)(2,1)} %reshape.229, bf16[]{:T(256)} %constant.72), dimensions={1}, to_apply=%all_to_all.15.reduce_sub_computation | reduce | bytes 1048578 | tf_op jit(solution)/shard_map/all_to_all | solution.py:198
  177.7 1.0 reshape.210
  (94 shorter events, 7.1 us)
Async XLA Ops:
  0.6 62.0 %copy-start = (bf16[4096,256]{1,0:T(8,128)(2,1)S(1)}, bf16[4096,256]{1,0:T(8,128)(2,1)}, u32[]{:S(2)}) copy-start(bf16[4096,256]{1,0:T(8,128)(2,1)} %param.15) | copy-start | bytes 6291460
  10.8 21.7 %all-to-all-start.1 = ((bf16[8,2,16384]{2,1,0:T(2,128)(2,1)}), bf16[8,2,16384]{2,1,0:T(2,128)(2,1)S(1)}, u32[]{:S(2)}, u32[]{:S(2)}) async-start(bf16[8,2,16384]{2,1,0:T(2,128)(2,1)} %reshape.230), calls=%async_computation.1 | async-start | bytes 1048576 | tf_op jit(solution)/shard_map/all_to_all | solution.py:150
  18.1 20.0 %copy-start.21 = (s32[4]{0:T(128)S(1)}, s32[4]{0:T(128)}, u32[]{:S(2)}) copy-start(s32[4]{0:T(128)} %constant.70.clone) | copy-start | bytes 52
  18.1 25.8 %copy-start.24 = (s32[1,2]{1,0:T(1,128)S(1)}, s32[1,2]{1,0:T(1,128)}, u32[]{:S(2)}) copy-start(s32[1,2]{1,0:T(1,128)} %param.18) | copy-start | bytes 28
  18.1 28.7 %collective-permute-start = (bf16[1,256,1024]{2,1,0:T(8,128)(2,1)}, bf16[1,256,1024]{2,1,0:T(8,128)(2,1)}, u32[]{:S(2)}, u32[]{:S(2)}) collective-permute-start(bf16[1,256,1024]{2,1,0:T(8,128)(2,1)} %bitcast.1), channel_id=1, source_target_pairs={{0,2},{1,3},{2,0},{3,1},{4,6},{5,7},{6,4},{7,5},{8,10},{9,11},{10,... | collective-permute-start | bytes 1572872 | tf_op jit(solution)/shard_map/ppermute | solution.py:69
  36.5 12.5 %collective-permute-start.4 = (bf16[1,256,1024]{2,1,0:T(8,128)(2,1)S(1)}, bf16[1,256,1024]{2,1,0:T(8,128)(2,1)}, u32[]{:S(2)}, u32[]{:S(2)}) collective-permute-start(bf16[1,256,1024]{2,1,0:T(8,128)(2,1)S(1)} %broadcast_in_dim_reshape.3), channel_id=1, source_target_pairs={{0,2},{1,3},{2,0},{3,1},{4,6},{5,7},{6,4},{7,5},{8,10},{9,11},{10,... | collective-permute-start | bytes 1572872 | tf_op jit(solution)/shard_map/ppermute | solution.py:69
  48.1 4.6 %collective-permute-start.1 = (bf16[2,256,1024]{2,1,0:T(8,128)(2,1)S(1)}, bf16[2,256,1024]{2,1,0:T(8,128)(2,1)S(1)}, u32[]{:S(2)}, u32[]{:S(2)}) collective-permute-start(bf16[2,256,1024]{2,1,0:T(8,128)(2,1)S(1)} %pad_maximum_fusion.2), channel_id=1, source_target_pairs={{0,1},{1,0},{2,3},{3,2},{4,5},{5,4},{6,7},{7,6},{8,9},{9,8},{10,11... | collective-permute-start | bytes 3145736 | tf_op jit(solution)/shard_map/ppermute | solution.py:69
  50.1 4.1 %collective-permute-start.5 = (bf16[2,256,1024]{2,1,0:T(8,128)(2,1)S(1)}, bf16[2,256,1024]{2,1,0:T(8,128)(2,1)S(1)}, u32[]{:S(2)}, u32[]{:S(2)}) collective-permute-start(bf16[2,256,1024]{2,1,0:T(8,128)(2,1)S(1)} %pad_maximum_fusion.4), channel_id=1, source_target_pairs={{0,1},{1,0},{2,3},{3,2},{4,5},{5,4},{6,7},{7,6},{8,9},{9,8},{10,11... | collective-permute-start | bytes 3145736 | tf_op jit(solution)/shard_map/ppermute | solution.py:69
  52.6 3.6 %slice-start = ((s8[8388608]{0:T(1024)(128)(4,1)}), s8[4194304]{0:T(1024)(128)(4,1)S(1)}, s32[]{:S(2)}) async-start(s8[8388608]{0:T(1024)(128)(4,1)} %bitcast.164), calls=%async_computation.2 | async-start | bytes 8388608
  54.3 3.2 %slice-start.1 = ((s8[8388608]{0:T(1024)(128)(4,1)}), s8[4194304]{0:T(1024)(128)(4,1)S(1)}, s32[]{:S(2)}) async-start(s8[8388608]{0:T(1024)(128)(4,1)} %bitcast.164), calls=%async_computation.3 | async-start | bytes 8388608
  54.9 0.8 copy-start.5
  54.9 1.3 copy-start.8
  55.0 1.3 copy-start.11
  55.0 19.3 %copy-start.3 = (bf16[256,1024]{1,0:T(8,128)(2,1)}, bf16[256,1024]{1,0:T(8,128)(2,1)S(1)}, u32[]{:S(2)}) copy-start(bf16[256,1024]{1,0:T(8,128)(2,1)S(1)} %get-tuple-element.44) | copy-start | bytes 1572868
  57.5 5.2 %copy-start.22 = (f32[4096]{0:T(1024)S(1)}, f32[4096]{0:T(1024)}, u32[]{:S(2)}) copy-start(f32[4096]{0:T(1024)} %param.12) | copy-start | bytes 49156
  62.7 3.3 %copy-start.6 = (bf16[256,1024]{1,0:T(8,128)(2,1)S(1)}, bf16[256,1024]{1,0:T(8,128)(2,1)}, u32[]{:S(2)}) copy-start(bf16[256,1024]{1,0:T(8,128)(2,1)} %copy-done.5) | copy-start | bytes 1572868
  62.7 3.3 %copy-start.9 = (bf16[256,1024]{1,0:T(8,128)(2,1)S(1)}, bf16[256,1024]{1,0:T(8,128)(2,1)}, u32[]{:S(2)}) copy-start(bf16[256,1024]{1,0:T(8,128)(2,1)} %copy-done.8) | copy-start | bytes 1572868
  62.7 3.3 %copy-start.12 = (bf16[256,1024]{1,0:T(8,128)(2,1)S(1)}, bf16[256,1024]{1,0:T(8,128)(2,1)}, u32[]{:S(2)}) copy-start(bf16[256,1024]{1,0:T(8,128)(2,1)} %copy-done.11) | copy-start | bytes 1572868
  72.0 2.3 %copy-start.17 = (bf16[4096,256]{1,0:T(8,128)(2,1)S(1)}, bf16[4096,256]{1,0:T(8,128)(2,1)}, u32[]{:S(2)}) copy-start(bf16[4096,256]{1,0:T(8,128)(2,1)} %param.14) | copy-start | bytes 6291460
  75.4 4.5 %copy-start.14 = (bf16[256,8,64]{2,0,1:T(8,128)(2,1)S(1)}, bf16[256,8,64]{2,0,1:T(8,128)(2,1)}, u32[]{:S(2)}) copy-start(bf16[256,8,64]{2,0,1:T(8,128)(2,1)} %copy.86) | copy-start | bytes 786436
  78.7 3.3 %copy-start.19 = (bf16[256,1024]{0,1:T(8,128)(2,1)S(1)}, bf16[256,1024]{0,1:T(8,128)(2,1)}, u32[]{:S(2)}) copy-start(bf16[256,1024]{0,1:T(8,128)(2,1)} %copy.90) | copy-start | bytes 1572868
  78.7 3.3 %copy-start.20 = (pred[256,256]{0,1:T(8,128)(4,1)S(1)}, pred[256,256]{0,1:T(8,128)(4,1)}, u32[]{:S(2)}) copy-start(pred[256,256]{0,1:T(8,128)(4,1)} %fusion.44) | copy-start | bytes 196612
  78.7 3.3 %copy-start.25 = (bf16[256,256]{0,1:T(8,128)(2,1)S(1)}, bf16[256,256]{0,1:T(8,128)(2,1)}, u32[]{:S(2)}) copy-start(bf16[256,256]{0,1:T(8,128)(2,1)} %convolution_convert_fusion.3) | copy-start | bytes 393220
  84.3 1.0 copy-start.15
  84.3 1.2 copy-start.16
  102.8 3.8 %copy-start.4 = (bf16[256,1024]{1,0:T(8,128)(2,1)S(1)}, bf16[256,1024]{1,0:T(8,128)(2,1)}, u32[]{:S(2)}) copy-start(bf16[256,1024]{1,0:T(8,128)(2,1)} %copy-done.3) | copy-start | bytes 1572868
  102.8 3.8 %copy-start.7 = (bf16[256,1024]{1,0:T(8,128)(2,1)S(1)}, bf16[256,1024]{1,0:T(8,128)(2,1)}, u32[]{:S(2)}) copy-start(bf16[256,1024]{1,0:T(8,128)(2,1)} %copy-done.5) | copy-start | bytes 1572868
  102.8 3.8 %copy-start.10 = (bf16[256,1024]{1,0:T(8,128)(2,1)S(1)}, bf16[256,1024]{1,0:T(8,128)(2,1)}, u32[]{:S(2)}) copy-start(bf16[256,1024]{1,0:T(8,128)(2,1)} %copy-done.8) | copy-start | bytes 1572868
  102.8 3.8 %copy-start.13 = (bf16[256,1024]{1,0:T(8,128)(2,1)S(1)}, bf16[256,1024]{1,0:T(8,128)(2,1)}, u32[]{:S(2)}) copy-start(bf16[256,1024]{1,0:T(8,128)(2,1)} %copy-done.11) | copy-start | bytes 1572868
  102.8 3.8 %copy-start.23 = (f32[4096]{0:T(1024)S(1)}, f32[4096]{0:T(1024)}, u32[]{:S(2)}) copy-start(f32[4096]{0:T(1024)} %param.12) | copy-start | bytes 49156
  106.5 4.5 %slice-start.2 = ((s8[8388608]{0:T(1024)(128)(4,1)}), s8[4194304]{0:T(1024)(128)(4,1)S(1)}, s32[]{:S(2)}) async-start(s8[8388608]{0:T(1024)(128)(4,1)} %bitcast.166), calls=%async_computation.4 | async-start | bytes 8388608
  106.6 5.3 %slice-start.3 = ((s8[8388608]{0:T(1024)(128)(4,1)}), s8[4194304]{0:T(1024)(128)(4,1)S(1)}, s32[]{:S(2)}) async-start(s8[8388608]{0:T(1024)(128)(4,1)} %bitcast.166), calls=%async_computation.5 | async-start | bytes 8388608
  107.9 2.6 %copy-start.2 = (f32[256,4096]{1,0:T(8,128)}, f32[256,4096]{1,0:T(8,128)S(1)}, u32[]{:S(2)}) copy-start(f32[256,4096]{1,0:T(8,128)S(1)} %get-tuple-element.43) | copy-start | bytes 12582916
  107.9 4.2 %copy-start.18 = (bf16[2,128,4,256]{3,1,2,0:T(8,128)(2,1)S(1)}, bf16[2,128,4,256]{3,1,2,0:T(8,128)(2,1)}, u32[]{:S(2)}) copy-start(bf16[2,128,4,256]{3,1,2,0:T(8,128)(2,1)} %get-tuple-element.41) | copy-start | bytes 1572868
  110.5 6.9 %collective-permute-start.6 = (bf16[2,256,1024]{2,1,0:T(8,128)(2,1)}, bf16[2,256,1024]{2,1,0:T(8,128)(2,1)}, u32[]{:S(2)}, u32[]{:S(2)}) collective-permute-start(bf16[2,256,1024]{2,1,0:T(8,128)(2,1)} %pad_maximum_fusion.5), channel_id=1, source_target_pairs={{0,1},{1,0},{2,3},{3,2},{4,5},{5,4},{6,7},{7,6},{8,9},{9,8},{10,11... | collective-permute-start | bytes 3145736 | tf_op jit(solution)/shard_map/ppermute | solution.py:98
  114.6 2.3 %copy-start.1 = (f32[256,4096]{1,0:T(8,128)}, f32[256,4096]{1,0:T(8,128)S(1)}, u32[]{:S(2)}) copy-start(f32[256,4096]{1,0:T(8,128)S(1)} %fusion.64) | copy-start | bytes 12582916
  117.0 4.3 %collective-permute-start.2 = (bf16[2,256,1024]{2,1,0:T(8,128)(2,1)}, bf16[2,256,1024]{2,1,0:T(8,128)(2,1)}, u32[]{:S(2)}, u32[]{:S(2)}) collective-permute-start(bf16[2,256,1024]{2,1,0:T(8,128)(2,1)} %pad_maximum_fusion.3), channel_id=1, source_target_pairs={{0,1},{1,0},{2,3},{3,2},{4,5},{5,4},{6,7},{7,6},{8,9},{9,8},{10,11... | collective-permute-start | bytes 3145736 | tf_op jit(solution)/shard_map/ppermute | solution.py:98
  119.8 25.4 %collective-permute-start.7 = (bf16[1,256,1024]{2,1,0:T(8,128)(2,1)}, bf16[1,256,1024]{2,1,0:T(8,128)(2,1)S(1)}, u32[]{:S(2)}, u32[]{:S(2)}) collective-permute-start(bf16[1,256,1024]{2,1,0:T(8,128)(2,1)} %fusion.36), channel_id=1, source_target_pairs={{0,2},{1,3},{2,0},{3,1},{4,6},{5,7},{6,4},{7,5},{8,10},{9,11},{10,... | collective-permute-start | bytes 1572872 | tf_op jit(solution)/shard_map/ppermute | solution.py:98
  123.6 21.6 %collective-permute-start.3 = (bf16[1,256,1024]{2,1,0:T(8,128)(2,1)}, bf16[1,256,1024]{2,1,0:T(8,128)(2,1)}, u32[]{:S(2)}, u32[]{:S(2)}) collective-permute-start(bf16[1,256,1024]{2,1,0:T(8,128)(2,1)} %fusion.35), channel_id=1, source_target_pairs={{0,2},{1,3},{2,0},{3,1},{4,6},{5,7},{6,4},{7,5},{8,10},{9,11},{10,... | collective-permute-start | bytes 1572872 | tf_op jit(solution)/shard_map/ppermute | solution.py:98
  124.1 1.1 collective-permute-start.8
  125.2 19.9 %collective-permute-start.9 = (f32[256]{0:T(256)S(1)}, f32[256]{0:T(256)S(1)}, u32[]{:S(2)}, u32[]{:S(2)}) collective-permute-start(f32[256]{0:T(256)S(1)} %add.155), channel_id=1, source_target_pairs={{0,2},{1,3},{2,0},{3,1},{4,6},{5,7},{6,4},{7,5},{8,10},{9,11},{10,... | collective-permute-start | bytes 3080 | tf_op jit(solution)/shard_map/ppermute | solution.py:113

commit v3 on v2

--- a/solution.py
+++ b/solution.py
@@ -146,15 +146,37 @@
     slot_index = jnp.arange(sources, dtype=jnp.int32)
     send_table = (owner_row[None, :] == slot_index[:, None]).astype(jnp.bfloat16)
 
-    owned_blocks = grad_output.reshape(block_count, -1)
-    arrived = lax.all_to_all(owned_blocks, "dp", split_axis=0, concat_axis=0, tiled=True)
-    grad_home = (
-        lax.dot_general(
-            send_table, arrived, (((0,), (0,)), ((), ())), preferred_element_type=jnp.float32
-        )
-        .astype(jnp.bfloat16)
-        .reshape(token_row_count, width_part)
-    )
+    home_rows = token_row_count // block_count
+    owned_blocks = grad_output.reshape(block_count, home_rows, width_part)
+    if sources <= 16:
+        returned = [lax.dynamic_index_in_dim(owned_blocks, data_index, 0, keepdims=False)]
+        for shift in range(1, sources):
+            pairs = [(a, (a + shift) % sources) for a in range(sources)]
+            piece = lax.dynamic_index_in_dim(
+                owned_blocks, (data_index + shift) % sources, 0, keepdims=False
+            )
+            returned.append(lax.ppermute(piece, "dp", pairs))
+        returned = jnp.stack(returned)
+        grad_home = jnp.concatenate(
+            [
+                lax.dynamic_index_in_dim(
+                    returned, (data_index - owner_row[j]) % sources, 0, keepdims=False
+                )
+                for j in range(block_count)
+            ],
+            axis=0,
+        )
+    else:
+        arrived = lax.all_to_all(
+            owned_blocks.reshape(block_count, -1), "dp", split_axis=0, concat_axis=0, tiled=True
+        )
+        grad_home = (
+            lax.dot_general(
+                send_table, arrived, (((0,), (0,)), ((), ())), preferred_element_type=jnp.float32
+            )
+            .astype(jnp.bfloat16)
+            .reshape(token_row_count, width_part)
+        )
 
     gathered = gather_features(tokens, "tensor", tensor_size, tensor_index)
     gathered_float = gathered.astype(jnp.float32)
@@ -191,13 +213,37 @@
     mixed_partial = jnp.dot(attended_flat, w_out, preferred_element_type=jnp.float32)
     mixed = scatter_features(mixed_partial, "tensor", tensor_size, tensor_index)
     output_home = (x_float + mixed).astype(jnp.bfloat16)
-    home_blocks = output_home.reshape(block_count, -1)
-    outgoing = jnp.dot(send_table, home_blocks, preferred_element_type=jnp.float32).astype(
-        jnp.bfloat16
-    )
-    relaid = lax.all_to_all(outgoing, "dp", split_axis=0, concat_axis=0, tiled=True).reshape(
-        token_row_count, width_part
-    )
+    home_blocks = output_home.reshape(block_count, home_rows, width_part)
+    if sources <= 16:
+        block_for = jnp.sum(
+            jnp.where(send_table > 0, jnp.arange(block_count, dtype=jnp.int32)[None, :], 0), axis=1
+        )
+        landed = [
+            lax.dynamic_index_in_dim(home_blocks, block_for[data_index], 0, keepdims=False)
+        ]
+        for shift in range(1, sources):
+            pairs = [(a, (a + shift) % sources) for a in range(sources)]
+            piece = lax.dynamic_index_in_dim(
+                home_blocks, block_for[(data_index + shift) % sources], 0, keepdims=False
+            )
+            landed.append(lax.ppermute(piece, "dp", pairs))
+        landed = jnp.stack(landed)
+        relaid = jnp.concatenate(
+            [
+                lax.dynamic_index_in_dim(
+                    landed, (data_index - b) % sources, 0, keepdims=False
+                )
+                for b in range(sources)
+            ],
+            axis=0,
+        )
+    else:
+        outgoing = jnp.dot(
+            send_table, home_blocks.reshape(block_count, -1), preferred_element_type=jnp.float32
+        ).astype(jnp.bfloat16)
+        relaid = lax.all_to_all(outgoing, "dp", split_axis=0, concat_axis=0, tiled=True).reshape(
+            token_row_count, width_part
+        )
 
     grad_full = gather_features(grad_home, "tensor", tensor_size, tensor_index)
     attended_gradient = lax.dot_general(

time: 180 us -> 166 us (0.922)
  waiting for transfers between devices: 31.4 us -> 8.2 us
  between operations: 8.92 us -> 29.5 us
  blocking collectives: 18.8 us -> 0 us
  starting transfers between devices: 15.1 us -> 30.5 us
  other arithmetic: 32.2 us -> 21.9 us
  local copies, waits for them, and re-layouts: 34.8 us -> 38.4 us
    ppermute x0 -> x14, starting transfers between devices: none -> 23.5 us  [the longest x7 13.8 us: per_device(): returned.append(lax.ppermute(piece, 'dp', pairs))]
    all_to_all x1 -> x0, blocking collectives: 18.8 us -> none  [per_device(): lax.all_to_all(outgoing, 'dp', split_axis=0, concat_axis=0, tiled=True)]
    ppermute x2, waiting for transfers between devices: 18.4 us -> 2.89 us  [sum_over(): values = values + lax.ppermute(values, axis_name, _xor_pairs(size, bit))]
    all_to_all x1 -> x0, waiting for transfers between devices: 12.2 us -> none  [per_device(): lax.all_to_all(owned_blocks, 'dp', split_axis=0, concat_axis=0, tiled=True)]
    all_to_all x3 -> x0, other arithmetic: 11.2 us -> none  [the longest x2 6.32 us: per_device(): lax.all_to_all(outgoing, 'dp', split_axis=0, concat_axis=0, tiled=True)]
    all_to_all x1 -> x0, starting transfers between devices: 7.25 us -> none  [per_device(): lax.all_to_all(owned_blocks, 'dp', split_axis=0, concat_axis=0, tiled=True)]
    unnamed x71 -> x101, local copies, waits for them, and re-layouts: 19.9 us -> 25 us
    ppermute x0 -> x14, waiting for transfers between devices: none -> 4.39 us  [the longest x7 4.37 us: per_device(): landed.append(lax.ppermute(piece, 'dp', pairs))]
  transfers between devices with their start and end apart: 11 -> 24, of which waited for: 4 -> 6; matrix products, arithmetic and copies ran while one was open for 12% -> 18% of each run, Pallas kernels for 0% -> 0%
where the time goes in v3:
time: 166 us; the launch traced here: 164 us
  local copies, waits for them, and re-layouts  38.4 us (23%)
  matrix products  35.7 us (22%)
  starting transfers between devices  30.5 us (18%)
  between operations  29.5 us (18%)
  other arithmetic  21.9 us (13%)
  waiting for transfers between devices  8.2 us (5%)
    unnamed x101, local copies, waits for them, and re-layouts  25 us
    ppermute x7, starting transfers between devices, per_device(): returned.append(lax.ppermute(piece, 'dp', pairs))  13.8 us
    ppermute x7, starting transfers between devices, per_device(): landed.append(lax.ppermute(piece, 'dp', pairs))  9.72 us
    dot_general x1, matrix products, per_device(): lax.dot_general(grad_query.reshape(token_row_count, query_width), w_query...  7.8 us
    dot_general x1, matrix products, per_device(): jnp.dot(normed_input, w_query, preferred_element_type=jnp.float32)  5.81 us
    concatenate x4, other arithmetic, gather_features(): held = jnp.concatenate([held, incoming], axis=0)  5.07 us
    convert_element_type x2, other arithmetic, scatter_features(): outgoing = jnp.stack([held[i] for i in send]).astype(jnp.bfloat16)  4.61 us
    ppermute x7, waiting for transfers between devices, per_device(): landed.append(lax.ppermute(piece, 'dp', pairs))  4.37 us
  transfers between devices with their start and end apart: 24, of which 6 were waited for; matrix products, arithmetic and copies ran while one was open for 18% of the time, Pallas kernels for 0%

profile of v3, /device:TPU:0, one launch (start us, length us, event | category | flops | bytes accessed | tf_op | source)
XLA Modules:
  0.0 164.2 jit_solution(6111623210287501206)
XLA Ops:
  0.8 1.9 %dynamic-slice_bitcast_fusion.8 = (bf16[32,1024]{1,0:T(8,128)(2,1)S(1)}, bf16[32,1024]{1,0:T(8,128)(2,1)S(1)}, bf16[32,1024]{1,0:T(8,128)(2,1)S(1)}, bf16[32,102...) fusion(bf16[8,32,1024]{2,1,0:T(8,128)(2,1)} %bitcast.284, ...), kind=kLoop, calls=%fused_computation.133 | loop fusion | bytes 1048608 | tf_op jit(solution)/shard_map/jit(dynamic_index_in_dim)/squeeze | solution.py:155
  2.7 2.9 %collective-permute-start.11 = (bf16[32,1024]{1,0:T(8,128)(2,1)S(1)}, bf16[32,1024]{1,0:T(8,128)(2,1)S(1)}, u32[]{:S(2)}, u32[]{:S(2)}) collective-permute-start(bf16[32,1024]{1,0:T(8,128)(2,1)S(1)} %get-tuple-element.34), channel_id=1, source_target_pairs={{0,4},{4,8},{8,12},{12,16},{16,20},{20,24},{24,28},{28,0},{1,5},{5... | collective-permute-start | bytes 196616 | tf_op jit(solution)/shard_map/ppermute | solution.py:158
  5.6 1.6 collective-permute-start.12
  7.2 2.6 %collective-permute-start.13 = (bf16[32,1024]{1,0:T(8,128)(2,1)S(1)}, bf16[32,1024]{1,0:T(8,128)(2,1)S(1)}, u32[]{:S(2)}, u32[]{:S(2)}) collective-permute-start(bf16[32,1024]{1,0:T(8,128)(2,1)S(1)} %get-tuple-element.32), channel_id=1, source_target_pairs={{0,12},{4,16},{8,20},{12,24},{16,28},{20,0},{24,4},{28,8},{1,13},{... | collective-permute-start | bytes 196616 | tf_op jit(solution)/shard_map/ppermute | solution.py:158
  9.8 1.2 collective-permute-start.14
  11.0 2.6 %collective-permute-start.15 = (bf16[32,1024]{1,0:T(8,128)(2,1)S(1)}, bf16[32,1024]{1,0:T(8,128)(2,1)S(1)}, u32[]{:S(2)}, u32[]{:S(2)}) collective-permute-start(bf16[32,1024]{1,0:T(8,128)(2,1)S(1)} %get-tuple-element.30), channel_id=1, source_target_pairs={{0,20},{4,24},{8,28},{12,0},{16,4},{20,8},{24,12},{28,16},{1,21},{... | collective-permute-start | bytes 196616 | tf_op jit(solution)/shard_map/ppermute | solution.py:158
  20.2 1.4 collective-permute-start.16
  22.2 1.4 collective-permute-start.17
  24.3 1.5 collective-permute-start
  29.0 0.8 constant_dynamic-update-slice_fusion.31
  29.8 0.8 constant_dynamic-update-slice_fusion.30
  30.7 0.8 constant_dynamic-update-slice_fusion.29
  31.5 0.8 constant_dynamic-update-slice_fusion.28
  32.4 0.8 constant_dynamic-update-slice_fusion.27
  33.2 0.8 constant_dynamic-update-slice_fusion.26
  34.0 0.8 constant_dynamic-update-slice_fusion.25
  34.9 0.8 constant_dynamic-update-slice_fusion.24
  36.5 0.8 copy-done.20
  37.3 1.1 pad_maximum_fusion.3
  47.5 1.1 pad_maximum_fusion.5
  50.1 1.6 pad_maximum_fusion
  51.7 1.2 pad_maximum_fusion.2
  53.6 0.8 copy-done.5
  54.9 1.1 slice-done.1
  55.9 3.2 %fusion.16 = bf16[256,1024]{1,0:T(8,128)(2,1)} fusion(bf16[1024,4096]{1,0:T(8,128)(2,1)S(1)} %bitcast.266, bf16[256,1024]{1,0:T(8,128)(2,1)S(1)} %get-tuple-element.11, bf16[256,1024]{1,0:T(8,128)(2,1)S(1)} %get-tuple-element.12, bf16[256,1024]{1,0:T(8,128)(2,1)S(1)} %get-tuple-element.13, bf16[256,1024]{1,0:T(8,128)(2,1)S(1)} %get-tuple-element.10), kind=kOutput, calls=%fused_computation.30 | convolution fusion | flops 2156134400 | bytes 11010048 | tf_op jit(solution)/shard_map/dot_general | solution.py:249
  59.1 2.0 %copy.51 = bf16[256,1024]{0,1:T(8,128)(2,1)} copy(bf16[256,1024]{1,0:T(8,128)(2,1)} %fusion.16) | data formatting | bytes 1048576 | tf_op jit(solution)/shard_map/convert_element_type | solution.py:254
  61.2 3.5 %convolution_convert_fusion.1 = bf16[256,256]{0,1:T(8,128)(2,1)} fusion(bf16[4096,256]{1,0:T(8,128)(2,1)S(1)} %copy-done, f32[4096]{0:T(1024)S(1)} %copy-done.27, f32[256]{0:T(256)S(1)} %get-tuple-element.49, bf16[256,1024]{1,0:T(8,128)(2,1)} %copy-done.11, bf16[256,1024]{1,0:T(8,128)(2,1)} %copy-done.8, bf16[256,1024]{1,0:T(8,128)(2,1)} %copy-done.5, ...), kind=kOutput, calls=%fused_computation.37 | convolution fusion | flops 548470784 | bytes 4342784 | tf_op jit(solution)/shard_map/dot_general | solution.py:187
  64.7 5.8 %convolution_bitcast_fusion = f32[32,8,8,128]{3,1,2,0:T(8,128)S(1)} fusion(bf16[4096,1024]{1,0:T(8,128)(2,1)} %param.13, f32[4096]{0:T(1024)S(1)} %copy-done.27, f32[256]{0:T(256)S(1)} %get-tuple-element.49, bf16[256,1024]{1,0:T(8,128)(2,1)S(1)} %copy-done.12, bf16[256,1024]{1,0:T(8,128)(2,1)S(1)} %copy-done.9, bf16[256,1024]{1,0:T(8,128)(2,1)S(1)} %copy-done.6, ...), kind=kOutput, calls=%fused_computation.27 | convolution fusion | flops 2159017984 | bytes 11551744 | tf_op jit(solution)/shard_map/dot_general | solution.py:185
  71.2 0.9 copy.49
  72.1 0.9 copy.48
  73.0 1.2 fusion.51
  74.9 1.7 %copy.81 = f32[256,2,64]{2,0,1:T(8,128)} copy(f32[256,2,64]{0,2,1:T(8,128)} %get-tuple-element.44) | data formatting | bytes 262144
  76.6 0.8 copy.80
  77.4 1.2 subtract_convert_fusion.3
  78.6 2.1 %fusion.15 = (f32[2,4,256]{2,1,0:T(4,128)S(1)}, f32[2,256,256,4]{2,1,3,0:T(8,128)S(1)}) fusion(pred[256,256]{0,1:T(8,128)(4,1)} %fusion.41, bf16[256,2,4,64]{3,0,2,1:T(8,128)(2,1)} %bitcast.278, bf16[256,2,4,64]{3,0,2,1:T(8,128)(2,1)} %bitcast.280, bf16[256,2,64]{2,0,1:T(8,128)(2,1)S(1)} %get-tuple-element.23, bf16[256,2,64]{2,0,1:T(8,128)(2,1)S(1)} %get-tuple-element.22), kind=kOutput, calls=%fused_computation.25 | convolution fusion | flops 137099264 | bytes 2826240 | tf_op jit(solution)/shard_map/qkgd,skd->kgqs/dot_general | solution.py:203
  80.7 1.7 %multiply_reduce_fusion = (f32[256,2,4]{0,2,1:T(4,128)S(1)}, bf16[2,128,4,256]{3,1,2,0:T(8,128)(2,1)}) fusion(bf16[256,1024]{0,1:T(8,128)(2,1)S(1)} %copy-done.23, bf16[256,2,128,1]{0,2,3,1:T(8,128)(2,1)S(1)} %bitcast.292, f32[2,4,256]{2,1,0:T(4,128)S(1)} %get-tuple-element.70, f32[2,256,256,4]{2,1,3,0:T(8,128)S(1)} %get-tuple-element.71, ...), kind=kOutput, calls=%fused_computation.60 | convolution fusion | flops 137623552 | bytes 3358720 | tf_op jit(solution)/shard_map/kgqs,skd->qkgd/dot_general | solution.py:209
  82.4 0.8 fusion.13
  84.3 1.2 fusion.20
  86.2 1.1 fusion.56
  87.3 2.4 %copy.83 = f32[256,8,64]{2,1,0:T(8,128)} copy(f32[256,8,64]{0,2,1:T(8,128)} %get-tuple-element.20) | data formatting | bytes 1048576
  89.7 2.4 %copy.82 = f32[256,8,64]{2,1,0:T(8,128)} copy(f32[256,8,64]{0,2,1:T(8,128)} %get-tuple-element.21) | data formatting | bytes 1048576
  92.1 1.8 %add_convert_fusion = (bf16[256,8,64]{2,1,0:T(8,128)(2,1)S(1)}, bf16[256,8,64]{2,1,0:T(8,128)(2,1)S(1)}) fusion(f32[256,8,64]{2,1,0:T(8,128)} %copy.83, f32[256,8,64]{2,1,0:T(8,128)} %copy.82, f32[256,64]{1,0:T(8,128)S(1)} %get-tuple-element.47, f32[256,64]{1,0:T(8,128)S(1)} %get-tuple-element.46), kind=kLoop, calls=%fused_computation.59 | loop fusion | flops 1048576 | bytes 1703936 | tf_op jit(solution)/shard_map/convert.12
  94.2 7.8 %fusion.36 = f32[256,4096]{1,0:T(8,128)} fusion(bf16[4096,1024]{1,0:T(8,128)(2,1)} %param.13, bf16[32,8,8,128]{3,2,1,0:T(8,128)(2,1)S(1)} %bitcast.283), kind=kOutput, calls=%fused_computation.71 | convolution fusion | flops 2147483648 | bytes 13107200 | tf_op jit(solution)/shard_map/dot_general | solution.py:282
  102.5 3.7 %convolution_add_fusion.1 = f32[256,4096]{1,0:T(8,128)S(1)} fusion(f32[256,4096]{1,0:T(8,128)} %fusion.36, bf16[256,256]{0,1:T(8,128)(2,1)S(1)} %bitcast.287, bf16[4096,256]{1,0:T(8,128)(2,1)} %param.14), kind=kOutput, calls=%fused_computation.4 | convolution fusion | flops 537919488 | bytes 10616832 | tf_op jit(solution)/shard_map/dot_general | solution.py:288
  106.3 1.3 fusion.3
  107.7 1.1 pad_maximum_fusion.6
  108.8 1.4 copy-done.4
  110.7 0.9 slice-done.3
  111.8 2.5 %fusion.61 = f32[256,4096]{1,0:T(8,128)S(1)} fusion(bf16[256,1024]{0,1:T(8,128)(2,1)S(1)} %bitcast.282, bf16[1024,4096]{1,0:T(8,128)(2,1)S(1)} %bitcast.268), kind=kOutput, calls=%fused_computation.170 | convolution fusion | flops 2147483648 | bytes 13107200 | tf_op jit(solution)/shard_map/dot_general | solution.py:213
  114.5 1.3 pad_maximum_fusion.4
  115.8 0.8 copy-done.1
  117.1 2.3 %fusion.35 = bf16[1,256,1024]{2,1,0:T(8,128)(2,1)} fusion(f32[256,4096]{1,0:T(8,128)} %copy-done.4, s32[]{:T(128)S(6)} %select_n.298, bf16[2,256,1024]{2,1,0:T(8,128)(2,1)} %collective-permute-done.20), kind=kLoop, calls=%fused_computation.70 | loop fusion | flops 786432 | bytes 2097156 | tf_op jit(solution)/shard_map/convert_element_type | solution.py:97
  119.4 1.9 %collective-permute-start.21 = (bf16[1,256,1024]{2,1,0:T(8,128)(2,1)}, bf16[1,256,1024]{2,1,0:T(8,128)(2,1)}, u32[]{:S(2)}, u32[]{:S(2)}) collective-permute-start(bf16[1,256,1024]{2,1,0:T(8,128)(2,1)} %fusion.35), channel_id=1, source_target_pairs={{0,2},{1,3},{2,0},{3,1},{4,6},{5,7},{6,4},{7,5},{8,10},{9,11},{10,... | collective-permute-start | bytes 1572872 | tf_op jit(solution)/shard_map/ppermute | solution.py:98
  121.3 2.3 %fusion.34 = bf16[1,256,1024]{2,1,0:T(8,128)(2,1)} fusion(f32[256,4096]{1,0:T(8,128)} %copy-done.1, s32[]{:T(128)S(6)} %select_n.298, bf16[2,256,1024]{2,1,0:T(8,128)(2,1)} %collective-permute-done.2), kind=kLoop, calls=%fused_computation.69 | loop fusion | flops 786432 | bytes 2097156 | tf_op jit(solution)/shard_map/convert_element_type | solution.py:97
  132.1 1.4 collective-permute-start.23
  142.5 2.9 %collective-permute-done.23 = f32[256]{0:T(256)S(1)} collective-permute-done((f32[256]{0:T(256)S(1)}, f32[256]{0:T(256)S(1)}, u32[]{:S(2)}, u32[]{:S(2)}) %collective-permute-start.23) | collective-permute-done | bytes 1056 | tf_op jit(solution)/shard_map/ppermute | solution.py:113
  145.4 3.6 %fusion.25 = (bf16[256,1024]{1,0:T(8,128)(2,1)}, bf16[256,1024]{1,0:T(8,128)(2,1)S(1)}) fusion(bf16[256,1024]{1,0:T(8,128)(2,1)S(1)} %copy-done.2, f32[256,4096]{1,0:T(8,128)} %copy-done.4, s32[]{:T(128)S(6)} %select_n.295, bf16[256,1024]{1,0:T(8,128)(2,1)S(1)} %constant_dynamic-update-slice_fusion.24, bf16[2,256,1024]{2,1,0:T(8,128)(2,1)} %collective-permute-done.20, ...), kind=kLoop, calls=%fused_computation.41 | loop fusion | flops 4980736 | bytes 6298628 | tf_op jit(solution)/shard_map/convert_element_type | solution.py:315
  150.4 1.0 collective-permute-start.6
  151.4 3.7 %collective-permute-start.7 = (bf16[32,1024]{1,0:T(8,128)(2,1)S(1)}, bf16[32,1024]{1,0:T(8,128)(2,1)S(1)}, u32[]{:S(2)}, u32[]{:S(2)}) collective-permute-start(bf16[32,1024]{1,0:T(8,128)(2,1)S(1)} %get-tuple-element.39), channel_id=1, source_target_pairs={{0,16},{4,20},{8,24},{12,28},{16,0},{20,4},{24,8},{28,12},{1,17},{... | collective-permute-start | bytes 196616 | tf_op jit(solution)/shard_map/ppermute | solution.py:229
  155.1 1.3 collective-permute-start.8
  157.5 1.8 %collective-permute-start.10 = (bf16[32,1024]{1,0:T(8,128)(2,1)S(1)}, bf16[32,1024]{1,0:T(8,128)(2,1)S(1)}, u32[]{:S(2)}, u32[]{:S(2)}) collective-permute-start(bf16[32,1024]{1,0:T(8,128)(2,1)S(1)} %get-tuple-element.36), channel_id=1, source_target_pairs={{0,28},{4,0},{8,4},{12,8},{16,12},{20,16},{24,20},{28,24},{1,29},{... | collective-permute-start | bytes 196616 | tf_op jit(solution)/shard_map/ppermute | solution.py:229
  159.3 2.2 %collective-permute-done.6 = bf16[32,1024]{1,0:T(8,128)(2,1)S(1)} collective-permute-done((bf16[32,1024]{1,0:T(8,128)(2,1)S(1)}, bf16[32,1024]{1,0:T(8,128)(2,1)S(1)}, u32[]{:S(2)}, u32[]{:S(2)}) %collective-permute-start.6) | collective-permute-done | bytes 65568 | tf_op jit(solution)/shard_map/ppermute | solution.py:229
  161.5 1.7 %collective-permute-done.8 = bf16[32,1024]{1,0:T(8,128)(2,1)S(1)} collective-permute-done((bf16[32,1024]{1,0:T(8,128)(2,1)S(1)}, bf16[32,1024]{1,0:T(8,128)(2,1)S(1)}, u32[]{:S(2)}, u32[]{:S(2)}) %collective-permute-start.8) | collective-permute-done | bytes 65568 | tf_op jit(solution)/shard_map/ppermute | solution.py:229
  163.4 0.8 copy-done.26
  (148 shorter events, 20.9 us)
Async XLA Ops:
  0.6 60.5 %copy-start = (bf16[4096,256]{1,0:T(8,128)(2,1)S(1)}, bf16[4096,256]{1,0:T(8,128)(2,1)}, u32[]{:S(2)}) copy-start(bf16[4096,256]{1,0:T(8,128)(2,1)} %param.15) | copy-start | bytes 6291460
  0.6 36.7 %copy-start.2 = (bf16[256,1024]{1,0:T(8,128)(2,1)S(1)}, bf16[256,1024]{1,0:T(8,128)(2,1)}, u32[]{:S(2)}) copy-start(bf16[256,1024]{1,0:T(8,128)(2,1)} %param.11) | copy-start | bytes 1572868
  2.7 17.5 %collective-permute-start.11 = (bf16[32,1024]{1,0:T(8,128)(2,1)S(1)}, bf16[32,1024]{1,0:T(8,128)(2,1)S(1)}, u32[]{:S(2)}, u32[]{:S(2)}) collective-permute-start(bf16[32,1024]{1,0:T(8,128)(2,1)S(1)} %get-tuple-element.34), channel_id=1, source_target_pairs={{0,4},{4,8},{8,12},{12,16},{16,20},{20,24},{24,28},{28,0},{1,5},{5... | collective-permute-start | bytes 196616 | tf_op jit(solution)/shard_map/ppermute | solution.py:158
  5.6 16.6 %collective-permute-start.12 = (bf16[32,1024]{1,0:T(8,128)(2,1)S(1)}, bf16[32,1024]{1,0:T(8,128)(2,1)S(1)}, u32[]{:S(2)}, u32[]{:S(2)}) collective-permute-start(bf16[32,1024]{1,0:T(8,128)(2,1)S(1)} %get-tuple-element.33), channel_id=1, source_target_pairs={{0,8},{4,12},{8,16},{12,20},{16,24},{20,28},{24,0},{28,4},{1,9},{5... | collective-permute-start | bytes 196616 | tf_op jit(solution)/shard_map/ppermute | solution.py:158
  7.2 17.1 %collective-permute-start.13 = (bf16[32,1024]{1,0:T(8,128)(2,1)S(1)}, bf16[32,1024]{1,0:T(8,128)(2,1)S(1)}, u32[]{:S(2)}, u32[]{:S(2)}) collective-permute-start(bf16[32,1024]{1,0:T(8,128)(2,1)S(1)} %get-tuple-element.32), channel_id=1, source_target_pairs={{0,12},{4,16},{8,20},{12,24},{16,28},{20,0},{24,4},{28,8},{1,13},{... | collective-permute-start | bytes 196616 | tf_op jit(solution)/shard_map/ppermute | solution.py:158
  9.8 16.7 %collective-permute-start.14 = (bf16[32,1024]{1,0:T(8,128)(2,1)S(1)}, bf16[32,1024]{1,0:T(8,128)(2,1)S(1)}, u32[]{:S(2)}, u32[]{:S(2)}) collective-permute-start(bf16[32,1024]{1,0:T(8,128)(2,1)S(1)} %get-tuple-element.31), channel_id=1, source_target_pairs={{0,16},{4,20},{8,24},{12,28},{16,0},{20,4},{24,8},{28,12},{1,17},{... | collective-permute-start | bytes 196616 | tf_op jit(solution)/shard_map/ppermute | solution.py:158
  11.0 16.1 %collective-permute-start.15 = (bf16[32,1024]{1,0:T(8,128)(2,1)S(1)}, bf16[32,1024]{1,0:T(8,128)(2,1)S(1)}, u32[]{:S(2)}, u32[]{:S(2)}) collective-permute-start(bf16[32,1024]{1,0:T(8,128)(2,1)S(1)} %get-tuple-element.30), channel_id=1, source_target_pairs={{0,20},{4,24},{8,28},{12,0},{16,4},{20,8},{24,12},{28,16},{1,21},{... | collective-permute-start | bytes 196616 | tf_op jit(solution)/shard_map/ppermute | solution.py:158
  18.9 19.6 %copy-start.25 = (s32[4]{0:T(128)S(1)}, s32[4]{0:T(128)}, u32[]{:S(2)}) copy-start(s32[4]{0:T(128)} %constant.269.clone) | copy-start | bytes 52
  20.1 24.1 %copy-start.29 = (s32[1,2]{1,0:T(1,128)S(1)}, s32[1,2]{1,0:T(1,128)}, u32[]{:S(2)}) copy-start(s32[1,2]{1,0:T(1,128)} %param.18) | copy-start | bytes 28
  20.2 7.5 %collective-permute-start.16 = (bf16[32,1024]{1,0:T(8,128)(2,1)S(1)}, bf16[32,1024]{1,0:T(8,128)(2,1)S(1)}, u32[]{:S(2)}, u32[]{:S(2)}) collective-permute-start(bf16[32,1024]{1,0:T(8,128)(2,1)S(1)} %get-tuple-element.29), channel_id=1, source_target_pairs={{0,24},{4,28},{8,0},{12,4},{16,8},{20,12},{24,16},{28,20},{1,25},{... | collective-permute-start | bytes 196616 | tf_op jit(solution)/shard_map/ppermute | solution.py:158
  22.2 6.1 %collective-permute-start.17 = (bf16[32,1024]{1,0:T(8,128)(2,1)S(1)}, bf16[32,1024]{1,0:T(8,128)(2,1)S(1)}, u32[]{:S(2)}, u32[]{:S(2)}) collective-permute-start(bf16[32,1024]{1,0:T(8,128)(2,1)S(1)} %get-tuple-element.28), channel_id=1, source_target_pairs={{0,28},{4,0},{8,4},{12,8},{16,12},{20,16},{24,20},{28,24},{1,29},{... | collective-permute-start | bytes 196616 | tf_op jit(solution)/shard_map/ppermute | solution.py:158
  24.3 12.3 %collective-permute-start = (bf16[1,256,1024]{2,1,0:T(8,128)(2,1)}, bf16[1,256,1024]{2,1,0:T(8,128)(2,1)S(1)}, u32[]{:S(2)}, u32[]{:S(2)}) collective-permute-start(bf16[1,256,1024]{2,1,0:T(8,128)(2,1)} %bitcast.273), channel_id=1, source_target_pairs={{0,2},{1,3},{2,0},{3,1},{4,6},{5,7},{6,4},{7,5},{8,10},{9,11},{10,... | collective-permute-start | bytes 1572872 | tf_op jit(solution)/shard_map/ppermute | solution.py:69
  35.7 11.8 %collective-permute-start.18 = (bf16[1,256,1024]{2,1,0:T(8,128)(2,1)S(1)}, bf16[1,256,1024]{2,1,0:T(8,128)(2,1)}, u32[]{:S(2)}, u32[]{:S(2)}) collective-permute-start(bf16[1,256,1024]{2,1,0:T(8,128)(2,1)S(1)} %bitcast.270), channel_id=1, source_target_pairs={{0,2},{1,3},{2,0},{3,1},{4,6},{5,7},{6,4},{7,5},{8,10},{9,11},{10,... | collective-permute-start | bytes 1572872 | tf_op jit(solution)/shard_map/ppermute | solution.py:69
  36.5 0.8 copy-start.20
  38.4 11.7 %collective-permute-start.1 = (bf16[2,256,1024]{2,1,0:T(8,128)(2,1)}, bf16[2,256,1024]{2,1,0:T(8,128)(2,1)}, u32[]{:S(2)}, u32[]{:S(2)}) collective-permute-start(bf16[2,256,1024]{2,1,0:T(8,128)(2,1)} %pad_maximum_fusion.3), channel_id=1, source_target_pairs={{0,1},{1,0},{2,3},{3,2},{4,5},{5,4},{6,7},{7,6},{8,9},{9,8},{10,11... | collective-permute-start | bytes 3145736 | tf_op jit(solution)/shard_map/ppermute | solution.py:69
  46.9 3.2 %copy-start.21 = (bf16[1,256,1024]{2,1,0:T(8,128)(2,1)S(1)}, bf16[1,256,1024]{2,1,0:T(8,128)(2,1)}, u32[]{:S(2)}) copy-start(bf16[1,256,1024]{2,1,0:T(8,128)(2,1)} %copy-done.20) | copy-start | bytes 1572868
  48.7 3.1 %collective-permute-start.19 = (bf16[2,256,1024]{2,1,0:T(8,128)(2,1)S(1)}, bf16[2,256,1024]{2,1,0:T(8,128)(2,1)S(1)}, u32[]{:S(2)}, u32[]{:S(2)}) collective-permute-start(bf16[2,256,1024]{2,1,0:T(8,128)(2,1)S(1)} %pad_maximum_fusion.5), channel_id=1, source_target_pairs={{0,1},{1,0},{2,3},{3,2},{4,5},{5,4},{6,7},{7,6},{8,9},{9,8},{10,11... | collective-permute-start | bytes 3145736 | tf_op jit(solution)/shard_map/ppermute | solution.py:69
  50.1 4.7 %slice-start = ((s8[8388608]{0:T(1024)(128)(4,1)}), s8[4194304]{0:T(1024)(128)(4,1)S(1)}, s32[]{:S(2)}) async-start(s8[8388608]{0:T(1024)(128)(4,1)} %bitcast.265), calls=%async_computation | async-start | bytes 8388608
  53.0 2.9 %slice-start.1 = ((s8[8388608]{0:T(1024)(128)(4,1)}), s8[4194304]{0:T(1024)(128)(4,1)S(1)}, s32[]{:S(2)}) async-start(s8[8388608]{0:T(1024)(128)(4,1)} %bitcast.265), calls=%async_computation.1 | async-start | bytes 8388608
  53.5 0.8 copy-start.5
  53.5 1.3 copy-start.8
  53.5 1.3 copy-start.11
  53.6 1.3 copy-start.14
  55.9 5.2 %copy-start.27 = (f32[4096]{0:T(1024)S(1)}, f32[4096]{0:T(1024)}, u32[]{:S(2)}) copy-start(f32[4096]{0:T(1024)} %param.12) | copy-start | bytes 49156
  61.2 3.5 %copy-start.6 = (bf16[256,1024]{1,0:T(8,128)(2,1)S(1)}, bf16[256,1024]{1,0:T(8,128)(2,1)}, u32[]{:S(2)}) copy-start(bf16[256,1024]{1,0:T(8,128)(2,1)} %copy-done.5) | copy-start | bytes 1572868
  61.2 3.5 %copy-start.9 = (bf16[256,1024]{1,0:T(8,128)(2,1)S(1)}, bf16[256,1024]{1,0:T(8,128)(2,1)}, u32[]{:S(2)}) copy-start(bf16[256,1024]{1,0:T(8,128)(2,1)} %copy-done.8) | copy-start | bytes 1572868
  61.2 3.5 %copy-start.12 = (bf16[256,1024]{1,0:T(8,128)(2,1)S(1)}, bf16[256,1024]{1,0:T(8,128)(2,1)}, u32[]{:S(2)}) copy-start(bf16[256,1024]{1,0:T(8,128)(2,1)} %copy-done.11) | copy-start | bytes 1572868
  61.2 3.5 %copy-start.15 = (bf16[256,1024]{1,0:T(8,128)(2,1)S(1)}, bf16[256,1024]{1,0:T(8,128)(2,1)}, u32[]{:S(2)}) copy-start(bf16[256,1024]{1,0:T(8,128)(2,1)} %copy-done.14) | copy-start | bytes 1572868
  70.7 2.3 %copy-start.19 = (bf16[4096,256]{1,0:T(8,128)(2,1)S(1)}, bf16[4096,256]{1,0:T(8,128)(2,1)}, u32[]{:S(2)}) copy-start(bf16[4096,256]{1,0:T(8,128)(2,1)} %param.14) | copy-start | bytes 6291460
  77.4 3.2 %copy-start.23 = (bf16[256,1024]{0,1:T(8,128)(2,1)S(1)}, bf16[256,1024]{0,1:T(8,128)(2,1)}, u32[]{:S(2)}) copy-start(bf16[256,1024]{0,1:T(8,128)(2,1)} %copy.51) | copy-start | bytes 1572868
  77.4 3.3 %copy-start.24 = (pred[256,256]{0,1:T(8,128)(4,1)S(1)}, pred[256,256]{0,1:T(8,128)(4,1)}, u32[]{:S(2)}) copy-start(pred[256,256]{0,1:T(8,128)(4,1)} %fusion.41) | copy-start | bytes 196612
  77.4 3.3 %copy-start.30 = (bf16[256,256]{0,1:T(8,128)(2,1)S(1)}, bf16[256,256]{0,1:T(8,128)(2,1)}, u32[]{:S(2)}) copy-start(bf16[256,256]{0,1:T(8,128)(2,1)} %convolution_convert_fusion.1) | copy-start | bytes 393220
  83.1 1.0 copy-start.17
  83.1 1.2 copy-start.18
  94.2 7.8 %copy-start.3 = (f32[256,2,128]{2,0,1:T(8,128)S(1)}, f32[256,2,128]{2,0,1:T(8,128)}, u32[]{:S(2)}) copy-start(f32[256,2,128]{2,0,1:T(8,128)} %fusion.20) | copy-start | bytes 786436
  102.4 3.8 %copy-start.7 = (bf16[256,1024]{1,0:T(8,128)(2,1)S(1)}, bf16[256,1024]{1,0:T(8,128)(2,1)}, u32[]{:S(2)}) copy-start(bf16[256,1024]{1,0:T(8,128)(2,1)} %copy-done.5) | copy-start | bytes 1572868
  102.4 3.8 %copy-start.10 = (bf16[256,1024]{1,0:T(8,128)(2,1)S(1)}, bf16[256,1024]{1,0:T(8,128)(2,1)}, u32[]{:S(2)}) copy-start(bf16[256,1024]{1,0:T(8,128)(2,1)} %copy-done.8) | copy-start | bytes 1572868
  102.4 3.8 %copy-start.13 = (bf16[256,1024]{1,0:T(8,128)(2,1)S(1)}, bf16[256,1024]{1,0:T(8,128)(2,1)}, u32[]{:S(2)}) copy-start(bf16[256,1024]{1,0:T(8,128)(2,1)} %copy-done.11) | copy-start | bytes 1572868
  102.5 3.8 %copy-start.16 = (bf16[256,1024]{1,0:T(8,128)(2,1)S(1)}, bf16[256,1024]{1,0:T(8,128)(2,1)}, u32[]{:S(2)}) copy-start(bf16[256,1024]{1,0:T(8,128)(2,1)} %copy-done.14) | copy-start | bytes 1572868
  102.5 3.8 %copy-start.28 = (f32[4096]{0:T(1024)S(1)}, f32[4096]{0:T(1024)}, u32[]{:S(2)}) copy-start(f32[4096]{0:T(1024)} %param.12) | copy-start | bytes 49156
  106.2 4.5 %slice-start.2 = ((s8[8388608]{0:T(1024)(128)(4,1)}), s8[4194304]{0:T(1024)(128)(4,1)S(1)}, s32[]{:S(2)}) async-start(s8[8388608]{0:T(1024)(128)(4,1)} %bitcast.267), calls=%async_computation.2 | async-start | bytes 8388608
  106.3 5.3 %slice-start.3 = ((s8[8388608]{0:T(1024)(128)(4,1)}), s8[4194304]{0:T(1024)(128)(4,1)S(1)}, s32[]{:S(2)}) async-start(s8[8388608]{0:T(1024)(128)(4,1)} %bitcast.267), calls=%async_computation.3 | async-start | bytes 8388608
  107.5 2.6 %copy-start.4 = (f32[256,4096]{1,0:T(8,128)}, f32[256,4096]{1,0:T(8,128)S(1)}, u32[]{:S(2)}) copy-start(f32[256,4096]{1,0:T(8,128)S(1)} %get-tuple-element.75) | copy-start | bytes 12582916
  107.5 4.2 %copy-start.22 = (bf16[2,128,4,256]{3,1,2,0:T(8,128)(2,1)S(1)}, bf16[2,128,4,256]{3,1,2,0:T(8,128)(2,1)}, u32[]{:S(2)}) copy-start(bf16[2,128,4,256]{3,1,2,0:T(8,128)(2,1)} %get-tuple-element.73) | copy-start | bytes 1572868
  110.2 6.9 %collective-permute-start.20 = (bf16[2,256,1024]{2,1,0:T(8,128)(2,1)}, bf16[2,256,1024]{2,1,0:T(8,128)(2,1)}, u32[]{:S(2)}, u32[]{:S(2)}) collective-permute-start(bf16[2,256,1024]{2,1,0:T(8,128)(2,1)} %pad_maximum_fusion.6), channel_id=1, source_target_pairs={{0,1},{1,0},{2,3},{3,2},{4,5},{5,4},{6,7},{7,6},{8,9},{9,8},{10,11... | collective-permute-start | bytes 3145736 | tf_op jit(solution)/shard_map/ppermute | solution.py:98
  114.3 2.3 %copy-start.1 = (f32[256,4096]{1,0:T(8,128)}, f32[256,4096]{1,0:T(8,128)S(1)}, u32[]{:S(2)}) copy-start(f32[256,4096]{1,0:T(8,128)S(1)} %fusion.61) | copy-start | bytes 12582916
  116.6 4.7 %collective-permute-start.2 = (bf16[2,256,1024]{2,1,0:T(8,128)(2,1)}, bf16[2,256,1024]{2,1,0:T(8,128)(2,1)}, u32[]{:S(2)}, u32[]{:S(2)}) collective-permute-start(bf16[2,256,1024]{2,1,0:T(8,128)(2,1)} %pad_maximum_fusion.4), channel_id=1, source_target_pairs={{0,1},{1,0},{2,3},{3,2},{4,5},{5,4},{6,7},{7,6},{8,9},{9,8},{10,11... | collective-permute-start | bytes 3145736 | tf_op jit(solution)/shard_map/ppermute | solution.py:98
  119.4 26.0 %collective-permute-start.21 = (bf16[1,256,1024]{2,1,0:T(8,128)(2,1)}, bf16[1,256,1024]{2,1,0:T(8,128)(2,1)}, u32[]{:S(2)}, u32[]{:S(2)}) collective-permute-start(bf16[1,256,1024]{2,1,0:T(8,128)(2,1)} %fusion.35), channel_id=1, source_target_pairs={{0,2},{1,3},{2,0},{3,1},{4,6},{5,7},{6,4},{7,5},{8,10},{9,11},{10,... | collective-permute-start | bytes 1572872 | tf_op jit(solution)/shard_map/ppermute | solution.py:98
  123.6 21.8 %collective-permute-start.3 = (bf16[1,256,1024]{2,1,0:T(8,128)(2,1)}, bf16[1,256,1024]{2,1,0:T(8,128)(2,1)}, u32[]{:S(2)}, u32[]{:S(2)}) collective-permute-start(bf16[1,256,1024]{2,1,0:T(8,128)(2,1)} %fusion.34), channel_id=1, source_target_pairs={{0,2},{1,3},{2,0},{3,1},{4,6},{5,7},{6,4},{7,5},{8,10},{9,11},{10,... | collective-permute-start | bytes 1572872 | tf_op jit(solution)/shard_map/ppermute | solution.py:98
  125.7 6.3 %collective-permute-start.22 = (f32[256]{0:T(256)S(1)}, f32[256]{0:T(256)S(1)}, u32[]{:S(2)}, u32[]{:S(2)}) collective-permute-start(f32[256]{0:T(256)S(1)} %get-tuple-element.74), channel_id=1, source_target_pairs={{0,1},{1,0},{2,3},{3,2},{4,5},{5,4},{6,7},{7,6},{8,9},{9,8},{10,11... | collective-permute-start | bytes 3080 | tf_op jit(solution)/shard_map/ppermute | solution.py:113
  132.1 13.3 %collective-permute-start.23 = (f32[256]{0:T(256)S(1)}, f32[256]{0:T(256)S(1)}, u32[]{:S(2)}, u32[]{:S(2)}) collective-permute-start(f32[256]{0:T(256)S(1)} %add.431), channel_id=1, source_target_pairs={{0,2},{1,3},{2,0},{3,1},{4,6},{5,7},{6,4},{7,5},{8,10},{9,11},{10,... | collective-permute-start | bytes 3080 | tf_op jit(solution)/shard_map/ppermute | solution.py:113
  149.1 7.8 %collective-permute-start.4 = (bf16[32,1024]{1,0:T(8,128)(2,1)S(1)}, bf16[32,1024]{1,0:T(8,128)(2,1)S(1)}, u32[]{:S(2)}, u32[]{:S(2)}) collective-permute-start(bf16[32,1024]{1,0:T(8,128)(2,1)S(1)} %get-tuple-element.42), channel_id=1, source_target_pairs={{0,4},{4,8},{8,12},{12,16},{16,20},{20,24},{24,28},{28,0},{1,5},{5... | collective-permute-start | bytes 196616 | tf_op jit(solution)/shard_map/ppermute | solution.py:229
  149.7 7.8 %collective-permute-start.5 = (bf16[32,1024]{1,0:T(8,128)(2,1)S(1)}, bf16[32,1024]{1,0:T(8,128)(2,1)S(1)}, u32[]{:S(2)}, u32[]{:S(2)}) collective-permute-start(bf16[32,1024]{1,0:T(8,128)(2,1)S(1)} %get-tuple-element.41), channel_id=1, source_target_pairs={{0,8},{4,12},{8,16},{12,20},{16,24},{20,28},{24,0},{28,4},{1,9},{5... | collective-permute-start | bytes 196616 | tf_op jit(solution)/shard_map/ppermute | solution.py:229
  150.4 11.1 %collective-permute-start.6 = (bf16[32,1024]{1,0:T(8,128)(2,1)S(1)}, bf16[32,1024]{1,0:T(8,128)(2,1)S(1)}, u32[]{:S(2)}, u32[]{:S(2)}) collective-permute-start(bf16[32,1024]{1,0:T(8,128)(2,1)S(1)} %get-tuple-element.40), channel_id=1, source_target_pairs={{0,12},{4,16},{8,20},{12,24},{16,28},{20,0},{24,4},{28,8},{1,13},{... | collective-permute-start | bytes 196616 | tf_op jit(solution)/shard_map/ppermute | solution.py:229
  151.4 10.1 %collective-permute-start.7 = (bf16[32,1024]{1,0:T(8,128)(2,1)S(1)}, bf16[32,1024]{1,0:T(8,128)(2,1)S(1)}, u32[]{:S(2)}, u32[]{:S(2)}) collective-permute-start(bf16[32,1024]{1,0:T(8,128)(2,1)S(1)} %get-tuple-element.39), channel_id=1, source_target_pairs={{0,16},{4,20},{8,24},{12,28},{16,0},{20,4},{24,8},{28,12},{1,17},{... | collective-permute-start | bytes 196616 | tf_op jit(solution)/shard_map/ppermute | solution.py:229
  155.1 8.1 %collective-permute-start.8 = (bf16[32,1024]{1,0:T(8,128)(2,1)S(1)}, bf16[32,1024]{1,0:T(8,128)(2,1)S(1)}, u32[]{:S(2)}, u32[]{:S(2)}) collective-permute-start(bf16[32,1024]{1,0:T(8,128)(2,1)S(1)} %get-tuple-element.38), channel_id=1, source_target_pairs={{0,20},{4,24},{8,28},{12,0},{16,4},{20,8},{24,12},{28,16},{1,21},{... | collective-permute-start | bytes 196616 | tf_op jit(solution)/shard_map/ppermute | solution.py:229
  156.9 6.3 %collective-permute-start.9 = (bf16[32,1024]{1,0:T(8,128)(2,1)S(1)}, bf16[32,1024]{1,0:T(8,128)(2,1)S(1)}, u32[]{:S(2)}, u32[]{:S(2)}) collective-permute-start(bf16[32,1024]{1,0:T(8,128)(2,1)S(1)} %get-tuple-element.37), channel_id=1, source_target_pairs={{0,24},{4,28},{8,0},{12,4},{16,8},{20,12},{24,16},{28,20},{1,25},{... | collective-permute-start | bytes 196616 | tf_op jit(solution)/shard_map/ppermute | solution.py:229
  157.5 5.8 %collective-permute-start.10 = (bf16[32,1024]{1,0:T(8,128)(2,1)S(1)}, bf16[32,1024]{1,0:T(8,128)(2,1)S(1)}, u32[]{:S(2)}, u32[]{:S(2)}) collective-permute-start(bf16[32,1024]{1,0:T(8,128)(2,1)S(1)} %get-tuple-element.36), channel_id=1, source_target_pairs={{0,28},{4,0},{8,4},{12,8},{16,12},{20,16},{24,20},{28,24},{1,29},{... | collective-permute-start | bytes 196616 | tf_op jit(solution)/shard_map/ppermute | solution.py:229
  163.4 0.8 copy-start.26

commit v4 on v3

--- a/solution.py
+++ b/solution.py
@@ -59,14 +59,16 @@
     return [(i, i ^ bit) for i in range(size)]
 
 
-def gather_features(shard, axis_name, size, position):
+def gather_features(shard, axis_name, size, position, tied=None):
     if not _is_pow2(size):
-        return lax.all_gather(shard, axis_name, axis=1, tiled=True)
+        return lax.all_gather(shard, axis_name, axis=1, tiled=True), tied
     held = shard[None]
     masks = [0]
     bit = size >> 1
     while bit:
         incoming = lax.ppermute(held, axis_name, _xor_pairs(size, bit))
+        if tied is not None:
+            incoming, tied = lax.optimization_barrier((incoming, tied))
         held = jnp.concatenate([held, incoming], axis=0)
         masks = masks + [m ^ bit for m in masks]
         bit >>= 1
@@ -75,16 +77,18 @@
         lax.dynamic_index_in_dim(held, table[s ^ position], axis=0, keepdims=False)
         for s in range(size)
     ]
-    return jnp.concatenate(blocks, axis=1)
-
-
-def scatter_features(partial, axis_name, size, position):
+    return jnp.concatenate(blocks, axis=1), tied
+
+
+def scatter_features(partial, axis_name, size, position, extra=None):
     width = partial.shape[1] // size
     if not _is_pow2(size):
         summed = lax.psum_scatter(
             partial.astype(jnp.bfloat16), axis_name, scatter_dimension=1, tiled=True
         )
-        return summed.astype(jnp.float32)
+        if extra is not None:
+            extra = lax.psum(extra, axis_name)
+        return summed.astype(jnp.float32), extra
     held = [
         lax.dynamic_slice_in_dim(partial, (position ^ m) * width, width, axis=1)
         for m in range(size)
@@ -95,24 +99,43 @@
         keep = [i for i, m in enumerate(masks) if not m & bit]
         send = [i for i, m in enumerate(masks) if m & bit]
         outgoing = jnp.stack([held[i] for i in send]).astype(jnp.bfloat16)
-        incoming = lax.ppermute(outgoing, axis_name, _xor_pairs(size, bit))
+        if extra is None:
+            incoming = lax.ppermute(outgoing, axis_name, _xor_pairs(size, bit))
+        else:
+            incoming, extra_in = lax.ppermute((outgoing, extra), axis_name, _xor_pairs(size, bit))
+            extra = extra + extra_in
         sent_masks = [masks[i] ^ bit for i in send]
         held = [
             held[i] + incoming[sent_masks.index(masks[i])].astype(jnp.float32) for i in keep
         ]
         masks = [masks[i] for i in keep]
         bit <<= 1
-    return held[0]
-
-
-def sum_over(values, axis_name, size):
-    if not _is_pow2(size):
-        return lax.psum(values, axis_name)
+    return held[0], extra
+
+
+def relay_blocks(blocks, select, place, axis_name, size):
+    held = jnp.einsum(
+        "mn,nrw->mrw", select, blocks, preferred_element_type=jnp.float32
+    ).astype(blocks.dtype)
+    items = [held[m] for m in range(size)]
+    dst = list(range(size))
+    src = [0] * size
     bit = 1
     while bit < size:
-        values = values + lax.ppermute(values, axis_name, _xor_pairs(size, bit))
+        send = [k for k in range(len(items)) if dst[k] & bit]
+        keep = [k for k in range(len(items)) if not dst[k] & bit]
+        incoming = lax.ppermute(
+            jnp.stack([items[k] for k in send]), axis_name, _xor_pairs(size, bit)
+        )
+        items = [items[k] for k in keep] + [incoming[n] for n in range(len(send))]
+        dst, src = (
+            [dst[k] for k in keep] + [dst[k] ^ bit for k in send],
+            [src[k] for k in keep] + [src[k] ^ bit for k in send],
+        )
         bit <<= 1
-    return values
+    arrived = jnp.stack(items)
+    ordered = jnp.einsum("bk,krw->brw", place(src), arrived, preferred_element_type=jnp.float32)
+    return ordered.astype(blocks.dtype)
 
 
 def per_device(
@@ -147,24 +170,22 @@
     send_table = (owner_row[None, :] == slot_index[:, None]).astype(jnp.bfloat16)
 
     home_rows = token_row_count // block_count
+    gathered, grad_output = gather_features(
+        tokens, "tensor", tensor_size, tensor_index, tied=grad_output
+    )
     owned_blocks = grad_output.reshape(block_count, home_rows, width_part)
-    if sources <= 16:
-        returned = [lax.dynamic_index_in_dim(owned_blocks, data_index, 0, keepdims=False)]
-        for shift in range(1, sources):
-            pairs = [(a, (a + shift) % sources) for a in range(sources)]
-            piece = lax.dynamic_index_in_dim(
-                owned_blocks, (data_index + shift) % sources, 0, keepdims=False
-            )
-            returned.append(lax.ppermute(piece, "dp", pairs))
-        returned = jnp.stack(returned)
-        grad_home = jnp.concatenate(
-            [
-                lax.dynamic_index_in_dim(
-                    returned, (data_index - owner_row[j]) % sources, 0, keepdims=False
-                )
-                for j in range(block_count)
-            ],
-            axis=0,
+    if _is_pow2(sources) and sources <= 16 and block_count == sources:
+        mask_index = jnp.arange(sources, dtype=jnp.int32)
+        pick_home = (
+            (mask_index[:, None] ^ data_index) == jnp.arange(block_count)[None, :]
+        ).astype(jnp.bfloat16)
+
+        def home_order(source_masks):
+            masks = jnp.asarray(source_masks, jnp.int32)
+            return ((owner_row[:, None] ^ data_index) == masks[None, :]).astype(jnp.bfloat16)
+
+        grad_home = relay_blocks(owned_blocks, pick_home, home_order, "dp", sources).reshape(
+            token_row_count, width_part
         )
     else:
         arrived = lax.all_to_all(
@@ -178,7 +199,6 @@
             .reshape(token_row_count, width_part)
         )
 
-    gathered = gather_features(tokens, "tensor", tensor_size, tensor_index)
     gathered_float = gathered.astype(jnp.float32)
     inverse = lax.rsqrt(jnp.mean(gathered_float * gathered_float, axis=1) + NORM_EPSILON)
     normed_input = (gathered_float * inverse[:, None] * norm_gain[None, :]).astype(jnp.bfloat16)
@@ -211,31 +231,21 @@
     ).astype(jnp.bfloat16)
     attended_flat = attended.reshape(token_row_count, query_width)
     mixed_partial = jnp.dot(attended_flat, w_out, preferred_element_type=jnp.float32)
-    mixed = scatter_features(mixed_partial, "tensor", tensor_size, tensor_index)
+    mixed, _ = scatter_features(mixed_partial, "tensor", tensor_size, tensor_index)
     output_home = (x_float + mixed).astype(jnp.bfloat16)
     home_blocks = output_home.reshape(block_count, home_rows, width_part)
-    if sources <= 16:
-        block_for = jnp.sum(
-            jnp.where(send_table > 0, jnp.arange(block_count, dtype=jnp.int32)[None, :], 0), axis=1
-        )
-        landed = [
-            lax.dynamic_index_in_dim(home_blocks, block_for[data_index], 0, keepdims=False)
-        ]
-        for shift in range(1, sources):
-            pairs = [(a, (a + shift) % sources) for a in range(sources)]
-            piece = lax.dynamic_index_in_dim(
-                home_blocks, block_for[(data_index + shift) % sources], 0, keepdims=False
-            )
-            landed.append(lax.ppermute(piece, "dp", pairs))
-        landed = jnp.stack(landed)
-        relaid = jnp.concatenate(
-            [
-                lax.dynamic_index_in_dim(
-                    landed, (data_index - b) % sources, 0, keepdims=False
-                )
-                for b in range(sources)
-            ],
-            axis=0,
+    if _is_pow2(sources) and sources <= 16 and block_count == sources:
+        mask_index = jnp.arange(sources, dtype=jnp.int32)
+        pick_owner = (owner_row[None, :] == (mask_index[:, None] ^ data_index)).astype(
+            jnp.bfloat16
+        )
+
+        def owner_order(source_masks):
+            masks = jnp.asarray(source_masks, jnp.int32)
+            return ((mask_index[:, None] ^ data_index) == masks[None, :]).astype(jnp.bfloat16)
+
+        relaid = relay_blocks(home_blocks, pick_owner, owner_order, "dp", sources).reshape(
+            token_row_count, width_part
         )
     else:
         outgoing = jnp.dot(
@@ -245,7 +255,7 @@
             token_row_count, width_part
         )
 
-    grad_full = gather_features(grad_home, "tensor", tensor_size, tensor_index)
+    grad_full, _ = gather_features(grad_home, "tensor", tensor_size, tensor_index)
     attended_gradient = lax.dot_general(
         grad_full,
         w_out,
@@ -299,13 +309,11 @@
         )
     )
     stat_partial = jnp.sum(normed_partial * norm_gain[None, :] * gathered_float, axis=1)
-    stat = sum_over(stat_partial, "tensor", tensor_size) / full_width
-    normed_gradient = scatter_features(
-        normed_partial,
-        "tensor",
-        tensor_size,
-        tensor_index,
-    )
+    relaid, normed_partial = lax.optimization_barrier((relaid, normed_partial))
+    normed_gradient, stat_sum = scatter_features(
+        normed_partial, "tensor", tensor_size, tensor_index, extra=stat_partial
+    )
+    stat = stat_sum / full_width
     cubed = inverse * inverse * inverse
     grad_x = (
         grad_home.astype(jnp.float32)

time: 166 us -> 201 us (1.21)
  waiting for transfers between devices: 8.2 us -> 75.5 us
  between operations: 29.5 us -> 8.92 us
  starting transfers between devices: 30.5 us -> 22.5 us
  local copies, waits for them, and re-layouts: 38.4 us -> 34.4 us
  other arithmetic: 21.9 us -> 24.6 us
    ppermute x16 -> x10, waiting for transfers between devices: 7.29 us -> 50.9 us  [the longest x6 36.6 us: relay_blocks(): lax.ppermute(jnp.stack([items[k] for k in send]), axis_name, _xor_pairs(s...]
    ppermute x4, waiting for transfers between devices: 0.9 us -> 18.2 us  [gather_features(): incoming = lax.ppermute(held, axis_name, _xor_pairs(size, bit))]
    unnamed x101 -> x99, local copies, waits for them, and re-layouts: 25 us -> 13.3 us
    ppermute x16 -> x10, starting transfers between devices: 24.9 us -> 15.6 us  [the longest x6 13.5 us: relay_blocks(): lax.ppermute(jnp.stack([items[k] for k in send]), axis_name, _xor_pairs(s...]
    ppermute x4 -> x2, waiting for transfers between devices: 0.01 us -> 6.46 us  [scatter_features(): incoming = lax.ppermute(outgoing, axis_name, _xor_pairs(size, bit))]
    dot_general x0 -> x4, matrix products: none -> 3.71 us  [the longest x2 2.84 us: relay_blocks(): jnp.einsum('bk,krw->brw', place(src), arrived, preferred_element_type=jnp...]
    convert_element_type x2, other arithmetic: 4.61 us -> 1.33 us  [scatter_features(): outgoing = jnp.stack([held[i] for i in send]).astype(jnp.bfloat16)]
    another operation x4, local copies, waits for them, and re-layouts: 2.42 us -> 5.64 us  [the longest x2 5.5 us: relay_blocks(): arrived = jnp.stack(items)]
  transfers between devices with their start and end apart: 24 -> 16, of which waited for: 6 -> 13; matrix products, arithmetic and copies ran while one was open for 18% -> 14% of each run, Pallas kernels for 0% -> 0%
where the time goes in v4:
time: 201 us; the launch traced here: 200 us
  waiting for transfers between devices  75.5 us (38%)
  local copies, waits for them, and re-layouts  34.4 us (17%)
  matrix products  34.4 us (17%)
  other arithmetic  24.6 us (12%)
  starting transfers between devices  22.5 us (11%)
  between operations  8.92 us (4%)
    ppermute x6, waiting for transfers between devices, relay_blocks(): lax.ppermute(jnp.stack([items[k] for k in send]), axis_name, _xor_pairs(s...  36.6 us
    ppermute x4, waiting for transfers between devices, gather_features(): incoming = lax.ppermute(held, axis_name, _xor_pairs(size, bit))  18.2 us
    ppermute x4, waiting for transfers between devices, scatter_features(): lax.ppermute((outgoing, extra), axis_name, _xor_pairs(size, bit))  14.3 us
    ppermute x6, starting transfers between devices, relay_blocks(): lax.ppermute(jnp.stack([items[k] for k in send]), axis_name, _xor_pairs(s...  13.5 us
    unnamed x99, local copies, waits for them, and re-layouts  13.3 us
    concatenate x4, other arithmetic, gather_features(): held = jnp.concatenate([held, incoming], axis=0)  6.6 us
    ppermute x2, waiting for transfers between devices, scatter_features(): incoming = lax.ppermute(outgoing, axis_name, _xor_pairs(size, bit))  6.46 us
    dot_general x1, matrix products, per_device(): jnp.dot(normed_input, w_query, preferred_element_type=jnp.float32)  6.42 us
  transfers between devices with their start and end apart: 16, of which 13 were waited for; matrix products, arithmetic and copies ran while one was open for 14% of the time, Pallas kernels for 0%

profile of v4, /device:TPU:0, one launch (start us, length us, event | category | flops | bytes accessed | tf_op | source)
XLA Modules:
  0.0 200.3 jit_solution(3545203756650391219)
XLA Ops:
  0.7 3.0 %collective-permute-start = (bf16[1,256,1024]{2,1,0:T(8,128)(2,1)}, bf16[1,256,1024]{2,1,0:T(8,128)(2,1)S(1)}, u32[]{:S(2)}, u32[]{:S(2)}) collective-permute-start(bf16[1,256,1024]{2,1,0:T(8,128)(2,1)} %bitcast.182), channel_id=1, source_target_pairs={{0,2},{1,3},{2,0},{3,1},{4,6},{5,7},{6,4},{7,5},{8,10},{9,11},{10,... | collective-permute-start | bytes 1572872 | tf_op jit(solution)/shard_map/ppermute | solution.py:69
  3.7 12.1 %collective-permute-done = bf16[1,256,1024]{2,1,0:T(8,128)(2,1)S(1)} collective-permute-done((bf16[1,256,1024]{2,1,0:T(8,128)(2,1)}, bf16[1,256,1024]{2,1,0:T(8,128)(2,1)S(1)}, u32[]{:S(2)}, u32[]{:S(2)}) %collective-permute-start) | collective-permute-done | bytes 524320 | tf_op jit(solution)/shard_map/ppermute | solution.py:69
  15.8 2.3 %pad_maximum_fusion.3 = bf16[2,256,1024]{2,1,0:T(8,128)(2,1)} fusion(bf16[1,256,1024]{2,1,0:T(8,128)(2,1)S(1)} %collective-permute-done, bf16[1,256,1024]{2,1,0:T(8,128)(2,1)} %bitcast.183), kind=kLoop, calls=%fused_computation.46 | loop fusion | flops 524288 | bytes 2097152 | tf_op jit(solution)/shard_map/concatenate | solution.py:72
  18.2 3.0 %collective-permute-done.1 = bf16[2,256,1024]{2,1,0:T(8,128)(2,1)} collective-permute-done((bf16[2,256,1024]{2,1,0:T(8,128)(2,1)}, bf16[2,256,1024]{2,1,0:T(8,128)(2,1)}, u32[]{:S(2)}, u32[]{:S(2)}) %collective-permute-start.1) | collective-permute-done | bytes 1048608 | tf_op jit(solution)/shard_map/ppermute | solution.py:69
  21.6 0.9 fusion.72
  23.1 1.8 collective-permute-start.7
  24.9 6.6 %collective-permute-done.7 = bf16[4,32,1024]{2,0,1:T(4,128)(2,1)S(1)} collective-permute-done((bf16[4,32,1024]{2,0,1:T(4,128)(2,1)S(1)}, bf16[4,32,1024]{2,0,1:T(4,128)(2,1)S(1)}, u32[]{:S(2)}, u32[]{:S(2)}) %collective-permute-start.7) | collective-permute-done | bytes 262176 | tf_op jit(solution)/shard_map/ppermute | solution.py:127
  32.5 1.9 collective-permute-start.8
  34.4 5.8 %collective-permute-done.8 = bf16[4,32,1024]{2,0,1:T(4,128)(2,1)S(1)} collective-permute-done((bf16[4,32,1024]{2,0,1:T(4,128)(2,1)S(1)}, bf16[4,32,1024]{2,0,1:T(4,128)(2,1)S(1)}, u32[]{:S(2)}, u32[]{:S(2)}) %collective-permute-start.8) | collective-permute-done | bytes 262176 | tf_op jit(solution)/shard_map/ppermute | solution.py:127
  41.2 2.8 %collective-permute-start.9 = (bf16[4,32,1024]{2,0,1:T(4,128)(2,1)S(1)}, bf16[4,32,1024]{2,0,1:T(4,128)(2,1)S(1)}, u32[]{:S(2)}, u32[]{:S(2)}) collective-permute-start(bf16[4,32,1024]{2,0,1:T(4,128)(2,1)S(1)} %pad_maximum_fusion.14), channel_id=1, source_target_pairs={{0,16},{4,20},{8,24},{12,28},{16,0},{20,4},{24,8},{28,12},{1,17},{... | collective-permute-start | bytes 786440 | tf_op jit(solution)/shard_map/ppermute | solution.py:127
  44.0 1.3 broadcast_xor_fusion
  45.3 9.2 %collective-permute-done.9 = bf16[4,32,1024]{2,0,1:T(4,128)(2,1)S(1)} collective-permute-done((bf16[4,32,1024]{2,0,1:T(4,128)(2,1)S(1)}, bf16[4,32,1024]{2,0,1:T(4,128)(2,1)S(1)}, u32[]{:S(2)}, u32[]{:S(2)}) %collective-permute-start.9) | collective-permute-done | bytes 262176 | tf_op jit(solution)/shard_map/ppermute | solution.py:127
  54.5 2.0 %stack.62 = bf16[8,32,1024]{2,0,1:T(8,128)(2,1)} concatenate(bf16[1,32,1024]{2,0,1:T(2,128)(2,1)S(1)} %get-tuple-element.47, bf16[1,32,1024]{2,0,1:T(2,128)(2,1)S(1)} %get-tuple-element.59, bf16[1,32,1024]{2,0,1:T(2,128)(2,1)S(1)} %get-tuple-element.63, bf16[1,32,1024]{2,0,1:T(2,128)(2,1)S(1)} %get-tuple-element.62, bf16[4,32,1024]{2,0,1:T(4,128)(2,1)S(1)} %collective-permute-done.9), dimensions={0} | concatenate | bytes 1048576 | tf_op jit(solution)/shard_map/stack | solution.py:136
  56.5 1.4 convolution_convert_fusion.1
  57.9 1.1 copy.64
  59.0 1.6 collective-permute-start.10
  69.0 3.0 %collective-permute-done.10 = bf16[1,256,1024]{2,1,0:T(8,128)(2,1)} collective-permute-done((bf16[1,256,1024]{2,1,0:T(8,128)(2,1)}, bf16[1,256,1024]{2,1,0:T(8,128)(2,1)}, u32[]{:S(2)}, u32[]{:S(2)}) %collective-permute-start.10) | collective-permute-done | bytes 524320 | tf_op jit(solution)/shard_map/ppermute | solution.py:69
  72.0 1.3 pad_maximum_fusion.5
  74.8 1.6 pad_maximum_fusion
  76.4 1.4 pad_maximum_fusion.2
  77.8 1.7 dynamic-slice_bitcast_fusion.3
  79.5 1.3 slice-done.1
  80.8 3.2 %fusion.16 = bf16[256,1024]{1,0:T(8,128)(2,1)} fusion(bf16[1024,4096]{1,0:T(8,128)(2,1)S(1)} %bitcast.178, bf16[256,1024]{1,0:T(8,128)(2,1)S(1)} %get-tuple-element.25, bf16[256,1024]{1,0:T(8,128)(2,1)S(1)} %get-tuple-element.26, bf16[256,1024]{1,0:T(8,128)(2,1)S(1)} %get-tuple-element.27, bf16[256,1024]{1,0:T(8,128)(2,1)S(1)} %get-tuple-element.24), kind=kOutput, calls=%fused_computation.30 | convolution fusion | flops 2156134400 | bytes 11010048 | tf_op jit(solution)/shard_map/dot_general | solution.py:259
  84.0 2.1 %copy.65 = bf16[256,1024]{0,1:T(8,128)(2,1)} copy(bf16[256,1024]{1,0:T(8,128)(2,1)} %fusion.16) | data formatting | bytes 1048576 | tf_op jit(solution)/shard_map/convert_element_type | solution.py:264
  86.1 2.2 %fusion = f32[256]{0:T(256)S(1)} fusion(bf16[256,1024]{1,0:T(8,128)(2,1)} %get-tuple-element.90, bf16[256,1024]{1,0:T(8,128)(2,1)} %get-tuple-element.89, bf16[256,1024]{1,0:T(8,128)(2,1)} %get-tuple-element.88, bf16[256,1024]{1,0:T(8,128)(2,1)} %get-tuple-element.91), kind=kLoop, calls=%fused_computation.5 | loop fusion | flops 10485504 | bytes 2098176 | tf_op jit(solution)/shard_map/reduce_sum | solution.py:203
  88.9 1.8 convolution_convert_fusion.5
  90.7 1.1 fusion.65
  92.5 1.7 copy.96
  95.0 6.4 %convolution_bitcast_fusion = f32[32,8,8,128]{3,1,2,0:T(8,128)S(1)} fusion(bf16[4096,1024]{1,0:T(8,128)(2,1)} %param.15, f32[4096]{0:T(1024)S(1)} %copy-done.28, f32[256]{0:T(256)} %copy-done.33, bf16[256,1024]{1,0:T(8,128)(2,1)} %get-tuple-element.90, bf16[256,1024]{1,0:T(8,128)(2,1)} %get-tuple-element.89, bf16[256,1024]{1,0:T(8,128)(2,1)} %get-tuple-element.88, ...), kind=kOutput, calls=%fused_computation.27 | convolution fusion | flops 2159017984 | bytes 11551744 | tf_op jit(solution)/shard_map/dot_general | solution.py:205
  103.1 0.9 fusion.15
  104.0 0.9 multiply_reduce_fusion
  107.0 1.7 slice-done.3
  108.7 2.4 %fusion.80 = f32[256,4096]{1,0:T(8,128)S(1)} fusion(bf16[256,1024]{0,1:T(8,128)(2,1)S(1)} %bitcast.191, bf16[1024,4096]{1,0:T(8,128)(2,1)S(1)} %bitcast.180), kind=kOutput, calls=%fused_computation.151 | convolution fusion | flops 2147483648 | bytes 13107200 | tf_op jit(solution)/shard_map/dot_general | solution.py:233
  111.3 1.4 pad_maximum_fusion.4
  112.6 0.9 copy-done.1
  114.9 1.8 convolution_multiply_fusion
  116.7 1.1 fusion.71
  117.8 2.4 %copy.98 = f32[256,8,64]{2,1,0:T(8,128)} copy(f32[256,8,64]{0,2,1:T(8,128)} %get-tuple-element.34) | data formatting | bytes 1048576
  120.2 2.4 %copy.97 = f32[256,8,64]{2,1,0:T(8,128)} copy(f32[256,8,64]{0,2,1:T(8,128)} %get-tuple-element.35) | data formatting | bytes 1048576
  122.6 2.0 add_convert_fusion
  125.4 1.2 fusion.34
  126.6 1.7 collective-permute-start.3
  128.3 5.7 %fusion.36 = f32[256,4096]{1,0:T(8,128)S(1)} fusion(bf16[4096,1024]{1,0:T(8,128)(2,1)} %param.15, bf16[32,8,8,128]{3,2,1,0:T(8,128)(2,1)S(1)} %bitcast.192), kind=kOutput, calls=%fused_computation.75 | convolution fusion | flops 2147483648 | bytes 13107200 | tf_op jit(solution)/shard_map/dot_general | solution.py:292
  134.0 6.5 %collective-permute-done.3 = bf16[1,256,1024]{2,1,0:T(8,128)(2,1)S(1)} collective-permute-done((bf16[1,256,1024]{2,1,0:T(8,128)(2,1)S(1)}, bf16[1,256,1024]{2,1,0:T(8,128)(2,1)S(1)}, u32[]{:S(2)}, u32[]{:S(2)}) %collective-permute-start.3) | collective-permute-done | bytes 524320 | tf_op jit(solution)/shard_map/ppermute | solution.py:103
  140.5 1.4 fusion.22
  142.3 0.9 fusion.73
  143.8 1.7 collective-permute-start.4
  146.3 4.9 %collective-permute-done.4 = bf16[4,32,1024]{2,0,1:T(4,128)(2,1)S(1)} collective-permute-done((bf16[4,32,1024]{2,0,1:T(4,128)(2,1)S(1)}, bf16[4,32,1024]{2,0,1:T(4,128)(2,1)S(1)}, u32[]{:S(2)}, u32[]{:S(2)}) %collective-permute-start.4) | collective-permute-done | bytes 262176 | tf_op jit(solution)/shard_map/ppermute | solution.py:127
  151.7 0.9 pad_maximum_fusion.10
  152.6 1.9 collective-permute-start.5
  155.2 4.0 %collective-permute-done.5 = bf16[4,32,1024]{2,0,1:T(4,128)(2,1)S(1)} collective-permute-done((bf16[4,32,1024]{2,0,1:T(4,128)(2,1)S(1)}, bf16[4,32,1024]{2,0,1:T(4,128)(2,1)S(1)}, u32[]{:S(2)}, u32[]{:S(2)}) %collective-permute-start.5) | collective-permute-done | bytes 262176 | tf_op jit(solution)/shard_map/ppermute | solution.py:127
  159.2 1.0 fusion.77
  160.9 3.4 %collective-permute-start.6 = (bf16[4,32,1024]{2,0,1:T(4,128)(2,1)S(1)}, bf16[4,32,1024]{2,0,1:T(4,128)(2,1)}, u32[]{:S(2)}, u32[]{:S(2)}) collective-permute-start(bf16[4,32,1024]{2,0,1:T(4,128)(2,1)S(1)} %pad_maximum_fusion.11), channel_id=1, source_target_pairs={{0,16},{4,20},{8,24},{12,28},{16,0},{20,4},{24,8},{28,12},{1,17},{... | collective-permute-start | bytes 786440 | tf_op jit(solution)/shard_map/ppermute | solution.py:127
  164.3 3.8 %fusion.3 = (f32[256]{0:T(256)}, f32[256,4096]{1,0:T(8,128)}) fusion(f32[4096]{0:T(1024)S(1)} %copy-done.28, bf16[256,1024]{1,0:T(8,128)(2,1)S(1)} %copy-done.11, bf16[256,1024]{1,0:T(8,128)(2,1)S(1)} %copy-done.9, bf16[256,1024]{1,0:T(8,128)(2,1)S(1)} %copy-done.7, bf16[256,1024]{1,0:T(8,128)(2,1)S(1)} %copy-done.13, ...), kind=kOutput, calls=%fused_computation.8 | convolution fusion | flops 549453568 | bytes 12731392 | tf_op jit(solution)/shard_map/dot_general | solution.py:304
  168.1 6.0 %collective-permute-done.6 = bf16[4,32,1024]{2,0,1:T(4,128)(2,1)} collective-permute-done((bf16[4,32,1024]{2,0,1:T(4,128)(2,1)S(1)}, bf16[4,32,1024]{2,0,1:T(4,128)(2,1)}, u32[]{:S(2)}, u32[]{:S(2)}) %collective-permute-start.6) | collective-permute-done | bytes 262176 | tf_op jit(solution)/shard_map/ppermute | solution.py:127
  174.1 3.5 %stack.58 = bf16[8,32,1024]{2,0,1:T(8,128)(2,1)} concatenate(bf16[1,32,1024]{2,0,1:T(2,128)(2,1)S(1)} %get-tuple-element.55, bf16[1,32,1024]{2,0,1:T(2,128)(2,1)S(1)} %get-tuple-element.67, bf16[1,32,1024]{2,0,1:T(2,128)(2,1)} %get-tuple-element.71, bf16[1,32,1024]{2,0,1:T(2,128)(2,1)S(1)} %get-tuple-element.70, bf16[4,32,1024]{2,0,1:T(4,128)(2,1)} %collective-permute-done.6), dimensions={0} | concatenate | bytes 1048576 | tf_op jit(solution)/shard_map/stack | solution.py:136
  177.6 1.4 convolution_convert_fusion.3
  179.0 1.1 copy.62
  180.1 1.8 fusion.32
  182.2 2.6 %collective-permute-done.12 = bf16[2,256,1024]{2,1,0:T(8,128)(2,1)S(1)} collective-permute-done((bf16[2,256,1024]{2,1,0:T(8,128)(2,1)S(1)}, bf16[2,256,1024]{2,1,0:T(8,128)(2,1)S(1)}, u32[]{:S(2)}, u32[]{:S(2)}) %collective-permute-start.12) | collective-permute-done | bytes 1048608 | tf_op jit(solution)/shard_map/ppermute | solution.py:105
  185.0 1.6 collective-permute-start.13
  186.6 1.1 collective-permute-done.14
  188.5 10.5 %collective-permute-done.15 = f32[256]{0:T(256)S(1)} collective-permute-done((f32[256]{0:T(256)S(1)}, f32[256]{0:T(256)S(1)}, u32[]{:S(2)}, u32[]{:S(2)}) %collective-permute-start.15) | collective-permute-done | bytes 1056 | tf_op jit(solution)/shard_map/ppermute | solution.py:105
  199.1 1.3 fusion.25
  (144 shorter events, 18.3 us)
Async XLA Ops:
  0.6 88.2 %copy-start = (bf16[4096,256]{1,0:T(8,128)(2,1)S(1)}, bf16[4096,256]{1,0:T(8,128)(2,1)}, u32[]{:S(2)}) copy-start(bf16[4096,256]{1,0:T(8,128)(2,1)} %param.17) | copy-start | bytes 6291460
  0.6 20.5 %copy-start.22 = (bf16[256,1024]{1,0:T(8,128)(2,1)S(1)}, bf16[256,1024]{1,0:T(8,128)(2,1)}, u32[]{:S(2)}) copy-start(bf16[256,1024]{1,0:T(8,128)(2,1)} %param.19) | copy-start | bytes 1572868
  0.7 15.2 %collective-permute-start = (bf16[1,256,1024]{2,1,0:T(8,128)(2,1)}, bf16[1,256,1024]{2,1,0:T(8,128)(2,1)S(1)}, u32[]{:S(2)}, u32[]{:S(2)}) collective-permute-start(bf16[1,256,1024]{2,1,0:T(8,128)(2,1)} %bitcast.182), channel_id=1, source_target_pairs={{0,2},{1,3},{2,0},{3,1},{4,6},{5,7},{6,4},{7,5},{8,10},{9,11},{10,... | collective-permute-start | bytes 1572872 | tf_op jit(solution)/shard_map/ppermute | solution.py:69
  15.8 5.3 %copy-start.16 = (bf16[1,256,1024]{2,1,0:T(8,128)(2,1)}, bf16[1,256,1024]{2,1,0:T(8,128)(2,1)S(1)}, u32[]{:S(2)}) copy-start(bf16[1,256,1024]{2,1,0:T(8,128)(2,1)S(1)} %collective-permute-done) | copy-start | bytes 1572868
  18.1 3.0 %collective-permute-start.1 = (bf16[2,256,1024]{2,1,0:T(8,128)(2,1)}, bf16[2,256,1024]{2,1,0:T(8,128)(2,1)}, u32[]{:S(2)}, u32[]{:S(2)}) collective-permute-start(bf16[2,256,1024]{2,1,0:T(8,128)(2,1)} %pad_maximum_fusion.3), channel_id=1, source_target_pairs={{0,1},{1,0},{2,3},{3,2},{4,5},{5,4},{6,7},{7,6},{8,9},{9,8},{10,11... | collective-permute-start | bytes 3145736 | tf_op jit(solution)/shard_map/ppermute | solution.py:69
  18.1 3.0 %copy-start.30 = (s32[8]{0:T(128)}, s32[8]{0:T(128)S(1)}, u32[]{:S(2)}) copy-start(s32[8]{0:T(128)S(1)} %iota_xor_fusion) | copy-start | bytes 100
  23.1 8.4 %collective-permute-start.7 = (bf16[4,32,1024]{2,0,1:T(4,128)(2,1)S(1)}, bf16[4,32,1024]{2,0,1:T(4,128)(2,1)S(1)}, u32[]{:S(2)}, u32[]{:S(2)}) collective-permute-start(bf16[4,32,1024]{2,0,1:T(4,128)(2,1)S(1)} %pad_maximum_fusion.12), channel_id=1, source_target_pairs={{0,4},{4,0},{8,12},{12,8},{16,20},{20,16},{24,28},{28,24},{1,5},{5... | collective-permute-start | bytes 786440 | tf_op jit(solution)/shard_map/ppermute | solution.py:127
  32.5 7.6 %collective-permute-start.8 = (bf16[4,32,1024]{2,0,1:T(4,128)(2,1)S(1)}, bf16[4,32,1024]{2,0,1:T(4,128)(2,1)S(1)}, u32[]{:S(2)}, u32[]{:S(2)}) collective-permute-start(bf16[4,32,1024]{2,0,1:T(4,128)(2,1)S(1)} %pad_maximum_fusion.13), channel_id=1, source_target_pairs={{0,8},{4,12},{8,0},{12,4},{16,24},{20,28},{24,16},{28,20},{1,9},{5... | collective-permute-start | bytes 786440 | tf_op jit(solution)/shard_map/ppermute | solution.py:127
  40.5 20.1 %copy-start.29 = (s32[4]{0:T(128)S(1)}, s32[4]{0:T(128)}, u32[]{:S(2)}) copy-start(s32[4]{0:T(128)} %constant.72.clone) | copy-start | bytes 52
  40.5 25.8 %copy-start.37 = (s32[1,2]{1,0:T(1,128)S(1)}, s32[1,2]{1,0:T(1,128)}, u32[]{:S(2)}) copy-start(s32[1,2]{1,0:T(1,128)} %param.20) | copy-start | bytes 28
  41.2 13.3 %collective-permute-start.9 = (bf16[4,32,1024]{2,0,1:T(4,128)(2,1)S(1)}, bf16[4,32,1024]{2,0,1:T(4,128)(2,1)S(1)}, u32[]{:S(2)}, u32[]{:S(2)}) collective-permute-start(bf16[4,32,1024]{2,0,1:T(4,128)(2,1)S(1)} %pad_maximum_fusion.14), channel_id=1, source_target_pairs={{0,16},{4,20},{8,24},{12,28},{16,0},{20,4},{24,8},{28,12},{1,17},{... | collective-permute-start | bytes 786440 | tf_op jit(solution)/shard_map/ppermute | solution.py:127
  56.5 18.3 %copy-start.3 = (bf16[256,1024]{1,0:T(8,128)(2,1)S(1)}, bf16[256,1024]{1,0:T(8,128)(2,1)}, u32[]{:S(2)}) copy-start(bf16[256,1024]{1,0:T(8,128)(2,1)} %param.13) | copy-start | bytes 1572868
  59.0 13.0 %collective-permute-start.10 = (bf16[1,256,1024]{2,1,0:T(8,128)(2,1)}, bf16[1,256,1024]{2,1,0:T(8,128)(2,1)}, u32[]{:S(2)}, u32[]{:S(2)}) collective-permute-start(bf16[1,256,1024]{2,1,0:T(8,128)(2,1)} %bitcast.37), channel_id=1, source_target_pairs={{0,2},{1,3},{2,0},{3,1},{4,6},{5,7},{6,4},{7,5},{8,10},{9,11},{10,... | collective-permute-start | bytes 1572872 | tf_op jit(solution)/shard_map/ppermute | solution.py:69
  69.0 5.8 %copy-start.17 = (bf16[1,256,1024]{2,1,0:T(8,128)(2,1)S(1)}, bf16[1,256,1024]{2,1,0:T(8,128)(2,1)}, u32[]{:S(2)}) copy-start(bf16[1,256,1024]{2,1,0:T(8,128)(2,1)} %copy-done.16) | copy-start | bytes 1572868
  73.3 3.1 %collective-permute-start.11 = (bf16[2,256,1024]{2,1,0:T(8,128)(2,1)S(1)}, bf16[2,256,1024]{2,1,0:T(8,128)(2,1)S(1)}, u32[]{:S(2)}, u32[]{:S(2)}) collective-permute-start(bf16[2,256,1024]{2,1,0:T(8,128)(2,1)S(1)} %pad_maximum_fusion.5), channel_id=1, source_target_pairs={{0,1},{1,0},{2,3},{3,2},{4,5},{5,4},{6,7},{7,6},{8,9},{9,8},{10,11... | collective-permute-start | bytes 3145736 | tf_op jit(solution)/shard_map/ppermute | solution.py:69
  74.8 4.7 %slice-start = ((s8[8388608]{0:T(1024)(128)(4,1)}), s8[4194304]{0:T(1024)(128)(4,1)S(1)}, s32[]{:S(2)}) async-start(s8[8388608]{0:T(1024)(128)(4,1)} %bitcast.177), calls=%async_computation | async-start | bytes 8388608
  77.8 2.9 %slice-start.1 = ((s8[8388608]{0:T(1024)(128)(4,1)}), s8[4194304]{0:T(1024)(128)(4,1)S(1)}, s32[]{:S(2)}) async-start(s8[8388608]{0:T(1024)(128)(4,1)} %bitcast.177), calls=%async_computation.1 | async-start | bytes 8388608
  84.0 4.9 %copy-start.28 = (f32[4096]{0:T(1024)S(1)}, f32[4096]{0:T(1024)}, u32[]{:S(2)}) copy-start(f32[4096]{0:T(1024)} %param.14) | copy-start | bytes 49156
  86.0 2.8 %copy-start.6 = (bf16[256,1024]{1,0:T(8,128)(2,1)S(1)}, bf16[256,1024]{1,0:T(8,128)(2,1)}, u32[]{:S(2)}) copy-start(bf16[256,1024]{1,0:T(8,128)(2,1)} %get-tuple-element.88) | copy-start | bytes 1572868
  86.0 2.8 %copy-start.8 = (bf16[256,1024]{1,0:T(8,128)(2,1)S(1)}, bf16[256,1024]{1,0:T(8,128)(2,1)}, u32[]{:S(2)}) copy-start(bf16[256,1024]{1,0:T(8,128)(2,1)} %get-tuple-element.89) | copy-start | bytes 1572868
  86.1 2.8 %copy-start.10 = (bf16[256,1024]{1,0:T(8,128)(2,1)S(1)}, bf16[256,1024]{1,0:T(8,128)(2,1)}, u32[]{:S(2)}) copy-start(bf16[256,1024]{1,0:T(8,128)(2,1)} %get-tuple-element.90) | copy-start | bytes 1572868
  86.1 2.8 %copy-start.12 = (bf16[256,1024]{1,0:T(8,128)(2,1)S(1)}, bf16[256,1024]{1,0:T(8,128)(2,1)}, u32[]{:S(2)}) copy-start(bf16[256,1024]{1,0:T(8,128)(2,1)} %get-tuple-element.91) | copy-start | bytes 1572868
  88.8 1.9 copy-start.33
  88.8 1.8 copy-start.14
  101.7 1.0 copy-start.18
  101.7 1.0 copy-start.19
  102.2 0.9 copy-start.26
  102.7 1.3 copy-start.20
  102.7 1.3 copy-start.38
  102.8 2.1 %copy-start.23 = (bf16[256,2,64]{2,0,1:T(8,128)(2,1)}, bf16[256,2,64]{2,0,1:T(8,128)(2,1)S(1)}, u32[]{:S(2)}) copy-start(bf16[256,2,64]{2,0,1:T(8,128)(2,1)S(1)} %get-tuple-element.36) | copy-start | bytes 196612
  102.8 2.1 %copy-start.24 = (bf16[256,2,64]{2,0,1:T(8,128)(2,1)}, bf16[256,2,64]{2,0,1:T(8,128)(2,1)S(1)}, u32[]{:S(2)}) copy-start(bf16[256,2,64]{2,0,1:T(8,128)(2,1)S(1)} %get-tuple-element.37) | copy-start | bytes 196612
  103.9 1.4 copy-start.39
  103.9 1.4 copy-start.41
  104.0 3.1 %slice-start.2 = ((s8[8388608]{0:T(1024)(128)(4,1)}), s8[4194304]{0:T(1024)(128)(4,1)S(1)}, s32[]{:S(2)}) async-start(s8[8388608]{0:T(1024)(128)(4,1)} %bitcast.179), calls=%async_computation.2 | async-start | bytes 8388608
  105.3 3.4 %slice-start.3 = ((s8[8388608]{0:T(1024)(128)(4,1)}), s8[4194304]{0:T(1024)(128)(4,1)S(1)}, s32[]{:S(2)}) async-start(s8[8388608]{0:T(1024)(128)(4,1)} %bitcast.179), calls=%async_computation.3 | async-start | bytes 8388608
  106.1 1.0 copy-start.4
  111.1 2.4 %copy-start.1 = (f32[256,4096]{1,0:T(8,128)}, f32[256,4096]{1,0:T(8,128)S(1)}, u32[]{:S(2)}) copy-start(f32[256,4096]{1,0:T(8,128)S(1)} %fusion.80) | copy-start | bytes 12582916
  113.5 11.3 %collective-permute-start.2 = (bf16[2,256,1024]{2,1,0:T(8,128)(2,1)}, bf16[2,256,1024]{2,1,0:T(8,128)(2,1)}, u32[]{:S(2)}, u32[]{:S(2)}) collective-permute-start(bf16[2,256,1024]{2,1,0:T(8,128)(2,1)} %pad_maximum_fusion.4), channel_id=1, source_target_pairs={{0,1},{1,0},{2,3},{3,2},{4,5},{5,4},{6,7},{7,6},{8,9},{9,8},{10,11... | collective-permute-start | bytes 3145736 | tf_op jit(solution)/shard_map/ppermute | solution.py:103
  122.6 2.8 %copy-start.2 = (f32[256,4096]{1,0:T(8,128)S(1)}, f32[256,4096]{1,0:T(8,128)}, u32[]{:S(2)}) copy-start(f32[256,4096]{1,0:T(8,128)} %copy-done.1) | copy-start | bytes 12582916
  126.6 13.9 %collective-permute-start.3 = (bf16[1,256,1024]{2,1,0:T(8,128)(2,1)S(1)}, bf16[1,256,1024]{2,1,0:T(8,128)(2,1)S(1)}, u32[]{:S(2)}, u32[]{:S(2)}) collective-permute-start(bf16[1,256,1024]{2,1,0:T(8,128)(2,1)S(1)} %fusion.34), channel_id=1, source_target_pairs={{0,2},{1,3},{2,0},{3,1},{4,6},{5,7},{6,4},{7,5},{8,10},{9,11},{10,... | collective-permute-start | bytes 1572872 | tf_op jit(solution)/shard_map/ppermute | solution.py:103
  134.0 7.9 %copy-start.31 = (s32[8]{0:T(128)S(1)}, s32[8]{0:T(128)}, u32[]{:S(2)}) copy-start(s32[8]{0:T(128)} %copy-done.30) | copy-start | bytes 100
  134.0 7.9 %copy-start.35 = (s32[8]{0:T(128)S(1)}, s32[8]{0:T(128)}, u32[]{:S(2)}) copy-start(s32[8]{0:T(128)} %get-tuple-element.17) | copy-start | bytes 100
  141.8 3.6 %copy-start.15 = (bf16[4096,256]{1,0:T(8,128)(2,1)S(1)}, bf16[4096,256]{1,0:T(8,128)(2,1)}, u32[]{:S(2)}) copy-start(bf16[4096,256]{1,0:T(8,128)(2,1)} %param.16) | copy-start | bytes 6291460
  141.9 3.6 %copy-start.25 = (bf16[256,2,128]{0,2,1:T(8,128)(2,1)S(1)}, bf16[256,2,128]{0,2,1:T(8,128)(2,1)}, u32[]{:S(2)}) copy-start(bf16[256,2,128]{0,2,1:T(8,128)(2,1)} %copy.75) | copy-start | bytes 393220
  143.8 7.4 %collective-permute-start.4 = (bf16[4,32,1024]{2,0,1:T(4,128)(2,1)S(1)}, bf16[4,32,1024]{2,0,1:T(4,128)(2,1)S(1)}, u32[]{:S(2)}, u32[]{:S(2)}) collective-permute-start(bf16[4,32,1024]{2,0,1:T(4,128)(2,1)S(1)} %pad_maximum_fusion.9), channel_id=1, source_target_pairs={{0,4},{4,0},{8,12},{12,8},{16,20},{20,16},{24,28},{28,24},{1,5},{5... | collective-permute-start | bytes 786440 | tf_op jit(solution)/shard_map/ppermute | solution.py:127
  145.5 9.0 %copy-start.21 = (bf16[256,1024]{0,1:T(8,128)(2,1)S(1)}, bf16[256,1024]{0,1:T(8,128)(2,1)}, u32[]{:S(2)}) copy-start(bf16[256,1024]{0,1:T(8,128)(2,1)} %copy.65) | copy-start | bytes 1572868
  145.5 9.0 %copy-start.27 = (pred[256,256]{0,1:T(8,128)(4,1)S(1)}, pred[256,256]{0,1:T(8,128)(4,1)}, u32[]{:S(2)}) copy-start(pred[256,256]{0,1:T(8,128)(4,1)} %fusion.43) | copy-start | bytes 196612
  145.5 9.0 %copy-start.40 = (f32[2,256,256,4]{2,1,3,0:T(8,128)S(1)}, f32[2,256,256,4]{2,1,3,0:T(8,128)}, u32[]{:S(2)}) copy-start(f32[2,256,256,4]{2,1,3,0:T(8,128)} %copy-done.39) | copy-start | bytes 6291460
  145.5 9.0 %copy-start.42 = (f32[2,4,256]{2,1,0:T(4,128)S(1)}, f32[2,4,256]{2,1,0:T(4,128)}, u32[]{:S(2)}) copy-start(f32[2,4,256]{2,1,0:T(4,128)} %copy-done.41) | copy-start | bytes 24580
  152.5 11.8 %copy-start.7 = (bf16[256,1024]{1,0:T(8,128)(2,1)S(1)}, bf16[256,1024]{1,0:T(8,128)(2,1)}, u32[]{:S(2)}) copy-start(bf16[256,1024]{1,0:T(8,128)(2,1)} %get-tuple-element.88) | copy-start | bytes 1572868
  152.6 11.8 %copy-start.9 = (bf16[256,1024]{1,0:T(8,128)(2,1)S(1)}, bf16[256,1024]{1,0:T(8,128)(2,1)}, u32[]{:S(2)}) copy-start(bf16[256,1024]{1,0:T(8,128)(2,1)} %get-tuple-element.89) | copy-start | bytes 1572868
  152.6 11.7 %copy-start.11 = (bf16[256,1024]{1,0:T(8,128)(2,1)S(1)}, bf16[256,1024]{1,0:T(8,128)(2,1)}, u32[]{:S(2)}) copy-start(bf16[256,1024]{1,0:T(8,128)(2,1)} %get-tuple-element.90) | copy-start | bytes 1572868
  152.6 11.7 %copy-start.13 = (bf16[256,1024]{1,0:T(8,128)(2,1)S(1)}, bf16[256,1024]{1,0:T(8,128)(2,1)}, u32[]{:S(2)}) copy-start(bf16[256,1024]{1,0:T(8,128)(2,1)} %get-tuple-element.91) | copy-start | bytes 1572868
  152.6 6.6 %collective-permute-start.5 = (bf16[4,32,1024]{2,0,1:T(4,128)(2,1)S(1)}, bf16[4,32,1024]{2,0,1:T(4,128)(2,1)S(1)}, u32[]{:S(2)}, u32[]{:S(2)}) collective-permute-start(bf16[4,32,1024]{2,0,1:T(4,128)(2,1)S(1)} %pad_maximum_fusion.10), channel_id=1, source_target_pairs={{0,8},{4,12},{8,0},{12,4},{16,24},{20,28},{24,16},{28,20},{1,9},{5... | collective-permute-start | bytes 786440 | tf_op jit(solution)/shard_map/ppermute | solution.py:127
  160.9 13.2 %collective-permute-start.6 = (bf16[4,32,1024]{2,0,1:T(4,128)(2,1)S(1)}, bf16[4,32,1024]{2,0,1:T(4,128)(2,1)}, u32[]{:S(2)}, u32[]{:S(2)}) collective-permute-start(bf16[4,32,1024]{2,0,1:T(4,128)(2,1)S(1)} %pad_maximum_fusion.11), channel_id=1, source_target_pairs={{0,16},{4,20},{8,24},{12,28},{16,0},{20,4},{24,8},{28,12},{1,17},{... | collective-permute-start | bytes 786440 | tf_op jit(solution)/shard_map/ppermute | solution.py:127
  180.1 4.7 %copy-start.5 = (f32[256,4096]{1,0:T(8,128)S(1)}, f32[256,4096]{1,0:T(8,128)}, u32[]{:S(2)}) copy-start(f32[256,4096]{1,0:T(8,128)} %get-tuple-element.13) | copy-start | bytes 12582916
  181.9 4.6 %copy-start.36 = (f32[256]{0:T(256)S(1)}, f32[256]{0:T(256)}, u32[]{:S(2)}) copy-start(f32[256]{0:T(256)} %get-tuple-element.86) | copy-start | bytes 3076
  182.0 17.0 %dynamic-slice-start = ((f32[4096]{0:T(1024)}, s32[]{:T(128)}), f32[1024]{0:T(1024)S(1)}, s32[]{:S(2)}) async-start(f32[4096]{0:T(1024)} %param.14, s32[]{:T(128)} %select_n.80), calls=%async_computation.4 | async-start | bytes 8704 | tf_op jit(solution)/shard_map/dynamic_slice | solution.py:164
  182.1 17.0 %copy-start.32 = (f32[256]{0:T(256)S(1)}, f32[256]{0:T(256)}, u32[]{:S(2)}) copy-start(f32[256]{0:T(256)} %get-tuple-element.76) | copy-start | bytes 3076
  182.1 17.0 %copy-start.34 = (f32[256]{0:T(256)S(1)}, f32[256]{0:T(256)}, u32[]{:S(2)}) copy-start(f32[256]{0:T(256)} %copy-done.33) | copy-start | bytes 3076
  182.1 2.7 %collective-permute-start.12 = (bf16[2,256,1024]{2,1,0:T(8,128)(2,1)S(1)}, bf16[2,256,1024]{2,1,0:T(8,128)(2,1)S(1)}, u32[]{:S(2)}, u32[]{:S(2)}) collective-permute-start(bf16[2,256,1024]{2,1,0:T(8,128)(2,1)S(1)} %pad_maximum_fusion.6), channel_id=1, source_target_pairs={{0,1},{1,0},{2,3},{3,2},{4,5},{5,4},{6,7},{7,6},{8,9},{9,8},{10,11... | collective-permute-start | bytes 3145736 | tf_op jit(solution)/shard_map/ppermute | solution.py:105
  185.0 14.1 %collective-permute-start.13 = (bf16[1,256,1024]{2,1,0:T(8,128)(2,1)S(1)}, bf16[1,256,1024]{2,1,0:T(8,128)(2,1)S(1)}, u32[]{:S(2)}, u32[]{:S(2)}) collective-permute-start(bf16[1,256,1024]{2,1,0:T(8,128)(2,1)S(1)} %fusion.35), channel_id=1, source_target_pairs={{0,2},{1,3},{2,0},{3,1},{4,6},{5,7},{6,4},{7,5},{8,10},{9,11},{10,... | collective-permute-start | bytes 1572872 | tf_op jit(solution)/shard_map/ppermute | solution.py:105
  186.6 1.1 collective-permute-start.14
  187.7 11.3 %collective-permute-start.15 = (f32[256]{0:T(256)S(1)}, f32[256]{0:T(256)S(1)}, u32[]{:S(2)}, u32[]{:S(2)}) collective-permute-start(f32[256]{0:T(256)S(1)} %add.155), channel_id=1, source_target_pairs={{0,2},{1,3},{2,0},{3,1},{4,6},{5,7},{6,4},{7,5},{8,10},{9,11},{10,... | collective-permute-start | bytes 3080 | tf_op jit(solution)/shard_map/ppermute | solution.py:105

commit v5 on v4

--- a/solution.py
+++ b/solution.py
@@ -59,16 +59,14 @@
     return [(i, i ^ bit) for i in range(size)]
 
 
-def gather_features(shard, axis_name, size, position, tied=None):
+def gather_features(shard, axis_name, size, position):
     if not _is_pow2(size):
-        return lax.all_gather(shard, axis_name, axis=1, tiled=True), tied
+        return lax.all_gather(shard, axis_name, axis=1, tiled=True)
     held = shard[None]
     masks = [0]
     bit = size >> 1
     while bit:
         incoming = lax.ppermute(held, axis_name, _xor_pairs(size, bit))
-        if tied is not None:
-            incoming, tied = lax.optimization_barrier((incoming, tied))
         held = jnp.concatenate([held, incoming], axis=0)
         masks = masks + [m ^ bit for m in masks]
         bit >>= 1
@@ -77,7 +75,7 @@
         lax.dynamic_index_in_dim(held, table[s ^ position], axis=0, keepdims=False)
         for s in range(size)
     ]
-    return jnp.concatenate(blocks, axis=1), tied
+    return jnp.concatenate(blocks, axis=1)
 
 
 def scatter_features(partial, axis_name, size, position, extra=None):
@@ -113,31 +111,6 @@
     return held[0], extra
 
 
-def relay_blocks(blocks, select, place, axis_name, size):
-    held = jnp.einsum(
-        "mn,nrw->mrw", select, blocks, preferred_element_type=jnp.float32
-    ).astype(blocks.dtype)
-    items = [held[m] for m in range(size)]
-    dst = list(range(size))
-    src = [0] * size
-    bit = 1
-    while bit < size:
-        send = [k for k in range(len(items)) if dst[k] & bit]
-        keep = [k for k in range(len(items)) if not dst[k] & bit]
-        incoming = lax.ppermute(
-            jnp.stack([items[k] for k in send]), axis_name, _xor_pairs(size, bit)
-        )
-        items = [items[k] for k in keep] + [incoming[n] for n in range(len(send))]
-        dst, src = (
-            [dst[k] for k in keep] + [dst[k] ^ bit for k in send],
-            [src[k] for k in keep] + [src[k] ^ bit for k in send],
-        )
-        bit <<= 1
-    arrived = jnp.stack(items)
-    ordered = jnp.einsum("bk,krw->brw", place(src), arrived, preferred_element_type=jnp.float32)
-    return ordered.astype(blocks.dtype)
-
-
 def per_device(
     tokens,
     norm_gain,
@@ -170,22 +143,23 @@
     send_table = (owner_row[None, :] == slot_index[:, None]).astype(jnp.bfloat16)
 
     home_rows = token_row_count // block_count
-    gathered, grad_output = gather_features(
-        tokens, "tensor", tensor_size, tensor_index, tied=grad_output
-    )
     owned_blocks = grad_output.reshape(block_count, home_rows, width_part)
-    if _is_pow2(sources) and sources <= 16 and block_count == sources:
-        mask_index = jnp.arange(sources, dtype=jnp.int32)
-        pick_home = (
-            (mask_index[:, None] ^ data_index) == jnp.arange(block_count)[None, :]
+    if sources <= 16:
+        returned = [lax.dynamic_index_in_dim(owned_blocks, data_index, 0, keepdims=False)]
+        for shift in range(1, sources):
+            pairs = [(a, (a + shift) % sources) for a in range(sources)]
+            piece = lax.dynamic_index_in_dim(
+                owned_blocks, (data_index + shift) % sources, 0, keepdims=False
+            )
+            returned.append(lax.ppermute(piece, "dp", pairs))
+        returned = jnp.stack(returned)
+        came_over = (
+            ((data_index - owner_row) % sources)[:, None] == slot_index[None, :]
         ).astype(jnp.bfloat16)
-
-        def home_order(source_masks):
-            masks = jnp.asarray(source_masks, jnp.int32)
-            return ((owner_row[:, None] ^ data_index) == masks[None, :]).astype(jnp.bfloat16)
-
-        grad_home = relay_blocks(owned_blocks, pick_home, home_order, "dp", sources).reshape(
-            token_row_count, width_part
+        grad_home = (
+            jnp.einsum("js,srw->jrw", came_over, returned, preferred_element_type=jnp.float32)
+            .astype(jnp.bfloat16)
+            .reshape(token_row_count, width_part)
         )
     else:
         arrived = lax.all_to_all(
@@ -199,6 +173,7 @@
             .reshape(token_row_count, width_part)
         )
 
+    gathered = lax.all_gather(tokens, "tensor", axis=1, tiled=True)
     gathered_float = gathered.astype(jnp.float32)
     inverse = lax.rsqrt(jnp.mean(gathered_float * gathered_float, axis=1) + NORM_EPSILON)
     normed_input = (gathered_float * inverse[:, None] * norm_gain[None, :]).astype(jnp.bfloat16)
@@ -233,19 +208,63 @@
     mixed_partial = jnp.dot(attended_flat, w_out, preferred_element_type=jnp.float32)
     mixed, _ = scatter_features(mixed_partial, "tensor", tensor_size, tensor_index)
     output_home = (x_float + mixed).astype(jnp.bfloat16)
+    grad_full = lax.all_gather(grad_home, "tensor", axis=1, tiled=True)
+    attended_gradient = lax.dot_general(
+        grad_full,
+        w_out,
+        (((1,), (1,)), ((), ())),
+        preferred_element_type=jnp.float32,
+    ).astype(jnp.bfloat16)
+    grouped_gradient = attended_gradient.reshape(
+        token_row_count, kv_local, query_group_width, HEAD_SIZE
+    )
+    delta = jnp.sum(grouped_gradient.astype(jnp.float32) * attended.astype(jnp.float32), axis=-1)
+    grad_probs = jnp.einsum(
+        "qkgd,skd->kgqs", grouped_gradient, value_rows, preferred_element_type=jnp.float32
+    )
+    grad_scores = (probs * (grad_probs - jnp.transpose(delta, (1, 2, 0))[..., None])).astype(
+        jnp.bfloat16
+    )
+    grad_query_rot = (
+        jnp.einsum("kgqs,skd->qkgd", grad_scores, keys, preferred_element_type=jnp.float32)
+        * scale_factor
+    )
+    grad_keys_rot = (
+        jnp.einsum("kgqs,qkgd->skd", grad_scores, grouped_query, preferred_element_type=jnp.float32)
+        * scale_factor
+    )
+    value_gradient = jnp.einsum(
+        "kgqs,qkgd->skd", probs_low, grouped_gradient, preferred_element_type=jnp.float32
+    )
+    grad_query = unrotate(
+        grad_query_rot.reshape(token_row_count, heads_local, HEAD_SIZE), cosine, sine_table
+    ).astype(jnp.bfloat16)
+    key_gradient = unrotate(grad_keys_rot, cosine, sine_table).astype(jnp.bfloat16)
+    output_home, grad_query, key_gradient, value_gradient = lax.optimization_barrier(
+        (output_home, grad_query, key_gradient, value_gradient)
+    )
     home_blocks = output_home.reshape(block_count, home_rows, width_part)
-    if _is_pow2(sources) and sources <= 16 and block_count == sources:
-        mask_index = jnp.arange(sources, dtype=jnp.int32)
-        pick_owner = (owner_row[None, :] == (mask_index[:, None] ^ data_index)).astype(
-            jnp.bfloat16
-        )
-
-        def owner_order(source_masks):
-            masks = jnp.asarray(source_masks, jnp.int32)
-            return ((mask_index[:, None] ^ data_index) == masks[None, :]).astype(jnp.bfloat16)
-
-        relaid = relay_blocks(home_blocks, pick_owner, owner_order, "dp", sources).reshape(
-            token_row_count, width_part
+    if sources <= 16:
+        block_for = jnp.sum(
+            jnp.where(send_table > 0, jnp.arange(block_count, dtype=jnp.int32)[None, :], 0), axis=1
+        )
+        landed = [
+            lax.dynamic_index_in_dim(home_blocks, block_for[data_index], 0, keepdims=False)
+        ]
+        for shift in range(1, sources):
+            pairs = [(a, (a + shift) % sources) for a in range(sources)]
+            piece = lax.dynamic_index_in_dim(
+                home_blocks, block_for[(data_index + shift) % sources], 0, keepdims=False
+            )
+            landed.append(lax.ppermute(piece, "dp", pairs))
+        landed = jnp.stack(landed)
+        came_over = (
+            ((data_index - slot_index) % sources)[:, None] == slot_index[None, :]
+        ).astype(jnp.bfloat16)
+        relaid = (
+            jnp.einsum("bs,srw->brw", came_over, landed, preferred_element_type=jnp.float32)
+            .astype(jnp.bfloat16)
+            .reshape(token_row_count, width_part)
         )
     else:
         outgoing = jnp.dot(
@@ -255,38 +274,6 @@
             token_row_count, width_part
         )
 
-    grad_full, _ = gather_features(grad_home, "tensor", tensor_size, tensor_index)
-    attended_gradient = lax.dot_general(
-        grad_full,
-        w_out,
-        (((1,), (1,)), ((), ())),
-        preferred_element_type=jnp.float32,
-    ).astype(jnp.bfloat16)
-    grouped_gradient = attended_gradient.reshape(
-        token_row_count, kv_local, query_group_width, HEAD_SIZE
-    )
-    delta = jnp.sum(grouped_gradient.astype(jnp.float32) * attended.astype(jnp.float32), axis=-1)
-    grad_probs = jnp.einsum(
-        "qkgd,skd->kgqs", grouped_gradient, value_rows, preferred_element_type=jnp.float32
-    )
-    grad_scores = (probs * (grad_probs - jnp.transpose(delta, (1, 2, 0))[..., None])).astype(
-        jnp.bfloat16
-    )
-    grad_query_rot = (
-        jnp.einsum("kgqs,skd->qkgd", grad_scores, keys, preferred_element_type=jnp.float32)
-        * scale_factor
-    )
-    grad_keys_rot = (
-        jnp.einsum("kgqs,qkgd->skd", grad_scores, grouped_query, preferred_element_type=jnp.float32)
-        * scale_factor
-    )
-    value_gradient = jnp.einsum(
-        "kgqs,qkgd->skd", probs_low, grouped_gradient, preferred_element_type=jnp.float32
-    )
-    grad_query = unrotate(
-        grad_query_rot.reshape(token_row_count, heads_local, HEAD_SIZE), cosine, sine_table
-    ).astype(jnp.bfloat16)
-    key_gradient = unrotate(grad_keys_rot, cosine, sine_table).astype(jnp.bfloat16)
     contract_out = (((1,), (1,)), ((), ()))
     normed_partial = (
         lax.dot_general(
@@ -309,7 +296,6 @@
         )
     )
     stat_partial = jnp.sum(normed_partial * norm_gain[None, :] * gathered_float, axis=1)
-    relaid, normed_partial = lax.optimization_barrier((relaid, normed_partial))
     normed_gradient, stat_sum = scatter_features(
         normed_partial, "tensor", tensor_size, tensor_index, extra=stat_partial
     )

time: 201 us -> 170 us (0.85)
  waiting for transfers between devices: 75.5 us -> 20.6 us
  between operations: 8.92 us -> 29.9 us
  starting transfers between devices: 22.5 us -> 29.3 us
  matrix products: 34.4 us -> 40.2 us
  local copies, waits for them, and re-layouts: 34.4 us -> 28.8 us
  other arithmetic: 24.6 us -> 20.3 us
    ppermute x10 -> x14, waiting for transfers between devices: 54.7 us -> 0.04 us  [the longest x7 0.02 us: per_device(): returned.append(lax.ppermute(piece, 'dp', pairs))]
    ppermute x4, waiting for transfers between devices: 14.3 us -> 0.01 us  [scatter_features(): lax.ppermute((outgoing, extra), axis_name, _xor_pairs(size, bit))]
    ppermute x10 -> x14, starting transfers between devices: 18.1 us -> 26 us  [the longest x7 13.8 us: per_device(): returned.append(lax.ppermute(piece, 'dp', pairs))]
    another operation x4 -> x18, local copies, waits for them, and re-layouts: 5.64 us -> 13.4 us  [the longest x8 7.64 us: per_device(): landed = jnp.stack(landed)]
    all_gather x0 -> x2, waiting for transfers between devices: none -> 6.93 us  [the longest x1 5.77 us: per_device(): grad_full = lax.all_gather(grad_home, 'tensor', axis=1, tiled=True)]
    concatenate x4 -> x0, other arithmetic: 6.6 us -> none  [gather_features(): held = jnp.concatenate([held, incoming], axis=0)]
    ppermute x2, waiting for transfers between devices: 6.46 us -> 13 us  [scatter_features(): incoming = lax.ppermute(outgoing, axis_name, _xor_pairs(size, bit))]
    slice x6 -> x0, local copies, waits for them, and re-layouts: 3.9 us -> none  [the longest x4 2.16 us: relay_blocks(): items = [items[k] for k in keep] + [incoming[n] for n in range(len(send))]]
  transfers between devices with their start and end apart: 16 -> 22, of which waited for: 13 -> 3; matrix products, arithmetic and copies ran while one was open for 14% -> 31% of each run, Pallas kernels for 0% -> 0%
where the time goes in v5:
time: 170 us; the launch traced here: 169 us
  matrix products  40.2 us (24%)
  between operations  29.9 us (18%)
  starting transfers between devices  29.3 us (17%)
  local copies, waits for them, and re-layouts  28.8 us (17%)
  waiting for transfers between devices  20.6 us (12%)
  other arithmetic  20.3 us (12%)
    ppermute x7, starting transfers between devices, per_device(): returned.append(lax.ppermute(piece, 'dp', pairs))  13.8 us
    ppermute x2, waiting for transfers between devices, scatter_features(): incoming = lax.ppermute(outgoing, axis_name, _xor_pairs(size, bit))  13 us
    ppermute x7, starting transfers between devices, per_device(): landed.append(lax.ppermute(piece, 'dp', pairs))  12.2 us
    unnamed x77, local copies, waits for them, and re-layouts  9.59 us
    another operation x8, local copies, waits for them, and re-layouts, per_device(): landed = jnp.stack(landed)  7.64 us
    dot_general x1, matrix products, per_device(): jnp.dot(normed_input, w_query, preferred_element_type=jnp.float32)  6.76 us
    dot_general x1, matrix products, per_device(): lax.dot_general(grad_full, w_out, (((1,), (1,)), ((), ())), preferred_ele...  6.38 us
    all_gather x1, waiting for transfers between devices, per_device(): grad_full = lax.all_gather(grad_home, 'tensor', axis=1, tiled=True)  5.77 us
  transfers between devices with their start and end apart: 22, of which 3 were waited for; matrix products, arithmetic and copies ran while one was open for 31% of the time, Pallas kernels for 0%

profile of v5, /device:TPU:0, one launch (start us, length us, event | category | flops | bytes accessed | tf_op | source)
XLA Modules:
  0.0 169.1 jit_solution(6182677509585979329)
XLA Ops:
  7.2 0.7 all-gather.3.cloned.1.call-update
  8.1 1.1 dynamic-slice_bitcast_fusion.7
  9.2 3.0 %collective-permute-start.2 = (bf16[32,1024]{1,0:T(8,128)(2,1)S(1)}, bf16[32,1024]{1,0:T(8,128)(2,1)S(1)}, u32[]{:S(2)}, u32[]{:S(2)}) collective-permute-start(bf16[32,1024]{1,0:T(8,128)(2,1)S(1)} %get-tuple-element.42), channel_id=1, source_target_pairs={{0,4},{4,8},{8,12},{12,16},{16,20},{20,24},{24,28},{28,0},{1,5},{5... | collective-permute-start | bytes 196616 | tf_op jit(solution)/shard_map/ppermute | solution.py:154
  12.2 1.6 collective-permute-start.3
  13.8 2.6 %collective-permute-start.4 = (bf16[32,1024]{1,0:T(8,128)(2,1)S(1)}, bf16[32,1024]{1,0:T(8,128)(2,1)S(1)}, u32[]{:S(2)}, u32[]{:S(2)}) collective-permute-start(bf16[32,1024]{1,0:T(8,128)(2,1)S(1)} %get-tuple-element.40), channel_id=1, source_target_pairs={{0,12},{4,16},{8,20},{12,24},{16,28},{20,0},{24,4},{28,8},{1,13},{... | collective-permute-start | bytes 196616 | tf_op jit(solution)/shard_map/ppermute | solution.py:154
  16.3 1.2 collective-permute-start.5
  17.6 2.6 %collective-permute-start.6 = (bf16[32,1024]{1,0:T(8,128)(2,1)S(1)}, bf16[32,1024]{1,0:T(8,128)(2,1)S(1)}, u32[]{:S(2)}, u32[]{:S(2)}) collective-permute-start(bf16[32,1024]{1,0:T(8,128)(2,1)S(1)} %get-tuple-element.38), channel_id=1, source_target_pairs={{0,20},{4,24},{8,28},{12,0},{16,4},{20,8},{24,12},{28,16},{1,21},{... | collective-permute-start | bytes 196616 | tf_op jit(solution)/shard_map/ppermute | solution.py:154
  20.2 0.8 reduce-window.8
  21.0 0.7 fusion.38
  22.4 1.4 collective-permute-start.7
  23.8 1.4 collective-permute-start.8
  25.2 1.2 and_select_fusion
  26.9 0.8 copy.74
  27.7 0.8 copy.75
  28.4 0.8 copy.76
  29.2 2.9 %stack.86 = bf16[8,32,1024]{2,0,1:T(8,128)(2,1)S(1)} concatenate(bf16[1,32,1024]{2,0,1:T(2,128)(2,1)S(1)} %copy.118, bf16[1,32,1024]{2,0,1:T(2,128)(2,1)S(1)} %copy.70, bf16[1,32,1024]{2,0,1:T(2,128)(2,1)S(1)} %copy.71, bf16[1,32,1024]{2,0,1:T(2,128)(2,1)S(1)} %copy.72, bf16[1,32,1024]{2,0,1:T(2,128)(2,1)S(1)} %copy.73, bf16[1,32,1024]{2,0,1:T(2,128)(2,1)} %copy.74, ...), dimensions={0} | concatenate | bytes 1048576 | tf_op jit(solution)/shard_map/stack | solution.py:155
  32.5 1.1 copy.77
  33.7 1.2 all-gather.3.cloned.1.call-done
  34.9 2.2 %fusion = f32[256]{0:T(256)S(1)} fusion(bf16[256,4096]{1,0:T(8,128)(2,1)} %all-gather.3.cloned.1.call-done), kind=kLoop, calls=%fused_computation.5 | loop fusion | flops 3145472 | bytes 2098176 | tf_op jit(solution)/shard_map/reduce_sum | solution.py:178
  37.7 2.8 %fusion.47 = f32[256,256]{0,1:T(8,128)S(1)} fusion(bf16[4096,256]{1,0:T(8,128)(2,1)} %param.12, bf16[256,4096]{1,0:T(8,128)(2,1)S(1)} %copy-done.4, f32[4096]{0:T(1024)S(1)} %copy-done.20, f32[256]{0:T(256)S(1)} %get-tuple-element.49), kind=kOutput, calls=%fused_computation.128 | convolution fusion | flops 541065216 | bytes 4473856 | tf_op jit(solution)/shard_map/dot_general | solution.py:181
  40.7 6.8 %convolution_bitcast_fusion = f32[32,8,8,128]{3,1,2,0:T(8,128)S(1)} fusion(bf16[4096,1024]{1,0:T(8,128)(2,1)} %param.11, bf16[256,4096]{1,0:T(8,128)(2,1)} %all-gather.3.cloned.1.call-done, f32[4096]{0:T(1024)S(1)} %copy-done.20, f32[256]{0:T(256)S(1)} %get-tuple-element.49), kind=kOutput, calls=%fused_computation.16 | convolution fusion | flops 2151677952 | bytes 11551744 | tf_op jit(solution)/shard_map/dot_general | solution.py:180
  49.3 2.8 %fusion.7 = (f32[2,4,256]{2,1,0:T(4,128)}, f32[2,256,256,4]{2,1,3,0:T(8,128)}) fusion(pred[256,256]{0,1:T(8,128)(4,1)S(1)} %fusion.29, bf16[256,2,4,64]{3,0,2,1:T(8,128)(2,1)S(1)} %bitcast.206, bf16[256,2,4,64]{3,0,2,1:T(8,128)(2,1)S(1)} %bitcast.208, bf16[256,2,64]{2,0,1:T(8,128)(2,1)S(1)} %get-tuple-element.25, bf16[256,2,64]{2,0,1:T(8,128)(2,1)S(1)} %get-tuple-element.24), kind=kOutput, calls=%fused_computation.14 | convolution fusion | flops 137099264 | bytes 2826240 | tf_op jit(solution)/shard_map/qkgd,skd->kgqs/dot_general | solution.py:198
  52.0 1.8 %convolution_convert_fusion.4 = bf16[256,256]{0,1:T(8,128)(2,1)} fusion(bf16[4096,256]{1,0:T(8,128)(2,1)S(1)} %copy-done, bf16[256,4096]{1,0:T(8,128)(2,1)S(1)} %copy-done.5, f32[4096]{0:T(1024)S(1)} %copy-done.20, f32[256]{0:T(256)S(1)} %get-tuple-element.49), kind=kOutput, calls=%fused_computation.27 | convolution fusion | flops 541130752 | bytes 4342784 | tf_op jit(solution)/shard_map/dot_general | solution.py:182
  53.9 5.8 %all-gather.5.cloned.1.call-done = bf16[256,4096]{1,0:T(8,128)(2,1)} async-done(((bf16[256,1024]{1,0:T(8,128)(2,1)}), bf16[256,4096]{1,0:T(8,128)(2,1)}) %all-gather.5.cloned.1.call-update) | async-done | bytes 2097168 | tf_op jit(solution)/shard_map/all_gather | solution.py:211
  59.7 6.4 %convolution_convert_fusion = bf16[256,1024]{1,0:T(8,128)(2,1)S(1)} fusion(bf16[256,4096]{1,0:T(8,128)(2,1)} %all-gather.5.cloned.1.call-done, bf16[1024,4096]{1,0:T(8,128)(2,1)} %param.14), kind=kOutput, calls=%fused_computation.19 | convolution fusion | flops 2147745792 | bytes 11010048 | tf_op jit(solution)/shard_map/dot_general | solution.py:212
  66.3 2.6 %multiply_reduce_fusion = (f32[256,2,4]{0,2,1:T(4,128)S(1)}, bf16[2,128,4,256]{3,1,2,0:T(8,128)(2,1)S(1)}) fusion(bf16[256,1024]{0,1:T(8,128)(2,1)S(1)} %copy.78, bf16[256,2,128,1]{0,2,3,1:T(8,128)(2,1)} %bitcast.237, f32[2,4,256]{2,1,0:T(4,128)} %get-tuple-element.58, f32[2,256,256,4]{2,1,3,0:T(8,128)} %get-tuple-element.59, pred[256,256]{0,1:T(8,128)(4,1)} %copy-done.17), kind=kOutput, calls=%fused_computation.48 | convolution fusion | flops 137623552 | bytes 3358720 | tf_op jit(solution)/shard_map/kgqs,skd->qkgd/dot_general | solution.py:204
  69.0 2.0 %fusion.5 = bf16[2,4,256,256]{2,3,1,0:T(8,128)(2,1)S(1)} fusion(bf16[256,2,128,1]{0,2,3,1:T(8,128)(2,1)S(1)} %bitcast.238, bf16[256,2,4,128]{0,3,2,1:T(8,128)(2,1)} %bitcast.213, f32[2,4,256]{2,1,0:T(4,128)S(1)} %bitcast.239, f32[2,4,256]{2,1,0:T(4,128)S(1)} %copy-done.29, f32[2,256,256,4]{2,1,3,0:T(8,128)S(1)} %copy-done.27, ...), kind=kOutput, calls=%fused_computation.11 | convolution fusion | flops 137363456 | bytes 3883008 | tf_op jit(solution)/shard_map/qkgd,skd->kgqs/dot_general | solution.py:222
  71.8 2.6 %fusion.56 = f32[256,4096]{1,0:T(8,128)S(1)} fusion(bf16[256,1024]{0,1:T(8,128)(2,1)S(1)} %bitcast.210, bf16[1024,4096]{1,0:T(8,128)(2,1)S(1)} %bitcast.201), kind=kOutput, calls=%fused_computation.132 | convolution fusion | flops 2147483648 | bytes 13107200 | tf_op jit(solution)/shard_map/dot_general | solution.py:208
  74.6 1.3 pad_maximum_fusion
  75.8 0.9 copy-done.2
  77.0 1.1 fusion.53
  78.1 2.4 %copy.119 = f32[256,8,64]{2,1,0:T(8,128)} copy(f32[256,8,64]{0,2,1:T(8,128)} %get-tuple-element.23) | data formatting | bytes 1048576
  80.4 2.4 %copy.120 = f32[256,8,64]{2,1,0:T(8,128)} copy(f32[256,8,64]{0,2,1:T(8,128)} %get-tuple-element.22) | data formatting | bytes 1048576
  82.9 1.9 %add_convert_fusion = (bf16[256,8,64]{2,1,0:T(8,128)(2,1)S(1)}, bf16[256,8,64]{2,1,0:T(8,128)(2,1)S(1)}) fusion(f32[256,8,64]{2,1,0:T(8,128)} %copy.120, f32[256,8,64]{2,1,0:T(8,128)} %copy.119, f32[256,64]{1,0:T(8,128)S(1)} %get-tuple-element.47, f32[256,64]{1,0:T(8,128)S(1)} %get-tuple-element.46), kind=kLoop, calls=%fused_computation.47 | loop fusion | flops 1048576 | bytes 1703936 | tf_op jit(solution)/shard_map/convert.12
  85.9 1.1 copy-done.3
  87.0 1.4 fusion.22
  88.9 0.6 convolution_bitcast_fusion.2
  89.6 12.9 %collective-permute-done.1 = bf16[1,256,1024]{2,1,0:T(8,128)(2,1)S(1)} collective-permute-done((bf16[1,256,1024]{2,1,0:T(8,128)(2,1)S(1)}, bf16[1,256,1024]{2,1,0:T(8,128)(2,1)S(1)}, u32[]{:S(2)}, u32[]{:S(2)}) %collective-permute-start.1) | collective-permute-done | bytes 524320 | tf_op jit(solution)/shard_map/ppermute | solution.py:101
  102.5 1.4 fusion.10
  103.9 4.4 %fusion.24 = f32[256,4096]{1,0:T(8,128)} fusion(bf16[4096,1024]{1,0:T(8,128)(2,1)S(1)} %bitcast.235, bf16[32,8,8,128]{3,2,1,0:T(8,128)(2,1)S(1)} %bitcast.211), kind=kOutput, calls=%fused_computation.59 | convolution fusion | flops 2147483648 | bytes 13107200 | tf_op jit(solution)/shard_map/dot_general | solution.py:279
  108.4 3.7 %convolution_add_fusion.1 = f32[256,4096]{1,0:T(8,128)S(1)} fusion(f32[256,4096]{1,0:T(8,128)} %fusion.24, bf16[256,256]{0,1:T(8,128)(2,1)S(1)} %bitcast.216, bf16[4096,256]{1,0:T(8,128)(2,1)} %param.12), kind=kOutput, calls=%fused_computation.4 | convolution fusion | flops 537919488 | bytes 10616832 | tf_op jit(solution)/shard_map/dot_general | solution.py:285
  112.2 1.1 fusion.3
  113.4 1.3 pad_maximum_fusion.1
  114.7 0.8 copy-done.1
  115.7 0.7 fusion.55
  132.0 1.5 collective-permute-start.9
  133.5 1.5 collective-permute-start.10
  135.0 2.4 %collective-permute-start.11 = (bf16[32,1024]{1,0:T(8,128)(2,1)S(1)}, bf16[32,1024]{1,0:T(8,128)(2,1)S(1)}, u32[]{:S(2)}, u32[]{:S(2)}) collective-permute-start(bf16[32,1024]{1,0:T(8,128)(2,1)S(1)} %get-tuple-element.30), channel_id=1, source_target_pairs={{0,12},{4,16},{8,20},{12,24},{16,28},{20,0},{24,4},{28,8},{1,13},{... | collective-permute-start | bytes 196616 | tf_op jit(solution)/shard_map/ppermute | solution.py:259
  137.9 2.3 %fusion.23 = bf16[1,256,1024]{2,1,0:T(8,128)(2,1)} fusion(f32[256,4096]{1,0:T(8,128)} %copy-done.1, s32[]{:T(128)S(6)} %select_n.156, bf16[2,256,1024]{2,1,0:T(8,128)(2,1)} %collective-permute-done.16), kind=kLoop, calls=%fused_computation.58 | loop fusion | flops 786432 | bytes 2097156 | tf_op jit(solution)/shard_map/convert_element_type | solution.py:99
  140.3 1.5 collective-permute-start.17
  141.7 0.6 and_select_fusion.1
  142.5 1.5 collective-permute-start.12
  143.9 2.4 %collective-permute-start.13 = (bf16[32,1024]{1,0:T(8,128)(2,1)S(1)}, bf16[32,1024]{1,0:T(8,128)(2,1)S(1)}, u32[]{:S(2)}, u32[]{:S(2)}) collective-permute-start(bf16[32,1024]{1,0:T(8,128)(2,1)S(1)} %get-tuple-element.28), channel_id=1, source_target_pairs={{0,20},{4,24},{8,28},{12,0},{16,4},{20,8},{24,12},{28,16},{1,21},{... | collective-permute-start | bytes 196616 | tf_op jit(solution)/shard_map/ppermute | solution.py:259
  146.4 1.4 collective-permute-start.14
  147.8 1.5 collective-permute-start.15
  149.5 0.8 copy.92
  150.2 0.7 copy.93
  151.0 0.8 copy.94
  151.8 0.7 copy.95
  152.5 0.7 copy.96
  153.2 3.7 %stack.94 = bf16[8,32,1024]{2,0,1:T(8,128)(2,1)} concatenate(bf16[1,32,1024]{2,0,1:T(2,128)(2,1)S(1)} %copy.121, bf16[1,32,1024]{2,0,1:T(2,128)(2,1)S(1)} %copy.90, bf16[1,32,1024]{2,0,1:T(2,128)(2,1)S(1)} %copy.91, bf16[1,32,1024]{2,0,1:T(2,128)(2,1)} %copy.92, bf16[1,32,1024]{2,0,1:T(2,128)(2,1)} %copy.93, bf16[1,32,1024]{2,0,1:T(2,128)(2,1)} %copy.94, ...), dimensions={0} | concatenate | bytes 1048576 | tf_op jit(solution)/shard_map/stack | solution.py:260
  156.9 1.4 convolution_convert_fusion.2
  158.3 1.1 copy.97
  159.5 2.8 %fusion.13 = bf16[256,1024]{1,0:T(8,128)(2,1)} fusion(bf16[256,1024]{1,0:T(8,128)(2,1)S(1)} %copy-done.8, f32[256,4096]{1,0:T(8,128)} %copy-done.1, s32[]{:T(128)} %select_n.153, bf16[2,256,1024]{2,1,0:T(8,128)(2,1)} %collective-permute-done.16, bf16[1,256,1024]{2,1,0:T(8,128)(2,1)} %collective-permute-done.17, f32[256]{0:T(256)S(1)} %add_multiply_fusion, ...), kind=kLoop, calls=%fused_computation.31 | loop fusion | flops 3407872 | bytes 3677188 | tf_op jit(solution)/shard_map/convert_element_type | solution.py:309
  (133 shorter events, 9.0 us)
Async XLA Ops:
  7.2 44.9 %copy-start = (bf16[4096,256]{1,0:T(8,128)(2,1)S(1)}, bf16[4096,256]{1,0:T(8,128)(2,1)}, u32[]{:S(2)}) copy-start(bf16[4096,256]{1,0:T(8,128)(2,1)} %param.13) | copy-start | bytes 6291460
  7.2 27.7 %all-gather.3.cloned.1.call-start = ((), (), s32[]{:S(2)}) async-start(), calls=%async_computation | async-start | bytes 2621440 | tf_op jit(solution)/shard_map/all_gather | solution.py:176
  7.9 51.7 %all-gather.5.cloned.1.call-start = ((), (), s32[]{:S(2)}) async-start(), calls=%async_computation.1 | async-start | bytes 2621440 | tf_op jit(solution)/shard_map/all_gather | solution.py:211
  9.2 13.2 %collective-permute-start.2 = (bf16[32,1024]{1,0:T(8,128)(2,1)S(1)}, bf16[32,1024]{1,0:T(8,128)(2,1)S(1)}, u32[]{:S(2)}, u32[]{:S(2)}) collective-permute-start(bf16[32,1024]{1,0:T(8,128)(2,1)S(1)} %get-tuple-element.42), channel_id=1, source_target_pairs={{0,4},{4,8},{8,12},{12,16},{16,20},{20,24},{24,28},{28,0},{1,5},{5... | collective-permute-start | bytes 196616 | tf_op jit(solution)/shard_map/ppermute | solution.py:154
  12.2 11.6 %collective-permute-start.3 = (bf16[32,1024]{1,0:T(8,128)(2,1)S(1)}, bf16[32,1024]{1,0:T(8,128)(2,1)S(1)}, u32[]{:S(2)}, u32[]{:S(2)}) collective-permute-start(bf16[32,1024]{1,0:T(8,128)(2,1)S(1)} %get-tuple-element.41), channel_id=1, source_target_pairs={{0,8},{4,12},{8,16},{12,20},{16,24},{20,28},{24,0},{28,4},{1,9},{5... | collective-permute-start | bytes 196616 | tf_op jit(solution)/shard_map/ppermute | solution.py:154
  13.8 12.9 %collective-permute-start.4 = (bf16[32,1024]{1,0:T(8,128)(2,1)S(1)}, bf16[32,1024]{1,0:T(8,128)(2,1)S(1)}, u32[]{:S(2)}, u32[]{:S(2)}) collective-permute-start(bf16[32,1024]{1,0:T(8,128)(2,1)S(1)} %get-tuple-element.40), channel_id=1, source_target_pairs={{0,12},{4,16},{8,20},{12,24},{16,28},{20,0},{24,4},{28,8},{1,13},{... | collective-permute-start | bytes 196616 | tf_op jit(solution)/shard_map/ppermute | solution.py:154
  16.3 10.5 %collective-permute-start.5 = (bf16[32,1024]{1,0:T(8,128)(2,1)S(1)}, bf16[32,1024]{1,0:T(8,128)(2,1)S(1)}, u32[]{:S(2)}, u32[]{:S(2)}) collective-permute-start(bf16[32,1024]{1,0:T(8,128)(2,1)S(1)} %get-tuple-element.39), channel_id=1, source_target_pairs={{0,16},{4,20},{8,24},{12,28},{16,0},{20,4},{24,8},{28,12},{1,17},{... | collective-permute-start | bytes 196616 | tf_op jit(solution)/shard_map/ppermute | solution.py:154
  17.6 9.3 %collective-permute-start.6 = (bf16[32,1024]{1,0:T(8,128)(2,1)S(1)}, bf16[32,1024]{1,0:T(8,128)(2,1)S(1)}, u32[]{:S(2)}, u32[]{:S(2)}) collective-permute-start(bf16[32,1024]{1,0:T(8,128)(2,1)S(1)} %get-tuple-element.38), channel_id=1, source_target_pairs={{0,20},{4,24},{8,28},{12,0},{16,4},{20,8},{24,12},{28,16},{1,21},{... | collective-permute-start | bytes 196616 | tf_op jit(solution)/shard_map/ppermute | solution.py:154
  22.4 5.3 %collective-permute-start.7 = (bf16[32,1024]{1,0:T(8,128)(2,1)S(1)}, bf16[32,1024]{1,0:T(8,128)(2,1)S(1)}, u32[]{:S(2)}, u32[]{:S(2)}) collective-permute-start(bf16[32,1024]{1,0:T(8,128)(2,1)S(1)} %get-tuple-element.37), channel_id=1, source_target_pairs={{0,24},{4,28},{8,0},{12,4},{16,8},{20,12},{24,16},{28,20},{1,25},{... | collective-permute-start | bytes 196616 | tf_op jit(solution)/shard_map/ppermute | solution.py:154
  23.8 4.6 %collective-permute-start.8 = (bf16[32,1024]{1,0:T(8,128)(2,1)S(1)}, bf16[32,1024]{1,0:T(8,128)(2,1)S(1)}, u32[]{:S(2)}, u32[]{:S(2)}) collective-permute-start(bf16[32,1024]{1,0:T(8,128)(2,1)S(1)} %get-tuple-element.36), channel_id=1, source_target_pairs={{0,28},{4,0},{8,4},{12,8},{16,12},{20,16},{24,20},{28,24},{1,29},{... | collective-permute-start | bytes 196616 | tf_op jit(solution)/shard_map/ppermute | solution.py:154
  32.1 1.5 copy-start.21
  32.5 5.2 %copy-start.20 = (f32[4096]{0:T(1024)S(1)}, f32[4096]{0:T(1024)}, u32[]{:S(2)}) copy-start(f32[4096]{0:T(1024)} %param.10) | copy-start | bytes 49156
  33.7 14.8 %copy-start.17 = (pred[256,256]{0,1:T(8,128)(4,1)}, pred[256,256]{0,1:T(8,128)(4,1)S(1)}, u32[]{:S(2)}) copy-start(pred[256,256]{0,1:T(8,128)(4,1)S(1)} %fusion.29) | copy-start | bytes 196612
  34.9 2.8 %copy-start.4 = (bf16[256,4096]{1,0:T(8,128)(2,1)S(1)}, bf16[256,4096]{1,0:T(8,128)(2,1)}, u32[]{:S(2)}) copy-start(bf16[256,4096]{1,0:T(8,128)(2,1)} %all-gather.3.cloned.1.call-done) | copy-start | bytes 6291460
  37.7 14.4 %copy-start.23 = (f32[256]{0:T(256)}, f32[256]{0:T(256)S(1)}, u32[]{:S(2)}) copy-start(f32[256]{0:T(256)S(1)} %get-tuple-element.49) | copy-start | bytes 3076
  48.3 0.8 copy-start.9
  48.4 0.9 copy-start.11
  48.4 3.6 %copy-start.5 = (bf16[256,4096]{1,0:T(8,128)(2,1)S(1)}, bf16[256,4096]{1,0:T(8,128)(2,1)}, u32[]{:S(2)}) copy-start(bf16[256,4096]{1,0:T(8,128)(2,1)} %all-gather.3.cloned.1.call-done) | copy-start | bytes 6291460
  48.5 5.4 %copy-start.15 = (bf16[256,2,64]{2,0,1:T(8,128)(2,1)}, bf16[256,2,64]{2,0,1:T(8,128)(2,1)S(1)}, u32[]{:S(2)}) copy-start(bf16[256,2,64]{2,0,1:T(8,128)(2,1)S(1)} %get-tuple-element.25) | copy-start | bytes 196612
  66.3 2.7 %copy-start.13 = (bf16[256,1024]{0,1:T(8,128)(2,1)}, bf16[256,1024]{0,1:T(8,128)(2,1)S(1)}, u32[]{:S(2)}) copy-start(bf16[256,1024]{0,1:T(8,128)(2,1)S(1)} %copy.78) | copy-start | bytes 1572868
  66.3 2.7 %copy-start.18 = (pred[256,256]{0,1:T(8,128)(4,1)S(1)}, pred[256,256]{0,1:T(8,128)(4,1)}, u32[]{:S(2)}) copy-start(pred[256,256]{0,1:T(8,128)(4,1)} %copy-done.17) | copy-start | bytes 196612
  66.3 2.7 %copy-start.26 = (bf16[256,256]{0,1:T(8,128)(2,1)S(1)}, bf16[256,256]{0,1:T(8,128)(2,1)}, u32[]{:S(2)}) copy-start(bf16[256,256]{0,1:T(8,128)(2,1)} %convolution_convert_fusion.4) | copy-start | bytes 393220
  66.3 2.7 %copy-start.27 = (f32[2,256,256,4]{2,1,3,0:T(8,128)S(1)}, f32[2,256,256,4]{2,1,3,0:T(8,128)}, u32[]{:S(2)}) copy-start(f32[2,256,256,4]{2,1,3,0:T(8,128)} %get-tuple-element.59) | copy-start | bytes 6291460
  66.3 2.7 %copy-start.29 = (f32[2,4,256]{2,1,0:T(4,128)S(1)}, f32[2,4,256]{2,1,0:T(4,128)}, u32[]{:S(2)}) copy-start(f32[2,4,256]{2,1,0:T(4,128)} %get-tuple-element.58) | copy-start | bytes 24580
  66.3 5.1 %slice-start = ((s8[8388608]{0:T(1024)(128)(4,1)}), s8[4194304]{0:T(1024)(128)(4,1)S(1)}, s32[]{:S(2)}) async-start(s8[8388608]{0:T(1024)(128)(4,1)} %bitcast.200), calls=%async_computation.2 | async-start | bytes 8388608
  69.0 2.0 %copy-start.16 = (bf16[256,2,64]{2,0,1:T(8,128)(2,1)S(1)}, bf16[256,2,64]{2,0,1:T(8,128)(2,1)}, u32[]{:S(2)}) copy-start(bf16[256,2,64]{2,0,1:T(8,128)(2,1)} %copy-done.15) | copy-start | bytes 196612
  69.0 2.8 %slice-start.1 = ((s8[8388608]{0:T(1024)(128)(4,1)}), s8[4194304]{0:T(1024)(128)(4,1)S(1)}, s32[]{:S(2)}) async-start(s8[8388608]{0:T(1024)(128)(4,1)} %bitcast.200), calls=%async_computation.3 | async-start | bytes 8388608
  74.4 2.3 %copy-start.2 = (f32[256,4096]{1,0:T(8,128)}, f32[256,4096]{1,0:T(8,128)S(1)}, u32[]{:S(2)}) copy-start(f32[256,4096]{1,0:T(8,128)S(1)} %fusion.56) | copy-start | bytes 12582916
  76.7 9.1 %collective-permute-start = (bf16[2,256,1024]{2,1,0:T(8,128)(2,1)}, bf16[2,256,1024]{2,1,0:T(8,128)(2,1)}, u32[]{:S(2)}, u32[]{:S(2)}) collective-permute-start(bf16[2,256,1024]{2,1,0:T(8,128)(2,1)} %pad_maximum_fusion), channel_id=1, source_target_pairs={{0,1},{1,0},{2,3},{3,2},{4,5},{5,4},{6,7},{7,6},{8,9},{9,8},{10,11... | collective-permute-start | bytes 3145736 | tf_op jit(solution)/shard_map/ppermute | solution.py:101
  82.9 2.2 %copy-start.10 = (bf16[256,8,64]{2,0,1:T(8,128)(2,1)S(1)}, bf16[256,8,64]{2,0,1:T(8,128)(2,1)}, u32[]{:S(2)}) copy-start(bf16[256,8,64]{2,0,1:T(8,128)(2,1)} %copy-done.9) | copy-start | bytes 786436
  82.9 2.2 %copy-start.12 = (bf16[256,8,64]{2,0,1:T(8,128)(2,1)S(1)}, bf16[256,8,64]{2,0,1:T(8,128)(2,1)}, u32[]{:S(2)}) copy-start(bf16[256,8,64]{2,0,1:T(8,128)(2,1)} %copy-done.11) | copy-start | bytes 786436
  84.8 2.2 %copy-start.3 = (f32[256,4096]{1,0:T(8,128)S(1)}, f32[256,4096]{1,0:T(8,128)}, u32[]{:S(2)}) copy-start(f32[256,4096]{1,0:T(8,128)} %copy-done.2) | copy-start | bytes 12582916
  85.7 3.2 %copy-start.14 = (bf16[256,1024]{0,1:T(8,128)(2,1)S(1)}, bf16[256,1024]{0,1:T(8,128)(2,1)}, u32[]{:S(2)}) copy-start(bf16[256,1024]{0,1:T(8,128)(2,1)} %copy-done.13) | copy-start | bytes 1572868
  85.7 3.2 %copy-start.19 = (pred[256,256]{0,1:T(8,128)(4,1)S(1)}, pred[256,256]{0,1:T(8,128)(4,1)}, u32[]{:S(2)}) copy-start(pred[256,256]{0,1:T(8,128)(4,1)} %copy-done.17) | copy-start | bytes 196612
  85.7 3.2 %copy-start.28 = (f32[2,256,256,4]{2,1,3,0:T(8,128)S(1)}, f32[2,256,256,4]{2,1,3,0:T(8,128)}, u32[]{:S(2)}) copy-start(f32[2,256,256,4]{2,1,3,0:T(8,128)} %get-tuple-element.59) | copy-start | bytes 6291460
  85.7 3.2 %copy-start.30 = (f32[2,4,256]{2,1,0:T(4,128)S(1)}, f32[2,4,256]{2,1,0:T(4,128)}, u32[]{:S(2)}) copy-start(f32[2,4,256]{2,1,0:T(4,128)} %get-tuple-element.58) | copy-start | bytes 24580
  87.0 16.9 %slice-start.2 = ((s8[8388608]{0:T(1024)(128)(4,1)}), s8[4194304]{0:T(1024)(128)(4,1)S(1)}, s32[]{:S(2)}) async-start(s8[8388608]{0:T(1024)(128)(4,1)} %bitcast.234), calls=%async_computation.5 | async-start | bytes 8388608
  88.3 14.2 %collective-permute-start.1 = (bf16[1,256,1024]{2,1,0:T(8,128)(2,1)S(1)}, bf16[1,256,1024]{2,1,0:T(8,128)(2,1)S(1)}, u32[]{:S(2)}, u32[]{:S(2)}) collective-permute-start(bf16[1,256,1024]{2,1,0:T(8,128)(2,1)S(1)} %fusion.22), channel_id=1, source_target_pairs={{0,2},{1,3},{2,0},{3,1},{4,6},{5,7},{6,4},{7,5},{8,10},{9,11},{10,... | collective-permute-start | bytes 1572872 | tf_op jit(solution)/shard_map/ppermute | solution.py:101
  88.9 13.6 %copy-start.8 = (bf16[256,1024]{1,0:T(8,128)(2,1)S(1)}, bf16[256,1024]{1,0:T(8,128)(2,1)}, u32[]{:S(2)}) copy-start(bf16[256,1024]{1,0:T(8,128)(2,1)} %param.9) | copy-start | bytes 1572868
  88.9 15.0 %slice-start.3 = ((s8[8388608]{0:T(1024)(128)(4,1)}), s8[4194304]{0:T(1024)(128)(4,1)S(1)}, s32[]{:S(2)}) async-start(s8[8388608]{0:T(1024)(128)(4,1)} %bitcast.234), calls=%async_computation.6 | async-start | bytes 8388608
  108.4 3.8 %copy-start.6 = (bf16[256,4096]{1,0:T(8,128)(2,1)S(1)}, bf16[256,4096]{1,0:T(8,128)(2,1)}, u32[]{:S(2)}) copy-start(bf16[256,4096]{1,0:T(8,128)(2,1)} %all-gather.3.cloned.1.call-done) | copy-start | bytes 6291460
  113.2 2.3 %copy-start.1 = (f32[256,4096]{1,0:T(8,128)}, f32[256,4096]{1,0:T(8,128)S(1)}, u32[]{:S(2)}) copy-start(f32[256,4096]{1,0:T(8,128)S(1)} %get-tuple-element.63) | copy-start | bytes 12582916
  113.2 2.3 %copy-start.25 = (s32[8]{0:T(128)S(1)}, s32[8]{0:T(128)}, u32[]{:S(2)}) copy-start(s32[8]{0:T(128)} %get-tuple-element.13) | copy-start | bytes 100
  115.6 22.4 %collective-permute-start.16 = (bf16[2,256,1024]{2,1,0:T(8,128)(2,1)}, bf16[2,256,1024]{2,1,0:T(8,128)(2,1)}, u32[]{:S(2)}, u32[]{:S(2)}) collective-permute-start(bf16[2,256,1024]{2,1,0:T(8,128)(2,1)} %pad_maximum_fusion.1), channel_id=1, source_target_pairs={{0,1},{1,0},{2,3},{3,2},{4,5},{5,4},{6,7},{7,6},{8,9},{9,8},{10,11... | collective-permute-start | bytes 3145736 | tf_op jit(solution)/shard_map/ppermute | solution.py:103
  131.3 6.0 %collective-permute-start.18 = (f32[256]{0:T(256)S(1)}, f32[256]{0:T(256)S(1)}, u32[]{:S(2)}, u32[]{:S(2)}) collective-permute-start(f32[256]{0:T(256)S(1)} %get-tuple-element.62), channel_id=1, source_target_pairs={{0,1},{1,0},{2,3},{3,2},{4,5},{5,4},{6,7},{7,6},{8,9},{9,8},{10,11... | collective-permute-start | bytes 3080 | tf_op jit(solution)/shard_map/ppermute | solution.py:103
  132.0 12.0 %collective-permute-start.9 = (bf16[32,1024]{1,0:T(8,128)(2,1)S(1)}, bf16[32,1024]{1,0:T(8,128)(2,1)S(1)}, u32[]{:S(2)}, u32[]{:S(2)}) collective-permute-start(bf16[32,1024]{1,0:T(8,128)(2,1)S(1)} %get-tuple-element.32), channel_id=1, source_target_pairs={{0,4},{4,8},{8,12},{12,16},{16,20},{20,24},{24,28},{28,0},{1,5},{5... | collective-permute-start | bytes 196616 | tf_op jit(solution)/shard_map/ppermute | solution.py:259
  133.5 12.9 %collective-permute-start.10 = (bf16[32,1024]{1,0:T(8,128)(2,1)S(1)}, bf16[32,1024]{1,0:T(8,128)(2,1)S(1)}, u32[]{:S(2)}, u32[]{:S(2)}) collective-permute-start(bf16[32,1024]{1,0:T(8,128)(2,1)S(1)} %get-tuple-element.31), channel_id=1, source_target_pairs={{0,8},{4,12},{8,16},{12,20},{16,24},{20,28},{24,0},{28,4},{1,9},{5... | collective-permute-start | bytes 196616 | tf_op jit(solution)/shard_map/ppermute | solution.py:259
  135.0 12.8 %collective-permute-start.11 = (bf16[32,1024]{1,0:T(8,128)(2,1)S(1)}, bf16[32,1024]{1,0:T(8,128)(2,1)S(1)}, u32[]{:S(2)}, u32[]{:S(2)}) collective-permute-start(bf16[32,1024]{1,0:T(8,128)(2,1)S(1)} %get-tuple-element.30), channel_id=1, source_target_pairs={{0,12},{4,16},{8,20},{12,24},{16,28},{20,0},{24,4},{28,8},{1,13},{... | collective-permute-start | bytes 196616 | tf_op jit(solution)/shard_map/ppermute | solution.py:259
  137.4 5.1 %collective-permute-start.19 = (f32[256]{0:T(256)S(1)}, f32[256]{0:T(256)S(1)}, u32[]{:S(2)}, u32[]{:S(2)}) collective-permute-start(f32[256]{0:T(256)S(1)} %add.263), channel_id=1, source_target_pairs={{0,2},{1,3},{2,0},{3,1},{4,6},{5,7},{6,4},{7,5},{8,10},{9,11},{10,... | collective-permute-start | bytes 3080 | tf_op jit(solution)/shard_map/ppermute | solution.py:103
  140.3 19.2 %collective-permute-start.17 = (bf16[1,256,1024]{2,1,0:T(8,128)(2,1)}, bf16[1,256,1024]{2,1,0:T(8,128)(2,1)}, u32[]{:S(2)}, u32[]{:S(2)}) collective-permute-start(bf16[1,256,1024]{2,1,0:T(8,128)(2,1)} %fusion.23), channel_id=1, source_target_pairs={{0,2},{1,3},{2,0},{3,1},{4,6},{5,7},{6,4},{7,5},{8,10},{9,11},{10,... | collective-permute-start | bytes 1572872 | tf_op jit(solution)/shard_map/ppermute | solution.py:103
  142.5 7.8 %collective-permute-start.12 = (bf16[32,1024]{1,0:T(8,128)(2,1)S(1)}, bf16[32,1024]{1,0:T(8,128)(2,1)S(1)}, u32[]{:S(2)}, u32[]{:S(2)}) collective-permute-start(bf16[32,1024]{1,0:T(8,128)(2,1)S(1)} %get-tuple-element.29), channel_id=1, source_target_pairs={{0,16},{4,20},{8,24},{12,28},{16,0},{20,4},{24,8},{28,12},{1,17},{... | collective-permute-start | bytes 196616 | tf_op jit(solution)/shard_map/ppermute | solution.py:259
  143.9 7.0 %collective-permute-start.13 = (bf16[32,1024]{1,0:T(8,128)(2,1)S(1)}, bf16[32,1024]{1,0:T(8,128)(2,1)S(1)}, u32[]{:S(2)}, u32[]{:S(2)}) collective-permute-start(bf16[32,1024]{1,0:T(8,128)(2,1)S(1)} %get-tuple-element.28), channel_id=1, source_target_pairs={{0,20},{4,24},{8,28},{12,0},{16,4},{20,8},{24,12},{28,16},{1,21},{... | collective-permute-start | bytes 196616 | tf_op jit(solution)/shard_map/ppermute | solution.py:259
  146.4 5.4 %collective-permute-start.14 = (bf16[32,1024]{1,0:T(8,128)(2,1)S(1)}, bf16[32,1024]{1,0:T(8,128)(2,1)S(1)}, u32[]{:S(2)}, u32[]{:S(2)}) collective-permute-start(bf16[32,1024]{1,0:T(8,128)(2,1)S(1)} %get-tuple-element.27), channel_id=1, source_target_pairs={{0,24},{4,28},{8,0},{12,4},{16,8},{20,12},{24,16},{28,20},{1,25},{... | collective-permute-start | bytes 196616 | tf_op jit(solution)/shard_map/ppermute | solution.py:259
  147.8 4.7 %collective-permute-start.15 = (bf16[32,1024]{1,0:T(8,128)(2,1)S(1)}, bf16[32,1024]{1,0:T(8,128)(2,1)S(1)}, u32[]{:S(2)}, u32[]{:S(2)}) collective-permute-start(bf16[32,1024]{1,0:T(8,128)(2,1)S(1)} %get-tuple-element.26), channel_id=1, source_target_pairs={{0,28},{4,0},{8,4},{12,8},{16,12},{20,16},{24,20},{28,24},{1,29},{... | collective-permute-start | bytes 196616 | tf_op jit(solution)/shard_map/ppermute | solution.py:259
  151.0 8.5 %copy-start.7 = (bf16[8,32,1024]{2,1,0:T(8,128)(2,1)S(1)}, bf16[8,32,1024]{2,1,0:T(8,128)(2,1)}, u32[]{:S(2)}) copy-start(bf16[8,32,1024]{2,1,0:T(8,128)(2,1)} %copy.77) | copy-start | bytes 1572868
  151.0 8.5 %dynamic-slice-start = ((f32[4096]{0:T(1024)}, s32[]{:T(128)}), f32[1024]{0:T(1024)S(1)}, s32[]{:S(2)}) async-start(f32[4096]{0:T(1024)} %param.10, s32[]{:T(128)} %select_n.153), calls=%async_computation.4 | async-start | bytes 8704 | tf_op jit(solution)/shard_map/dynamic_slice | solution.py:137
  151.0 8.5 %copy-start.22 = (f32[256]{0:T(256)S(1)}, f32[256]{0:T(256)}, u32[]{:S(2)}) copy-start(f32[256]{0:T(256)} %get-tuple-element.48) | copy-start | bytes 3076
  151.0 8.5 %copy-start.24 = (f32[256]{0:T(256)S(1)}, f32[256]{0:T(256)}, u32[]{:S(2)}) copy-start(f32[256]{0:T(256)} %copy-done.23) | copy-start | bytes 3076
Sparse Core Ops, SparseCore 0:
  9.6 25.2 all-gather.2
  37.0 22.5 all-gather.4

commit v6 on v5

--- a/solution.py
+++ b/solution.py
@@ -205,8 +205,18 @@
         "kgqs,skd->qkgd", probs_low, value_rows, preferred_element_type=jnp.float32
     ).astype(jnp.bfloat16)
     attended_flat = attended.reshape(token_row_count, query_width)
-    mixed_partial = jnp.dot(attended_flat, w_out, preferred_element_type=jnp.float32)
-    mixed, _ = scatter_features(mixed_partial, "tensor", tensor_size, tensor_index)
+    mixed = (
+        lax.psum_scatter(
+            lax.dot_general(
+                w_out, attended_flat, (((0,), (1,)), ((), ())), preferred_element_type=jnp.float32
+            ).astype(jnp.bfloat16),
+            "tensor",
+            scatter_dimension=0,
+            tiled=True,
+        )
+        .astype(jnp.float32)
+        .T
+    )
     output_home = (x_float + mixed).astype(jnp.bfloat16)
     grad_full = lax.all_gather(grad_home, "tensor", axis=1, tiled=True)
     attended_gradient = lax.dot_general(

time: 170 us -> 179 us (1.053)
  matrix products: 40.2 us -> 50.4 us
  waiting for transfers between devices: 20.6 us -> 25.1 us
  other arithmetic: 20.3 us -> 16.7 us
    reduce_scatter x0 -> x1, waiting for transfers between devices: none -> 17.4 us  [per_device(): lax.psum_scatter(lax.dot_general(w_out, attended_flat, (((0,), (1,)), (()...]
    ppermute x2 -> x0, waiting for transfers between devices: 13 us -> none  [scatter_features(): incoming = lax.ppermute(outgoing, axis_name, _xor_pairs(size, bit))]
    dot_general x1, matrix products: 2.62 us -> 7.1 us  [per_device(): lax.dot_general(w_out, attended_flat, (((0,), (1,)), ((), ())), preferred...]
    dot_general x1, matrix products: 4.36 us -> 7.92 us  [per_device(): lax.dot_general(grad_query.reshape(token_row_count, query_width), w_query...]
    unnamed x77 -> x63, local copies, waits for them, and re-layouts: 9.59 us -> 7.75 us
    convert_element_type x2 -> x1, other arithmetic: 3.67 us -> 2.31 us  [scatter_features(): outgoing = jnp.stack([held[i] for i in send]).astype(jnp.bfloat16)]
  transfers between devices with their start and end apart: 22 -> 21, of which waited for: 3 -> 3; matrix products, arithmetic and copies ran while one was open for 31% -> 32% of each run, Pallas kernels for 0% -> 0%
where the time goes in v6:
time: 179 us; the launch traced here: 178 us
  matrix products  50.4 us (28%)
  between operations  29.8 us (17%)
  starting transfers between devices  28.8 us (16%)
  local copies, waits for them, and re-layouts  27.3 us (15%)
  waiting for transfers between devices  25.1 us (14%)
  other arithmetic  16.7 us (9%)
    reduce_scatter x1, waiting for transfers between devices, per_device(): lax.psum_scatter(lax.dot_general(w_out, attended_flat, (((0,), (1,)), (()...  17.4 us
    ppermute x7, starting transfers between devices, per_device(): returned.append(lax.ppermute(piece, 'dp', pairs))  13.8 us
    ppermute x7, starting transfers between devices, per_device(): landed.append(lax.ppermute(piece, 'dp', pairs))  12.1 us
    dot_general x1, matrix products, per_device(): lax.dot_general(grad_query.reshape(token_row_count, query_width), w_query...  7.92 us
    unnamed x63, local copies, waits for them, and re-layouts  7.75 us
    another operation x8, local copies, waits for them, and re-layouts, per_device(): landed = jnp.stack(landed)  7.65 us
    dot_general x1, matrix products, per_device(): lax.dot_general(w_out, attended_flat, (((0,), (1,)), ((), ())), preferred...  7.1 us
    dot_general x1, matrix products, per_device(): jnp.dot(normed_input, w_query, preferred_element_type=jnp.float32)  6.75 us
  transfers between devices with their start and end apart: 21, of which 3 were waited for; matrix products, arithmetic and copies ran while one was open for 32% of the time, Pallas kernels for 0%

profile of v6, /device:TPU:0, one launch (start us, length us, event | category | flops | bytes accessed | tf_op | source)
XLA Modules:
  0.0 178.1 jit_solution(8625591975100982769)
XLA Ops:
  7.2 0.7 all-gather.3.cloned.1.call-update
  8.1 1.1 dynamic-slice_bitcast_fusion.7
  9.2 3.0 %collective-permute-start = (bf16[32,1024]{1,0:T(8,128)(2,1)S(1)}, bf16[32,1024]{1,0:T(8,128)(2,1)S(1)}, u32[]{:S(2)}, u32[]{:S(2)}) collective-permute-start(bf16[32,1024]{1,0:T(8,128)(2,1)S(1)} %get-tuple-element.40), channel_id=1, source_target_pairs={{0,4},{4,8},{8,12},{12,16},{16,20},{20,24},{24,28},{28,0},{1,5},{5... | collective-permute-start | bytes 196616 | tf_op jit(solution)/shard_map/ppermute | solution.py:154
  12.2 1.6 collective-permute-start.1
  13.8 2.6 %collective-permute-start.2 = (bf16[32,1024]{1,0:T(8,128)(2,1)S(1)}, bf16[32,1024]{1,0:T(8,128)(2,1)S(1)}, u32[]{:S(2)}, u32[]{:S(2)}) collective-permute-start(bf16[32,1024]{1,0:T(8,128)(2,1)S(1)} %get-tuple-element.38), channel_id=1, source_target_pairs={{0,12},{4,16},{8,20},{12,24},{16,28},{20,0},{24,4},{28,8},{1,13},{... | collective-permute-start | bytes 196616 | tf_op jit(solution)/shard_map/ppermute | solution.py:154
  16.3 1.2 collective-permute-start.3
  17.6 2.6 %collective-permute-start.4 = (bf16[32,1024]{1,0:T(8,128)(2,1)S(1)}, bf16[32,1024]{1,0:T(8,128)(2,1)S(1)}, u32[]{:S(2)}, u32[]{:S(2)}) collective-permute-start(bf16[32,1024]{1,0:T(8,128)(2,1)S(1)} %get-tuple-element.36), channel_id=1, source_target_pairs={{0,20},{4,24},{8,28},{12,0},{16,4},{20,8},{24,12},{28,16},{1,21},{... | collective-permute-start | bytes 196616 | tf_op jit(solution)/shard_map/ppermute | solution.py:154
  20.2 0.8 reduce-window.8
  21.0 0.6 fusion.35
  22.3 1.4 collective-permute-start.5
  23.7 1.4 collective-permute-start.6
  25.1 1.3 and_select_fusion
  26.9 0.8 copy.74
  27.6 0.8 copy.75
  28.4 0.8 copy.76
  29.1 2.8 %stack.70 = bf16[8,32,1024]{2,0,1:T(8,128)(2,1)S(1)} concatenate(bf16[1,32,1024]{2,0,1:T(2,128)(2,1)S(1)} %copy.118, bf16[1,32,1024]{2,0,1:T(2,128)(2,1)S(1)} %copy.70, bf16[1,32,1024]{2,0,1:T(2,128)(2,1)S(1)} %copy.71, bf16[1,32,1024]{2,0,1:T(2,128)(2,1)S(1)} %copy.72, bf16[1,32,1024]{2,0,1:T(2,128)(2,1)S(1)} %copy.73, bf16[1,32,1024]{2,0,1:T(2,128)(2,1)} %copy.74, ...), dimensions={0} | concatenate | bytes 1048576 | tf_op jit(solution)/shard_map/stack | solution.py:155
  32.3 1.1 copy.77
  33.7 1.2 all-gather.3.cloned.1.call-done
  34.9 2.2 %fusion.1 = f32[256]{0:T(256)S(1)} fusion(bf16[256,4096]{1,0:T(8,128)(2,1)} %all-gather.3.cloned.1.call-done), kind=kLoop, calls=%fused_computation.7 | loop fusion | flops 3145472 | bytes 2098176 | tf_op jit(solution)/shard_map/reduce_sum | solution.py:178
  37.1 0.6 multiply_multiply_fusion
  37.8 2.8 %fusion.44 = f32[256,256]{0,1:T(8,128)S(1)} fusion(bf16[4096,256]{1,0:T(8,128)(2,1)} %param.12, bf16[256,4096]{1,0:T(8,128)(2,1)S(1)} %copy-done.2, f32[4096]{0:T(1024)S(1)} %copy-done.18, f32[256]{0:T(256)S(1)} %get-tuple-element.47), kind=kOutput, calls=%fused_computation.118 | convolution fusion | flops 541065216 | bytes 4473856 | tf_op jit(solution)/shard_map/dot_general | solution.py:181
  40.8 6.8 %convolution_bitcast_fusion = f32[32,8,8,128]{3,1,2,0:T(8,128)S(1)} fusion(bf16[4096,1024]{1,0:T(8,128)(2,1)} %param.11, bf16[256,4096]{1,0:T(8,128)(2,1)} %all-gather.3.cloned.1.call-done, f32[4096]{0:T(1024)S(1)} %copy-done.18, f32[256]{0:T(256)S(1)} %get-tuple-element.47), kind=kOutput, calls=%fused_computation.18 | convolution fusion | flops 2151677952 | bytes 11551744 | tf_op jit(solution)/shard_map/dot_general | solution.py:180
  48.6 0.6 copy-done.9
  49.3 2.7 %fusion.8 = (f32[2,4,256]{2,1,0:T(4,128)}, f32[2,256,256,4]{2,1,3,0:T(8,128)}) fusion(pred[256,256]{0,1:T(8,128)(4,1)S(1)} %fusion.26, bf16[256,2,4,64]{3,0,2,1:T(8,128)(2,1)S(1)} %bitcast.189, bf16[256,2,4,64]{3,0,2,1:T(8,128)(2,1)S(1)} %bitcast.191, bf16[256,2,64]{2,0,1:T(8,128)(2,1)S(1)} %get-tuple-element.23, bf16[256,2,64]{2,0,1:T(8,128)(2,1)S(1)} %get-tuple-element.22), kind=kOutput, calls=%fused_computation.16 | convolution fusion | flops 137099264 | bytes 2826240 | tf_op jit(solution)/shard_map/qkgd,skd->kgqs/dot_general | solution.py:198
  52.1 1.9 %convolution_convert_fusion.5 = bf16[256,256]{0,1:T(8,128)(2,1)} fusion(bf16[4096,256]{1,0:T(8,128)(2,1)S(1)} %copy-done, bf16[256,4096]{1,0:T(8,128)(2,1)S(1)} %copy-done.3, f32[4096]{0:T(1024)S(1)} %copy-done.18, f32[256]{0:T(256)S(1)} %get-tuple-element.47), kind=kOutput, calls=%fused_computation.29 | convolution fusion | flops 541130752 | bytes 4342784 | tf_op jit(solution)/shard_map/dot_general | solution.py:182
  53.9 5.7 %all-gather.5.cloned.1.call-done = bf16[256,4096]{1,0:T(8,128)(2,1)} async-done(((bf16[256,1024]{1,0:T(8,128)(2,1)}), bf16[256,4096]{1,0:T(8,128)(2,1)}) %all-gather.5.cloned.1.call-update) | async-done | bytes 2097168 | tf_op jit(solution)/shard_map/all_gather | solution.py:221
  59.7 6.4 %convolution_convert_fusion.1 = bf16[256,1024]{1,0:T(8,128)(2,1)S(1)} fusion(bf16[256,4096]{1,0:T(8,128)(2,1)} %all-gather.5.cloned.1.call-done, bf16[1024,4096]{1,0:T(8,128)(2,1)} %param.14), kind=kOutput, calls=%fused_computation.21 | convolution fusion | flops 2147745792 | bytes 11010048 | tf_op jit(solution)/shard_map/dot_general | solution.py:222
  66.3 2.5 %multiply_reduce_fusion = (f32[256,2,4]{0,2,1:T(4,128)S(1)}, bf16[2,128,4,256]{3,1,2,0:T(8,128)(2,1)S(1)}) fusion(bf16[256,1024]{0,1:T(8,128)(2,1)S(1)} %copy.78, bf16[256,2,128,1]{0,2,3,1:T(8,128)(2,1)} %bitcast.218, f32[2,4,256]{2,1,0:T(4,128)} %get-tuple-element.56, f32[2,256,256,4]{2,1,3,0:T(8,128)} %get-tuple-element.57, pred[256,256]{0,1:T(8,128)(4,1)} %copy-done.15), kind=kOutput, calls=%fused_computation.45 | convolution fusion | flops 137623552 | bytes 3358720 | tf_op jit(solution)/shard_map/kgqs,skd->qkgd/dot_general | solution.py:204
  68.8 7.1 %fusion = bf16[4096,256]{0,1:T(8,128)(2,1)} fusion(bf16[256,1024]{0,1:T(8,128)(2,1)S(1)} %bitcast.193, bf16[1024,4096]{1,0:T(8,128)(2,1)} %param.14), kind=kOutput, calls=%fused_computation.6 | convolution fusion | flops 2148532224 | bytes 11010048 | tf_op jit(solution)/shard_map/dot_general | solution.py:210
  76.0 0.8 copy-done.16
  76.8 2.6 %fusion.6 = bf16[2,4,256,256]{2,3,1,0:T(8,128)(2,1)S(1)} fusion(bf16[256,2,128,1]{0,2,3,1:T(8,128)(2,1)S(1)} %bitcast.219, bf16[256,2,4,128]{0,3,2,1:T(8,128)(2,1)S(1)} %bitcast.196, f32[2,4,256]{2,1,0:T(4,128)S(1)} %bitcast.220, f32[2,4,256]{2,1,0:T(4,128)S(1)} %copy-done.26, f32[2,256,256,4]{2,1,3,0:T(8,128)} %get-tuple-element.57, ...), kind=kOutput, calls=%fused_computation.13 | convolution fusion | flops 137363456 | bytes 3883008 | tf_op jit(solution)/shard_map/qkgd,skd->kgqs/dot_general | solution.py:232
  79.9 1.1 fusion.50
  81.0 1.5 copy.119
  82.5 2.5 %copy.120 = f32[256,8,64]{2,1,0:T(8,128)} copy(f32[256,8,64]{0,2,1:T(8,128)} %get-tuple-element.20) | data formatting | bytes 1048576
  85.0 2.2 %fusion.10 = f32[256,2,128]{2,0,1:T(8,128)S(1)} fusion(bf16[2,4,256,256]{2,3,1,0:T(8,128)(2,1)} %copy-done.8, bf16[256,2,4,64]{3,0,2,1:T(8,128)(2,1)} %bitcast.190, bf16[256,2,4,64]{3,0,2,1:T(8,128)(2,1)} %bitcast.192), kind=kOutput, calls=%fused_computation.27 | convolution fusion | flops 135331840 | bytes 1835008 | tf_op jit(solution)/shard_map/kgqs,qkgd->skd/dot_general | solution.py:243
  87.8 1.1 pad_maximum_fusion.2
  89.4 0.6 convolution_bitcast_fusion.2
  90.1 17.4 %reduce-scatter.2.cloned.1.call-done = bf16[1024,256]{0,1:T(8,128)(2,1)} async-done(((bf16[4096,256]{0,1:T(8,128)(2,1)}), bf16[1024,256]{0,1:T(8,128)(2,1)}) %reduce-scatter.2.cloned.1.call-update) | async-done | bytes 524304 | tf_op jit(solution)/shard_map/reduce_scatter | solution.py:209
  107.5 1.2 fusion.11
  108.7 7.9 %fusion.21 = f32[256,4096]{1,0:T(8,128)} fusion(bf16[4096,1024]{1,0:T(8,128)(2,1)} %param.11, bf16[32,8,8,128]{3,2,1,0:T(8,128)(2,1)} %bitcast.194), kind=kOutput, calls=%fused_computation.51 | convolution fusion | flops 2147483648 | bytes 13107200 | tf_op jit(solution)/shard_map/dot_general | solution.py:289
  116.8 3.7 %convolution_add_fusion.1 = f32[256,4096]{1,0:T(8,128)S(1)} fusion(f32[256,4096]{1,0:T(8,128)} %fusion.21, bf16[256,256]{0,1:T(8,128)(2,1)S(1)} %bitcast.199, bf16[4096,256]{1,0:T(8,128)(2,1)} %param.12), kind=kOutput, calls=%fused_computation.4 | convolution fusion | flops 537919488 | bytes 10616832 | tf_op jit(solution)/shard_map/dot_general | solution.py:295
  120.5 1.1 fusion.4
  121.8 1.3 pad_maximum_fusion
  123.1 0.8 copy-done.1
  124.0 0.7 fusion.52
  140.7 0.7 dynamic-slice_bitcast_fusion
  141.4 1.5 collective-permute-start.7
  142.9 1.5 collective-permute-start.8
  144.4 2.4 %collective-permute-start.9 = (bf16[32,1024]{1,0:T(8,128)(2,1)S(1)}, bf16[32,1024]{1,0:T(8,128)(2,1)S(1)}, u32[]{:S(2)}, u32[]{:S(2)}) collective-permute-start(bf16[32,1024]{1,0:T(8,128)(2,1)S(1)} %get-tuple-element.28), channel_id=1, source_target_pairs={{0,12},{4,16},{8,20},{12,24},{16,28},{20,0},{24,4},{28,8},{1,13},{... | collective-permute-start | bytes 196616 | tf_op jit(solution)/shard_map/ppermute | solution.py:269
  147.3 2.3 %fusion.20 = bf16[1,256,1024]{2,1,0:T(8,128)(2,1)} fusion(f32[256,4096]{1,0:T(8,128)} %copy-done.1, s32[]{:T(128)S(6)} %select_n.177, bf16[2,256,1024]{2,1,0:T(8,128)(2,1)} %collective-permute-done.14), kind=kLoop, calls=%fused_computation.50 | loop fusion | flops 786432 | bytes 2097156 | tf_op jit(solution)/shard_map/convert_element_type | solution.py:99
  149.7 1.5 collective-permute-start.15
  151.8 1.5 collective-permute-start.10
  153.3 2.4 %collective-permute-start.11 = (bf16[32,1024]{1,0:T(8,128)(2,1)}, bf16[32,1024]{1,0:T(8,128)(2,1)S(1)}, u32[]{:S(2)}, u32[]{:S(2)}) collective-permute-start(bf16[32,1024]{1,0:T(8,128)(2,1)} %get-tuple-element.26), channel_id=1, source_target_pairs={{0,20},{4,24},{8,28},{12,0},{16,4},{20,8},{24,12},{28,16},{1,21},{... | collective-permute-start | bytes 196616 | tf_op jit(solution)/shard_map/ppermute | solution.py:269
  155.7 1.4 collective-permute-start.12
  157.1 1.5 collective-permute-start.13
  158.8 0.7 copy.92
  159.6 0.8 copy.93
  160.3 0.8 copy.94
  161.1 0.7 copy.95
  161.8 0.7 copy.96
  162.6 3.7 %stack.78 = bf16[8,32,1024]{2,0,1:T(8,128)(2,1)} concatenate(bf16[1,32,1024]{2,0,1:T(2,128)(2,1)S(1)} %copy.121, bf16[1,32,1024]{2,0,1:T(2,128)(2,1)S(1)} %copy.90, bf16[1,32,1024]{2,0,1:T(2,128)(2,1)S(1)} %copy.91, bf16[1,32,1024]{2,0,1:T(2,128)(2,1)} %copy.92, bf16[1,32,1024]{2,0,1:T(2,128)(2,1)} %copy.93, bf16[1,32,1024]{2,0,1:T(2,128)(2,1)} %copy.94, ...), dimensions={0} | concatenate | bytes 1048576 | tf_op jit(solution)/shard_map/stack | solution.py:270
  166.3 1.4 convolution_convert_fusion.3
  167.7 1.1 copy.97
  168.8 2.8 %fusion.14 = bf16[256,1024]{1,0:T(8,128)(2,1)} fusion(bf16[256,1024]{1,0:T(8,128)(2,1)S(1)} %copy-done.5, f32[256,4096]{1,0:T(8,128)} %copy-done.1, s32[]{:T(128)} %select_n.174, bf16[2,256,1024]{2,1,0:T(8,128)(2,1)} %collective-permute-done.14, bf16[1,256,1024]{2,1,0:T(8,128)(2,1)} %collective-permute-done.15, f32[256]{0:T(256)S(1)} %add_multiply_fusion, ...), kind=kLoop, calls=%fused_computation.33 | loop fusion | flops 3407872 | bytes 3677188 | tf_op jit(solution)/shard_map/convert_element_type | solution.py:319
  (113 shorter events, 7.6 us)
Async XLA Ops:
  7.2 44.9 %copy-start = (bf16[4096,256]{1,0:T(8,128)(2,1)S(1)}, bf16[4096,256]{1,0:T(8,128)(2,1)}, u32[]{:S(2)}) copy-start(bf16[4096,256]{1,0:T(8,128)(2,1)} %param.13) | copy-start | bytes 6291460
  7.2 27.7 %all-gather.3.cloned.1.call-start = ((), (), s32[]{:S(2)}) async-start(), calls=%async_computation.1 | async-start | bytes 2621440 | tf_op jit(solution)/shard_map/all_gather | solution.py:176
  7.9 51.7 %all-gather.5.cloned.1.call-start = ((), (), s32[]{:S(2)}) async-start(), calls=%async_computation.3 | async-start | bytes 2621440 | tf_op jit(solution)/shard_map/all_gather | solution.py:221
  9.2 13.1 %collective-permute-start = (bf16[32,1024]{1,0:T(8,128)(2,1)S(1)}, bf16[32,1024]{1,0:T(8,128)(2,1)S(1)}, u32[]{:S(2)}, u32[]{:S(2)}) collective-permute-start(bf16[32,1024]{1,0:T(8,128)(2,1)S(1)} %get-tuple-element.40), channel_id=1, source_target_pairs={{0,4},{4,8},{8,12},{12,16},{16,20},{20,24},{24,28},{28,0},{1,5},{5... | collective-permute-start | bytes 196616 | tf_op jit(solution)/shard_map/ppermute | solution.py:154
  12.2 11.5 %collective-permute-start.1 = (bf16[32,1024]{1,0:T(8,128)(2,1)S(1)}, bf16[32,1024]{1,0:T(8,128)(2,1)S(1)}, u32[]{:S(2)}, u32[]{:S(2)}) collective-permute-start(bf16[32,1024]{1,0:T(8,128)(2,1)S(1)} %get-tuple-element.39), channel_id=1, source_target_pairs={{0,8},{4,12},{8,16},{12,20},{16,24},{20,28},{24,0},{28,4},{1,9},{5... | collective-permute-start | bytes 196616 | tf_op jit(solution)/shard_map/ppermute | solution.py:154
  13.8 12.9 %collective-permute-start.2 = (bf16[32,1024]{1,0:T(8,128)(2,1)S(1)}, bf16[32,1024]{1,0:T(8,128)(2,1)S(1)}, u32[]{:S(2)}, u32[]{:S(2)}) collective-permute-start(bf16[32,1024]{1,0:T(8,128)(2,1)S(1)} %get-tuple-element.38), channel_id=1, source_target_pairs={{0,12},{4,16},{8,20},{12,24},{16,28},{20,0},{24,4},{28,8},{1,13},{... | collective-permute-start | bytes 196616 | tf_op jit(solution)/shard_map/ppermute | solution.py:154
  16.3 10.4 %collective-permute-start.3 = (bf16[32,1024]{1,0:T(8,128)(2,1)S(1)}, bf16[32,1024]{1,0:T(8,128)(2,1)S(1)}, u32[]{:S(2)}, u32[]{:S(2)}) collective-permute-start(bf16[32,1024]{1,0:T(8,128)(2,1)S(1)} %get-tuple-element.37), channel_id=1, source_target_pairs={{0,16},{4,20},{8,24},{12,28},{16,0},{20,4},{24,8},{28,12},{1,17},{... | collective-permute-start | bytes 196616 | tf_op jit(solution)/shard_map/ppermute | solution.py:154
  17.6 9.3 %collective-permute-start.4 = (bf16[32,1024]{1,0:T(8,128)(2,1)S(1)}, bf16[32,1024]{1,0:T(8,128)(2,1)S(1)}, u32[]{:S(2)}, u32[]{:S(2)}) collective-permute-start(bf16[32,1024]{1,0:T(8,128)(2,1)S(1)} %get-tuple-element.36), channel_id=1, source_target_pairs={{0,20},{4,24},{8,28},{12,0},{16,4},{20,8},{24,12},{28,16},{1,21},{... | collective-permute-start | bytes 196616 | tf_op jit(solution)/shard_map/ppermute | solution.py:154
  22.3 5.3 %collective-permute-start.5 = (bf16[32,1024]{1,0:T(8,128)(2,1)S(1)}, bf16[32,1024]{1,0:T(8,128)(2,1)S(1)}, u32[]{:S(2)}, u32[]{:S(2)}) collective-permute-start(bf16[32,1024]{1,0:T(8,128)(2,1)S(1)} %get-tuple-element.35), channel_id=1, source_target_pairs={{0,24},{4,28},{8,0},{12,4},{16,8},{20,12},{24,16},{28,20},{1,25},{... | collective-permute-start | bytes 196616 | tf_op jit(solution)/shard_map/ppermute | solution.py:154
  23.7 4.7 %collective-permute-start.6 = (bf16[32,1024]{1,0:T(8,128)(2,1)S(1)}, bf16[32,1024]{1,0:T(8,128)(2,1)S(1)}, u32[]{:S(2)}, u32[]{:S(2)}) collective-permute-start(bf16[32,1024]{1,0:T(8,128)(2,1)S(1)} %get-tuple-element.34), channel_id=1, source_target_pairs={{0,28},{4,0},{8,4},{12,8},{16,12},{20,16},{24,20},{28,24},{1,29},{... | collective-permute-start | bytes 196616 | tf_op jit(solution)/shard_map/ppermute | solution.py:154
  31.9 1.7 copy-start.19
  32.3 5.5 %copy-start.18 = (f32[4096]{0:T(1024)S(1)}, f32[4096]{0:T(1024)}, u32[]{:S(2)}) copy-start(f32[4096]{0:T(1024)} %param.10) | copy-start | bytes 49156
  33.4 74.1 %reduce-scatter.2.cloned.1.call-start = ((), (), s32[]{:S(2)}) async-start(), calls=%async_computation.2 | async-start | bytes 2621440 | tf_op jit(solution)/shard_map/reduce_scatter | solution.py:209
  33.7 14.8 %copy-start.15 = (pred[256,256]{0,1:T(8,128)(4,1)}, pred[256,256]{0,1:T(8,128)(4,1)S(1)}, u32[]{:S(2)}) copy-start(pred[256,256]{0,1:T(8,128)(4,1)S(1)} %fusion.26) | copy-start | bytes 196612
  34.9 2.9 %copy-start.2 = (bf16[256,4096]{1,0:T(8,128)(2,1)S(1)}, bf16[256,4096]{1,0:T(8,128)(2,1)}, u32[]{:S(2)}) copy-start(bf16[256,4096]{1,0:T(8,128)(2,1)} %all-gather.3.cloned.1.call-done) | copy-start | bytes 6291460
  37.7 14.3 %copy-start.21 = (f32[256]{0:T(256)}, f32[256]{0:T(256)S(1)}, u32[]{:S(2)}) copy-start(f32[256]{0:T(256)S(1)} %get-tuple-element.47) | copy-start | bytes 3076
  48.4 0.8 copy-start.9
  48.5 0.9 copy-start.10
  48.5 3.6 %copy-start.3 = (bf16[256,4096]{1,0:T(8,128)(2,1)S(1)}, bf16[256,4096]{1,0:T(8,128)(2,1)}, u32[]{:S(2)}) copy-start(bf16[256,4096]{1,0:T(8,128)(2,1)} %all-gather.3.cloned.1.call-done) | copy-start | bytes 6291460
  48.6 5.4 %copy-start.13 = (bf16[256,2,64]{2,0,1:T(8,128)(2,1)}, bf16[256,2,64]{2,0,1:T(8,128)(2,1)S(1)}, u32[]{:S(2)}) copy-start(bf16[256,2,64]{2,0,1:T(8,128)(2,1)S(1)} %get-tuple-element.23) | copy-start | bytes 196612
  66.2 9.7 %copy-start.11 = (bf16[256,1024]{0,1:T(8,128)(2,1)}, bf16[256,1024]{0,1:T(8,128)(2,1)S(1)}, u32[]{:S(2)}) copy-start(bf16[256,1024]{0,1:T(8,128)(2,1)S(1)} %copy.78) | copy-start | bytes 1572868
  75.9 0.8 copy-start.16
  75.9 0.9 copy-start.24
  75.9 0.9 copy-start.26
  76.8 2.6 %copy-start.14 = (bf16[256,2,64]{2,0,1:T(8,128)(2,1)S(1)}, bf16[256,2,64]{2,0,1:T(8,128)(2,1)}, u32[]{:S(2)}) copy-start(bf16[256,2,64]{2,0,1:T(8,128)(2,1)} %copy-done.13) | copy-start | bytes 196612
  79.4 1.6 copy-start.8
  85.0 2.5 %copy-start.7 = (f32[256,8,64]{2,1,0:T(8,128)S(1)}, f32[256,8,64]{2,1,0:T(8,128)}, u32[]{:S(2)}) copy-start(f32[256,8,64]{2,1,0:T(8,128)} %copy.120) | copy-start | bytes 1572868
  87.4 1.5 copy-start.12
  87.4 1.4 copy-start.17
  87.5 2.0 %copy-start.25 = (f32[2,256,256,4]{2,1,3,0:T(8,128)S(1)}, f32[2,256,256,4]{2,1,3,0:T(8,128)}, u32[]{:S(2)}) copy-start(f32[2,256,256,4]{2,1,3,0:T(8,128)} %get-tuple-element.57) | copy-start | bytes 6291460
  87.5 2.0 %copy-start.27 = (f32[2,4,256]{2,1,0:T(4,128)S(1)}, f32[2,4,256]{2,1,0:T(4,128)}, u32[]{:S(2)}) copy-start(f32[2,4,256]{2,1,0:T(4,128)} %get-tuple-element.56) | copy-start | bytes 24580
  89.4 18.1 %copy-start.5 = (bf16[256,1024]{1,0:T(8,128)(2,1)S(1)}, bf16[256,1024]{1,0:T(8,128)(2,1)}, u32[]{:S(2)}) copy-start(bf16[256,1024]{1,0:T(8,128)(2,1)} %param.9) | copy-start | bytes 1572868
  116.8 3.7 %copy-start.4 = (bf16[256,4096]{1,0:T(8,128)(2,1)S(1)}, bf16[256,4096]{1,0:T(8,128)(2,1)}, u32[]{:S(2)}) copy-start(bf16[256,4096]{1,0:T(8,128)(2,1)} %all-gather.3.cloned.1.call-done) | copy-start | bytes 6291460
  121.6 2.3 %copy-start.1 = (f32[256,4096]{1,0:T(8,128)}, f32[256,4096]{1,0:T(8,128)S(1)}, u32[]{:S(2)}) copy-start(f32[256,4096]{1,0:T(8,128)S(1)} %get-tuple-element.61) | copy-start | bytes 12582916
  121.6 2.3 %copy-start.23 = (s32[8]{0:T(128)S(1)}, s32[8]{0:T(128)}, u32[]{:S(2)}) copy-start(s32[8]{0:T(128)} %get-tuple-element.13) | copy-start | bytes 100
  123.9 23.4 %collective-permute-start.14 = (bf16[2,256,1024]{2,1,0:T(8,128)(2,1)}, bf16[2,256,1024]{2,1,0:T(8,128)(2,1)}, u32[]{:S(2)}, u32[]{:S(2)}) collective-permute-start(bf16[2,256,1024]{2,1,0:T(8,128)(2,1)} %pad_maximum_fusion), channel_id=1, source_target_pairs={{0,1},{1,0},{2,3},{3,2},{4,5},{5,4},{6,7},{7,6},{8,9},{9,8},{10,11... | collective-permute-start | bytes 3145736 | tf_op jit(solution)/shard_map/ppermute | solution.py:103
  140.1 6.6 %collective-permute-start.16 = (f32[256]{0:T(256)S(1)}, f32[256]{0:T(256)S(1)}, u32[]{:S(2)}, u32[]{:S(2)}) collective-permute-start(f32[256]{0:T(256)S(1)} %get-tuple-element.60), channel_id=1, source_target_pairs={{0,1},{1,0},{2,3},{3,2},{4,5},{5,4},{6,7},{7,6},{8,9},{9,8},{10,11... | collective-permute-start | bytes 3080 | tf_op jit(solution)/shard_map/ppermute | solution.py:103
  141.4 11.8 %collective-permute-start.7 = (bf16[32,1024]{1,0:T(8,128)(2,1)S(1)}, bf16[32,1024]{1,0:T(8,128)(2,1)S(1)}, u32[]{:S(2)}, u32[]{:S(2)}) collective-permute-start(bf16[32,1024]{1,0:T(8,128)(2,1)S(1)} %get-tuple-element.30), channel_id=1, source_target_pairs={{0,4},{4,8},{8,12},{12,16},{16,20},{20,24},{24,28},{28,0},{1,5},{5... | collective-permute-start | bytes 196616 | tf_op jit(solution)/shard_map/ppermute | solution.py:269
  142.9 12.8 %collective-permute-start.8 = (bf16[32,1024]{1,0:T(8,128)(2,1)S(1)}, bf16[32,1024]{1,0:T(8,128)(2,1)S(1)}, u32[]{:S(2)}, u32[]{:S(2)}) collective-permute-start(bf16[32,1024]{1,0:T(8,128)(2,1)S(1)} %get-tuple-element.29), channel_id=1, source_target_pairs={{0,8},{4,12},{8,16},{12,20},{16,24},{20,28},{24,0},{28,4},{1,9},{5... | collective-permute-start | bytes 196616 | tf_op jit(solution)/shard_map/ppermute | solution.py:269
  144.4 12.8 %collective-permute-start.9 = (bf16[32,1024]{1,0:T(8,128)(2,1)S(1)}, bf16[32,1024]{1,0:T(8,128)(2,1)S(1)}, u32[]{:S(2)}, u32[]{:S(2)}) collective-permute-start(bf16[32,1024]{1,0:T(8,128)(2,1)S(1)} %get-tuple-element.28), channel_id=1, source_target_pairs={{0,12},{4,16},{8,20},{12,24},{16,28},{20,0},{24,4},{28,8},{1,13},{... | collective-permute-start | bytes 196616 | tf_op jit(solution)/shard_map/ppermute | solution.py:269
  146.8 5.0 %collective-permute-start.17 = (f32[256]{0:T(256)S(1)}, f32[256]{0:T(256)S(1)}, u32[]{:S(2)}, u32[]{:S(2)}) collective-permute-start(f32[256]{0:T(256)S(1)} %add.249), channel_id=1, source_target_pairs={{0,2},{1,3},{2,0},{3,1},{4,6},{5,7},{6,4},{7,5},{8,10},{9,11},{10,... | collective-permute-start | bytes 3080 | tf_op jit(solution)/shard_map/ppermute | solution.py:103
  149.7 19.1 %collective-permute-start.15 = (bf16[1,256,1024]{2,1,0:T(8,128)(2,1)}, bf16[1,256,1024]{2,1,0:T(8,128)(2,1)}, u32[]{:S(2)}, u32[]{:S(2)}) collective-permute-start(bf16[1,256,1024]{2,1,0:T(8,128)(2,1)} %fusion.20), channel_id=1, source_target_pairs={{0,2},{1,3},{2,0},{3,1},{4,6},{5,7},{6,4},{7,5},{8,10},{9,11},{10,... | collective-permute-start | bytes 1572872 | tf_op jit(solution)/shard_map/ppermute | solution.py:103
  151.8 7.8 %collective-permute-start.10 = (bf16[32,1024]{1,0:T(8,128)(2,1)}, bf16[32,1024]{1,0:T(8,128)(2,1)S(1)}, u32[]{:S(2)}, u32[]{:S(2)}) collective-permute-start(bf16[32,1024]{1,0:T(8,128)(2,1)} %get-tuple-element.27), channel_id=1, source_target_pairs={{0,16},{4,20},{8,24},{12,28},{16,0},{20,4},{24,8},{28,12},{1,17},{... | collective-permute-start | bytes 196616 | tf_op jit(solution)/shard_map/ppermute | solution.py:269
  153.3 7.0 %collective-permute-start.11 = (bf16[32,1024]{1,0:T(8,128)(2,1)}, bf16[32,1024]{1,0:T(8,128)(2,1)S(1)}, u32[]{:S(2)}, u32[]{:S(2)}) collective-permute-start(bf16[32,1024]{1,0:T(8,128)(2,1)} %get-tuple-element.26), channel_id=1, source_target_pairs={{0,20},{4,24},{8,28},{12,0},{16,4},{20,8},{24,12},{28,16},{1,21},{... | collective-permute-start | bytes 196616 | tf_op jit(solution)/shard_map/ppermute | solution.py:269
  155.7 5.4 %collective-permute-start.12 = (bf16[32,1024]{1,0:T(8,128)(2,1)}, bf16[32,1024]{1,0:T(8,128)(2,1)S(1)}, u32[]{:S(2)}, u32[]{:S(2)}) collective-permute-start(bf16[32,1024]{1,0:T(8,128)(2,1)} %get-tuple-element.25), channel_id=1, source_target_pairs={{0,24},{4,28},{8,0},{12,4},{16,8},{20,12},{24,16},{28,20},{1,25},{... | collective-permute-start | bytes 196616 | tf_op jit(solution)/shard_map/ppermute | solution.py:269
  157.1 4.7 %collective-permute-start.13 = (bf16[32,1024]{1,0:T(8,128)(2,1)}, bf16[32,1024]{1,0:T(8,128)(2,1)S(1)}, u32[]{:S(2)}, u32[]{:S(2)}) collective-permute-start(bf16[32,1024]{1,0:T(8,128)(2,1)} %get-tuple-element.24), channel_id=1, source_target_pairs={{0,28},{4,0},{8,4},{12,8},{16,12},{20,16},{24,20},{28,24},{1,29},{... | collective-permute-start | bytes 196616 | tf_op jit(solution)/shard_map/ppermute | solution.py:269
  160.3 8.5 %copy-start.6 = (bf16[8,32,1024]{2,1,0:T(8,128)(2,1)S(1)}, bf16[8,32,1024]{2,1,0:T(8,128)(2,1)}, u32[]{:S(2)}) copy-start(bf16[8,32,1024]{2,1,0:T(8,128)(2,1)} %copy.77) | copy-start | bytes 1572868
  160.3 8.5 %dynamic-slice-start = ((f32[4096]{0:T(1024)}, s32[]{:T(128)}), f32[1024]{0:T(1024)S(1)}, s32[]{:S(2)}) async-start(f32[4096]{0:T(1024)} %param.10, s32[]{:T(128)} %select_n.174), calls=%async_computation.4 | async-start | bytes 8704 | tf_op jit(solution)/shard_map/dynamic_slice | solution.py:137
  160.3 8.5 %copy-start.20 = (f32[256]{0:T(256)S(1)}, f32[256]{0:T(256)}, u32[]{:S(2)}) copy-start(f32[256]{0:T(256)} %get-tuple-element.46) | copy-start | bytes 3076
  160.3 8.5 %copy-start.22 = (f32[256]{0:T(256)S(1)}, f32[256]{0:T(256)}, u32[]{:S(2)}) copy-start(f32[256]{0:T(256)} %copy-done.21) | copy-start | bytes 3076
Sparse Core Ops, SparseCore 0:
  9.6 25.2 all-gather.2
  37.0 22.5 all-gather.4
  76.0 31.4 reduce-scatter.1

commit v7 on v5

--- a/solution.py
+++ b/solution.py
@@ -244,35 +244,12 @@
         (output_home, grad_query, key_gradient, value_gradient)
     )
     home_blocks = output_home.reshape(block_count, home_rows, width_part)
-    if sources <= 16:
-        block_for = jnp.sum(
-            jnp.where(send_table > 0, jnp.arange(block_count, dtype=jnp.int32)[None, :], 0), axis=1
-        )
-        landed = [
-            lax.dynamic_index_in_dim(home_blocks, block_for[data_index], 0, keepdims=False)
-        ]
-        for shift in range(1, sources):
-            pairs = [(a, (a + shift) % sources) for a in range(sources)]
-            piece = lax.dynamic_index_in_dim(
-                home_blocks, block_for[(data_index + shift) % sources], 0, keepdims=False
-            )
-            landed.append(lax.ppermute(piece, "dp", pairs))
-        landed = jnp.stack(landed)
-        came_over = (
-            ((data_index - slot_index) % sources)[:, None] == slot_index[None, :]
-        ).astype(jnp.bfloat16)
-        relaid = (
-            jnp.einsum("bs,srw->brw", came_over, landed, preferred_element_type=jnp.float32)
-            .astype(jnp.bfloat16)
-            .reshape(token_row_count, width_part)
-        )
-    else:
-        outgoing = jnp.dot(
-            send_table, home_blocks.reshape(block_count, -1), preferred_element_type=jnp.float32
-        ).astype(jnp.bfloat16)
-        relaid = lax.all_to_all(outgoing, "dp", split_axis=0, concat_axis=0, tiled=True).reshape(
-            token_row_count, width_part
-        )
+    outgoing = jnp.dot(
+        send_table, home_blocks.reshape(block_count, -1), preferred_element_type=jnp.float32
+    ).astype(jnp.bfloat16)
+    relaid = lax.all_to_all(outgoing, "dp", split_axis=0, concat_axis=0, tiled=True).reshape(
+        token_row_count, width_part
+    )
 
     contract_out = (((1,), (1,)), ((), ()))
     normed_partial = (

time: 170 us -> 166 us (0.976)
  between operations: 29.9 us -> 14.9 us
  waiting for transfers between devices: 20.6 us -> 32.9 us
  other arithmetic: 20.3 us -> 27.7 us
  starting transfers between devices: 29.3 us -> 22.1 us
    ppermute x4, waiting for transfers between devices: 0.01 us -> 12.4 us  [scatter_features(): lax.ppermute((outgoing, extra), axis_name, _xor_pairs(size, bit))]
    ppermute x7 -> x0, starting transfers between devices: 12.2 us -> none  [per_device(): landed.append(lax.ppermute(piece, 'dp', pairs))]
    all_to_all x0 -> x2, other arithmetic: none -> 7.23 us  [per_device(): lax.all_to_all(outgoing, 'dp', split_axis=0, concat_axis=0, tiled=True)]
    another operation x10 -> x3, local copies, waits for them, and re-layouts: 7.78 us -> 1.42 us  [the longest x1 1.28 us: per_device(): home_blocks.reshape(block_count, -1)]
    all_to_all x0 -> x1, starting transfers between devices: none -> 5.52 us  [per_device(): lax.all_to_all(outgoing, 'dp', split_axis=0, concat_axis=0, tiled=True)]
    unnamed x77 -> x78, local copies, waits for them, and re-layouts: 9.59 us -> 14.1 us
    reshape x0 -> x1, local copies, waits for them, and re-layouts: none -> 2.07 us  [per_device(): lax.all_to_all(outgoing, 'dp', split_axis=0, concat_axis=0, tiled=True)]
  transfers between devices with their start and end apart: 22 -> 16, of which waited for: 3 -> 5; matrix products, arithmetic and copies ran while one was open for 31% -> 35% of each run, Pallas kernels for 0% -> 0%
where the time goes in v7:
time: 166 us; the launch traced here: 165 us
  matrix products  39.9 us (24%)
  waiting for transfers between devices  32.9 us (20%)
  local copies, waits for them, and re-layouts  27.7 us (17%)
  other arithmetic  27.7 us (17%)
  starting transfers between devices  22.1 us (13%)
  between operations  14.9 us (9%)
    unnamed x78, local copies, waits for them, and re-layouts  14.1 us
    ppermute x7, starting transfers between devices, per_device(): returned.append(lax.ppermute(piece, 'dp', pairs))  13.8 us
    ppermute x2, waiting for transfers between devices, scatter_features(): incoming = lax.ppermute(outgoing, axis_name, _xor_pairs(size, bit))  13 us
    ppermute x4, waiting for transfers between devices, scatter_features(): lax.ppermute((outgoing, extra), axis_name, _xor_pairs(size, bit))  12.4 us
    all_to_all x2, other arithmetic, per_device(): lax.all_to_all(outgoing, 'dp', split_axis=0, concat_axis=0, tiled=True)  7.23 us
    dot_general x1, matrix products, per_device(): jnp.dot(normed_input, w_query, preferred_element_type=jnp.float32)  6.76 us
    dot_general x1, matrix products, per_device(): lax.dot_general(grad_full, w_out, (((1,), (1,)), ((), ())), preferred_ele...  6.38 us
    all_gather x1, waiting for transfers between devices, per_device(): grad_full = lax.all_gather(grad_home, 'tensor', axis=1, tiled=True)  5.71 us
  transfers between devices with their start and end apart: 16, of which 5 were waited for; matrix products, arithmetic and copies ran while one was open for 35% of the time, Pallas kernels for 0%

profile of v7, /device:TPU:0, one launch (start us, length us, event | category | flops | bytes accessed | tf_op | source)
XLA Modules:
  0.0 165.1 jit_solution(10889609049031632852)
XLA Ops:
  7.2 0.7 all-gather.3.cloned.1.call-update
  8.1 1.1 dynamic-slice_bitcast_fusion
  9.2 3.0 %collective-permute-start.2 = (bf16[32,1024]{1,0:T(8,128)(2,1)S(1)}, bf16[32,1024]{1,0:T(8,128)(2,1)S(1)}, u32[]{:S(2)}, u32[]{:S(2)}) collective-permute-start(bf16[32,1024]{1,0:T(8,128)(2,1)S(1)} %get-tuple-element.34), channel_id=1, source_target_pairs={{0,4},{4,8},{8,12},{12,16},{16,20},{20,24},{24,28},{28,0},{1,5},{5... | collective-permute-start | bytes 196616 | tf_op jit(solution)/shard_map/ppermute | solution.py:154
  12.2 1.6 collective-permute-start.3
  13.8 2.6 %collective-permute-start.4 = (bf16[32,1024]{1,0:T(8,128)(2,1)S(1)}, bf16[32,1024]{1,0:T(8,128)(2,1)S(1)}, u32[]{:S(2)}, u32[]{:S(2)}) collective-permute-start(bf16[32,1024]{1,0:T(8,128)(2,1)S(1)} %get-tuple-element.32), channel_id=1, source_target_pairs={{0,12},{4,16},{8,20},{12,24},{16,28},{20,0},{24,4},{28,8},{1,13},{... | collective-permute-start | bytes 196616 | tf_op jit(solution)/shard_map/ppermute | solution.py:154
  16.3 1.2 collective-permute-start.5
  17.5 2.6 %collective-permute-start.6 = (bf16[32,1024]{1,0:T(8,128)(2,1)S(1)}, bf16[32,1024]{1,0:T(8,128)(2,1)S(1)}, u32[]{:S(2)}, u32[]{:S(2)}) collective-permute-start(bf16[32,1024]{1,0:T(8,128)(2,1)S(1)} %get-tuple-element.30), channel_id=1, source_target_pairs={{0,20},{4,24},{8,28},{12,0},{16,4},{20,8},{24,12},{28,16},{1,21},{... | collective-permute-start | bytes 196616 | tf_op jit(solution)/shard_map/ppermute | solution.py:154
  20.2 0.8 reduce-window.8
  21.0 0.6 fusion.36
  21.6 0.5 multiply_cosine_fusion
  22.3 1.4 collective-permute-start.7
  23.7 1.4 collective-permute-start.8
  25.2 1.3 and_select_fusion
  26.9 0.8 copy.118
  27.7 0.8 copy.119
  28.4 0.7 copy.120
  29.2 2.9 %stack.61 = bf16[8,32,1024]{2,0,1:T(8,128)(2,1)S(1)} concatenate(bf16[1,32,1024]{2,0,1:T(2,128)(2,1)S(1)} %copy.154, bf16[1,32,1024]{2,0,1:T(2,128)(2,1)S(1)} %copy.114, bf16[1,32,1024]{2,0,1:T(2,128)(2,1)S(1)} %copy.115, bf16[1,32,1024]{2,0,1:T(2,128)(2,1)S(1)} %copy.116, bf16[1,32,1024]{2,0,1:T(2,128)(2,1)S(1)} %copy.117, bf16[1,32,1024]{2,0,1:T(2,128)(2,1)} %copy.118, ...), dimensions={0} | concatenate | bytes 1048576 | tf_op jit(solution)/shard_map/stack | solution.py:155
  32.5 1.1 copy.121
  33.7 1.2 all-gather.3.cloned.1.call-done
  34.9 2.2 %fusion.1 = f32[256]{0:T(256)S(1)} fusion(bf16[256,4096]{1,0:T(8,128)(2,1)} %all-gather.3.cloned.1.call-done), kind=kLoop, calls=%fused_computation.7 | loop fusion | flops 3145472 | bytes 2098176 | tf_op jit(solution)/shard_map/reduce_sum | solution.py:178
  37.1 0.6 multiply_multiply_fusion
  37.7 2.8 %fusion.44 = f32[256,256]{0,1:T(8,128)S(1)} fusion(bf16[4096,256]{1,0:T(8,128)(2,1)} %param.12, bf16[256,4096]{1,0:T(8,128)(2,1)S(1)} %copy-done.4, f32[4096]{0:T(1024)S(1)} %copy-done.20, f32[256]{0:T(256)S(1)} %get-tuple-element.41), kind=kOutput, calls=%fused_computation.113 | convolution fusion | flops 541065216 | bytes 4473856 | tf_op jit(solution)/shard_map/dot_general | solution.py:181
  40.8 6.8 %convolution_bitcast_fusion = f32[32,8,8,128]{3,1,2,0:T(8,128)S(1)} fusion(bf16[4096,1024]{1,0:T(8,128)(2,1)} %param.11, bf16[256,4096]{1,0:T(8,128)(2,1)} %all-gather.3.cloned.1.call-done, f32[4096]{0:T(1024)S(1)} %copy-done.20, f32[256]{0:T(256)S(1)} %get-tuple-element.41), kind=kOutput, calls=%fused_computation.18 | convolution fusion | flops 2151677952 | bytes 11551744 | tf_op jit(solution)/shard_map/dot_general | solution.py:180
  47.8 0.5 subtract_convert_fusion.1
  48.6 0.6 copy-done.9
  49.3 2.8 %fusion.8 = (f32[2,4,256]{2,1,0:T(4,128)}, f32[2,256,256,4]{2,1,3,0:T(8,128)}) fusion(pred[256,256]{0,1:T(8,128)(4,1)S(1)} %fusion.30, bf16[256,2,4,64]{3,0,2,1:T(8,128)(2,1)S(1)} %bitcast.173, bf16[256,2,4,64]{3,0,2,1:T(8,128)(2,1)S(1)} %bitcast.175, bf16[256,2,64]{2,0,1:T(8,128)(2,1)S(1)} %get-tuple-element.25, bf16[256,2,64]{2,0,1:T(8,128)(2,1)S(1)} %get-tuple-element.24), kind=kOutput, calls=%fused_computation.16 | convolution fusion | flops 137099264 | bytes 2826240 | tf_op jit(solution)/shard_map/qkgd,skd->kgqs/dot_general | solution.py:198
  52.1 1.8 %convolution_convert_fusion.4 = bf16[256,256]{0,1:T(8,128)(2,1)} fusion(bf16[4096,256]{1,0:T(8,128)(2,1)S(1)} %copy-done, bf16[256,4096]{1,0:T(8,128)(2,1)S(1)} %copy-done.5, f32[4096]{0:T(1024)S(1)} %copy-done.20, f32[256]{0:T(256)S(1)} %get-tuple-element.41), kind=kOutput, calls=%fused_computation.28 | convolution fusion | flops 541130752 | bytes 4342784 | tf_op jit(solution)/shard_map/dot_general | solution.py:182
  53.9 5.7 %all-gather.5.cloned.1.call-done = bf16[256,4096]{1,0:T(8,128)(2,1)} async-done(((bf16[256,1024]{1,0:T(8,128)(2,1)}), bf16[256,4096]{1,0:T(8,128)(2,1)}) %all-gather.5.cloned.1.call-update) | async-done | bytes 2097168 | tf_op jit(solution)/shard_map/all_gather | solution.py:211
  59.7 6.4 %convolution_convert_fusion.1 = bf16[256,1024]{1,0:T(8,128)(2,1)S(1)} fusion(bf16[256,4096]{1,0:T(8,128)(2,1)} %all-gather.5.cloned.1.call-done, bf16[1024,4096]{1,0:T(8,128)(2,1)} %param.14), kind=kOutput, calls=%fused_computation.21 | convolution fusion | flops 2147745792 | bytes 11010048 | tf_op jit(solution)/shard_map/dot_general | solution.py:212
  66.3 2.6 %multiply_reduce_fusion = (f32[256,2,4]{0,2,1:T(4,128)S(1)}, bf16[2,128,4,256]{3,1,2,0:T(8,128)(2,1)S(1)}) fusion(bf16[256,1024]{0,1:T(8,128)(2,1)S(1)} %copy.122, bf16[256,2,128,1]{0,2,3,1:T(8,128)(2,1)} %bitcast.196, f32[2,4,256]{2,1,0:T(4,128)} %get-tuple-element.42, f32[2,256,256,4]{2,1,3,0:T(8,128)} %get-tuple-element.43, pred[256,256]{0,1:T(8,128)(4,1)} %copy-done.17), kind=kOutput, calls=%fused_computation.49 | convolution fusion | flops 137623552 | bytes 3358720 | tf_op jit(solution)/shard_map/kgqs,skd->qkgd/dot_general | solution.py:204
  69.0 2.0 %fusion.6 = bf16[2,4,256,256]{2,3,1,0:T(8,128)(2,1)S(1)} fusion(bf16[256,2,128,1]{0,2,3,1:T(8,128)(2,1)S(1)} %bitcast.197, bf16[256,2,4,128]{0,3,2,1:T(8,128)(2,1)} %bitcast.180, f32[2,4,256]{2,1,0:T(4,128)S(1)} %bitcast.198, f32[2,4,256]{2,1,0:T(4,128)S(1)} %copy-done.29, f32[2,256,256,4]{2,1,3,0:T(8,128)S(1)} %copy-done.27, ...), kind=kOutput, calls=%fused_computation.13 | convolution fusion | flops 137363456 | bytes 3883008 | tf_op jit(solution)/shard_map/qkgd,skd->kgqs/dot_general | solution.py:222
  71.8 2.6 %fusion.52 = f32[256,4096]{1,0:T(8,128)S(1)} fusion(bf16[256,1024]{0,1:T(8,128)(2,1)S(1)} %bitcast.177, bf16[1024,4096]{1,0:T(8,128)(2,1)S(1)} %bitcast.169), kind=kOutput, calls=%fused_computation.116 | convolution fusion | flops 2147483648 | bytes 13107200 | tf_op jit(solution)/shard_map/dot_general | solution.py:208
  74.6 1.3 pad_maximum_fusion
  75.9 0.9 copy-done.2
  77.0 1.1 fusion.50
  78.0 2.3 %copy.155 = f32[256,8,64]{2,1,0:T(8,128)} copy(f32[256,8,64]{0,2,1:T(8,128)} %get-tuple-element.23) | data formatting | bytes 1048576
  80.4 2.4 %copy.156 = f32[256,8,64]{2,1,0:T(8,128)} copy(f32[256,8,64]{0,2,1:T(8,128)} %get-tuple-element.22) | data formatting | bytes 1048576
  82.8 1.9 %add_convert_fusion = (bf16[256,8,64]{2,1,0:T(8,128)(2,1)S(1)}, bf16[256,8,64]{2,1,0:T(8,128)(2,1)S(1)}) fusion(f32[256,8,64]{2,1,0:T(8,128)} %copy.156, f32[256,8,64]{2,1,0:T(8,128)} %copy.155, f32[256,64]{1,0:T(8,128)S(1)} %get-tuple-element.39, f32[256,64]{1,0:T(8,128)S(1)} %get-tuple-element.38), kind=kLoop, calls=%fused_computation.48 | loop fusion | flops 1048576 | bytes 1703936 | tf_op jit(solution)/shard_map/convert.12
  85.0 0.5 fusion.10
  85.8 1.1 copy-done.3
  86.9 1.4 fusion.23
  88.8 0.6 convolution_bitcast_fusion.2
  89.5 12.9 %collective-permute-done.1 = bf16[1,256,1024]{2,1,0:T(8,128)(2,1)S(1)} collective-permute-done((bf16[1,256,1024]{2,1,0:T(8,128)(2,1)S(1)}, bf16[1,256,1024]{2,1,0:T(8,128)(2,1)S(1)}, u32[]{:S(2)}, u32[]{:S(2)}) %collective-permute-start.1) | collective-permute-done | bytes 524320 | tf_op jit(solution)/shard_map/ppermute | solution.py:101
  102.4 2.2 %fusion.11 = bf16[256,1024]{1,0:T(8,128)(2,1)} fusion(bf16[256,1024]{1,0:T(8,128)(2,1)S(1)} %copy-done.8, f32[256,4096]{1,0:T(8,128)S(1)} %copy-done.3, s32[]{:T(128)} %select_n.95, bf16[2,256,1024]{2,1,0:T(8,128)(2,1)} %collective-permute-done, bf16[1,256,1024]{2,1,0:T(8,128)(2,1)S(1)} %collective-permute-done.1), kind=kLoop, calls=%fused_computation.29 | loop fusion | flops 1835008 | bytes 3145732 | tf_op jit(solution)/shard_map/convert_element_type | solution.py:210
  104.6 4.3 %fusion.25 = f32[256,4096]{1,0:T(8,128)} fusion(bf16[4096,1024]{1,0:T(8,128)(2,1)S(1)} %bitcast.194, bf16[32,8,8,128]{3,2,1,0:T(8,128)(2,1)S(1)} %bitcast.178), kind=kOutput, calls=%fused_computation.60 | convolution fusion | flops 2147483648 | bytes 13107200 | tf_op jit(solution)/shard_map/dot_general | solution.py:256
  109.1 3.7 %convolution_add_fusion.1 = f32[256,4096]{1,0:T(8,128)S(1)} fusion(f32[256,4096]{1,0:T(8,128)} %fusion.25, bf16[256,256]{0,1:T(8,128)(2,1)S(1)} %bitcast.182, bf16[4096,256]{1,0:T(8,128)(2,1)} %param.12), kind=kOutput, calls=%fused_computation.6 | convolution fusion | flops 537919488 | bytes 10616832 | tf_op jit(solution)/shard_map/dot_general | solution.py:262
  112.8 1.1 fusion.4
  114.1 1.3 pad_maximum_fusion.1
  115.4 0.8 copy-done.1
  116.2 1.3 reshape_reshape.3
  117.5 1.1 fusion
  118.6 0.6 broadcast.139
  119.2 2.1 %reduce.1 = bf16[8,32768]{1,0:T(8,128)(2,1)S(1)} reduce(bf16[8,1,32768]{2,0,1:T(8,128)(2,1)} %fusion, bf16[]{:T(256)} %broadcast.139), dimensions={1}, to_apply=%copy.133.reduce_sub_computation | reduce | bytes 1048578 | tf_op jit(solution)/shard_map/all_to_all | solution.py:250
  121.3 1.2 reshape.243
  122.4 5.5 %all-to-all-start = ((bf16[8,2,16384]{2,1,0:T(2,128)(2,1)}), bf16[8,2,16384]{2,1,0:T(2,128)(2,1)}, u32[]{:S(2)}, u32[]{:S(2)}) async-start(bf16[8,2,16384]{2,1,0:T(2,128)(2,1)} %reshape.243), calls=%async_computation | async-start | bytes 1048576 | tf_op jit(solution)/shard_map/all_to_all | solution.py:250
  128.0 2.3 %fusion.24 = bf16[1,256,1024]{2,1,0:T(8,128)(2,1)} fusion(f32[256,4096]{1,0:T(8,128)} %copy-done.1, s32[]{:T(128)S(6)} %select_n.98, bf16[2,256,1024]{2,1,0:T(8,128)(2,1)} %collective-permute-done.9), kind=kLoop, calls=%fused_computation.59 | loop fusion | flops 786432 | bytes 2097156 | tf_op jit(solution)/shard_map/convert_element_type | solution.py:99
  130.3 0.5 collective-permute-start.10
  130.8 1.1 collective-permute-done.11
  132.0 1.5 collective-permute-start.12
  133.4 11.2 %collective-permute-done.12 = f32[256]{0:T(256)S(1)} collective-permute-done((f32[256]{0:T(256)S(1)}, f32[256]{0:T(256)S(1)}, u32[]{:S(2)}, u32[]{:S(2)}) %collective-permute-start.12) | collective-permute-done | bytes 1056 | tf_op jit(solution)/shard_map/ppermute | solution.py:103
  144.7 3.5 %reshape.244 = bf16[8,1,32768]{2,1,0:T(2,128)(2,1)} reshape(bf16[8,2,16384]{2,1,0:T(2,128)(2,1)} %all-to-all-done) | data formatting | bytes 1048576
  148.2 5.1 %reduce = bf16[8,32768]{1,0:T(8,128)(2,1)} reduce(bf16[8,1,32768]{2,1,0:T(2,128)(2,1)} %reshape.244, bf16[]{:T(256)} %constant.116), dimensions={1}, to_apply=%all_to_all.7.reduce_sub_computation | reduce | bytes 1048578 | tf_op jit(solution)/shard_map/all_to_all | solution.py:250
  153.4 2.1 %reshape.225 = bf16[256,1024]{1,0:T(8,128)(2,1)} reshape(bf16[8,32768]{1,0:T(8,128)(2,1)} %reduce) | data formatting | bytes 1048576 | tf_op jit(solution)/shard_map/reshape | solution.py:250
  155.5 2.8 %fusion.14 = bf16[256,1024]{1,0:T(8,128)(2,1)} fusion(bf16[256,1024]{1,0:T(8,128)(2,1)S(1)} %copy-done.8, f32[256,4096]{1,0:T(8,128)} %copy-done.1, s32[]{:T(128)} %select_n.95, bf16[2,256,1024]{2,1,0:T(8,128)(2,1)} %collective-permute-done.9, bf16[1,256,1024]{2,1,0:T(8,128)(2,1)} %collective-permute-done.10, f32[256]{0:T(256)S(1)} %add_multiply_fusion, ...), kind=kLoop, calls=%fused_computation.32 | loop fusion | flops 3407872 | bytes 3677188 | tf_op jit(solution)/shard_map/convert_element_type | solution.py:286
  (114 shorter events, 4.7 us)
Async XLA Ops:
  7.2 44.9 %copy-start = (bf16[4096,256]{1,0:T(8,128)(2,1)S(1)}, bf16[4096,256]{1,0:T(8,128)(2,1)}, u32[]{:S(2)}) copy-start(bf16[4096,256]{1,0:T(8,128)(2,1)} %param.13) | copy-start | bytes 6291460
  7.2 27.7 %all-gather.3.cloned.1.call-start = ((), (), s32[]{:S(2)}) async-start(), calls=%async_computation.1 | async-start | bytes 2621440 | tf_op jit(solution)/shard_map/all_gather | solution.py:176
  7.9 51.7 %all-gather.5.cloned.1.call-start = ((), (), s32[]{:S(2)}) async-start(), calls=%async_computation.2 | async-start | bytes 2621440 | tf_op jit(solution)/shard_map/all_gather | solution.py:211
  9.2 13.1 %collective-permute-start.2 = (bf16[32,1024]{1,0:T(8,128)(2,1)S(1)}, bf16[32,1024]{1,0:T(8,128)(2,1)S(1)}, u32[]{:S(2)}, u32[]{:S(2)}) collective-permute-start(bf16[32,1024]{1,0:T(8,128)(2,1)S(1)} %get-tuple-element.34), channel_id=1, source_target_pairs={{0,4},{4,8},{8,12},{12,16},{16,20},{20,24},{24,28},{28,0},{1,5},{5... | collective-permute-start | bytes 196616 | tf_op jit(solution)/shard_map/ppermute | solution.py:154
  12.2 11.5 %collective-permute-start.3 = (bf16[32,1024]{1,0:T(8,128)(2,1)S(1)}, bf16[32,1024]{1,0:T(8,128)(2,1)S(1)}, u32[]{:S(2)}, u32[]{:S(2)}) collective-permute-start(bf16[32,1024]{1,0:T(8,128)(2,1)S(1)} %get-tuple-element.33), channel_id=1, source_target_pairs={{0,8},{4,12},{8,16},{12,20},{16,24},{20,28},{24,0},{28,4},{1,9},{5... | collective-permute-start | bytes 196616 | tf_op jit(solution)/shard_map/ppermute | solution.py:154
  13.8 12.9 %collective-permute-start.4 = (bf16[32,1024]{1,0:T(8,128)(2,1)S(1)}, bf16[32,1024]{1,0:T(8,128)(2,1)S(1)}, u32[]{:S(2)}, u32[]{:S(2)}) collective-permute-start(bf16[32,1024]{1,0:T(8,128)(2,1)S(1)} %get-tuple-element.32), channel_id=1, source_target_pairs={{0,12},{4,16},{8,20},{12,24},{16,28},{20,0},{24,4},{28,8},{1,13},{... | collective-permute-start | bytes 196616 | tf_op jit(solution)/shard_map/ppermute | solution.py:154
  16.3 10.5 %collective-permute-start.5 = (bf16[32,1024]{1,0:T(8,128)(2,1)S(1)}, bf16[32,1024]{1,0:T(8,128)(2,1)S(1)}, u32[]{:S(2)}, u32[]{:S(2)}) collective-permute-start(bf16[32,1024]{1,0:T(8,128)(2,1)S(1)} %get-tuple-element.31), channel_id=1, source_target_pairs={{0,16},{4,20},{8,24},{12,28},{16,0},{20,4},{24,8},{28,12},{1,17},{... | collective-permute-start | bytes 196616 | tf_op jit(solution)/shard_map/ppermute | solution.py:154
  17.5 9.4 %collective-permute-start.6 = (bf16[32,1024]{1,0:T(8,128)(2,1)S(1)}, bf16[32,1024]{1,0:T(8,128)(2,1)S(1)}, u32[]{:S(2)}, u32[]{:S(2)}) collective-permute-start(bf16[32,1024]{1,0:T(8,128)(2,1)S(1)} %get-tuple-element.30), channel_id=1, source_target_pairs={{0,20},{4,24},{8,28},{12,0},{16,4},{20,8},{24,12},{28,16},{1,21},{... | collective-permute-start | bytes 196616 | tf_op jit(solution)/shard_map/ppermute | solution.py:154
  22.3 5.3 %collective-permute-start.7 = (bf16[32,1024]{1,0:T(8,128)(2,1)S(1)}, bf16[32,1024]{1,0:T(8,128)(2,1)S(1)}, u32[]{:S(2)}, u32[]{:S(2)}) collective-permute-start(bf16[32,1024]{1,0:T(8,128)(2,1)S(1)} %get-tuple-element.29), channel_id=1, source_target_pairs={{0,24},{4,28},{8,0},{12,4},{16,8},{20,12},{24,16},{28,20},{1,25},{... | collective-permute-start | bytes 196616 | tf_op jit(solution)/shard_map/ppermute | solution.py:154
  23.7 4.7 %collective-permute-start.8 = (bf16[32,1024]{1,0:T(8,128)(2,1)S(1)}, bf16[32,1024]{1,0:T(8,128)(2,1)S(1)}, u32[]{:S(2)}, u32[]{:S(2)}) collective-permute-start(bf16[32,1024]{1,0:T(8,128)(2,1)S(1)} %get-tuple-element.28), channel_id=1, source_target_pairs={{0,28},{4,0},{8,4},{12,8},{16,12},{20,16},{24,20},{28,24},{1,29},{... | collective-permute-start | bytes 196616 | tf_op jit(solution)/shard_map/ppermute | solution.py:154
  32.1 1.5 copy-start.21
  32.5 5.2 %copy-start.20 = (f32[4096]{0:T(1024)S(1)}, f32[4096]{0:T(1024)}, u32[]{:S(2)}) copy-start(f32[4096]{0:T(1024)} %param.10) | copy-start | bytes 49156
  33.7 14.8 %copy-start.17 = (pred[256,256]{0,1:T(8,128)(4,1)}, pred[256,256]{0,1:T(8,128)(4,1)S(1)}, u32[]{:S(2)}) copy-start(pred[256,256]{0,1:T(8,128)(4,1)S(1)} %fusion.30) | copy-start | bytes 196612
  34.9 2.8 %copy-start.4 = (bf16[256,4096]{1,0:T(8,128)(2,1)S(1)}, bf16[256,4096]{1,0:T(8,128)(2,1)}, u32[]{:S(2)}) copy-start(bf16[256,4096]{1,0:T(8,128)(2,1)} %all-gather.3.cloned.1.call-done) | copy-start | bytes 6291460
  37.7 14.4 %copy-start.23 = (f32[256]{0:T(256)}, f32[256]{0:T(256)S(1)}, u32[]{:S(2)}) copy-start(f32[256]{0:T(256)S(1)} %get-tuple-element.41) | copy-start | bytes 3076
  48.3 0.8 copy-start.9
  48.4 0.9 copy-start.11
  48.4 3.6 %copy-start.5 = (bf16[256,4096]{1,0:T(8,128)(2,1)S(1)}, bf16[256,4096]{1,0:T(8,128)(2,1)}, u32[]{:S(2)}) copy-start(bf16[256,4096]{1,0:T(8,128)(2,1)} %all-gather.3.cloned.1.call-done) | copy-start | bytes 6291460
  48.5 5.4 %copy-start.15 = (bf16[256,2,64]{2,0,1:T(8,128)(2,1)}, bf16[256,2,64]{2,0,1:T(8,128)(2,1)S(1)}, u32[]{:S(2)}) copy-start(bf16[256,2,64]{2,0,1:T(8,128)(2,1)S(1)} %get-tuple-element.25) | copy-start | bytes 196612
  66.2 2.7 %copy-start.13 = (bf16[256,1024]{0,1:T(8,128)(2,1)}, bf16[256,1024]{0,1:T(8,128)(2,1)S(1)}, u32[]{:S(2)}) copy-start(bf16[256,1024]{0,1:T(8,128)(2,1)S(1)} %copy.122) | copy-start | bytes 1572868
  66.3 2.7 %copy-start.18 = (pred[256,256]{0,1:T(8,128)(4,1)S(1)}, pred[256,256]{0,1:T(8,128)(4,1)}, u32[]{:S(2)}) copy-start(pred[256,256]{0,1:T(8,128)(4,1)} %copy-done.17) | copy-start | bytes 196612
  66.3 2.7 %copy-start.26 = (bf16[256,256]{0,1:T(8,128)(2,1)S(1)}, bf16[256,256]{0,1:T(8,128)(2,1)}, u32[]{:S(2)}) copy-start(bf16[256,256]{0,1:T(8,128)(2,1)} %convolution_convert_fusion.4) | copy-start | bytes 393220
  66.3 2.7 %copy-start.27 = (f32[2,256,256,4]{2,1,3,0:T(8,128)S(1)}, f32[2,256,256,4]{2,1,3,0:T(8,128)}, u32[]{:S(2)}) copy-start(f32[2,256,256,4]{2,1,3,0:T(8,128)} %get-tuple-element.43) | copy-start | bytes 6291460
  66.3 2.7 %copy-start.29 = (f32[2,4,256]{2,1,0:T(4,128)S(1)}, f32[2,4,256]{2,1,0:T(4,128)}, u32[]{:S(2)}) copy-start(f32[2,4,256]{2,1,0:T(4,128)} %get-tuple-element.42) | copy-start | bytes 24580
  66.3 5.1 %slice-start = ((s8[8388608]{0:T(1024)(128)(4,1)}), s8[4194304]{0:T(1024)(128)(4,1)S(1)}, s32[]{:S(2)}) async-start(s8[8388608]{0:T(1024)(128)(4,1)} %bitcast.168), calls=%async_computation.3 | async-start | bytes 8388608
  69.0 2.0 %copy-start.16 = (bf16[256,2,64]{2,0,1:T(8,128)(2,1)S(1)}, bf16[256,2,64]{2,0,1:T(8,128)(2,1)}, u32[]{:S(2)}) copy-start(bf16[256,2,64]{2,0,1:T(8,128)(2,1)} %copy-done.15) | copy-start | bytes 196612
  69.0 2.8 %slice-start.1 = ((s8[8388608]{0:T(1024)(128)(4,1)}), s8[4194304]{0:T(1024)(128)(4,1)S(1)}, s32[]{:S(2)}) async-start(s8[8388608]{0:T(1024)(128)(4,1)} %bitcast.168), calls=%async_computation.4 | async-start | bytes 8388608
  74.4 2.3 %copy-start.2 = (f32[256,4096]{1,0:T(8,128)}, f32[256,4096]{1,0:T(8,128)S(1)}, u32[]{:S(2)}) copy-start(f32[256,4096]{1,0:T(8,128)S(1)} %fusion.52) | copy-start | bytes 12582916
  76.7 9.0 %collective-permute-start = (bf16[2,256,1024]{2,1,0:T(8,128)(2,1)}, bf16[2,256,1024]{2,1,0:T(8,128)(2,1)}, u32[]{:S(2)}, u32[]{:S(2)}) collective-permute-start(bf16[2,256,1024]{2,1,0:T(8,128)(2,1)} %pad_maximum_fusion), channel_id=1, source_target_pairs={{0,1},{1,0},{2,3},{3,2},{4,5},{5,4},{6,7},{7,6},{8,9},{9,8},{10,11... | collective-permute-start | bytes 3145736 | tf_op jit(solution)/shard_map/ppermute | solution.py:101
  82.8 2.2 %copy-start.10 = (bf16[256,8,64]{2,0,1:T(8,128)(2,1)S(1)}, bf16[256,8,64]{2,0,1:T(8,128)(2,1)}, u32[]{:S(2)}) copy-start(bf16[256,8,64]{2,0,1:T(8,128)(2,1)} %copy-done.9) | copy-start | bytes 786436
  82.8 2.2 %copy-start.12 = (bf16[256,8,64]{2,0,1:T(8,128)(2,1)S(1)}, bf16[256,8,64]{2,0,1:T(8,128)(2,1)}, u32[]{:S(2)}) copy-start(bf16[256,8,64]{2,0,1:T(8,128)(2,1)} %copy-done.11) | copy-start | bytes 786436
  84.7 2.2 %copy-start.3 = (f32[256,4096]{1,0:T(8,128)S(1)}, f32[256,4096]{1,0:T(8,128)}, u32[]{:S(2)}) copy-start(f32[256,4096]{1,0:T(8,128)} %copy-done.2) | copy-start | bytes 12582916
  85.6 3.2 %copy-start.14 = (bf16[256,1024]{0,1:T(8,128)(2,1)S(1)}, bf16[256,1024]{0,1:T(8,128)(2,1)}, u32[]{:S(2)}) copy-start(bf16[256,1024]{0,1:T(8,128)(2,1)} %copy-done.13) | copy-start | bytes 1572868
  85.6 3.2 %copy-start.19 = (pred[256,256]{0,1:T(8,128)(4,1)S(1)}, pred[256,256]{0,1:T(8,128)(4,1)}, u32[]{:S(2)}) copy-start(pred[256,256]{0,1:T(8,128)(4,1)} %copy-done.17) | copy-start | bytes 196612
  85.6 3.2 %copy-start.28 = (f32[2,256,256,4]{2,1,3,0:T(8,128)S(1)}, f32[2,256,256,4]{2,1,3,0:T(8,128)}, u32[]{:S(2)}) copy-start(f32[2,256,256,4]{2,1,3,0:T(8,128)} %get-tuple-element.43) | copy-start | bytes 6291460
  85.6 3.2 %copy-start.30 = (f32[2,4,256]{2,1,0:T(4,128)S(1)}, f32[2,4,256]{2,1,0:T(4,128)}, u32[]{:S(2)}) copy-start(f32[2,4,256]{2,1,0:T(4,128)} %get-tuple-element.42) | copy-start | bytes 24580
  86.9 17.7 %slice-start.2 = ((s8[8388608]{0:T(1024)(128)(4,1)}), s8[4194304]{0:T(1024)(128)(4,1)S(1)}, s32[]{:S(2)}) async-start(s8[8388608]{0:T(1024)(128)(4,1)} %bitcast.193), calls=%async_computation.6 | async-start | bytes 8388608
  88.3 14.2 %collective-permute-start.1 = (bf16[1,256,1024]{2,1,0:T(8,128)(2,1)S(1)}, bf16[1,256,1024]{2,1,0:T(8,128)(2,1)S(1)}, u32[]{:S(2)}, u32[]{:S(2)}) collective-permute-start(bf16[1,256,1024]{2,1,0:T(8,128)(2,1)S(1)} %fusion.23), channel_id=1, source_target_pairs={{0,2},{1,3},{2,0},{3,1},{4,6},{5,7},{6,4},{7,5},{8,10},{9,11},{10,... | collective-permute-start | bytes 1572872 | tf_op jit(solution)/shard_map/ppermute | solution.py:101
  88.8 13.6 %copy-start.8 = (bf16[256,1024]{1,0:T(8,128)(2,1)S(1)}, bf16[256,1024]{1,0:T(8,128)(2,1)}, u32[]{:S(2)}) copy-start(bf16[256,1024]{1,0:T(8,128)(2,1)} %param.9) | copy-start | bytes 1572868
  88.8 15.8 %slice-start.3 = ((s8[8388608]{0:T(1024)(128)(4,1)}), s8[4194304]{0:T(1024)(128)(4,1)S(1)}, s32[]{:S(2)}) async-start(s8[8388608]{0:T(1024)(128)(4,1)} %bitcast.193), calls=%async_computation.7 | async-start | bytes 8388608
  109.1 3.8 %copy-start.6 = (bf16[256,4096]{1,0:T(8,128)(2,1)S(1)}, bf16[256,4096]{1,0:T(8,128)(2,1)}, u32[]{:S(2)}) copy-start(bf16[256,4096]{1,0:T(8,128)(2,1)} %all-gather.3.cloned.1.call-done) | copy-start | bytes 6291460
  113.9 2.3 %copy-start.1 = (f32[256,4096]{1,0:T(8,128)}, f32[256,4096]{1,0:T(8,128)S(1)}, u32[]{:S(2)}) copy-start(f32[256,4096]{1,0:T(8,128)S(1)} %get-tuple-element.47) | copy-start | bytes 12582916
  114.1 3.4 %copy-start.25 = (s32[8]{0:T(128)S(1)}, s32[8]{0:T(128)}, u32[]{:S(2)}) copy-start(s32[8]{0:T(128)} %get-tuple-element.13) | copy-start | bytes 100
  116.2 11.8 %collective-permute-start.9 = (bf16[2,256,1024]{2,1,0:T(8,128)(2,1)}, bf16[2,256,1024]{2,1,0:T(8,128)(2,1)}, u32[]{:S(2)}, u32[]{:S(2)}) collective-permute-start(bf16[2,256,1024]{2,1,0:T(8,128)(2,1)} %pad_maximum_fusion.1), channel_id=1, source_target_pairs={{0,1},{1,0},{2,3},{3,2},{4,5},{5,4},{6,7},{7,6},{8,9},{9,8},{10,11... | collective-permute-start | bytes 3145736 | tf_op jit(solution)/shard_map/ppermute | solution.py:103
  122.4 22.3 %all-to-all-start = ((bf16[8,2,16384]{2,1,0:T(2,128)(2,1)}), bf16[8,2,16384]{2,1,0:T(2,128)(2,1)}, u32[]{:S(2)}, u32[]{:S(2)}) async-start(bf16[8,2,16384]{2,1,0:T(2,128)(2,1)} %reshape.243), calls=%async_computation | async-start | bytes 1048576 | tf_op jit(solution)/shard_map/all_to_all | solution.py:250
  130.3 25.2 %collective-permute-start.10 = (bf16[1,256,1024]{2,1,0:T(8,128)(2,1)}, bf16[1,256,1024]{2,1,0:T(8,128)(2,1)}, u32[]{:S(2)}, u32[]{:S(2)}) collective-permute-start(bf16[1,256,1024]{2,1,0:T(8,128)(2,1)} %fusion.24), channel_id=1, source_target_pairs={{0,2},{1,3},{2,0},{3,1},{4,6},{5,7},{6,4},{7,5},{8,10},{9,11},{10,... | collective-permute-start | bytes 1572872 | tf_op jit(solution)/shard_map/ppermute | solution.py:103
  130.8 1.1 collective-permute-start.11
  132.0 12.7 %collective-permute-start.12 = (f32[256]{0:T(256)S(1)}, f32[256]{0:T(256)S(1)}, u32[]{:S(2)}, u32[]{:S(2)}) collective-permute-start(f32[256]{0:T(256)S(1)} %add.200), channel_id=1, source_target_pairs={{0,2},{1,3},{2,0},{3,1},{4,6},{5,7},{6,4},{7,5},{8,10},{9,11},{10,... | collective-permute-start | bytes 3080 | tf_op jit(solution)/shard_map/ppermute | solution.py:103
  144.7 10.8 %copy-start.7 = (bf16[8,32,1024]{2,1,0:T(8,128)(2,1)S(1)}, bf16[8,32,1024]{2,1,0:T(8,128)(2,1)}, u32[]{:S(2)}) copy-start(bf16[8,32,1024]{2,1,0:T(8,128)(2,1)} %copy.121) | copy-start | bytes 1572868
  144.7 10.8 %dynamic-slice-start = ((f32[4096]{0:T(1024)}, s32[]{:T(128)}), f32[1024]{0:T(1024)S(1)}, s32[]{:S(2)}) async-start(f32[4096]{0:T(1024)} %param.10, s32[]{:T(128)} %select_n.95), calls=%async_computation.5 | async-start | bytes 8704 | tf_op jit(solution)/shard_map/dynamic_slice | solution.py:137
  144.7 10.8 %copy-start.22 = (f32[256]{0:T(256)S(1)}, f32[256]{0:T(256)}, u32[]{:S(2)}) copy-start(f32[256]{0:T(256)} %get-tuple-element.40) | copy-start | bytes 3076
  144.7 10.8 %copy-start.24 = (f32[256]{0:T(256)S(1)}, f32[256]{0:T(256)}, u32[]{:S(2)}) copy-start(f32[256]{0:T(256)} %copy-done.23) | copy-start | bytes 3076
Sparse Core Ops, SparseCore 0:
  9.6 25.2 all-gather.2
  37.0 22.5 all-gather.4

commit v8 on v7

--- a/solution.py
+++ b/solution.py
@@ -244,8 +244,8 @@
         (output_home, grad_query, key_gradient, value_gradient)
     )
     home_blocks = output_home.reshape(block_count, home_rows, width_part)
-    outgoing = jnp.dot(
-        send_table, home_blocks.reshape(block_count, -1), preferred_element_type=jnp.float32
+    outgoing = jnp.einsum(
+        "dj,jrw->drw", send_table, home_blocks, preferred_element_type=jnp.float32
     ).astype(jnp.bfloat16)
     relaid = lax.all_to_all(outgoing, "dp", split_axis=0, concat_axis=0, tiled=True).reshape(
         token_row_count, width_part

time: 166 us -> 152 us (0.916)
  other arithmetic: 27.7 us -> 19.6 us
  local copies, waits for them, and re-layouts: 27.7 us -> 22.1 us
    all_to_all x2 -> x0, other arithmetic: 7.23 us -> none  [per_device(): lax.all_to_all(outgoing, 'dp', split_axis=0, concat_axis=0, tiled=True)]
    unnamed x78 -> x77, local copies, waits for them, and re-layouts: 14.1 us -> 11.4 us
    reshape x1 -> x0, local copies, waits for them, and re-layouts: 2.07 us -> none  [per_device(): lax.all_to_all(outgoing, 'dp', split_axis=0, concat_axis=0, tiled=True)]
  transfers between devices with their start and end apart: 16 -> 16, of which waited for: 5 -> 5; matrix products, arithmetic and copies ran while one was open for 35% -> 29% of each run, Pallas kernels for 0% -> 0%
where the time goes in v8:
time: 152 us; the launch traced here: 151 us
  matrix products  39.2 us (26%)
  waiting for transfers between devices  32.9 us (22%)
  local copies, waits for them, and re-layouts  22.1 us (15%)
  starting transfers between devices  22 us (14%)
  other arithmetic  19.6 us (13%)
  between operations  14.9 us (10%)
    ppermute x7, starting transfers between devices, per_device(): returned.append(lax.ppermute(piece, 'dp', pairs))  13.8 us
    ppermute x2, waiting for transfers between devices, scatter_features(): incoming = lax.ppermute(outgoing, axis_name, _xor_pairs(size, bit))  13 us
    ppermute x4, waiting for transfers between devices, scatter_features(): lax.ppermute((outgoing, extra), axis_name, _xor_pairs(size, bit))  12.4 us
    unnamed x77, local copies, waits for them, and re-layouts  11.4 us
    dot_general x1, matrix products, per_device(): jnp.dot(normed_input, w_query, preferred_element_type=jnp.float32)  6.76 us
    dot_general x1, matrix products, per_device(): lax.dot_general(grad_full, w_out, (((1,), (1,)), ((), ())), preferred_ele...  6.38 us
    all_gather x1, waiting for transfers between devices, per_device(): grad_full = lax.all_gather(grad_home, 'tensor', axis=1, tiled=True)  5.74 us
    another operation x8, local copies, waits for them, and re-layouts, per_device(): returned = jnp.stack(returned)  5.61 us
  transfers between devices with their start and end apart: 16, of which 5 were waited for; matrix products, arithmetic and copies ran while one was open for 29% of the time, Pallas kernels for 0%

profile of v8, /device:TPU:0, one launch (start us, length us, event | category | flops | bytes accessed | tf_op | source)
XLA Modules:
  0.0 150.9 jit_solution(12224035944126114711)
XLA Ops:
  7.2 0.7 all-gather.3.cloned.1.call-update
  8.1 1.1 dynamic-slice_bitcast_fusion
  9.2 3.0 %collective-permute-start.2 = (bf16[32,1024]{1,0:T(8,128)(2,1)S(1)}, bf16[32,1024]{1,0:T(8,128)(2,1)S(1)}, u32[]{:S(2)}, u32[]{:S(2)}) collective-permute-start(bf16[32,1024]{1,0:T(8,128)(2,1)S(1)} %get-tuple-element.34), channel_id=1, source_target_pairs={{0,4},{4,8},{8,12},{12,16},{16,20},{20,24},{24,28},{28,0},{1,5},{5... | collective-permute-start | bytes 196616 | tf_op jit(solution)/shard_map/ppermute | solution.py:154
  12.2 1.6 %collective-permute-start.3 = (bf16[32,1024]{1,0:T(8,128)(2,1)S(1)}, bf16[32,1024]{1,0:T(8,128)(2,1)S(1)}, u32[]{:S(2)}, u32[]{:S(2)}) collective-permute-start(bf16[32,1024]{1,0:T(8,128)(2,1)S(1)} %get-tuple-element.33), channel_id=1, source_target_pairs={{0,8},{4,12},{8,16},{12,20},{16,24},{20,28},{24,0},{28,4},{1,9},{5... | collective-permute-start | bytes 196616 | tf_op jit(solution)/shard_map/ppermute | solution.py:154
  13.8 2.6 %collective-permute-start.4 = (bf16[32,1024]{1,0:T(8,128)(2,1)S(1)}, bf16[32,1024]{1,0:T(8,128)(2,1)S(1)}, u32[]{:S(2)}, u32[]{:S(2)}) collective-permute-start(bf16[32,1024]{1,0:T(8,128)(2,1)S(1)} %get-tuple-element.32), channel_id=1, source_target_pairs={{0,12},{4,16},{8,20},{12,24},{16,28},{20,0},{24,4},{28,8},{1,13},{... | collective-permute-start | bytes 196616 | tf_op jit(solution)/shard_map/ppermute | solution.py:154
  16.3 1.2 collective-permute-start.5
  17.5 2.6 %collective-permute-start.6 = (bf16[32,1024]{1,0:T(8,128)(2,1)S(1)}, bf16[32,1024]{1,0:T(8,128)(2,1)S(1)}, u32[]{:S(2)}, u32[]{:S(2)}) collective-permute-start(bf16[32,1024]{1,0:T(8,128)(2,1)S(1)} %get-tuple-element.30), channel_id=1, source_target_pairs={{0,20},{4,24},{8,28},{12,0},{16,4},{20,8},{24,12},{28,16},{1,21},{... | collective-permute-start | bytes 196616 | tf_op jit(solution)/shard_map/ppermute | solution.py:154
  20.2 0.8 reduce-window.8
  21.0 0.7 fusion.38
  21.7 0.5 multiply_cosine_fusion
  22.4 1.4 collective-permute-start.7
  23.8 1.4 collective-permute-start.8
  25.2 1.2 and_select_fusion
  26.9 0.8 copy.95
  27.7 0.8 copy.96
  28.4 0.8 copy.97
  29.2 2.9 %stack.61 = bf16[8,32,1024]{2,0,1:T(8,128)(2,1)S(1)} concatenate(bf16[1,32,1024]{2,0,1:T(2,128)(2,1)S(1)} %copy.132, bf16[1,32,1024]{2,0,1:T(2,128)(2,1)S(1)} %copy.91, bf16[1,32,1024]{2,0,1:T(2,128)(2,1)S(1)} %copy.92, bf16[1,32,1024]{2,0,1:T(2,128)(2,1)S(1)} %copy.93, bf16[1,32,1024]{2,0,1:T(2,128)(2,1)S(1)} %copy.94, bf16[1,32,1024]{2,0,1:T(2,128)(2,1)} %copy.95, ...), dimensions={0} | concatenate | bytes 1048576 | tf_op jit(solution)/shard_map/stack | solution.py:155
  32.1 0.4 convolution_convert_fusion.3
  32.5 1.1 copy.98
  33.7 1.2 all-gather.3.cloned.1.call-done
  34.9 2.2 %fusion = f32[256]{0:T(256)S(1)} fusion(bf16[256,4096]{1,0:T(8,128)(2,1)} %all-gather.3.cloned.1.call-done), kind=kLoop, calls=%fused_computation.5 | loop fusion | flops 3145472 | bytes 2098176 | tf_op jit(solution)/shard_map/reduce_sum | solution.py:178
  37.1 0.6 multiply_multiply_fusion
  37.7 2.8 %fusion.46 = f32[256,256]{0,1:T(8,128)S(1)} fusion(bf16[4096,256]{1,0:T(8,128)(2,1)} %param.12, bf16[256,4096]{1,0:T(8,128)(2,1)S(1)} %copy-done.4, f32[4096]{0:T(1024)S(1)} %copy-done.20, f32[256]{0:T(256)S(1)} %get-tuple-element.41), kind=kOutput, calls=%fused_computation.114 | convolution fusion | flops 541065216 | bytes 4473856 | tf_op jit(solution)/shard_map/dot_general | solution.py:181
  40.8 6.8 %convolution_bitcast_fusion = f32[32,8,8,128]{3,1,2,0:T(8,128)S(1)} fusion(bf16[4096,1024]{1,0:T(8,128)(2,1)} %param.11, bf16[256,4096]{1,0:T(8,128)(2,1)} %all-gather.3.cloned.1.call-done, f32[4096]{0:T(1024)S(1)} %copy-done.20, f32[256]{0:T(256)S(1)} %get-tuple-element.41), kind=kOutput, calls=%fused_computation.16 | convolution fusion | flops 2151677952 | bytes 11551744 | tf_op jit(solution)/shard_map/dot_general | solution.py:180
  47.8 0.5 subtract_convert_fusion.1
  48.6 0.6 copy-done.9
  49.3 2.7 %fusion.7 = (f32[2,4,256]{2,1,0:T(4,128)}, f32[2,256,256,4]{2,1,3,0:T(8,128)}) fusion(pred[256,256]{0,1:T(8,128)(4,1)S(1)} %fusion.30, bf16[256,2,4,64]{3,0,2,1:T(8,128)(2,1)S(1)} %bitcast.177, bf16[256,2,4,64]{3,0,2,1:T(8,128)(2,1)S(1)} %bitcast.175, bf16[256,2,64]{2,0,1:T(8,128)(2,1)S(1)} %get-tuple-element.25, bf16[256,2,64]{2,0,1:T(8,128)(2,1)S(1)} %get-tuple-element.24), kind=kOutput, calls=%fused_computation.14 | convolution fusion | flops 137099264 | bytes 2826240 | tf_op jit(solution)/shard_map/qkgd,skd->kgqs/dot_general | solution.py:198
  52.1 1.8 %convolution_convert_fusion.4 = bf16[256,256]{0,1:T(8,128)(2,1)} fusion(bf16[4096,256]{1,0:T(8,128)(2,1)S(1)} %copy-done, bf16[256,4096]{1,0:T(8,128)(2,1)S(1)} %copy-done.5, f32[4096]{0:T(1024)S(1)} %copy-done.20, f32[256]{0:T(256)S(1)} %get-tuple-element.41), kind=kOutput, calls=%fused_computation.27 | convolution fusion | flops 541130752 | bytes 4342784 | tf_op jit(solution)/shard_map/dot_general | solution.py:182
  53.9 5.7 %all-gather.5.cloned.1.call-done = bf16[256,4096]{1,0:T(8,128)(2,1)} async-done(((bf16[256,1024]{1,0:T(8,128)(2,1)}), bf16[256,4096]{1,0:T(8,128)(2,1)}) %all-gather.5.cloned.1.call-update) | async-done | bytes 2097168 | tf_op jit(solution)/shard_map/all_gather | solution.py:211
  59.7 6.4 %convolution_convert_fusion = bf16[256,1024]{1,0:T(8,128)(2,1)S(1)} fusion(bf16[256,4096]{1,0:T(8,128)(2,1)} %all-gather.5.cloned.1.call-done, bf16[1024,4096]{1,0:T(8,128)(2,1)} %param.14), kind=kOutput, calls=%fused_computation.19 | convolution fusion | flops 2147745792 | bytes 11010048 | tf_op jit(solution)/shard_map/dot_general | solution.py:212
  66.3 2.6 %multiply_reduce_fusion = (f32[256,2,4]{0,2,1:T(4,128)S(1)}, bf16[2,128,4,256]{3,1,2,0:T(8,128)(2,1)S(1)}) fusion(bf16[256,1024]{0,1:T(8,128)(2,1)S(1)} %copy.99, bf16[256,2,128,1]{0,2,3,1:T(8,128)(2,1)} %bitcast.199, f32[2,4,256]{2,1,0:T(4,128)} %get-tuple-element.42, f32[2,256,256,4]{2,1,3,0:T(8,128)} %get-tuple-element.43, pred[256,256]{0,1:T(8,128)(4,1)} %copy-done.17), kind=kOutput, calls=%fused_computation.48 | convolution fusion | flops 137623552 | bytes 3358720 | tf_op jit(solution)/shard_map/kgqs,skd->qkgd/dot_general | solution.py:204
  69.0 2.0 %fusion.5 = bf16[2,4,256,256]{2,3,1,0:T(8,128)(2,1)S(1)} fusion(bf16[256,2,128,1]{0,2,3,1:T(8,128)(2,1)S(1)} %bitcast.200, bf16[256,2,4,128]{0,3,2,1:T(8,128)(2,1)} %bitcast.183, f32[2,4,256]{2,1,0:T(4,128)S(1)} %bitcast.201, f32[2,4,256]{2,1,0:T(4,128)S(1)} %copy-done.29, f32[2,256,256,4]{2,1,3,0:T(8,128)S(1)} %copy-done.27, ...), kind=kOutput, calls=%fused_computation.11 | convolution fusion | flops 137363456 | bytes 3883008 | tf_op jit(solution)/shard_map/qkgd,skd->kgqs/dot_general | solution.py:222
  71.0 0.4 convolution_multiply_fusion
  71.5 0.3 slice-done.1
  71.8 2.6 %fusion.54 = f32[256,4096]{1,0:T(8,128)S(1)} fusion(bf16[256,1024]{0,1:T(8,128)(2,1)S(1)} %bitcast.180, bf16[1024,4096]{1,0:T(8,128)(2,1)S(1)} %bitcast.171), kind=kOutput, calls=%fused_computation.117 | convolution fusion | flops 2147483648 | bytes 13107200 | tf_op jit(solution)/shard_map/dot_general | solution.py:208
  74.6 1.3 pad_maximum_fusion
  75.9 0.9 copy-done.2
  77.0 1.1 fusion.52
  78.1 2.4 %copy.133 = f32[256,8,64]{2,1,0:T(8,128)} copy(f32[256,8,64]{0,2,1:T(8,128)} %get-tuple-element.23) | data formatting | bytes 1048576
  80.4 2.4 %copy.134 = f32[256,8,64]{2,1,0:T(8,128)} copy(f32[256,8,64]{0,2,1:T(8,128)} %get-tuple-element.22) | data formatting | bytes 1048576
  82.9 1.9 %add_convert_fusion = (bf16[256,8,64]{2,1,0:T(8,128)(2,1)S(1)}, bf16[256,8,64]{2,1,0:T(8,128)(2,1)S(1)}) fusion(f32[256,8,64]{2,1,0:T(8,128)} %copy.134, f32[256,8,64]{2,1,0:T(8,128)} %copy.133, f32[256,64]{1,0:T(8,128)S(1)} %get-tuple-element.39, f32[256,64]{1,0:T(8,128)S(1)} %get-tuple-element.38), kind=kLoop, calls=%fused_computation.47 | loop fusion | flops 1048576 | bytes 1703936 | tf_op jit(solution)/shard_map/convert.12
  84.8 0.3 pad_maximum_fusion.3
  85.1 0.5 fusion.9
  85.8 1.1 copy-done.3
  87.0 1.4 fusion.22
  88.3 0.4 collective-permute-start.1
  88.9 0.6 convolution_bitcast_fusion.2
  89.5 13.0 %collective-permute-done.1 = bf16[1,256,1024]{2,1,0:T(8,128)(2,1)S(1)} collective-permute-done((bf16[1,256,1024]{2,1,0:T(8,128)(2,1)S(1)}, bf16[1,256,1024]{2,1,0:T(8,128)(2,1)S(1)}, u32[]{:S(2)}, u32[]{:S(2)}) %collective-permute-start.1) | collective-permute-done | bytes 524320 | tf_op jit(solution)/shard_map/ppermute | solution.py:101
  102.5 1.4 fusion.10
  103.9 4.4 %fusion.24 = f32[256,4096]{1,0:T(8,128)} fusion(bf16[4096,1024]{1,0:T(8,128)(2,1)S(1)} %bitcast.197, bf16[32,8,8,128]{3,2,1,0:T(8,128)(2,1)S(1)} %bitcast.181), kind=kOutput, calls=%fused_computation.59 | convolution fusion | flops 2147483648 | bytes 13107200 | tf_op jit(solution)/shard_map/dot_general | solution.py:256
  108.4 3.7 %convolution_add_fusion.1 = f32[256,4096]{1,0:T(8,128)S(1)} fusion(f32[256,4096]{1,0:T(8,128)} %fusion.24, bf16[256,256]{0,1:T(8,128)(2,1)S(1)} %bitcast.185, bf16[4096,256]{1,0:T(8,128)(2,1)} %param.12), kind=kOutput, calls=%fused_computation.4 | convolution fusion | flops 537919488 | bytes 10616832 | tf_op jit(solution)/shard_map/dot_general | solution.py:262
  112.1 1.1 fusion.3
  113.4 1.3 pad_maximum_fusion.1
  114.7 0.9 copy-done.1
  115.6 0.4 convolution_convert_fusion.2
  116.0 1.1 copy.111
  117.1 5.5 %all-to-all-start = ((bf16[8,32,1024]{2,1,0:T(8,128)(2,1)}), bf16[8,32,1024]{2,1,0:T(8,128)(2,1)}, u32[]{:S(2)}, u32[]{:S(2)}) async-start(bf16[8,32,1024]{2,1,0:T(8,128)(2,1)} %copy.111), calls=%async_computation | async-start | bytes 1048576 | tf_op jit(solution)/shard_map/all_to_all | solution.py:250
  122.6 2.3 %fusion.23 = bf16[1,256,1024]{2,1,0:T(8,128)(2,1)} fusion(f32[256,4096]{1,0:T(8,128)} %copy-done.1, s32[]{:T(128)S(6)} %select_n.98, bf16[2,256,1024]{2,1,0:T(8,128)(2,1)} %collective-permute-done.9), kind=kLoop, calls=%fused_computation.58 | loop fusion | flops 786432 | bytes 2097156 | tf_op jit(solution)/shard_map/convert_element_type | solution.py:99
  124.9 0.5 collective-permute-start.10
  125.5 1.1 collective-permute-done.11
  126.6 1.5 collective-permute-start.12
  128.1 11.2 %collective-permute-done.12 = f32[256]{0:T(256)S(1)} collective-permute-done((f32[256]{0:T(256)S(1)}, f32[256]{0:T(256)S(1)}, u32[]{:S(2)}, u32[]{:S(2)}) %collective-permute-start.12) | collective-permute-done | bytes 1056 | tf_op jit(solution)/shard_map/ppermute | solution.py:103
  139.4 2.8 %fusion.13 = bf16[256,1024]{1,0:T(8,128)(2,1)} fusion(bf16[256,1024]{1,0:T(8,128)(2,1)S(1)} %copy-done.8, f32[256,4096]{1,0:T(8,128)} %copy-done.1, s32[]{:T(128)} %select_n.95, bf16[2,256,1024]{2,1,0:T(8,128)(2,1)} %collective-permute-done.9, bf16[1,256,1024]{2,1,0:T(8,128)(2,1)} %collective-permute-done.10, f32[256]{0:T(256)S(1)} %add_multiply_fusion, ...), kind=kLoop, calls=%fused_computation.31 | loop fusion | flops 3407872 | bytes 3677188 | tf_op jit(solution)/shard_map/convert_element_type | solution.py:286
  142.2 1.9 %copy.144 = bf16[256,1024]{1,0:T(8,128)(2,1)} copy(bf16[256,1024]{1,0:T(8,128)(2,1)} %bitcast.52) | data formatting | bytes 1048576
  (109 shorter events, 2.9 us)
Async XLA Ops:
  7.2 44.9 %copy-start = (bf16[4096,256]{1,0:T(8,128)(2,1)S(1)}, bf16[4096,256]{1,0:T(8,128)(2,1)}, u32[]{:S(2)}) copy-start(bf16[4096,256]{1,0:T(8,128)(2,1)} %param.13) | copy-start | bytes 6291460
  7.2 27.7 %all-gather.3.cloned.1.call-start = ((), (), s32[]{:S(2)}) async-start(), calls=%async_computation.1 | async-start | bytes 2621440 | tf_op jit(solution)/shard_map/all_gather | solution.py:176
  7.9 51.8 %all-gather.5.cloned.1.call-start = ((), (), s32[]{:S(2)}) async-start(), calls=%async_computation.2 | async-start | bytes 2621440 | tf_op jit(solution)/shard_map/all_gather | solution.py:211
  9.2 13.2 %collective-permute-start.2 = (bf16[32,1024]{1,0:T(8,128)(2,1)S(1)}, bf16[32,1024]{1,0:T(8,128)(2,1)S(1)}, u32[]{:S(2)}, u32[]{:S(2)}) collective-permute-start(bf16[32,1024]{1,0:T(8,128)(2,1)S(1)} %get-tuple-element.34), channel_id=1, source_target_pairs={{0,4},{4,8},{8,12},{12,16},{16,20},{20,24},{24,28},{28,0},{1,5},{5... | collective-permute-start | bytes 196616 | tf_op jit(solution)/shard_map/ppermute | solution.py:154
  12.2 11.6 %collective-permute-start.3 = (bf16[32,1024]{1,0:T(8,128)(2,1)S(1)}, bf16[32,1024]{1,0:T(8,128)(2,1)S(1)}, u32[]{:S(2)}, u32[]{:S(2)}) collective-permute-start(bf16[32,1024]{1,0:T(8,128)(2,1)S(1)} %get-tuple-element.33), channel_id=1, source_target_pairs={{0,8},{4,12},{8,16},{12,20},{16,24},{20,28},{24,0},{28,4},{1,9},{5... | collective-permute-start | bytes 196616 | tf_op jit(solution)/shard_map/ppermute | solution.py:154
  13.8 12.9 %collective-permute-start.4 = (bf16[32,1024]{1,0:T(8,128)(2,1)S(1)}, bf16[32,1024]{1,0:T(8,128)(2,1)S(1)}, u32[]{:S(2)}, u32[]{:S(2)}) collective-permute-start(bf16[32,1024]{1,0:T(8,128)(2,1)S(1)} %get-tuple-element.32), channel_id=1, source_target_pairs={{0,12},{4,16},{8,20},{12,24},{16,28},{20,0},{24,4},{28,8},{1,13},{... | collective-permute-start | bytes 196616 | tf_op jit(solution)/shard_map/ppermute | solution.py:154
  16.3 10.5 %collective-permute-start.5 = (bf16[32,1024]{1,0:T(8,128)(2,1)S(1)}, bf16[32,1024]{1,0:T(8,128)(2,1)S(1)}, u32[]{:S(2)}, u32[]{:S(2)}) collective-permute-start(bf16[32,1024]{1,0:T(8,128)(2,1)S(1)} %get-tuple-element.31), channel_id=1, source_target_pairs={{0,16},{4,20},{8,24},{12,28},{16,0},{20,4},{24,8},{28,12},{1,17},{... | collective-permute-start | bytes 196616 | tf_op jit(solution)/shard_map/ppermute | solution.py:154
  17.5 9.3 %collective-permute-start.6 = (bf16[32,1024]{1,0:T(8,128)(2,1)S(1)}, bf16[32,1024]{1,0:T(8,128)(2,1)S(1)}, u32[]{:S(2)}, u32[]{:S(2)}) collective-permute-start(bf16[32,1024]{1,0:T(8,128)(2,1)S(1)} %get-tuple-element.30), channel_id=1, source_target_pairs={{0,20},{4,24},{8,28},{12,0},{16,4},{20,8},{24,12},{28,16},{1,21},{... | collective-permute-start | bytes 196616 | tf_op jit(solution)/shard_map/ppermute | solution.py:154
  22.4 5.3 %collective-permute-start.7 = (bf16[32,1024]{1,0:T(8,128)(2,1)S(1)}, bf16[32,1024]{1,0:T(8,128)(2,1)S(1)}, u32[]{:S(2)}, u32[]{:S(2)}) collective-permute-start(bf16[32,1024]{1,0:T(8,128)(2,1)S(1)} %get-tuple-element.29), channel_id=1, source_target_pairs={{0,24},{4,28},{8,0},{12,4},{16,8},{20,12},{24,16},{28,20},{1,25},{... | collective-permute-start | bytes 196616 | tf_op jit(solution)/shard_map/ppermute | solution.py:154
  23.8 4.6 %collective-permute-start.8 = (bf16[32,1024]{1,0:T(8,128)(2,1)S(1)}, bf16[32,1024]{1,0:T(8,128)(2,1)S(1)}, u32[]{:S(2)}, u32[]{:S(2)}) collective-permute-start(bf16[32,1024]{1,0:T(8,128)(2,1)S(1)} %get-tuple-element.28), channel_id=1, source_target_pairs={{0,28},{4,0},{8,4},{12,8},{16,12},{20,16},{24,20},{28,24},{1,29},{... | collective-permute-start | bytes 196616 | tf_op jit(solution)/shard_map/ppermute | solution.py:154
  32.1 1.5 copy-start.21
  32.5 5.3 %copy-start.20 = (f32[4096]{0:T(1024)S(1)}, f32[4096]{0:T(1024)}, u32[]{:S(2)}) copy-start(f32[4096]{0:T(1024)} %param.10) | copy-start | bytes 49156
  33.7 14.9 %copy-start.17 = (pred[256,256]{0,1:T(8,128)(4,1)}, pred[256,256]{0,1:T(8,128)(4,1)S(1)}, u32[]{:S(2)}) copy-start(pred[256,256]{0,1:T(8,128)(4,1)S(1)} %fusion.30) | copy-start | bytes 196612
  34.9 2.8 %copy-start.4 = (bf16[256,4096]{1,0:T(8,128)(2,1)S(1)}, bf16[256,4096]{1,0:T(8,128)(2,1)}, u32[]{:S(2)}) copy-start(bf16[256,4096]{1,0:T(8,128)(2,1)} %all-gather.3.cloned.1.call-done) | copy-start | bytes 6291460
  37.7 14.3 %copy-start.23 = (f32[256]{0:T(256)}, f32[256]{0:T(256)S(1)}, u32[]{:S(2)}) copy-start(f32[256]{0:T(256)S(1)} %get-tuple-element.41) | copy-start | bytes 3076
  48.4 0.8 copy-start.9
  48.5 0.9 copy-start.11
  48.5 3.6 %copy-start.5 = (bf16[256,4096]{1,0:T(8,128)(2,1)S(1)}, bf16[256,4096]{1,0:T(8,128)(2,1)}, u32[]{:S(2)}) copy-start(bf16[256,4096]{1,0:T(8,128)(2,1)} %all-gather.3.cloned.1.call-done) | copy-start | bytes 6291460
  48.6 5.4 %copy-start.15 = (bf16[256,2,64]{2,0,1:T(8,128)(2,1)}, bf16[256,2,64]{2,0,1:T(8,128)(2,1)S(1)}, u32[]{:S(2)}) copy-start(bf16[256,2,64]{2,0,1:T(8,128)(2,1)S(1)} %get-tuple-element.25) | copy-start | bytes 196612
  66.3 2.7 %copy-start.13 = (bf16[256,1024]{0,1:T(8,128)(2,1)}, bf16[256,1024]{0,1:T(8,128)(2,1)S(1)}, u32[]{:S(2)}) copy-start(bf16[256,1024]{0,1:T(8,128)(2,1)S(1)} %copy.99) | copy-start | bytes 1572868
  66.3 2.7 %copy-start.18 = (pred[256,256]{0,1:T(8,128)(4,1)S(1)}, pred[256,256]{0,1:T(8,128)(4,1)}, u32[]{:S(2)}) copy-start(pred[256,256]{0,1:T(8,128)(4,1)} %copy-done.17) | copy-start | bytes 196612
  66.3 2.7 %copy-start.26 = (bf16[256,256]{0,1:T(8,128)(2,1)S(1)}, bf16[256,256]{0,1:T(8,128)(2,1)}, u32[]{:S(2)}) copy-start(bf16[256,256]{0,1:T(8,128)(2,1)} %convolution_convert_fusion.4) | copy-start | bytes 393220
  66.3 2.7 %copy-start.27 = (f32[2,256,256,4]{2,1,3,0:T(8,128)S(1)}, f32[2,256,256,4]{2,1,3,0:T(8,128)}, u32[]{:S(2)}) copy-start(f32[2,256,256,4]{2,1,3,0:T(8,128)} %get-tuple-element.43) | copy-start | bytes 6291460
  66.3 2.7 %copy-start.29 = (f32[2,4,256]{2,1,0:T(4,128)S(1)}, f32[2,4,256]{2,1,0:T(4,128)}, u32[]{:S(2)}) copy-start(f32[2,4,256]{2,1,0:T(4,128)} %get-tuple-element.42) | copy-start | bytes 24580
  66.3 5.1 %slice-start = ((s8[8388608]{0:T(1024)(128)(4,1)}), s8[4194304]{0:T(1024)(128)(4,1)S(1)}, s32[]{:S(2)}) async-start(s8[8388608]{0:T(1024)(128)(4,1)} %bitcast.170), calls=%async_computation.3 | async-start | bytes 8388608
  69.0 2.0 %copy-start.16 = (bf16[256,2,64]{2,0,1:T(8,128)(2,1)S(1)}, bf16[256,2,64]{2,0,1:T(8,128)(2,1)}, u32[]{:S(2)}) copy-start(bf16[256,2,64]{2,0,1:T(8,128)(2,1)} %copy-done.15) | copy-start | bytes 196612
  69.0 2.8 %slice-start.1 = ((s8[8388608]{0:T(1024)(128)(4,1)}), s8[4194304]{0:T(1024)(128)(4,1)S(1)}, s32[]{:S(2)}) async-start(s8[8388608]{0:T(1024)(128)(4,1)} %bitcast.170), calls=%async_computation.4 | async-start | bytes 8388608
  74.4 2.4 %copy-start.2 = (f32[256,4096]{1,0:T(8,128)}, f32[256,4096]{1,0:T(8,128)S(1)}, u32[]{:S(2)}) copy-start(f32[256,4096]{1,0:T(8,128)S(1)} %fusion.54) | copy-start | bytes 12582916
  76.8 9.1 %collective-permute-start = (bf16[2,256,1024]{2,1,0:T(8,128)(2,1)}, bf16[2,256,1024]{2,1,0:T(8,128)(2,1)}, u32[]{:S(2)}, u32[]{:S(2)}) collective-permute-start(bf16[2,256,1024]{2,1,0:T(8,128)(2,1)} %pad_maximum_fusion), channel_id=1, source_target_pairs={{0,1},{1,0},{2,3},{3,2},{4,5},{5,4},{6,7},{7,6},{8,9},{9,8},{10,11... | collective-permute-start | bytes 3145736 | tf_op jit(solution)/shard_map/ppermute | solution.py:101
  82.9 2.2 %copy-start.10 = (bf16[256,8,64]{2,0,1:T(8,128)(2,1)S(1)}, bf16[256,8,64]{2,0,1:T(8,128)(2,1)}, u32[]{:S(2)}) copy-start(bf16[256,8,64]{2,0,1:T(8,128)(2,1)} %copy-done.9) | copy-start | bytes 786436
  82.9 2.2 %copy-start.12 = (bf16[256,8,64]{2,0,1:T(8,128)(2,1)S(1)}, bf16[256,8,64]{2,0,1:T(8,128)(2,1)}, u32[]{:S(2)}) copy-start(bf16[256,8,64]{2,0,1:T(8,128)(2,1)} %copy-done.11) | copy-start | bytes 786436
  84.8 2.2 %copy-start.3 = (f32[256,4096]{1,0:T(8,128)S(1)}, f32[256,4096]{1,0:T(8,128)}, u32[]{:S(2)}) copy-start(f32[256,4096]{1,0:T(8,128)} %copy-done.2) | copy-start | bytes 12582916
  85.6 3.2 %copy-start.14 = (bf16[256,1024]{0,1:T(8,128)(2,1)S(1)}, bf16[256,1024]{0,1:T(8,128)(2,1)}, u32[]{:S(2)}) copy-start(bf16[256,1024]{0,1:T(8,128)(2,1)} %copy-done.13) | copy-start | bytes 1572868
  85.6 3.2 %copy-start.19 = (pred[256,256]{0,1:T(8,128)(4,1)S(1)}, pred[256,256]{0,1:T(8,128)(4,1)}, u32[]{:S(2)}) copy-start(pred[256,256]{0,1:T(8,128)(4,1)} %copy-done.17) | copy-start | bytes 196612
  85.7 3.2 %copy-start.28 = (f32[2,256,256,4]{2,1,3,0:T(8,128)S(1)}, f32[2,256,256,4]{2,1,3,0:T(8,128)}, u32[]{:S(2)}) copy-start(f32[2,256,256,4]{2,1,3,0:T(8,128)} %get-tuple-element.43) | copy-start | bytes 6291460
  85.7 3.2 %copy-start.30 = (f32[2,4,256]{2,1,0:T(4,128)S(1)}, f32[2,4,256]{2,1,0:T(4,128)}, u32[]{:S(2)}) copy-start(f32[2,4,256]{2,1,0:T(4,128)} %get-tuple-element.42) | copy-start | bytes 24580
  87.0 16.9 %slice-start.2 = ((s8[8388608]{0:T(1024)(128)(4,1)}), s8[4194304]{0:T(1024)(128)(4,1)S(1)}, s32[]{:S(2)}) async-start(s8[8388608]{0:T(1024)(128)(4,1)} %bitcast.196), calls=%async_computation.6 | async-start | bytes 8388608
  88.3 14.2 %collective-permute-start.1 = (bf16[1,256,1024]{2,1,0:T(8,128)(2,1)S(1)}, bf16[1,256,1024]{2,1,0:T(8,128)(2,1)S(1)}, u32[]{:S(2)}, u32[]{:S(2)}) collective-permute-start(bf16[1,256,1024]{2,1,0:T(8,128)(2,1)S(1)} %fusion.22), channel_id=1, source_target_pairs={{0,2},{1,3},{2,0},{3,1},{4,6},{5,7},{6,4},{7,5},{8,10},{9,11},{10,... | collective-permute-start | bytes 1572872 | tf_op jit(solution)/shard_map/ppermute | solution.py:101
  88.8 13.6 %copy-start.8 = (bf16[256,1024]{1,0:T(8,128)(2,1)S(1)}, bf16[256,1024]{1,0:T(8,128)(2,1)}, u32[]{:S(2)}) copy-start(bf16[256,1024]{1,0:T(8,128)(2,1)} %param.9) | copy-start | bytes 1572868
  88.9 15.0 %slice-start.3 = ((s8[8388608]{0:T(1024)(128)(4,1)}), s8[4194304]{0:T(1024)(128)(4,1)S(1)}, s32[]{:S(2)}) async-start(s8[8388608]{0:T(1024)(128)(4,1)} %bitcast.196), calls=%async_computation.7 | async-start | bytes 8388608
  108.4 3.7 %copy-start.6 = (bf16[256,4096]{1,0:T(8,128)(2,1)S(1)}, bf16[256,4096]{1,0:T(8,128)(2,1)}, u32[]{:S(2)}) copy-start(bf16[256,4096]{1,0:T(8,128)(2,1)} %all-gather.3.cloned.1.call-done) | copy-start | bytes 6291460
  113.2 2.3 %copy-start.1 = (f32[256,4096]{1,0:T(8,128)}, f32[256,4096]{1,0:T(8,128)S(1)}, u32[]{:S(2)}) copy-start(f32[256,4096]{1,0:T(8,128)S(1)} %get-tuple-element.47) | copy-start | bytes 12582916
  113.2 2.3 %copy-start.25 = (s32[8]{0:T(128)S(1)}, s32[8]{0:T(128)}, u32[]{:S(2)}) copy-start(s32[8]{0:T(128)} %get-tuple-element.13) | copy-start | bytes 100
  115.6 7.1 %collective-permute-start.9 = (bf16[2,256,1024]{2,1,0:T(8,128)(2,1)}, bf16[2,256,1024]{2,1,0:T(8,128)(2,1)}, u32[]{:S(2)}, u32[]{:S(2)}) collective-permute-start(bf16[2,256,1024]{2,1,0:T(8,128)(2,1)} %pad_maximum_fusion.1), channel_id=1, source_target_pairs={{0,1},{1,0},{2,3},{3,2},{4,5},{5,4},{6,7},{7,6},{8,9},{9,8},{10,11... | collective-permute-start | bytes 3145736 | tf_op jit(solution)/shard_map/ppermute | solution.py:103
  116.0 23.4 %copy-start.7 = (bf16[8,32,1024]{2,1,0:T(8,128)(2,1)S(1)}, bf16[8,32,1024]{2,1,0:T(8,128)(2,1)}, u32[]{:S(2)}) copy-start(bf16[8,32,1024]{2,1,0:T(8,128)(2,1)} %copy.98) | copy-start | bytes 1572868
  116.0 23.4 %dynamic-slice-start = ((f32[4096]{0:T(1024)}, s32[]{:T(128)}), f32[1024]{0:T(1024)S(1)}, s32[]{:S(2)}) async-start(f32[4096]{0:T(1024)} %param.10, s32[]{:T(128)} %select_n.95), calls=%async_computation.5 | async-start | bytes 8704 | tf_op jit(solution)/shard_map/dynamic_slice | solution.py:137
  116.0 23.4 %copy-start.22 = (f32[256]{0:T(256)S(1)}, f32[256]{0:T(256)}, u32[]{:S(2)}) copy-start(f32[256]{0:T(256)} %get-tuple-element.40) | copy-start | bytes 3076
  116.0 23.4 %copy-start.24 = (f32[256]{0:T(256)S(1)}, f32[256]{0:T(256)}, u32[]{:S(2)}) copy-start(f32[256]{0:T(256)} %copy-done.23) | copy-start | bytes 3076
  117.1 22.2 %all-to-all-start = ((bf16[8,32,1024]{2,1,0:T(8,128)(2,1)}), bf16[8,32,1024]{2,1,0:T(8,128)(2,1)}, u32[]{:S(2)}, u32[]{:S(2)}) async-start(bf16[8,32,1024]{2,1,0:T(8,128)(2,1)} %copy.111), calls=%async_computation | async-start | bytes 1048576 | tf_op jit(solution)/shard_map/all_to_all | solution.py:250
  124.9 14.4 %collective-permute-start.10 = (bf16[1,256,1024]{2,1,0:T(8,128)(2,1)}, bf16[1,256,1024]{2,1,0:T(8,128)(2,1)}, u32[]{:S(2)}, u32[]{:S(2)}) collective-permute-start(bf16[1,256,1024]{2,1,0:T(8,128)(2,1)} %fusion.23), channel_id=1, source_target_pairs={{0,2},{1,3},{2,0},{3,1},{4,6},{5,7},{6,4},{7,5},{8,10},{9,11},{10,... | collective-permute-start | bytes 1572872 | tf_op jit(solution)/shard_map/ppermute | solution.py:103
  125.5 1.1 collective-permute-start.11
  126.6 12.7 %collective-permute-start.12 = (f32[256]{0:T(256)S(1)}, f32[256]{0:T(256)S(1)}, u32[]{:S(2)}, u32[]{:S(2)}) collective-permute-start(f32[256]{0:T(256)S(1)} %add.200), channel_id=1, source_target_pairs={{0,2},{1,3},{2,0},{3,1},{4,6},{5,7},{6,4},{7,5},{8,10},{9,11},{10,... | collective-permute-start | bytes 3080 | tf_op jit(solution)/shard_map/ppermute | solution.py:103
Sparse Core Ops, SparseCore 0:
  9.6 25.2 all-gather.2
  37.0 22.5 all-gather.4

commit v9 on v8

--- a/solution.py
+++ b/solution.py
@@ -240,17 +240,6 @@
         grad_query_rot.reshape(token_row_count, heads_local, HEAD_SIZE), cosine, sine_table
     ).astype(jnp.bfloat16)
     key_gradient = unrotate(grad_keys_rot, cosine, sine_table).astype(jnp.bfloat16)
-    output_home, grad_query, key_gradient, value_gradient = lax.optimization_barrier(
-        (output_home, grad_query, key_gradient, value_gradient)
-    )
-    home_blocks = output_home.reshape(block_count, home_rows, width_part)
-    outgoing = jnp.einsum(
-        "dj,jrw->drw", send_table, home_blocks, preferred_element_type=jnp.float32
-    ).astype(jnp.bfloat16)
-    relaid = lax.all_to_all(outgoing, "dp", split_axis=0, concat_axis=0, tiled=True).reshape(
-        token_row_count, width_part
-    )
-
     contract_out = (((1,), (1,)), ((), ()))
     normed_partial = (
         lax.dot_general(
@@ -272,7 +261,16 @@
             preferred_element_type=jnp.float32,
         )
     )
+    output_home, normed_partial = lax.optimization_barrier((output_home, normed_partial))
     stat_partial = jnp.sum(normed_partial * norm_gain[None, :] * gathered_float, axis=1)
+    home_blocks = output_home.reshape(block_count, home_rows, width_part)
+    outgoing = jnp.einsum(
+        "dj,jrw->drw", send_table, home_blocks, preferred_element_type=jnp.float32
+    ).astype(jnp.bfloat16)
+    relaid = lax.all_to_all(outgoing, "dp", split_axis=0, concat_axis=0, tiled=True).reshape(
+        token_row_count, width_part
+    )
+
     normed_gradient, stat_sum = scatter_features(
         normed_partial, "tensor", tensor_size, tensor_index, extra=stat_partial
     )

time: 152 us -> 147 us (0.967)
  waiting for transfers between devices: 32.9 us -> 27.6 us
  local copies, waits for them, and re-layouts: 22.1 us -> 24.6 us
    dot_general x1, matrix products: 2.62 us -> 5.94 us  [per_device(): jnp.dot(attended_flat, w_out, preferred_element_type=jnp.float32)]
    dot_general x1, matrix products: 3.73 us -> 0.76 us  [per_device(): lax.dot_general(key_gradient.reshape(token_row_count, key_width), key_wei...]
    ppermute x4, waiting for transfers between devices: 12.4 us -> 9.47 us  [scatter_features(): lax.ppermute((outgoing, extra), axis_name, _xor_pairs(size, bit))]
    reduce_sum x0 -> x1, other arithmetic: none -> 2.82 us  [per_device(): jnp.sum(normed_partial * norm_gain[None, :] * gathered_float, axis=1)]
    convert_element_type x1, local copies, waits for them, and re-layouts: 0.2 us -> 2.05 us  [per_device(): attended_gradient = lax.dot_general(grad_full, w_out, (((1,), (1,)), ((),...]
    dot_general x1, matrix products: 2.76 us -> 1.16 us  [per_device(): jnp.dot(normed_input, key_weight, preferred_element_type=jnp.float32)]
    unnamed x77 -> x71, local copies, waits for them, and re-layouts: 11.4 us -> 11.1 us
  transfers between devices with their start and end apart: 16 -> 16, of which waited for: 5 -> 5; matrix products, arithmetic and copies ran while one was open for 29% -> 32% of each run, Pallas kernels for 0% -> 0%
where the time goes in v9:
time: 147 us; the launch traced here: 146 us
  matrix products  39.8 us (27%)
  waiting for transfers between devices  27.6 us (19%)
  local copies, waits for them, and re-layouts  24.6 us (17%)
  starting transfers between devices  20.9 us (14%)
  other arithmetic  18.2 us (12%)
  between operations  14.7 us (10%)
    ppermute x7, starting transfers between devices, per_device(): returned.append(lax.ppermute(piece, 'dp', pairs))  12.5 us
    ppermute x2, waiting for transfers between devices, scatter_features(): incoming = lax.ppermute(outgoing, axis_name, _xor_pairs(size, bit))  11.6 us
    unnamed x71, local copies, waits for them, and re-layouts  11.1 us
    ppermute x4, waiting for transfers between devices, scatter_features(): lax.ppermute((outgoing, extra), axis_name, _xor_pairs(size, bit))  9.47 us
    dot_general x1, matrix products, per_device(): lax.dot_general(grad_full, w_out, (((1,), (1,)), ((), ())), preferred_ele...  7.18 us
    dot_general x1, matrix products, per_device(): jnp.dot(normed_input, w_query, preferred_element_type=jnp.float32)  7.1 us
    another operation x8, local copies, waits for them, and re-layouts, per_device(): returned = jnp.stack(returned)  6.43 us
    dot_general x1, matrix products, per_device(): jnp.dot(attended_flat, w_out, preferred_element_type=jnp.float32)  5.94 us
  transfers between devices with their start and end apart: 16, of which 5 were waited for; matrix products, arithmetic and copies ran while one was open for 32% of the time, Pallas kernels for 0%

profile of v9, /device:TPU:0, one launch (start us, length us, event | category | flops | bytes accessed | tf_op | source)
XLA Modules:
  0.0 145.8 jit_solution(15019460032149513648)
XLA Ops:
  7.2 0.7 all-gather.3.cloned.1.call-update
  8.1 1.1 dynamic-slice_bitcast_fusion
  9.2 6.0 %collective-permute-start.8 = (bf16[32,1024]{1,0:T(8,128)(2,1)S(1)}, bf16[32,1024]{1,0:T(8,128)(2,1)S(1)}, u32[]{:S(2)}, u32[]{:S(2)}) collective-permute-start(bf16[32,1024]{1,0:T(8,128)(2,1)S(1)} %get-tuple-element.24), channel_id=1, source_target_pairs={{0,28},{4,0},{8,4},{12,8},{16,12},{20,16},{24,20},{28,24},{1,29},{... | collective-permute-start | bytes 196616 | tf_op jit(solution)/shard_map/ppermute | solution.py:154
  15.2 0.4 collective-permute-start.7
  15.7 3.0 %collective-permute-start.5 = (bf16[32,1024]{1,0:T(8,128)(2,1)S(1)}, bf16[32,1024]{1,0:T(8,128)(2,1)S(1)}, u32[]{:S(2)}, u32[]{:S(2)}) collective-permute-start(bf16[32,1024]{1,0:T(8,128)(2,1)S(1)} %get-tuple-element.27), channel_id=1, source_target_pairs={{0,16},{4,20},{8,24},{12,28},{16,0},{20,4},{24,8},{28,12},{1,17},{... | collective-permute-start | bytes 196616 | tf_op jit(solution)/shard_map/ppermute | solution.py:154
  18.7 0.8 reduce-window.8
  19.5 0.7 fusion.39
  20.2 0.5 multiply_cosine_fusion
  20.9 1.9 %collective-permute-start.3 = (bf16[32,1024]{1,0:T(8,128)(2,1)S(1)}, bf16[32,1024]{1,0:T(8,128)(2,1)S(1)}, u32[]{:S(2)}, u32[]{:S(2)}) collective-permute-start(bf16[32,1024]{1,0:T(8,128)(2,1)S(1)} %get-tuple-element.29), channel_id=1, source_target_pairs={{0,8},{4,12},{8,16},{12,20},{16,24},{20,28},{24,0},{28,4},{1,9},{5... | collective-permute-start | bytes 196616 | tf_op jit(solution)/shard_map/ppermute | solution.py:154
  22.8 1.1 collective-permute-start.2
  23.9 1.3 and_select_fusion
  25.5 0.6 copy-done.16
  26.1 0.9 copy.94
  27.1 1.5 %collective-permute-done.4 = bf16[32,1024]{1,0:T(8,128)(2,1)S(1)} collective-permute-done((bf16[32,1024]{1,0:T(8,128)(2,1)S(1)}, bf16[32,1024]{1,0:T(8,128)(2,1)S(1)}, u32[]{:S(2)}, u32[]{:S(2)}) %collective-permute-start.4) | collective-permute-done | bytes 65568 | tf_op jit(solution)/shard_map/ppermute | solution.py:154
  28.6 0.8 copy.93
  29.3 0.8 copy.92
  30.1 0.8 copy.91
  30.8 2.9 %stack.61 = bf16[8,32,1024]{2,0,1:T(8,128)(2,1)S(1)} concatenate(bf16[1,32,1024]{2,0,1:T(2,128)(2,1)S(1)} %copy.132, bf16[1,32,1024]{2,0,1:T(2,128)(2,1)} %copy.91, bf16[1,32,1024]{2,0,1:T(2,128)(2,1)} %copy.92, bf16[1,32,1024]{2,0,1:T(2,128)(2,1)} %copy.93, bf16[1,32,1024]{2,0,1:T(2,128)(2,1)S(1)} %copy.94, bf16[1,32,1024]{2,0,1:T(2,128)(2,1)S(1)} %copy.95, ...), dimensions={0} | concatenate | bytes 1048576 | tf_op jit(solution)/shard_map/stack | solution.py:155
  33.8 0.4 convolution_convert_fusion.3
  34.2 1.1 copy.98
  35.3 0.7 fusion.31
  36.0 2.2 %fusion = f32[256]{0:T(256)S(1)} fusion(bf16[256,4096]{1,0:T(8,128)(2,1)} %all-gather.3.cloned.1.call-done), kind=kLoop, calls=%fused_computation.5 | loop fusion | flops 3145472 | bytes 2098176 | tf_op jit(solution)/shard_map/reduce_sum | solution.py:178
  38.2 0.6 multiply_multiply_fusion
  38.8 1.2 fusion.47
  40.0 0.8 copy.131
  40.8 0.8 copy.130
  41.7 7.1 %convolution_bitcast_fusion = f32[32,8,8,128]{3,1,2,0:T(8,128)S(1)} fusion(bf16[4096,1024]{1,0:T(8,128)(2,1)} %param.11, bf16[256,4096]{1,0:T(8,128)(2,1)} %all-gather.3.cloned.1.call-done, f32[4096]{0:T(1024)S(1)} %copy-done.20, f32[256]{0:T(256)S(1)} %get-tuple-element.37), kind=kOutput, calls=%fused_computation.16 | convolution fusion | flops 2151677952 | bytes 11551744 | tf_op jit(solution)/shard_map/dot_general | solution.py:180
  49.0 0.5 subtract_convert_fusion.1
  50.1 0.6 copy-done.14
  50.8 2.7 %fusion.7 = (f32[2,4,256]{2,1,0:T(4,128)}, f32[2,256,256,4]{2,1,3,0:T(8,128)}) fusion(pred[256,256]{0,1:T(8,128)(4,1)S(1)} %copy-done.17, bf16[256,2,4,64]{3,0,2,1:T(8,128)(2,1)S(1)} %bitcast.177, bf16[256,2,4,64]{3,0,2,1:T(8,128)(2,1)S(1)} %bitcast.175, bf16[256,2,64]{2,0,1:T(8,128)(2,1)S(1)} %get-tuple-element.21, ...), kind=kOutput, calls=%fused_computation.14 | convolution fusion | flops 137099264 | bytes 2826240 | tf_op jit(solution)/shard_map/qkgd,skd->kgqs/dot_general | solution.py:198
  53.5 1.9 %convolution_convert_fusion.4 = bf16[256,256]{0,1:T(8,128)(2,1)} fusion(bf16[4096,256]{1,0:T(8,128)(2,1)S(1)} %copy-done.8, bf16[256,4096]{1,0:T(8,128)(2,1)S(1)} %copy-done.3, f32[4096]{0:T(1024)S(1)} %copy-done.20, f32[256]{0:T(256)S(1)} %copy-done.24), kind=kOutput, calls=%fused_computation.28 | convolution fusion | flops 541130752 | bytes 4342784 | tf_op jit(solution)/shard_map/dot_general | solution.py:182
  55.3 4.3 %all-gather.5.cloned.1.call-done = bf16[256,4096]{1,0:T(8,128)(2,1)} async-done(((bf16[256,1024]{1,0:T(8,128)(2,1)}), bf16[256,4096]{1,0:T(8,128)(2,1)}) %all-gather.5.cloned.1.call-update) | async-done | bytes 2097168 | tf_op jit(solution)/shard_map/all_gather | solution.py:211
  59.7 7.2 %convolution_convert_fusion = bf16[256,1024]{1,0:T(8,128)(2,1)} fusion(bf16[256,4096]{1,0:T(8,128)(2,1)} %all-gather.5.cloned.1.call-done, bf16[1024,4096]{1,0:T(8,128)(2,1)} %param.14), kind=kOutput, calls=%fused_computation.19 | convolution fusion | flops 2147745792 | bytes 11010048 | tf_op jit(solution)/shard_map/dot_general | solution.py:212
  66.9 2.1 %copy.99 = bf16[256,1024]{0,1:T(8,128)(2,1)} copy(bf16[256,1024]{1,0:T(8,128)(2,1)} %convolution_convert_fusion) | data formatting | bytes 1048576 | tf_op jit(solution)/shard_map/convert_element_type | solution.py:217
  68.9 3.4 %multiply_reduce_fusion = (f32[256,2,4]{0,2,1:T(4,128)S(1)}, bf16[2,128,4,256]{3,1,2,0:T(8,128)(2,1)}) fusion(bf16[256,1024]{0,1:T(8,128)(2,1)} %copy.99, bf16[256,2,128,1]{0,2,3,1:T(8,128)(2,1)} %bitcast.197, f32[2,4,256]{2,1,0:T(4,128)} %get-tuple-element.38, f32[2,256,256,4]{2,1,3,0:T(8,128)} %get-tuple-element.39, pred[256,256]{0,1:T(8,128)(4,1)} %fusion.31), kind=kOutput, calls=%fused_computation.49 | convolution fusion | flops 137623552 | bytes 3358720 | tf_op jit(solution)/shard_map/kgqs,skd->qkgd/dot_general | solution.py:204
  72.4 0.7 fusion.5
  73.1 0.5 fusion.9
  73.7 0.4 copy-done.15
  74.0 0.4 convolution_multiply_fusion
  74.5 1.1 fusion.53
  75.5 0.4 add_convert_fusion.2
  76.1 1.5 %copy.134 = f32[256,8,64]{2,1,0:T(8,128)S(1)} copy(f32[256,8,64]{0,2,1:T(8,128)} %get-tuple-element.18) | data formatting | bytes 1048576
  77.6 2.4 %copy.133 = f32[256,8,64]{2,1,0:T(8,128)} copy(f32[256,8,64]{0,2,1:T(8,128)} %get-tuple-element.19) | data formatting | bytes 1048576
  80.0 5.9 %fusion.55 = f32[256,4096]{1,0:T(8,128)S(1)} fusion(bf16[256,1024]{0,1:T(8,128)(2,1)} %bitcast.180, bf16[1024,4096]{1,0:T(8,128)(2,1)} %param.14), kind=kOutput, calls=%fused_computation.118 | convolution fusion | flops 2147483648 | bytes 13107200 | tf_op jit(solution)/shard_map/dot_general | solution.py:208
  86.5 0.6 copy-done.7
  87.7 5.8 %fusion.25 = f32[256,4096]{1,0:T(8,128)S(1)} fusion(bf16[4096,1024]{1,0:T(8,128)(2,1)} %param.11, bf16[32,8,8,128]{3,2,1,0:T(8,128)(2,1)S(1)} %bitcast.181), kind=kOutput, calls=%fused_computation.60 | convolution fusion | flops 2147483648 | bytes 13107200 | tf_op jit(solution)/shard_map/dot_general | solution.py:245
  93.5 0.8 convolution_add_fusion.1
  94.5 0.4 collective-permute-start.1
  95.1 0.4 copy-done.13
  95.5 0.7 fusion.10
  96.3 0.8 convolution_add_fusion
  97.1 11.5 %collective-permute-done.1 = bf16[1,256,1024]{2,1,0:T(8,128)(2,1)S(1)} collective-permute-done((bf16[1,256,1024]{2,1,0:T(8,128)(2,1)S(1)}, bf16[1,256,1024]{2,1,0:T(8,128)(2,1)S(1)}, u32[]{:S(2)}, u32[]{:S(2)}) %collective-permute-start.1) | collective-permute-done | bytes 524320 | tf_op jit(solution)/shard_map/ppermute | solution.py:101
  109.1 1.1 pad_maximum_fusion.1
  110.3 0.4 convolution_convert_fusion.2
  110.7 1.1 copy.112
  111.8 5.5 %all-to-all-start = ((bf16[8,32,1024]{2,1,0:T(8,128)(2,1)}), bf16[8,32,1024]{2,1,0:T(8,128)(2,1)}, u32[]{:S(2)}, u32[]{:S(2)}) async-start(bf16[8,32,1024]{2,1,0:T(8,128)(2,1)} %copy.112), calls=%async_computation | async-start | bytes 1048576 | tf_op jit(solution)/shard_map/all_to_all | solution.py:270
  117.3 2.5 %fusion.24 = bf16[1,256,1024]{2,1,0:T(8,128)(2,1)} fusion(f32[256,4096]{1,0:T(8,128)} %copy-done.1, s32[]{:T(128)S(6)} %select_n.98, bf16[2,256,1024]{2,1,0:T(8,128)(2,1)} %collective-permute-done.9), kind=kLoop, calls=%fused_computation.59 | loop fusion | flops 786432 | bytes 2097156 | tf_op jit(solution)/shard_map/convert_element_type | solution.py:99
  119.8 0.6 collective-permute-start.10
  120.4 2.8 %fusion.3 = f32[256]{0:T(256)S(1)} fusion(bf16[256,4096]{1,0:T(8,128)(2,1)S(1)} %copy-done.4, f32[256,4096]{1,0:T(8,128)} %copy-done.1, f32[4096]{0:T(1024)S(1)} %copy-done.20), kind=kLoop, calls=%fused_computation.8 | loop fusion | flops 4194048 | bytes 6308864 | tf_op jit(solution)/shard_map/reduce_sum | solution.py:265
  123.3 1.1 collective-permute-done.11
  124.4 1.5 %collective-permute-start.12 = (f32[256]{0:T(256)S(1)}, f32[256]{0:T(256)S(1)}, u32[]{:S(2)}, u32[]{:S(2)}) collective-permute-start(f32[256]{0:T(256)S(1)} %add.200), channel_id=1, source_target_pairs={{0,2},{1,3},{2,0},{3,1},{4,6},{5,7},{6,4},{7,5},{8,10},{9,11},{10,... | collective-permute-start | bytes 3080 | tf_op jit(solution)/shard_map/ppermute | solution.py:103
  125.9 8.3 %collective-permute-done.12 = f32[256]{0:T(256)S(1)} collective-permute-done((f32[256]{0:T(256)S(1)}, f32[256]{0:T(256)S(1)}, u32[]{:S(2)}, u32[]{:S(2)}) %collective-permute-start.12) | collective-permute-done | bytes 1056 | tf_op jit(solution)/shard_map/ppermute | solution.py:103
  134.3 2.8 %fusion.14 = bf16[256,1024]{1,0:T(8,128)(2,1)} fusion(bf16[256,1024]{1,0:T(8,128)(2,1)S(1)} %copy-done.6, f32[256,4096]{1,0:T(8,128)} %copy-done.1, s32[]{:T(128)} %select_n.95, bf16[2,256,1024]{2,1,0:T(8,128)(2,1)} %collective-permute-done.9, bf16[1,256,1024]{2,1,0:T(8,128)(2,1)} %collective-permute-done.10, f32[256]{0:T(256)S(1)} %add_multiply_fusion, ...), kind=kLoop, calls=%fused_computation.32 | loop fusion | flops 3407872 | bytes 3677188 | tf_op jit(solution)/shard_map/convert_element_type | solution.py:284
  137.1 1.9 %copy.144 = bf16[256,1024]{1,0:T(8,128)(2,1)} copy(bf16[256,1024]{1,0:T(8,128)(2,1)} %bitcast.54) | data formatting | bytes 1048576
  (102 shorter events, 3.8 us)
Async XLA Ops:
  7.2 31.6 %copy-start = (bf16[4096,256]{1,0:T(8,128)(2,1)S(1)}, bf16[4096,256]{1,0:T(8,128)(2,1)}, u32[]{:S(2)}) copy-start(bf16[4096,256]{1,0:T(8,128)(2,1)} %param.12) | copy-start | bytes 6291460
  7.2 28.8 %all-gather.3.cloned.1.call-start = ((), (), s32[]{:S(2)}) async-start(), calls=%async_computation.1 | async-start | bytes 2621440 | tf_op jit(solution)/shard_map/all_gather | solution.py:176
  7.9 51.8 %all-gather.5.cloned.1.call-start = ((), (), s32[]{:S(2)}) async-start(), calls=%async_computation.2 | async-start | bytes 2621440 | tf_op jit(solution)/shard_map/all_gather | solution.py:211
  9.2 11.7 %collective-permute-start.8 = (bf16[32,1024]{1,0:T(8,128)(2,1)S(1)}, bf16[32,1024]{1,0:T(8,128)(2,1)S(1)}, u32[]{:S(2)}, u32[]{:S(2)}) collective-permute-start(bf16[32,1024]{1,0:T(8,128)(2,1)S(1)} %get-tuple-element.24), channel_id=1, source_target_pairs={{0,28},{4,0},{8,4},{12,8},{16,12},{20,16},{24,20},{28,24},{1,29},{... | collective-permute-start | bytes 196616 | tf_op jit(solution)/shard_map/ppermute | solution.py:154
  15.2 7.5 %collective-permute-start.7 = (bf16[32,1024]{1,0:T(8,128)(2,1)S(1)}, bf16[32,1024]{1,0:T(8,128)(2,1)S(1)}, u32[]{:S(2)}, u32[]{:S(2)}) collective-permute-start(bf16[32,1024]{1,0:T(8,128)(2,1)S(1)} %get-tuple-element.25), channel_id=1, source_target_pairs={{0,24},{4,28},{8,0},{12,4},{16,8},{20,12},{24,16},{28,20},{1,25},{... | collective-permute-start | bytes 196616 | tf_op jit(solution)/shard_map/ppermute | solution.py:154
  15.7 9.7 %collective-permute-start.6 = (bf16[32,1024]{1,0:T(8,128)(2,1)S(1)}, bf16[32,1024]{1,0:T(8,128)(2,1)S(1)}, u32[]{:S(2)}, u32[]{:S(2)}) collective-permute-start(bf16[32,1024]{1,0:T(8,128)(2,1)S(1)} %get-tuple-element.26), channel_id=1, source_target_pairs={{0,20},{4,24},{8,28},{12,0},{16,4},{20,8},{24,12},{28,16},{1,21},{... | collective-permute-start | bytes 196616 | tf_op jit(solution)/shard_map/ppermute | solution.py:154
  15.7 9.8 %collective-permute-start.5 = (bf16[32,1024]{1,0:T(8,128)(2,1)S(1)}, bf16[32,1024]{1,0:T(8,128)(2,1)S(1)}, u32[]{:S(2)}, u32[]{:S(2)}) collective-permute-start(bf16[32,1024]{1,0:T(8,128)(2,1)S(1)} %get-tuple-element.27), channel_id=1, source_target_pairs={{0,16},{4,20},{8,24},{12,28},{16,0},{20,4},{24,8},{28,12},{1,17},{... | collective-permute-start | bytes 196616 | tf_op jit(solution)/shard_map/ppermute | solution.py:154
  18.7 9.9 %collective-permute-start.4 = (bf16[32,1024]{1,0:T(8,128)(2,1)S(1)}, bf16[32,1024]{1,0:T(8,128)(2,1)S(1)}, u32[]{:S(2)}, u32[]{:S(2)}) collective-permute-start(bf16[32,1024]{1,0:T(8,128)(2,1)S(1)} %get-tuple-element.28), channel_id=1, source_target_pairs={{0,12},{4,16},{8,20},{12,24},{16,28},{20,0},{24,4},{28,8},{1,13},{... | collective-permute-start | bytes 196616 | tf_op jit(solution)/shard_map/ppermute | solution.py:154
  20.9 8.4 %collective-permute-start.3 = (bf16[32,1024]{1,0:T(8,128)(2,1)S(1)}, bf16[32,1024]{1,0:T(8,128)(2,1)S(1)}, u32[]{:S(2)}, u32[]{:S(2)}) collective-permute-start(bf16[32,1024]{1,0:T(8,128)(2,1)S(1)} %get-tuple-element.29), channel_id=1, source_target_pairs={{0,8},{4,12},{8,16},{12,20},{16,24},{20,28},{24,0},{28,4},{1,9},{5... | collective-permute-start | bytes 196616 | tf_op jit(solution)/shard_map/ppermute | solution.py:154
  22.8 7.3 %collective-permute-start.2 = (bf16[32,1024]{1,0:T(8,128)(2,1)S(1)}, bf16[32,1024]{1,0:T(8,128)(2,1)S(1)}, u32[]{:S(2)}, u32[]{:S(2)}) collective-permute-start(bf16[32,1024]{1,0:T(8,128)(2,1)S(1)} %get-tuple-element.30), channel_id=1, source_target_pairs={{0,4},{4,8},{8,12},{12,16},{16,20},{20,24},{24,28},{28,0},{1,5},{5... | collective-permute-start | bytes 196616 | tf_op jit(solution)/shard_map/ppermute | solution.py:154
  25.5 0.6 copy-start.16
  33.8 1.5 %copy-start.21 = (s32[256]{0:T(256)S(1)}, s32[256]{0:T(256)}, u32[]{:S(2)}) copy-start(s32[256]{0:T(256)} %get-tuple-element.6) | copy-start | bytes 3076
  34.1 4.7 %copy-start.20 = (f32[4096]{0:T(1024)S(1)}, f32[4096]{0:T(1024)}, u32[]{:S(2)}) copy-start(f32[4096]{0:T(1024)} %param.10) | copy-start | bytes 49156
  36.0 2.8 %copy-start.2 = (bf16[256,4096]{1,0:T(8,128)(2,1)S(1)}, bf16[256,4096]{1,0:T(8,128)(2,1)}, u32[]{:S(2)}) copy-start(bf16[256,4096]{1,0:T(8,128)(2,1)} %all-gather.3.cloned.1.call-done) | copy-start | bytes 6291460
  38.8 2.9 %copy-start.23 = (f32[256]{0:T(256)}, f32[256]{0:T(256)S(1)}, u32[]{:S(2)}) copy-start(f32[256]{0:T(256)S(1)} %get-tuple-element.37) | copy-start | bytes 3076
  49.0 1.0 copy-start.10
  49.0 1.0 copy-start.11
  49.5 1.2 copy-start.17
  50.0 3.5 %copy-start.3 = (bf16[256,4096]{1,0:T(8,128)(2,1)S(1)}, bf16[256,4096]{1,0:T(8,128)(2,1)}, u32[]{:S(2)}) copy-start(bf16[256,4096]{1,0:T(8,128)(2,1)} %all-gather.3.cloned.1.call-done) | copy-start | bytes 6291460
  50.0 3.5 %copy-start.8 = (bf16[4096,256]{1,0:T(8,128)(2,1)S(1)}, bf16[4096,256]{1,0:T(8,128)(2,1)}, u32[]{:S(2)}) copy-start(bf16[4096,256]{1,0:T(8,128)(2,1)} %param.13) | copy-start | bytes 6291460
  50.0 3.5 %copy-start.24 = (f32[256]{0:T(256)S(1)}, f32[256]{0:T(256)}, u32[]{:S(2)}) copy-start(f32[256]{0:T(256)} %copy-done.23) | copy-start | bytes 3076
  50.1 0.7 copy-start.14
  68.9 3.4 %copy-start.12 = (bf16[256,1024]{0,1:T(8,128)(2,1)S(1)}, bf16[256,1024]{0,1:T(8,128)(2,1)}, u32[]{:S(2)}) copy-start(bf16[256,1024]{0,1:T(8,128)(2,1)} %copy.99) | copy-start | bytes 1572868
  68.9 3.4 %copy-start.18 = (pred[256,256]{0,1:T(8,128)(4,1)S(1)}, pred[256,256]{0,1:T(8,128)(4,1)}, u32[]{:S(2)}) copy-start(pred[256,256]{0,1:T(8,128)(4,1)} %fusion.31) | copy-start | bytes 196612
  68.9 3.4 %copy-start.27 = (bf16[256,256]{0,1:T(8,128)(2,1)S(1)}, bf16[256,256]{0,1:T(8,128)(2,1)}, u32[]{:S(2)}) copy-start(bf16[256,256]{0,1:T(8,128)(2,1)} %convolution_convert_fusion.4) | copy-start | bytes 393220
  68.9 3.4 %copy-start.28 = (f32[2,256,256,4]{2,1,3,0:T(8,128)S(1)}, f32[2,256,256,4]{2,1,3,0:T(8,128)}, u32[]{:S(2)}) copy-start(f32[2,256,256,4]{2,1,3,0:T(8,128)} %get-tuple-element.39) | copy-start | bytes 6291460
  68.9 3.4 %copy-start.30 = (f32[2,4,256]{2,1,0:T(4,128)S(1)}, f32[2,4,256]{2,1,0:T(4,128)}, u32[]{:S(2)}) copy-start(f32[2,4,256]{2,1,0:T(4,128)} %get-tuple-element.38) | copy-start | bytes 24580
  73.1 0.9 copy-start.15
  85.9 1.2 copy-start.7
  86.2 8.1 %collective-permute-start = (bf16[2,256,1024]{2,1,0:T(8,128)(2,1)S(1)}, bf16[2,256,1024]{2,1,0:T(8,128)(2,1)S(1)}, u32[]{:S(2)}, u32[]{:S(2)}) collective-permute-start(bf16[2,256,1024]{2,1,0:T(8,128)(2,1)S(1)} %pad_maximum_fusion), channel_id=1, source_target_pairs={{0,1},{1,0},{2,3},{3,2},{4,5},{5,4},{6,7},{7,6},{8,9},{9,8},{10,11... | collective-permute-start | bytes 3145736 | tf_op jit(solution)/shard_map/ppermute | solution.py:101
  93.5 1.6 %copy-start.29 = (f32[2,256,256,4]{2,1,3,0:T(8,128)S(1)}, f32[2,256,256,4]{2,1,3,0:T(8,128)}, u32[]{:S(2)}) copy-start(f32[2,256,256,4]{2,1,3,0:T(8,128)} %get-tuple-element.39) | copy-start | bytes 6291460
  94.3 1.2 copy-start.13
  94.3 1.2 copy-start.19
  94.3 1.2 copy-start.31
  94.5 1.8 %copy-start.9 = (bf16[4096,256]{1,0:T(8,128)(2,1)S(1)}, bf16[4096,256]{1,0:T(8,128)(2,1)}, u32[]{:S(2)}) copy-start(bf16[4096,256]{1,0:T(8,128)(2,1)} %param.13) | copy-start | bytes 6291460
  94.5 14.1 %collective-permute-start.1 = (bf16[1,256,1024]{2,1,0:T(8,128)(2,1)S(1)}, bf16[1,256,1024]{2,1,0:T(8,128)(2,1)S(1)}, u32[]{:S(2)}, u32[]{:S(2)}) collective-permute-start(bf16[1,256,1024]{2,1,0:T(8,128)(2,1)S(1)} %fusion.23), channel_id=1, source_target_pairs={{0,2},{1,3},{2,0},{3,1},{4,6},{5,7},{6,4},{7,5},{8,10},{9,11},{10,... | collective-permute-start | bytes 1572872 | tf_op jit(solution)/shard_map/ppermute | solution.py:101
  96.3 12.4 %copy-start.6 = (bf16[256,1024]{1,0:T(8,128)(2,1)S(1)}, bf16[256,1024]{1,0:T(8,128)(2,1)}, u32[]{:S(2)}) copy-start(bf16[256,1024]{1,0:T(8,128)(2,1)} %param.9) | copy-start | bytes 1572868
  97.1 12.1 %copy-start.1 = (f32[256,4096]{1,0:T(8,128)}, f32[256,4096]{1,0:T(8,128)S(1)}, u32[]{:S(2)}) copy-start(f32[256,4096]{1,0:T(8,128)S(1)} %convolution_add_fusion) | copy-start | bytes 12582916
  108.9 1.3 copy-start.26
  110.3 7.0 %collective-permute-start.9 = (bf16[2,256,1024]{2,1,0:T(8,128)(2,1)}, bf16[2,256,1024]{2,1,0:T(8,128)(2,1)}, u32[]{:S(2)}, u32[]{:S(2)}) collective-permute-start(bf16[2,256,1024]{2,1,0:T(8,128)(2,1)} %pad_maximum_fusion.1), channel_id=1, source_target_pairs={{0,1},{1,0},{2,3},{3,2},{4,5},{5,4},{6,7},{7,6},{8,9},{9,8},{10,11... | collective-permute-start | bytes 3145736 | tf_op jit(solution)/shard_map/ppermute | solution.py:103
  111.8 22.5 %all-to-all-start = ((bf16[8,32,1024]{2,1,0:T(8,128)(2,1)}), bf16[8,32,1024]{2,1,0:T(8,128)(2,1)}, u32[]{:S(2)}, u32[]{:S(2)}) async-start(bf16[8,32,1024]{2,1,0:T(8,128)(2,1)} %copy.112), calls=%async_computation | async-start | bytes 1048576 | tf_op jit(solution)/shard_map/all_to_all | solution.py:270
  117.3 3.1 %copy-start.4 = (bf16[256,4096]{1,0:T(8,128)(2,1)S(1)}, bf16[256,4096]{1,0:T(8,128)(2,1)}, u32[]{:S(2)}) copy-start(bf16[256,4096]{1,0:T(8,128)(2,1)} %all-gather.3.cloned.1.call-done) | copy-start | bytes 6291460
  119.8 14.5 %copy-start.5 = (bf16[8,32,1024]{2,1,0:T(8,128)(2,1)S(1)}, bf16[8,32,1024]{2,1,0:T(8,128)(2,1)}, u32[]{:S(2)}) copy-start(bf16[8,32,1024]{2,1,0:T(8,128)(2,1)} %copy.98) | copy-start | bytes 1572868
  119.8 14.5 %dynamic-slice-start = ((f32[4096]{0:T(1024)}, s32[]{:T(128)}), f32[1024]{0:T(1024)S(1)}, s32[]{:S(2)}) async-start(f32[4096]{0:T(1024)} %param.10, s32[]{:T(128)} %select_n.95), calls=%async_computation.3 | async-start | bytes 8704 | tf_op jit(solution)/shard_map/dynamic_slice | solution.py:137
  119.8 14.5 %copy-start.22 = (f32[256]{0:T(256)S(1)}, f32[256]{0:T(256)}, u32[]{:S(2)}) copy-start(f32[256]{0:T(256)} %get-tuple-element.36) | copy-start | bytes 3076
  119.8 14.5 %copy-start.25 = (f32[256]{0:T(256)S(1)}, f32[256]{0:T(256)}, u32[]{:S(2)}) copy-start(f32[256]{0:T(256)} %copy-done.23) | copy-start | bytes 3076
  119.8 14.5 %collective-permute-start.10 = (bf16[1,256,1024]{2,1,0:T(8,128)(2,1)}, bf16[1,256,1024]{2,1,0:T(8,128)(2,1)}, u32[]{:S(2)}, u32[]{:S(2)}) collective-permute-start(bf16[1,256,1024]{2,1,0:T(8,128)(2,1)} %fusion.24), channel_id=1, source_target_pairs={{0,2},{1,3},{2,0},{3,1},{4,6},{5,7},{6,4},{7,5},{8,10},{9,11},{10,... | collective-permute-start | bytes 1572872 | tf_op jit(solution)/shard_map/ppermute | solution.py:103
  123.2 1.2 collective-permute-start.11
  124.4 9.8 %collective-permute-start.12 = (f32[256]{0:T(256)S(1)}, f32[256]{0:T(256)S(1)}, u32[]{:S(2)}, u32[]{:S(2)}) collective-permute-start(f32[256]{0:T(256)S(1)} %add.200), channel_id=1, source_target_pairs={{0,2},{1,3},{2,0},{3,1},{4,6},{5,7},{6,4},{7,5},{8,10},{9,11},{10,... | collective-permute-start | bytes 3080 | tf_op jit(solution)/shard_map/ppermute | solution.py:103
Sparse Core Ops, SparseCore 0:
  9.6 25.2 all-gather.2
  37.0 22.6 all-gather.4

commit v10 on v9

--- a/solution.py
+++ b/solution.py
@@ -206,9 +206,10 @@
     ).astype(jnp.bfloat16)
     attended_flat = attended.reshape(token_row_count, query_width)
     mixed_partial = jnp.dot(attended_flat, w_out, preferred_element_type=jnp.float32)
+    grad_full = lax.all_gather(grad_home, "tensor", axis=1, tiled=True)
+    mixed_partial, grad_full = lax.optimization_barrier((mixed_partial, grad_full))
     mixed, _ = scatter_features(mixed_partial, "tensor", tensor_size, tensor_index)
     output_home = (x_float + mixed).astype(jnp.bfloat16)
-    grad_full = lax.all_gather(grad_home, "tensor", axis=1, tiled=True)
     attended_gradient = lax.dot_general(
         grad_full,
         w_out,

time: 147 us -> 141 us (0.959)
  matrix products: 39.8 us -> 34.4 us
  waiting for transfers between devices: 27.6 us -> 25.9 us
  local copies, waits for them, and re-layouts: 24.6 us -> 26.3 us
    all_gather x1, waiting for transfers between devices: 4.34 us -> 1.14 us  [per_device(): grad_full = lax.all_gather(grad_home, 'tensor', axis=1, tiled=True)]
    dot_general x1, matrix products: 3.38 us -> 0.66 us  [per_device(): jnp.einsum('kgqs,skd->qkgd', probs_low, value_rows, preferred_element_typ...]
    dot_general x1, matrix products: 2.72 us -> 0.85 us  [per_device(): jnp.einsum('qkgd,skd->kgqs', grouped_query, keys, preferred_element_type=...]
    unnamed x71 -> x73, local copies, waits for them, and re-layouts: 11.1 us -> 12.9 us
    dot_general x1, matrix products: 0.75 us -> 2.48 us  [per_device(): jnp.einsum('qkgd,skd->kgqs', grouped_gradient, value_rows, preferred_elem...]
    another operation x2, local copies, waits for them, and re-layouts: 0.33 us -> 1.95 us  [scatter_features(): outgoing = jnp.stack([held[i] for i in send]).astype(jnp.bfloat16)]
  transfers between devices with their start and end apart: 16 -> 16, of which waited for: 5 -> 5; matrix products, arithmetic and copies ran while one was open for 32% -> 33% of each run, Pallas kernels for 0% -> 0%
where the time goes in v10:
time: 141 us; the launch traced here: 140 us
  matrix products  34.4 us (24%)
  local copies, waits for them, and re-layouts  26.3 us (19%)
  waiting for transfers between devices  25.9 us (18%)
  starting transfers between devices  20.9 us (15%)
  other arithmetic  17.6 us (12%)
  between operations  14.8 us (10%)
    unnamed x73, local copies, waits for them, and re-layouts  12.9 us
    ppermute x7, starting transfers between devices, per_device(): returned.append(lax.ppermute(piece, 'dp', pairs))  12.5 us
    ppermute x2, waiting for transfers between devices, scatter_features(): incoming = lax.ppermute(outgoing, axis_name, _xor_pairs(size, bit))  11.6 us
    ppermute x4, waiting for transfers between devices, scatter_features(): lax.ppermute((outgoing, extra), axis_name, _xor_pairs(size, bit))  9.47 us
    dot_general x1, matrix products, per_device(): lax.dot_general(grad_full, w_out, (((1,), (1,)), ((), ())), preferred_ele...  7.4 us
    dot_general x1, matrix products, per_device(): jnp.dot(normed_input, w_query, preferred_element_type=jnp.float32)  6.52 us
    dot_general x1, matrix products, per_device(): lax.dot_general(grad_query.reshape(token_row_count, query_width), w_query...  5.76 us
    another operation x8, local copies, waits for them, and re-layouts, per_device(): returned = jnp.stack(returned)  5.59 us
  transfers between devices with their start and end apart: 16, of which 5 were waited for; matrix products, arithmetic and copies ran while one was open for 33% of the time, Pallas kernels for 0%

profile of v10, /device:TPU:0, one launch (start us, length us, event | category | flops | bytes accessed | tf_op | source)
XLA Modules:
  0.0 139.9 jit_solution(18293396534091298463)
XLA Ops:
  7.2 0.7 all-gather.3.cloned.1.call-update
  8.1 1.1 dynamic-slice_bitcast_fusion
  9.2 6.0 %collective-permute-start.6 = (bf16[32,1024]{1,0:T(8,128)(2,1)S(1)}, bf16[32,1024]{1,0:T(8,128)(2,1)S(1)}, u32[]{:S(2)}, u32[]{:S(2)}) collective-permute-start(bf16[32,1024]{1,0:T(8,128)(2,1)S(1)} %get-tuple-element.28), channel_id=1, source_target_pairs={{0,28},{4,0},{8,4},{12,8},{16,12},{20,16},{24,20},{28,24},{1,29},{... | collective-permute-start | bytes 196616 | tf_op jit(solution)/shard_map/ppermute | solution.py:154
  15.2 0.4 collective-permute-start.5
  15.7 3.0 %collective-permute-start.3 = (bf16[32,1024]{1,0:T(8,128)(2,1)S(1)}, bf16[32,1024]{1,0:T(8,128)(2,1)S(1)}, u32[]{:S(2)}, u32[]{:S(2)}) collective-permute-start(bf16[32,1024]{1,0:T(8,128)(2,1)S(1)} %get-tuple-element.31), channel_id=1, source_target_pairs={{0,16},{4,20},{8,24},{12,28},{16,0},{20,4},{24,8},{28,12},{1,17},{... | collective-permute-start | bytes 196616 | tf_op jit(solution)/shard_map/ppermute | solution.py:154
  18.7 0.8 reduce-window.8
  19.6 0.5 multiply_cosine_fusion
  20.2 0.7 fusion.31
  21.0 1.9 %collective-permute-start.1 = (bf16[32,1024]{1,0:T(8,128)(2,1)S(1)}, bf16[32,1024]{1,0:T(8,128)(2,1)S(1)}, u32[]{:S(2)}, u32[]{:S(2)}) collective-permute-start(bf16[32,1024]{1,0:T(8,128)(2,1)S(1)} %get-tuple-element.33), channel_id=1, source_target_pairs={{0,8},{4,12},{8,16},{12,20},{16,24},{20,28},{24,0},{28,4},{1,9},{5... | collective-permute-start | bytes 196616 | tf_op jit(solution)/shard_map/ppermute | solution.py:154
  22.9 1.1 collective-permute-start
  24.0 1.2 and_select_fusion
  25.7 2.9 %collective-permute-done.2 = bf16[32,1024]{1,0:T(8,128)(2,1)S(1)} collective-permute-done((bf16[32,1024]{1,0:T(8,128)(2,1)S(1)}, bf16[32,1024]{1,0:T(8,128)(2,1)S(1)}, u32[]{:S(2)}, u32[]{:S(2)}) %collective-permute-start.2) | collective-permute-done | bytes 65568 | tf_op jit(solution)/shard_map/ppermute | solution.py:154
  28.6 0.7 copy.93
  29.3 0.8 copy.92
  30.1 0.8 copy.91
  30.8 2.9 %stack.58 = bf16[8,32,1024]{2,0,1:T(8,128)(2,1)S(1)} concatenate(bf16[1,32,1024]{2,0,1:T(2,128)(2,1)S(1)} %copy.132, bf16[1,32,1024]{2,0,1:T(2,128)(2,1)} %copy.91, bf16[1,32,1024]{2,0,1:T(2,128)(2,1)} %copy.92, bf16[1,32,1024]{2,0,1:T(2,128)(2,1)} %copy.93, bf16[1,32,1024]{2,0,1:T(2,128)(2,1)S(1)} %copy.94, bf16[1,32,1024]{2,0,1:T(2,128)(2,1)S(1)} %copy.95, ...), dimensions={0} | concatenate | bytes 1048576 | tf_op jit(solution)/shard_map/stack | solution.py:155
  33.8 0.4 convolution_convert_fusion.3
  34.1 1.1 copy.98
  35.3 2.2 %fusion = f32[256]{0:T(256)S(1)} fusion(bf16[256,4096]{1,0:T(8,128)(2,1)} %all-gather.3.cloned.1.call-done), kind=kLoop, calls=%fused_computation.5 | loop fusion | flops 3145472 | bytes 2098176 | tf_op jit(solution)/shard_map/reduce_sum | solution.py:178
  37.5 0.5 multiply_multiply_fusion
  38.1 1.2 fusion.47
  39.5 6.5 %convolution_bitcast_fusion = f32[32,8,8,128]{3,1,2,0:T(8,128)S(1)} fusion(bf16[4096,1024]{1,0:T(8,128)(2,1)} %param.11, bf16[256,4096]{1,0:T(8,128)(2,1)} %all-gather.3.cloned.1.call-done, f32[4096]{0:T(1024)S(1)} %copy-done.21, f32[256]{0:T(256)S(1)} %get-tuple-element.41), kind=kOutput, calls=%fused_computation.16 | convolution fusion | flops 2151677952 | bytes 11551744 | tf_op jit(solution)/shard_map/dot_general | solution.py:180
  46.3 0.5 subtract_convert_fusion.1
  47.1 0.6 copy-done.11
  47.8 0.9 fusion.7
  48.9 0.6 copy-done.15
  49.5 1.2 convolution_convert_fusion.4
  50.9 0.7 convolution_convert_fusion.1
  51.6 0.9 slice-done
  52.5 1.4 %slice-done.1 = s8[4194304]{0:T(1024)(128)(4,1)S(1)} async-done(((s8[8388608]{0:T(1024)(128)(4,1)}), s8[4194304]{0:T(1024)(128)(4,1)S(1)}, s32[]{:S(2)}) %slice-start.1) | async-done | bytes 4194328
  54.0 4.5 %fusion.55 = f32[256,4096]{1,0:T(8,128)} fusion(bf16[256,1024]{0,1:T(8,128)(2,1)S(1)} %bitcast.175, bf16[1024,4096]{1,0:T(8,128)(2,1)S(1)} %bitcast.171), kind=kOutput, calls=%fused_computation.118 | convolution fusion | flops 2147483648 | bytes 13107200 | tf_op jit(solution)/shard_map/dot_general | solution.py:208
  58.5 1.1 all-gather.5.cloned.1.call-done
  59.7 7.4 %convolution_convert_fusion = bf16[256,1024]{1,0:T(8,128)(2,1)} fusion(bf16[256,4096]{1,0:T(8,128)(2,1)} %all-gather.5.cloned.1.call-done, bf16[1024,4096]{1,0:T(8,128)(2,1)} %param.14), kind=kOutput, calls=%fused_computation.19 | convolution fusion | flops 2147745792 | bytes 11010048 | tf_op jit(solution)/shard_map/dot_general | solution.py:213
  67.1 1.2 copy.99
  68.5 2.5 %fusion.5 = bf16[2,4,256,256]{2,3,1,0:T(8,128)(2,1)S(1)} fusion(bf16[256,2,128,1]{0,2,3,1:T(8,128)(2,1)} %bitcast.199, bf16[256,2,4,128]{0,3,2,1:T(8,128)(2,1)S(1)} %bitcast.176, f32[2,4,256]{2,1,0:T(4,128)S(1)} %bitcast.195, f32[2,4,256]{2,1,0:T(4,128)} %copy-done.29, f32[2,256,256,4]{2,1,3,0:T(8,128)} %copy-done.27, pred[256,256]{0,1:T(8,128)(4,1)} %fusion.31), kind=kOutput, calls=%fused_computation.11 | convolution fusion | flops 137363456 | bytes 3883008 | tf_op jit(solution)/shard_map/qkgd,skd->kgqs/dot_general | solution.py:223
  71.0 0.5 fusion.9
  71.6 0.4 copy-done.18
  71.9 0.4 convolution_multiply_fusion
  72.4 1.1 fusion.53
  73.8 1.5 %copy.134 = f32[256,8,64]{2,1,0:T(8,128)S(1)} copy(f32[256,8,64]{0,2,1:T(8,128)} %get-tuple-element.22) | data formatting | bytes 1048576
  75.3 2.4 %copy.133 = f32[256,8,64]{2,1,0:T(8,128)} copy(f32[256,8,64]{0,2,1:T(8,128)} %get-tuple-element.23) | data formatting | bytes 1048576
  77.6 1.8 %fusion.19 = (bf16[1,256,1024]{2,1,0:T(8,128)(2,1)S(1)}, bf16[1,256,1024]{2,1,0:T(8,128)(2,1)S(1)}) fusion(f32[256,4096]{1,0:T(8,128)} %fusion.55, s32[]{:T(128)S(6)} %select_n.111, s32[]{:T(128)S(6)} %select_n.112), kind=kLoop, calls=%fused_computation.54 | loop fusion | bytes 2097160 | tf_op jit(solution)/shard_map/stack | solution.py:99
  79.8 0.3 add_convert_fusion
  80.5 5.8 %fusion.25 = f32[256,4096]{1,0:T(8,128)S(1)} fusion(bf16[4096,1024]{1,0:T(8,128)(2,1)} %param.11, bf16[32,8,8,128]{3,2,1,0:T(8,128)(2,1)S(1)} %bitcast.183), kind=kOutput, calls=%fused_computation.60 | convolution fusion | flops 2147483648 | bytes 13107200 | tf_op jit(solution)/shard_map/dot_general | solution.py:246
  86.2 0.8 convolution_add_fusion.1
  87.1 1.4 copy-done.2
  88.6 0.4 collective-permute-start.8
  89.3 0.7 fusion.10
  90.0 0.3 copy-done.16
  90.3 0.8 convolution_add_fusion
  91.1 11.6 %collective-permute-done.8 = bf16[1,256,1024]{2,1,0:T(8,128)(2,1)S(1)} collective-permute-done((bf16[1,256,1024]{2,1,0:T(8,128)(2,1)S(1)}, bf16[1,256,1024]{2,1,0:T(8,128)(2,1)S(1)}, u32[]{:S(2)}, u32[]{:S(2)}) %collective-permute-start.8) | collective-permute-done | bytes 524320 | tf_op jit(solution)/shard_map/ppermute | solution.py:101
  102.8 0.3 fusion.11
  103.3 1.1 pad_maximum_fusion.1
  104.4 0.4 convolution_convert_fusion.2
  104.8 1.1 copy.112
  105.9 5.5 %all-to-all-start = ((bf16[8,32,1024]{2,1,0:T(8,128)(2,1)}), bf16[8,32,1024]{2,1,0:T(8,128)(2,1)}, u32[]{:S(2)}, u32[]{:S(2)}) async-start(bf16[8,32,1024]{2,1,0:T(8,128)(2,1)} %copy.112), calls=%async_computation | async-start | bytes 1048576 | tf_op jit(solution)/shard_map/all_to_all | solution.py:271
  111.4 2.5 %fusion.24 = bf16[1,256,1024]{2,1,0:T(8,128)(2,1)} fusion(f32[256,4096]{1,0:T(8,128)} %copy-done.1, s32[]{:T(128)S(6)} %select_n.113, bf16[2,256,1024]{2,1,0:T(8,128)(2,1)} %collective-permute-done.9), kind=kLoop, calls=%fused_computation.59 | loop fusion | flops 786432 | bytes 2097156 | tf_op jit(solution)/shard_map/convert_element_type | solution.py:99
  114.0 0.6 collective-permute-start.10
  114.6 2.8 %fusion.3 = f32[256]{0:T(256)S(1)} fusion(bf16[256,4096]{1,0:T(8,128)(2,1)S(1)} %copy-done.5, f32[256,4096]{1,0:T(8,128)} %copy-done.1, f32[4096]{0:T(1024)S(1)} %copy-done.21), kind=kLoop, calls=%fused_computation.8 | loop fusion | flops 4194048 | bytes 6308864 | tf_op jit(solution)/shard_map/reduce_sum | solution.py:266
  117.5 1.1 collective-permute-done.11
  118.6 1.5 %collective-permute-start.12 = (f32[256]{0:T(256)S(1)}, f32[256]{0:T(256)S(1)}, u32[]{:S(2)}, u32[]{:S(2)}) collective-permute-start(f32[256]{0:T(256)S(1)} %add.200), channel_id=1, source_target_pairs={{0,2},{1,3},{2,0},{3,1},{4,6},{5,7},{6,4},{7,5},{8,10},{9,11},{10,... | collective-permute-start | bytes 3080 | tf_op jit(solution)/shard_map/ppermute | solution.py:103
  120.1 8.3 %collective-permute-done.12 = f32[256]{0:T(256)S(1)} collective-permute-done((f32[256]{0:T(256)S(1)}, f32[256]{0:T(256)S(1)}, u32[]{:S(2)}, u32[]{:S(2)}) %collective-permute-start.12) | collective-permute-done | bytes 1056 | tf_op jit(solution)/shard_map/ppermute | solution.py:103
  128.5 2.8 %fusion.14 = bf16[256,1024]{1,0:T(8,128)(2,1)} fusion(bf16[256,1024]{1,0:T(8,128)(2,1)S(1)} %copy-done.7, f32[256,4096]{1,0:T(8,128)} %copy-done.1, s32[]{:T(128)} %select_n.110, bf16[2,256,1024]{2,1,0:T(8,128)(2,1)} %collective-permute-done.9, bf16[1,256,1024]{2,1,0:T(8,128)(2,1)} %collective-permute-done.10, f32[256]{0:T(256)S(1)} %add_multiply_fusion, ...), kind=kLoop, calls=%fused_computation.32 | loop fusion | flops 3407872 | bytes 3677188 | tf_op jit(solution)/shard_map/convert_element_type | solution.py:285
  131.2 1.9 %copy.144 = bf16[256,1024]{1,0:T(8,128)(2,1)} copy(bf16[256,1024]{1,0:T(8,128)(2,1)} %bitcast.54) | data formatting | bytes 1048576
  (106 shorter events, 4.1 us)
Async XLA Ops:
  7.2 30.9 %copy-start = (bf16[4096,256]{1,0:T(8,128)(2,1)S(1)}, bf16[4096,256]{1,0:T(8,128)(2,1)}, u32[]{:S(2)}) copy-start(bf16[4096,256]{1,0:T(8,128)(2,1)} %param.12) | copy-start | bytes 6291460
  7.2 28.1 %all-gather.3.cloned.1.call-start = ((), (), s32[]{:S(2)}) async-start(), calls=%async_computation.1 | async-start | bytes 2621440 | tf_op jit(solution)/shard_map/all_gather | solution.py:176
  7.9 51.7 %all-gather.5.cloned.1.call-start = ((), (), s32[]{:S(2)}) async-start(), calls=%async_computation.2 | async-start | bytes 2621440 | tf_op jit(solution)/shard_map/all_gather | solution.py:209
  9.2 11.8 %collective-permute-start.6 = (bf16[32,1024]{1,0:T(8,128)(2,1)S(1)}, bf16[32,1024]{1,0:T(8,128)(2,1)S(1)}, u32[]{:S(2)}, u32[]{:S(2)}) collective-permute-start(bf16[32,1024]{1,0:T(8,128)(2,1)S(1)} %get-tuple-element.28), channel_id=1, source_target_pairs={{0,28},{4,0},{8,4},{12,8},{16,12},{20,16},{24,20},{28,24},{1,29},{... | collective-permute-start | bytes 196616 | tf_op jit(solution)/shard_map/ppermute | solution.py:154
  15.2 7.7 %collective-permute-start.5 = (bf16[32,1024]{1,0:T(8,128)(2,1)S(1)}, bf16[32,1024]{1,0:T(8,128)(2,1)S(1)}, u32[]{:S(2)}, u32[]{:S(2)}) collective-permute-start(bf16[32,1024]{1,0:T(8,128)(2,1)S(1)} %get-tuple-element.29), channel_id=1, source_target_pairs={{0,24},{4,28},{8,0},{12,4},{16,8},{20,12},{24,16},{28,20},{1,25},{... | collective-permute-start | bytes 196616 | tf_op jit(solution)/shard_map/ppermute | solution.py:154
  15.7 9.8 %collective-permute-start.4 = (bf16[32,1024]{1,0:T(8,128)(2,1)S(1)}, bf16[32,1024]{1,0:T(8,128)(2,1)S(1)}, u32[]{:S(2)}, u32[]{:S(2)}) collective-permute-start(bf16[32,1024]{1,0:T(8,128)(2,1)S(1)} %get-tuple-element.30), channel_id=1, source_target_pairs={{0,20},{4,24},{8,28},{12,0},{16,4},{20,8},{24,12},{28,16},{1,21},{... | collective-permute-start | bytes 196616 | tf_op jit(solution)/shard_map/ppermute | solution.py:154
  15.7 9.9 %collective-permute-start.3 = (bf16[32,1024]{1,0:T(8,128)(2,1)S(1)}, bf16[32,1024]{1,0:T(8,128)(2,1)S(1)}, u32[]{:S(2)}, u32[]{:S(2)}) collective-permute-start(bf16[32,1024]{1,0:T(8,128)(2,1)S(1)} %get-tuple-element.31), channel_id=1, source_target_pairs={{0,16},{4,20},{8,24},{12,28},{16,0},{20,4},{24,8},{28,12},{1,17},{... | collective-permute-start | bytes 196616 | tf_op jit(solution)/shard_map/ppermute | solution.py:154
  18.7 9.9 %collective-permute-start.2 = (bf16[32,1024]{1,0:T(8,128)(2,1)S(1)}, bf16[32,1024]{1,0:T(8,128)(2,1)S(1)}, u32[]{:S(2)}, u32[]{:S(2)}) collective-permute-start(bf16[32,1024]{1,0:T(8,128)(2,1)S(1)} %get-tuple-element.32), channel_id=1, source_target_pairs={{0,12},{4,16},{8,20},{12,24},{16,28},{20,0},{24,4},{28,8},{1,13},{... | collective-permute-start | bytes 196616 | tf_op jit(solution)/shard_map/ppermute | solution.py:154
  21.0 8.3 %collective-permute-start.1 = (bf16[32,1024]{1,0:T(8,128)(2,1)S(1)}, bf16[32,1024]{1,0:T(8,128)(2,1)S(1)}, u32[]{:S(2)}, u32[]{:S(2)}) collective-permute-start(bf16[32,1024]{1,0:T(8,128)(2,1)S(1)} %get-tuple-element.33), channel_id=1, source_target_pairs={{0,8},{4,12},{8,16},{12,20},{16,24},{20,28},{24,0},{28,4},{1,9},{5... | collective-permute-start | bytes 196616 | tf_op jit(solution)/shard_map/ppermute | solution.py:154
  22.9 7.2 %collective-permute-start = (bf16[32,1024]{1,0:T(8,128)(2,1)S(1)}, bf16[32,1024]{1,0:T(8,128)(2,1)S(1)}, u32[]{:S(2)}, u32[]{:S(2)}) collective-permute-start(bf16[32,1024]{1,0:T(8,128)(2,1)S(1)} %get-tuple-element.34), channel_id=1, source_target_pairs={{0,4},{4,8},{8,12},{12,16},{16,20},{20,24},{24,28},{28,0},{1,5},{5... | collective-permute-start | bytes 196616 | tf_op jit(solution)/shard_map/ppermute | solution.py:154
  34.1 3.9 %copy-start.21 = (f32[4096]{0:T(1024)S(1)}, f32[4096]{0:T(1024)}, u32[]{:S(2)}) copy-start(f32[4096]{0:T(1024)} %param.10) | copy-start | bytes 49156
  35.3 2.8 %copy-start.3 = (bf16[256,4096]{1,0:T(8,128)(2,1)S(1)}, bf16[256,4096]{1,0:T(8,128)(2,1)}, u32[]{:S(2)}) copy-start(bf16[256,4096]{1,0:T(8,128)(2,1)} %all-gather.3.cloned.1.call-done) | copy-start | bytes 6291460
  38.1 10.6 %copy-start.23 = (f32[256]{0:T(256)}, f32[256]{0:T(256)S(1)}, u32[]{:S(2)}) copy-start(f32[256]{0:T(256)S(1)} %get-tuple-element.41) | copy-start | bytes 3076
  46.8 1.0 copy-start.19
  46.9 0.8 copy-start.11
  47.0 0.9 copy-start.13
  47.0 1.9 %copy-start.4 = (bf16[256,4096]{1,0:T(8,128)(2,1)S(1)}, bf16[256,4096]{1,0:T(8,128)(2,1)}, u32[]{:S(2)}) copy-start(bf16[256,4096]{1,0:T(8,128)(2,1)} %all-gather.3.cloned.1.call-done) | copy-start | bytes 6291460
  47.0 2.6 %copy-start.15 = (bf16[4096,256]{1,0:T(8,128)(2,1)S(1)}, bf16[4096,256]{1,0:T(8,128)(2,1)}, u32[]{:S(2)}) copy-start(bf16[4096,256]{1,0:T(8,128)(2,1)} %param.13) | copy-start | bytes 6291460
  47.1 3.7 %copy-start.17 = (bf16[256,2,64]{2,0,1:T(8,128)(2,1)}, bf16[256,2,64]{2,0,1:T(8,128)(2,1)S(1)}, u32[]{:S(2)}) copy-start(bf16[256,2,64]{2,0,1:T(8,128)(2,1)S(1)} %get-tuple-element.25) | copy-start | bytes 196612
  49.5 1.4 copy-start.27
  49.5 1.4 copy-start.29
  49.5 3.0 %slice-start = ((s8[8388608]{0:T(1024)(128)(4,1)}), s8[4194304]{0:T(1024)(128)(4,1)S(1)}, s32[]{:S(2)}) async-start(s8[8388608]{0:T(1024)(128)(4,1)} %bitcast.170), calls=%async_computation.3 | async-start | bytes 8388608
  50.8 0.8 copy-start.26
  50.9 3.1 %slice-start.1 = ((s8[8388608]{0:T(1024)(128)(4,1)}), s8[4194304]{0:T(1024)(128)(4,1)S(1)}, s32[]{:S(2)}) async-start(s8[8388608]{0:T(1024)(128)(4,1)} %bitcast.170), calls=%async_computation.4 | async-start | bytes 8388608
  68.3 2.7 %copy-start.9 = (bf16[256,1024]{0,1:T(8,128)(2,1)}, bf16[256,1024]{0,1:T(8,128)(2,1)S(1)}, u32[]{:S(2)}) copy-start(bf16[256,1024]{0,1:T(8,128)(2,1)S(1)} %copy.99) | copy-start | bytes 1572868
  68.5 2.5 %copy-start.12 = (bf16[256,8,64]{2,0,1:T(8,128)(2,1)S(1)}, bf16[256,8,64]{2,0,1:T(8,128)(2,1)}, u32[]{:S(2)}) copy-start(bf16[256,8,64]{2,0,1:T(8,128)(2,1)} %copy-done.11) | copy-start | bytes 786436
  68.5 2.5 %copy-start.14 = (bf16[256,8,64]{2,0,1:T(8,128)(2,1)S(1)}, bf16[256,8,64]{2,0,1:T(8,128)(2,1)}, u32[]{:S(2)}) copy-start(bf16[256,8,64]{2,0,1:T(8,128)(2,1)} %copy-done.13) | copy-start | bytes 786436
  71.0 0.9 copy-start.18
  77.6 2.2 %copy-start.8 = (f32[256,8,64]{2,1,0:T(8,128)S(1)}, f32[256,8,64]{2,1,0:T(8,128)}, u32[]{:S(2)}) copy-start(f32[256,8,64]{2,1,0:T(8,128)} %copy.133) | copy-start | bytes 1572868
  79.5 7.5 %collective-permute-start.7 = (bf16[2,256,1024]{2,1,0:T(8,128)(2,1)S(1)}, bf16[2,256,1024]{2,1,0:T(8,128)(2,1)S(1)}, u32[]{:S(2)}, u32[]{:S(2)}) collective-permute-start(bf16[2,256,1024]{2,1,0:T(8,128)(2,1)S(1)} %pad_maximum_fusion), channel_id=1, source_target_pairs={{0,1},{1,0},{2,3},{3,2},{4,5},{5,4},{6,7},{7,6},{8,9},{9,8},{10,11... | collective-permute-start | bytes 3145736 | tf_op jit(solution)/shard_map/ppermute | solution.py:101
  86.2 2.2 %copy-start.2 = (f32[256,4096]{1,0:T(8,128)S(1)}, f32[256,4096]{1,0:T(8,128)}, u32[]{:S(2)}) copy-start(f32[256,4096]{1,0:T(8,128)} %fusion.55) | copy-start | bytes 12582916
  86.2 2.9 %copy-start.28 = (f32[2,256,256,4]{2,1,3,0:T(8,128)S(1)}, f32[2,256,256,4]{2,1,3,0:T(8,128)}, u32[]{:S(2)}) copy-start(f32[2,256,256,4]{2,1,3,0:T(8,128)} %copy-done.27) | copy-start | bytes 6291460
  87.0 2.3 %copy-start.10 = (bf16[256,1024]{0,1:T(8,128)(2,1)S(1)}, bf16[256,1024]{0,1:T(8,128)(2,1)}, u32[]{:S(2)}) copy-start(bf16[256,1024]{0,1:T(8,128)(2,1)} %copy-done.9) | copy-start | bytes 1572868
  87.0 2.3 %copy-start.20 = (pred[256,256]{0,1:T(8,128)(4,1)S(1)}, pred[256,256]{0,1:T(8,128)(4,1)}, u32[]{:S(2)}) copy-start(pred[256,256]{0,1:T(8,128)(4,1)} %fusion.31) | copy-start | bytes 196612
  87.0 2.3 %copy-start.30 = (f32[2,4,256]{2,1,0:T(4,128)S(1)}, f32[2,4,256]{2,1,0:T(4,128)}, u32[]{:S(2)}) copy-start(f32[2,4,256]{2,1,0:T(4,128)} %copy-done.29) | copy-start | bytes 24580
  88.6 1.8 %copy-start.16 = (bf16[4096,256]{1,0:T(8,128)(2,1)S(1)}, bf16[4096,256]{1,0:T(8,128)(2,1)}, u32[]{:S(2)}) copy-start(bf16[4096,256]{1,0:T(8,128)(2,1)} %param.13) | copy-start | bytes 6291460
  88.6 14.2 %collective-permute-start.8 = (bf16[1,256,1024]{2,1,0:T(8,128)(2,1)S(1)}, bf16[1,256,1024]{2,1,0:T(8,128)(2,1)S(1)}, u32[]{:S(2)}, u32[]{:S(2)}) collective-permute-start(bf16[1,256,1024]{2,1,0:T(8,128)(2,1)S(1)} %fusion.23), channel_id=1, source_target_pairs={{0,2},{1,3},{2,0},{3,1},{4,6},{5,7},{6,4},{7,5},{8,10},{9,11},{10,... | collective-permute-start | bytes 1572872 | tf_op jit(solution)/shard_map/ppermute | solution.py:101
  90.3 12.4 %copy-start.7 = (bf16[256,1024]{1,0:T(8,128)(2,1)S(1)}, bf16[256,1024]{1,0:T(8,128)(2,1)}, u32[]{:S(2)}) copy-start(bf16[256,1024]{1,0:T(8,128)(2,1)} %param.9) | copy-start | bytes 1572868
  91.1 12.2 %copy-start.1 = (f32[256,4096]{1,0:T(8,128)}, f32[256,4096]{1,0:T(8,128)S(1)}, u32[]{:S(2)}) copy-start(f32[256,4096]{1,0:T(8,128)S(1)} %convolution_add_fusion) | copy-start | bytes 12582916
  103.1 1.3 copy-start.25
  104.4 7.0 %collective-permute-start.9 = (bf16[2,256,1024]{2,1,0:T(8,128)(2,1)}, bf16[2,256,1024]{2,1,0:T(8,128)(2,1)}, u32[]{:S(2)}, u32[]{:S(2)}) collective-permute-start(bf16[2,256,1024]{2,1,0:T(8,128)(2,1)} %pad_maximum_fusion.1), channel_id=1, source_target_pairs={{0,1},{1,0},{2,3},{3,2},{4,5},{5,4},{6,7},{7,6},{8,9},{9,8},{10,11... | collective-permute-start | bytes 3145736 | tf_op jit(solution)/shard_map/ppermute | solution.py:103
  105.9 22.5 %all-to-all-start = ((bf16[8,32,1024]{2,1,0:T(8,128)(2,1)}), bf16[8,32,1024]{2,1,0:T(8,128)(2,1)}, u32[]{:S(2)}, u32[]{:S(2)}) async-start(bf16[8,32,1024]{2,1,0:T(8,128)(2,1)} %copy.112), calls=%async_computation | async-start | bytes 1048576 | tf_op jit(solution)/shard_map/all_to_all | solution.py:271
  111.4 3.1 %copy-start.5 = (bf16[256,4096]{1,0:T(8,128)(2,1)S(1)}, bf16[256,4096]{1,0:T(8,128)(2,1)}, u32[]{:S(2)}) copy-start(bf16[256,4096]{1,0:T(8,128)(2,1)} %all-gather.3.cloned.1.call-done) | copy-start | bytes 6291460
  113.9 14.5 %copy-start.6 = (bf16[8,32,1024]{2,1,0:T(8,128)(2,1)S(1)}, bf16[8,32,1024]{2,1,0:T(8,128)(2,1)}, u32[]{:S(2)}) copy-start(bf16[8,32,1024]{2,1,0:T(8,128)(2,1)} %copy.98) | copy-start | bytes 1572868
  113.9 14.5 %dynamic-slice-start = ((f32[4096]{0:T(1024)}, s32[]{:T(128)}), f32[1024]{0:T(1024)S(1)}, s32[]{:S(2)}) async-start(f32[4096]{0:T(1024)} %param.10, s32[]{:T(128)} %select_n.110), calls=%async_computation.5 | async-start | bytes 8704 | tf_op jit(solution)/shard_map/dynamic_slice | solution.py:137
  113.9 14.5 %copy-start.22 = (f32[256]{0:T(256)S(1)}, f32[256]{0:T(256)}, u32[]{:S(2)}) copy-start(f32[256]{0:T(256)} %get-tuple-element.40) | copy-start | bytes 3076
  113.9 14.5 %copy-start.24 = (f32[256]{0:T(256)S(1)}, f32[256]{0:T(256)}, u32[]{:S(2)}) copy-start(f32[256]{0:T(256)} %copy-done.23) | copy-start | bytes 3076
  114.0 14.5 %collective-permute-start.10 = (bf16[1,256,1024]{2,1,0:T(8,128)(2,1)}, bf16[1,256,1024]{2,1,0:T(8,128)(2,1)}, u32[]{:S(2)}, u32[]{:S(2)}) collective-permute-start(bf16[1,256,1024]{2,1,0:T(8,128)(2,1)} %fusion.24), channel_id=1, source_target_pairs={{0,2},{1,3},{2,0},{3,1},{4,6},{5,7},{6,4},{7,5},{8,10},{9,11},{10,... | collective-permute-start | bytes 1572872 | tf_op jit(solution)/shard_map/ppermute | solution.py:103
  117.4 1.2 collective-permute-start.11
  118.6 9.8 %collective-permute-start.12 = (f32[256]{0:T(256)S(1)}, f32[256]{0:T(256)S(1)}, u32[]{:S(2)}, u32[]{:S(2)}) collective-permute-start(f32[256]{0:T(256)S(1)} %add.200), channel_id=1, source_target_pairs={{0,2},{1,3},{2,0},{3,1},{4,6},{5,7},{6,4},{7,5},{8,10},{9,11},{10,... | collective-permute-start | bytes 3080 | tf_op jit(solution)/shard_map/ppermute | solution.py:103
Sparse Core Ops, SparseCore 0:
  9.6 25.2 all-gather.2
  37.0 22.5 all-gather.4

commit v11 on v10

--- a/solution.py
+++ b/solution.py
@@ -78,7 +78,7 @@
     return jnp.concatenate(blocks, axis=1)
 
 
-def scatter_features(partial, axis_name, size, position, extra=None):
+def scatter_features(partial, axis_name, size, position, extra=None, ties=()):
     width = partial.shape[1] // size
     if not _is_pow2(size):
         summed = lax.psum_scatter(
@@ -86,12 +86,13 @@
         )
         if extra is not None:
             extra = lax.psum(extra, axis_name)
-        return summed.astype(jnp.float32), extra
+        return summed.astype(jnp.float32), extra, ties
     held = [
         lax.dynamic_slice_in_dim(partial, (position ^ m) * width, width, axis=1)
         for m in range(size)
     ]
     masks = list(range(size))
+    done_ties = []
     bit = 1
     while bit < size:
         keep = [i for i, m in enumerate(masks) if not m & bit]
@@ -102,13 +103,17 @@
         else:
             incoming, extra_in = lax.ppermute((outgoing, extra), axis_name, _xor_pairs(size, bit))
             extra = extra + extra_in
+        if ties:
+            incoming, first = lax.optimization_barrier((incoming, ties[0]))
+            ties = ties[1:]
+            done_ties.append(first)
         sent_masks = [masks[i] ^ bit for i in send]
         held = [
             held[i] + incoming[sent_masks.index(masks[i])].astype(jnp.float32) for i in keep
         ]
         masks = [masks[i] for i in keep]
         bit <<= 1
-    return held[0], extra
+    return held[0], extra, tuple(done_ties) + tuple(ties)
 
 
 def per_device(
@@ -208,14 +213,16 @@
     mixed_partial = jnp.dot(attended_flat, w_out, preferred_element_type=jnp.float32)
     grad_full = lax.all_gather(grad_home, "tensor", axis=1, tiled=True)
     mixed_partial, grad_full = lax.optimization_barrier((mixed_partial, grad_full))
-    mixed, _ = scatter_features(mixed_partial, "tensor", tensor_size, tensor_index)
-    output_home = (x_float + mixed).astype(jnp.bfloat16)
     attended_gradient = lax.dot_general(
         grad_full,
         w_out,
         (((1,), (1,)), ((), ())),
         preferred_element_type=jnp.float32,
     ).astype(jnp.bfloat16)
+    mixed, _, (attended_gradient,) = scatter_features(
+        mixed_partial, "tensor", tensor_size, tensor_index, ties=(attended_gradient,)
+    )
+    output_home = (x_float + mixed).astype(jnp.bfloat16)
     grouped_gradient = attended_gradient.reshape(
         token_row_count, kv_local, query_group_width, HEAD_SIZE
     )
@@ -272,7 +279,7 @@
         token_row_count, width_part
     )
 
-    normed_gradient, stat_sum = scatter_features(
+    normed_gradient, stat_sum, _ = scatter_features(
         normed_partial, "tensor", tensor_size, tensor_index, extra=stat_partial
     )
     stat = stat_sum / full_width

time: 141 us -> 137 us (0.972)
  waiting for transfers between devices: 25.9 us -> 14.1 us
  other arithmetic: 17.6 us -> 24.8 us
    ppermute x2, waiting for transfers between devices: 11.6 us -> 0.01 us  [scatter_features(): incoming = lax.ppermute(outgoing, axis_name, _xor_pairs(size, bit))]
    convert_element_type x1, other arithmetic: 0.34 us -> 3.06 us  [per_device(): output_home = (x_float + mixed).astype(jnp.bfloat16)]
    convert_element_type x2, other arithmetic: 2.66 us -> 4.79 us  [scatter_features(): outgoing = jnp.stack([held[i] for i in send]).astype(jnp.bfloat16)]
    unnamed x73 -> x69, local copies, waits for them, and re-layouts: 12.9 us -> 13 us
  transfers between devices with their start and end apart: 16 -> 16, of which waited for: 5 -> 4; matrix products, arithmetic and copies ran while one was open for 33% -> 42% of each run, Pallas kernels for 0% -> 0%
where the time goes in v11:
time: 137 us; the launch traced here: 135 us
  matrix products  34.5 us (25%)
  local copies, waits for them, and re-layouts  26.4 us (19%)
  other arithmetic  24.8 us (18%)
  starting transfers between devices  21 us (15%)
  between operations  14.8 us (11%)
  waiting for transfers between devices  14.1 us (10%)
    unnamed x69, local copies, waits for them, and re-layouts  13 us
    ppermute x7, starting transfers between devices, per_device(): returned.append(lax.ppermute(piece, 'dp', pairs))  12.5 us
    ppermute x4, waiting for transfers between devices, scatter_features(): lax.ppermute((outgoing, extra), axis_name, _xor_pairs(size, bit))  9.47 us
    dot_general x1, matrix products, per_device(): lax.dot_general(grad_full, w_out, (((1,), (1,)), ((), ())), preferred_ele...  7.41 us
    dot_general x1, matrix products, per_device(): jnp.dot(normed_input, w_query, preferred_element_type=jnp.float32)  6.54 us
    dot_general x1, matrix products, per_device(): lax.dot_general(grad_query.reshape(token_row_count, query_width), w_query...  5.76 us
    all_to_all x1, starting transfers between devices, per_device(): lax.all_to_all(outgoing, 'dp', split_axis=0, concat_axis=0, tiled=True)  5.67 us
    another operation x8, local copies, waits for them, and re-layouts, per_device(): returned = jnp.stack(returned)  5.59 us
  transfers between devices with their start and end apart: 16, of which 4 were waited for; matrix products, arithmetic and copies ran while one was open for 42% of the time, Pallas kernels for 0%

profile of v11, /device:TPU:0, one launch (start us, length us, event | category | flops | bytes accessed | tf_op | source)
XLA Modules:
  0.0 135.5 jit_solution(18284474825684612165)
XLA Ops:
  7.2 0.7 all-gather.3.cloned.1.call-update
  8.1 1.1 dynamic-slice_bitcast_fusion
  9.2 6.0 %collective-permute-start.6 = (bf16[32,1024]{1,0:T(8,128)(2,1)S(1)}, bf16[32,1024]{1,0:T(8,128)(2,1)S(1)}, u32[]{:S(2)}, u32[]{:S(2)}) collective-permute-start(bf16[32,1024]{1,0:T(8,128)(2,1)S(1)} %get-tuple-element.32), channel_id=1, source_target_pairs={{0,28},{4,0},{8,4},{12,8},{16,12},{20,16},{24,20},{28,24},{1,29},{... | collective-permute-start | bytes 196616 | tf_op jit(solution)/shard_map/ppermute | solution.py:159
  15.2 0.4 collective-permute-start.5
  15.7 3.0 %collective-permute-start.3 = (bf16[32,1024]{1,0:T(8,128)(2,1)S(1)}, bf16[32,1024]{1,0:T(8,128)(2,1)S(1)}, u32[]{:S(2)}, u32[]{:S(2)}) collective-permute-start(bf16[32,1024]{1,0:T(8,128)(2,1)S(1)} %get-tuple-element.35), channel_id=1, source_target_pairs={{0,16},{4,20},{8,24},{12,28},{16,0},{20,4},{24,8},{28,12},{1,17},{... | collective-permute-start | bytes 196616 | tf_op jit(solution)/shard_map/ppermute | solution.py:159
  18.7 0.8 reduce-window.8
  19.6 0.5 multiply_cosine_fusion
  20.2 0.7 fusion.31
  21.0 1.9 %collective-permute-start.1 = (bf16[32,1024]{1,0:T(8,128)(2,1)S(1)}, bf16[32,1024]{1,0:T(8,128)(2,1)S(1)}, u32[]{:S(2)}, u32[]{:S(2)}) collective-permute-start(bf16[32,1024]{1,0:T(8,128)(2,1)S(1)} %get-tuple-element.37), channel_id=1, source_target_pairs={{0,8},{4,12},{8,16},{12,20},{16,24},{20,28},{24,0},{28,4},{1,9},{5... | collective-permute-start | bytes 196616 | tf_op jit(solution)/shard_map/ppermute | solution.py:159
  22.9 1.1 collective-permute-start
  24.0 1.3 and_select_fusion
  25.8 2.8 %collective-permute-done.2 = bf16[32,1024]{1,0:T(8,128)(2,1)S(1)} collective-permute-done((bf16[32,1024]{1,0:T(8,128)(2,1)S(1)}, bf16[32,1024]{1,0:T(8,128)(2,1)S(1)}, u32[]{:S(2)}, u32[]{:S(2)}) %collective-permute-start.2) | collective-permute-done | bytes 65568 | tf_op jit(solution)/shard_map/ppermute | solution.py:159
  28.6 0.8 copy.93
  29.3 0.8 copy.92
  30.1 0.8 copy.91
  30.8 2.9 %stack.58 = bf16[8,32,1024]{2,0,1:T(8,128)(2,1)S(1)} concatenate(bf16[1,32,1024]{2,0,1:T(2,128)(2,1)S(1)} %copy.132, bf16[1,32,1024]{2,0,1:T(2,128)(2,1)} %copy.91, bf16[1,32,1024]{2,0,1:T(2,128)(2,1)} %copy.92, bf16[1,32,1024]{2,0,1:T(2,128)(2,1)} %copy.93, bf16[1,32,1024]{2,0,1:T(2,128)(2,1)S(1)} %copy.94, bf16[1,32,1024]{2,0,1:T(2,128)(2,1)S(1)} %copy.95, ...), dimensions={0} | concatenate | bytes 1048576 | tf_op jit(solution)/shard_map/stack | solution.py:160
  33.8 0.4 convolution_convert_fusion.3
  34.1 1.1 copy.98
  35.3 2.2 %fusion = f32[256]{0:T(256)S(1)} fusion(bf16[256,4096]{1,0:T(8,128)(2,1)} %all-gather.3.cloned.1.call-done), kind=kLoop, calls=%fused_computation.5 | loop fusion | flops 3145472 | bytes 2098176 | tf_op jit(solution)/shard_map/reduce_sum | solution.py:183
  37.5 0.6 multiply_multiply_fusion
  38.1 1.2 fusion.47
  39.6 6.5 %convolution_bitcast_fusion = f32[32,8,8,128]{3,1,2,0:T(8,128)S(1)} fusion(bf16[4096,1024]{1,0:T(8,128)(2,1)} %param.11, bf16[256,4096]{1,0:T(8,128)(2,1)} %all-gather.3.cloned.1.call-done, f32[4096]{0:T(1024)S(1)} %copy-done.19, f32[256]{0:T(256)S(1)} %get-tuple-element.45), kind=kOutput, calls=%fused_computation.16 | convolution fusion | flops 2151677952 | bytes 11551744 | tf_op jit(solution)/shard_map/dot_general | solution.py:185
  46.3 0.5 subtract_convert_fusion.1
  47.2 0.6 copy-done.9
  47.9 0.9 fusion.7
  49.0 0.6 copy-done.13
  49.6 1.2 convolution_convert_fusion.4
  51.0 0.7 convolution_convert_fusion.1
  51.7 0.9 slice-done
  52.6 1.4 %slice-done.1 = s8[4194304]{0:T(1024)(128)(4,1)S(1)} async-done(((s8[8388608]{0:T(1024)(128)(4,1)}), s8[4194304]{0:T(1024)(128)(4,1)S(1)}, s32[]{:S(2)}) %slice-start.1) | async-done | bytes 4194328
  54.1 4.5 %fusion.55 = f32[256,4096]{1,0:T(8,128)} fusion(bf16[256,1024]{0,1:T(8,128)(2,1)S(1)} %bitcast.171, bf16[1024,4096]{1,0:T(8,128)(2,1)S(1)} %bitcast.167), kind=kOutput, calls=%fused_computation.116 | convolution fusion | flops 2147483648 | bytes 13107200 | tf_op jit(solution)/shard_map/dot_general | solution.py:213
  58.6 1.1 all-gather.5.cloned.1.call-done
  59.7 1.7 %fusion.19 = (bf16[1,256,1024]{2,1,0:T(8,128)(2,1)S(1)}, bf16[1,256,1024]{2,1,0:T(8,128)(2,1)S(1)}) fusion(f32[256,4096]{1,0:T(8,128)} %fusion.55, s32[]{:T(128)S(6)} %select_n.111, s32[]{:T(128)S(6)} %select_n.112), kind=kLoop, calls=%fused_computation.54 | loop fusion | bytes 2097160 | tf_op jit(solution)/shard_map/stack | solution.py:100
  61.4 1.1 pad_maximum_fusion
  62.7 7.4 %convolution_convert_fusion = bf16[256,1024]{1,0:T(8,128)(2,1)} fusion(bf16[256,4096]{1,0:T(8,128)(2,1)} %all-gather.5.cloned.1.call-done, bf16[1024,4096]{1,0:T(8,128)(2,1)} %param.14), kind=kOutput, calls=%fused_computation.19 | convolution fusion | flops 2147745792 | bytes 11010048 | tf_op jit(solution)/shard_map/dot_general | solution.py:216
  70.1 1.2 copy.99
  71.6 2.5 %fusion.5 = bf16[2,4,256,256]{2,3,1,0:T(8,128)(2,1)S(1)} fusion(bf16[256,2,128,1]{0,2,3,1:T(8,128)(2,1)} %bitcast.195, bf16[256,2,4,128]{0,3,2,1:T(8,128)(2,1)S(1)} %bitcast.172, f32[2,4,256]{2,1,0:T(4,128)S(1)} %bitcast.191, f32[2,4,256]{2,1,0:T(4,128)} %copy-done.27, f32[2,256,256,4]{2,1,3,0:T(8,128)} %copy-done.25, pred[256,256]{0,1:T(8,128)(4,1)} %fusion.31), kind=kOutput, calls=%fused_computation.11 | convolution fusion | flops 137363456 | bytes 3883008 | tf_op jit(solution)/shard_map/qkgd,skd->kgqs/dot_general | solution.py:230
  74.1 0.5 fusion.9
  74.6 0.4 copy-done.16
  75.0 0.4 convolution_multiply_fusion
  75.4 1.1 fusion.53
  77.0 1.5 %copy.134 = f32[256,8,64]{2,1,0:T(8,128)S(1)} copy(f32[256,8,64]{0,2,1:T(8,128)} %get-tuple-element.26) | data formatting | bytes 1048576
  78.4 2.3 %fusion.23 = bf16[1,256,1024]{2,1,0:T(8,128)(2,1)} fusion(f32[256,4096]{1,0:T(8,128)} %fusion.55, s32[]{:T(128)S(6)} %select_n.113, bf16[2,256,1024]{2,1,0:T(8,128)(2,1)} %collective-permute-done.7), kind=kLoop, calls=%fused_computation.58 | loop fusion | flops 786432 | bytes 2097156 | tf_op jit(solution)/shard_map/convert_element_type | solution.py:100
  81.1 2.4 %copy.133 = f32[256,8,64]{2,1,0:T(8,128)} copy(f32[256,8,64]{0,2,1:T(8,128)} %get-tuple-element.27) | data formatting | bytes 1048576
  83.4 1.5 %add_convert_fusion = (bf16[256,8,64]{2,1,0:T(8,128)(2,1)S(1)}, bf16[256,8,64]{2,1,0:T(8,128)(2,1)S(1)}) fusion(f32[256,8,64]{2,1,0:T(8,128)S(1)} %copy.134, f32[256,8,64]{2,1,0:T(8,128)} %copy.133, f32[256,64]{1,0:T(8,128)S(1)} %get-tuple-element.43, f32[256,64]{1,0:T(8,128)S(1)} %get-tuple-element.42), kind=kLoop, calls=%fused_computation.48 | loop fusion | flops 1048576 | bytes 1703936 | tf_op jit(solution)/shard_map/convert.12
  85.2 5.8 %fusion.25 = f32[256,4096]{1,0:T(8,128)S(1)} fusion(bf16[4096,1024]{1,0:T(8,128)(2,1)} %param.11, bf16[32,8,8,128]{3,2,1,0:T(8,128)(2,1)S(1)} %bitcast.179), kind=kOutput, calls=%fused_computation.60 | convolution fusion | flops 2147483648 | bytes 13107200 | tf_op jit(solution)/shard_map/dot_general | solution.py:253
  91.0 0.8 convolution_add_fusion.1
  92.0 0.7 copy-done.26
  92.8 0.7 fusion.10
  93.4 0.9 copy-done.14
  94.4 0.8 convolution_add_fusion
  95.4 3.1 %fusion.11 = bf16[256,1024]{1,0:T(8,128)(2,1)S(1)} fusion(bf16[256,1024]{1,0:T(8,128)(2,1)S(1)} %copy-done.6, f32[256,4096]{1,0:T(8,128)} %fusion.55, s32[]{:T(128)} %select_n.110, bf16[1,256,1024]{2,1,0:T(8,128)(2,1)} %collective-permute-done.8, bf16[2,256,1024]{2,1,0:T(8,128)(2,1)} %collective-permute-done.7), kind=kLoop, calls=%fused_computation.29 | loop fusion | flops 1835008 | bytes 3145732 | tf_op jit(solution)/shard_map/convert_element_type | solution.py:225
  98.7 1.1 pad_maximum_fusion.1
  99.8 0.4 convolution_convert_fusion.2
  100.2 1.1 copy.112
  101.3 5.7 %all-to-all-start = ((bf16[8,32,1024]{2,1,0:T(8,128)(2,1)}), bf16[8,32,1024]{2,1,0:T(8,128)(2,1)}, u32[]{:S(2)}, u32[]{:S(2)}) async-start(bf16[8,32,1024]{2,1,0:T(8,128)(2,1)} %copy.112), calls=%async_computation | async-start | bytes 1048576 | tf_op jit(solution)/shard_map/all_to_all | solution.py:278
  107.0 2.5 %fusion.24 = bf16[1,256,1024]{2,1,0:T(8,128)(2,1)} fusion(f32[256,4096]{1,0:T(8,128)} %copy-done.1, s32[]{:T(128)S(6)} %select_n.113, bf16[2,256,1024]{2,1,0:T(8,128)(2,1)} %collective-permute-done.9), kind=kLoop, calls=%fused_computation.59 | loop fusion | flops 786432 | bytes 2097156 | tf_op jit(solution)/shard_map/convert_element_type | solution.py:100
  109.5 1.5 %collective-permute-start.10 = (bf16[1,256,1024]{2,1,0:T(8,128)(2,1)}, bf16[1,256,1024]{2,1,0:T(8,128)(2,1)}, u32[]{:S(2)}, u32[]{:S(2)}) collective-permute-start(bf16[1,256,1024]{2,1,0:T(8,128)(2,1)} %fusion.24), channel_id=1, source_target_pairs={{0,2},{1,3},{2,0},{3,1},{4,6},{5,7},{6,4},{7,5},{8,10},{9,11},{10,... | collective-permute-start | bytes 1572872 | tf_op jit(solution)/shard_map/ppermute | solution.py:104
  111.0 2.8 %fusion.3 = f32[256]{0:T(256)S(1)} fusion(bf16[256,4096]{1,0:T(8,128)(2,1)S(1)} %copy-done.4, f32[256,4096]{1,0:T(8,128)} %copy-done.1, f32[4096]{0:T(1024)S(1)} %copy-done.19), kind=kLoop, calls=%fused_computation.8 | loop fusion | flops 4194048 | bytes 6308864 | tf_op jit(solution)/shard_map/reduce_sum | solution.py:273
  113.9 1.1 collective-permute-done.11
  115.1 0.5 collective-permute-start.12
  115.6 8.3 %collective-permute-done.12 = f32[256]{0:T(256)S(1)} collective-permute-done((f32[256]{0:T(256)S(1)}, f32[256]{0:T(256)S(1)}, u32[]{:S(2)}, u32[]{:S(2)}) %collective-permute-start.12) | collective-permute-done | bytes 1056 | tf_op jit(solution)/shard_map/ppermute | solution.py:104
  124.0 2.8 %fusion.14 = bf16[256,1024]{1,0:T(8,128)(2,1)} fusion(bf16[256,1024]{1,0:T(8,128)(2,1)S(1)} %copy-done.6, f32[256,4096]{1,0:T(8,128)} %copy-done.1, s32[]{:T(128)} %select_n.110, bf16[2,256,1024]{2,1,0:T(8,128)(2,1)} %collective-permute-done.9, bf16[1,256,1024]{2,1,0:T(8,128)(2,1)} %collective-permute-done.10, f32[256]{0:T(256)S(1)} %add_multiply_fusion, ...), kind=kLoop, calls=%fused_computation.32 | loop fusion | flops 3407872 | bytes 3677188 | tf_op jit(solution)/shard_map/convert_element_type | solution.py:292
  126.8 1.9 %copy.144 = bf16[256,1024]{1,0:T(8,128)(2,1)} copy(bf16[256,1024]{1,0:T(8,128)(2,1)} %bitcast.54) | data formatting | bytes 1048576
  (102 shorter events, 4.2 us)
Async XLA Ops:
  7.2 31.0 %copy-start = (bf16[4096,256]{1,0:T(8,128)(2,1)S(1)}, bf16[4096,256]{1,0:T(8,128)(2,1)}, u32[]{:S(2)}) copy-start(bf16[4096,256]{1,0:T(8,128)(2,1)} %param.12) | copy-start | bytes 6291460
  7.2 28.1 %all-gather.3.cloned.1.call-start = ((), (), s32[]{:S(2)}) async-start(), calls=%async_computation.1 | async-start | bytes 2621440 | tf_op jit(solution)/shard_map/all_gather | solution.py:181
  7.9 51.8 %all-gather.5.cloned.1.call-start = ((), (), s32[]{:S(2)}) async-start(), calls=%async_computation.2 | async-start | bytes 2621440 | tf_op jit(solution)/shard_map/all_gather | solution.py:214
  9.2 11.8 %collective-permute-start.6 = (bf16[32,1024]{1,0:T(8,128)(2,1)S(1)}, bf16[32,1024]{1,0:T(8,128)(2,1)S(1)}, u32[]{:S(2)}, u32[]{:S(2)}) collective-permute-start(bf16[32,1024]{1,0:T(8,128)(2,1)S(1)} %get-tuple-element.32), channel_id=1, source_target_pairs={{0,28},{4,0},{8,4},{12,8},{16,12},{20,16},{24,20},{28,24},{1,29},{... | collective-permute-start | bytes 196616 | tf_op jit(solution)/shard_map/ppermute | solution.py:159
  15.2 7.7 %collective-permute-start.5 = (bf16[32,1024]{1,0:T(8,128)(2,1)S(1)}, bf16[32,1024]{1,0:T(8,128)(2,1)S(1)}, u32[]{:S(2)}, u32[]{:S(2)}) collective-permute-start(bf16[32,1024]{1,0:T(8,128)(2,1)S(1)} %get-tuple-element.33), channel_id=1, source_target_pairs={{0,24},{4,28},{8,0},{12,4},{16,8},{20,12},{24,16},{28,20},{1,25},{... | collective-permute-start | bytes 196616 | tf_op jit(solution)/shard_map/ppermute | solution.py:159
  15.7 9.9 %collective-permute-start.4 = (bf16[32,1024]{1,0:T(8,128)(2,1)S(1)}, bf16[32,1024]{1,0:T(8,128)(2,1)S(1)}, u32[]{:S(2)}, u32[]{:S(2)}) collective-permute-start(bf16[32,1024]{1,0:T(8,128)(2,1)S(1)} %get-tuple-element.34), channel_id=1, source_target_pairs={{0,20},{4,24},{8,28},{12,0},{16,4},{20,8},{24,12},{28,16},{1,21},{... | collective-permute-start | bytes 196616 | tf_op jit(solution)/shard_map/ppermute | solution.py:159
  15.7 10.0 %collective-permute-start.3 = (bf16[32,1024]{1,0:T(8,128)(2,1)S(1)}, bf16[32,1024]{1,0:T(8,128)(2,1)S(1)}, u32[]{:S(2)}, u32[]{:S(2)}) collective-permute-start(bf16[32,1024]{1,0:T(8,128)(2,1)S(1)} %get-tuple-element.35), channel_id=1, source_target_pairs={{0,16},{4,20},{8,24},{12,28},{16,0},{20,4},{24,8},{28,12},{1,17},{... | collective-permute-start | bytes 196616 | tf_op jit(solution)/shard_map/ppermute | solution.py:159
  18.7 9.9 %collective-permute-start.2 = (bf16[32,1024]{1,0:T(8,128)(2,1)S(1)}, bf16[32,1024]{1,0:T(8,128)(2,1)S(1)}, u32[]{:S(2)}, u32[]{:S(2)}) collective-permute-start(bf16[32,1024]{1,0:T(8,128)(2,1)S(1)} %get-tuple-element.36), channel_id=1, source_target_pairs={{0,12},{4,16},{8,20},{12,24},{16,28},{20,0},{24,4},{28,8},{1,13},{... | collective-permute-start | bytes 196616 | tf_op jit(solution)/shard_map/ppermute | solution.py:159
  21.0 8.3 %collective-permute-start.1 = (bf16[32,1024]{1,0:T(8,128)(2,1)S(1)}, bf16[32,1024]{1,0:T(8,128)(2,1)S(1)}, u32[]{:S(2)}, u32[]{:S(2)}) collective-permute-start(bf16[32,1024]{1,0:T(8,128)(2,1)S(1)} %get-tuple-element.37), channel_id=1, source_target_pairs={{0,8},{4,12},{8,16},{12,20},{16,24},{20,28},{24,0},{28,4},{1,9},{5... | collective-permute-start | bytes 196616 | tf_op jit(solution)/shard_map/ppermute | solution.py:159
  22.9 7.2 %collective-permute-start = (bf16[32,1024]{1,0:T(8,128)(2,1)S(1)}, bf16[32,1024]{1,0:T(8,128)(2,1)S(1)}, u32[]{:S(2)}, u32[]{:S(2)}) collective-permute-start(bf16[32,1024]{1,0:T(8,128)(2,1)S(1)} %get-tuple-element.38), channel_id=1, source_target_pairs={{0,4},{4,8},{8,12},{12,16},{16,20},{20,24},{24,28},{28,0},{1,5},{5... | collective-permute-start | bytes 196616 | tf_op jit(solution)/shard_map/ppermute | solution.py:159
  34.1 4.0 %copy-start.19 = (f32[4096]{0:T(1024)S(1)}, f32[4096]{0:T(1024)}, u32[]{:S(2)}) copy-start(f32[4096]{0:T(1024)} %param.10) | copy-start | bytes 49156
  35.3 2.8 %copy-start.2 = (bf16[256,4096]{1,0:T(8,128)(2,1)S(1)}, bf16[256,4096]{1,0:T(8,128)(2,1)}, u32[]{:S(2)}) copy-start(bf16[256,4096]{1,0:T(8,128)(2,1)} %all-gather.3.cloned.1.call-done) | copy-start | bytes 6291460
  38.1 10.7 %copy-start.21 = (f32[256]{0:T(256)}, f32[256]{0:T(256)S(1)}, u32[]{:S(2)}) copy-start(f32[256]{0:T(256)S(1)} %get-tuple-element.45) | copy-start | bytes 3076
  46.9 1.1 copy-start.17
  46.9 0.8 copy-start.9
  47.0 0.9 copy-start.11
  47.0 1.9 %copy-start.3 = (bf16[256,4096]{1,0:T(8,128)(2,1)S(1)}, bf16[256,4096]{1,0:T(8,128)(2,1)}, u32[]{:S(2)}) copy-start(bf16[256,4096]{1,0:T(8,128)(2,1)} %all-gather.3.cloned.1.call-done) | copy-start | bytes 6291460
  47.1 2.6 %copy-start.13 = (bf16[4096,256]{1,0:T(8,128)(2,1)S(1)}, bf16[4096,256]{1,0:T(8,128)(2,1)}, u32[]{:S(2)}) copy-start(bf16[4096,256]{1,0:T(8,128)(2,1)} %param.13) | copy-start | bytes 6291460
  47.1 3.7 %copy-start.15 = (bf16[256,2,64]{2,0,1:T(8,128)(2,1)}, bf16[256,2,64]{2,0,1:T(8,128)(2,1)S(1)}, u32[]{:S(2)}) copy-start(bf16[256,2,64]{2,0,1:T(8,128)(2,1)S(1)} %get-tuple-element.29) | copy-start | bytes 196612
  49.6 1.4 %copy-start.25 = (f32[2,256,256,4]{2,1,3,0:T(8,128)}, f32[2,256,256,4]{2,1,3,0:T(8,128)S(1)}, u32[]{:S(2)}) copy-start(f32[2,256,256,4]{2,1,3,0:T(8,128)S(1)} %get-tuple-element.47) | copy-start | bytes 6291460
  49.6 1.4 %copy-start.27 = (f32[2,4,256]{2,1,0:T(4,128)}, f32[2,4,256]{2,1,0:T(4,128)S(1)}, u32[]{:S(2)}) copy-start(f32[2,4,256]{2,1,0:T(4,128)S(1)} %get-tuple-element.46) | copy-start | bytes 24580
  49.6 3.0 %slice-start = ((s8[8388608]{0:T(1024)(128)(4,1)}), s8[4194304]{0:T(1024)(128)(4,1)S(1)}, s32[]{:S(2)}) async-start(s8[8388608]{0:T(1024)(128)(4,1)} %bitcast.166), calls=%async_computation.3 | async-start | bytes 8388608
  50.8 0.8 copy-start.24
  51.0 3.1 %slice-start.1 = ((s8[8388608]{0:T(1024)(128)(4,1)}), s8[4194304]{0:T(1024)(128)(4,1)S(1)}, s32[]{:S(2)}) async-start(s8[8388608]{0:T(1024)(128)(4,1)} %bitcast.166), calls=%async_computation.4 | async-start | bytes 8388608
  62.5 7.7 %collective-permute-start.7 = (bf16[2,256,1024]{2,1,0:T(8,128)(2,1)}, bf16[2,256,1024]{2,1,0:T(8,128)(2,1)}, u32[]{:S(2)}, u32[]{:S(2)}) collective-permute-start(bf16[2,256,1024]{2,1,0:T(8,128)(2,1)} %pad_maximum_fusion), channel_id=1, source_target_pairs={{0,1},{1,0},{2,3},{3,2},{4,5},{5,4},{6,7},{7,6},{8,9},{9,8},{10,11... | collective-permute-start | bytes 3145736 | tf_op jit(solution)/shard_map/ppermute | solution.py:102
  71.4 2.7 %copy-start.7 = (bf16[256,1024]{0,1:T(8,128)(2,1)}, bf16[256,1024]{0,1:T(8,128)(2,1)S(1)}, u32[]{:S(2)}) copy-start(bf16[256,1024]{0,1:T(8,128)(2,1)S(1)} %copy.99) | copy-start | bytes 1572868
  71.6 2.5 %copy-start.10 = (bf16[256,8,64]{2,0,1:T(8,128)(2,1)S(1)}, bf16[256,8,64]{2,0,1:T(8,128)(2,1)}, u32[]{:S(2)}) copy-start(bf16[256,8,64]{2,0,1:T(8,128)(2,1)} %copy-done.9) | copy-start | bytes 786436
  71.6 2.5 %copy-start.12 = (bf16[256,8,64]{2,0,1:T(8,128)(2,1)S(1)}, bf16[256,8,64]{2,0,1:T(8,128)(2,1)}, u32[]{:S(2)}) copy-start(bf16[256,8,64]{2,0,1:T(8,128)(2,1)} %copy-done.11) | copy-start | bytes 786436
  74.1 0.9 copy-start.16
  80.7 14.4 %collective-permute-start.8 = (bf16[1,256,1024]{2,1,0:T(8,128)(2,1)}, bf16[1,256,1024]{2,1,0:T(8,128)(2,1)}, u32[]{:S(2)}, u32[]{:S(2)}) collective-permute-start(bf16[1,256,1024]{2,1,0:T(8,128)(2,1)} %fusion.23), channel_id=1, source_target_pairs={{0,2},{1,3},{2,0},{3,1},{4,6},{5,7},{6,4},{7,5},{8,10},{9,11},{10,... | collective-permute-start | bytes 1572872 | tf_op jit(solution)/shard_map/ppermute | solution.py:102
  91.0 1.0 copy-start.8
  91.0 1.0 copy-start.18
  91.0 1.8 %copy-start.26 = (f32[2,256,256,4]{2,1,3,0:T(8,128)S(1)}, f32[2,256,256,4]{2,1,3,0:T(8,128)}, u32[]{:S(2)}) copy-start(f32[2,256,256,4]{2,1,3,0:T(8,128)} %copy-done.25) | copy-start | bytes 6291460
  91.0 1.8 %copy-start.28 = (f32[2,4,256]{2,1,0:T(4,128)S(1)}, f32[2,4,256]{2,1,0:T(4,128)}, u32[]{:S(2)}) copy-start(f32[2,4,256]{2,1,0:T(4,128)} %copy-done.27) | copy-start | bytes 24580
  92.8 1.6 %copy-start.14 = (bf16[4096,256]{1,0:T(8,128)(2,1)S(1)}, bf16[4096,256]{1,0:T(8,128)(2,1)}, u32[]{:S(2)}) copy-start(bf16[4096,256]{1,0:T(8,128)(2,1)} %param.13) | copy-start | bytes 6291460
  94.4 1.0 copy-start.6
  95.1 3.5 %copy-start.1 = (f32[256,4096]{1,0:T(8,128)}, f32[256,4096]{1,0:T(8,128)S(1)}, u32[]{:S(2)}) copy-start(f32[256,4096]{1,0:T(8,128)S(1)} %convolution_add_fusion) | copy-start | bytes 12582916
  98.5 1.4 copy-start.23
  99.8 7.2 %collective-permute-start.9 = (bf16[2,256,1024]{2,1,0:T(8,128)(2,1)}, bf16[2,256,1024]{2,1,0:T(8,128)(2,1)}, u32[]{:S(2)}, u32[]{:S(2)}) collective-permute-start(bf16[2,256,1024]{2,1,0:T(8,128)(2,1)} %pad_maximum_fusion.1), channel_id=1, source_target_pairs={{0,1},{1,0},{2,3},{3,2},{4,5},{5,4},{6,7},{7,6},{8,9},{9,8},{10,11... | collective-permute-start | bytes 3145736 | tf_op jit(solution)/shard_map/ppermute | solution.py:104
  101.3 22.6 %all-to-all-start = ((bf16[8,32,1024]{2,1,0:T(8,128)(2,1)}), bf16[8,32,1024]{2,1,0:T(8,128)(2,1)}, u32[]{:S(2)}, u32[]{:S(2)}) async-start(bf16[8,32,1024]{2,1,0:T(8,128)(2,1)} %copy.112), calls=%async_computation | async-start | bytes 1048576 | tf_op jit(solution)/shard_map/all_to_all | solution.py:278
  107.0 4.0 %copy-start.4 = (bf16[256,4096]{1,0:T(8,128)(2,1)S(1)}, bf16[256,4096]{1,0:T(8,128)(2,1)}, u32[]{:S(2)}) copy-start(bf16[256,4096]{1,0:T(8,128)(2,1)} %all-gather.3.cloned.1.call-done) | copy-start | bytes 6291460
  109.5 14.5 %copy-start.5 = (bf16[8,32,1024]{2,1,0:T(8,128)(2,1)S(1)}, bf16[8,32,1024]{2,1,0:T(8,128)(2,1)}, u32[]{:S(2)}) copy-start(bf16[8,32,1024]{2,1,0:T(8,128)(2,1)} %copy.98) | copy-start | bytes 1572868
  109.5 14.5 %dynamic-slice-start = ((f32[4096]{0:T(1024)}, s32[]{:T(128)}), f32[1024]{0:T(1024)S(1)}, s32[]{:S(2)}) async-start(f32[4096]{0:T(1024)} %param.10, s32[]{:T(128)} %select_n.110), calls=%async_computation.5 | async-start | bytes 8704 | tf_op jit(solution)/shard_map/dynamic_slice | solution.py:142
  109.5 14.5 %copy-start.20 = (f32[256]{0:T(256)S(1)}, f32[256]{0:T(256)}, u32[]{:S(2)}) copy-start(f32[256]{0:T(256)} %get-tuple-element.44) | copy-start | bytes 3076
  109.5 14.5 %copy-start.22 = (f32[256]{0:T(256)S(1)}, f32[256]{0:T(256)}, u32[]{:S(2)}) copy-start(f32[256]{0:T(256)} %copy-done.21) | copy-start | bytes 3076
  109.5 14.5 %collective-permute-start.10 = (bf16[1,256,1024]{2,1,0:T(8,128)(2,1)}, bf16[1,256,1024]{2,1,0:T(8,128)(2,1)}, u32[]{:S(2)}, u32[]{:S(2)}) collective-permute-start(bf16[1,256,1024]{2,1,0:T(8,128)(2,1)} %fusion.24), channel_id=1, source_target_pairs={{0,2},{1,3},{2,0},{3,1},{4,6},{5,7},{6,4},{7,5},{8,10},{9,11},{10,... | collective-permute-start | bytes 1572872 | tf_op jit(solution)/shard_map/ppermute | solution.py:104
  113.9 1.2 collective-permute-start.11
  115.1 8.9 %collective-permute-start.12 = (f32[256]{0:T(256)S(1)}, f32[256]{0:T(256)S(1)}, u32[]{:S(2)}, u32[]{:S(2)}) collective-permute-start(f32[256]{0:T(256)S(1)} %add.200), channel_id=1, source_target_pairs={{0,2},{1,3},{2,0},{3,1},{4,6},{5,7},{6,4},{7,5},{8,10},{9,11},{10,... | collective-permute-start | bytes 3080 | tf_op jit(solution)/shard_map/ppermute | solution.py:104
Sparse Core Ops, SparseCore 0:
  9.6 25.2 all-gather.2
  37.0 22.5 all-gather.4

commit v12 on v11

--- a/solution.py
+++ b/solution.py
@@ -275,12 +275,11 @@
     outgoing = jnp.einsum(
         "dj,jrw->drw", send_table, home_blocks, preferred_element_type=jnp.float32
     ).astype(jnp.bfloat16)
+    normed_gradient, stat_sum, (outgoing,) = scatter_features(
+        normed_partial, "tensor", tensor_size, tensor_index, extra=stat_partial, ties=(outgoing,)
+    )
     relaid = lax.all_to_all(outgoing, "dp", split_axis=0, concat_axis=0, tiled=True).reshape(
         token_row_count, width_part
-    )
-
-    normed_gradient, stat_sum, _ = scatter_features(
-        normed_partial, "tensor", tensor_size, tensor_index, extra=stat_partial
     )
     stat = stat_sum / full_width
     cubed = inverse * inverse * inverse

time: 137 us -> 135 us (0.985)
  other arithmetic: 24.8 us -> 22.8 us
    ppermute x4, waiting for transfers between devices: 9.47 us -> 10.9 us  [scatter_features(): lax.ppermute((outgoing, extra), axis_name, _xor_pairs(size, bit))]
  transfers between devices with their start and end apart: 16 -> 16, of which waited for: 4 -> 5; matrix products, arithmetic and copies ran while one was open for 42% -> 43% of each run, Pallas kernels for 0% -> 0%
where the time goes in v12:
time: 135 us; the launch traced here: 134 us
  matrix products  34.6 us (26%)
  local copies, waits for them, and re-layouts  25.4 us (19%)
  other arithmetic  22.8 us (17%)
  starting transfers between devices  21.3 us (16%)
  waiting for transfers between devices  14.8 us (11%)
  between operations  14.8 us (11%)
    ppermute x7, starting transfers between devices, per_device(): returned.append(lax.ppermute(piece, 'dp', pairs))  12.5 us
    unnamed x69, local copies, waits for them, and re-layouts  12 us
    ppermute x4, waiting for transfers between devices, scatter_features(): lax.ppermute((outgoing, extra), axis_name, _xor_pairs(size, bit))  10.9 us
    dot_general x1, matrix products, per_device(): lax.dot_general(grad_full, w_out, (((1,), (1,)), ((), ())), preferred_ele...  7.42 us
    dot_general x1, matrix products, per_device(): jnp.dot(normed_input, w_query, preferred_element_type=jnp.float32)  6.67 us
    dot_general x1, matrix products, per_device(): lax.dot_general(grad_query.reshape(token_row_count, query_width), w_query...  5.75 us
    another operation x8, local copies, waits for them, and re-layouts, per_device(): returned = jnp.stack(returned)  5.59 us
    all_to_all x1, starting transfers between devices, per_device(): lax.all_to_all(outgoing, 'dp', split_axis=0, concat_axis=0, tiled=True)  5.18 us
  transfers between devices with their start and end apart: 16, of which 5 were waited for; matrix products, arithmetic and copies ran while one was open for 43% of the time, Pallas kernels for 0%

profile of v12, /device:TPU:0, one launch (start us, length us, event | category | flops | bytes accessed | tf_op | source)
XLA Modules:
  0.0 133.7 jit_solution(13853256746741725114)
XLA Ops:
  7.2 0.7 all-gather.3.cloned.1.call-update
  8.1 1.1 dynamic-slice_bitcast_fusion
  9.2 6.0 %collective-permute-start.6 = (bf16[32,1024]{1,0:T(8,128)(2,1)S(1)}, bf16[32,1024]{1,0:T(8,128)(2,1)S(1)}, u32[]{:S(2)}, u32[]{:S(2)}) collective-permute-start(bf16[32,1024]{1,0:T(8,128)(2,1)S(1)} %get-tuple-element.36), channel_id=1, source_target_pairs={{0,28},{4,0},{8,4},{12,8},{16,12},{20,16},{24,20},{28,24},{1,29},{... | collective-permute-start | bytes 196616 | tf_op jit(solution)/shard_map/ppermute | solution.py:159
  15.2 0.4 collective-permute-start.5
  15.7 3.0 %collective-permute-start.3 = (bf16[32,1024]{1,0:T(8,128)(2,1)S(1)}, bf16[32,1024]{1,0:T(8,128)(2,1)S(1)}, u32[]{:S(2)}, u32[]{:S(2)}) collective-permute-start(bf16[32,1024]{1,0:T(8,128)(2,1)S(1)} %get-tuple-element.39), channel_id=1, source_target_pairs={{0,16},{4,20},{8,24},{12,28},{16,0},{20,4},{24,8},{28,12},{1,17},{... | collective-permute-start | bytes 196616 | tf_op jit(solution)/shard_map/ppermute | solution.py:159
  18.7 0.8 reduce-window.8
  19.6 0.5 multiply_cosine_fusion
  20.2 0.7 fusion.31
  21.0 1.9 %collective-permute-start.1 = (bf16[32,1024]{1,0:T(8,128)(2,1)S(1)}, bf16[32,1024]{1,0:T(8,128)(2,1)S(1)}, u32[]{:S(2)}, u32[]{:S(2)}) collective-permute-start(bf16[32,1024]{1,0:T(8,128)(2,1)S(1)} %get-tuple-element.41), channel_id=1, source_target_pairs={{0,8},{4,12},{8,16},{12,20},{16,24},{20,28},{24,0},{28,4},{1,9},{5... | collective-permute-start | bytes 196616 | tf_op jit(solution)/shard_map/ppermute | solution.py:159
  22.9 1.1 collective-permute-start
  24.0 1.3 and_select_fusion
  25.8 2.8 %collective-permute-done.2 = bf16[32,1024]{1,0:T(8,128)(2,1)S(1)} collective-permute-done((bf16[32,1024]{1,0:T(8,128)(2,1)S(1)}, bf16[32,1024]{1,0:T(8,128)(2,1)S(1)}, u32[]{:S(2)}, u32[]{:S(2)}) %collective-permute-start.2) | collective-permute-done | bytes 65568 | tf_op jit(solution)/shard_map/ppermute | solution.py:159
  28.6 0.8 copy.93
  29.3 0.8 copy.92
  30.1 0.8 copy.91
  30.8 2.9 %stack.58 = bf16[8,32,1024]{2,0,1:T(8,128)(2,1)S(1)} concatenate(bf16[1,32,1024]{2,0,1:T(2,128)(2,1)S(1)} %copy.132, bf16[1,32,1024]{2,0,1:T(2,128)(2,1)} %copy.91, bf16[1,32,1024]{2,0,1:T(2,128)(2,1)} %copy.92, bf16[1,32,1024]{2,0,1:T(2,128)(2,1)} %copy.93, bf16[1,32,1024]{2,0,1:T(2,128)(2,1)S(1)} %copy.94, bf16[1,32,1024]{2,0,1:T(2,128)(2,1)S(1)} %copy.95, ...), dimensions={0} | concatenate | bytes 1048576 | tf_op jit(solution)/shard_map/stack | solution.py:160
  33.8 0.4 convolution_convert_fusion.3
  34.1 1.1 copy.98
  35.3 2.2 %fusion = f32[256]{0:T(256)S(1)} fusion(bf16[256,4096]{1,0:T(8,128)(2,1)} %all-gather.3.cloned.1.call-done), kind=kLoop, calls=%fused_computation.5 | loop fusion | flops 3145472 | bytes 2098176 | tf_op jit(solution)/shard_map/reduce_sum | solution.py:183
  37.5 0.6 multiply_multiply_fusion
  38.1 1.2 fusion.47
  39.6 6.7 %convolution_bitcast_fusion = f32[32,8,8,128]{3,1,2,0:T(8,128)S(1)} fusion(bf16[4096,1024]{1,0:T(8,128)(2,1)} %param.11, bf16[256,4096]{1,0:T(8,128)(2,1)} %all-gather.3.cloned.1.call-done, f32[4096]{0:T(1024)S(1)} %copy-done.19, f32[256]{0:T(256)S(1)} %get-tuple-element.49), kind=kOutput, calls=%fused_computation.16 | convolution fusion | flops 2151677952 | bytes 11551744 | tf_op jit(solution)/shard_map/dot_general | solution.py:185
  46.5 0.5 subtract_convert_fusion.1
  47.3 0.6 copy-done.9
  48.0 0.9 fusion.7
  49.1 0.7 copy-done.13
  49.8 1.2 convolution_convert_fusion.4
  51.1 0.7 convolution_convert_fusion.1
  51.8 1.0 slice-done
  52.8 1.4 %slice-done.1 = s8[4194304]{0:T(1024)(128)(4,1)S(1)} async-done(((s8[8388608]{0:T(1024)(128)(4,1)}), s8[4194304]{0:T(1024)(128)(4,1)S(1)}, s32[]{:S(2)}) %slice-start.1) | async-done | bytes 4194328
  54.2 4.5 %fusion.55 = f32[256,4096]{1,0:T(8,128)} fusion(bf16[256,1024]{0,1:T(8,128)(2,1)S(1)} %bitcast.167, bf16[1024,4096]{1,0:T(8,128)(2,1)S(1)} %bitcast.163), kind=kOutput, calls=%fused_computation.114 | convolution fusion | flops 2147483648 | bytes 13107200 | tf_op jit(solution)/shard_map/dot_general | solution.py:213
  59.1 1.7 %fusion.19 = (bf16[1,256,1024]{2,1,0:T(8,128)(2,1)S(1)}, bf16[1,256,1024]{2,1,0:T(8,128)(2,1)S(1)}) fusion(f32[256,4096]{1,0:T(8,128)} %fusion.55, s32[]{:T(128)S(6)} %select_n.111, s32[]{:T(128)S(6)} %select_n.112), kind=kLoop, calls=%fused_computation.54 | loop fusion | bytes 2097160 | tf_op jit(solution)/shard_map/stack | solution.py:100
  60.8 1.1 pad_maximum_fusion
  62.1 7.4 %convolution_convert_fusion = bf16[256,1024]{1,0:T(8,128)(2,1)} fusion(bf16[256,4096]{1,0:T(8,128)(2,1)} %all-gather.5.cloned.1.call-done, bf16[1024,4096]{1,0:T(8,128)(2,1)} %param.14), kind=kOutput, calls=%fused_computation.19 | convolution fusion | flops 2147745792 | bytes 11010048 | tf_op jit(solution)/shard_map/dot_general | solution.py:216
  69.5 1.2 copy.99
  71.0 2.5 %fusion.5 = bf16[2,4,256,256]{2,3,1,0:T(8,128)(2,1)S(1)} fusion(bf16[256,2,128,1]{0,2,3,1:T(8,128)(2,1)} %bitcast.192, bf16[256,2,4,128]{0,3,2,1:T(8,128)(2,1)S(1)} %bitcast.168, f32[2,4,256]{2,1,0:T(4,128)S(1)} %bitcast.188, f32[2,4,256]{2,1,0:T(4,128)} %copy-done.27, f32[2,256,256,4]{2,1,3,0:T(8,128)} %copy-done.25, pred[256,256]{0,1:T(8,128)(4,1)} %fusion.31), kind=kOutput, calls=%fused_computation.11 | convolution fusion | flops 137363456 | bytes 3883008 | tf_op jit(solution)/shard_map/qkgd,skd->kgqs/dot_general | solution.py:230
  73.5 0.5 fusion.9
  74.1 0.4 copy-done.16
  74.4 0.4 convolution_multiply_fusion
  74.8 1.1 fusion.53
  76.3 1.5 %copy.134 = f32[256,8,64]{2,1,0:T(8,128)S(1)} copy(f32[256,8,64]{0,2,1:T(8,128)} %get-tuple-element.30) | data formatting | bytes 1048576
  77.8 2.3 %fusion.23 = bf16[1,256,1024]{2,1,0:T(8,128)(2,1)} fusion(f32[256,4096]{1,0:T(8,128)} %fusion.55, s32[]{:T(128)S(6)} %select_n.113, bf16[2,256,1024]{2,1,0:T(8,128)(2,1)} %collective-permute-done.7), kind=kLoop, calls=%fused_computation.58 | loop fusion | flops 786432 | bytes 2097156 | tf_op jit(solution)/shard_map/convert_element_type | solution.py:100
  80.1 0.9 collective-permute-start.8
  81.0 2.4 %copy.133 = f32[256,8,64]{2,1,0:T(8,128)} copy(f32[256,8,64]{0,2,1:T(8,128)} %get-tuple-element.31) | data formatting | bytes 1048576
  83.3 1.5 %add_convert_fusion = (bf16[256,8,64]{2,1,0:T(8,128)(2,1)S(1)}, bf16[256,8,64]{2,1,0:T(8,128)(2,1)S(1)}) fusion(f32[256,8,64]{2,1,0:T(8,128)S(1)} %copy.134, f32[256,8,64]{2,1,0:T(8,128)} %copy.133, f32[256,64]{1,0:T(8,128)S(1)} %get-tuple-element.47, f32[256,64]{1,0:T(8,128)S(1)} %get-tuple-element.46), kind=kLoop, calls=%fused_computation.48 | loop fusion | flops 1048576 | bytes 1703936 | tf_op jit(solution)/shard_map/convert.12
  85.1 5.8 %fusion.25 = f32[256,4096]{1,0:T(8,128)S(1)} fusion(bf16[4096,1024]{1,0:T(8,128)(2,1)} %param.11, bf16[32,8,8,128]{3,2,1,0:T(8,128)(2,1)S(1)} %bitcast.176), kind=kOutput, calls=%fused_computation.60 | convolution fusion | flops 2147483648 | bytes 13107200 | tf_op jit(solution)/shard_map/dot_general | solution.py:253
  90.9 0.8 convolution_add_fusion.1
  92.0 0.7 copy-done.26
  92.7 0.7 fusion.10
  93.4 0.9 copy-done.14
  94.3 0.8 convolution_add_fusion
  95.3 3.1 %fusion.11 = bf16[256,1024]{1,0:T(8,128)(2,1)S(1)} fusion(bf16[256,1024]{1,0:T(8,128)(2,1)S(1)} %copy-done.6, f32[256,4096]{1,0:T(8,128)} %fusion.55, s32[]{:T(128)} %select_n.110, bf16[1,256,1024]{2,1,0:T(8,128)(2,1)} %collective-permute-done.8, bf16[2,256,1024]{2,1,0:T(8,128)(2,1)} %collective-permute-done.7), kind=kLoop, calls=%fused_computation.29 | loop fusion | flops 1835008 | bytes 3145732 | tf_op jit(solution)/shard_map/convert_element_type | solution.py:225
  99.1 0.4 convolution_convert_fusion.2
  99.5 2.1 %collective-permute-done.9 = bf16[2,256,1024]{2,1,0:T(8,128)(2,1)} collective-permute-done((bf16[2,256,1024]{2,1,0:T(8,128)(2,1)S(1)}, bf16[2,256,1024]{2,1,0:T(8,128)(2,1)}, u32[]{:S(2)}, u32[]{:S(2)}) %collective-permute-start.9) | collective-permute-done | bytes 1048608 | tf_op jit(solution)/shard_map/ppermute | solution.py:104
  101.6 1.1 copy.112
  102.6 5.2 %all-to-all-start = ((bf16[8,32,1024]{2,1,0:T(8,128)(2,1)}), bf16[8,32,1024]{2,1,0:T(8,128)(2,1)S(1)}, u32[]{:S(2)}, u32[]{:S(2)}) async-start(bf16[8,32,1024]{2,1,0:T(8,128)(2,1)} %copy.112), calls=%async_computation | async-start | bytes 1048576 | tf_op jit(solution)/shard_map/all_to_all | solution.py:281
  107.8 1.7 %fusion.24 = bf16[1,256,1024]{2,1,0:T(8,128)(2,1)S(1)} fusion(f32[256,4096]{1,0:T(8,128)} %copy-done.1, s32[]{:T(128)S(6)} %select_n.113, bf16[2,256,1024]{2,1,0:T(8,128)(2,1)} %collective-permute-done.9), kind=kLoop, calls=%fused_computation.59 | loop fusion | flops 786432 | bytes 2097156 | tf_op jit(solution)/shard_map/convert_element_type | solution.py:100
  109.5 1.6 %collective-permute-start.10 = (bf16[1,256,1024]{2,1,0:T(8,128)(2,1)S(1)}, bf16[1,256,1024]{2,1,0:T(8,128)(2,1)S(1)}, u32[]{:S(2)}, u32[]{:S(2)}) collective-permute-start(bf16[1,256,1024]{2,1,0:T(8,128)(2,1)S(1)} %fusion.24), channel_id=1, source_target_pairs={{0,2},{1,3},{2,0},{3,1},{4,6},{5,7},{6,4},{7,5},{8,10},{9,11},{10,... | collective-permute-start | bytes 1572872 | tf_op jit(solution)/shard_map/ppermute | solution.py:104
  111.1 2.8 %fusion.3 = f32[256]{0:T(256)S(1)} fusion(bf16[256,4096]{1,0:T(8,128)(2,1)S(1)} %copy-done.4, f32[256,4096]{1,0:T(8,128)} %copy-done.1, f32[4096]{0:T(1024)S(1)} %copy-done.19), kind=kLoop, calls=%fused_computation.8 | loop fusion | flops 4194048 | bytes 6308864 | tf_op jit(solution)/shard_map/reduce_sum | solution.py:273
  114.0 1.1 collective-permute-done.11
  115.1 0.5 collective-permute-start.12
  115.7 7.7 %collective-permute-done.12 = f32[256]{0:T(256)S(1)} collective-permute-done((f32[256]{0:T(256)S(1)}, f32[256]{0:T(256)S(1)}, u32[]{:S(2)}, u32[]{:S(2)}) %collective-permute-start.12) | collective-permute-done | bytes 1056 | tf_op jit(solution)/shard_map/ppermute | solution.py:104
  123.4 2.6 %fusion.14 = bf16[256,1024]{1,0:T(8,128)(2,1)} fusion(bf16[256,1024]{1,0:T(8,128)(2,1)S(1)} %copy-done.6, f32[256,4096]{1,0:T(8,128)} %copy-done.1, s32[]{:T(128)} %select_n.110, bf16[1,256,1024]{2,1,0:T(8,128)(2,1)S(1)} %collective-permute-done.10, f32[256]{0:T(256)S(1)} %add_multiply_fusion, f32[256]{0:T(256)S(1)} %copy-done.20, ...), kind=kLoop, calls=%fused_computation.32 | loop fusion | flops 3407872 | bytes 3677188 | tf_op jit(solution)/shard_map/convert_element_type | solution.py:291
  126.0 0.8 copy.144
  (102 shorter events, 4.7 us)
Async XLA Ops:
  7.2 31.0 %copy-start = (bf16[4096,256]{1,0:T(8,128)(2,1)S(1)}, bf16[4096,256]{1,0:T(8,128)(2,1)}, u32[]{:S(2)}) copy-start(bf16[4096,256]{1,0:T(8,128)(2,1)} %param.12) | copy-start | bytes 6291460
  7.2 28.1 %all-gather.3.cloned.1.call-start = ((), (), s32[]{:S(2)}) async-start(), calls=%async_computation.1 | async-start | bytes 2621440 | tf_op jit(solution)/shard_map/all_gather | solution.py:181
  7.9 51.2 %all-gather.5.cloned.1.call-start = ((), (), s32[]{:S(2)}) async-start(), calls=%async_computation.2 | async-start | bytes 2621440 | tf_op jit(solution)/shard_map/all_gather | solution.py:214
  9.2 11.8 %collective-permute-start.6 = (bf16[32,1024]{1,0:T(8,128)(2,1)S(1)}, bf16[32,1024]{1,0:T(8,128)(2,1)S(1)}, u32[]{:S(2)}, u32[]{:S(2)}) collective-permute-start(bf16[32,1024]{1,0:T(8,128)(2,1)S(1)} %get-tuple-element.36), channel_id=1, source_target_pairs={{0,28},{4,0},{8,4},{12,8},{16,12},{20,16},{24,20},{28,24},{1,29},{... | collective-permute-start | bytes 196616 | tf_op jit(solution)/shard_map/ppermute | solution.py:159
  15.2 7.7 %collective-permute-start.5 = (bf16[32,1024]{1,0:T(8,128)(2,1)S(1)}, bf16[32,1024]{1,0:T(8,128)(2,1)S(1)}, u32[]{:S(2)}, u32[]{:S(2)}) collective-permute-start(bf16[32,1024]{1,0:T(8,128)(2,1)S(1)} %get-tuple-element.37), channel_id=1, source_target_pairs={{0,24},{4,28},{8,0},{12,4},{16,8},{20,12},{24,16},{28,20},{1,25},{... | collective-permute-start | bytes 196616 | tf_op jit(solution)/shard_map/ppermute | solution.py:159
  15.7 9.9 %collective-permute-start.4 = (bf16[32,1024]{1,0:T(8,128)(2,1)S(1)}, bf16[32,1024]{1,0:T(8,128)(2,1)S(1)}, u32[]{:S(2)}, u32[]{:S(2)}) collective-permute-start(bf16[32,1024]{1,0:T(8,128)(2,1)S(1)} %get-tuple-element.38), channel_id=1, source_target_pairs={{0,20},{4,24},{8,28},{12,0},{16,4},{20,8},{24,12},{28,16},{1,21},{... | collective-permute-start | bytes 196616 | tf_op jit(solution)/shard_map/ppermute | solution.py:159
  15.7 10.0 %collective-permute-start.3 = (bf16[32,1024]{1,0:T(8,128)(2,1)S(1)}, bf16[32,1024]{1,0:T(8,128)(2,1)S(1)}, u32[]{:S(2)}, u32[]{:S(2)}) collective-permute-start(bf16[32,1024]{1,0:T(8,128)(2,1)S(1)} %get-tuple-element.39), channel_id=1, source_target_pairs={{0,16},{4,20},{8,24},{12,28},{16,0},{20,4},{24,8},{28,12},{1,17},{... | collective-permute-start | bytes 196616 | tf_op jit(solution)/shard_map/ppermute | solution.py:159
  18.7 9.9 %collective-permute-start.2 = (bf16[32,1024]{1,0:T(8,128)(2,1)S(1)}, bf16[32,1024]{1,0:T(8,128)(2,1)S(1)}, u32[]{:S(2)}, u32[]{:S(2)}) collective-permute-start(bf16[32,1024]{1,0:T(8,128)(2,1)S(1)} %get-tuple-element.40), channel_id=1, source_target_pairs={{0,12},{4,16},{8,20},{12,24},{16,28},{20,0},{24,4},{28,8},{1,13},{... | collective-permute-start | bytes 196616 | tf_op jit(solution)/shard_map/ppermute | solution.py:159
  21.0 8.3 %collective-permute-start.1 = (bf16[32,1024]{1,0:T(8,128)(2,1)S(1)}, bf16[32,1024]{1,0:T(8,128)(2,1)S(1)}, u32[]{:S(2)}, u32[]{:S(2)}) collective-permute-start(bf16[32,1024]{1,0:T(8,128)(2,1)S(1)} %get-tuple-element.41), channel_id=1, source_target_pairs={{0,8},{4,12},{8,16},{12,20},{16,24},{20,28},{24,0},{28,4},{1,9},{5... | collective-permute-start | bytes 196616 | tf_op jit(solution)/shard_map/ppermute | solution.py:159
  22.9 7.2 %collective-permute-start = (bf16[32,1024]{1,0:T(8,128)(2,1)S(1)}, bf16[32,1024]{1,0:T(8,128)(2,1)S(1)}, u32[]{:S(2)}, u32[]{:S(2)}) collective-permute-start(bf16[32,1024]{1,0:T(8,128)(2,1)S(1)} %get-tuple-element.42), channel_id=1, source_target_pairs={{0,4},{4,8},{8,12},{12,16},{16,20},{20,24},{24,28},{28,0},{1,5},{5... | collective-permute-start | bytes 196616 | tf_op jit(solution)/shard_map/ppermute | solution.py:159
  34.1 4.0 %copy-start.19 = (f32[4096]{0:T(1024)S(1)}, f32[4096]{0:T(1024)}, u32[]{:S(2)}) copy-start(f32[4096]{0:T(1024)} %param.10) | copy-start | bytes 49156
  35.3 2.8 %copy-start.2 = (bf16[256,4096]{1,0:T(8,128)(2,1)S(1)}, bf16[256,4096]{1,0:T(8,128)(2,1)}, u32[]{:S(2)}) copy-start(bf16[256,4096]{1,0:T(8,128)(2,1)} %all-gather.3.cloned.1.call-done) | copy-start | bytes 6291460
  38.1 10.8 %copy-start.21 = (f32[256]{0:T(256)}, f32[256]{0:T(256)S(1)}, u32[]{:S(2)}) copy-start(f32[256]{0:T(256)S(1)} %get-tuple-element.49) | copy-start | bytes 3076
  47.0 1.1 copy-start.17
  47.1 0.8 copy-start.9
  47.2 0.9 copy-start.11
  47.2 1.9 %copy-start.3 = (bf16[256,4096]{1,0:T(8,128)(2,1)S(1)}, bf16[256,4096]{1,0:T(8,128)(2,1)}, u32[]{:S(2)}) copy-start(bf16[256,4096]{1,0:T(8,128)(2,1)} %all-gather.3.cloned.1.call-done) | copy-start | bytes 6291460
  47.2 2.6 %copy-start.13 = (bf16[4096,256]{1,0:T(8,128)(2,1)S(1)}, bf16[4096,256]{1,0:T(8,128)(2,1)}, u32[]{:S(2)}) copy-start(bf16[4096,256]{1,0:T(8,128)(2,1)} %param.13) | copy-start | bytes 6291460
  47.3 3.7 %copy-start.15 = (bf16[256,2,64]{2,0,1:T(8,128)(2,1)}, bf16[256,2,64]{2,0,1:T(8,128)(2,1)S(1)}, u32[]{:S(2)}) copy-start(bf16[256,2,64]{2,0,1:T(8,128)(2,1)S(1)} %get-tuple-element.33) | copy-start | bytes 196612
  49.8 1.4 %copy-start.25 = (f32[2,256,256,4]{2,1,3,0:T(8,128)}, f32[2,256,256,4]{2,1,3,0:T(8,128)S(1)}, u32[]{:S(2)}) copy-start(f32[2,256,256,4]{2,1,3,0:T(8,128)S(1)} %get-tuple-element.51) | copy-start | bytes 6291460
  49.8 1.4 %copy-start.27 = (f32[2,4,256]{2,1,0:T(4,128)}, f32[2,4,256]{2,1,0:T(4,128)S(1)}, u32[]{:S(2)}) copy-start(f32[2,4,256]{2,1,0:T(4,128)S(1)} %get-tuple-element.50) | copy-start | bytes 24580
  49.8 3.0 %slice-start = ((s8[8388608]{0:T(1024)(128)(4,1)}), s8[4194304]{0:T(1024)(128)(4,1)S(1)}, s32[]{:S(2)}) async-start(s8[8388608]{0:T(1024)(128)(4,1)} %bitcast.162), calls=%async_computation.3 | async-start | bytes 8388608
  51.0 0.8 copy-start.24
  51.1 3.1 %slice-start.1 = ((s8[8388608]{0:T(1024)(128)(4,1)}), s8[4194304]{0:T(1024)(128)(4,1)S(1)}, s32[]{:S(2)}) async-start(s8[8388608]{0:T(1024)(128)(4,1)} %bitcast.162), calls=%async_computation.4 | async-start | bytes 8388608
  61.9 7.7 %collective-permute-start.7 = (bf16[2,256,1024]{2,1,0:T(8,128)(2,1)}, bf16[2,256,1024]{2,1,0:T(8,128)(2,1)}, u32[]{:S(2)}, u32[]{:S(2)}) collective-permute-start(bf16[2,256,1024]{2,1,0:T(8,128)(2,1)} %pad_maximum_fusion), channel_id=1, source_target_pairs={{0,1},{1,0},{2,3},{3,2},{4,5},{5,4},{6,7},{7,6},{8,9},{9,8},{10,11... | collective-permute-start | bytes 3145736 | tf_op jit(solution)/shard_map/ppermute | solution.py:102
  70.8 2.7 %copy-start.7 = (bf16[256,1024]{0,1:T(8,128)(2,1)}, bf16[256,1024]{0,1:T(8,128)(2,1)S(1)}, u32[]{:S(2)}) copy-start(bf16[256,1024]{0,1:T(8,128)(2,1)S(1)} %copy.99) | copy-start | bytes 1572868
  71.0 2.5 %copy-start.10 = (bf16[256,8,64]{2,0,1:T(8,128)(2,1)S(1)}, bf16[256,8,64]{2,0,1:T(8,128)(2,1)}, u32[]{:S(2)}) copy-start(bf16[256,8,64]{2,0,1:T(8,128)(2,1)} %copy-done.9) | copy-start | bytes 786436
  71.0 2.5 %copy-start.12 = (bf16[256,8,64]{2,0,1:T(8,128)(2,1)S(1)}, bf16[256,8,64]{2,0,1:T(8,128)(2,1)}, u32[]{:S(2)}) copy-start(bf16[256,8,64]{2,0,1:T(8,128)(2,1)} %copy-done.11) | copy-start | bytes 786436
  73.5 0.9 copy-start.16
  80.1 15.0 %collective-permute-start.8 = (bf16[1,256,1024]{2,1,0:T(8,128)(2,1)}, bf16[1,256,1024]{2,1,0:T(8,128)(2,1)}, u32[]{:S(2)}, u32[]{:S(2)}) collective-permute-start(bf16[1,256,1024]{2,1,0:T(8,128)(2,1)} %fusion.23), channel_id=1, source_target_pairs={{0,2},{1,3},{2,0},{3,1},{4,6},{5,7},{6,4},{7,5},{8,10},{9,11},{10,... | collective-permute-start | bytes 1572872 | tf_op jit(solution)/shard_map/ppermute | solution.py:102
  90.9 1.0 copy-start.8
  90.9 1.0 copy-start.18
  90.9 1.8 %copy-start.26 = (f32[2,256,256,4]{2,1,3,0:T(8,128)S(1)}, f32[2,256,256,4]{2,1,3,0:T(8,128)}, u32[]{:S(2)}) copy-start(f32[2,256,256,4]{2,1,3,0:T(8,128)} %copy-done.25) | copy-start | bytes 6291460
  90.9 1.8 %copy-start.28 = (f32[2,4,256]{2,1,0:T(4,128)S(1)}, f32[2,4,256]{2,1,0:T(4,128)}, u32[]{:S(2)}) copy-start(f32[2,4,256]{2,1,0:T(4,128)} %copy-done.27) | copy-start | bytes 24580
  92.7 1.6 %copy-start.14 = (bf16[4096,256]{1,0:T(8,128)(2,1)S(1)}, bf16[4096,256]{1,0:T(8,128)(2,1)}, u32[]{:S(2)}) copy-start(bf16[4096,256]{1,0:T(8,128)(2,1)} %param.13) | copy-start | bytes 6291460
  94.3 1.0 copy-start.6
  95.1 3.5 %copy-start.1 = (f32[256,4096]{1,0:T(8,128)}, f32[256,4096]{1,0:T(8,128)S(1)}, u32[]{:S(2)}) copy-start(f32[256,4096]{1,0:T(8,128)S(1)} %convolution_add_fusion) | copy-start | bytes 12582916
  98.4 0.7 copy-start.23
  98.7 2.9 %collective-permute-start.9 = (bf16[2,256,1024]{2,1,0:T(8,128)(2,1)S(1)}, bf16[2,256,1024]{2,1,0:T(8,128)(2,1)}, u32[]{:S(2)}, u32[]{:S(2)}) collective-permute-start(bf16[2,256,1024]{2,1,0:T(8,128)(2,1)S(1)} %pad_maximum_fusion.1), channel_id=1, source_target_pairs={{0,1},{1,0},{2,3},{3,2},{4,5},{5,4},{6,7},{7,6},{8,9},{9,8},{10,11... | collective-permute-start | bytes 3145736 | tf_op jit(solution)/shard_map/ppermute | solution.py:104
  102.6 23.4 %all-to-all-start = ((bf16[8,32,1024]{2,1,0:T(8,128)(2,1)}), bf16[8,32,1024]{2,1,0:T(8,128)(2,1)S(1)}, u32[]{:S(2)}, u32[]{:S(2)}) async-start(bf16[8,32,1024]{2,1,0:T(8,128)(2,1)} %copy.112), calls=%async_computation | async-start | bytes 1048576 | tf_op jit(solution)/shard_map/all_to_all | solution.py:281
  107.8 3.3 %copy-start.4 = (bf16[256,4096]{1,0:T(8,128)(2,1)S(1)}, bf16[256,4096]{1,0:T(8,128)(2,1)}, u32[]{:S(2)}) copy-start(bf16[256,4096]{1,0:T(8,128)(2,1)} %all-gather.3.cloned.1.call-done) | copy-start | bytes 6291460
  109.5 13.9 %copy-start.5 = (bf16[8,32,1024]{2,1,0:T(8,128)(2,1)S(1)}, bf16[8,32,1024]{2,1,0:T(8,128)(2,1)}, u32[]{:S(2)}) copy-start(bf16[8,32,1024]{2,1,0:T(8,128)(2,1)} %copy.98) | copy-start | bytes 1572868
  109.5 13.9 %dynamic-slice-start = ((f32[4096]{0:T(1024)}, s32[]{:T(128)}), f32[1024]{0:T(1024)S(1)}, s32[]{:S(2)}) async-start(f32[4096]{0:T(1024)} %param.10, s32[]{:T(128)} %select_n.110), calls=%async_computation.5 | async-start | bytes 8704 | tf_op jit(solution)/shard_map/dynamic_slice | solution.py:142
  109.5 13.9 %copy-start.20 = (f32[256]{0:T(256)S(1)}, f32[256]{0:T(256)}, u32[]{:S(2)}) copy-start(f32[256]{0:T(256)} %get-tuple-element.48) | copy-start | bytes 3076
  109.5 13.9 %copy-start.22 = (f32[256]{0:T(256)S(1)}, f32[256]{0:T(256)}, u32[]{:S(2)}) copy-start(f32[256]{0:T(256)} %copy-done.21) | copy-start | bytes 3076
  109.5 13.8 %collective-permute-start.10 = (bf16[1,256,1024]{2,1,0:T(8,128)(2,1)S(1)}, bf16[1,256,1024]{2,1,0:T(8,128)(2,1)S(1)}, u32[]{:S(2)}, u32[]{:S(2)}) collective-permute-start(bf16[1,256,1024]{2,1,0:T(8,128)(2,1)S(1)} %fusion.24), channel_id=1, source_target_pairs={{0,2},{1,3},{2,0},{3,1},{4,6},{5,7},{6,4},{7,5},{8,10},{9,11},{10,... | collective-permute-start | bytes 1572872 | tf_op jit(solution)/shard_map/ppermute | solution.py:104
  113.9 1.2 collective-permute-start.11
  115.1 8.2 %collective-permute-start.12 = (f32[256]{0:T(256)S(1)}, f32[256]{0:T(256)S(1)}, u32[]{:S(2)}, u32[]{:S(2)}) collective-permute-start(f32[256]{0:T(256)S(1)} %add.200), channel_id=1, source_target_pairs={{0,2},{1,3},{2,0},{3,1},{4,6},{5,7},{6,4},{7,5},{8,10},{9,11},{10,... | collective-permute-start | bytes 3080 | tf_op jit(solution)/shard_map/ppermute | solution.py:104
Sparse Core Ops, SparseCore 0:
  9.6 25.2 all-gather.2
  36.5 22.5 all-gather.4

commit v13 on v12

--- a/solution.py
+++ b/solution.py
@@ -78,7 +78,7 @@
     return jnp.concatenate(blocks, axis=1)
 
 
-def scatter_features(partial, axis_name, size, position, extra=None, ties=()):
+def scatter_features(partial, axis_name, size, position, extra=None, ties=(), pieces=1):
     width = partial.shape[1] // size
     if not _is_pow2(size):
         summed = lax.psum_scatter(
@@ -98,11 +98,21 @@
         keep = [i for i, m in enumerate(masks) if not m & bit]
         send = [i for i, m in enumerate(masks) if m & bit]
         outgoing = jnp.stack([held[i] for i in send]).astype(jnp.bfloat16)
-        if extra is None:
+        if pieces > 1 and bit == size >> 1:
+            step = outgoing.shape[1] // pieces
+            incoming = jnp.concatenate(
+                [
+                    lax.ppermute(
+                        outgoing[:, k * step : (k + 1) * step], axis_name, _xor_pairs(size, bit)
+                    )
+                    for k in range(pieces)
+                ],
+                axis=1,
+            )
+        else:
             incoming = lax.ppermute(outgoing, axis_name, _xor_pairs(size, bit))
-        else:
-            incoming, extra_in = lax.ppermute((outgoing, extra), axis_name, _xor_pairs(size, bit))
-            extra = extra + extra_in
+        if extra is not None:
+            extra = extra + lax.ppermute(extra, axis_name, _xor_pairs(size, bit))
         if ties:
             incoming, first = lax.optimization_barrier((incoming, ties[0]))
             ties = ties[1:]
@@ -276,7 +286,13 @@
         "dj,jrw->drw", send_table, home_blocks, preferred_element_type=jnp.float32
     ).astype(jnp.bfloat16)
     normed_gradient, stat_sum, (outgoing,) = scatter_features(
-        normed_partial, "tensor", tensor_size, tensor_index, extra=stat_partial, ties=(outgoing,)
+        normed_partial,
+        "tensor",
+        tensor_size,
+        tensor_index,
+        extra=stat_partial,
+        ties=(outgoing,),
+        pieces=2,
     )
     relaid = lax.all_to_all(outgoing, "dp", split_axis=0, concat_axis=0, tiled=True).reshape(
         token_row_count, width_part

time: 135 us -> 135 us (level)
  starting transfers between devices: 21.3 us -> 22.9 us
  waiting for transfers between devices: 14.8 us -> 13.4 us
    ppermute x4, waiting for transfers between devices: 10.9 us -> 7.28 us  [the longest x2 7.28 us: scatter_features(): extra = extra + lax.ppermute(extra, axis_name, _xor_pairs(size, bit))]
    ppermute x2 -> x3, waiting for transfers between devices: 0.01 us -> 2.16 us  [scatter_features(): incoming = lax.ppermute(outgoing, axis_name, _xor_pairs(size, bit))]
  transfers between devices with their start and end apart: 16 -> 17, of which waited for: 5 -> 5; matrix products, arithmetic and copies ran while one was open for 43% -> 43% of each run, Pallas kernels for 0% -> 0%
where the time goes in v13:
time: 135 us; the launch traced here: 134 us
  matrix products  34.6 us (26%)
  local copies, waits for them, and re-layouts  25.3 us (19%)
  starting transfers between devices  22.9 us (17%)
  other arithmetic  22.7 us (17%)
  between operations  14.8 us (11%)
  waiting for transfers between devices  13.4 us (10%)
    ppermute x7, starting transfers between devices, per_device(): returned.append(lax.ppermute(piece, 'dp', pairs))  12.5 us
    unnamed x69, local copies, waits for them, and re-layouts  12 us
    dot_general x1, matrix products, per_device(): lax.dot_general(grad_full, w_out, (((1,), (1,)), ((), ())), preferred_ele...  7.42 us
    ppermute x2, waiting for transfers between devices, scatter_features(): extra = extra + lax.ppermute(extra, axis_name, _xor_pairs(size, bit))  7.28 us
    dot_general x1, matrix products, per_device(): jnp.dot(normed_input, w_query, preferred_element_type=jnp.float32)  6.67 us
    dot_general x1, matrix products, per_device(): lax.dot_general(grad_query.reshape(token_row_count, query_width), w_query...  5.75 us
    another operation x8, local copies, waits for them, and re-layouts, per_device(): returned = jnp.stack(returned)  5.59 us
    all_to_all x1, starting transfers between devices, per_device(): lax.all_to_all(outgoing, 'dp', split_axis=0, concat_axis=0, tiled=True)  5.16 us
  transfers between devices with their start and end apart: 17, of which 5 were waited for; matrix products, arithmetic and copies ran while one was open for 43% of the time, Pallas kernels for 0%

profile of v13, /device:TPU:0, one launch (start us, length us, event | category | flops | bytes accessed | tf_op | source)
XLA Modules:
  0.0 133.7 jit_solution(5920795878669407290)
XLA Ops:
  7.2 0.7 all-gather.3.cloned.1.call-update
  8.1 1.1 dynamic-slice_bitcast_fusion
  9.2 6.0 %collective-permute-start.6 = (bf16[32,1024]{1,0:T(8,128)(2,1)S(1)}, bf16[32,1024]{1,0:T(8,128)(2,1)S(1)}, u32[]{:S(2)}, u32[]{:S(2)}) collective-permute-start(bf16[32,1024]{1,0:T(8,128)(2,1)S(1)} %get-tuple-element.38), channel_id=1, source_target_pairs={{0,28},{4,0},{8,4},{12,8},{16,12},{20,16},{24,20},{28,24},{1,29},{... | collective-permute-start | bytes 196616 | tf_op jit(solution)/shard_map/ppermute | solution.py:169
  15.2 0.4 collective-permute-start.5
  15.7 3.0 %collective-permute-start.3 = (bf16[32,1024]{1,0:T(8,128)(2,1)S(1)}, bf16[32,1024]{1,0:T(8,128)(2,1)S(1)}, u32[]{:S(2)}, u32[]{:S(2)}) collective-permute-start(bf16[32,1024]{1,0:T(8,128)(2,1)S(1)} %get-tuple-element.41), channel_id=1, source_target_pairs={{0,16},{4,20},{8,24},{12,28},{16,0},{20,4},{24,8},{28,12},{1,17},{... | collective-permute-start | bytes 196616 | tf_op jit(solution)/shard_map/ppermute | solution.py:169
  18.7 0.8 reduce-window.8
  19.6 0.5 multiply_cosine_fusion
  20.2 0.7 fusion.31
  21.0 1.9 %collective-permute-start.1 = (bf16[32,1024]{1,0:T(8,128)(2,1)S(1)}, bf16[32,1024]{1,0:T(8,128)(2,1)S(1)}, u32[]{:S(2)}, u32[]{:S(2)}) collective-permute-start(bf16[32,1024]{1,0:T(8,128)(2,1)S(1)} %get-tuple-element.43), channel_id=1, source_target_pairs={{0,8},{4,12},{8,16},{12,20},{16,24},{20,28},{24,0},{28,4},{1,9},{5... | collective-permute-start | bytes 196616 | tf_op jit(solution)/shard_map/ppermute | solution.py:169
  22.9 1.1 collective-permute-start
  24.0 1.2 and_select_fusion
  25.7 2.9 %collective-permute-done.2 = bf16[32,1024]{1,0:T(8,128)(2,1)S(1)} collective-permute-done((bf16[32,1024]{1,0:T(8,128)(2,1)S(1)}, bf16[32,1024]{1,0:T(8,128)(2,1)S(1)}, u32[]{:S(2)}, u32[]{:S(2)}) %collective-permute-start.2) | collective-permute-done | bytes 65568 | tf_op jit(solution)/shard_map/ppermute | solution.py:169
  28.6 0.7 copy.93
  29.3 0.8 copy.92
  30.1 0.8 copy.91
  30.8 2.9 %stack.58 = bf16[8,32,1024]{2,0,1:T(8,128)(2,1)S(1)} concatenate(bf16[1,32,1024]{2,0,1:T(2,128)(2,1)S(1)} %copy.132, bf16[1,32,1024]{2,0,1:T(2,128)(2,1)} %copy.91, bf16[1,32,1024]{2,0,1:T(2,128)(2,1)} %copy.92, bf16[1,32,1024]{2,0,1:T(2,128)(2,1)} %copy.93, bf16[1,32,1024]{2,0,1:T(2,128)(2,1)S(1)} %copy.94, bf16[1,32,1024]{2,0,1:T(2,128)(2,1)S(1)} %copy.95, ...), dimensions={0} | concatenate | bytes 1048576 | tf_op jit(solution)/shard_map/stack | solution.py:170
  34.1 1.1 copy.98
  35.3 2.2 %fusion = f32[256]{0:T(256)S(1)} fusion(bf16[256,4096]{1,0:T(8,128)(2,1)} %all-gather.3.cloned.1.call-done), kind=kLoop, calls=%fused_computation.5 | loop fusion | flops 3145472 | bytes 2098176 | tf_op jit(solution)/shard_map/reduce_sum | solution.py:193
  37.5 0.6 multiply_multiply_fusion
  38.2 1.2 fusion.47
  39.6 6.7 %convolution_bitcast_fusion = f32[32,8,8,128]{3,1,2,0:T(8,128)S(1)} fusion(bf16[4096,1024]{1,0:T(8,128)(2,1)} %param.11, bf16[256,4096]{1,0:T(8,128)(2,1)} %all-gather.3.cloned.1.call-done, f32[4096]{0:T(1024)S(1)} %copy-done.19, f32[256]{0:T(256)S(1)} %get-tuple-element.51), kind=kOutput, calls=%fused_computation.16 | convolution fusion | flops 2151677952 | bytes 11551744 | tf_op jit(solution)/shard_map/dot_general | solution.py:195
  46.5 0.5 subtract_convert_fusion.1
  47.3 0.6 copy-done.9
  48.1 0.9 fusion.7
  49.1 0.7 copy-done.13
  49.8 1.2 convolution_convert_fusion.4
  51.2 0.7 convolution_convert_fusion.1
  51.8 1.0 slice-done
  52.8 1.4 %slice-done.1 = s8[4194304]{0:T(1024)(128)(4,1)S(1)} async-done(((s8[8388608]{0:T(1024)(128)(4,1)}), s8[4194304]{0:T(1024)(128)(4,1)S(1)}, s32[]{:S(2)}) %slice-start.1) | async-done | bytes 4194328
  54.3 4.5 %fusion.56 = f32[256,4096]{1,0:T(8,128)} fusion(bf16[256,1024]{0,1:T(8,128)(2,1)S(1)} %bitcast.169, bf16[1024,4096]{1,0:T(8,128)(2,1)S(1)} %bitcast.165), kind=kOutput, calls=%fused_computation.116 | convolution fusion | flops 2147483648 | bytes 13107200 | tf_op jit(solution)/shard_map/dot_general | solution.py:223
  59.1 1.7 %fusion.19 = (bf16[1,256,1024]{2,1,0:T(8,128)(2,1)S(1)}, bf16[1,256,1024]{2,1,0:T(8,128)(2,1)S(1)}) fusion(f32[256,4096]{1,0:T(8,128)} %fusion.56, s32[]{:T(128)S(6)} %select_n.111, s32[]{:T(128)S(6)} %select_n.112), kind=kLoop, calls=%fused_computation.54 | loop fusion | bytes 2097160 | tf_op jit(solution)/shard_map/stack | solution.py:100
  60.8 1.1 pad_maximum_fusion
  62.1 7.4 %convolution_convert_fusion = bf16[256,1024]{1,0:T(8,128)(2,1)} fusion(bf16[256,4096]{1,0:T(8,128)(2,1)} %all-gather.5.cloned.1.call-done, bf16[1024,4096]{1,0:T(8,128)(2,1)} %param.14), kind=kOutput, calls=%fused_computation.19 | convolution fusion | flops 2147745792 | bytes 11010048 | tf_op jit(solution)/shard_map/dot_general | solution.py:226
  69.6 1.2 copy.99
  71.0 2.5 %fusion.5 = bf16[2,4,256,256]{2,3,1,0:T(8,128)(2,1)S(1)} fusion(bf16[256,2,128,1]{0,2,3,1:T(8,128)(2,1)} %bitcast.194, bf16[256,2,4,128]{0,3,2,1:T(8,128)(2,1)S(1)} %bitcast.171, f32[2,4,256]{2,1,0:T(4,128)S(1)} %bitcast.190, f32[2,4,256]{2,1,0:T(4,128)} %copy-done.27, f32[2,256,256,4]{2,1,3,0:T(8,128)} %copy-done.25, pred[256,256]{0,1:T(8,128)(4,1)} %fusion.31), kind=kOutput, calls=%fused_computation.11 | convolution fusion | flops 137363456 | bytes 3883008 | tf_op jit(solution)/shard_map/qkgd,skd->kgqs/dot_general | solution.py:240
  73.5 0.5 fusion.9
  74.1 0.4 copy-done.16
  74.4 0.4 convolution_multiply_fusion
  74.9 1.1 fusion.53
  76.3 1.5 %copy.134 = f32[256,8,64]{2,1,0:T(8,128)S(1)} copy(f32[256,8,64]{0,2,1:T(8,128)} %get-tuple-element.30) | data formatting | bytes 1048576
  77.8 2.3 %fusion.23 = bf16[1,256,1024]{2,1,0:T(8,128)(2,1)} fusion(f32[256,4096]{1,0:T(8,128)} %fusion.56, s32[]{:T(128)S(6)} %select_n.113, bf16[2,256,1024]{2,1,0:T(8,128)(2,1)} %collective-permute-done.7), kind=kLoop, calls=%fused_computation.58 | loop fusion | flops 786432 | bytes 2097156 | tf_op jit(solution)/shard_map/convert_element_type | solution.py:100
  80.1 0.9 collective-permute-start.8
  81.0 2.4 %copy.133 = f32[256,8,64]{2,1,0:T(8,128)} copy(f32[256,8,64]{0,2,1:T(8,128)} %get-tuple-element.31) | data formatting | bytes 1048576
  83.4 1.5 %add_convert_fusion = (bf16[256,8,64]{2,1,0:T(8,128)(2,1)S(1)}, bf16[256,8,64]{2,1,0:T(8,128)(2,1)S(1)}) fusion(f32[256,8,64]{2,1,0:T(8,128)S(1)} %copy.134, f32[256,8,64]{2,1,0:T(8,128)} %copy.133, f32[256,64]{1,0:T(8,128)S(1)} %get-tuple-element.49, f32[256,64]{1,0:T(8,128)S(1)} %get-tuple-element.48), kind=kLoop, calls=%fused_computation.48 | loop fusion | flops 1048576 | bytes 1703936 | tf_op jit(solution)/shard_map/convert.12
  85.2 5.8 %fusion.25 = f32[256,4096]{1,0:T(8,128)S(1)} fusion(bf16[4096,1024]{1,0:T(8,128)(2,1)} %param.11, bf16[32,8,8,128]{3,2,1,0:T(8,128)(2,1)S(1)} %bitcast.178), kind=kOutput, calls=%fused_computation.60 | convolution fusion | flops 2147483648 | bytes 13107200 | tf_op jit(solution)/shard_map/dot_general | solution.py:263
  91.0 0.8 convolution_add_fusion.1
  92.0 0.7 copy-done.26
  92.7 0.7 fusion.10
  93.4 0.9 copy-done.14
  94.3 0.8 convolution_add_fusion
  95.4 3.1 %fusion.11 = bf16[256,1024]{1,0:T(8,128)(2,1)S(1)} fusion(bf16[256,1024]{1,0:T(8,128)(2,1)S(1)} %copy-done.6, f32[256,4096]{1,0:T(8,128)} %fusion.56, s32[]{:T(128)} %select_n.110, bf16[1,256,1024]{2,1,0:T(8,128)(2,1)} %collective-permute-done.8, bf16[2,256,1024]{2,1,0:T(8,128)(2,1)} %collective-permute-done.7), kind=kLoop, calls=%fused_computation.29 | loop fusion | flops 1835008 | bytes 3145732 | tf_op jit(solution)/shard_map/convert_element_type | solution.py:235
  99.0 0.4 convolution_convert_fusion.2
  99.4 2.2 %collective-permute-done.9 = bf16[2,256,1024]{2,1,0:T(8,128)(2,1)} collective-permute-done((bf16[2,256,1024]{2,1,0:T(8,128)(2,1)S(1)}, bf16[2,256,1024]{2,1,0:T(8,128)(2,1)}, u32[]{:S(2)}, u32[]{:S(2)}) %collective-permute-start.9) | collective-permute-done | bytes 1048608 | tf_op jit(solution)/shard_map/ppermute | solution.py:113
  101.6 1.1 copy.112
  102.7 5.2 %all-to-all-start = ((bf16[8,32,1024]{2,1,0:T(8,128)(2,1)}), bf16[8,32,1024]{2,1,0:T(8,128)(2,1)S(1)}, u32[]{:S(2)}, u32[]{:S(2)}) async-start(bf16[8,32,1024]{2,1,0:T(8,128)(2,1)} %copy.112), calls=%async_computation | async-start | bytes 1048576 | tf_op jit(solution)/shard_map/all_to_all | solution.py:297
  107.8 1.7 %fusion.24 = bf16[1,256,1024]{2,1,0:T(8,128)(2,1)S(1)} fusion(f32[256,4096]{1,0:T(8,128)} %copy-done.1, s32[]{:T(128)S(6)} %select_n.113, bf16[2,256,1024]{2,1,0:T(8,128)(2,1)} %collective-permute-done.9), kind=kLoop, calls=%fused_computation.59 | loop fusion | flops 786432 | bytes 2097156 | tf_op jit(solution)/shard_map/convert_element_type | solution.py:100
  109.6 1.5 %collective-permute-start.10 = (bf16[1,128,1024]{2,1,0:T(8,128)(2,1)S(1)}, bf16[1,128,1024]{2,1,0:T(8,128)(2,1)S(1)}, u32[]{:S(2)}, u32[]{:S(2)}) collective-permute-start(bf16[1,128,1024]{2,1,0:T(8,128)(2,1)S(1)} %get-tuple-element.34), channel_id=1, source_target_pairs={{0,2},{1,3},{2,0},{3,1},{4,6},{5,7},{6,4},{7,5},{8,10},{9,11},{10,... | collective-permute-start | bytes 786440 | tf_op jit(solution)/shard_map/ppermute | solution.py:105
  111.1 0.6 collective-permute-start.11
  111.7 2.8 %fusion.3 = f32[256]{0:T(256)S(1)} fusion(bf16[256,4096]{1,0:T(8,128)(2,1)S(1)} %copy-done.4, f32[256,4096]{1,0:T(8,128)} %copy-done.1, f32[4096]{0:T(1024)S(1)} %copy-done.19), kind=kLoop, calls=%fused_computation.8 | loop fusion | flops 4194048 | bytes 6308864 | tf_op jit(solution)/shard_map/reduce_sum | solution.py:283
  114.6 1.1 collective-permute-done.12
  115.7 1.5 %collective-permute-start.13 = (f32[256]{0:T(256)S(1)}, f32[256]{0:T(256)S(1)}, u32[]{:S(2)}, u32[]{:S(2)}) collective-permute-start(f32[256]{0:T(256)S(1)} %add.200), channel_id=1, source_target_pairs={{0,2},{1,3},{2,0},{3,1},{4,6},{5,7},{6,4},{7,5},{8,10},{9,11},{10,... | collective-permute-start | bytes 3080 | tf_op jit(solution)/shard_map/ppermute | solution.py:115
  117.2 6.2 %collective-permute-done.13 = f32[256]{0:T(256)S(1)} collective-permute-done((f32[256]{0:T(256)S(1)}, f32[256]{0:T(256)S(1)}, u32[]{:S(2)}, u32[]{:S(2)}) %collective-permute-start.13) | collective-permute-done | bytes 1056 | tf_op jit(solution)/shard_map/ppermute | solution.py:115
  123.4 2.6 %fusion.14 = bf16[256,1024]{1,0:T(8,128)(2,1)} fusion(bf16[256,1024]{1,0:T(8,128)(2,1)S(1)} %copy-done.6, f32[256,4096]{1,0:T(8,128)} %copy-done.1, s32[]{:T(128)} %select_n.110, bf16[1,128,1024]{2,1,0:T(8,128)(2,1)S(1)} %collective-permute-done.11, bf16[1,128,1024]{2,1,0:T(8,128)(2,1)S(1)} %collective-permute-done.10, f32[256]{0:T(256)S(1)} %add_multiply_fusion, ...), kind=kLoop, calls=%fused_computation.32 | loop fusion | flops 4456448 | bytes 3677188 | tf_op jit(solution)/shard_map/convert_element_type | solution.py:307
  126.0 0.8 copy.144
  (105 shorter events, 4.9 us)
Async XLA Ops:
  7.2 31.0 %copy-start = (bf16[4096,256]{1,0:T(8,128)(2,1)S(1)}, bf16[4096,256]{1,0:T(8,128)(2,1)}, u32[]{:S(2)}) copy-start(bf16[4096,256]{1,0:T(8,128)(2,1)} %param.12) | copy-start | bytes 6291460
  7.2 28.1 %all-gather.3.cloned.1.call-start = ((), (), s32[]{:S(2)}) async-start(), calls=%async_computation.1 | async-start | bytes 2621440 | tf_op jit(solution)/shard_map/all_gather | solution.py:191
  7.9 51.2 %all-gather.5.cloned.1.call-start = ((), (), s32[]{:S(2)}) async-start(), calls=%async_computation.2 | async-start | bytes 2621440 | tf_op jit(solution)/shard_map/all_gather | solution.py:224
  9.2 11.8 %collective-permute-start.6 = (bf16[32,1024]{1,0:T(8,128)(2,1)S(1)}, bf16[32,1024]{1,0:T(8,128)(2,1)S(1)}, u32[]{:S(2)}, u32[]{:S(2)}) collective-permute-start(bf16[32,1024]{1,0:T(8,128)(2,1)S(1)} %get-tuple-element.38), channel_id=1, source_target_pairs={{0,28},{4,0},{8,4},{12,8},{16,12},{20,16},{24,20},{28,24},{1,29},{... | collective-permute-start | bytes 196616 | tf_op jit(solution)/shard_map/ppermute | solution.py:169
  15.2 7.7 %collective-permute-start.5 = (bf16[32,1024]{1,0:T(8,128)(2,1)S(1)}, bf16[32,1024]{1,0:T(8,128)(2,1)S(1)}, u32[]{:S(2)}, u32[]{:S(2)}) collective-permute-start(bf16[32,1024]{1,0:T(8,128)(2,1)S(1)} %get-tuple-element.39), channel_id=1, source_target_pairs={{0,24},{4,28},{8,0},{12,4},{16,8},{20,12},{24,16},{28,20},{1,25},{... | collective-permute-start | bytes 196616 | tf_op jit(solution)/shard_map/ppermute | solution.py:169
  15.7 9.8 %collective-permute-start.4 = (bf16[32,1024]{1,0:T(8,128)(2,1)S(1)}, bf16[32,1024]{1,0:T(8,128)(2,1)S(1)}, u32[]{:S(2)}, u32[]{:S(2)}) collective-permute-start(bf16[32,1024]{1,0:T(8,128)(2,1)S(1)} %get-tuple-element.40), channel_id=1, source_target_pairs={{0,20},{4,24},{8,28},{12,0},{16,4},{20,8},{24,12},{28,16},{1,21},{... | collective-permute-start | bytes 196616 | tf_op jit(solution)/shard_map/ppermute | solution.py:169
  15.7 9.9 %collective-permute-start.3 = (bf16[32,1024]{1,0:T(8,128)(2,1)S(1)}, bf16[32,1024]{1,0:T(8,128)(2,1)S(1)}, u32[]{:S(2)}, u32[]{:S(2)}) collective-permute-start(bf16[32,1024]{1,0:T(8,128)(2,1)S(1)} %get-tuple-element.41), channel_id=1, source_target_pairs={{0,16},{4,20},{8,24},{12,28},{16,0},{20,4},{24,8},{28,12},{1,17},{... | collective-permute-start | bytes 196616 | tf_op jit(solution)/shard_map/ppermute | solution.py:169
  18.7 9.9 %collective-permute-start.2 = (bf16[32,1024]{1,0:T(8,128)(2,1)S(1)}, bf16[32,1024]{1,0:T(8,128)(2,1)S(1)}, u32[]{:S(2)}, u32[]{:S(2)}) collective-permute-start(bf16[32,1024]{1,0:T(8,128)(2,1)S(1)} %get-tuple-element.42), channel_id=1, source_target_pairs={{0,12},{4,16},{8,20},{12,24},{16,28},{20,0},{24,4},{28,8},{1,13},{... | collective-permute-start | bytes 196616 | tf_op jit(solution)/shard_map/ppermute | solution.py:169
  21.0 8.3 %collective-permute-start.1 = (bf16[32,1024]{1,0:T(8,128)(2,1)S(1)}, bf16[32,1024]{1,0:T(8,128)(2,1)S(1)}, u32[]{:S(2)}, u32[]{:S(2)}) collective-permute-start(bf16[32,1024]{1,0:T(8,128)(2,1)S(1)} %get-tuple-element.43), channel_id=1, source_target_pairs={{0,8},{4,12},{8,16},{12,20},{16,24},{20,28},{24,0},{28,4},{1,9},{5... | collective-permute-start | bytes 196616 | tf_op jit(solution)/shard_map/ppermute | solution.py:169
  22.9 7.2 %collective-permute-start = (bf16[32,1024]{1,0:T(8,128)(2,1)S(1)}, bf16[32,1024]{1,0:T(8,128)(2,1)S(1)}, u32[]{:S(2)}, u32[]{:S(2)}) collective-permute-start(bf16[32,1024]{1,0:T(8,128)(2,1)S(1)} %get-tuple-element.44), channel_id=1, source_target_pairs={{0,4},{4,8},{8,12},{12,16},{16,20},{20,24},{24,28},{28,0},{1,5},{5... | collective-permute-start | bytes 196616 | tf_op jit(solution)/shard_map/ppermute | solution.py:169
  34.1 4.0 %copy-start.19 = (f32[4096]{0:T(1024)S(1)}, f32[4096]{0:T(1024)}, u32[]{:S(2)}) copy-start(f32[4096]{0:T(1024)} %param.10) | copy-start | bytes 49156
  35.3 2.9 %copy-start.2 = (bf16[256,4096]{1,0:T(8,128)(2,1)S(1)}, bf16[256,4096]{1,0:T(8,128)(2,1)}, u32[]{:S(2)}) copy-start(bf16[256,4096]{1,0:T(8,128)(2,1)} %all-gather.3.cloned.1.call-done) | copy-start | bytes 6291460
  38.1 10.8 %copy-start.21 = (f32[256]{0:T(256)}, f32[256]{0:T(256)S(1)}, u32[]{:S(2)}) copy-start(f32[256]{0:T(256)S(1)} %get-tuple-element.51) | copy-start | bytes 3076
  47.0 1.1 copy-start.17
  47.1 0.8 copy-start.9
  47.2 0.9 copy-start.11
  47.2 1.9 %copy-start.3 = (bf16[256,4096]{1,0:T(8,128)(2,1)S(1)}, bf16[256,4096]{1,0:T(8,128)(2,1)}, u32[]{:S(2)}) copy-start(bf16[256,4096]{1,0:T(8,128)(2,1)} %all-gather.3.cloned.1.call-done) | copy-start | bytes 6291460
  47.2 2.6 %copy-start.13 = (bf16[4096,256]{1,0:T(8,128)(2,1)S(1)}, bf16[4096,256]{1,0:T(8,128)(2,1)}, u32[]{:S(2)}) copy-start(bf16[4096,256]{1,0:T(8,128)(2,1)} %param.13) | copy-start | bytes 6291460
  47.3 3.7 %copy-start.15 = (bf16[256,2,64]{2,0,1:T(8,128)(2,1)}, bf16[256,2,64]{2,0,1:T(8,128)(2,1)S(1)}, u32[]{:S(2)}) copy-start(bf16[256,2,64]{2,0,1:T(8,128)(2,1)S(1)} %get-tuple-element.33) | copy-start | bytes 196612
  49.8 1.4 %copy-start.25 = (f32[2,256,256,4]{2,1,3,0:T(8,128)}, f32[2,256,256,4]{2,1,3,0:T(8,128)S(1)}, u32[]{:S(2)}) copy-start(f32[2,256,256,4]{2,1,3,0:T(8,128)S(1)} %get-tuple-element.53) | copy-start | bytes 6291460
  49.8 1.4 %copy-start.27 = (f32[2,4,256]{2,1,0:T(4,128)}, f32[2,4,256]{2,1,0:T(4,128)S(1)}, u32[]{:S(2)}) copy-start(f32[2,4,256]{2,1,0:T(4,128)S(1)} %get-tuple-element.52) | copy-start | bytes 24580
  49.8 3.0 %slice-start = ((s8[8388608]{0:T(1024)(128)(4,1)}), s8[4194304]{0:T(1024)(128)(4,1)S(1)}, s32[]{:S(2)}) async-start(s8[8388608]{0:T(1024)(128)(4,1)} %bitcast.164), calls=%async_computation.3 | async-start | bytes 8388608
  51.0 0.8 copy-start.24
  51.2 3.1 %slice-start.1 = ((s8[8388608]{0:T(1024)(128)(4,1)}), s8[4194304]{0:T(1024)(128)(4,1)S(1)}, s32[]{:S(2)}) async-start(s8[8388608]{0:T(1024)(128)(4,1)} %bitcast.164), calls=%async_computation.4 | async-start | bytes 8388608
  61.9 7.7 %collective-permute-start.7 = (bf16[2,256,1024]{2,1,0:T(8,128)(2,1)}, bf16[2,256,1024]{2,1,0:T(8,128)(2,1)}, u32[]{:S(2)}, u32[]{:S(2)}) collective-permute-start(bf16[2,256,1024]{2,1,0:T(8,128)(2,1)} %pad_maximum_fusion), channel_id=1, source_target_pairs={{0,1},{1,0},{2,3},{3,2},{4,5},{5,4},{6,7},{7,6},{8,9},{9,8},{10,11... | collective-permute-start | bytes 3145736 | tf_op jit(solution)/shard_map/ppermute | solution.py:113
  70.8 2.7 %copy-start.7 = (bf16[256,1024]{0,1:T(8,128)(2,1)}, bf16[256,1024]{0,1:T(8,128)(2,1)S(1)}, u32[]{:S(2)}) copy-start(bf16[256,1024]{0,1:T(8,128)(2,1)S(1)} %copy.99) | copy-start | bytes 1572868
  71.0 2.5 %copy-start.10 = (bf16[256,8,64]{2,0,1:T(8,128)(2,1)S(1)}, bf16[256,8,64]{2,0,1:T(8,128)(2,1)}, u32[]{:S(2)}) copy-start(bf16[256,8,64]{2,0,1:T(8,128)(2,1)} %copy-done.9) | copy-start | bytes 786436
  71.0 2.5 %copy-start.12 = (bf16[256,8,64]{2,0,1:T(8,128)(2,1)S(1)}, bf16[256,8,64]{2,0,1:T(8,128)(2,1)}, u32[]{:S(2)}) copy-start(bf16[256,8,64]{2,0,1:T(8,128)(2,1)} %copy-done.11) | copy-start | bytes 786436
  73.5 0.9 copy-start.16
  80.1 15.0 %collective-permute-start.8 = (bf16[1,256,1024]{2,1,0:T(8,128)(2,1)}, bf16[1,256,1024]{2,1,0:T(8,128)(2,1)}, u32[]{:S(2)}, u32[]{:S(2)}) collective-permute-start(bf16[1,256,1024]{2,1,0:T(8,128)(2,1)} %fusion.23), channel_id=1, source_target_pairs={{0,2},{1,3},{2,0},{3,1},{4,6},{5,7},{6,4},{7,5},{8,10},{9,11},{10,... | collective-permute-start | bytes 1572872 | tf_op jit(solution)/shard_map/ppermute | solution.py:113
  90.9 1.0 copy-start.8
  91.0 1.0 copy-start.18
  91.0 1.8 %copy-start.26 = (f32[2,256,256,4]{2,1,3,0:T(8,128)S(1)}, f32[2,256,256,4]{2,1,3,0:T(8,128)}, u32[]{:S(2)}) copy-start(f32[2,256,256,4]{2,1,3,0:T(8,128)} %copy-done.25) | copy-start | bytes 6291460
  91.0 1.8 %copy-start.28 = (f32[2,4,256]{2,1,0:T(4,128)S(1)}, f32[2,4,256]{2,1,0:T(4,128)}, u32[]{:S(2)}) copy-start(f32[2,4,256]{2,1,0:T(4,128)} %copy-done.27) | copy-start | bytes 24580
  92.7 1.6 %copy-start.14 = (bf16[4096,256]{1,0:T(8,128)(2,1)S(1)}, bf16[4096,256]{1,0:T(8,128)(2,1)}, u32[]{:S(2)}) copy-start(bf16[4096,256]{1,0:T(8,128)(2,1)} %param.13) | copy-start | bytes 6291460
  94.3 1.0 copy-start.6
  95.1 3.5 %copy-start.1 = (f32[256,4096]{1,0:T(8,128)}, f32[256,4096]{1,0:T(8,128)S(1)}, u32[]{:S(2)}) copy-start(f32[256,4096]{1,0:T(8,128)S(1)} %convolution_add_fusion) | copy-start | bytes 12582916
  98.4 0.6 copy-start.23
  98.7 2.9 %collective-permute-start.9 = (bf16[2,256,1024]{2,1,0:T(8,128)(2,1)S(1)}, bf16[2,256,1024]{2,1,0:T(8,128)(2,1)}, u32[]{:S(2)}, u32[]{:S(2)}) collective-permute-start(bf16[2,256,1024]{2,1,0:T(8,128)(2,1)S(1)} %pad_maximum_fusion.1), channel_id=1, source_target_pairs={{0,1},{1,0},{2,3},{3,2},{4,5},{5,4},{6,7},{7,6},{8,9},{9,8},{10,11... | collective-permute-start | bytes 3145736 | tf_op jit(solution)/shard_map/ppermute | solution.py:113
  102.7 23.4 %all-to-all-start = ((bf16[8,32,1024]{2,1,0:T(8,128)(2,1)}), bf16[8,32,1024]{2,1,0:T(8,128)(2,1)S(1)}, u32[]{:S(2)}, u32[]{:S(2)}) async-start(bf16[8,32,1024]{2,1,0:T(8,128)(2,1)} %copy.112), calls=%async_computation | async-start | bytes 1048576 | tf_op jit(solution)/shard_map/all_to_all | solution.py:297
  107.8 3.9 %copy-start.4 = (bf16[256,4096]{1,0:T(8,128)(2,1)S(1)}, bf16[256,4096]{1,0:T(8,128)(2,1)}, u32[]{:S(2)}) copy-start(bf16[256,4096]{1,0:T(8,128)(2,1)} %all-gather.3.cloned.1.call-done) | copy-start | bytes 6291460
  109.6 13.8 %collective-permute-start.10 = (bf16[1,128,1024]{2,1,0:T(8,128)(2,1)S(1)}, bf16[1,128,1024]{2,1,0:T(8,128)(2,1)S(1)}, u32[]{:S(2)}, u32[]{:S(2)}) collective-permute-start(bf16[1,128,1024]{2,1,0:T(8,128)(2,1)S(1)} %get-tuple-element.34), channel_id=1, source_target_pairs={{0,2},{1,3},{2,0},{3,1},{4,6},{5,7},{6,4},{7,5},{8,10},{9,11},{10,... | collective-permute-start | bytes 786440 | tf_op jit(solution)/shard_map/ppermute | solution.py:105
  111.1 12.3 %copy-start.5 = (bf16[8,32,1024]{2,1,0:T(8,128)(2,1)S(1)}, bf16[8,32,1024]{2,1,0:T(8,128)(2,1)}, u32[]{:S(2)}) copy-start(bf16[8,32,1024]{2,1,0:T(8,128)(2,1)} %copy.98) | copy-start | bytes 1572868
  111.1 12.3 %dynamic-slice-start = ((f32[4096]{0:T(1024)}, s32[]{:T(128)}), f32[1024]{0:T(1024)S(1)}, s32[]{:S(2)}) async-start(f32[4096]{0:T(1024)} %param.10, s32[]{:T(128)} %select_n.110), calls=%async_computation.5 | async-start | bytes 8704 | tf_op jit(solution)/shard_map/dynamic_slice | solution.py:152
  111.1 12.3 %copy-start.20 = (f32[256]{0:T(256)S(1)}, f32[256]{0:T(256)}, u32[]{:S(2)}) copy-start(f32[256]{0:T(256)} %get-tuple-element.50) | copy-start | bytes 3076
  111.1 12.3 %copy-start.22 = (f32[256]{0:T(256)S(1)}, f32[256]{0:T(256)}, u32[]{:S(2)}) copy-start(f32[256]{0:T(256)} %copy-done.21) | copy-start | bytes 3076
  111.1 12.3 %collective-permute-start.11 = (bf16[1,128,1024]{2,1,0:T(8,128)(2,1)S(1)}, bf16[1,128,1024]{2,1,0:T(8,128)(2,1)S(1)}, u32[]{:S(2)}, u32[]{:S(2)}) collective-permute-start(bf16[1,128,1024]{2,1,0:T(8,128)(2,1)S(1)} %get-tuple-element.35), channel_id=1, source_target_pairs={{0,2},{1,3},{2,0},{3,1},{4,6},{5,7},{6,4},{7,5},{8,10},{9,11},{10,... | collective-permute-start | bytes 786440 | tf_op jit(solution)/shard_map/ppermute | solution.py:105
  114.5 1.2 collective-permute-start.12
  115.7 7.6 %collective-permute-start.13 = (f32[256]{0:T(256)S(1)}, f32[256]{0:T(256)S(1)}, u32[]{:S(2)}, u32[]{:S(2)}) collective-permute-start(f32[256]{0:T(256)S(1)} %add.200), channel_id=1, source_target_pairs={{0,2},{1,3},{2,0},{3,1},{4,6},{5,7},{6,4},{7,5},{8,10},{9,11},{10,... | collective-permute-start | bytes 3080 | tf_op jit(solution)/shard_map/ppermute | solution.py:115
Sparse Core Ops, SparseCore 0:
  9.6 25.2 all-gather.2
  36.5 22.5 all-gather.4

commit v14 on v12

--- a/solution.py
+++ b/solution.py
@@ -149,36 +149,14 @@
 
     home_rows = token_row_count // block_count
     owned_blocks = grad_output.reshape(block_count, home_rows, width_part)
-    if sources <= 16:
-        returned = [lax.dynamic_index_in_dim(owned_blocks, data_index, 0, keepdims=False)]
-        for shift in range(1, sources):
-            pairs = [(a, (a + shift) % sources) for a in range(sources)]
-            piece = lax.dynamic_index_in_dim(
-                owned_blocks, (data_index + shift) % sources, 0, keepdims=False
-            )
-            returned.append(lax.ppermute(piece, "dp", pairs))
-        returned = jnp.stack(returned)
-        came_over = (
-            ((data_index - owner_row) % sources)[:, None] == slot_index[None, :]
-        ).astype(jnp.bfloat16)
-        grad_home = (
-            jnp.einsum("js,srw->jrw", came_over, returned, preferred_element_type=jnp.float32)
-            .astype(jnp.bfloat16)
-            .reshape(token_row_count, width_part)
-        )
-    else:
-        arrived = lax.all_to_all(
-            owned_blocks.reshape(block_count, -1), "dp", split_axis=0, concat_axis=0, tiled=True
-        )
-        grad_home = (
-            lax.dot_general(
-                send_table, arrived, (((0,), (0,)), ((), ())), preferred_element_type=jnp.float32
-            )
-            .astype(jnp.bfloat16)
-            .reshape(token_row_count, width_part)
-        )
-
-    gathered = lax.all_gather(tokens, "tensor", axis=1, tiled=True)
+    arrived = lax.all_to_all(owned_blocks, "dp", split_axis=0, concat_axis=0, tiled=True)
+    grad_home = (
+        jnp.einsum("dj,drw->jrw", send_table, arrived, preferred_element_type=jnp.float32)
+        .astype(jnp.bfloat16)
+        .reshape(token_row_count, width_part)
+    )
+
+    gathered = gather_features(tokens, "tensor", tensor_size, tensor_index)
     gathered_float = gathered.astype(jnp.float32)
     inverse = lax.rsqrt(jnp.mean(gathered_float * gathered_float, axis=1) + NORM_EPSILON)
     normed_input = (gathered_float * inverse[:, None] * norm_gain[None, :]).astype(jnp.bfloat16)

time: 135 us -> 146 us (1.081)
  between operations: 14.8 us -> 22.3 us
  other arithmetic: 22.8 us -> 25.3 us
  waiting for transfers between devices: 14.8 us -> 17.3 us
  starting transfers between devices: 21.3 us -> 19 us
    ppermute x7 -> x2, starting transfers between devices: 12.5 us -> 3.03 us  [gather_features(): incoming = lax.ppermute(held, axis_name, _xor_pairs(size, bit))]
    all_to_all x0 -> x1, starting transfers between devices: none -> 5.81 us  [per_device(): lax.all_to_all(owned_blocks, 'dp', split_axis=0, concat_axis=0, tiled=True)]
    another operation x10 -> x2, local copies, waits for them, and re-layouts: 5.73 us -> 0.14 us  [the longest x8 5.59 us: per_device(): returned = jnp.stack(returned)]
    concatenate x0 -> x2, other arithmetic: none -> 3.84 us  [gather_features(): held = jnp.concatenate([held, incoming], axis=0)]
    ppermute x7 -> x2, waiting for transfers between devices: 2.83 us -> 6.37 us  [gather_features(): incoming = lax.ppermute(held, axis_name, _xor_pairs(size, bit))]
    unnamed x69 -> x88, local copies, waits for them, and re-layouts: 12 us -> 15.5 us
    reduce_sum x1, other arithmetic: 2.23 us -> 0.5 us  [per_device(): jnp.mean(gathered_float * gathered_float, axis=1) + NORM_EPSILON]
  transfers between devices with their start and end apart: 16 -> 11, of which waited for: 5 -> 4; matrix products, arithmetic and copies ran while one was open for 43% -> 40% of each run, Pallas kernels for 0% -> 0%
where the time goes in v14:
time: 146 us; the launch traced here: 145 us
  matrix products  34.7 us (24%)
  local copies, waits for them, and re-layouts  26.6 us (18%)
  other arithmetic  25.3 us (17%)
  between operations  22.3 us (15%)
  starting transfers between devices  19 us (13%)
  waiting for transfers between devices  17.3 us (12%)
    unnamed x88, local copies, waits for them, and re-layouts  15.5 us
    ppermute x4, waiting for transfers between devices, scatter_features(): lax.ppermute((outgoing, extra), axis_name, _xor_pairs(size, bit))  10.9 us
    dot_general x1, matrix products, per_device(): lax.dot_general(grad_full, w_out, (((1,), (1,)), ((), ())), preferred_ele...  7.39 us
    dot_general x1, matrix products, per_device(): jnp.dot(normed_input, w_query, preferred_element_type=jnp.float32)  6.82 us
    ppermute x2, waiting for transfers between devices, gather_features(): incoming = lax.ppermute(held, axis_name, _xor_pairs(size, bit))  6.37 us
    all_to_all x1, starting transfers between devices, per_device(): lax.all_to_all(owned_blocks, 'dp', split_axis=0, concat_axis=0, tiled=True)  5.81 us
    dot_general x1, matrix products, per_device(): lax.dot_general(grad_query.reshape(token_row_count, query_width), w_query...  5.79 us
    all_to_all x1, starting transfers between devices, per_device(): lax.all_to_all(outgoing, 'dp', split_axis=0, concat_axis=0, tiled=True)  5.72 us
  transfers between devices with their start and end apart: 11, of which 4 were waited for; matrix products, arithmetic and copies ran while one was open for 40% of the time, Pallas kernels for 0%

profile of v14, /device:TPU:0, one launch (start us, length us, event | category | flops | bytes accessed | tf_op | source)
XLA Modules:
  0.0 145.3 jit_solution(15774452710769416486)
XLA Ops:
  7.2 3.0 %collective-permute-start = (bf16[1,256,1024]{2,1,0:T(8,128)(2,1)}, bf16[1,256,1024]{2,1,0:T(8,128)(2,1)}, u32[]{:S(2)}, u32[]{:S(2)}) collective-permute-start(bf16[1,256,1024]{2,1,0:T(8,128)(2,1)} %bitcast.154), channel_id=1, source_target_pairs={{0,2},{1,3},{2,0},{3,1},{4,6},{5,7},{6,4},{7,5},{8,10},{9,11},{10,... | collective-permute-start | bytes 1572872 | tf_op jit(solution)/shard_map/ppermute | solution.py:69
  10.2 5.8 %all-to-all-start = ((bf16[8,32,1024]{2,1,0:T(8,128)(2,1)}), bf16[8,32,1024]{2,1,0:T(8,128)(2,1)S(1)}, u32[]{:S(2)}, u32[]{:S(2)}) async-start(bf16[8,32,1024]{2,1,0:T(8,128)(2,1)} %bitcast.168), calls=%async_computation | async-start | bytes 1048576 | tf_op jit(solution)/shard_map/all_to_all | solution.py:152
  16.1 6.4 %collective-permute-done = bf16[1,256,1024]{2,1,0:T(8,128)(2,1)} collective-permute-done((bf16[1,256,1024]{2,1,0:T(8,128)(2,1)}, bf16[1,256,1024]{2,1,0:T(8,128)(2,1)}, u32[]{:S(2)}, u32[]{:S(2)}) %collective-permute-start) | collective-permute-done | bytes 524320 | tf_op jit(solution)/shard_map/ppermute | solution.py:69
  22.5 2.3 %pad_maximum_fusion.2 = bf16[2,256,1024]{2,1,0:T(8,128)(2,1)} fusion(bf16[1,256,1024]{2,1,0:T(8,128)(2,1)} %collective-permute-done, bf16[1,256,1024]{2,1,0:T(8,128)(2,1)} %bitcast.155), kind=kLoop, calls=%fused_computation.35 | loop fusion | flops 524288 | bytes 2097152 | tf_op jit(solution)/shard_map/concatenate | solution.py:70
  24.7 0.7 fusion.41
  25.4 1.4 fusion.53
  31.9 0.8 reduce-window.8
  35.4 0.7 fusion.32
  36.1 0.5 multiply_cosine_fusion
  36.6 0.4 convolution_convert_fusion.3
  37.1 1.1 copy.82
  38.2 1.6 %pad_maximum_fusion = bf16[4,256,1024]{2,1,0:T(8,128)(2,1)S(1)} fusion(bf16[2,256,1024]{2,1,0:T(8,128)(2,1)} %collective-permute-done.1, bf16[1,256,1024]{2,1,0:T(8,128)(2,1)} %collective-permute-done, bf16[1,256,1024]{2,1,0:T(8,128)(2,1)S(1)} %bitcast.156), kind=kLoop, calls=%fused_computation.9 | loop fusion | flops 2097152 | bytes 4194304 | tf_op jit(solution)/shard_map/concatenate | solution.py:70
  40.0 0.5 fusion
  40.5 0.6 multiply_multiply_fusion
  41.1 1.2 fusion.46
  42.3 0.7 fusion.52
  43.0 1.8 %copy.117 = f32[256,2,64]{2,0,1:T(8,128)} copy(f32[256,2,64]{0,2,1:T(8,128)} %get-tuple-element.38) | data formatting | bytes 262144
  44.8 0.8 copy.116
  45.6 6.8 %convolution_bitcast_fusion = f32[32,8,8,128]{3,1,2,0:T(8,128)S(1)} fusion(bf16[4096,1024]{1,0:T(8,128)(2,1)} %param.12, f32[4096]{0:T(1024)S(1)} %copy-done.27, f32[256]{0:T(256)} %copy-done.29, bf16[256,1024]{1,0:T(8,128)(2,1)} %copy-done.4, bf16[256,1024]{1,0:T(8,128)(2,1)} %copy-done.6, bf16[256,1024]{1,0:T(8,128)(2,1)} %copy-done.8, ...), kind=kOutput, calls=%fused_computation.18 | convolution fusion | flops 2159017984 | bytes 11551744 | tf_op jit(solution)/shard_map/dot_general | solution.py:163
  52.7 0.5 subtract_convert_fusion.1
  53.5 0.6 copy-done.12
  54.4 0.9 fusion.7
  55.3 0.5 copy-done.16
  55.8 1.1 convolution_convert_fusion.4
  57.1 0.7 convolution_convert_fusion.1
  57.8 0.8 copy-done.10
  58.6 0.7 slice-done.1
  59.3 4.4 %fusion.54 = f32[256,4096]{1,0:T(8,128)} fusion(bf16[256,1024]{0,1:T(8,128)(2,1)S(1)} %bitcast.159, bf16[1024,4096]{1,0:T(8,128)(2,1)S(1)} %bitcast.152), kind=kOutput, calls=%fused_computation.109 | convolution fusion | flops 2147483648 | bytes 13107200 | tf_op jit(solution)/shard_map/dot_general | solution.py:191
  63.6 1.7 %fusion.19 = (bf16[1,256,1024]{2,1,0:T(8,128)(2,1)S(1)}, bf16[1,256,1024]{2,1,0:T(8,128)(2,1)S(1)}) fusion(f32[256,4096]{1,0:T(8,128)} %fusion.54, s32[]{:T(128)S(6)} %select_n.65, s32[]{:T(128)S(6)} %select_n.66), kind=kLoop, calls=%fused_computation.57 | loop fusion | bytes 2097160 | tf_op jit(solution)/shard_map/stack | solution.py:100
  65.3 1.1 pad_maximum_fusion.3
  66.4 0.4 collective-permute-start.2
  66.8 7.4 %convolution_convert_fusion = bf16[256,1024]{1,0:T(8,128)(2,1)} fusion(bf16[256,4096]{1,0:T(8,128)(2,1)} %all-gather.2.cloned.1.call-done, bf16[1024,4096]{1,0:T(8,128)(2,1)} %param.15), kind=kOutput, calls=%fused_computation.21 | convolution fusion | flops 2147745792 | bytes 11010048 | tf_op jit(solution)/shard_map/dot_general | solution.py:194
  74.2 2.1 %copy.83 = bf16[256,1024]{0,1:T(8,128)(2,1)} copy(bf16[256,1024]{1,0:T(8,128)(2,1)} %convolution_convert_fusion) | data formatting | bytes 1048576 | tf_op jit(solution)/shard_map/optimization_barrier | solution.py:107
  76.3 1.4 multiply_reduce_fusion
  77.7 2.6 %fusion.5 = bf16[2,4,256,256]{2,3,1,0:T(8,128)(2,1)S(1)} fusion(bf16[256,2,128,1]{0,2,3,1:T(8,128)(2,1)} %bitcast.176, bf16[256,2,4,128]{0,3,2,1:T(8,128)(2,1)} %bitcast.160, f32[2,4,256]{2,1,0:T(4,128)S(1)} %bitcast.172, f32[2,4,256]{2,1,0:T(4,128)} %copy-done.37, f32[2,256,256,4]{2,1,3,0:T(8,128)} %copy-done.35, pred[256,256]{0,1:T(8,128)(4,1)} %fusion.32), kind=kOutput, calls=%fused_computation.13 | convolution fusion | flops 137363456 | bytes 3883008 | tf_op jit(solution)/shard_map/qkgd,skd->kgqs/dot_general | solution.py:208
  80.3 0.5 fusion.9
  80.8 0.4 convolution_multiply_fusion
  81.2 1.1 fusion.51
  82.6 0.8 copy.93
  83.4 2.4 %copy.119 = f32[256,8,64]{2,1,0:T(8,128)} copy(f32[256,8,64]{0,2,1:T(8,128)} %get-tuple-element.32) | data formatting | bytes 1048576
  85.8 2.3 %fusion.23 = bf16[1,256,1024]{2,1,0:T(8,128)(2,1)} fusion(f32[256,4096]{1,0:T(8,128)} %fusion.54, s32[]{:T(128)S(6)} %select_n.67, bf16[2,256,1024]{2,1,0:T(8,128)(2,1)} %collective-permute-done.2), kind=kLoop, calls=%fused_computation.61 | loop fusion | flops 786432 | bytes 2097156 | tf_op jit(solution)/shard_map/convert_element_type | solution.py:100
  88.1 1.7 %collective-permute-start.3 = (bf16[1,256,1024]{2,1,0:T(8,128)(2,1)}, bf16[1,256,1024]{2,1,0:T(8,128)(2,1)}, u32[]{:S(2)}, u32[]{:S(2)}) collective-permute-start(bf16[1,256,1024]{2,1,0:T(8,128)(2,1)} %fusion.23), channel_id=1, source_target_pairs={{0,2},{1,3},{2,0},{3,1},{4,6},{5,7},{6,4},{7,5},{8,10},{9,11},{10,... | collective-permute-start | bytes 1572872 | tf_op jit(solution)/shard_map/ppermute | solution.py:102
  89.8 2.4 %copy.118 = f32[256,8,64]{2,1,0:T(8,128)} copy(f32[256,8,64]{0,2,1:T(8,128)} %get-tuple-element.33) | data formatting | bytes 1048576
  92.2 1.8 %add_convert_fusion = (bf16[256,8,64]{2,1,0:T(8,128)(2,1)S(1)}, bf16[256,8,64]{2,1,0:T(8,128)(2,1)S(1)}) fusion(f32[256,8,64]{2,1,0:T(8,128)} %copy.119, f32[256,8,64]{2,1,0:T(8,128)} %copy.118, f32[256,64]{1,0:T(8,128)S(1)} %get-tuple-element.41, f32[256,64]{1,0:T(8,128)S(1)} %get-tuple-element.40), kind=kLoop, calls=%fused_computation.51 | loop fusion | flops 1048576 | bytes 1703936 | tf_op jit(solution)/shard_map/convert.12
  94.4 5.8 %fusion.25 = f32[256,4096]{1,0:T(8,128)S(1)} fusion(bf16[4096,1024]{1,0:T(8,128)(2,1)} %param.12, bf16[32,8,8,128]{3,2,1,0:T(8,128)(2,1)S(1)} %bitcast.167), kind=kOutput, calls=%fused_computation.63 | convolution fusion | flops 2147483648 | bytes 13107200 | tf_op jit(solution)/shard_map/dot_general | solution.py:231
  100.2 0.8 convolution_add_fusion.1
  101.2 0.7 copy-done.36
  102.0 0.7 fusion.10
  102.6 0.9 copy-done.17
  103.6 0.8 convolution_add_fusion
  104.4 3.3 %fusion.11 = bf16[256,1024]{1,0:T(8,128)(2,1)S(1)} fusion(bf16[256,1024]{1,0:T(8,128)(2,1)S(1)} %copy-done.2, f32[256,4096]{1,0:T(8,128)} %fusion.54, s32[]{:T(128)} %select_n.64, bf16[1,256,1024]{2,1,0:T(8,128)(2,1)} %collective-permute-done.3, bf16[2,256,1024]{2,1,0:T(8,128)(2,1)} %collective-permute-done.2), kind=kLoop, calls=%fused_computation.31 | loop fusion | flops 1835008 | bytes 3145732 | tf_op jit(solution)/shard_map/convert_element_type | solution.py:203
  108.1 0.4 convolution_convert_fusion.2
  108.5 2.2 %collective-permute-done.4 = bf16[2,256,1024]{2,1,0:T(8,128)(2,1)S(1)} collective-permute-done((bf16[2,256,1024]{2,1,0:T(8,128)(2,1)S(1)}, bf16[2,256,1024]{2,1,0:T(8,128)(2,1)S(1)}, u32[]{:S(2)}, u32[]{:S(2)}) %collective-permute-start.4) | collective-permute-done | bytes 1048608 | tf_op jit(solution)/shard_map/ppermute | solution.py:104
  110.7 1.0 copy-done.18
  111.7 1.1 copy.96
  112.8 5.7 %all-to-all-start.1 = ((bf16[8,32,1024]{2,1,0:T(8,128)(2,1)}), bf16[8,32,1024]{2,1,0:T(8,128)(2,1)}, u32[]{:S(2)}, u32[]{:S(2)}) async-start(bf16[8,32,1024]{2,1,0:T(8,128)(2,1)} %copy.96), calls=%async_computation.1 | async-start | bytes 1048576 | tf_op jit(solution)/shard_map/all_to_all | solution.py:259
  118.6 1.6 %fusion.24 = bf16[1,256,1024]{2,1,0:T(8,128)(2,1)S(1)} fusion(f32[256,4096]{1,0:T(8,128)} %copy-done.1, s32[]{:T(128)S(6)} %select_n.67, bf16[2,256,1024]{2,1,0:T(8,128)(2,1)} %copy-done.18), kind=kLoop, calls=%fused_computation.62 | loop fusion | flops 786432 | bytes 2097156 | tf_op jit(solution)/shard_map/convert_element_type | solution.py:100
  120.2 0.6 collective-permute-start.5
  120.8 3.0 %fusion.3 = f32[256]{0:T(256)S(1)} fusion(f32[256,4096]{1,0:T(8,128)} %copy-done.1, f32[4096]{0:T(1024)S(1)} %copy-done.27, bf16[256,1024]{1,0:T(8,128)(2,1)} %copy-done.4, bf16[256,1024]{1,0:T(8,128)(2,1)} %copy-done.6, bf16[256,1024]{1,0:T(8,128)(2,1)} %copy-done.8, bf16[256,1024]{1,0:T(8,128)(2,1)S(1)} %get-tuple-element.26), kind=kLoop, calls=%fused_computation.8 | loop fusion | flops 11534080 | bytes 6308864 | tf_op jit(solution)/shard_map/reduce_sum | solution.py:251
  123.8 1.1 collective-permute-done.6
  125.0 1.5 %collective-permute-start.7 = (f32[256]{0:T(256)S(1)}, f32[256]{0:T(256)S(1)}, u32[]{:S(2)}, u32[]{:S(2)}) collective-permute-start(f32[256]{0:T(256)S(1)} %add.135), channel_id=1, source_target_pairs={{0,2},{1,3},{2,0},{3,1},{4,6},{5,7},{6,4},{7,5},{8,10},{9,11},{10,... | collective-permute-start | bytes 3080 | tf_op jit(solution)/shard_map/ppermute | solution.py:104
  126.4 7.6 %collective-permute-done.7 = f32[256]{0:T(256)S(1)} collective-permute-done((f32[256]{0:T(256)S(1)}, f32[256]{0:T(256)S(1)}, u32[]{:S(2)}, u32[]{:S(2)}) %collective-permute-start.7) | collective-permute-done | bytes 1056 | tf_op jit(solution)/shard_map/ppermute | solution.py:104
  134.0 2.5 %fusion.14 = bf16[256,1024]{1,0:T(8,128)(2,1)} fusion(bf16[256,1024]{1,0:T(8,128)(2,1)S(1)} %copy-done.2, f32[256,4096]{1,0:T(8,128)} %copy-done.1, s32[]{:T(128)} %select_n.64, bf16[1,256,1024]{2,1,0:T(8,128)(2,1)S(1)} %collective-permute-done.5, f32[256]{0:T(256)S(1)} %add_multiply_fusion, f32[256]{0:T(256)S(1)} %copy-done.28, ...), kind=kLoop, calls=%fused_computation.34 | loop fusion | flops 3407872 | bytes 3677188 | tf_op jit(solution)/shard_map/convert_element_type | solution.py:269
  136.6 1.9 %copy.131 = bf16[256,1024]{1,0:T(8,128)(2,1)} copy(bf16[256,1024]{1,0:T(8,128)(2,1)} %bitcast.51) | data formatting | bytes 1048576
  (105 shorter events, 2.7 us)
Async XLA Ops:
  7.2 34.0 %copy-start = (bf16[4096,256]{1,0:T(8,128)(2,1)S(1)}, bf16[4096,256]{1,0:T(8,128)(2,1)}, u32[]{:S(2)}) copy-start(bf16[4096,256]{1,0:T(8,128)(2,1)} %param.13) | copy-start | bytes 6291460
  7.2 31.0 %copy-start.2 = (bf16[256,1024]{1,0:T(8,128)(2,1)S(1)}, bf16[256,1024]{1,0:T(8,128)(2,1)}, u32[]{:S(2)}) copy-start(bf16[256,1024]{1,0:T(8,128)(2,1)} %param.10) | copy-start | bytes 1572868
  7.2 15.3 %collective-permute-start = (bf16[1,256,1024]{2,1,0:T(8,128)(2,1)}, bf16[1,256,1024]{2,1,0:T(8,128)(2,1)}, u32[]{:S(2)}, u32[]{:S(2)}) collective-permute-start(bf16[1,256,1024]{2,1,0:T(8,128)(2,1)} %bitcast.154), channel_id=1, source_target_pairs={{0,2},{1,3},{2,0},{3,1},{4,6},{5,7},{6,4},{7,5},{8,10},{9,11},{10,... | collective-permute-start | bytes 1572872 | tf_op jit(solution)/shard_map/ppermute | solution.py:69
  10.2 26.4 %all-to-all-start = ((bf16[8,32,1024]{2,1,0:T(8,128)(2,1)}), bf16[8,32,1024]{2,1,0:T(8,128)(2,1)S(1)}, u32[]{:S(2)}, u32[]{:S(2)}) async-start(bf16[8,32,1024]{2,1,0:T(8,128)(2,1)} %bitcast.168), calls=%async_computation | async-start | bytes 1048576 | tf_op jit(solution)/shard_map/all_to_all | solution.py:152
  16.0 47.6 %all-gather.2.cloned.1.call-start = ((), (), s32[]{:S(2)}) async-start(), calls=%async_computation.2 | async-start | bytes 2621440 | tf_op jit(solution)/shard_map/all_gather | solution.py:192
  24.7 13.4 %collective-permute-start.1 = (bf16[2,256,1024]{2,1,0:T(8,128)(2,1)}, bf16[2,256,1024]{2,1,0:T(8,128)(2,1)}, u32[]{:S(2)}, u32[]{:S(2)}) collective-permute-start(bf16[2,256,1024]{2,1,0:T(8,128)(2,1)} %pad_maximum_fusion.2), channel_id=1, source_target_pairs={{0,1},{1,0},{2,3},{3,2},{4,5},{5,4},{6,7},{7,6},{8,9},{9,8},{10,11... | collective-permute-start | bytes 3145736 | tf_op jit(solution)/shard_map/ppermute | solution.py:69
  25.4 14.6 %copy-start.32 = (s32[8]{0:T(128)}, s32[8]{0:T(128)S(1)}, u32[]{:S(2)}) copy-start(s32[8]{0:T(128)S(1)} %fusion.41) | copy-start | bytes 100
  39.7 1.4 copy-start.27
  40.0 2.3 %copy-start.4 = (bf16[256,1024]{1,0:T(8,128)(2,1)}, bf16[256,1024]{1,0:T(8,128)(2,1)S(1)}, u32[]{:S(2)}) copy-start(bf16[256,1024]{1,0:T(8,128)(2,1)S(1)} %get-tuple-element.27) | copy-start | bytes 1572868
  40.0 2.3 %copy-start.6 = (bf16[256,1024]{1,0:T(8,128)(2,1)}, bf16[256,1024]{1,0:T(8,128)(2,1)S(1)}, u32[]{:S(2)}) copy-start(bf16[256,1024]{1,0:T(8,128)(2,1)S(1)} %get-tuple-element.28) | copy-start | bytes 1572868
  40.0 2.3 %copy-start.8 = (bf16[256,1024]{1,0:T(8,128)(2,1)}, bf16[256,1024]{1,0:T(8,128)(2,1)S(1)}, u32[]{:S(2)}) copy-start(bf16[256,1024]{1,0:T(8,128)(2,1)S(1)} %get-tuple-element.29) | copy-start | bytes 1572868
  41.1 1.2 copy-start.29
  52.4 1.0 copy-start.20
  52.4 1.0 copy-start.21
  52.4 1.9 %copy-start.25 = (pred[256,256]{0,1:T(8,128)(4,1)S(1)}, pred[256,256]{0,1:T(8,128)(4,1)}, u32[]{:S(2)}) copy-start(pred[256,256]{0,1:T(8,128)(4,1)} %fusion.32) | copy-start | bytes 196612
  53.2 2.1 %copy-start.5 = (bf16[256,1024]{1,0:T(8,128)(2,1)S(1)}, bf16[256,1024]{1,0:T(8,128)(2,1)}, u32[]{:S(2)}) copy-start(bf16[256,1024]{1,0:T(8,128)(2,1)} %copy-done.4) | copy-start | bytes 1572868
  53.2 2.1 %copy-start.7 = (bf16[256,1024]{1,0:T(8,128)(2,1)S(1)}, bf16[256,1024]{1,0:T(8,128)(2,1)}, u32[]{:S(2)}) copy-start(bf16[256,1024]{1,0:T(8,128)(2,1)} %copy-done.6) | copy-start | bytes 1572868
  53.2 2.1 %copy-start.9 = (bf16[256,1024]{1,0:T(8,128)(2,1)S(1)}, bf16[256,1024]{1,0:T(8,128)(2,1)}, u32[]{:S(2)}) copy-start(bf16[256,1024]{1,0:T(8,128)(2,1)} %copy-done.8) | copy-start | bytes 1572868
  53.2 2.6 %copy-start.16 = (bf16[4096,256]{1,0:T(8,128)(2,1)S(1)}, bf16[4096,256]{1,0:T(8,128)(2,1)}, u32[]{:S(2)}) copy-start(bf16[4096,256]{1,0:T(8,128)(2,1)} %param.14) | copy-start | bytes 6291460
  53.2 2.5 %copy-start.30 = (f32[256]{0:T(256)S(1)}, f32[256]{0:T(256)}, u32[]{:S(2)}) copy-start(f32[256]{0:T(256)} %copy-done.29) | copy-start | bytes 3076
  53.3 0.8 copy-start.12
  53.5 0.9 copy-start.14
  53.5 0.9 copy-start.22
  54.4 4.2 %slice-start = ((s8[8388608]{0:T(1024)(128)(4,1)}), s8[4194304]{0:T(1024)(128)(4,1)S(1)}, s32[]{:S(2)}) async-start(s8[8388608]{0:T(1024)(128)(4,1)} %bitcast.151), calls=%async_computation.3 | async-start | bytes 8388608
  55.8 1.4 copy-start.35
  55.8 1.4 copy-start.37
  55.8 3.5 %slice-start.1 = ((s8[8388608]{0:T(1024)(128)(4,1)}), s8[4194304]{0:T(1024)(128)(4,1)S(1)}, s32[]{:S(2)}) async-start(s8[8388608]{0:T(1024)(128)(4,1)} %bitcast.151), calls=%async_computation.4 | async-start | bytes 8388608
  56.9 0.9 copy-start.34
  57.8 0.8 copy-start.10
  66.4 7.8 %collective-permute-start.2 = (bf16[2,256,1024]{2,1,0:T(8,128)(2,1)}, bf16[2,256,1024]{2,1,0:T(8,128)(2,1)}, u32[]{:S(2)}, u32[]{:S(2)}) collective-permute-start(bf16[2,256,1024]{2,1,0:T(8,128)(2,1)} %pad_maximum_fusion.3), channel_id=1, source_target_pairs={{0,1},{1,0},{2,3},{3,2},{4,5},{5,4},{6,7},{7,6},{8,9},{9,8},{10,11... | collective-permute-start | bytes 3145736 | tf_op jit(solution)/shard_map/ppermute | solution.py:102
  77.7 2.6 %copy-start.13 = (bf16[256,8,64]{2,0,1:T(8,128)(2,1)S(1)}, bf16[256,8,64]{2,0,1:T(8,128)(2,1)}, u32[]{:S(2)}) copy-start(bf16[256,8,64]{2,0,1:T(8,128)(2,1)} %copy-done.12) | copy-start | bytes 786436
  77.7 2.6 %copy-start.15 = (bf16[256,8,64]{2,0,1:T(8,128)(2,1)S(1)}, bf16[256,8,64]{2,0,1:T(8,128)(2,1)}, u32[]{:S(2)}) copy-start(bf16[256,8,64]{2,0,1:T(8,128)(2,1)} %copy-done.14) | copy-start | bytes 786436
  77.7 3.1 %copy-start.23 = (bf16[256,2,64]{2,0,1:T(8,128)(2,1)S(1)}, bf16[256,2,64]{2,0,1:T(8,128)(2,1)}, u32[]{:S(2)}) copy-start(bf16[256,2,64]{2,0,1:T(8,128)(2,1)} %copy-done.22) | copy-start | bytes 196612
  88.1 16.3 %collective-permute-start.3 = (bf16[1,256,1024]{2,1,0:T(8,128)(2,1)}, bf16[1,256,1024]{2,1,0:T(8,128)(2,1)}, u32[]{:S(2)}, u32[]{:S(2)}) collective-permute-start(bf16[1,256,1024]{2,1,0:T(8,128)(2,1)} %fusion.23), channel_id=1, source_target_pairs={{0,2},{1,3},{2,0},{3,1},{4,6},{5,7},{6,4},{7,5},{8,10},{9,11},{10,... | collective-permute-start | bytes 1572872 | tf_op jit(solution)/shard_map/ppermute | solution.py:102
  94.4 5.8 %copy-start.24 = (bf16[256,2,128]{0,2,1:T(8,128)(2,1)S(1)}, bf16[256,2,128]{0,2,1:T(8,128)(2,1)}, u32[]{:S(2)}) copy-start(bf16[256,2,128]{0,2,1:T(8,128)(2,1)} %copy.93) | copy-start | bytes 393220
  100.2 1.0 copy-start.11
  100.2 1.0 copy-start.26
  100.2 1.8 %copy-start.36 = (f32[2,256,256,4]{2,1,3,0:T(8,128)S(1)}, f32[2,256,256,4]{2,1,3,0:T(8,128)}, u32[]{:S(2)}) copy-start(f32[2,256,256,4]{2,1,3,0:T(8,128)} %copy-done.35) | copy-start | bytes 6291460
  100.2 1.8 %copy-start.38 = (f32[2,4,256]{2,1,0:T(4,128)S(1)}, f32[2,4,256]{2,1,0:T(4,128)}, u32[]{:S(2)}) copy-start(f32[2,4,256]{2,1,0:T(4,128)} %copy-done.37) | copy-start | bytes 24580
  102.0 1.6 %copy-start.17 = (bf16[4096,256]{1,0:T(8,128)(2,1)S(1)}, bf16[4096,256]{1,0:T(8,128)(2,1)}, u32[]{:S(2)}) copy-start(bf16[4096,256]{1,0:T(8,128)(2,1)} %param.14) | copy-start | bytes 6291460
  104.3 4.1 %copy-start.1 = (f32[256,4096]{1,0:T(8,128)}, f32[256,4096]{1,0:T(8,128)S(1)}, u32[]{:S(2)}) copy-start(f32[256,4096]{1,0:T(8,128)S(1)} %convolution_add_fusion) | copy-start | bytes 12582916
  104.3 3.7 %copy-start.33 = (s32[8]{0:T(128)S(1)}, s32[8]{0:T(128)}, u32[]{:S(2)}) copy-start(s32[8]{0:T(128)} %copy-done.32) | copy-start | bytes 100
  108.0 2.7 %collective-permute-start.4 = (bf16[2,256,1024]{2,1,0:T(8,128)(2,1)S(1)}, bf16[2,256,1024]{2,1,0:T(8,128)(2,1)S(1)}, u32[]{:S(2)}, u32[]{:S(2)}) collective-permute-start(bf16[2,256,1024]{2,1,0:T(8,128)(2,1)S(1)} %pad_maximum_fusion.4), channel_id=1, source_target_pairs={{0,1},{1,0},{2,3},{3,2},{4,5},{5,4},{6,7},{7,6},{8,9},{9,8},{10,11... | collective-permute-start | bytes 3145736 | tf_op jit(solution)/shard_map/ppermute | solution.py:104
  110.7 1.0 copy-start.18
  112.8 23.8 %all-to-all-start.1 = ((bf16[8,32,1024]{2,1,0:T(8,128)(2,1)}), bf16[8,32,1024]{2,1,0:T(8,128)(2,1)}, u32[]{:S(2)}, u32[]{:S(2)}) async-start(bf16[8,32,1024]{2,1,0:T(8,128)(2,1)} %copy.96), calls=%async_computation.1 | async-start | bytes 1048576 | tf_op jit(solution)/shard_map/all_to_all | solution.py:259
  118.5 15.5 %copy-start.3 = (bf16[8,32,1024]{2,1,0:T(8,128)(2,1)S(1)}, bf16[8,32,1024]{2,1,0:T(8,128)(2,1)}, u32[]{:S(2)}) copy-start(bf16[8,32,1024]{2,1,0:T(8,128)(2,1)} %copy.82) | copy-start | bytes 1572868
  118.5 15.5 %copy-start.19 = (bf16[2,256,1024]{2,1,0:T(8,128)(2,1)S(1)}, bf16[2,256,1024]{2,1,0:T(8,128)(2,1)}, u32[]{:S(2)}) copy-start(bf16[2,256,1024]{2,1,0:T(8,128)(2,1)} %copy-done.18) | copy-start | bytes 3145732
  118.5 15.5 %dynamic-slice-start = ((f32[4096]{0:T(1024)}, s32[]{:T(128)}), f32[1024]{0:T(1024)S(1)}, s32[]{:S(2)}) async-start(f32[4096]{0:T(1024)} %param.11, s32[]{:T(128)} %select_n.64), calls=%async_computation.5 | async-start | bytes 8704 | tf_op jit(solution)/shard_map/dynamic_slice | solution.py:142
  118.5 15.5 %copy-start.28 = (f32[256]{0:T(256)S(1)}, f32[256]{0:T(256)}, u32[]{:S(2)}) copy-start(f32[256]{0:T(256)} %get-tuple-element.42) | copy-start | bytes 3076
  118.5 15.5 %copy-start.31 = (f32[256]{0:T(256)S(1)}, f32[256]{0:T(256)}, u32[]{:S(2)}) copy-start(f32[256]{0:T(256)} %copy-done.29) | copy-start | bytes 3076
  120.2 13.8 %collective-permute-start.5 = (bf16[1,256,1024]{2,1,0:T(8,128)(2,1)S(1)}, bf16[1,256,1024]{2,1,0:T(8,128)(2,1)S(1)}, u32[]{:S(2)}, u32[]{:S(2)}) collective-permute-start(bf16[1,256,1024]{2,1,0:T(8,128)(2,1)S(1)} %fusion.24), channel_id=1, source_target_pairs={{0,2},{1,3},{2,0},{3,1},{4,6},{5,7},{6,4},{7,5},{8,10},{9,11},{10,... | collective-permute-start | bytes 1572872 | tf_op jit(solution)/shard_map/ppermute | solution.py:104
  123.8 1.2 collective-permute-start.6
  125.0 9.0 %collective-permute-start.7 = (f32[256]{0:T(256)S(1)}, f32[256]{0:T(256)S(1)}, u32[]{:S(2)}, u32[]{:S(2)}) collective-permute-start(f32[256]{0:T(256)S(1)} %add.135), channel_id=1, source_target_pairs={{0,2},{1,3},{2,0},{3,1},{4,6},{5,7},{6,4},{7,5},{8,10},{9,11},{10,... | collective-permute-start | bytes 3080 | tf_op jit(solution)/shard_map/ppermute | solution.py:104
Sparse Core Ops, SparseCore 0:
  38.3 24.2 all-gather.1

commit v15 on v14

--- a/solution.py
+++ b/solution.py
@@ -148,6 +148,8 @@
     send_table = (owner_row[None, :] == slot_index[:, None]).astype(jnp.bfloat16)
 
     home_rows = token_row_count // block_count
+    gathered = gather_features(tokens, "tensor", tensor_size, tensor_index)
+    gathered, grad_output = lax.optimization_barrier((gathered, grad_output))
     owned_blocks = grad_output.reshape(block_count, home_rows, width_part)
     arrived = lax.all_to_all(owned_blocks, "dp", split_axis=0, concat_axis=0, tiled=True)
     grad_home = (
@@ -156,7 +158,6 @@
         .reshape(token_row_count, width_part)
     )
 
-    gathered = gather_features(tokens, "tensor", tensor_size, tensor_index)
     gathered_float = gathered.astype(jnp.float32)
     inverse = lax.rsqrt(jnp.mean(gathered_float * gathered_float, axis=1) + NORM_EPSILON)
     normed_input = (gathered_float * inverse[:, None] * norm_gain[None, :]).astype(jnp.bfloat16)

time: 146 us -> 160 us (1.096)
  waiting for transfers between devices: 17.3 us -> 35 us
  local copies, waits for them, and re-layouts: 26.6 us -> 22.4 us
    all_to_all x1, waiting for transfers between devices: 0.01 us -> 9.68 us  [per_device(): lax.all_to_all(owned_blocks, 'dp', split_axis=0, concat_axis=0, tiled=True)]
    ppermute x2, waiting for transfers between devices: 6.37 us -> 12.1 us  [gather_features(): incoming = lax.ppermute(held, axis_name, _xor_pairs(size, bit))]
    unnamed x88 -> x76, local copies, waits for them, and re-layouts: 15.5 us -> 11.8 us
    all_gather x1, waiting for transfers between devices: 0.01 us -> 1.64 us  [per_device(): grad_full = lax.all_gather(grad_home, 'tensor', axis=1, tiled=True)]
    ppermute x2, starting transfers between devices: 2.18 us -> 0.54 us  [scatter_features(): incoming = lax.ppermute(outgoing, axis_name, _xor_pairs(size, bit))]
  transfers between devices with their start and end apart: 11 -> 11, of which waited for: 4 -> 7; matrix products, arithmetic and copies ran while one was open for 40% -> 31% of each run, Pallas kernels for 0% -> 0%
where the time goes in v15:
time: 160 us; the launch traced here: 159 us
  matrix products  35.3 us (22%)
  waiting for transfers between devices  35 us (22%)
  other arithmetic  26.7 us (17%)
  local copies, waits for them, and re-layouts  22.4 us (14%)
  between operations  22.2 us (14%)
  starting transfers between devices  17.8 us (11%)
    ppermute x2, waiting for transfers between devices, gather_features(): incoming = lax.ppermute(held, axis_name, _xor_pairs(size, bit))  12.1 us
    unnamed x76, local copies, waits for them, and re-layouts  11.8 us
    ppermute x4, waiting for transfers between devices, scatter_features(): lax.ppermute((outgoing, extra), axis_name, _xor_pairs(size, bit))  10.9 us
    all_to_all x1, waiting for transfers between devices, per_device(): lax.all_to_all(owned_blocks, 'dp', split_axis=0, concat_axis=0, tiled=True)  9.68 us
    dot_general x1, matrix products, per_device(): lax.dot_general(grad_full, w_out, (((1,), (1,)), ((), ())), preferred_ele...  7.39 us
    dot_general x1, matrix products, per_device(): jnp.dot(normed_input, w_query, preferred_element_type=jnp.float32)  6.45 us
    all_to_all x1, starting transfers between devices, per_device(): lax.all_to_all(owned_blocks, 'dp', split_axis=0, concat_axis=0, tiled=True)  6.16 us
    dot_general x1, matrix products, per_device(): lax.dot_general(grad_query.reshape(token_row_count, query_width), w_query...  5.79 us
  transfers between devices with their start and end apart: 11, of which 7 were waited for; matrix products, arithmetic and copies ran while one was open for 31% of the time, Pallas kernels for 0%

profile of v15, /device:TPU:0, one launch (start us, length us, event | category | flops | bytes accessed | tf_op | source)
XLA Modules:
  0.0 159.3 jit_solution(11282244135893771739)
XLA Ops:
  7.2 3.0 %collective-permute-start = (bf16[1,256,1024]{2,1,0:T(8,128)(2,1)}, bf16[1,256,1024]{2,1,0:T(8,128)(2,1)S(1)}, u32[]{:S(2)}, u32[]{:S(2)}) collective-permute-start(bf16[1,256,1024]{2,1,0:T(8,128)(2,1)} %bitcast.154), channel_id=1, source_target_pairs={{0,2},{1,3},{2,0},{3,1},{4,6},{5,7},{6,4},{7,5},{8,10},{9,11},{10,... | collective-permute-start | bytes 1572872 | tf_op jit(solution)/shard_map/ppermute | solution.py:69
  10.2 12.1 %collective-permute-done = bf16[1,256,1024]{2,1,0:T(8,128)(2,1)S(1)} collective-permute-done((bf16[1,256,1024]{2,1,0:T(8,128)(2,1)}, bf16[1,256,1024]{2,1,0:T(8,128)(2,1)S(1)}, u32[]{:S(2)}, u32[]{:S(2)}) %collective-permute-start) | collective-permute-done | bytes 524320 | tf_op jit(solution)/shard_map/ppermute | solution.py:69
  22.4 2.1 %pad_maximum_fusion.2 = bf16[2,256,1024]{2,1,0:T(8,128)(2,1)} fusion(bf16[1,256,1024]{2,1,0:T(8,128)(2,1)S(1)} %collective-permute-done, bf16[1,256,1024]{2,1,0:T(8,128)(2,1)} %bitcast.155), kind=kLoop, calls=%fused_computation.35 | loop fusion | flops 524288 | bytes 2097152 | tf_op jit(solution)/shard_map/concatenate | solution.py:70
  24.5 0.7 fusion.53
  33.1 0.7 fusion.32
  33.8 0.5 multiply_cosine_fusion
  34.3 1.4 pad_maximum_fusion
  36.0 1.5 pad_maximum_fusion.1
  37.5 6.2 %all-to-all-start = ((bf16[8,32,1024]{2,1,0:T(8,128)(2,1)}), bf16[8,32,1024]{2,1,0:T(8,128)(2,1)S(1)}, u32[]{:S(2)}, u32[]{:S(2)}) async-start(bf16[8,32,1024]{2,1,0:T(8,128)(2,1)} %bitcast.169), calls=%async_computation | async-start | bytes 1048576 | tf_op jit(solution)/shard_map/all_to_all | solution.py:154
  43.7 0.8 fusion.41
  44.5 2.1 %fusion = f32[256]{0:T(256)S(1)} fusion(bf16[256,4096]{1,0:T(8,128)(2,1)} %pad_maximum_fusion.1), kind=kLoop, calls=%fused_computation.5 | loop fusion | flops 3145472 | bytes 2098176 | tf_op jit(solution)/shard_map/reduce_sum | solution.py:162
  46.6 0.6 multiply_multiply_fusion
  47.2 1.9 %fusion.46 = f32[256,256]{0,1:T(8,128)} fusion(bf16[4096,256]{1,0:T(8,128)(2,1)S(1)} %copy-done, bf16[256,4096]{1,0:T(8,128)(2,1)S(1)} %copy-done.2, f32[4096]{0:T(1024)S(1)} %copy-done.19, f32[256]{0:T(256)S(1)} %get-tuple-element.47), kind=kOutput, calls=%fused_computation.105 | convolution fusion | flops 541065216 | bytes 4473856 | tf_op jit(solution)/shard_map/dot_general | solution.py:165
  49.1 9.7 %all-to-all-done = bf16[8,32,1024]{2,1,0:T(8,128)(2,1)S(1)} async-done(((bf16[8,32,1024]{2,1,0:T(8,128)(2,1)}), bf16[8,32,1024]{2,1,0:T(8,128)(2,1)S(1)}, u32[]{:S(2)}, u32[]{:S(2)}) %all-to-all-start) | async-done | bytes 524320 | tf_op jit(solution)/shard_map/all_to_all | solution.py:154
  58.8 0.4 convolution_convert_fusion.3
  59.2 1.1 copy.82
  60.3 1.0 fusion.52
  61.6 6.4 %convolution_bitcast_fusion = f32[32,8,8,128]{3,1,2,0:T(8,128)S(1)} fusion(bf16[4096,1024]{1,0:T(8,128)(2,1)} %param.12, bf16[256,4096]{1,0:T(8,128)(2,1)} %pad_maximum_fusion.1, f32[4096]{0:T(1024)S(1)} %copy-done.19, f32[256]{0:T(256)} %copy-done.22), kind=kOutput, calls=%fused_computation.18 | convolution fusion | flops 2151677952 | bytes 11551744 | tf_op jit(solution)/shard_map/dot_general | solution.py:164
  68.3 0.5 subtract_convert_fusion.1
  69.1 0.6 copy-done.8
  69.9 0.9 fusion.7
  70.9 0.6 copy-done.12
  71.6 1.2 convolution_convert_fusion.4
  72.9 0.7 convolution_convert_fusion.1
  73.6 1.0 slice-done
  74.6 1.4 slice-done.1
  76.0 4.5 %fusion.54 = f32[256,4096]{1,0:T(8,128)} fusion(bf16[256,1024]{0,1:T(8,128)(2,1)S(1)} %bitcast.159, bf16[1024,4096]{1,0:T(8,128)(2,1)S(1)} %bitcast.152), kind=kOutput, calls=%fused_computation.109 | convolution fusion | flops 2147483648 | bytes 13107200 | tf_op jit(solution)/shard_map/dot_general | solution.py:192
  80.5 1.6 %all-gather.2.cloned.1.call-done = bf16[256,4096]{1,0:T(8,128)(2,1)} async-done(((bf16[256,1024]{1,0:T(8,128)(2,1)}), bf16[256,4096]{1,0:T(8,128)(2,1)}) %all-gather.2.cloned.1.call-update) | async-done | bytes 2097168 | tf_op jit(solution)/shard_map/all_gather | solution.py:193
  82.2 1.7 %fusion.19 = (bf16[1,256,1024]{2,1,0:T(8,128)(2,1)S(1)}, bf16[1,256,1024]{2,1,0:T(8,128)(2,1)S(1)}) fusion(f32[256,4096]{1,0:T(8,128)} %fusion.54, s32[]{:T(128)S(6)} %select_n.65, s32[]{:T(128)S(6)} %select_n.66), kind=kLoop, calls=%fused_computation.57 | loop fusion | bytes 2097160 | tf_op jit(solution)/shard_map/stack | solution.py:100
  83.9 1.1 pad_maximum_fusion.3
  85.2 7.4 %convolution_convert_fusion = bf16[256,1024]{1,0:T(8,128)(2,1)} fusion(bf16[256,4096]{1,0:T(8,128)(2,1)} %all-gather.2.cloned.1.call-done, bf16[1024,4096]{1,0:T(8,128)(2,1)} %param.15), kind=kOutput, calls=%fused_computation.21 | convolution fusion | flops 2147745792 | bytes 11010048 | tf_op jit(solution)/shard_map/dot_general | solution.py:195
  92.6 2.0 %copy.83 = bf16[256,1024]{0,1:T(8,128)(2,1)} copy(bf16[256,1024]{1,0:T(8,128)(2,1)} %convolution_convert_fusion) | data formatting | bytes 1048576 | tf_op jit(solution)/shard_map/optimization_barrier | solution.py:107
  94.7 1.2 multiply_reduce_fusion
  95.9 2.6 %fusion.5 = bf16[2,4,256,256]{2,3,1,0:T(8,128)(2,1)S(1)} fusion(bf16[256,2,128,1]{0,2,3,1:T(8,128)(2,1)} %bitcast.177, bf16[256,2,4,128]{0,3,2,1:T(8,128)(2,1)} %bitcast.160, f32[2,4,256]{2,1,0:T(4,128)S(1)} %bitcast.173, f32[2,4,256]{2,1,0:T(4,128)} %copy-done.31, f32[2,256,256,4]{2,1,3,0:T(8,128)} %copy-done.29, pred[256,256]{0,1:T(8,128)(4,1)} %fusion.32), kind=kOutput, calls=%fused_computation.13 | convolution fusion | flops 137363456 | bytes 3883008 | tf_op jit(solution)/shard_map/qkgd,skd->kgqs/dot_general | solution.py:209
  98.5 0.5 fusion.9
  99.0 0.4 copy-done.15
  99.4 0.4 convolution_multiply_fusion
  99.8 0.9 fusion.51
  101.0 0.8 copy.93
  101.7 2.4 %copy.119 = f32[256,8,64]{2,1,0:T(8,128)} copy(f32[256,8,64]{0,2,1:T(8,128)} %get-tuple-element.36) | data formatting | bytes 1048576
  104.1 2.3 %fusion.23 = bf16[1,256,1024]{2,1,0:T(8,128)(2,1)} fusion(f32[256,4096]{1,0:T(8,128)} %fusion.54, s32[]{:T(128)S(6)} %select_n.67, bf16[2,256,1024]{2,1,0:T(8,128)(2,1)} %collective-permute-done.2), kind=kLoop, calls=%fused_computation.61 | loop fusion | flops 786432 | bytes 2097156 | tf_op jit(solution)/shard_map/convert_element_type | solution.py:100
  106.4 0.3 collective-permute-start.3
  106.7 1.4 copy.118
  108.1 1.8 %add_convert_fusion = (bf16[256,8,64]{2,1,0:T(8,128)(2,1)S(1)}, bf16[256,8,64]{2,1,0:T(8,128)(2,1)S(1)}) fusion(f32[256,8,64]{2,1,0:T(8,128)} %copy.119, f32[256,8,64]{2,1,0:T(8,128)} %copy.118, f32[256,64]{1,0:T(8,128)S(1)} %get-tuple-element.45, f32[256,64]{1,0:T(8,128)S(1)} %get-tuple-element.44), kind=kLoop, calls=%fused_computation.51 | loop fusion | flops 1048576 | bytes 1703936 | tf_op jit(solution)/shard_map/convert.12
  110.2 5.8 %fusion.25 = f32[256,4096]{1,0:T(8,128)S(1)} fusion(bf16[4096,1024]{1,0:T(8,128)(2,1)} %param.12, bf16[32,8,8,128]{3,2,1,0:T(8,128)(2,1)S(1)} %bitcast.168), kind=kOutput, calls=%fused_computation.63 | convolution fusion | flops 2147483648 | bytes 13107200 | tf_op jit(solution)/shard_map/dot_general | solution.py:232
  116.1 0.8 convolution_add_fusion.1
  117.1 0.7 copy-done.30
  117.8 0.7 fusion.10
  118.5 0.9 copy-done.13
  119.4 0.8 convolution_add_fusion
  120.2 0.6 collective-permute-done.3
  120.8 2.7 %fusion.11 = bf16[256,1024]{1,0:T(8,128)(2,1)S(1)} fusion(bf16[256,1024]{1,0:T(8,128)(2,1)S(1)} %copy-done.5, f32[256,4096]{1,0:T(8,128)} %fusion.54, s32[]{:T(128)} %select_n.64, bf16[1,256,1024]{2,1,0:T(8,128)(2,1)} %collective-permute-done.3, bf16[2,256,1024]{2,1,0:T(8,128)(2,1)} %collective-permute-done.2), kind=kLoop, calls=%fused_computation.31 | loop fusion | flops 1835008 | bytes 3145732 | tf_op jit(solution)/shard_map/convert_element_type | solution.py:204
  124.2 0.4 convolution_convert_fusion.2
  124.6 2.1 %collective-permute-done.4 = bf16[2,256,1024]{2,1,0:T(8,128)(2,1)} collective-permute-done((bf16[2,256,1024]{2,1,0:T(8,128)(2,1)S(1)}, bf16[2,256,1024]{2,1,0:T(8,128)(2,1)}, u32[]{:S(2)}, u32[]{:S(2)}) %collective-permute-start.4) | collective-permute-done | bytes 1048608 | tf_op jit(solution)/shard_map/ppermute | solution.py:104
  126.6 1.1 copy.96
  127.7 5.8 %all-to-all-start.1 = ((bf16[8,32,1024]{2,1,0:T(8,128)(2,1)}), bf16[8,32,1024]{2,1,0:T(8,128)(2,1)S(1)}, u32[]{:S(2)}, u32[]{:S(2)}) async-start(bf16[8,32,1024]{2,1,0:T(8,128)(2,1)} %copy.96), calls=%async_computation.1 | async-start | bytes 1048576 | tf_op jit(solution)/shard_map/all_to_all | solution.py:260
  133.5 1.7 %fusion.24 = bf16[1,256,1024]{2,1,0:T(8,128)(2,1)S(1)} fusion(f32[256,4096]{1,0:T(8,128)} %copy-done.1, s32[]{:T(128)S(6)} %select_n.67, bf16[2,256,1024]{2,1,0:T(8,128)(2,1)} %collective-permute-done.4), kind=kLoop, calls=%fused_computation.62 | loop fusion | flops 786432 | bytes 2097156 | tf_op jit(solution)/shard_map/convert_element_type | solution.py:100
  135.2 1.6 collective-permute-start.5
  136.8 2.8 %fusion.3 = f32[256]{0:T(256)S(1)} fusion(bf16[256,4096]{1,0:T(8,128)(2,1)S(1)} %copy-done.4, f32[256,4096]{1,0:T(8,128)} %copy-done.1, f32[4096]{0:T(1024)S(1)} %copy-done.19), kind=kLoop, calls=%fused_computation.8 | loop fusion | flops 4194048 | bytes 6308864 | tf_op jit(solution)/shard_map/reduce_sum | solution.py:252
  139.7 1.1 collective-permute-done.6
  140.8 0.5 collective-permute-start.7
  141.3 7.7 %collective-permute-done.7 = f32[256]{0:T(256)S(1)} collective-permute-done((f32[256]{0:T(256)S(1)}, f32[256]{0:T(256)S(1)}, u32[]{:S(2)}, u32[]{:S(2)}) %collective-permute-start.7) | collective-permute-done | bytes 1056 | tf_op jit(solution)/shard_map/ppermute | solution.py:104
  149.1 2.6 %fusion.14 = bf16[256,1024]{1,0:T(8,128)(2,1)} fusion(bf16[256,1024]{1,0:T(8,128)(2,1)S(1)} %copy-done.5, f32[256,4096]{1,0:T(8,128)} %copy-done.1, s32[]{:T(128)} %select_n.64, bf16[1,256,1024]{2,1,0:T(8,128)(2,1)S(1)} %collective-permute-done.5, f32[256]{0:T(256)S(1)} %add_multiply_fusion, f32[256]{0:T(256)S(1)} %copy-done.21, ...), kind=kLoop, calls=%fused_computation.34 | loop fusion | flops 3407872 | bytes 3677188 | tf_op jit(solution)/shard_map/convert_element_type | solution.py:270
  151.7 0.8 copy.131
  (94 shorter events, 3.6 us)
Async XLA Ops:
  7.2 40.1 %copy-start = (bf16[4096,256]{1,0:T(8,128)(2,1)S(1)}, bf16[4096,256]{1,0:T(8,128)(2,1)}, u32[]{:S(2)}) copy-start(bf16[4096,256]{1,0:T(8,128)(2,1)} %param.13) | copy-start | bytes 6291460
  7.2 17.4 %copy-start.20 = (s32[4]{0:T(128)S(1)}, s32[4]{0:T(128)}, u32[]{:S(2)}) copy-start(s32[4]{0:T(128)} %constant.62.clone) | copy-start | bytes 52
  7.2 27.1 %copy-start.5 = (bf16[256,1024]{1,0:T(8,128)(2,1)S(1)}, bf16[256,1024]{1,0:T(8,128)(2,1)}, u32[]{:S(2)}) copy-start(bf16[256,1024]{1,0:T(8,128)(2,1)} %param.10) | copy-start | bytes 1572868
  7.2 23.0 %copy-start.27 = (s32[1,2]{1,0:T(1,128)S(1)}, s32[1,2]{1,0:T(1,128)}, u32[]{:S(2)}) copy-start(s32[1,2]{1,0:T(1,128)} %param.17) | copy-start | bytes 28
  7.2 15.2 %collective-permute-start = (bf16[1,256,1024]{2,1,0:T(8,128)(2,1)}, bf16[1,256,1024]{2,1,0:T(8,128)(2,1)S(1)}, u32[]{:S(2)}, u32[]{:S(2)}) collective-permute-start(bf16[1,256,1024]{2,1,0:T(8,128)(2,1)} %bitcast.154), channel_id=1, source_target_pairs={{0,2},{1,3},{2,0},{3,1},{4,6},{5,7},{6,4},{7,5},{8,10},{9,11},{10,... | collective-permute-start | bytes 1572872 | tf_op jit(solution)/shard_map/ppermute | solution.py:69
  24.5 9.8 %collective-permute-start.1 = (bf16[2,256,1024]{2,1,0:T(8,128)(2,1)}, bf16[2,256,1024]{2,1,0:T(8,128)(2,1)}, u32[]{:S(2)}, u32[]{:S(2)}) collective-permute-start(bf16[2,256,1024]{2,1,0:T(8,128)(2,1)} %pad_maximum_fusion.2), channel_id=1, source_target_pairs={{0,1},{1,0},{2,3},{3,2},{4,5},{5,4},{6,7},{7,6},{8,9},{9,8},{10,11... | collective-permute-start | bytes 3145736 | tf_op jit(solution)/shard_map/ppermute | solution.py:69
  37.5 9.8 %copy-start.19 = (f32[4096]{0:T(1024)S(1)}, f32[4096]{0:T(1024)}, u32[]{:S(2)}) copy-start(f32[4096]{0:T(1024)} %param.11) | copy-start | bytes 49156
  37.5 21.3 %all-to-all-start = ((bf16[8,32,1024]{2,1,0:T(8,128)(2,1)}), bf16[8,32,1024]{2,1,0:T(8,128)(2,1)S(1)}, u32[]{:S(2)}, u32[]{:S(2)}) async-start(bf16[8,32,1024]{2,1,0:T(8,128)(2,1)} %bitcast.169), calls=%async_computation | async-start | bytes 1048576 | tf_op jit(solution)/shard_map/all_to_all | solution.py:154
  43.6 38.5 %all-gather.2.cloned.1.call-start = ((), (), s32[]{:S(2)}) async-start(), calls=%async_computation.2 | async-start | bytes 2621440 | tf_op jit(solution)/shard_map/all_gather | solution.py:193
  43.7 3.6 %copy-start.2 = (bf16[256,4096]{1,0:T(8,128)(2,1)S(1)}, bf16[256,4096]{1,0:T(8,128)(2,1)}, u32[]{:S(2)}) copy-start(bf16[256,4096]{1,0:T(8,128)(2,1)} %pad_maximum_fusion.1) | copy-start | bytes 6291460
  44.5 14.3 %copy-start.25 = (s32[8]{0:T(128)}, s32[8]{0:T(128)S(1)}, u32[]{:S(2)}) copy-start(s32[8]{0:T(128)S(1)} %fusion.41) | copy-start | bytes 100
  47.2 1.9 %copy-start.22 = (f32[256]{0:T(256)}, f32[256]{0:T(256)S(1)}, u32[]{:S(2)}) copy-start(f32[256]{0:T(256)S(1)} %get-tuple-element.47) | copy-start | bytes 3076
  68.8 1.1 copy-start.17
  68.9 0.8 copy-start.8
  69.0 0.9 copy-start.10
  69.0 1.9 %copy-start.3 = (bf16[256,4096]{1,0:T(8,128)(2,1)S(1)}, bf16[256,4096]{1,0:T(8,128)(2,1)}, u32[]{:S(2)}) copy-start(bf16[256,4096]{1,0:T(8,128)(2,1)} %pad_maximum_fusion.1) | copy-start | bytes 6291460
  69.0 2.6 %copy-start.12 = (bf16[4096,256]{1,0:T(8,128)(2,1)S(1)}, bf16[4096,256]{1,0:T(8,128)(2,1)}, u32[]{:S(2)}) copy-start(bf16[4096,256]{1,0:T(8,128)(2,1)} %param.14) | copy-start | bytes 6291460
  69.0 2.6 %copy-start.23 = (f32[256]{0:T(256)S(1)}, f32[256]{0:T(256)}, u32[]{:S(2)}) copy-start(f32[256]{0:T(256)} %copy-done.22) | copy-start | bytes 3076
  69.1 0.8 copy-start.14
  71.5 1.4 copy-start.29
  71.5 1.4 copy-start.31
  71.6 3.0 %slice-start = ((s8[8388608]{0:T(1024)(128)(4,1)}), s8[4194304]{0:T(1024)(128)(4,1)S(1)}, s32[]{:S(2)}) async-start(s8[8388608]{0:T(1024)(128)(4,1)} %bitcast.151), calls=%async_computation.3 | async-start | bytes 8388608
  72.8 0.8 copy-start.28
  72.9 3.1 %slice-start.1 = ((s8[8388608]{0:T(1024)(128)(4,1)}), s8[4194304]{0:T(1024)(128)(4,1)S(1)}, s32[]{:S(2)}) async-start(s8[8388608]{0:T(1024)(128)(4,1)} %bitcast.151), calls=%async_computation.4 | async-start | bytes 8388608
  85.0 7.6 %collective-permute-start.2 = (bf16[2,256,1024]{2,1,0:T(8,128)(2,1)}, bf16[2,256,1024]{2,1,0:T(8,128)(2,1)}, u32[]{:S(2)}, u32[]{:S(2)}) collective-permute-start(bf16[2,256,1024]{2,1,0:T(8,128)(2,1)} %pad_maximum_fusion.3), channel_id=1, source_target_pairs={{0,1},{1,0},{2,3},{3,2},{4,5},{5,4},{6,7},{7,6},{8,9},{9,8},{10,11... | collective-permute-start | bytes 3145736 | tf_op jit(solution)/shard_map/ppermute | solution.py:102
  95.9 2.6 %copy-start.9 = (bf16[256,8,64]{2,0,1:T(8,128)(2,1)S(1)}, bf16[256,8,64]{2,0,1:T(8,128)(2,1)}, u32[]{:S(2)}) copy-start(bf16[256,8,64]{2,0,1:T(8,128)(2,1)} %copy-done.8) | copy-start | bytes 786436
  95.9 2.6 %copy-start.11 = (bf16[256,8,64]{2,0,1:T(8,128)(2,1)S(1)}, bf16[256,8,64]{2,0,1:T(8,128)(2,1)}, u32[]{:S(2)}) copy-start(bf16[256,8,64]{2,0,1:T(8,128)(2,1)} %copy-done.10) | copy-start | bytes 786436
  98.5 0.9 copy-start.15
  106.4 14.4 %collective-permute-start.3 = (bf16[1,256,1024]{2,1,0:T(8,128)(2,1)}, bf16[1,256,1024]{2,1,0:T(8,128)(2,1)}, u32[]{:S(2)}, u32[]{:S(2)}) collective-permute-start(bf16[1,256,1024]{2,1,0:T(8,128)(2,1)} %fusion.23), channel_id=1, source_target_pairs={{0,2},{1,3},{2,0},{3,1},{4,6},{5,7},{6,4},{7,5},{8,10},{9,11},{10,... | collective-permute-start | bytes 1572872 | tf_op jit(solution)/shard_map/ppermute | solution.py:102
  110.2 5.8 %copy-start.16 = (bf16[256,2,128]{0,2,1:T(8,128)(2,1)S(1)}, bf16[256,2,128]{0,2,1:T(8,128)(2,1)}, u32[]{:S(2)}) copy-start(bf16[256,2,128]{0,2,1:T(8,128)(2,1)} %copy.93) | copy-start | bytes 393220
  116.0 1.0 copy-start.7
  116.0 1.0 copy-start.18
  116.0 1.8 %copy-start.30 = (f32[2,256,256,4]{2,1,3,0:T(8,128)S(1)}, f32[2,256,256,4]{2,1,3,0:T(8,128)}, u32[]{:S(2)}) copy-start(f32[2,256,256,4]{2,1,3,0:T(8,128)} %copy-done.29) | copy-start | bytes 6291460
  116.0 1.8 %copy-start.32 = (f32[2,4,256]{2,1,0:T(4,128)S(1)}, f32[2,4,256]{2,1,0:T(4,128)}, u32[]{:S(2)}) copy-start(f32[2,4,256]{2,1,0:T(4,128)} %copy-done.31) | copy-start | bytes 24580
  117.8 1.6 copy-start.13
  120.2 3.5 %copy-start.1 = (f32[256,4096]{1,0:T(8,128)}, f32[256,4096]{1,0:T(8,128)S(1)}, u32[]{:S(2)}) copy-start(f32[256,4096]{1,0:T(8,128)S(1)} %convolution_add_fusion) | copy-start | bytes 12582916
  123.5 0.7 copy-start.26
  123.8 2.9 %collective-permute-start.4 = (bf16[2,256,1024]{2,1,0:T(8,128)(2,1)S(1)}, bf16[2,256,1024]{2,1,0:T(8,128)(2,1)}, u32[]{:S(2)}, u32[]{:S(2)}) collective-permute-start(bf16[2,256,1024]{2,1,0:T(8,128)(2,1)S(1)} %pad_maximum_fusion.4), channel_id=1, source_target_pairs={{0,1},{1,0},{2,3},{3,2},{4,5},{5,4},{6,7},{7,6},{8,9},{9,8},{10,11... | collective-permute-start | bytes 3145736 | tf_op jit(solution)/shard_map/ppermute | solution.py:104
  127.7 24.0 %all-to-all-start.1 = ((bf16[8,32,1024]{2,1,0:T(8,128)(2,1)}), bf16[8,32,1024]{2,1,0:T(8,128)(2,1)S(1)}, u32[]{:S(2)}, u32[]{:S(2)}) async-start(bf16[8,32,1024]{2,1,0:T(8,128)(2,1)} %copy.96), calls=%async_computation.1 | async-start | bytes 1048576 | tf_op jit(solution)/shard_map/all_to_all | solution.py:260
  133.5 3.3 %copy-start.4 = (bf16[256,4096]{1,0:T(8,128)(2,1)S(1)}, bf16[256,4096]{1,0:T(8,128)(2,1)}, u32[]{:S(2)}) copy-start(bf16[256,4096]{1,0:T(8,128)(2,1)} %pad_maximum_fusion.1) | copy-start | bytes 6291460
  135.2 13.9 %copy-start.6 = (bf16[8,32,1024]{2,1,0:T(8,128)(2,1)S(1)}, bf16[8,32,1024]{2,1,0:T(8,128)(2,1)}, u32[]{:S(2)}) copy-start(bf16[8,32,1024]{2,1,0:T(8,128)(2,1)} %copy.82) | copy-start | bytes 1572868
  135.2 13.9 %dynamic-slice-start = ((f32[4096]{0:T(1024)}, s32[]{:T(128)}), f32[1024]{0:T(1024)S(1)}, s32[]{:S(2)}) async-start(f32[4096]{0:T(1024)} %param.11, s32[]{:T(128)} %select_n.64), calls=%async_computation.5 | async-start | bytes 8704 | tf_op jit(solution)/shard_map/dynamic_slice | solution.py:142
  135.2 13.9 %copy-start.21 = (f32[256]{0:T(256)S(1)}, f32[256]{0:T(256)}, u32[]{:S(2)}) copy-start(f32[256]{0:T(256)} %get-tuple-element.46) | copy-start | bytes 3076
  135.2 13.9 %copy-start.24 = (f32[256]{0:T(256)S(1)}, f32[256]{0:T(256)}, u32[]{:S(2)}) copy-start(f32[256]{0:T(256)} %copy-done.22) | copy-start | bytes 3076
  135.2 13.8 %collective-permute-start.5 = (bf16[1,256,1024]{2,1,0:T(8,128)(2,1)S(1)}, bf16[1,256,1024]{2,1,0:T(8,128)(2,1)S(1)}, u32[]{:S(2)}, u32[]{:S(2)}) collective-permute-start(bf16[1,256,1024]{2,1,0:T(8,128)(2,1)S(1)} %fusion.24), channel_id=1, source_target_pairs={{0,2},{1,3},{2,0},{3,1},{4,6},{5,7},{6,4},{7,5},{8,10},{9,11},{10,... | collective-permute-start | bytes 1572872 | tf_op jit(solution)/shard_map/ppermute | solution.py:104
  139.6 1.2 collective-permute-start.6
  140.8 8.2 %collective-permute-start.7 = (f32[256]{0:T(256)S(1)}, f32[256]{0:T(256)S(1)}, u32[]{:S(2)}, u32[]{:S(2)}) collective-permute-start(f32[256]{0:T(256)S(1)} %add.135), channel_id=1, source_target_pairs={{0,2},{1,3},{2,0},{3,1},{4,6},{5,7},{6,4},{7,5},{8,10},{9,11},{10,... | collective-permute-start | bytes 3080 | tf_op jit(solution)/shard_map/ppermute | solution.py:104
Sparse Core Ops, SparseCore 0:
  60.5 21.6 all-gather.1

commit v16 on v12

--- a/solution.py
+++ b/solution.py
@@ -98,15 +98,17 @@
         keep = [i for i, m in enumerate(masks) if not m & bit]
         send = [i for i, m in enumerate(masks) if m & bit]
         outgoing = jnp.stack([held[i] for i in send]).astype(jnp.bfloat16)
-        if extra is None:
-            incoming = lax.ppermute(outgoing, axis_name, _xor_pairs(size, bit))
-        else:
-            incoming, extra_in = lax.ppermute((outgoing, extra), axis_name, _xor_pairs(size, bit))
-            extra = extra + extra_in
+        incoming = lax.ppermute(outgoing, axis_name, _xor_pairs(size, bit))
         if ties:
             incoming, first = lax.optimization_barrier((incoming, ties[0]))
             ties = ties[1:]
             done_ties.append(first)
+        if extra is not None and bit == 1:
+            incoming, extra = lax.optimization_barrier((incoming, extra))
+            extra = extra + sum(
+                lax.ppermute(extra, axis_name, _xor_pairs(size, other))
+                for other in range(1, size)
+            )
         sent_masks = [masks[i] ^ bit for i in send]
         held = [
             held[i] + incoming[sent_masks.index(masks[i])].astype(jnp.float32) for i in keep

time: 135 us -> 136 us (level)
  other arithmetic: 22.8 us -> 20.5 us
  local copies, waits for them, and re-layouts: 25.4 us -> 27.1 us
    reduce_sum x1, other arithmetic: 2.82 us -> 0.63 us  [per_device(): jnp.sum(normed_partial * norm_gain[None, :] * gathered_float, axis=1)]
    ppermute x2 -> x4, starting transfers between devices: 1.13 us -> 2.96 us  [scatter_features(): incoming = lax.ppermute(outgoing, axis_name, _xor_pairs(size, bit))]
    unnamed x69, local copies, waits for them, and re-layouts: 12 us -> 13.8 us
    ppermute x4 -> x3, waiting for transfers between devices: 10.9 us -> 10.4 us  [scatter_features(): lax.ppermute(extra, axis_name, _xor_pairs(size, other))]
  transfers between devices with their start and end apart: 16 -> 17, of which waited for: 5 -> 5; matrix products, arithmetic and copies ran while one was open for 43% -> 41% of each run, Pallas kernels for 0% -> 0%
where the time goes in v16:
time: 136 us; the launch traced here: 135 us
  matrix products  34.6 us (25%)
  local copies, waits for them, and re-layouts  27.1 us (20%)
  starting transfers between devices  22.6 us (17%)
  other arithmetic  20.5 us (15%)
  waiting for transfers between devices  15 us (11%)
  between operations  14.8 us (11%)
    unnamed x69, local copies, waits for them, and re-layouts  13.8 us
    ppermute x7, starting transfers between devices, per_device(): returned.append(lax.ppermute(piece, 'dp', pairs))  12.5 us
    ppermute x3, waiting for transfers between devices, scatter_features(): lax.ppermute(extra, axis_name, _xor_pairs(size, other))  10.4 us
    dot_general x1, matrix products, per_device(): lax.dot_general(grad_full, w_out, (((1,), (1,)), ((), ())), preferred_ele...  7.41 us
    dot_general x1, matrix products, per_device(): jnp.dot(normed_input, w_query, preferred_element_type=jnp.float32)  6.67 us
    dot_general x1, matrix products, per_device(): lax.dot_general(grad_query.reshape(token_row_count, query_width), w_query...  5.76 us
    another operation x8, local copies, waits for them, and re-layouts, per_device(): returned = jnp.stack(returned)  5.59 us
    all_to_all x1, starting transfers between devices, per_device(): lax.all_to_all(outgoing, 'dp', split_axis=0, concat_axis=0, tiled=True)  5.17 us
  transfers between devices with their start and end apart: 17, of which 5 were waited for; matrix products, arithmetic and copies ran while one was open for 41% of the time, Pallas kernels for 0%

profile of v16, /device:TPU:0, one launch (start us, length us, event | category | flops | bytes accessed | tf_op | source)
XLA Modules:
  0.0 134.7 jit_solution(11829787056730899403)
XLA Ops:
  7.2 0.7 all-gather.3.cloned.1.call-update
  8.1 1.1 dynamic-slice_bitcast_fusion
  9.2 6.0 %collective-permute-start.6 = (bf16[32,1024]{1,0:T(8,128)(2,1)S(1)}, bf16[32,1024]{1,0:T(8,128)(2,1)S(1)}, u32[]{:S(2)}, u32[]{:S(2)}) collective-permute-start(bf16[32,1024]{1,0:T(8,128)(2,1)S(1)} %get-tuple-element.40), channel_id=1, source_target_pairs={{0,28},{4,0},{8,4},{12,8},{16,12},{20,16},{24,20},{28,24},{1,29},{... | collective-permute-start | bytes 196616 | tf_op jit(solution)/shard_map/ppermute | solution.py:161
  15.2 0.4 collective-permute-start.5
  15.7 3.0 %collective-permute-start.3 = (bf16[32,1024]{1,0:T(8,128)(2,1)S(1)}, bf16[32,1024]{1,0:T(8,128)(2,1)S(1)}, u32[]{:S(2)}, u32[]{:S(2)}) collective-permute-start(bf16[32,1024]{1,0:T(8,128)(2,1)S(1)} %get-tuple-element.43), channel_id=1, source_target_pairs={{0,16},{4,20},{8,24},{12,28},{16,0},{20,4},{24,8},{28,12},{1,17},{... | collective-permute-start | bytes 196616 | tf_op jit(solution)/shard_map/ppermute | solution.py:161
  18.7 0.8 reduce-window.8
  19.6 0.5 multiply_cosine_fusion
  20.2 0.7 fusion.31
  21.0 1.9 %collective-permute-start.1 = (bf16[32,1024]{1,0:T(8,128)(2,1)S(1)}, bf16[32,1024]{1,0:T(8,128)(2,1)S(1)}, u32[]{:S(2)}, u32[]{:S(2)}) collective-permute-start(bf16[32,1024]{1,0:T(8,128)(2,1)S(1)} %get-tuple-element.45), channel_id=1, source_target_pairs={{0,8},{4,12},{8,16},{12,20},{16,24},{20,28},{24,0},{28,4},{1,9},{5... | collective-permute-start | bytes 196616 | tf_op jit(solution)/shard_map/ppermute | solution.py:161
  22.9 1.1 collective-permute-start
  24.0 1.3 and_select_fusion
  25.7 2.8 %collective-permute-done.2 = bf16[32,1024]{1,0:T(8,128)(2,1)S(1)} collective-permute-done((bf16[32,1024]{1,0:T(8,128)(2,1)S(1)}, bf16[32,1024]{1,0:T(8,128)(2,1)S(1)}, u32[]{:S(2)}, u32[]{:S(2)}) %collective-permute-start.2) | collective-permute-done | bytes 65568 | tf_op jit(solution)/shard_map/ppermute | solution.py:161
  28.6 0.7 copy.93
  29.3 0.8 copy.92
  30.1 0.8 copy.91
  30.8 2.9 %stack.58 = bf16[8,32,1024]{2,0,1:T(8,128)(2,1)S(1)} concatenate(bf16[1,32,1024]{2,0,1:T(2,128)(2,1)S(1)} %copy.132, bf16[1,32,1024]{2,0,1:T(2,128)(2,1)} %copy.91, bf16[1,32,1024]{2,0,1:T(2,128)(2,1)} %copy.92, bf16[1,32,1024]{2,0,1:T(2,128)(2,1)} %copy.93, bf16[1,32,1024]{2,0,1:T(2,128)(2,1)S(1)} %copy.94, bf16[1,32,1024]{2,0,1:T(2,128)(2,1)S(1)} %copy.95, ...), dimensions={0} | concatenate | bytes 1048576 | tf_op jit(solution)/shard_map/stack | solution.py:162
  34.1 1.1 copy.98
  35.3 2.2 %fusion = f32[256]{0:T(256)S(1)} fusion(bf16[256,4096]{1,0:T(8,128)(2,1)} %all-gather.3.cloned.1.call-done), kind=kLoop, calls=%fused_computation.5 | loop fusion | flops 3145472 | bytes 2098176 | tf_op jit(solution)/shard_map/reduce_sum | solution.py:185
  37.5 0.6 multiply_multiply_fusion
  38.1 1.2 fusion.47
  39.6 6.7 %convolution_bitcast_fusion = f32[32,8,8,128]{3,1,2,0:T(8,128)S(1)} fusion(bf16[4096,1024]{1,0:T(8,128)(2,1)} %param.11, bf16[256,4096]{1,0:T(8,128)(2,1)} %all-gather.3.cloned.1.call-done, f32[4096]{0:T(1024)S(1)} %copy-done.19, f32[256]{0:T(256)S(1)} %get-tuple-element.53), kind=kOutput, calls=%fused_computation.16 | convolution fusion | flops 2151677952 | bytes 11551744 | tf_op jit(solution)/shard_map/dot_general | solution.py:187
  46.5 0.5 subtract_convert_fusion.1
  47.3 0.6 copy-done.9
  48.1 0.9 fusion.7
  49.1 0.7 copy-done.13
  49.8 1.2 convolution_convert_fusion.4
  51.1 0.7 convolution_convert_fusion.1
  51.8 1.0 slice-done
  52.8 1.4 %slice-done.1 = s8[4194304]{0:T(1024)(128)(4,1)S(1)} async-done(((s8[8388608]{0:T(1024)(128)(4,1)}), s8[4194304]{0:T(1024)(128)(4,1)S(1)}, s32[]{:S(2)}) %slice-start.1) | async-done | bytes 4194328
  54.2 4.5 %fusion.55 = f32[256,4096]{1,0:T(8,128)} fusion(bf16[256,1024]{0,1:T(8,128)(2,1)S(1)} %bitcast.167, bf16[1024,4096]{1,0:T(8,128)(2,1)S(1)} %bitcast.163), kind=kOutput, calls=%fused_computation.114 | convolution fusion | flops 2147483648 | bytes 13107200 | tf_op jit(solution)/shard_map/dot_general | solution.py:215
  59.1 1.7 %fusion.19 = (bf16[1,256,1024]{2,1,0:T(8,128)(2,1)S(1)}, bf16[1,256,1024]{2,1,0:T(8,128)(2,1)S(1)}) fusion(f32[256,4096]{1,0:T(8,128)} %fusion.55, s32[]{:T(128)S(6)} %select_n.111, s32[]{:T(128)S(6)} %select_n.112), kind=kLoop, calls=%fused_computation.54 | loop fusion | bytes 2097160 | tf_op jit(solution)/shard_map/stack | solution.py:100
  60.8 1.1 pad_maximum_fusion
  62.1 7.4 %convolution_convert_fusion = bf16[256,1024]{1,0:T(8,128)(2,1)} fusion(bf16[256,4096]{1,0:T(8,128)(2,1)} %all-gather.5.cloned.1.call-done, bf16[1024,4096]{1,0:T(8,128)(2,1)} %param.14), kind=kOutput, calls=%fused_computation.19 | convolution fusion | flops 2147745792 | bytes 11010048 | tf_op jit(solution)/shard_map/dot_general | solution.py:218
  69.6 1.2 copy.99
  71.0 2.5 %fusion.5 = bf16[2,4,256,256]{2,3,1,0:T(8,128)(2,1)S(1)} fusion(bf16[256,2,128,1]{0,2,3,1:T(8,128)(2,1)} %bitcast.191, bf16[256,2,4,128]{0,3,2,1:T(8,128)(2,1)S(1)} %bitcast.168, f32[2,4,256]{2,1,0:T(4,128)S(1)} %bitcast.187, f32[2,4,256]{2,1,0:T(4,128)} %copy-done.27, f32[2,256,256,4]{2,1,3,0:T(8,128)} %copy-done.25, pred[256,256]{0,1:T(8,128)(4,1)} %fusion.31), kind=kOutput, calls=%fused_computation.11 | convolution fusion | flops 137363456 | bytes 3883008 | tf_op jit(solution)/shard_map/qkgd,skd->kgqs/dot_general | solution.py:232
  73.5 0.5 fusion.9
  74.4 0.4 convolution_multiply_fusion
  74.9 1.1 fusion.53
  76.3 1.5 %copy.134 = f32[256,8,64]{2,1,0:T(8,128)S(1)} copy(f32[256,8,64]{0,2,1:T(8,128)} %get-tuple-element.34) | data formatting | bytes 1048576
  77.8 2.3 %fusion.23 = bf16[1,256,1024]{2,1,0:T(8,128)(2,1)} fusion(f32[256,4096]{1,0:T(8,128)} %fusion.55, s32[]{:T(128)S(6)} %select_n.113, bf16[2,256,1024]{2,1,0:T(8,128)(2,1)} %collective-permute-done.7), kind=kLoop, calls=%fused_computation.58 | loop fusion | flops 786432 | bytes 2097156 | tf_op jit(solution)/shard_map/convert_element_type | solution.py:100
  80.1 0.9 collective-permute-start.8
  81.0 2.4 %copy.133 = f32[256,8,64]{2,1,0:T(8,128)} copy(f32[256,8,64]{0,2,1:T(8,128)} %get-tuple-element.35) | data formatting | bytes 1048576
  83.4 1.5 %add_convert_fusion = (bf16[256,8,64]{2,1,0:T(8,128)(2,1)S(1)}, bf16[256,8,64]{2,1,0:T(8,128)(2,1)S(1)}) fusion(f32[256,8,64]{2,1,0:T(8,128)S(1)} %copy.134, f32[256,8,64]{2,1,0:T(8,128)} %copy.133, f32[256,64]{1,0:T(8,128)S(1)} %get-tuple-element.51, f32[256,64]{1,0:T(8,128)S(1)} %get-tuple-element.50), kind=kLoop, calls=%fused_computation.48 | loop fusion | flops 1048576 | bytes 1703936 | tf_op jit(solution)/shard_map/convert.12
  85.2 5.8 %fusion.25 = f32[256,4096]{1,0:T(8,128)S(1)} fusion(bf16[4096,1024]{1,0:T(8,128)(2,1)} %param.11, bf16[32,8,8,128]{3,2,1,0:T(8,128)(2,1)S(1)} %bitcast.175), kind=kOutput, calls=%fused_computation.60 | convolution fusion | flops 2147483648 | bytes 13107200 | tf_op jit(solution)/shard_map/dot_general | solution.py:255
  91.0 0.8 convolution_add_fusion.1
  92.0 0.7 copy-done.26
  92.7 0.6 fusion.10
  93.4 0.9 copy-done.14
  94.3 0.8 convolution_add_fusion
  95.4 3.1 %fusion.11 = bf16[256,1024]{1,0:T(8,128)(2,1)S(1)} fusion(bf16[256,1024]{1,0:T(8,128)(2,1)S(1)} %copy-done.6, f32[256,4096]{1,0:T(8,128)} %fusion.55, s32[]{:T(128)} %select_n.110, bf16[1,256,1024]{2,1,0:T(8,128)(2,1)} %collective-permute-done.8, bf16[2,256,1024]{2,1,0:T(8,128)(2,1)} %collective-permute-done.7), kind=kLoop, calls=%fused_computation.29 | loop fusion | flops 1835008 | bytes 3145732 | tf_op jit(solution)/shard_map/convert_element_type | solution.py:227
  99.2 0.4 convolution_convert_fusion.2
  99.6 0.7 copy-done.4
  100.3 0.6 fusion.3
  100.9 0.7 collective-permute-done.9
  101.6 1.1 copy.112
  102.7 5.2 %all-to-all-start = ((bf16[8,32,1024]{2,1,0:T(8,128)(2,1)}), bf16[8,32,1024]{2,1,0:T(8,128)(2,1)}, u32[]{:S(2)}, u32[]{:S(2)}) async-start(bf16[8,32,1024]{2,1,0:T(8,128)(2,1)} %copy.112), calls=%async_computation | async-start | bytes 1048576 | tf_op jit(solution)/shard_map/all_to_all | solution.py:283
  107.9 1.5 %fusion.24 = bf16[1,256,1024]{2,1,0:T(8,128)(2,1)S(1)} fusion(f32[256,4096]{1,0:T(8,128)} %copy-done.1, s32[]{:T(128)S(6)} %select_n.113, bf16[2,256,1024]{2,1,0:T(8,128)(2,1)} %collective-permute-done.9), kind=kLoop, calls=%fused_computation.59 | loop fusion | flops 786432 | bytes 2097156 | tf_op jit(solution)/shard_map/convert_element_type | solution.py:100
  109.4 1.5 %collective-permute-start.10 = (bf16[1,256,1024]{2,1,0:T(8,128)(2,1)S(1)}, bf16[1,256,1024]{2,1,0:T(8,128)(2,1)S(1)}, u32[]{:S(2)}, u32[]{:S(2)}) collective-permute-start(bf16[1,256,1024]{2,1,0:T(8,128)(2,1)S(1)} %fusion.24), channel_id=1, source_target_pairs={{0,2},{1,3},{2,0},{3,1},{4,6},{5,7},{6,4},{7,5},{8,10},{9,11},{10,... | collective-permute-start | bytes 1572872 | tf_op jit(solution)/shard_map/ppermute | solution.py:101
  110.9 1.2 collective-permute-start.12
  112.2 0.7 collective-permute-start.11
  112.8 9.4 %collective-permute-done.13 = f32[256]{0:T(256)S(1)} collective-permute-done((f32[256]{0:T(256)S(1)}, f32[256]{0:T(256)S(1)}, u32[]{:S(2)}, u32[]{:S(2)}) %collective-permute-start.13) | collective-permute-done | bytes 1056 | tf_op jit(solution)/shard_map/ppermute | solution.py:109
  122.2 1.0 collective-permute-done.12
  123.3 2.6 %fusion.14 = bf16[256,1024]{1,0:T(8,128)(2,1)} fusion(bf16[256,1024]{1,0:T(8,128)(2,1)S(1)} %copy-done.6, f32[256,4096]{1,0:T(8,128)} %copy-done.1, s32[]{:T(128)} %select_n.110, bf16[1,256,1024]{2,1,0:T(8,128)(2,1)S(1)} %collective-permute-done.10, f32[256]{0:T(256)S(1)} %add_multiply_fusion, f32[256]{0:T(256)S(1)} %copy-done.20, ...), kind=kLoop, calls=%fused_computation.32 | loop fusion | flops 3407872 | bytes 3677188 | tf_op jit(solution)/shard_map/convert_element_type | solution.py:293
  125.9 1.9 %copy.144 = bf16[256,1024]{1,0:T(8,128)(2,1)} copy(bf16[256,1024]{1,0:T(8,128)(2,1)} %bitcast.56) | data formatting | bytes 1048576
  (103 shorter events, 5.2 us)
Async XLA Ops:
  7.2 31.0 %copy-start = (bf16[4096,256]{1,0:T(8,128)(2,1)S(1)}, bf16[4096,256]{1,0:T(8,128)(2,1)}, u32[]{:S(2)}) copy-start(bf16[4096,256]{1,0:T(8,128)(2,1)} %param.12) | copy-start | bytes 6291460
  7.2 28.1 %all-gather.3.cloned.1.call-start = ((), (), s32[]{:S(2)}) async-start(), calls=%async_computation.1 | async-start | bytes 2621440 | tf_op jit(solution)/shard_map/all_gather | solution.py:183
  7.9 51.2 %all-gather.5.cloned.1.call-start = ((), (), s32[]{:S(2)}) async-start(), calls=%async_computation.2 | async-start | bytes 2621440 | tf_op jit(solution)/shard_map/all_gather | solution.py:216
  9.2 11.8 %collective-permute-start.6 = (bf16[32,1024]{1,0:T(8,128)(2,1)S(1)}, bf16[32,1024]{1,0:T(8,128)(2,1)S(1)}, u32[]{:S(2)}, u32[]{:S(2)}) collective-permute-start(bf16[32,1024]{1,0:T(8,128)(2,1)S(1)} %get-tuple-element.40), channel_id=1, source_target_pairs={{0,28},{4,0},{8,4},{12,8},{16,12},{20,16},{24,20},{28,24},{1,29},{... | collective-permute-start | bytes 196616 | tf_op jit(solution)/shard_map/ppermute | solution.py:161
  15.2 7.7 %collective-permute-start.5 = (bf16[32,1024]{1,0:T(8,128)(2,1)S(1)}, bf16[32,1024]{1,0:T(8,128)(2,1)S(1)}, u32[]{:S(2)}, u32[]{:S(2)}) collective-permute-start(bf16[32,1024]{1,0:T(8,128)(2,1)S(1)} %get-tuple-element.41), channel_id=1, source_target_pairs={{0,24},{4,28},{8,0},{12,4},{16,8},{20,12},{24,16},{28,20},{1,25},{... | collective-permute-start | bytes 196616 | tf_op jit(solution)/shard_map/ppermute | solution.py:161
  15.7 9.8 %collective-permute-start.4 = (bf16[32,1024]{1,0:T(8,128)(2,1)S(1)}, bf16[32,1024]{1,0:T(8,128)(2,1)S(1)}, u32[]{:S(2)}, u32[]{:S(2)}) collective-permute-start(bf16[32,1024]{1,0:T(8,128)(2,1)S(1)} %get-tuple-element.42), channel_id=1, source_target_pairs={{0,20},{4,24},{8,28},{12,0},{16,4},{20,8},{24,12},{28,16},{1,21},{... | collective-permute-start | bytes 196616 | tf_op jit(solution)/shard_map/ppermute | solution.py:161
  15.7 10.0 %collective-permute-start.3 = (bf16[32,1024]{1,0:T(8,128)(2,1)S(1)}, bf16[32,1024]{1,0:T(8,128)(2,1)S(1)}, u32[]{:S(2)}, u32[]{:S(2)}) collective-permute-start(bf16[32,1024]{1,0:T(8,128)(2,1)S(1)} %get-tuple-element.43), channel_id=1, source_target_pairs={{0,16},{4,20},{8,24},{12,28},{16,0},{20,4},{24,8},{28,12},{1,17},{... | collective-permute-start | bytes 196616 | tf_op jit(solution)/shard_map/ppermute | solution.py:161
  18.7 9.9 %collective-permute-start.2 = (bf16[32,1024]{1,0:T(8,128)(2,1)S(1)}, bf16[32,1024]{1,0:T(8,128)(2,1)S(1)}, u32[]{:S(2)}, u32[]{:S(2)}) collective-permute-start(bf16[32,1024]{1,0:T(8,128)(2,1)S(1)} %get-tuple-element.44), channel_id=1, source_target_pairs={{0,12},{4,16},{8,20},{12,24},{16,28},{20,0},{24,4},{28,8},{1,13},{... | collective-permute-start | bytes 196616 | tf_op jit(solution)/shard_map/ppermute | solution.py:161
  21.0 8.3 %collective-permute-start.1 = (bf16[32,1024]{1,0:T(8,128)(2,1)S(1)}, bf16[32,1024]{1,0:T(8,128)(2,1)S(1)}, u32[]{:S(2)}, u32[]{:S(2)}) collective-permute-start(bf16[32,1024]{1,0:T(8,128)(2,1)S(1)} %get-tuple-element.45), channel_id=1, source_target_pairs={{0,8},{4,12},{8,16},{12,20},{16,24},{20,28},{24,0},{28,4},{1,9},{5... | collective-permute-start | bytes 196616 | tf_op jit(solution)/shard_map/ppermute | solution.py:161
  22.9 7.2 %collective-permute-start = (bf16[32,1024]{1,0:T(8,128)(2,1)S(1)}, bf16[32,1024]{1,0:T(8,128)(2,1)S(1)}, u32[]{:S(2)}, u32[]{:S(2)}) collective-permute-start(bf16[32,1024]{1,0:T(8,128)(2,1)S(1)} %get-tuple-element.46), channel_id=1, source_target_pairs={{0,4},{4,8},{8,12},{12,16},{16,20},{20,24},{24,28},{28,0},{1,5},{5... | collective-permute-start | bytes 196616 | tf_op jit(solution)/shard_map/ppermute | solution.py:161
  34.1 4.0 %copy-start.19 = (f32[4096]{0:T(1024)S(1)}, f32[4096]{0:T(1024)}, u32[]{:S(2)}) copy-start(f32[4096]{0:T(1024)} %param.10) | copy-start | bytes 49156
  35.3 2.8 %copy-start.2 = (bf16[256,4096]{1,0:T(8,128)(2,1)S(1)}, bf16[256,4096]{1,0:T(8,128)(2,1)}, u32[]{:S(2)}) copy-start(bf16[256,4096]{1,0:T(8,128)(2,1)} %all-gather.3.cloned.1.call-done) | copy-start | bytes 6291460
  38.1 10.8 %copy-start.21 = (f32[256]{0:T(256)}, f32[256]{0:T(256)S(1)}, u32[]{:S(2)}) copy-start(f32[256]{0:T(256)S(1)} %get-tuple-element.53) | copy-start | bytes 3076
  47.0 1.1 copy-start.17
  47.1 0.8 copy-start.9
  47.2 0.9 copy-start.11
  47.2 1.9 %copy-start.3 = (bf16[256,4096]{1,0:T(8,128)(2,1)S(1)}, bf16[256,4096]{1,0:T(8,128)(2,1)}, u32[]{:S(2)}) copy-start(bf16[256,4096]{1,0:T(8,128)(2,1)} %all-gather.3.cloned.1.call-done) | copy-start | bytes 6291460
  47.2 2.6 %copy-start.13 = (bf16[4096,256]{1,0:T(8,128)(2,1)S(1)}, bf16[4096,256]{1,0:T(8,128)(2,1)}, u32[]{:S(2)}) copy-start(bf16[4096,256]{1,0:T(8,128)(2,1)} %param.13) | copy-start | bytes 6291460
  47.3 3.7 %copy-start.15 = (bf16[256,2,64]{2,0,1:T(8,128)(2,1)}, bf16[256,2,64]{2,0,1:T(8,128)(2,1)S(1)}, u32[]{:S(2)}) copy-start(bf16[256,2,64]{2,0,1:T(8,128)(2,1)S(1)} %get-tuple-element.37) | copy-start | bytes 196612
  49.8 1.4 %copy-start.25 = (f32[2,256,256,4]{2,1,3,0:T(8,128)}, f32[2,256,256,4]{2,1,3,0:T(8,128)S(1)}, u32[]{:S(2)}) copy-start(f32[2,256,256,4]{2,1,3,0:T(8,128)S(1)} %get-tuple-element.55) | copy-start | bytes 6291460
  49.8 1.4 %copy-start.27 = (f32[2,4,256]{2,1,0:T(4,128)}, f32[2,4,256]{2,1,0:T(4,128)S(1)}, u32[]{:S(2)}) copy-start(f32[2,4,256]{2,1,0:T(4,128)S(1)} %get-tuple-element.54) | copy-start | bytes 24580
  49.8 3.0 %slice-start = ((s8[8388608]{0:T(1024)(128)(4,1)}), s8[4194304]{0:T(1024)(128)(4,1)S(1)}, s32[]{:S(2)}) async-start(s8[8388608]{0:T(1024)(128)(4,1)} %bitcast.162), calls=%async_computation.3 | async-start | bytes 8388608
  51.0 0.8 copy-start.24
  51.1 3.1 %slice-start.1 = ((s8[8388608]{0:T(1024)(128)(4,1)}), s8[4194304]{0:T(1024)(128)(4,1)S(1)}, s32[]{:S(2)}) async-start(s8[8388608]{0:T(1024)(128)(4,1)} %bitcast.162), calls=%async_computation.4 | async-start | bytes 8388608
  61.9 7.7 %collective-permute-start.7 = (bf16[2,256,1024]{2,1,0:T(8,128)(2,1)}, bf16[2,256,1024]{2,1,0:T(8,128)(2,1)}, u32[]{:S(2)}, u32[]{:S(2)}) collective-permute-start(bf16[2,256,1024]{2,1,0:T(8,128)(2,1)} %pad_maximum_fusion), channel_id=1, source_target_pairs={{0,1},{1,0},{2,3},{3,2},{4,5},{5,4},{6,7},{7,6},{8,9},{9,8},{10,11... | collective-permute-start | bytes 3145736 | tf_op jit(solution)/shard_map/ppermute | solution.py:101
  70.8 2.7 %copy-start.7 = (bf16[256,1024]{0,1:T(8,128)(2,1)}, bf16[256,1024]{0,1:T(8,128)(2,1)S(1)}, u32[]{:S(2)}) copy-start(bf16[256,1024]{0,1:T(8,128)(2,1)S(1)} %copy.99) | copy-start | bytes 1572868
  71.0 2.5 %copy-start.10 = (bf16[256,8,64]{2,0,1:T(8,128)(2,1)S(1)}, bf16[256,8,64]{2,0,1:T(8,128)(2,1)}, u32[]{:S(2)}) copy-start(bf16[256,8,64]{2,0,1:T(8,128)(2,1)} %copy-done.9) | copy-start | bytes 786436
  71.0 2.5 %copy-start.12 = (bf16[256,8,64]{2,0,1:T(8,128)(2,1)S(1)}, bf16[256,8,64]{2,0,1:T(8,128)(2,1)}, u32[]{:S(2)}) copy-start(bf16[256,8,64]{2,0,1:T(8,128)(2,1)} %copy-done.11) | copy-start | bytes 786436
  73.5 0.9 copy-start.16
  80.1 15.0 %collective-permute-start.8 = (bf16[1,256,1024]{2,1,0:T(8,128)(2,1)}, bf16[1,256,1024]{2,1,0:T(8,128)(2,1)}, u32[]{:S(2)}, u32[]{:S(2)}) collective-permute-start(bf16[1,256,1024]{2,1,0:T(8,128)(2,1)} %fusion.23), channel_id=1, source_target_pairs={{0,2},{1,3},{2,0},{3,1},{4,6},{5,7},{6,4},{7,5},{8,10},{9,11},{10,... | collective-permute-start | bytes 1572872 | tf_op jit(solution)/shard_map/ppermute | solution.py:101
  90.9 1.0 copy-start.8
  90.9 1.0 copy-start.18
  91.0 1.8 %copy-start.26 = (f32[2,256,256,4]{2,1,3,0:T(8,128)S(1)}, f32[2,256,256,4]{2,1,3,0:T(8,128)}, u32[]{:S(2)}) copy-start(f32[2,256,256,4]{2,1,3,0:T(8,128)} %copy-done.25) | copy-start | bytes 6291460
  91.0 1.8 %copy-start.28 = (f32[2,4,256]{2,1,0:T(4,128)S(1)}, f32[2,4,256]{2,1,0:T(4,128)}, u32[]{:S(2)}) copy-start(f32[2,4,256]{2,1,0:T(4,128)} %copy-done.27) | copy-start | bytes 24580
  92.7 1.6 %copy-start.14 = (bf16[4096,256]{1,0:T(8,128)(2,1)S(1)}, bf16[4096,256]{1,0:T(8,128)(2,1)}, u32[]{:S(2)}) copy-start(bf16[4096,256]{1,0:T(8,128)(2,1)} %param.13) | copy-start | bytes 6291460
  94.3 1.0 copy-start.6
  95.1 4.4 %copy-start.1 = (f32[256,4096]{1,0:T(8,128)}, f32[256,4096]{1,0:T(8,128)S(1)}, u32[]{:S(2)}) copy-start(f32[256,4096]{1,0:T(8,128)S(1)} %convolution_add_fusion) | copy-start | bytes 12582916
  98.5 0.7 copy-start.23
  98.7 1.6 %copy-start.4 = (bf16[256,4096]{1,0:T(8,128)(2,1)S(1)}, bf16[256,4096]{1,0:T(8,128)(2,1)}, u32[]{:S(2)}) copy-start(bf16[256,4096]{1,0:T(8,128)(2,1)} %all-gather.3.cloned.1.call-done) | copy-start | bytes 6291460
  98.8 2.9 %collective-permute-start.9 = (bf16[2,256,1024]{2,1,0:T(8,128)(2,1)S(1)}, bf16[2,256,1024]{2,1,0:T(8,128)(2,1)}, u32[]{:S(2)}, u32[]{:S(2)}) collective-permute-start(bf16[2,256,1024]{2,1,0:T(8,128)(2,1)S(1)} %pad_maximum_fusion.1), channel_id=1, source_target_pairs={{0,1},{1,0},{2,3},{3,2},{4,5},{5,4},{6,7},{7,6},{8,9},{9,8},{10,11... | collective-permute-start | bytes 3145736 | tf_op jit(solution)/shard_map/ppermute | solution.py:101
  100.9 22.4 %copy-start.5 = (bf16[8,32,1024]{2,1,0:T(8,128)(2,1)S(1)}, bf16[8,32,1024]{2,1,0:T(8,128)(2,1)}, u32[]{:S(2)}) copy-start(bf16[8,32,1024]{2,1,0:T(8,128)(2,1)} %copy.98) | copy-start | bytes 1572868
  100.9 22.4 %dynamic-slice-start = ((f32[4096]{0:T(1024)}, s32[]{:T(128)}), f32[1024]{0:T(1024)S(1)}, s32[]{:S(2)}) async-start(f32[4096]{0:T(1024)} %param.10, s32[]{:T(128)} %select_n.110), calls=%async_computation.5 | async-start | bytes 8704 | tf_op jit(solution)/shard_map/dynamic_slice | solution.py:144
  100.9 22.4 %copy-start.20 = (f32[256]{0:T(256)S(1)}, f32[256]{0:T(256)}, u32[]{:S(2)}) copy-start(f32[256]{0:T(256)} %get-tuple-element.52) | copy-start | bytes 3076
  100.9 22.4 %copy-start.22 = (f32[256]{0:T(256)S(1)}, f32[256]{0:T(256)}, u32[]{:S(2)}) copy-start(f32[256]{0:T(256)} %copy-done.21) | copy-start | bytes 3076
  102.7 23.2 %all-to-all-start = ((bf16[8,32,1024]{2,1,0:T(8,128)(2,1)}), bf16[8,32,1024]{2,1,0:T(8,128)(2,1)}, u32[]{:S(2)}, u32[]{:S(2)}) async-start(bf16[8,32,1024]{2,1,0:T(8,128)(2,1)} %copy.112), calls=%async_computation | async-start | bytes 1048576 | tf_op jit(solution)/shard_map/all_to_all | solution.py:283
  109.4 13.8 %collective-permute-start.10 = (bf16[1,256,1024]{2,1,0:T(8,128)(2,1)S(1)}, bf16[1,256,1024]{2,1,0:T(8,128)(2,1)S(1)}, u32[]{:S(2)}, u32[]{:S(2)}) collective-permute-start(bf16[1,256,1024]{2,1,0:T(8,128)(2,1)S(1)} %fusion.24), channel_id=1, source_target_pairs={{0,2},{1,3},{2,0},{3,1},{4,6},{5,7},{6,4},{7,5},{8,10},{9,11},{10,... | collective-permute-start | bytes 1572872 | tf_op jit(solution)/shard_map/ppermute | solution.py:101
  110.9 11.3 %collective-permute-start.13 = (f32[256]{0:T(256)S(1)}, f32[256]{0:T(256)S(1)}, u32[]{:S(2)}, u32[]{:S(2)}) collective-permute-start(f32[256]{0:T(256)S(1)} %fusion.3), channel_id=1, source_target_pairs={{0,3},{1,2},{2,1},{3,0},{4,7},{5,6},{6,5},{7,4},{8,11},{9,10},{10,... | collective-permute-start | bytes 3080 | tf_op jit(solution)/shard_map/ppermute | solution.py:109
  110.9 12.3 %collective-permute-start.12 = (f32[256]{0:T(256)S(1)}, f32[256]{0:T(256)S(1)}, u32[]{:S(2)}, u32[]{:S(2)}) collective-permute-start(f32[256]{0:T(256)S(1)} %fusion.3), channel_id=1, source_target_pairs={{0,2},{1,3},{2,0},{3,1},{4,6},{5,7},{6,4},{7,5},{8,10},{9,11},{10,... | collective-permute-start | bytes 3080 | tf_op jit(solution)/shard_map/ppermute | solution.py:109
  112.2 11.1 %collective-permute-start.11 = (f32[256]{0:T(256)S(1)}, f32[256]{0:T(256)S(1)}, u32[]{:S(2)}, u32[]{:S(2)}) collective-permute-start(f32[256]{0:T(256)S(1)} %fusion.3), channel_id=1, source_target_pairs={{0,1},{1,0},{2,3},{3,2},{4,5},{5,4},{6,7},{7,6},{8,9},{9,8},{10,11... | collective-permute-start | bytes 3080 | tf_op jit(solution)/shard_map/ppermute | solution.py:109
Sparse Core Ops, SparseCore 0:
  9.6 25.2 all-gather.2
  36.5 22.5 all-gather.4

commit v17 on v12

--- a/solution.py
+++ b/solution.py
@@ -269,7 +269,6 @@
             preferred_element_type=jnp.float32,
         )
     )
-    output_home, normed_partial = lax.optimization_barrier((output_home, normed_partial))
     stat_partial = jnp.sum(normed_partial * norm_gain[None, :] * gathered_float, axis=1)
     home_blocks = output_home.reshape(block_count, home_rows, width_part)
     outgoing = jnp.einsum(

time: 135 us -> 136 us (level)
  other arithmetic: 22.8 us -> 19.6 us
  matrix products: 34.6 us -> 37.7 us
    reduce_sum x1 -> x0, other arithmetic: 2.82 us -> none  [per_device(): jnp.sum(normed_partial * norm_gain[None, :] * gathered_float, axis=1)]
    dot_general x1, matrix products: 0.65 us -> 3.04 us  [per_device(): jnp.einsum('kgqs,qkgd->skd', probs_low, grouped_gradient, preferred_eleme...]
    dot_general x1, matrix products: 2.48 us -> 0.75 us  [per_device(): jnp.einsum('qkgd,skd->kgqs', grouped_gradient, value_rows, preferred_elem...]
    ppermute x4, waiting for transfers between devices: 10.9 us -> 12.6 us  [scatter_features(): lax.ppermute((outgoing, extra), axis_name, _xor_pairs(size, bit))]
    dot_general x1, matrix products: 1.16 us -> 2.76 us  [per_device(): jnp.dot(normed_input, key_weight, preferred_element_type=jnp.float32)]
    unnamed x69 -> x67, local copies, waits for them, and re-layouts: 12 us -> 12.6 us
  transfers between devices with their start and end apart: 16 -> 16, of which waited for: 5 -> 4; matrix products, arithmetic and copies ran while one was open for 43% -> 44% of each run, Pallas kernels for 0% -> 0%
where the time goes in v17:
time: 136 us; the launch traced here: 135 us
  matrix products  37.7 us (28%)
  local copies, waits for them, and re-layouts  25.9 us (19%)
  starting transfers between devices  20.6 us (15%)
  other arithmetic  19.6 us (14%)
  waiting for transfers between devices  16.1 us (12%)
  between operations  14.8 us (11%)
    unnamed x67, local copies, waits for them, and re-layouts  12.6 us
    ppermute x4, waiting for transfers between devices, scatter_features(): lax.ppermute((outgoing, extra), axis_name, _xor_pairs(size, bit))  12.6 us
    ppermute x7, starting transfers between devices, per_device(): returned.append(lax.ppermute(piece, 'dp', pairs))  12.5 us
    dot_general x1, matrix products, per_device(): lax.dot_general(grad_full, w_out, (((1,), (1,)), ((), ())), preferred_ele...  7.42 us
    dot_general x1, matrix products, per_device(): jnp.dot(normed_input, w_query, preferred_element_type=jnp.float32)  7.1 us
    dot_general x1, matrix products, per_device(): lax.dot_general(grad_query.reshape(token_row_count, query_width), w_query...  5.9 us
    another operation x8, local copies, waits for them, and re-layouts, per_device(): returned = jnp.stack(returned)  5.59 us
    dot_general x1, matrix products, per_device(): jnp.dot(attended_flat, w_out, preferred_element_type=jnp.float32)  4.53 us
  transfers between devices with their start and end apart: 16, of which 4 were waited for; matrix products, arithmetic and copies ran while one was open for 44% of the time, Pallas kernels for 0%

profile of v17, /device:TPU:0, one launch (start us, length us, event | category | flops | bytes accessed | tf_op | source)
XLA Modules:
  0.0 134.6 jit_solution(3806723822536161108)
XLA Ops:
  7.2 0.7 all-gather.3.cloned.1.call-update
  8.1 1.1 dynamic-slice_bitcast_fusion
  9.2 6.0 %collective-permute-start.6 = (bf16[32,1024]{1,0:T(8,128)(2,1)S(1)}, bf16[32,1024]{1,0:T(8,128)(2,1)S(1)}, u32[]{:S(2)}, u32[]{:S(2)}) collective-permute-start(bf16[32,1024]{1,0:T(8,128)(2,1)S(1)} %get-tuple-element.32), channel_id=1, source_target_pairs={{0,28},{4,0},{8,4},{12,8},{16,12},{20,16},{24,20},{28,24},{1,29},{... | collective-permute-start | bytes 196616 | tf_op jit(solution)/shard_map/ppermute | solution.py:159
  15.2 0.4 collective-permute-start.5
  15.7 3.0 %collective-permute-start.3 = (bf16[32,1024]{1,0:T(8,128)(2,1)S(1)}, bf16[32,1024]{1,0:T(8,128)(2,1)S(1)}, u32[]{:S(2)}, u32[]{:S(2)}) collective-permute-start(bf16[32,1024]{1,0:T(8,128)(2,1)S(1)} %get-tuple-element.35), channel_id=1, source_target_pairs={{0,16},{4,20},{8,24},{12,28},{16,0},{20,4},{24,8},{28,12},{1,17},{... | collective-permute-start | bytes 196616 | tf_op jit(solution)/shard_map/ppermute | solution.py:159
  18.7 0.8 reduce-window.8
  19.6 0.5 multiply_cosine_fusion
  20.2 0.7 fusion.31
  21.0 1.9 %collective-permute-start.1 = (bf16[32,1024]{1,0:T(8,128)(2,1)S(1)}, bf16[32,1024]{1,0:T(8,128)(2,1)S(1)}, u32[]{:S(2)}, u32[]{:S(2)}) collective-permute-start(bf16[32,1024]{1,0:T(8,128)(2,1)S(1)} %get-tuple-element.37), channel_id=1, source_target_pairs={{0,8},{4,12},{8,16},{12,20},{16,24},{20,28},{24,0},{28,4},{1,9},{5... | collective-permute-start | bytes 196616 | tf_op jit(solution)/shard_map/ppermute | solution.py:159
  22.9 1.1 collective-permute-start
  24.0 1.3 and_select_fusion
  25.8 2.8 %collective-permute-done.2 = bf16[32,1024]{1,0:T(8,128)(2,1)S(1)} collective-permute-done((bf16[32,1024]{1,0:T(8,128)(2,1)S(1)}, bf16[32,1024]{1,0:T(8,128)(2,1)S(1)}, u32[]{:S(2)}, u32[]{:S(2)}) %collective-permute-start.2) | collective-permute-done | bytes 65568 | tf_op jit(solution)/shard_map/ppermute | solution.py:159
  28.6 0.8 copy.93
  29.3 0.8 copy.92
  30.1 0.8 copy.91
  30.8 2.9 %stack.58 = bf16[8,32,1024]{2,0,1:T(8,128)(2,1)S(1)} concatenate(bf16[1,32,1024]{2,0,1:T(2,128)(2,1)S(1)} %copy.132, bf16[1,32,1024]{2,0,1:T(2,128)(2,1)} %copy.91, bf16[1,32,1024]{2,0,1:T(2,128)(2,1)} %copy.92, bf16[1,32,1024]{2,0,1:T(2,128)(2,1)} %copy.93, bf16[1,32,1024]{2,0,1:T(2,128)(2,1)S(1)} %copy.94, bf16[1,32,1024]{2,0,1:T(2,128)(2,1)S(1)} %copy.95, ...), dimensions={0} | concatenate | bytes 1048576 | tf_op jit(solution)/shard_map/stack | solution.py:160
  33.8 0.4 convolution_convert_fusion.3
  34.1 1.1 copy.98
  35.3 2.2 %fusion = f32[256]{0:T(256)S(1)} fusion(bf16[256,4096]{1,0:T(8,128)(2,1)} %all-gather.3.cloned.1.call-done), kind=kLoop, calls=%fused_computation.5 | loop fusion | flops 3145472 | bytes 2098176 | tf_op jit(solution)/shard_map/reduce_sum | solution.py:183
  37.5 0.6 multiply_multiply_fusion
  38.1 2.8 %fusion.48 = f32[256,256]{0,1:T(8,128)S(1)} fusion(bf16[4096,256]{1,0:T(8,128)(2,1)} %param.12, bf16[256,4096]{1,0:T(8,128)(2,1)S(1)} %copy-done.2, f32[4096]{0:T(1024)S(1)} %copy-done.17, f32[256]{0:T(256)S(1)} %get-tuple-element.45), kind=kOutput, calls=%fused_computation.111 | convolution fusion | flops 541065216 | bytes 4473856 | tf_op jit(solution)/shard_map/dot_general | solution.py:186
  41.2 7.1 %convolution_bitcast_fusion = f32[32,8,8,128]{3,1,2,0:T(8,128)S(1)} fusion(bf16[4096,1024]{1,0:T(8,128)(2,1)} %param.11, bf16[256,4096]{1,0:T(8,128)(2,1)} %all-gather.3.cloned.1.call-done, f32[4096]{0:T(1024)S(1)} %copy-done.17, f32[256]{0:T(256)S(1)} %get-tuple-element.45), kind=kOutput, calls=%fused_computation.16 | convolution fusion | flops 2151677952 | bytes 11551744 | tf_op jit(solution)/shard_map/dot_general | solution.py:185
  48.5 0.5 subtract_convert_fusion.1
  49.3 0.6 copy-done.7
  50.1 0.9 fusion.7
  51.2 1.2 convolution_convert_fusion.4
  52.5 0.7 convolution_convert_fusion.1
  53.2 1.0 slice-done
  54.2 1.4 %slice-done.1 = s8[4194304]{0:T(1024)(128)(4,1)S(1)} async-done(((s8[8388608]{0:T(1024)(128)(4,1)}), s8[4194304]{0:T(1024)(128)(4,1)S(1)}, s32[]{:S(2)}) %slice-start.1) | async-done | bytes 4194328
  55.6 4.5 %fusion.55 = f32[256,4096]{1,0:T(8,128)} fusion(bf16[256,1024]{0,1:T(8,128)(2,1)S(1)} %bitcast.167, bf16[1024,4096]{1,0:T(8,128)(2,1)S(1)} %bitcast.163), kind=kOutput, calls=%fused_computation.114 | convolution fusion | flops 2147483648 | bytes 13107200 | tf_op jit(solution)/shard_map/dot_general | solution.py:213
  60.1 1.7 %fusion.19 = (bf16[1,256,1024]{2,1,0:T(8,128)(2,1)S(1)}, bf16[1,256,1024]{2,1,0:T(8,128)(2,1)S(1)}) fusion(f32[256,4096]{1,0:T(8,128)} %fusion.55, s32[]{:T(128)S(6)} %select_n.110, s32[]{:T(128)S(6)} %select_n.111), kind=kLoop, calls=%fused_computation.54 | loop fusion | bytes 2097160 | tf_op jit(solution)/shard_map/stack | solution.py:100
  61.8 1.1 pad_maximum_fusion
  62.9 7.4 %convolution_convert_fusion = bf16[256,1024]{1,0:T(8,128)(2,1)} fusion(bf16[256,4096]{1,0:T(8,128)(2,1)} %all-gather.5.cloned.1.call-done, bf16[1024,4096]{1,0:T(8,128)(2,1)} %param.14), kind=kOutput, calls=%fused_computation.19 | convolution fusion | flops 2147745792 | bytes 11010048 | tf_op jit(solution)/shard_map/dot_general | solution.py:216
  70.4 1.2 copy.99
  71.8 3.0 %fusion.10 = bf16[2,128,256]{2,1,0:T(8,128)(2,1)} fusion(bf16[256,2,4,128]{0,3,2,1:T(8,128)(2,1)S(1)} %bitcast.168, f32[2,256,256,4]{2,1,3,0:T(8,128)} %copy-done.24, f32[2,4,256]{2,1,0:T(4,128)} %copy-done.26, pred[256,256]{0,1:T(8,128)(4,1)} %fusion.31), kind=kOutput, calls=%fused_computation.27 | convolution fusion | flops 136380416 | bytes 2826240 | tf_op jit(solution)/shard_map/kgqs,qkgd->skd/dot_general | solution.py:244
  74.9 0.8 fusion.5
  76.1 0.5 fusion.9
  76.6 0.4 copy-done.13
  77.0 0.4 convolution_multiply_fusion
  77.4 1.1 fusion.53
  78.9 1.5 %copy.134 = f32[256,8,64]{2,1,0:T(8,128)S(1)} copy(f32[256,8,64]{0,2,1:T(8,128)} %get-tuple-element.26) | data formatting | bytes 1048576
  80.4 2.3 %fusion.23 = bf16[1,256,1024]{2,1,0:T(8,128)(2,1)} fusion(f32[256,4096]{1,0:T(8,128)} %fusion.55, s32[]{:T(128)S(6)} %select_n.113, bf16[2,256,1024]{2,1,0:T(8,128)(2,1)} %collective-permute-done.7), kind=kLoop, calls=%fused_computation.58 | loop fusion | flops 786432 | bytes 2097156 | tf_op jit(solution)/shard_map/convert_element_type | solution.py:100
  82.7 1.5 %collective-permute-start.9 = (bf16[1,256,1024]{2,1,0:T(8,128)(2,1)}, bf16[1,256,1024]{2,1,0:T(8,128)(2,1)}, u32[]{:S(2)}, u32[]{:S(2)}) collective-permute-start(bf16[1,256,1024]{2,1,0:T(8,128)(2,1)} %fusion.23), channel_id=1, source_target_pairs={{0,2},{1,3},{2,0},{3,1},{4,6},{5,7},{6,4},{7,5},{8,10},{9,11},{10,... | collective-permute-start | bytes 1572872 | tf_op jit(solution)/shard_map/ppermute | solution.py:102
  84.2 2.4 %copy.133 = f32[256,8,64]{2,1,0:T(8,128)} copy(f32[256,8,64]{0,2,1:T(8,128)} %get-tuple-element.27) | data formatting | bytes 1048576
  86.6 1.5 %add_convert_fusion = (bf16[256,8,64]{2,1,0:T(8,128)(2,1)S(1)}, bf16[256,8,64]{2,1,0:T(8,128)(2,1)S(1)}) fusion(f32[256,8,64]{2,1,0:T(8,128)S(1)} %copy.134, f32[256,8,64]{2,1,0:T(8,128)} %copy.133, f32[256,64]{1,0:T(8,128)S(1)} %get-tuple-element.43, f32[256,64]{1,0:T(8,128)S(1)} %get-tuple-element.42), kind=kLoop, calls=%fused_computation.48 | loop fusion | flops 1048576 | bytes 1703936 | tf_op jit(solution)/shard_map/convert.12
  88.1 0.3 pad_maximum_fusion.3
  88.4 5.9 %fusion.25 = f32[256,4096]{1,0:T(8,128)S(1)} fusion(bf16[4096,1024]{1,0:T(8,128)(2,1)} %param.11, bf16[32,8,8,128]{3,2,1,0:T(8,128)(2,1)S(1)} %bitcast.175), kind=kOutput, calls=%fused_computation.60 | convolution fusion | flops 2147483648 | bytes 13107200 | tf_op jit(solution)/shard_map/dot_general | solution.py:253
  94.3 0.8 convolution_add_fusion.1
  95.1 0.8 copy-done.4
  95.9 1.1 fusion.3
  97.1 1.1 pad_maximum_fusion.1
  98.2 1.1 copy-done.1
  99.5 1.8 %fusion.11 = bf16[256,1024]{1,0:T(8,128)(2,1)S(1)} fusion(bf16[256,1024]{1,0:T(8,128)(2,1)S(1)} %copy-done.6, f32[256,4096]{1,0:T(8,128)} %fusion.55, s32[]{:T(128)} %select_n.112, bf16[1,256,1024]{2,1,0:T(8,128)(2,1)} %collective-permute-done.9, bf16[2,256,1024]{2,1,0:T(8,128)(2,1)} %collective-permute-done.7), kind=kLoop, calls=%fused_computation.29 | loop fusion | flops 1835008 | bytes 3145732 | tf_op jit(solution)/shard_map/convert_element_type | solution.py:225
  101.4 0.4 convolution_convert_fusion.2
  101.8 0.5 collective-permute-done.8
  102.3 1.1 copy.112
  103.4 4.2 %all-to-all-start = ((bf16[8,32,1024]{2,1,0:T(8,128)(2,1)}), bf16[8,32,1024]{2,1,0:T(8,128)(2,1)}, u32[]{:S(2)}, u32[]{:S(2)}) async-start(bf16[8,32,1024]{2,1,0:T(8,128)(2,1)} %copy.112), calls=%async_computation | async-start | bytes 1048576 | tf_op jit(solution)/shard_map/all_to_all | solution.py:280
  107.5 1.5 %fusion.24 = bf16[1,256,1024]{2,1,0:T(8,128)(2,1)S(1)} fusion(f32[256,4096]{1,0:T(8,128)} %copy-done.1, s32[]{:T(128)S(6)} %select_n.113, bf16[2,256,1024]{2,1,0:T(8,128)(2,1)} %collective-permute-done.8), kind=kLoop, calls=%fused_computation.59 | loop fusion | flops 786432 | bytes 2097156 | tf_op jit(solution)/shard_map/convert_element_type | solution.py:100
  109.1 1.6 %collective-permute-start.10 = (bf16[1,256,1024]{2,1,0:T(8,128)(2,1)S(1)}, bf16[1,256,1024]{2,1,0:T(8,128)(2,1)S(1)}, u32[]{:S(2)}, u32[]{:S(2)}) collective-permute-start(bf16[1,256,1024]{2,1,0:T(8,128)(2,1)S(1)} %fusion.24), channel_id=1, source_target_pairs={{0,2},{1,3},{2,0},{3,1},{4,6},{5,7},{6,4},{7,5},{8,10},{9,11},{10,... | collective-permute-start | bytes 1572872 | tf_op jit(solution)/shard_map/ppermute | solution.py:104
  110.6 1.1 collective-permute-done.11
  111.8 0.5 collective-permute-start.12
  112.3 10.9 %collective-permute-done.12 = f32[256]{0:T(256)S(1)} collective-permute-done((f32[256]{0:T(256)S(1)}, f32[256]{0:T(256)S(1)}, u32[]{:S(2)}, u32[]{:S(2)}) %collective-permute-start.12) | collective-permute-done | bytes 1056 | tf_op jit(solution)/shard_map/ppermute | solution.py:104
  123.3 2.6 %fusion.14 = bf16[256,1024]{1,0:T(8,128)(2,1)} fusion(bf16[256,1024]{1,0:T(8,128)(2,1)S(1)} %copy-done.6, f32[256,4096]{1,0:T(8,128)} %copy-done.1, s32[]{:T(128)} %select_n.112, bf16[1,256,1024]{2,1,0:T(8,128)(2,1)S(1)} %collective-permute-done.10, f32[256]{0:T(256)S(1)} %add_multiply_fusion, f32[256]{0:T(256)S(1)} %copy-done.18, ...), kind=kLoop, calls=%fused_computation.32 | loop fusion | flops 3407872 | bytes 3677188 | tf_op jit(solution)/shard_map/convert_element_type | solution.py:290
  125.9 1.9 %copy.144 = bf16[256,1024]{1,0:T(8,128)(2,1)} copy(bf16[256,1024]{1,0:T(8,128)(2,1)} %bitcast.56) | data formatting | bytes 1048576
  (99 shorter events, 3.4 us)
Async XLA Ops:
  7.2 43.8 %copy-start = (bf16[4096,256]{1,0:T(8,128)(2,1)S(1)}, bf16[4096,256]{1,0:T(8,128)(2,1)}, u32[]{:S(2)}) copy-start(bf16[4096,256]{1,0:T(8,128)(2,1)} %param.13) | copy-start | bytes 6291460
  7.2 28.1 %all-gather.3.cloned.1.call-start = ((), (), s32[]{:S(2)}) async-start(), calls=%async_computation.1 | async-start | bytes 2621440 | tf_op jit(solution)/shard_map/all_gather | solution.py:181
  7.9 52.2 %all-gather.5.cloned.1.call-start = ((), (), s32[]{:S(2)}) async-start(), calls=%async_computation.2 | async-start | bytes 2621440 | tf_op jit(solution)/shard_map/all_gather | solution.py:214
  9.2 11.8 %collective-permute-start.6 = (bf16[32,1024]{1,0:T(8,128)(2,1)S(1)}, bf16[32,1024]{1,0:T(8,128)(2,1)S(1)}, u32[]{:S(2)}, u32[]{:S(2)}) collective-permute-start(bf16[32,1024]{1,0:T(8,128)(2,1)S(1)} %get-tuple-element.32), channel_id=1, source_target_pairs={{0,28},{4,0},{8,4},{12,8},{16,12},{20,16},{24,20},{28,24},{1,29},{... | collective-permute-start | bytes 196616 | tf_op jit(solution)/shard_map/ppermute | solution.py:159
  15.2 7.7 %collective-permute-start.5 = (bf16[32,1024]{1,0:T(8,128)(2,1)S(1)}, bf16[32,1024]{1,0:T(8,128)(2,1)S(1)}, u32[]{:S(2)}, u32[]{:S(2)}) collective-permute-start(bf16[32,1024]{1,0:T(8,128)(2,1)S(1)} %get-tuple-element.33), channel_id=1, source_target_pairs={{0,24},{4,28},{8,0},{12,4},{16,8},{20,12},{24,16},{28,20},{1,25},{... | collective-permute-start | bytes 196616 | tf_op jit(solution)/shard_map/ppermute | solution.py:159
  15.7 9.9 %collective-permute-start.4 = (bf16[32,1024]{1,0:T(8,128)(2,1)S(1)}, bf16[32,1024]{1,0:T(8,128)(2,1)S(1)}, u32[]{:S(2)}, u32[]{:S(2)}) collective-permute-start(bf16[32,1024]{1,0:T(8,128)(2,1)S(1)} %get-tuple-element.34), channel_id=1, source_target_pairs={{0,20},{4,24},{8,28},{12,0},{16,4},{20,8},{24,12},{28,16},{1,21},{... | collective-permute-start | bytes 196616 | tf_op jit(solution)/shard_map/ppermute | solution.py:159
  15.7 10.0 %collective-permute-start.3 = (bf16[32,1024]{1,0:T(8,128)(2,1)S(1)}, bf16[32,1024]{1,0:T(8,128)(2,1)S(1)}, u32[]{:S(2)}, u32[]{:S(2)}) collective-permute-start(bf16[32,1024]{1,0:T(8,128)(2,1)S(1)} %get-tuple-element.35), channel_id=1, source_target_pairs={{0,16},{4,20},{8,24},{12,28},{16,0},{20,4},{24,8},{28,12},{1,17},{... | collective-permute-start | bytes 196616 | tf_op jit(solution)/shard_map/ppermute | solution.py:159
  18.7 9.9 %collective-permute-start.2 = (bf16[32,1024]{1,0:T(8,128)(2,1)S(1)}, bf16[32,1024]{1,0:T(8,128)(2,1)S(1)}, u32[]{:S(2)}, u32[]{:S(2)}) collective-permute-start(bf16[32,1024]{1,0:T(8,128)(2,1)S(1)} %get-tuple-element.36), channel_id=1, source_target_pairs={{0,12},{4,16},{8,20},{12,24},{16,28},{20,0},{24,4},{28,8},{1,13},{... | collective-permute-start | bytes 196616 | tf_op jit(solution)/shard_map/ppermute | solution.py:159
  21.0 8.3 %collective-permute-start.1 = (bf16[32,1024]{1,0:T(8,128)(2,1)S(1)}, bf16[32,1024]{1,0:T(8,128)(2,1)S(1)}, u32[]{:S(2)}, u32[]{:S(2)}) collective-permute-start(bf16[32,1024]{1,0:T(8,128)(2,1)S(1)} %get-tuple-element.37), channel_id=1, source_target_pairs={{0,8},{4,12},{8,16},{12,20},{16,24},{20,28},{24,0},{28,4},{1,9},{5... | collective-permute-start | bytes 196616 | tf_op jit(solution)/shard_map/ppermute | solution.py:159
  22.9 7.2 %collective-permute-start = (bf16[32,1024]{1,0:T(8,128)(2,1)S(1)}, bf16[32,1024]{1,0:T(8,128)(2,1)S(1)}, u32[]{:S(2)}, u32[]{:S(2)}) collective-permute-start(bf16[32,1024]{1,0:T(8,128)(2,1)S(1)} %get-tuple-element.38), channel_id=1, source_target_pairs={{0,4},{4,8},{8,12},{12,16},{16,20},{20,24},{24,28},{28,0},{1,5},{5... | collective-permute-start | bytes 196616 | tf_op jit(solution)/shard_map/ppermute | solution.py:159
  34.1 4.0 %copy-start.17 = (f32[4096]{0:T(1024)S(1)}, f32[4096]{0:T(1024)}, u32[]{:S(2)}) copy-start(f32[4096]{0:T(1024)} %param.10) | copy-start | bytes 49156
  35.3 2.8 %copy-start.2 = (bf16[256,4096]{1,0:T(8,128)(2,1)S(1)}, bf16[256,4096]{1,0:T(8,128)(2,1)}, u32[]{:S(2)}) copy-start(bf16[256,4096]{1,0:T(8,128)(2,1)} %all-gather.3.cloned.1.call-done) | copy-start | bytes 6291460
  38.1 12.8 %copy-start.19 = (f32[256]{0:T(256)}, f32[256]{0:T(256)S(1)}, u32[]{:S(2)}) copy-start(f32[256]{0:T(256)S(1)} %get-tuple-element.45) | copy-start | bytes 3076
  49.0 1.1 copy-start.15
  49.1 0.8 copy-start.7
  49.2 0.9 copy-start.9
  49.2 2.0 %copy-start.3 = (bf16[256,4096]{1,0:T(8,128)(2,1)S(1)}, bf16[256,4096]{1,0:T(8,128)(2,1)}, u32[]{:S(2)}) copy-start(bf16[256,4096]{1,0:T(8,128)(2,1)} %all-gather.3.cloned.1.call-done) | copy-start | bytes 6291460
  49.3 3.1 %copy-start.12 = (bf16[256,2,64]{2,0,1:T(8,128)(2,1)}, bf16[256,2,64]{2,0,1:T(8,128)(2,1)S(1)}, u32[]{:S(2)}) copy-start(bf16[256,2,64]{2,0,1:T(8,128)(2,1)S(1)} %get-tuple-element.29) | copy-start | bytes 196612
  51.2 1.3 copy-start.24
  51.2 1.3 copy-start.26
  51.2 3.0 %slice-start = ((s8[8388608]{0:T(1024)(128)(4,1)}), s8[4194304]{0:T(1024)(128)(4,1)S(1)}, s32[]{:S(2)}) async-start(s8[8388608]{0:T(1024)(128)(4,1)} %bitcast.162), calls=%async_computation.3 | async-start | bytes 8388608
  52.4 0.8 copy-start.22
  52.5 3.1 %slice-start.1 = ((s8[8388608]{0:T(1024)(128)(4,1)}), s8[4194304]{0:T(1024)(128)(4,1)S(1)}, s32[]{:S(2)}) async-start(s8[8388608]{0:T(1024)(128)(4,1)} %bitcast.162), calls=%async_computation.4 | async-start | bytes 8388608
  62.9 7.4 %collective-permute-start.7 = (bf16[2,256,1024]{2,1,0:T(8,128)(2,1)}, bf16[2,256,1024]{2,1,0:T(8,128)(2,1)}, u32[]{:S(2)}, u32[]{:S(2)}) collective-permute-start(bf16[2,256,1024]{2,1,0:T(8,128)(2,1)} %pad_maximum_fusion), channel_id=1, source_target_pairs={{0,1},{1,0},{2,3},{3,2},{4,5},{5,4},{6,7},{7,6},{8,9},{9,8},{10,11... | collective-permute-start | bytes 3145736 | tf_op jit(solution)/shard_map/ppermute | solution.py:102
  71.8 3.1 %copy-start.16 = (pred[256,256]{0,1:T(8,128)(4,1)S(1)}, pred[256,256]{0,1:T(8,128)(4,1)}, u32[]{:S(2)}) copy-start(pred[256,256]{0,1:T(8,128)(4,1)} %fusion.31) | copy-start | bytes 196612
  71.8 3.1 %copy-start.23 = (bf16[256,256]{0,1:T(8,128)(2,1)S(1)}, bf16[256,256]{0,1:T(8,128)(2,1)}, u32[]{:S(2)}) copy-start(bf16[256,256]{0,1:T(8,128)(2,1)} %copy-done.22) | copy-start | bytes 393220
  71.8 3.1 %copy-start.25 = (f32[2,256,256,4]{2,1,3,0:T(8,128)S(1)}, f32[2,256,256,4]{2,1,3,0:T(8,128)}, u32[]{:S(2)}) copy-start(f32[2,256,256,4]{2,1,3,0:T(8,128)} %copy-done.24) | copy-start | bytes 6291460
  71.8 3.1 %copy-start.27 = (f32[2,4,256]{2,1,0:T(4,128)S(1)}, f32[2,4,256]{2,1,0:T(4,128)}, u32[]{:S(2)}) copy-start(f32[2,4,256]{2,1,0:T(4,128)} %copy-done.26) | copy-start | bytes 24580
  74.9 1.0 copy-start.8
  74.9 1.2 copy-start.10
  76.1 0.9 copy-start.13
  82.7 16.8 %collective-permute-start.9 = (bf16[1,256,1024]{2,1,0:T(8,128)(2,1)}, bf16[1,256,1024]{2,1,0:T(8,128)(2,1)}, u32[]{:S(2)}, u32[]{:S(2)}) collective-permute-start(bf16[1,256,1024]{2,1,0:T(8,128)(2,1)} %fusion.23), channel_id=1, source_target_pairs={{0,2},{1,3},{2,0},{3,1},{4,6},{5,7},{6,4},{7,5},{8,10},{9,11},{10,... | collective-permute-start | bytes 1572872 | tf_op jit(solution)/shard_map/ppermute | solution.py:102
  88.4 5.9 %copy-start.11 = (bf16[4096,256]{1,0:T(8,128)(2,1)S(1)}, bf16[4096,256]{1,0:T(8,128)(2,1)}, u32[]{:S(2)}) copy-start(bf16[4096,256]{1,0:T(8,128)(2,1)} %param.12) | copy-start | bytes 6291460
  94.3 1.6 %copy-start.4 = (bf16[256,4096]{1,0:T(8,128)(2,1)S(1)}, bf16[256,4096]{1,0:T(8,128)(2,1)}, u32[]{:S(2)}) copy-start(bf16[256,4096]{1,0:T(8,128)(2,1)} %all-gather.3.cloned.1.call-done) | copy-start | bytes 6291460
  94.3 1.6 %copy-start.14 = (bf16[2,128,256]{2,1,0:T(8,128)(2,1)S(1)}, bf16[2,128,256]{2,1,0:T(8,128)(2,1)}, u32[]{:S(2)}) copy-start(bf16[2,128,256]{2,1,0:T(8,128)(2,1)} %fusion.10) | copy-start | bytes 393220
  96.9 2.3 %copy-start.1 = (f32[256,4096]{1,0:T(8,128)}, f32[256,4096]{1,0:T(8,128)S(1)}, u32[]{:S(2)}) copy-start(f32[256,4096]{1,0:T(8,128)S(1)} %get-tuple-element.49) | copy-start | bytes 12582916
  97.0 2.6 %copy-start.6 = (bf16[256,1024]{1,0:T(8,128)(2,1)S(1)}, bf16[256,1024]{1,0:T(8,128)(2,1)}, u32[]{:S(2)}) copy-start(bf16[256,1024]{1,0:T(8,128)(2,1)} %param.9) | copy-start | bytes 1572868
  99.3 2.1 %copy-start.21 = (s32[8]{0:T(128)S(1)}, s32[8]{0:T(128)}, u32[]{:S(2)}) copy-start(s32[8]{0:T(128)} %get-tuple-element.17) | copy-start | bytes 100
  99.3 3.0 %collective-permute-start.8 = (bf16[2,256,1024]{2,1,0:T(8,128)(2,1)}, bf16[2,256,1024]{2,1,0:T(8,128)(2,1)}, u32[]{:S(2)}, u32[]{:S(2)}) collective-permute-start(bf16[2,256,1024]{2,1,0:T(8,128)(2,1)} %pad_maximum_fusion.1), channel_id=1, source_target_pairs={{0,1},{1,0},{2,3},{3,2},{4,5},{5,4},{6,7},{7,6},{8,9},{9,8},{10,11... | collective-permute-start | bytes 3145736 | tf_op jit(solution)/shard_map/ppermute | solution.py:104
  101.8 21.5 %copy-start.5 = (bf16[8,32,1024]{2,1,0:T(8,128)(2,1)S(1)}, bf16[8,32,1024]{2,1,0:T(8,128)(2,1)}, u32[]{:S(2)}) copy-start(bf16[8,32,1024]{2,1,0:T(8,128)(2,1)} %copy.98) | copy-start | bytes 1572868
  101.8 21.5 %dynamic-slice-start = ((f32[4096]{0:T(1024)}, s32[]{:T(128)}), f32[1024]{0:T(1024)S(1)}, s32[]{:S(2)}) async-start(f32[4096]{0:T(1024)} %param.10, s32[]{:T(128)} %select_n.112), calls=%async_computation.5 | async-start | bytes 8704 | tf_op jit(solution)/shard_map/dynamic_slice | solution.py:142
  101.8 21.5 %copy-start.18 = (f32[256]{0:T(256)S(1)}, f32[256]{0:T(256)}, u32[]{:S(2)}) copy-start(f32[256]{0:T(256)} %get-tuple-element.44) | copy-start | bytes 3076
  101.8 21.5 %copy-start.20 = (f32[256]{0:T(256)S(1)}, f32[256]{0:T(256)}, u32[]{:S(2)}) copy-start(f32[256]{0:T(256)} %copy-done.19) | copy-start | bytes 3076
  103.4 22.5 %all-to-all-start = ((bf16[8,32,1024]{2,1,0:T(8,128)(2,1)}), bf16[8,32,1024]{2,1,0:T(8,128)(2,1)}, u32[]{:S(2)}, u32[]{:S(2)}) async-start(bf16[8,32,1024]{2,1,0:T(8,128)(2,1)} %copy.112), calls=%async_computation | async-start | bytes 1048576 | tf_op jit(solution)/shard_map/all_to_all | solution.py:280
  109.1 14.2 %collective-permute-start.10 = (bf16[1,256,1024]{2,1,0:T(8,128)(2,1)S(1)}, bf16[1,256,1024]{2,1,0:T(8,128)(2,1)S(1)}, u32[]{:S(2)}, u32[]{:S(2)}) collective-permute-start(bf16[1,256,1024]{2,1,0:T(8,128)(2,1)S(1)} %fusion.24), channel_id=1, source_target_pairs={{0,2},{1,3},{2,0},{3,1},{4,6},{5,7},{6,4},{7,5},{8,10},{9,11},{10,... | collective-permute-start | bytes 1572872 | tf_op jit(solution)/shard_map/ppermute | solution.py:104
  110.6 1.1 collective-permute-start.11
  111.8 11.5 %collective-permute-start.12 = (f32[256]{0:T(256)S(1)}, f32[256]{0:T(256)S(1)}, u32[]{:S(2)}, u32[]{:S(2)}) collective-permute-start(f32[256]{0:T(256)S(1)} %add.200), channel_id=1, source_target_pairs={{0,2},{1,3},{2,0},{3,1},{4,6},{5,7},{6,4},{7,5},{8,10},{9,11},{10,... | collective-permute-start | bytes 3080 | tf_op jit(solution)/shard_map/ppermute | solution.py:104
Sparse Core Ops, SparseCore 0:
  9.6 25.2 all-gather.2
  36.5 22.5 all-gather.4

commit v18 on v12

--- a/solution.py
+++ b/solution.py
@@ -281,6 +281,7 @@
     relaid = lax.all_to_all(outgoing, "dp", split_axis=0, concat_axis=0, tiled=True).reshape(
         token_row_count, width_part
     )
+    relaid, stat_sum = lax.optimization_barrier((relaid, stat_sum))
     stat = stat_sum / full_width
     cubed = inverse * inverse * inverse
     grad_x = (

time: 135 us -> 138 us (1.022)
  transfers between devices with their start and end apart: 16 -> 16, of which waited for: 5 -> 5; matrix products, arithmetic and copies ran while one was open for 43% -> 41% of each run, Pallas kernels for 0% -> 0%
where the time goes in v18:
time: 138 us; the launch traced here: 137 us
  matrix products  34.5 us (25%)
  local copies, waits for them, and re-layouts  26.6 us (19%)
  other arithmetic  23.8 us (17%)
  starting transfers between devices  21.1 us (15%)
  waiting for transfers between devices  15.8 us (11%)
  between operations  14.8 us (11%)
    unnamed x69, local copies, waits for them, and re-layouts  13.2 us
    ppermute x7, starting transfers between devices, per_device(): returned.append(lax.ppermute(piece, 'dp', pairs))  12.5 us
    ppermute x4, waiting for transfers between devices, scatter_features(): lax.ppermute((outgoing, extra), axis_name, _xor_pairs(size, bit))  11.2 us
    dot_general x1, matrix products, per_device(): lax.dot_general(grad_full, w_out, (((1,), (1,)), ((), ())), preferred_ele...  7.41 us
    dot_general x1, matrix products, per_device(): jnp.dot(normed_input, w_query, preferred_element_type=jnp.float32)  6.54 us
    dot_general x1, matrix products, per_device(): lax.dot_general(grad_query.reshape(token_row_count, query_width), w_query...  5.76 us
    all_to_all x1, starting transfers between devices, per_device(): lax.all_to_all(outgoing, 'dp', split_axis=0, concat_axis=0, tiled=True)  5.74 us
    another operation x8, local copies, waits for them, and re-layouts, per_device(): returned = jnp.stack(returned)  5.59 us
  transfers between devices with their start and end apart: 16, of which 5 were waited for; matrix products, arithmetic and copies ran while one was open for 41% of the time, Pallas kernels for 0%

profile of v18, /device:TPU:0, one launch (start us, length us, event | category | flops | bytes accessed | tf_op | source)
XLA Modules:
  0.0 136.6 jit_solution(3277634549355331535)
XLA Ops:
  7.2 0.7 all-gather.3.cloned.1.call-update
  8.1 1.1 dynamic-slice_bitcast_fusion
  9.2 6.0 %collective-permute-start.6 = (bf16[32,1024]{1,0:T(8,128)(2,1)S(1)}, bf16[32,1024]{1,0:T(8,128)(2,1)S(1)}, u32[]{:S(2)}, u32[]{:S(2)}) collective-permute-start(bf16[32,1024]{1,0:T(8,128)(2,1)S(1)} %get-tuple-element.40), channel_id=1, source_target_pairs={{0,28},{4,0},{8,4},{12,8},{16,12},{20,16},{24,20},{28,24},{1,29},{... | collective-permute-start | bytes 196616 | tf_op jit(solution)/shard_map/ppermute | solution.py:159
  15.2 0.4 collective-permute-start.5
  15.7 3.0 %collective-permute-start.3 = (bf16[32,1024]{1,0:T(8,128)(2,1)S(1)}, bf16[32,1024]{1,0:T(8,128)(2,1)S(1)}, u32[]{:S(2)}, u32[]{:S(2)}) collective-permute-start(bf16[32,1024]{1,0:T(8,128)(2,1)S(1)} %get-tuple-element.43), channel_id=1, source_target_pairs={{0,16},{4,20},{8,24},{12,28},{16,0},{20,4},{24,8},{28,12},{1,17},{... | collective-permute-start | bytes 196616 | tf_op jit(solution)/shard_map/ppermute | solution.py:159
  18.7 0.8 reduce-window.8
  19.6 0.5 multiply_cosine_fusion
  20.2 0.7 fusion.31
  21.0 1.9 %collective-permute-start.1 = (bf16[32,1024]{1,0:T(8,128)(2,1)S(1)}, bf16[32,1024]{1,0:T(8,128)(2,1)S(1)}, u32[]{:S(2)}, u32[]{:S(2)}) collective-permute-start(bf16[32,1024]{1,0:T(8,128)(2,1)S(1)} %get-tuple-element.45), channel_id=1, source_target_pairs={{0,8},{4,12},{8,16},{12,20},{16,24},{20,28},{24,0},{28,4},{1,9},{5... | collective-permute-start | bytes 196616 | tf_op jit(solution)/shard_map/ppermute | solution.py:159
  22.9 1.1 collective-permute-start
  24.0 1.3 and_select_fusion
  25.8 2.8 %collective-permute-done.2 = bf16[32,1024]{1,0:T(8,128)(2,1)S(1)} collective-permute-done((bf16[32,1024]{1,0:T(8,128)(2,1)S(1)}, bf16[32,1024]{1,0:T(8,128)(2,1)S(1)}, u32[]{:S(2)}, u32[]{:S(2)}) %collective-permute-start.2) | collective-permute-done | bytes 65568 | tf_op jit(solution)/shard_map/ppermute | solution.py:159
  28.6 0.8 copy.93
  29.3 0.8 copy.92
  30.1 0.8 copy.91
  30.8 2.9 %stack.58 = bf16[8,32,1024]{2,0,1:T(8,128)(2,1)S(1)} concatenate(bf16[1,32,1024]{2,0,1:T(2,128)(2,1)S(1)} %copy.132, bf16[1,32,1024]{2,0,1:T(2,128)(2,1)} %copy.91, bf16[1,32,1024]{2,0,1:T(2,128)(2,1)} %copy.92, bf16[1,32,1024]{2,0,1:T(2,128)(2,1)} %copy.93, bf16[1,32,1024]{2,0,1:T(2,128)(2,1)S(1)} %copy.94, bf16[1,32,1024]{2,0,1:T(2,128)(2,1)S(1)} %copy.95, ...), dimensions={0} | concatenate | bytes 1048576 | tf_op jit(solution)/shard_map/stack | solution.py:160
  33.8 0.4 convolution_convert_fusion.3
  34.1 1.1 copy.98
  35.3 2.2 %fusion = f32[256]{0:T(256)S(1)} fusion(bf16[256,4096]{1,0:T(8,128)(2,1)} %all-gather.3.cloned.1.call-done), kind=kLoop, calls=%fused_computation.5 | loop fusion | flops 3145472 | bytes 2098176 | tf_op jit(solution)/shard_map/reduce_sum | solution.py:183
  37.5 0.6 multiply_multiply_fusion
  38.1 1.2 fusion.47
  39.6 6.5 %convolution_bitcast_fusion = f32[32,8,8,128]{3,1,2,0:T(8,128)S(1)} fusion(bf16[4096,1024]{1,0:T(8,128)(2,1)} %param.11, bf16[256,4096]{1,0:T(8,128)(2,1)} %all-gather.3.cloned.1.call-done, f32[4096]{0:T(1024)S(1)} %copy-done.19, f32[256]{0:T(256)S(1)} %get-tuple-element.53), kind=kOutput, calls=%fused_computation.16 | convolution fusion | flops 2151677952 | bytes 11551744 | tf_op jit(solution)/shard_map/dot_general | solution.py:185
  46.3 0.5 subtract_convert_fusion.1
  47.2 0.6 copy-done.9
  47.9 0.9 fusion.7
  49.0 0.6 copy-done.13
  49.6 1.2 convolution_convert_fusion.4
  51.0 0.7 convolution_convert_fusion.1
  51.7 0.9 slice-done
  52.6 1.4 %slice-done.1 = s8[4194304]{0:T(1024)(128)(4,1)S(1)} async-done(((s8[8388608]{0:T(1024)(128)(4,1)}), s8[4194304]{0:T(1024)(128)(4,1)S(1)}, s32[]{:S(2)}) %slice-start.1) | async-done | bytes 4194328
  54.1 4.5 %fusion.55 = f32[256,4096]{1,0:T(8,128)} fusion(bf16[256,1024]{0,1:T(8,128)(2,1)S(1)} %bitcast.167, bf16[1024,4096]{1,0:T(8,128)(2,1)S(1)} %bitcast.163), kind=kOutput, calls=%fused_computation.114 | convolution fusion | flops 2147483648 | bytes 13107200 | tf_op jit(solution)/shard_map/dot_general | solution.py:213
  58.6 1.1 all-gather.5.cloned.1.call-done
  59.7 1.7 %fusion.19 = (bf16[1,256,1024]{2,1,0:T(8,128)(2,1)S(1)}, bf16[1,256,1024]{2,1,0:T(8,128)(2,1)S(1)}) fusion(f32[256,4096]{1,0:T(8,128)} %fusion.55, s32[]{:T(128)S(6)} %select_n.111, s32[]{:T(128)S(6)} %select_n.112), kind=kLoop, calls=%fused_computation.54 | loop fusion | bytes 2097160 | tf_op jit(solution)/shard_map/stack | solution.py:100
  61.4 1.1 pad_maximum_fusion
  62.7 7.4 %convolution_convert_fusion = bf16[256,1024]{1,0:T(8,128)(2,1)} fusion(bf16[256,4096]{1,0:T(8,128)(2,1)} %all-gather.5.cloned.1.call-done, bf16[1024,4096]{1,0:T(8,128)(2,1)} %param.14), kind=kOutput, calls=%fused_computation.19 | convolution fusion | flops 2147745792 | bytes 11010048 | tf_op jit(solution)/shard_map/dot_general | solution.py:216
  70.1 1.2 copy.99
  71.6 2.5 %fusion.5 = bf16[2,4,256,256]{2,3,1,0:T(8,128)(2,1)S(1)} fusion(bf16[256,2,128,1]{0,2,3,1:T(8,128)(2,1)} %bitcast.191, bf16[256,2,4,128]{0,3,2,1:T(8,128)(2,1)S(1)} %bitcast.168, f32[2,4,256]{2,1,0:T(4,128)S(1)} %bitcast.187, f32[2,4,256]{2,1,0:T(4,128)} %copy-done.27, f32[2,256,256,4]{2,1,3,0:T(8,128)} %copy-done.25, pred[256,256]{0,1:T(8,128)(4,1)} %fusion.31), kind=kOutput, calls=%fused_computation.11 | convolution fusion | flops 137363456 | bytes 3883008 | tf_op jit(solution)/shard_map/qkgd,skd->kgqs/dot_general | solution.py:230
  74.1 0.5 fusion.9
  74.6 0.4 copy-done.16
  75.0 0.4 convolution_multiply_fusion
  75.4 1.1 fusion.53
  77.0 1.5 %copy.134 = f32[256,8,64]{2,1,0:T(8,128)S(1)} copy(f32[256,8,64]{0,2,1:T(8,128)} %get-tuple-element.34) | data formatting | bytes 1048576
  78.4 2.3 %fusion.23 = bf16[1,256,1024]{2,1,0:T(8,128)(2,1)} fusion(f32[256,4096]{1,0:T(8,128)} %fusion.55, s32[]{:T(128)S(6)} %select_n.113, bf16[2,256,1024]{2,1,0:T(8,128)(2,1)} %collective-permute-done.7), kind=kLoop, calls=%fused_computation.58 | loop fusion | flops 786432 | bytes 2097156 | tf_op jit(solution)/shard_map/convert_element_type | solution.py:100
  81.1 2.4 %copy.133 = f32[256,8,64]{2,1,0:T(8,128)} copy(f32[256,8,64]{0,2,1:T(8,128)} %get-tuple-element.35) | data formatting | bytes 1048576
  83.4 1.5 %add_convert_fusion = (bf16[256,8,64]{2,1,0:T(8,128)(2,1)S(1)}, bf16[256,8,64]{2,1,0:T(8,128)(2,1)S(1)}) fusion(f32[256,8,64]{2,1,0:T(8,128)S(1)} %copy.134, f32[256,8,64]{2,1,0:T(8,128)} %copy.133, f32[256,64]{1,0:T(8,128)S(1)} %get-tuple-element.51, f32[256,64]{1,0:T(8,128)S(1)} %get-tuple-element.50), kind=kLoop, calls=%fused_computation.48 | loop fusion | flops 1048576 | bytes 1703936 | tf_op jit(solution)/shard_map/convert.12
  85.2 5.8 %fusion.25 = f32[256,4096]{1,0:T(8,128)S(1)} fusion(bf16[4096,1024]{1,0:T(8,128)(2,1)} %param.11, bf16[32,8,8,128]{3,2,1,0:T(8,128)(2,1)S(1)} %bitcast.175), kind=kOutput, calls=%fused_computation.60 | convolution fusion | flops 2147483648 | bytes 13107200 | tf_op jit(solution)/shard_map/dot_general | solution.py:253
  91.0 0.8 convolution_add_fusion.1
  92.0 0.7 copy-done.26
  92.8 0.7 fusion.10
  93.4 0.9 copy-done.14
  94.4 0.8 convolution_add_fusion
  95.4 3.1 %fusion.11 = bf16[256,1024]{1,0:T(8,128)(2,1)S(1)} fusion(bf16[256,1024]{1,0:T(8,128)(2,1)S(1)} %copy-done.6, f32[256,4096]{1,0:T(8,128)} %fusion.55, s32[]{:T(128)} %select_n.110, bf16[1,256,1024]{2,1,0:T(8,128)(2,1)} %collective-permute-done.8, bf16[2,256,1024]{2,1,0:T(8,128)(2,1)} %collective-permute-done.7), kind=kLoop, calls=%fused_computation.29 | loop fusion | flops 1835008 | bytes 3145732 | tf_op jit(solution)/shard_map/convert_element_type | solution.py:225
  99.2 0.4 convolution_convert_fusion.2
  99.6 2.1 %collective-permute-done.9 = bf16[2,256,1024]{2,1,0:T(8,128)(2,1)} collective-permute-done((bf16[2,256,1024]{2,1,0:T(8,128)(2,1)S(1)}, bf16[2,256,1024]{2,1,0:T(8,128)(2,1)}, u32[]{:S(2)}, u32[]{:S(2)}) %collective-permute-start.9) | collective-permute-done | bytes 1048608 | tf_op jit(solution)/shard_map/ppermute | solution.py:104
  101.6 1.1 copy.112
  102.7 5.7 %all-to-all-start = ((bf16[8,32,1024]{2,1,0:T(8,128)(2,1)}), bf16[8,32,1024]{2,1,0:T(8,128)(2,1)}, u32[]{:S(2)}, u32[]{:S(2)}) async-start(bf16[8,32,1024]{2,1,0:T(8,128)(2,1)} %copy.112), calls=%async_computation | async-start | bytes 1048576 | tf_op jit(solution)/shard_map/all_to_all | solution.py:281
  108.5 2.5 %fusion.24 = bf16[1,256,1024]{2,1,0:T(8,128)(2,1)} fusion(f32[256,4096]{1,0:T(8,128)} %copy-done.1, s32[]{:T(128)S(6)} %select_n.113, bf16[2,256,1024]{2,1,0:T(8,128)(2,1)} %collective-permute-done.9), kind=kLoop, calls=%fused_computation.59 | loop fusion | flops 786432 | bytes 2097156 | tf_op jit(solution)/shard_map/convert_element_type | solution.py:100
  110.9 1.5 %collective-permute-start.12 = (bf16[1,256,1024]{2,1,0:T(8,128)(2,1)}, bf16[1,256,1024]{2,1,0:T(8,128)(2,1)}, u32[]{:S(2)}, u32[]{:S(2)}) collective-permute-start(bf16[1,256,1024]{2,1,0:T(8,128)(2,1)} %fusion.24), channel_id=1, source_target_pairs={{0,2},{1,3},{2,0},{3,1},{4,6},{5,7},{6,4},{7,5},{8,10},{9,11},{10,... | collective-permute-start | bytes 1572872 | tf_op jit(solution)/shard_map/ppermute | solution.py:104
  112.5 2.8 %fusion.3 = f32[256]{0:T(256)S(1)} fusion(bf16[256,4096]{1,0:T(8,128)(2,1)S(1)} %copy-done.4, f32[256,4096]{1,0:T(8,128)} %copy-done.1, f32[4096]{0:T(1024)S(1)} %copy-done.19), kind=kLoop, calls=%fused_computation.8 | loop fusion | flops 4194048 | bytes 6308864 | tf_op jit(solution)/shard_map/reduce_sum | solution.py:273
  115.4 1.1 collective-permute-done.10
  116.5 0.5 collective-permute-start.11
  117.1 8.0 %collective-permute-done.11 = f32[256]{0:T(256)S(1)} collective-permute-done((f32[256]{0:T(256)S(1)}, f32[256]{0:T(256)S(1)}, u32[]{:S(2)}, u32[]{:S(2)}) %collective-permute-start.11) | collective-permute-done | bytes 1056 | tf_op jit(solution)/shard_map/ppermute | solution.py:104
  125.1 2.8 %fusion.14 = bf16[256,1024]{1,0:T(8,128)(2,1)} fusion(bf16[256,1024]{1,0:T(8,128)(2,1)S(1)} %copy-done.6, f32[256,4096]{1,0:T(8,128)} %copy-done.1, s32[]{:T(128)} %select_n.110, bf16[1,256,1024]{2,1,0:T(8,128)(2,1)} %collective-permute-done.12, f32[256]{0:T(256)S(1)} %broadcast_multiply_fusion, f32[256]{0:T(256)S(1)} %copy-done.20, ...), kind=kLoop, calls=%fused_computation.32 | loop fusion | flops 3407872 | bytes 3677188 | tf_op jit(solution)/shard_map/convert_element_type | solution.py:292
  127.9 1.9 %copy.144 = bf16[256,1024]{1,0:T(8,128)(2,1)} copy(bf16[256,1024]{1,0:T(8,128)(2,1)} %bitcast.56) | data formatting | bytes 1048576
  (103 shorter events, 4.6 us)
Async XLA Ops:
  7.2 31.0 %copy-start = (bf16[4096,256]{1,0:T(8,128)(2,1)S(1)}, bf16[4096,256]{1,0:T(8,128)(2,1)}, u32[]{:S(2)}) copy-start(bf16[4096,256]{1,0:T(8,128)(2,1)} %param.12) | copy-start | bytes 6291460
  7.2 28.1 %all-gather.3.cloned.1.call-start = ((), (), s32[]{:S(2)}) async-start(), calls=%async_computation.1 | async-start | bytes 2621440 | tf_op jit(solution)/shard_map/all_gather | solution.py:181
  7.9 51.8 %all-gather.5.cloned.1.call-start = ((), (), s32[]{:S(2)}) async-start(), calls=%async_computation.2 | async-start | bytes 2621440 | tf_op jit(solution)/shard_map/all_gather | solution.py:214
  9.2 11.8 %collective-permute-start.6 = (bf16[32,1024]{1,0:T(8,128)(2,1)S(1)}, bf16[32,1024]{1,0:T(8,128)(2,1)S(1)}, u32[]{:S(2)}, u32[]{:S(2)}) collective-permute-start(bf16[32,1024]{1,0:T(8,128)(2,1)S(1)} %get-tuple-element.40), channel_id=1, source_target_pairs={{0,28},{4,0},{8,4},{12,8},{16,12},{20,16},{24,20},{28,24},{1,29},{... | collective-permute-start | bytes 196616 | tf_op jit(solution)/shard_map/ppermute | solution.py:159
  15.2 7.7 %collective-permute-start.5 = (bf16[32,1024]{1,0:T(8,128)(2,1)S(1)}, bf16[32,1024]{1,0:T(8,128)(2,1)S(1)}, u32[]{:S(2)}, u32[]{:S(2)}) collective-permute-start(bf16[32,1024]{1,0:T(8,128)(2,1)S(1)} %get-tuple-element.41), channel_id=1, source_target_pairs={{0,24},{4,28},{8,0},{12,4},{16,8},{20,12},{24,16},{28,20},{1,25},{... | collective-permute-start | bytes 196616 | tf_op jit(solution)/shard_map/ppermute | solution.py:159
  15.7 9.9 %collective-permute-start.4 = (bf16[32,1024]{1,0:T(8,128)(2,1)S(1)}, bf16[32,1024]{1,0:T(8,128)(2,1)S(1)}, u32[]{:S(2)}, u32[]{:S(2)}) collective-permute-start(bf16[32,1024]{1,0:T(8,128)(2,1)S(1)} %get-tuple-element.42), channel_id=1, source_target_pairs={{0,20},{4,24},{8,28},{12,0},{16,4},{20,8},{24,12},{28,16},{1,21},{... | collective-permute-start | bytes 196616 | tf_op jit(solution)/shard_map/ppermute | solution.py:159
  15.7 10.0 %collective-permute-start.3 = (bf16[32,1024]{1,0:T(8,128)(2,1)S(1)}, bf16[32,1024]{1,0:T(8,128)(2,1)S(1)}, u32[]{:S(2)}, u32[]{:S(2)}) collective-permute-start(bf16[32,1024]{1,0:T(8,128)(2,1)S(1)} %get-tuple-element.43), channel_id=1, source_target_pairs={{0,16},{4,20},{8,24},{12,28},{16,0},{20,4},{24,8},{28,12},{1,17},{... | collective-permute-start | bytes 196616 | tf_op jit(solution)/shard_map/ppermute | solution.py:159
  18.7 9.9 %collective-permute-start.2 = (bf16[32,1024]{1,0:T(8,128)(2,1)S(1)}, bf16[32,1024]{1,0:T(8,128)(2,1)S(1)}, u32[]{:S(2)}, u32[]{:S(2)}) collective-permute-start(bf16[32,1024]{1,0:T(8,128)(2,1)S(1)} %get-tuple-element.44), channel_id=1, source_target_pairs={{0,12},{4,16},{8,20},{12,24},{16,28},{20,0},{24,4},{28,8},{1,13},{... | collective-permute-start | bytes 196616 | tf_op jit(solution)/shard_map/ppermute | solution.py:159
  21.0 8.3 %collective-permute-start.1 = (bf16[32,1024]{1,0:T(8,128)(2,1)S(1)}, bf16[32,1024]{1,0:T(8,128)(2,1)S(1)}, u32[]{:S(2)}, u32[]{:S(2)}) collective-permute-start(bf16[32,1024]{1,0:T(8,128)(2,1)S(1)} %get-tuple-element.45), channel_id=1, source_target_pairs={{0,8},{4,12},{8,16},{12,20},{16,24},{20,28},{24,0},{28,4},{1,9},{5... | collective-permute-start | bytes 196616 | tf_op jit(solution)/shard_map/ppermute | solution.py:159
  22.9 7.2 %collective-permute-start = (bf16[32,1024]{1,0:T(8,128)(2,1)S(1)}, bf16[32,1024]{1,0:T(8,128)(2,1)S(1)}, u32[]{:S(2)}, u32[]{:S(2)}) collective-permute-start(bf16[32,1024]{1,0:T(8,128)(2,1)S(1)} %get-tuple-element.46), channel_id=1, source_target_pairs={{0,4},{4,8},{8,12},{12,16},{16,20},{20,24},{24,28},{28,0},{1,5},{5... | collective-permute-start | bytes 196616 | tf_op jit(solution)/shard_map/ppermute | solution.py:159
  34.1 4.0 %copy-start.19 = (f32[4096]{0:T(1024)S(1)}, f32[4096]{0:T(1024)}, u32[]{:S(2)}) copy-start(f32[4096]{0:T(1024)} %param.10) | copy-start | bytes 49156
  35.3 2.8 %copy-start.2 = (bf16[256,4096]{1,0:T(8,128)(2,1)S(1)}, bf16[256,4096]{1,0:T(8,128)(2,1)}, u32[]{:S(2)}) copy-start(bf16[256,4096]{1,0:T(8,128)(2,1)} %all-gather.3.cloned.1.call-done) | copy-start | bytes 6291460
  38.1 10.7 %copy-start.21 = (f32[256]{0:T(256)}, f32[256]{0:T(256)S(1)}, u32[]{:S(2)}) copy-start(f32[256]{0:T(256)S(1)} %get-tuple-element.53) | copy-start | bytes 3076
  46.9 1.1 copy-start.17
  46.9 0.8 copy-start.9
  47.0 0.9 copy-start.11
  47.0 1.9 %copy-start.3 = (bf16[256,4096]{1,0:T(8,128)(2,1)S(1)}, bf16[256,4096]{1,0:T(8,128)(2,1)}, u32[]{:S(2)}) copy-start(bf16[256,4096]{1,0:T(8,128)(2,1)} %all-gather.3.cloned.1.call-done) | copy-start | bytes 6291460
  47.1 2.6 %copy-start.13 = (bf16[4096,256]{1,0:T(8,128)(2,1)S(1)}, bf16[4096,256]{1,0:T(8,128)(2,1)}, u32[]{:S(2)}) copy-start(bf16[4096,256]{1,0:T(8,128)(2,1)} %param.13) | copy-start | bytes 6291460
  47.1 3.7 %copy-start.15 = (bf16[256,2,64]{2,0,1:T(8,128)(2,1)}, bf16[256,2,64]{2,0,1:T(8,128)(2,1)S(1)}, u32[]{:S(2)}) copy-start(bf16[256,2,64]{2,0,1:T(8,128)(2,1)S(1)} %get-tuple-element.37) | copy-start | bytes 196612
  49.6 1.4 copy-start.25
  49.6 1.4 %copy-start.27 = (f32[2,4,256]{2,1,0:T(4,128)}, f32[2,4,256]{2,1,0:T(4,128)S(1)}, u32[]{:S(2)}) copy-start(f32[2,4,256]{2,1,0:T(4,128)S(1)} %get-tuple-element.54) | copy-start | bytes 24580
  49.6 3.0 %slice-start = ((s8[8388608]{0:T(1024)(128)(4,1)}), s8[4194304]{0:T(1024)(128)(4,1)S(1)}, s32[]{:S(2)}) async-start(s8[8388608]{0:T(1024)(128)(4,1)} %bitcast.162), calls=%async_computation.3 | async-start | bytes 8388608
  50.8 0.8 copy-start.24
  51.0 3.1 %slice-start.1 = ((s8[8388608]{0:T(1024)(128)(4,1)}), s8[4194304]{0:T(1024)(128)(4,1)S(1)}, s32[]{:S(2)}) async-start(s8[8388608]{0:T(1024)(128)(4,1)} %bitcast.162), calls=%async_computation.4 | async-start | bytes 8388608
  62.5 7.7 %collective-permute-start.7 = (bf16[2,256,1024]{2,1,0:T(8,128)(2,1)}, bf16[2,256,1024]{2,1,0:T(8,128)(2,1)}, u32[]{:S(2)}, u32[]{:S(2)}) collective-permute-start(bf16[2,256,1024]{2,1,0:T(8,128)(2,1)} %pad_maximum_fusion), channel_id=1, source_target_pairs={{0,1},{1,0},{2,3},{3,2},{4,5},{5,4},{6,7},{7,6},{8,9},{9,8},{10,11... | collective-permute-start | bytes 3145736 | tf_op jit(solution)/shard_map/ppermute | solution.py:102
  71.4 2.7 %copy-start.7 = (bf16[256,1024]{0,1:T(8,128)(2,1)}, bf16[256,1024]{0,1:T(8,128)(2,1)S(1)}, u32[]{:S(2)}) copy-start(bf16[256,1024]{0,1:T(8,128)(2,1)S(1)} %copy.99) | copy-start | bytes 1572868
  71.6 2.5 %copy-start.10 = (bf16[256,8,64]{2,0,1:T(8,128)(2,1)S(1)}, bf16[256,8,64]{2,0,1:T(8,128)(2,1)}, u32[]{:S(2)}) copy-start(bf16[256,8,64]{2,0,1:T(8,128)(2,1)} %copy-done.9) | copy-start | bytes 786436
  71.6 2.5 %copy-start.12 = (bf16[256,8,64]{2,0,1:T(8,128)(2,1)S(1)}, bf16[256,8,64]{2,0,1:T(8,128)(2,1)}, u32[]{:S(2)}) copy-start(bf16[256,8,64]{2,0,1:T(8,128)(2,1)} %copy-done.11) | copy-start | bytes 786436
  74.1 0.9 copy-start.16
  80.7 14.4 %collective-permute-start.8 = (bf16[1,256,1024]{2,1,0:T(8,128)(2,1)}, bf16[1,256,1024]{2,1,0:T(8,128)(2,1)}, u32[]{:S(2)}, u32[]{:S(2)}) collective-permute-start(bf16[1,256,1024]{2,1,0:T(8,128)(2,1)} %fusion.23), channel_id=1, source_target_pairs={{0,2},{1,3},{2,0},{3,1},{4,6},{5,7},{6,4},{7,5},{8,10},{9,11},{10,... | collective-permute-start | bytes 1572872 | tf_op jit(solution)/shard_map/ppermute | solution.py:102
  91.0 1.0 copy-start.8
  91.0 1.0 copy-start.18
  91.0 1.8 %copy-start.26 = (f32[2,256,256,4]{2,1,3,0:T(8,128)S(1)}, f32[2,256,256,4]{2,1,3,0:T(8,128)}, u32[]{:S(2)}) copy-start(f32[2,256,256,4]{2,1,3,0:T(8,128)} %copy-done.25) | copy-start | bytes 6291460
  91.0 1.8 %copy-start.28 = (f32[2,4,256]{2,1,0:T(4,128)S(1)}, f32[2,4,256]{2,1,0:T(4,128)}, u32[]{:S(2)}) copy-start(f32[2,4,256]{2,1,0:T(4,128)} %copy-done.27) | copy-start | bytes 24580
  92.8 1.6 %copy-start.14 = (bf16[4096,256]{1,0:T(8,128)(2,1)S(1)}, bf16[4096,256]{1,0:T(8,128)(2,1)}, u32[]{:S(2)}) copy-start(bf16[4096,256]{1,0:T(8,128)(2,1)} %param.13) | copy-start | bytes 6291460
  94.4 1.0 copy-start.6
  95.1 3.5 %copy-start.1 = (f32[256,4096]{1,0:T(8,128)}, f32[256,4096]{1,0:T(8,128)S(1)}, u32[]{:S(2)}) copy-start(f32[256,4096]{1,0:T(8,128)S(1)} %convolution_add_fusion) | copy-start | bytes 12582916
  98.5 0.7 copy-start.23
  98.8 2.9 %collective-permute-start.9 = (bf16[2,256,1024]{2,1,0:T(8,128)(2,1)S(1)}, bf16[2,256,1024]{2,1,0:T(8,128)(2,1)}, u32[]{:S(2)}, u32[]{:S(2)}) collective-permute-start(bf16[2,256,1024]{2,1,0:T(8,128)(2,1)S(1)} %pad_maximum_fusion.1), channel_id=1, source_target_pairs={{0,1},{1,0},{2,3},{3,2},{4,5},{5,4},{6,7},{7,6},{8,9},{9,8},{10,11... | collective-permute-start | bytes 3145736 | tf_op jit(solution)/shard_map/ppermute | solution.py:104
  102.7 22.3 %all-to-all-start = ((bf16[8,32,1024]{2,1,0:T(8,128)(2,1)}), bf16[8,32,1024]{2,1,0:T(8,128)(2,1)}, u32[]{:S(2)}, u32[]{:S(2)}) async-start(bf16[8,32,1024]{2,1,0:T(8,128)(2,1)} %copy.112), calls=%async_computation | async-start | bytes 1048576 | tf_op jit(solution)/shard_map/all_to_all | solution.py:281
  108.5 4.0 %copy-start.4 = (bf16[256,4096]{1,0:T(8,128)(2,1)S(1)}, bf16[256,4096]{1,0:T(8,128)(2,1)}, u32[]{:S(2)}) copy-start(bf16[256,4096]{1,0:T(8,128)(2,1)} %all-gather.3.cloned.1.call-done) | copy-start | bytes 6291460
  110.9 14.1 %copy-start.5 = (bf16[8,32,1024]{2,1,0:T(8,128)(2,1)S(1)}, bf16[8,32,1024]{2,1,0:T(8,128)(2,1)}, u32[]{:S(2)}) copy-start(bf16[8,32,1024]{2,1,0:T(8,128)(2,1)} %copy.98) | copy-start | bytes 1572868
  110.9 14.1 %dynamic-slice-start = ((f32[4096]{0:T(1024)}, s32[]{:T(128)}), f32[1024]{0:T(1024)S(1)}, s32[]{:S(2)}) async-start(f32[4096]{0:T(1024)} %param.10, s32[]{:T(128)} %select_n.110), calls=%async_computation.5 | async-start | bytes 8704 | tf_op jit(solution)/shard_map/dynamic_slice | solution.py:142
  110.9 14.1 %copy-start.20 = (f32[256]{0:T(256)S(1)}, f32[256]{0:T(256)}, u32[]{:S(2)}) copy-start(f32[256]{0:T(256)} %get-tuple-element.52) | copy-start | bytes 3076
  110.9 14.1 %copy-start.22 = (f32[256]{0:T(256)S(1)}, f32[256]{0:T(256)}, u32[]{:S(2)}) copy-start(f32[256]{0:T(256)} %copy-done.21) | copy-start | bytes 3076
  110.9 14.1 %collective-permute-start.12 = (bf16[1,256,1024]{2,1,0:T(8,128)(2,1)}, bf16[1,256,1024]{2,1,0:T(8,128)(2,1)}, u32[]{:S(2)}, u32[]{:S(2)}) collective-permute-start(bf16[1,256,1024]{2,1,0:T(8,128)(2,1)} %fusion.24), channel_id=1, source_target_pairs={{0,2},{1,3},{2,0},{3,1},{4,6},{5,7},{6,4},{7,5},{8,10},{9,11},{10,... | collective-permute-start | bytes 1572872 | tf_op jit(solution)/shard_map/ppermute | solution.py:104
  115.3 1.2 collective-permute-start.10
  116.5 8.5 %collective-permute-start.11 = (f32[256]{0:T(256)S(1)}, f32[256]{0:T(256)S(1)}, u32[]{:S(2)}, u32[]{:S(2)}) collective-permute-start(f32[256]{0:T(256)S(1)} %add.196), channel_id=1, source_target_pairs={{0,2},{1,3},{2,0},{3,1},{4,6},{5,7},{6,4},{7,5},{8,10},{9,11},{10,... | collective-permute-start | bytes 3080 | tf_op jit(solution)/shard_map/ppermute | solution.py:104
Sparse Core Ops, SparseCore 0:
  9.6 25.2 all-gather.2
  37.0 22.5 all-gather.4

commit v19 on v17

--- a/solution.py
+++ b/solution.py
@@ -79,7 +79,9 @@
 
 
 def scatter_features(partial, axis_name, size, position, extra=None, ties=()):
-    width = partial.shape[1] // size
+    if not _is_pow2(size) and isinstance(partial, list):
+        partial = jnp.concatenate(partial, axis=1)
+    width = None if isinstance(partial, list) else partial.shape[1] // size
     if not _is_pow2(size):
         summed = lax.psum_scatter(
             partial.astype(jnp.bfloat16), axis_name, scatter_dimension=1, tiled=True
@@ -87,10 +89,13 @@
         if extra is not None:
             extra = lax.psum(extra, axis_name)
         return summed.astype(jnp.float32), extra, ties
-    held = [
-        lax.dynamic_slice_in_dim(partial, (position ^ m) * width, width, axis=1)
-        for m in range(size)
-    ]
+    if isinstance(partial, list):
+        held = list(partial)
+    else:
+        held = [
+            lax.dynamic_slice_in_dim(partial, (position ^ m) * width, width, axis=1)
+            for m in range(size)
+        ]
     masks = list(range(size))
     done_ties = []
     bit = 1
@@ -249,33 +254,53 @@
     ).astype(jnp.bfloat16)
     key_gradient = unrotate(grad_keys_rot, cosine, sine_table).astype(jnp.bfloat16)
     contract_out = (((1,), (1,)), ((), ()))
-    normed_partial = (
-        lax.dot_general(
-            grad_query.reshape(token_row_count, query_width),
-            w_query,
-            contract_out,
-            preferred_element_type=jnp.float32,
-        )
-        + lax.dot_general(
-            key_gradient.reshape(token_row_count, key_width),
-            key_weight,
-            contract_out,
-            preferred_element_type=jnp.float32,
-        )
-        + lax.dot_general(
-            value_gradient.astype(jnp.bfloat16).reshape(token_row_count, key_width),
-            value_weight,
-            contract_out,
-            preferred_element_type=jnp.float32,
-        )
-    )
-    stat_partial = jnp.sum(normed_partial * norm_gain[None, :] * gathered_float, axis=1)
+    grad_query_flat = grad_query.reshape(token_row_count, query_width)
+    grad_key_flat = key_gradient.reshape(token_row_count, key_width)
+    grad_value_flat = value_gradient.astype(jnp.bfloat16).reshape(token_row_count, key_width)
+
+    def normed_block(shard):
+        start = shard * width_part
+        return (
+            lax.dot_general(
+                grad_query_flat,
+                lax.dynamic_slice_in_dim(w_query, start, width_part, axis=0),
+                contract_out,
+                preferred_element_type=jnp.float32,
+            )
+            + lax.dot_general(
+                grad_key_flat,
+                lax.dynamic_slice_in_dim(key_weight, start, width_part, axis=0),
+                contract_out,
+                preferred_element_type=jnp.float32,
+            )
+            + lax.dot_general(
+                grad_value_flat,
+                lax.dynamic_slice_in_dim(value_weight, start, width_part, axis=0),
+                contract_out,
+                preferred_element_type=jnp.float32,
+            )
+        )
+
+    if _is_pow2(tensor_size):
+        shard_of = [tensor_index ^ m for m in range(tensor_size)]
+    else:
+        shard_of = list(range(tensor_size))
+    parts = [normed_block(s) for s in shard_of]
+    stat_partial = sum(
+        jnp.sum(
+            part
+            * lax.dynamic_slice_in_dim(norm_gain, s * width_part, width_part)[None, :]
+            * lax.dynamic_slice_in_dim(gathered_float, s * width_part, width_part, axis=1),
+            axis=1,
+        )
+        for s, part in zip(shard_of, parts)
+    )
     home_blocks = output_home.reshape(block_count, home_rows, width_part)
     outgoing = jnp.einsum(
         "dj,jrw->drw", send_table, home_blocks, preferred_element_type=jnp.float32
     ).astype(jnp.bfloat16)
     normed_gradient, stat_sum, (outgoing,) = scatter_features(
-        normed_partial, "tensor", tensor_size, tensor_index, extra=stat_partial, ties=(outgoing,)
+        parts, "tensor", tensor_size, tensor_index, extra=stat_partial, ties=(outgoing,)
     )
     relaid = lax.all_to_all(outgoing, "dp", split_axis=0, concat_axis=0, tiled=True).reshape(
         token_row_count, width_part

time: 136 us -> 153 us (1.12)
  matrix products: 37.7 us -> 47.3 us
  waiting for transfers between devices: 16.1 us -> 21.4 us
    dot_general x3 -> x12, matrix products: 7.72 us -> 18.1 us  [the longest x4 9.46 us: normed_block(): lax.dot_general(grad_query_flat, lax.dynamic_slice_in_dim(w_query, start,...]
    ppermute x2, waiting for transfers between devices: 0.01 us -> 8.23 us  [scatter_features(): incoming = lax.ppermute(outgoing, axis_name, _xor_pairs(size, bit))]
    convert_element_type x0 -> x1, other arithmetic: none -> 4.2 us  [per_device(): gathered_float = gathered.astype(jnp.float32)]
    ppermute x7, waiting for transfers between devices: 2.83 us -> 0.02 us  [per_device(): returned.append(lax.ppermute(piece, 'dp', pairs))]
    dot_general x1, matrix products: 3.04 us -> 0.65 us  [per_device(): jnp.einsum('kgqs,qkgd->skd', probs_low, grouped_gradient, preferred_eleme...]
    convert_element_type x2 -> x1, other arithmetic: 3.82 us -> 1.66 us  [scatter_features(): outgoing = jnp.stack([held[i] for i in send]).astype(jnp.bfloat16)]
    dot_general x1, matrix products: 0.75 us -> 2.48 us  [per_device(): jnp.einsum('qkgd,skd->kgqs', grouped_gradient, value_rows, preferred_elem...]
    unnamed x67 -> x87, local copies, waits for them, and re-layouts: 12.6 us -> 13.1 us
  transfers between devices with their start and end apart: 16 -> 16, of which waited for: 4 -> 5; matrix products, arithmetic and copies ran while one was open for 44% -> 37% of each run, Pallas kernels for 0% -> 0%
where the time goes in v19:
time: 153 us; the launch traced here: 152 us
  matrix products  47.3 us (31%)
  local copies, waits for them, and re-layouts  27 us (18%)
  starting transfers between devices  22.1 us (14%)
  waiting for transfers between devices  21.4 us (14%)
  other arithmetic  19.2 us (13%)
  between operations  14.9 us (10%)
    ppermute x7, starting transfers between devices, per_device(): returned.append(lax.ppermute(piece, 'dp', pairs))  13.8 us
    unnamed x87, local copies, waits for them, and re-layouts  13.1 us
    ppermute x4, waiting for transfers between devices, scatter_features(): lax.ppermute((outgoing, extra), axis_name, _xor_pairs(size, bit))  11 us
    dot_general x4, matrix products, normed_block(): lax.dot_general(grad_query_flat, lax.dynamic_slice_in_dim(w_query, start,...  9.46 us
    ppermute x2, waiting for transfers between devices, scatter_features(): incoming = lax.ppermute(outgoing, axis_name, _xor_pairs(size, bit))  8.23 us
    dot_general x1, matrix products, per_device(): lax.dot_general(grad_full, w_out, (((1,), (1,)), ((), ())), preferred_ele...  6.78 us
    dot_general x1, matrix products, per_device(): jnp.dot(normed_input, w_query, preferred_element_type=jnp.float32)  6.76 us
    another operation x8, local copies, waits for them, and re-layouts, per_device(): returned = jnp.stack(returned)  5.6 us
  transfers between devices with their start and end apart: 16, of which 5 were waited for; matrix products, arithmetic and copies ran while one was open for 37% of the time, Pallas kernels for 0%

profile of v19, /device:TPU:0, one launch (start us, length us, event | category | flops | bytes accessed | tf_op | source)
XLA Modules:
  0.0 151.9 jit_solution(15616862667632512385)
XLA Ops:
  7.2 0.7 all-gather.3.cloned.1.call-update
  8.1 1.1 dynamic-slice_bitcast_fusion
  9.2 3.0 %collective-permute-start = (bf16[32,1024]{1,0:T(8,128)(2,1)S(1)}, bf16[32,1024]{1,0:T(8,128)(2,1)S(1)}, u32[]{:S(2)}, u32[]{:S(2)}) collective-permute-start(bf16[32,1024]{1,0:T(8,128)(2,1)S(1)} %get-tuple-element.41), channel_id=1, source_target_pairs={{0,4},{4,8},{8,12},{12,16},{16,20},{20,24},{24,28},{28,0},{1,5},{5... | collective-permute-start | bytes 196616 | tf_op jit(solution)/shard_map/ppermute | solution.py:164
  12.2 1.6 %collective-permute-start.1 = (bf16[32,1024]{1,0:T(8,128)(2,1)S(1)}, bf16[32,1024]{1,0:T(8,128)(2,1)S(1)}, u32[]{:S(2)}, u32[]{:S(2)}) collective-permute-start(bf16[32,1024]{1,0:T(8,128)(2,1)S(1)} %get-tuple-element.40), channel_id=1, source_target_pairs={{0,8},{4,12},{8,16},{12,20},{16,24},{20,28},{24,0},{28,4},{1,9},{5... | collective-permute-start | bytes 196616 | tf_op jit(solution)/shard_map/ppermute | solution.py:164
  13.8 2.6 %collective-permute-start.2 = (bf16[32,1024]{1,0:T(8,128)(2,1)S(1)}, bf16[32,1024]{1,0:T(8,128)(2,1)S(1)}, u32[]{:S(2)}, u32[]{:S(2)}) collective-permute-start(bf16[32,1024]{1,0:T(8,128)(2,1)S(1)} %get-tuple-element.39), channel_id=1, source_target_pairs={{0,12},{4,16},{8,20},{12,24},{16,28},{20,0},{24,4},{28,8},{1,13},{... | collective-permute-start | bytes 196616 | tf_op jit(solution)/shard_map/ppermute | solution.py:164
  16.3 1.2 collective-permute-start.3
  17.5 2.6 %collective-permute-start.4 = (bf16[32,1024]{1,0:T(8,128)(2,1)S(1)}, bf16[32,1024]{1,0:T(8,128)(2,1)S(1)}, u32[]{:S(2)}, u32[]{:S(2)}) collective-permute-start(bf16[32,1024]{1,0:T(8,128)(2,1)S(1)} %get-tuple-element.37), channel_id=1, source_target_pairs={{0,20},{4,24},{8,28},{12,0},{16,4},{20,8},{24,12},{28,16},{1,21},{... | collective-permute-start | bytes 196616 | tf_op jit(solution)/shard_map/ppermute | solution.py:164
  20.2 0.8 reduce-window.8
  21.1 0.5 multiply_cosine_fusion
  21.6 0.7 fusion.46
  22.5 1.4 collective-permute-start.5
  23.9 1.4 collective-permute-start.6
  25.3 1.2 and_select_fusion
  27.0 0.8 copy.95
  27.8 0.8 copy.96
  28.6 0.7 copy.97
  29.3 2.9 %stack.58 = bf16[8,32,1024]{2,0,1:T(8,128)(2,1)S(1)} concatenate(bf16[1,32,1024]{2,0,1:T(2,128)(2,1)S(1)} %copy.132, bf16[1,32,1024]{2,0,1:T(2,128)(2,1)S(1)} %copy.91, bf16[1,32,1024]{2,0,1:T(2,128)(2,1)S(1)} %copy.92, bf16[1,32,1024]{2,0,1:T(2,128)(2,1)S(1)} %copy.93, bf16[1,32,1024]{2,0,1:T(2,128)(2,1)S(1)} %copy.94, bf16[1,32,1024]{2,0,1:T(2,128)(2,1)} %copy.95, ...), dimensions={0} | concatenate | bytes 1048576 | tf_op jit(solution)/shard_map/stack | solution.py:165
  32.6 1.1 copy.98
  33.7 1.2 all-gather.3.cloned.1.call-done
  34.9 2.2 %multiply_reduce_fusion = f32[256]{0:T(256)S(1)} fusion(bf16[256,4096]{1,0:T(8,128)(2,1)} %all-gather.3.cloned.1.call-done), kind=kLoop, calls=%fused_computation.1 | loop fusion | flops 3145472 | bytes 2098176 | tf_op jit(solution)/shard_map/reduce_sum | solution.py:188
  37.1 0.6 multiply_multiply_fusion
  37.7 2.8 %fusion.73 = f32[256,256]{0,1:T(8,128)S(1)} fusion(bf16[4096,256]{1,0:T(8,128)(2,1)} %param.12, f32[4096]{0:T(1024)S(1)} %copy-done.25, f32[256]{0:T(256)S(1)} %get-tuple-element.52, bf16[256,4096]{1,0:T(8,128)(2,1)S(1)} %copy-done.3), kind=kOutput, calls=%fused_computation.148 | convolution fusion | flops 541065216 | bytes 4473856 | tf_op jit(solution)/shard_map/dot_general | solution.py:191
  40.8 6.8 %convolution_bitcast_fusion = f32[32,8,8,128]{3,1,2,0:T(8,128)S(1)} fusion(bf16[4096,1024]{1,0:T(8,128)(2,1)} %param.11, f32[4096]{0:T(1024)S(1)} %copy-done.25, f32[256]{0:T(256)S(1)} %get-tuple-element.52, bf16[256,4096]{1,0:T(8,128)(2,1)} %all-gather.3.cloned.1.call-done), kind=kOutput, calls=%fused_computation.25 | convolution fusion | flops 2151677952 | bytes 11551744 | tf_op jit(solution)/shard_map/dot_general | solution.py:190
  47.8 0.5 subtract_convert_fusion.1
  48.6 0.6 copy-done.14
  49.3 0.9 fusion.11
  50.4 1.2 convolution_convert_fusion.4
  51.7 0.7 convolution_convert_fusion.1
  52.4 1.0 slice-done
  53.4 1.4 slice-done.1
  54.9 4.6 %fusion.82 = f32[256,4096]{1,0:T(8,128)} fusion(bf16[256,1024]{0,1:T(8,128)(2,1)S(1)} %bitcast.186, bf16[1024,4096]{1,0:T(8,128)(2,1)S(1)} %bitcast.172), kind=kOutput, calls=%fused_computation.152 | convolution fusion | flops 2147483648 | bytes 13107200 | tf_op jit(solution)/shard_map/dot_general | solution.py:218
  59.7 1.7 %fusion.23 = (bf16[1,256,1024]{2,1,0:T(8,128)(2,1)S(1)}, bf16[1,256,1024]{2,1,0:T(8,128)(2,1)S(1)}) fusion(f32[256,4096]{1,0:T(8,128)} %fusion.82, s32[]{:T(128)S(6)} %select_n.126, s32[]{:T(128)S(6)} %select_n.127), kind=kLoop, calls=%fused_computation.65 | loop fusion | bytes 2097160 | tf_op jit(solution)/shard_map/stack | solution.py:105
  61.3 1.1 pad_maximum_fusion
  62.7 0.7 fusion.79
  63.4 4.2 %convert_element_type.129 = f32[256,4096]{1,0:T(8,128)} convert(bf16[256,4096]{1,0:T(8,128)(2,1)} %all-gather.3.cloned.1.call-done) | non-fusion elementwise | flops 1048576 | bytes 6291456 | tf_op jit(solution)/shard_map/convert_element_type | solution.py:187
  67.6 6.8 %convolution_convert_fusion = bf16[256,1024]{1,0:T(8,128)(2,1)} fusion(bf16[256,4096]{1,0:T(8,128)(2,1)S(1)} %copy-done.30, bf16[1024,4096]{1,0:T(8,128)(2,1)} %param.14), kind=kOutput, calls=%fused_computation.28 | convolution fusion | flops 2147745792 | bytes 11010048 | tf_op jit(solution)/shard_map/dot_general | solution.py:221
  74.4 1.2 copy.99
  75.8 2.5 %fusion.1 = bf16[2,4,256,256]{2,3,1,0:T(8,128)(2,1)S(1)} fusion(bf16[256,2,128,1]{0,2,3,1:T(8,128)(2,1)} %bitcast.211, bf16[256,2,4,128]{0,3,2,1:T(8,128)(2,1)S(1)} %bitcast.191, f32[2,4,256]{2,1,0:T(4,128)S(1)} %bitcast.207, f32[2,4,256]{2,1,0:T(4,128)} %copy-done.34, f32[2,256,256,4]{2,1,3,0:T(8,128)} %copy-done.32, pred[256,256]{0,1:T(8,128)(4,1)} %fusion.46), kind=kOutput, calls=%fused_computation.4 | convolution fusion | flops 137363456 | bytes 3883008 | tf_op jit(solution)/shard_map/qkgd,skd->kgqs/dot_general | solution.py:235
  78.4 1.2 fusion.13
  79.6 0.4 convolution_multiply_fusion
  80.0 1.0 fusion.77
  81.1 1.5 copy.133
  82.6 2.3 %copy.134 = f32[256,8,64]{2,1,0:T(8,128)} copy(f32[256,8,64]{0,2,1:T(8,128)} %get-tuple-element.29) | data formatting | bytes 1048576
  84.9 1.5 add_convert_fusion
  86.7 3.4 %fusion.2 = f32[256,1024]{1,0:T(8,128)} fusion(bf16[4096,1024]{1,0:T(8,128)(2,1)} %param.11, s32[]{:T(128)S(6)} %select_n.129, bf16[32,8,8,128]{3,2,1,0:T(8,128)(2,1)S(1)} %bitcast.173), kind=kOutput, calls=%fused_computation.6 | convolution fusion | flops 536870912 | bytes 3670020 | tf_op jit(solution)/shard_map/dot_general | solution.py:264
  90.2 2.5 %fusion.4 = f32[256,1024]{1,0:T(8,128)S(1)} fusion(bf16[4096,1024]{1,0:T(8,128)(2,1)} %param.11, s32[]{:T(128)S(6)} %select_n.128, bf16[32,8,8,128]{3,2,1,0:T(8,128)(2,1)S(1)} %bitcast.174), kind=kOutput, calls=%fused_computation.8 | convolution fusion | flops 536870912 | bytes 3670020 | tf_op jit(solution)/shard_map/dot_general | solution.py:264
  92.7 0.7 fusion.14
  93.4 1.5 slice-done.3
  94.9 1.7 %fusion.8 = f32[256,1024]{1,0:T(8,128)} fusion(bf16[4096,1024]{1,0:T(8,128)(2,1)S(1)} %bitcast.179, s32[]{:T(128)S(6)} %select_n.126, bf16[32,8,8,128]{3,2,1,0:T(8,128)(2,1)S(1)} %bitcast.175), kind=kOutput, calls=%fused_computation.12 | convolution fusion | flops 536870912 | bytes 3670020 | tf_op jit(solution)/shard_map/dot_general | solution.py:264
  96.6 1.8 %fusion.6 = f32[256,1024]{1,0:T(8,128)} fusion(bf16[4096,1024]{1,0:T(8,128)(2,1)S(1)} %bitcast.179, s32[]{:T(128)S(6)} %select_n.127, bf16[32,8,8,128]{3,2,1,0:T(8,128)(2,1)S(1)} %bitcast.176), kind=kOutput, calls=%fused_computation.10 | convolution fusion | flops 536870912 | bytes 3670020 | tf_op jit(solution)/shard_map/dot_general | solution.py:264
  98.9 1.7 %fusion.25 = bf16[1,256,1024]{2,1,0:T(8,128)(2,1)S(1)} fusion(f32[256,4096]{1,0:T(8,128)} %fusion.82, s32[]{:T(128)S(6)} %select_n.129, bf16[2,256,1024]{2,1,0:T(8,128)(2,1)} %collective-permute-done.7), kind=kLoop, calls=%fused_computation.67 | loop fusion | flops 786432 | bytes 2097156 | tf_op jit(solution)/shard_map/convert_element_type | solution.py:105
  100.9 2.4 %convolution_add_fusion.1 = f32[256,1024]{1,0:T(8,128)} fusion(f32[256,1024]{1,0:T(8,128)S(1)} %copy-done.8, bf16[256,256]{0,1:T(8,128)(2,1)S(1)} %bitcast.182, bf16[4096,256]{1,0:T(8,128)(2,1)} %param.12, s32[]{:T(128)S(6)} %select_n.129), kind=kOutput, calls=%fused_computation.17 | convolution fusion | flops 134479872 | bytes 2752516 | tf_op jit(solution)/shard_map/dot_general | solution.py:270
  106.5 8.2 %collective-permute-done.9 = bf16[1,256,1024]{2,1,0:T(8,128)(2,1)S(1)} collective-permute-done((bf16[1,256,1024]{2,1,0:T(8,128)(2,1)S(1)}, bf16[1,256,1024]{2,1,0:T(8,128)(2,1)S(1)}, u32[]{:S(2)}, u32[]{:S(2)}) %collective-permute-start.9) | collective-permute-done | bytes 524320 | tf_op jit(solution)/shard_map/ppermute | solution.py:107
  114.7 1.7 %fusion.15 = bf16[256,1024]{1,0:T(8,128)(2,1)S(1)} fusion(bf16[256,1024]{1,0:T(8,128)(2,1)S(1)} %copy-done.6, f32[256,4096]{1,0:T(8,128)} %fusion.82, s32[]{:T(128)S(6)} %select_n.128, bf16[1,256,1024]{2,1,0:T(8,128)(2,1)S(1)} %collective-permute-done.9, bf16[2,256,1024]{2,1,0:T(8,128)(2,1)} %collective-permute-done.7), kind=kLoop, calls=%fused_computation.38 | loop fusion | flops 1835008 | bytes 3145732 | tf_op jit(solution)/shard_map/convert_element_type | solution.py:230
  116.8 1.0 copy-done.19
  117.8 1.1 copy.112
  118.9 5.5 %all-to-all-start = ((bf16[8,32,1024]{2,1,0:T(8,128)(2,1)}), bf16[8,32,1024]{2,1,0:T(8,128)(2,1)}, u32[]{:S(2)}, u32[]{:S(2)}) async-start(bf16[8,32,1024]{2,1,0:T(8,128)(2,1)} %copy.112), calls=%async_computation | async-start | bytes 1048576 | tf_op jit(solution)/shard_map/all_to_all | solution.py:305
  124.5 4.2 %multiply_reduce_fusion.3 = (f32[256]{0:T(256)S(1)}, f32[256]{0:T(256)S(1)}, f32[256]{0:T(256)S(1)}, f32[256]{0:T(256)S(1)}, bf16[1,256,1024]{2,1,0:T(8,128)(2,1)S(1)}) fusion(f32[256,4096]{1,0:T(8,128)} %convert_element_type.129, s32[]{:T(128)S(6)} %select_n.126, f32[256,1024]{1,0:T(8,128)} %copy-done.1, f32[1024]{0:T(1024)S(1)} %get-tuple-element.46, ...), kind=kOutput, calls=%fused_computation.56 | convolution fusion | flops 138411008 | bytes 10115584 | tf_op jit(solution)/shard_map/dot_general | solution.py:276
  128.7 0.6 collective-permute-start.10
  129.3 1.1 collective-permute-done.11
  130.4 1.5 collective-permute-start.12
  131.9 9.9 %collective-permute-done.12 = f32[256]{0:T(256)S(1)} collective-permute-done((f32[256]{0:T(256)S(1)}, f32[256]{0:T(256)S(1)}, u32[]{:S(2)}, u32[]{:S(2)}) %collective-permute-start.12) | collective-permute-done | bytes 1056 | tf_op jit(solution)/shard_map/ppermute | solution.py:109
  141.9 1.3 fusion.18
  143.2 1.9 %copy.156 = bf16[256,1024]{1,0:T(8,128)(2,1)} copy(bf16[256,1024]{1,0:T(8,128)(2,1)} %bitcast.57) | data formatting | bytes 1048576
  (129 shorter events, 7.5 us)
Async XLA Ops:
  7.2 43.1 %copy-start = (bf16[4096,256]{1,0:T(8,128)(2,1)S(1)}, bf16[4096,256]{1,0:T(8,128)(2,1)}, u32[]{:S(2)}) copy-start(bf16[4096,256]{1,0:T(8,128)(2,1)} %param.13) | copy-start | bytes 6291460
  7.2 27.7 %all-gather.3.cloned.1.call-start = ((), (), s32[]{:S(2)}) async-start(), calls=%async_computation.1 | async-start | bytes 2621440 | tf_op jit(solution)/shard_map/all_gather | solution.py:186
  7.9 51.7 %all-gather.5.cloned.1.call-start = ((), (), s32[]{:S(2)}) async-start(), calls=%async_computation.2 | async-start | bytes 2621440 | tf_op jit(solution)/shard_map/all_gather | solution.py:219
  9.2 13.3 %collective-permute-start = (bf16[32,1024]{1,0:T(8,128)(2,1)S(1)}, bf16[32,1024]{1,0:T(8,128)(2,1)S(1)}, u32[]{:S(2)}, u32[]{:S(2)}) collective-permute-start(bf16[32,1024]{1,0:T(8,128)(2,1)S(1)} %get-tuple-element.41), channel_id=1, source_target_pairs={{0,4},{4,8},{8,12},{12,16},{16,20},{20,24},{24,28},{28,0},{1,5},{5... | collective-permute-start | bytes 196616 | tf_op jit(solution)/shard_map/ppermute | solution.py:164
  12.2 11.7 %collective-permute-start.1 = (bf16[32,1024]{1,0:T(8,128)(2,1)S(1)}, bf16[32,1024]{1,0:T(8,128)(2,1)S(1)}, u32[]{:S(2)}, u32[]{:S(2)}) collective-permute-start(bf16[32,1024]{1,0:T(8,128)(2,1)S(1)} %get-tuple-element.40), channel_id=1, source_target_pairs={{0,8},{4,12},{8,16},{12,20},{16,24},{20,28},{24,0},{28,4},{1,9},{5... | collective-permute-start | bytes 196616 | tf_op jit(solution)/shard_map/ppermute | solution.py:164
  13.8 13.0 %collective-permute-start.2 = (bf16[32,1024]{1,0:T(8,128)(2,1)S(1)}, bf16[32,1024]{1,0:T(8,128)(2,1)S(1)}, u32[]{:S(2)}, u32[]{:S(2)}) collective-permute-start(bf16[32,1024]{1,0:T(8,128)(2,1)S(1)} %get-tuple-element.39), channel_id=1, source_target_pairs={{0,12},{4,16},{8,20},{12,24},{16,28},{20,0},{24,4},{28,8},{1,13},{... | collective-permute-start | bytes 196616 | tf_op jit(solution)/shard_map/ppermute | solution.py:164
  16.3 10.6 %collective-permute-start.3 = (bf16[32,1024]{1,0:T(8,128)(2,1)S(1)}, bf16[32,1024]{1,0:T(8,128)(2,1)S(1)}, u32[]{:S(2)}, u32[]{:S(2)}) collective-permute-start(bf16[32,1024]{1,0:T(8,128)(2,1)S(1)} %get-tuple-element.38), channel_id=1, source_target_pairs={{0,16},{4,20},{8,24},{12,28},{16,0},{20,4},{24,8},{28,12},{1,17},{... | collective-permute-start | bytes 196616 | tf_op jit(solution)/shard_map/ppermute | solution.py:164
  17.5 9.5 %collective-permute-start.4 = (bf16[32,1024]{1,0:T(8,128)(2,1)S(1)}, bf16[32,1024]{1,0:T(8,128)(2,1)S(1)}, u32[]{:S(2)}, u32[]{:S(2)}) collective-permute-start(bf16[32,1024]{1,0:T(8,128)(2,1)S(1)} %get-tuple-element.37), channel_id=1, source_target_pairs={{0,20},{4,24},{8,28},{12,0},{16,4},{20,8},{24,12},{28,16},{1,21},{... | collective-permute-start | bytes 196616 | tf_op jit(solution)/shard_map/ppermute | solution.py:164
  22.5 5.3 %collective-permute-start.5 = (bf16[32,1024]{1,0:T(8,128)(2,1)S(1)}, bf16[32,1024]{1,0:T(8,128)(2,1)S(1)}, u32[]{:S(2)}, u32[]{:S(2)}) collective-permute-start(bf16[32,1024]{1,0:T(8,128)(2,1)S(1)} %get-tuple-element.36), channel_id=1, source_target_pairs={{0,24},{4,28},{8,0},{12,4},{16,8},{20,12},{24,16},{28,20},{1,25},{... | collective-permute-start | bytes 196616 | tf_op jit(solution)/shard_map/ppermute | solution.py:164
  23.9 4.7 %collective-permute-start.6 = (bf16[32,1024]{1,0:T(8,128)(2,1)S(1)}, bf16[32,1024]{1,0:T(8,128)(2,1)S(1)}, u32[]{:S(2)}, u32[]{:S(2)}) collective-permute-start(bf16[32,1024]{1,0:T(8,128)(2,1)S(1)} %get-tuple-element.35), channel_id=1, source_target_pairs={{0,28},{4,0},{8,4},{12,8},{16,12},{20,16},{24,20},{28,24},{1,29},{... | collective-permute-start | bytes 196616 | tf_op jit(solution)/shard_map/ppermute | solution.py:164
  32.6 5.1 %copy-start.25 = (f32[4096]{0:T(1024)S(1)}, f32[4096]{0:T(1024)}, u32[]{:S(2)}) copy-start(f32[4096]{0:T(1024)} %param.10) | copy-start | bytes 49156
  34.9 2.8 %copy-start.3 = (bf16[256,4096]{1,0:T(8,128)(2,1)S(1)}, bf16[256,4096]{1,0:T(8,128)(2,1)}, u32[]{:S(2)}) copy-start(bf16[256,4096]{1,0:T(8,128)(2,1)} %all-gather.3.cloned.1.call-done) | copy-start | bytes 6291460
  37.7 12.5 %copy-start.27 = (f32[256]{0:T(256)}, f32[256]{0:T(256)S(1)}, u32[]{:S(2)}) copy-start(f32[256]{0:T(256)S(1)} %get-tuple-element.52) | copy-start | bytes 3076
  48.3 1.1 copy-start.23
  48.4 0.8 copy-start.14
  48.5 0.9 copy-start.16
  48.5 1.9 %copy-start.4 = (bf16[256,4096]{1,0:T(8,128)(2,1)S(1)}, bf16[256,4096]{1,0:T(8,128)(2,1)}, u32[]{:S(2)}) copy-start(bf16[256,4096]{1,0:T(8,128)(2,1)} %all-gather.3.cloned.1.call-done) | copy-start | bytes 6291460
  48.6 3.1 %copy-start.21 = (bf16[256,2,64]{2,0,1:T(8,128)(2,1)}, bf16[256,2,64]{2,0,1:T(8,128)(2,1)S(1)}, u32[]{:S(2)}) copy-start(bf16[256,2,64]{2,0,1:T(8,128)(2,1)S(1)} %get-tuple-element.32) | copy-start | bytes 196612
  50.4 1.3 copy-start.32
  50.4 1.3 copy-start.34
  50.4 3.0 %slice-start = ((s8[8388608]{0:T(1024)(128)(4,1)}), s8[4194304]{0:T(1024)(128)(4,1)S(1)}, s32[]{:S(2)}) async-start(s8[8388608]{0:T(1024)(128)(4,1)} %bitcast.171), calls=%async_computation.3 | async-start | bytes 8388608
  51.6 0.8 copy-start.31
  51.7 3.1 %slice-start.1 = ((s8[8388608]{0:T(1024)(128)(4,1)}), s8[4194304]{0:T(1024)(128)(4,1)S(1)}, s32[]{:S(2)}) async-start(s8[8388608]{0:T(1024)(128)(4,1)} %bitcast.171), calls=%async_computation.4 | async-start | bytes 8388608
  62.4 12.0 %collective-permute-start.7 = (bf16[2,256,1024]{2,1,0:T(8,128)(2,1)}, bf16[2,256,1024]{2,1,0:T(8,128)(2,1)}, u32[]{:S(2)}, u32[]{:S(2)}) collective-permute-start(bf16[2,256,1024]{2,1,0:T(8,128)(2,1)} %pad_maximum_fusion), channel_id=1, source_target_pairs={{0,1},{1,0},{2,3},{3,2},{4,5},{5,4},{6,7},{7,6},{8,9},{9,8},{10,11... | collective-permute-start | bytes 3145736 | tf_op jit(solution)/shard_map/ppermute | solution.py:107
  63.4 4.2 %copy-start.30 = (bf16[256,4096]{1,0:T(8,128)(2,1)S(1)}, bf16[256,4096]{1,0:T(8,128)(2,1)}, u32[]{:S(2)}) copy-start(bf16[256,4096]{1,0:T(8,128)(2,1)} %all-gather.5.cloned.1.call-done) | copy-start | bytes 6291460
  75.6 2.7 %copy-start.12 = (bf16[256,1024]{0,1:T(8,128)(2,1)}, bf16[256,1024]{0,1:T(8,128)(2,1)S(1)}, u32[]{:S(2)}) copy-start(bf16[256,1024]{0,1:T(8,128)(2,1)S(1)} %copy.99) | copy-start | bytes 1572868
  75.8 2.5 %copy-start.15 = (bf16[256,8,64]{2,0,1:T(8,128)(2,1)S(1)}, bf16[256,8,64]{2,0,1:T(8,128)(2,1)}, u32[]{:S(2)}) copy-start(bf16[256,8,64]{2,0,1:T(8,128)(2,1)} %copy-done.14) | copy-start | bytes 786436
  75.8 2.5 %copy-start.17 = (bf16[256,8,64]{2,0,1:T(8,128)(2,1)S(1)}, bf16[256,8,64]{2,0,1:T(8,128)(2,1)}, u32[]{:S(2)}) copy-start(bf16[256,8,64]{2,0,1:T(8,128)(2,1)} %copy-done.16) | copy-start | bytes 786436
  78.3 1.3 copy-start.22
  86.7 6.7 %slice-start.2 = ((s8[8388608]{0:T(1024)(128)(4,1)}), s8[4194304]{0:T(1024)(128)(4,1)S(1)}, s32[]{:S(2)}) async-start(s8[8388608]{0:T(1024)(128)(4,1)} %bitcast.178), calls=%async_computation.5 | async-start | bytes 8388608
  90.2 2.5 %copy-start.13 = (bf16[256,1024]{0,1:T(8,128)(2,1)S(1)}, bf16[256,1024]{0,1:T(8,128)(2,1)}, u32[]{:S(2)}) copy-start(bf16[256,1024]{0,1:T(8,128)(2,1)} %copy-done.12) | copy-start | bytes 1572868
  90.2 2.5 %copy-start.24 = (pred[256,256]{0,1:T(8,128)(4,1)S(1)}, pred[256,256]{0,1:T(8,128)(4,1)}, u32[]{:S(2)}) copy-start(pred[256,256]{0,1:T(8,128)(4,1)} %fusion.46) | copy-start | bytes 196612
  90.2 2.5 %copy-start.33 = (f32[2,256,256,4]{2,1,3,0:T(8,128)S(1)}, f32[2,256,256,4]{2,1,3,0:T(8,128)}, u32[]{:S(2)}) copy-start(f32[2,256,256,4]{2,1,3,0:T(8,128)} %copy-done.32) | copy-start | bytes 6291460
  90.2 2.5 %copy-start.35 = (f32[2,4,256]{2,1,0:T(4,128)S(1)}, f32[2,4,256]{2,1,0:T(4,128)}, u32[]{:S(2)}) copy-start(f32[2,4,256]{2,1,0:T(4,128)} %copy-done.34) | copy-start | bytes 24580
  92.7 2.2 %slice-start.3 = ((s8[8388608]{0:T(1024)(128)(4,1)}), s8[4194304]{0:T(1024)(128)(4,1)S(1)}, s32[]{:S(2)}) async-start(s8[8388608]{0:T(1024)(128)(4,1)} %bitcast.178), calls=%async_computation.6 | async-start | bytes 8388608
  96.6 1.8 %copy-start.11 = (f32[256,2,128]{2,0,1:T(8,128)S(1)}, f32[256,2,128]{2,0,1:T(8,128)}, u32[]{:S(2)}) copy-start(f32[256,2,128]{2,0,1:T(8,128)} %fusion.13) | copy-start | bytes 786436
  98.8 2.1 %copy-start.8 = (f32[256,1024]{1,0:T(8,128)S(1)}, f32[256,1024]{1,0:T(8,128)}, u32[]{:S(2)}) copy-start(f32[256,1024]{1,0:T(8,128)} %fusion.2) | copy-start | bytes 3145732
  98.8 4.5 %copy-start.10 = (f32[256,1024]{1,0:T(8,128)S(1)}, f32[256,1024]{1,0:T(8,128)}, u32[]{:S(2)}) copy-start(f32[256,1024]{1,0:T(8,128)} %fusion.8) | copy-start | bytes 3145732
  98.9 4.5 %copy-start.18 = (bf16[4096,256]{1,0:T(8,128)(2,1)S(1)}, bf16[4096,256]{1,0:T(8,128)(2,1)}, u32[]{:S(2)}) copy-start(bf16[4096,256]{1,0:T(8,128)(2,1)} %param.12) | copy-start | bytes 6291460
  100.5 14.2 %collective-permute-start.9 = (bf16[1,256,1024]{2,1,0:T(8,128)(2,1)S(1)}, bf16[1,256,1024]{2,1,0:T(8,128)(2,1)S(1)}, u32[]{:S(2)}, u32[]{:S(2)}) collective-permute-start(bf16[1,256,1024]{2,1,0:T(8,128)(2,1)S(1)} %fusion.25), channel_id=1, source_target_pairs={{0,2},{1,3},{2,0},{3,1},{4,6},{5,7},{6,4},{7,5},{8,10},{9,11},{10,... | collective-permute-start | bytes 1572872 | tf_op jit(solution)/shard_map/ppermute | solution.py:107
  100.9 2.8 %copy-start.9 = (f32[256,1024]{1,0:T(8,128)S(1)}, f32[256,1024]{1,0:T(8,128)}, u32[]{:S(2)}) copy-start(f32[256,1024]{1,0:T(8,128)} %fusion.6) | copy-start | bytes 3145732
  104.4 1.0 copy-start.1
  104.8 1.0 copy-start.2
  105.8 9.0 %copy-start.6 = (bf16[256,1024]{1,0:T(8,128)(2,1)S(1)}, bf16[256,1024]{1,0:T(8,128)(2,1)}, u32[]{:S(2)}) copy-start(bf16[256,1024]{1,0:T(8,128)(2,1)} %param.9) | copy-start | bytes 1572868
  105.8 11.1 %collective-permute-start.8 = (bf16[2,256,1024]{2,1,0:T(8,128)(2,1)S(1)}, bf16[2,256,1024]{2,1,0:T(8,128)(2,1)S(1)}, u32[]{:S(2)}, u32[]{:S(2)}) collective-permute-start(bf16[2,256,1024]{2,1,0:T(8,128)(2,1)S(1)} %pad_maximum_fusion.1), channel_id=1, source_target_pairs={{0,1},{1,0},{2,3},{3,2},{4,5},{5,4},{6,7},{7,6},{8,9},{9,8},{10,11... | collective-permute-start | bytes 3145736 | tf_op jit(solution)/shard_map/ppermute | solution.py:109
  106.5 9.9 %copy-start.29 = (s32[8]{0:T(128)S(1)}, s32[8]{0:T(128)}, u32[]{:S(2)}) copy-start(s32[8]{0:T(128)} %get-tuple-element.21) | copy-start | bytes 100
  116.8 1.0 copy-start.19
  118.9 24.2 %all-to-all-start = ((bf16[8,32,1024]{2,1,0:T(8,128)(2,1)}), bf16[8,32,1024]{2,1,0:T(8,128)(2,1)}, u32[]{:S(2)}, u32[]{:S(2)}) async-start(bf16[8,32,1024]{2,1,0:T(8,128)(2,1)} %copy.112), calls=%async_computation | async-start | bytes 1048576 | tf_op jit(solution)/shard_map/all_to_all | solution.py:305
  124.4 17.4 %copy-start.5 = (bf16[8,32,1024]{2,1,0:T(8,128)(2,1)S(1)}, bf16[8,32,1024]{2,1,0:T(8,128)(2,1)}, u32[]{:S(2)}) copy-start(bf16[8,32,1024]{2,1,0:T(8,128)(2,1)} %copy.98) | copy-start | bytes 1572868
  124.4 17.4 %copy-start.7 = (bf16[256,1024]{1,0:T(8,128)(2,1)S(1)}, bf16[256,1024]{1,0:T(8,128)(2,1)}, u32[]{:S(2)}) copy-start(bf16[256,1024]{1,0:T(8,128)(2,1)} %param.9) | copy-start | bytes 1572868
  124.5 17.4 %copy-start.20 = (bf16[2,256,1024]{2,1,0:T(8,128)(2,1)S(1)}, bf16[2,256,1024]{2,1,0:T(8,128)(2,1)}, u32[]{:S(2)}) copy-start(bf16[2,256,1024]{2,1,0:T(8,128)(2,1)} %copy-done.19) | copy-start | bytes 3145732
  124.5 17.4 %copy-start.26 = (f32[256]{0:T(256)S(1)}, f32[256]{0:T(256)}, u32[]{:S(2)}) copy-start(f32[256]{0:T(256)} %get-tuple-element.51) | copy-start | bytes 3076
  124.5 17.4 %copy-start.28 = (f32[256]{0:T(256)S(1)}, f32[256]{0:T(256)}, u32[]{:S(2)}) copy-start(f32[256]{0:T(256)} %copy-done.27) | copy-start | bytes 3076
  128.7 13.1 %collective-permute-start.10 = (bf16[1,256,1024]{2,1,0:T(8,128)(2,1)S(1)}, bf16[1,256,1024]{2,1,0:T(8,128)(2,1)S(1)}, u32[]{:S(2)}, u32[]{:S(2)}) collective-permute-start(bf16[1,256,1024]{2,1,0:T(8,128)(2,1)S(1)} %get-tuple-element.28), channel_id=1, source_target_pairs={{0,2},{1,3},{2,0},{3,1},{4,6},{5,7},{6,4},{7,5},{8,10},{9,11},{10,... | collective-permute-start | bytes 1572872 | tf_op jit(solution)/shard_map/ppermute | solution.py:109
  129.3 1.1 collective-permute-start.11
  130.4 11.4 %collective-permute-start.12 = (f32[256]{0:T(256)S(1)}, f32[256]{0:T(256)S(1)}, u32[]{:S(2)}, u32[]{:S(2)}) collective-permute-start(f32[256]{0:T(256)S(1)} %add.252), channel_id=1, source_target_pairs={{0,2},{1,3},{2,0},{3,1},{4,6},{5,7},{6,4},{7,5},{8,10},{9,11},{10,... | collective-permute-start | bytes 3080 | tf_op jit(solution)/shard_map/ppermute | solution.py:109
Sparse Core Ops, SparseCore 0:
  9.6 25.2 all-gather.2
  37.0 22.5 all-gather.4

commit v20 on v12

--- a/solution.py
+++ b/solution.py
@@ -59,14 +59,19 @@
     return [(i, i ^ bit) for i in range(size)]
 
 
-def gather_features(shard, axis_name, size, position):
+def gather_features(shard, axis_name, size, position, tied=None):
     if not _is_pow2(size):
-        return lax.all_gather(shard, axis_name, axis=1, tiled=True)
+        return lax.all_gather(shard, axis_name, axis=1, tiled=True), tied
     held = shard[None]
     masks = [0]
+    tied_done = tied
     bit = size >> 1
     while bit:
         incoming = lax.ppermute(held, axis_name, _xor_pairs(size, bit))
+        if tied is not None:
+            incoming, tied = lax.optimization_barrier((incoming, tied))
+            tied_done = tied
+            tied = None
         held = jnp.concatenate([held, incoming], axis=0)
         masks = masks + [m ^ bit for m in masks]
         bit >>= 1
@@ -75,7 +80,7 @@
         lax.dynamic_index_in_dim(held, table[s ^ position], axis=0, keepdims=False)
         for s in range(size)
     ]
-    return jnp.concatenate(blocks, axis=1)
+    return jnp.concatenate(blocks, axis=1), tied_done
 
 
 def scatter_features(partial, axis_name, size, position, extra=None, ties=()):
@@ -148,6 +153,9 @@
     send_table = (owner_row[None, :] == slot_index[:, None]).astype(jnp.bfloat16)
 
     home_rows = token_row_count // block_count
+    gathered, grad_output = gather_features(
+        tokens, "tensor", tensor_size, tensor_index, tied=grad_output
+    )
     owned_blocks = grad_output.reshape(block_count, home_rows, width_part)
     if sources <= 16:
         returned = [lax.dynamic_index_in_dim(owned_blocks, data_index, 0, keepdims=False)]
@@ -178,7 +186,6 @@
             .reshape(token_row_count, width_part)
         )
 
-    gathered = lax.all_gather(tokens, "tensor", axis=1, tiled=True)
     gathered_float = gathered.astype(jnp.float32)
     inverse = lax.rsqrt(jnp.mean(gathered_float * gathered_float, axis=1) + NORM_EPSILON)
     normed_input = (gathered_float * inverse[:, None] * norm_gain[None, :]).astype(jnp.bfloat16)
@@ -211,7 +218,7 @@
     ).astype(jnp.bfloat16)
     attended_flat = attended.reshape(token_row_count, query_width)
     mixed_partial = jnp.dot(attended_flat, w_out, preferred_element_type=jnp.float32)
-    grad_full = lax.all_gather(grad_home, "tensor", axis=1, tiled=True)
+    grad_full, _ = gather_features(grad_home, "tensor", tensor_size, tensor_index)
     mixed_partial, grad_full = lax.optimization_barrier((mixed_partial, grad_full))
     attended_gradient = lax.dot_general(
         grad_full,

time: 135 us -> 161 us (1.19)
  waiting for transfers between devices: 14.8 us -> 29.6 us
  local copies, waits for them, and re-layouts: 25.4 us -> 34.7 us
  other arithmetic: 22.8 us -> 29.1 us
  between operations: 14.8 us -> 8.71 us
  starting transfers between devices: 21.3 us -> 24.2 us
    ppermute x0 -> x4, waiting for transfers between devices: none -> 13.6 us  [gather_features(): incoming = lax.ppermute(held, axis_name, _xor_pairs(size, bit))]
    concatenate x0 -> x5, other arithmetic: none -> 7.3 us  [the longest x4 5.24 us: gather_features(): held = jnp.concatenate([held, incoming], axis=0)]
    unnamed x69 -> x107, local copies, waits for them, and re-layouts: 12 us -> 18.6 us
    ppermute x0 -> x4, starting transfers between devices: none -> 4.62 us  [gather_features(): incoming = lax.ppermute(held, axis_name, _xor_pairs(size, bit))]
    ppermute x7, waiting for transfers between devices: 2.83 us -> 5.03 us  [per_device(): returned.append(lax.ppermute(piece, 'dp', pairs))]
    dot_general x1, matrix products: 4.52 us -> 2.38 us  [per_device(): jnp.dot(attended_flat, w_out, preferred_element_type=jnp.float32)]
    squeeze x0 -> x1, local copies, waits for them, and re-layouts: none -> 1.78 us  [gather_features(): lax.dynamic_index_in_dim(held, table[s ^ position], axis=0, keepdims=False)]
    reduce_sum x1, other arithmetic: 2.23 us -> 0.49 us  [per_device(): jnp.mean(gathered_float * gathered_float, axis=1) + NORM_EPSILON]
  transfers between devices with their start and end apart: 16 -> 18, of which waited for: 5 -> 7; matrix products, arithmetic and copies ran while one was open for 43% -> 22% of each run, Pallas kernels for 0% -> 0%
where the time goes in v20:
time: 161 us; the launch traced here: 160 us
  local copies, waits for them, and re-layouts  34.7 us (22%)
  matrix products  33.7 us (21%)
  waiting for transfers between devices  29.6 us (18%)
  other arithmetic  29.1 us (18%)
  starting transfers between devices  24.2 us (15%)
  between operations  8.71 us (5%)
    unnamed x107, local copies, waits for them, and re-layouts  18.6 us
    ppermute x4, waiting for transfers between devices, gather_features(): incoming = lax.ppermute(held, axis_name, _xor_pairs(size, bit))  13.6 us
    ppermute x7, starting transfers between devices, per_device(): returned.append(lax.ppermute(piece, 'dp', pairs))  11.2 us
    ppermute x4, waiting for transfers between devices, scatter_features(): lax.ppermute((outgoing, extra), axis_name, _xor_pairs(size, bit))  11 us
    dot_general x1, matrix products, per_device(): lax.dot_general(grad_full, w_out, (((1,), (1,)), ((), ())), preferred_ele...  7.18 us
    dot_general x1, matrix products, per_device(): jnp.dot(normed_input, w_query, preferred_element_type=jnp.float32)  6.42 us
    dot_general x1, matrix products, per_device(): lax.dot_general(grad_query.reshape(token_row_count, query_width), w_query...  5.79 us
    concatenate x4, other arithmetic, gather_features(): held = jnp.concatenate([held, incoming], axis=0)  5.24 us
  transfers between devices with their start and end apart: 18, of which 7 were waited for; matrix products, arithmetic and copies ran while one was open for 22% of the time, Pallas kernels for 0%

profile of v20, /device:TPU:0, one launch (start us, length us, event | category | flops | bytes accessed | tf_op | source)
XLA Modules:
  0.0 160.1 jit_solution(10567199215463632292)
XLA Ops:
  0.6 3.0 %collective-permute-start = (bf16[1,256,1024]{2,1,0:T(8,128)(2,1)}, bf16[1,256,1024]{2,1,0:T(8,128)(2,1)S(1)}, u32[]{:S(2)}, u32[]{:S(2)}) collective-permute-start(bf16[1,256,1024]{2,1,0:T(8,128)(2,1)} %bitcast.187), channel_id=1, source_target_pairs={{0,2},{1,3},{2,0},{3,1},{4,6},{5,7},{6,4},{7,5},{8,10},{9,11},{10,... | collective-permute-start | bytes 1572872 | tf_op jit(solution)/shard_map/ppermute | solution.py:70
  3.7 12.1 %collective-permute-done = bf16[1,256,1024]{2,1,0:T(8,128)(2,1)S(1)} collective-permute-done((bf16[1,256,1024]{2,1,0:T(8,128)(2,1)}, bf16[1,256,1024]{2,1,0:T(8,128)(2,1)S(1)}, u32[]{:S(2)}, u32[]{:S(2)}) %collective-permute-start) | collective-permute-done | bytes 524320 | tf_op jit(solution)/shard_map/ppermute | solution.py:70
  15.8 1.3 dynamic-slice_bitcast_fusion.8
  17.1 4.8 %collective-permute-start.8 = (bf16[32,1024]{1,0:T(8,128)(2,1)S(1)}, bf16[32,1024]{1,0:T(8,128)(2,1)S(1)}, u32[]{:S(2)}, u32[]{:S(2)}) collective-permute-start(bf16[32,1024]{1,0:T(8,128)(2,1)S(1)} %get-tuple-element.48), channel_id=1, source_target_pairs={{0,28},{4,0},{8,4},{12,8},{16,12},{20,16},{24,20},{28,24},{1,29},{... | collective-permute-start | bytes 196616 | tf_op jit(solution)/shard_map/ppermute | solution.py:167
  22.4 3.0 %collective-permute-start.5 = (bf16[32,1024]{1,0:T(8,128)(2,1)S(1)}, bf16[32,1024]{1,0:T(8,128)(2,1)S(1)}, u32[]{:S(2)}, u32[]{:S(2)}) collective-permute-start(bf16[32,1024]{1,0:T(8,128)(2,1)S(1)} %get-tuple-element.51), channel_id=1, source_target_pairs={{0,16},{4,20},{8,24},{12,28},{16,0},{20,4},{24,8},{28,12},{1,17},{... | collective-permute-start | bytes 196616 | tf_op jit(solution)/shard_map/ppermute | solution.py:167
  25.4 1.8 %collective-permute-start.3 = (bf16[32,1024]{1,0:T(8,128)(2,1)S(1)}, bf16[32,1024]{1,0:T(8,128)(2,1)S(1)}, u32[]{:S(2)}, u32[]{:S(2)}) collective-permute-start(bf16[32,1024]{1,0:T(8,128)(2,1)S(1)} %get-tuple-element.53), channel_id=1, source_target_pairs={{0,8},{4,12},{8,16},{12,20},{16,24},{20,28},{24,0},{28,4},{1,9},{5... | collective-permute-start | bytes 196616 | tf_op jit(solution)/shard_map/ppermute | solution.py:167
  27.2 1.1 collective-permute-start.2
  28.3 1.2 and_select_fusion
  30.0 1.3 collective-permute-done.5
  31.4 3.7 %collective-permute-done.4 = bf16[32,1024]{1,0:T(8,128)(2,1)S(1)} collective-permute-done((bf16[32,1024]{1,0:T(8,128)(2,1)S(1)}, bf16[32,1024]{1,0:T(8,128)(2,1)S(1)}, u32[]{:S(2)}, u32[]{:S(2)}) %collective-permute-start.4) | collective-permute-done | bytes 65568 | tf_op jit(solution)/shard_map/ppermute | solution.py:167
  35.3 0.7 copy.95
  36.1 3.6 %stack.58 = bf16[8,32,1024]{2,0,1:T(8,128)(2,1)} concatenate(bf16[1,32,1024]{2,0,1:T(2,128)(2,1)S(1)} %copy.137, bf16[1,32,1024]{2,0,1:T(2,128)(2,1)} %copy.95, bf16[1,32,1024]{2,0,1:T(2,128)(2,1)S(1)} %copy.96, bf16[1,32,1024]{2,0,1:T(2,128)(2,1)S(1)} %copy.97, bf16[1,32,1024]{2,0,1:T(2,128)(2,1)S(1)} %copy.98, bf16[1,32,1024]{2,0,1:T(2,128)(2,1)S(1)} %copy.99, ...), dimensions={0} | concatenate | bytes 1048576 | tf_op jit(solution)/shard_map/stack | solution.py:168
  39.7 1.5 convolution_convert_fusion.3
  41.1 1.1 copy.102
  42.2 1.5 collective-permute-start.9
  43.7 1.1 pad_maximum_fusion.4
  44.8 0.7 fusion.55
  53.0 1.4 collective-permute-done.9
  54.4 1.3 pad_maximum_fusion.5
  55.9 0.7 fusion.31
  57.2 1.4 pad_maximum_fusion
  58.7 1.4 pad_maximum_fusion.2
  60.1 1.8 %dynamic-slice_bitcast_fusion.3 = (bf16[256,1024]{1,0:T(8,128)(2,1)}, bf16[256,1024]{1,0:T(8,128)(2,1)}, bf16[256,1024]{1,0:T(8,128)(2,1)}, bf16[256,1024]{1,0:T...) fusion(bf16[4,256,1024]{2,1,0:T(8,128)(2,1)S(1)} %pad_maximum_f, ...), kind=kLoop, calls=%fused_computation.75 | loop fusion | bytes 8388624 | tf_op jit(solution)/shard_map/jit(dynamic_index_in_dim)/squeeze | solution.py:80
  62.9 1.3 copy-done.18
  64.2 1.8 %convolution_convert_fusion.4 = bf16[256,256]{0,1:T(8,128)(2,1)} fusion(bf16[4096,256]{1,0:T(8,128)(2,1)S(1)} %copy-done.18, f32[4096]{0:T(1024)S(1)} %copy-done.36, f32[256]{0:T(256)S(1)} %get-tuple-element.61, bf16[256,1024]{1,0:T(8,128)(2,1)S(1)} %get-tuple-element.70, bf16[256,1024]{1,0:T(8,128)(2,1)S(1)} %get-tuple-element.69, ...), kind=kOutput, calls=%fused_computation.32 | convolution fusion | flops 548470784 | bytes 4342784 | tf_op jit(solution)/shard_map/dot_general | solution.py:194
  66.0 1.1 fusion.47
  67.2 0.7 fusion.54
  67.9 1.8 %copy.136 = f32[256,2,64]{2,0,1:T(8,128)} copy(f32[256,2,64]{0,2,1:T(8,128)} %get-tuple-element.56) | data formatting | bytes 262144
  69.6 0.8 copy.135
  70.5 6.4 %convolution_bitcast_fusion = f32[32,8,8,128]{3,1,2,0:T(8,128)S(1)} fusion(bf16[4096,1024]{1,0:T(8,128)(2,1)} %param.13, f32[4096]{0:T(1024)S(1)} %copy-done.36, f32[256]{0:T(256)} %copy-done.39, bf16[256,1024]{1,0:T(8,128)(2,1)} %copy-done.8, bf16[256,1024]{1,0:T(8,128)(2,1)} %copy-done.6, bf16[256,1024]{1,0:T(8,128)(2,1)} %copy-done.4, ...), kind=kOutput, calls=%fused_computation.20 | convolution fusion | flops 2159017984 | bytes 11551744 | tf_op jit(solution)/shard_map/dot_general | solution.py:192
  78.5 0.9 fusion.7
  79.7 0.7 convolution_convert_fusion.1
  80.8 2.1 %slice-done.1 = s8[4194304]{0:T(1024)(128)(4,1)S(1)} async-done(((s8[8388608]{0:T(1024)(128)(4,1)}), s8[4194304]{0:T(1024)(128)(4,1)S(1)}, s32[]{:S(2)}) %slice-start.1) | async-done | bytes 4194328
  82.9 2.4 %fusion.56 = f32[256,4096]{1,0:T(8,128)S(1)} fusion(bf16[256,1024]{0,1:T(8,128)(2,1)S(1)} %bitcast.191, bf16[1024,4096]{1,0:T(8,128)(2,1)S(1)} %bitcast.185), kind=kOutput, calls=%fused_computation.129 | convolution fusion | flops 2147483648 | bytes 13107200 | tf_op jit(solution)/shard_map/dot_general | solution.py:220
  85.3 2.1 %pad_maximum_fusion.3 = bf16[256,4096]{1,0:T(8,128)(2,1)} fusion(bf16[256,1024]{1,0:T(8,128)(2,1)S(1)} %copy-done.21, bf16[256,1024]{1,0:T(8,128)(2,1)S(1)} %copy-done.22, bf16[256,1024]{1,0:T(8,128)(2,1)S(1)} %copy-done.23, bf16[256,1024]{1,0:T(8,128)(2,1)S(1)} %copy-done.20), kind=kLoop, calls=%fused_computation.12 | loop fusion | flops 8388608 | bytes 4194304 | tf_op jit(solution)/shard_map/concatenate | solution.py:83
  88.2 1.1 pad_maximum_fusion.6
  89.8 7.2 %convolution_convert_fusion = bf16[256,1024]{1,0:T(8,128)(2,1)} fusion(bf16[256,4096]{1,0:T(8,128)(2,1)} %pad_maximum_fusion.3, bf16[1024,4096]{1,0:T(8,128)(2,1)} %param.16), kind=kOutput, calls=%fused_computation.23 | convolution fusion | flops 2147745792 | bytes 11010048 | tf_op jit(solution)/shard_map/dot_general | solution.py:223
  96.9 2.0 %copy.103 = bf16[256,1024]{0,1:T(8,128)(2,1)} copy(bf16[256,1024]{1,0:T(8,128)(2,1)} %convolution_convert_fusion) | data formatting | bytes 1048576 | tf_op jit(solution)/shard_map/optimization_barrier | solution.py:112
  99.0 1.4 multiply_reduce_fusion
  100.4 2.6 %fusion.5 = bf16[2,4,256,256]{2,3,1,0:T(8,128)(2,1)S(1)} fusion(bf16[256,2,128,1]{0,2,3,1:T(8,128)(2,1)} %bitcast.214, bf16[256,2,4,128]{0,3,2,1:T(8,128)(2,1)} %bitcast.192, f32[2,4,256]{2,1,0:T(4,128)S(1)} %bitcast.211, f32[2,4,256]{2,1,0:T(4,128)} %copy-done.46, f32[2,256,256,4]{2,1,3,0:T(8,128)} %copy-done.44, pred[256,256]{0,1:T(8,128)(4,1)} %fusion.31), kind=kOutput, calls=%fused_computation.15 | convolution fusion | flops 137363456 | bytes 3883008 | tf_op jit(solution)/shard_map/qkgd,skd->kgqs/dot_general | solution.py:237
  104.3 1.1 fusion.53
  105.6 0.8 copy.113
  106.4 2.4 %copy.139 = f32[256,8,64]{2,1,0:T(8,128)} copy(f32[256,8,64]{0,2,1:T(8,128)} %get-tuple-element.42) | data formatting | bytes 1048576
  108.8 2.3 %fusion.23 = bf16[1,256,1024]{2,1,0:T(8,128)(2,1)} fusion(f32[256,4096]{1,0:T(8,128)} %copy-done.2, s32[]{:T(128)S(6)} %select_n.166, bf16[2,256,1024]{2,1,0:T(8,128)(2,1)} %collective-permute-done.11), kind=kLoop, calls=%fused_computation.64 | loop fusion | flops 786432 | bytes 2097156 | tf_op jit(solution)/shard_map/convert_element_type | solution.py:105
  111.1 1.5 collective-permute-start.12
  112.6 2.4 %copy.138 = f32[256,8,64]{2,1,0:T(8,128)} copy(f32[256,8,64]{0,2,1:T(8,128)} %get-tuple-element.43) | data formatting | bytes 1048576
  115.0 1.8 %add_convert_fusion = (bf16[256,8,64]{2,1,0:T(8,128)(2,1)S(1)}, bf16[256,8,64]{2,1,0:T(8,128)(2,1)S(1)}) fusion(f32[256,8,64]{2,1,0:T(8,128)} %copy.139, f32[256,8,64]{2,1,0:T(8,128)} %copy.138, f32[256,64]{1,0:T(8,128)S(1)} %get-tuple-element.59, f32[256,64]{1,0:T(8,128)S(1)} %get-tuple-element.58), kind=kLoop, calls=%fused_computation.54 | loop fusion | flops 1048576 | bytes 1703936 | tf_op jit(solution)/shard_map/convert.13
  117.1 5.8 %fusion.25 = f32[256,4096]{1,0:T(8,128)S(1)} fusion(bf16[4096,1024]{1,0:T(8,128)(2,1)} %param.13, bf16[32,8,8,128]{3,2,1,0:T(8,128)(2,1)S(1)} %bitcast.199), kind=kOutput, calls=%fused_computation.66 | convolution fusion | flops 2147483648 | bytes 13107200 | tf_op jit(solution)/shard_map/dot_general | solution.py:260
  123.0 0.8 convolution_add_fusion.1
  124.0 0.7 copy-done.45
  125.4 0.9 copy-done.19
  126.3 0.8 convolution_add_fusion
  127.1 3.3 %fusion.11 = bf16[256,1024]{1,0:T(8,128)(2,1)S(1)} fusion(bf16[256,1024]{1,0:T(8,128)(2,1)S(1)} %copy-done.3, f32[256,4096]{1,0:T(8,128)} %copy-done.2, s32[]{:T(128)} %select_n.163, bf16[1,256,1024]{2,1,0:T(8,128)(2,1)} %collective-permute-done.12, bf16[2,256,1024]{2,1,0:T(8,128)(2,1)} %collective-permute-done.11), kind=kLoop, calls=%fused_computation.33 | loop fusion | flops 1835008 | bytes 3145732 | tf_op jit(solution)/shard_map/convert_element_type | solution.py:232
  131.5 2.0 %collective-permute-done.13 = bf16[2,256,1024]{2,1,0:T(8,128)(2,1)S(1)} collective-permute-done((bf16[2,256,1024]{2,1,0:T(8,128)(2,1)S(1)}, bf16[2,256,1024]{2,1,0:T(8,128)(2,1)S(1)}, u32[]{:S(2)}, u32[]{:S(2)}) %collective-permute-start.13) | collective-permute-done | bytes 1048608 | tf_op jit(solution)/shard_map/ppermute | solution.py:109
  133.5 1.0 copy-done.29
  134.5 1.1 copy.116
  135.6 4.1 %all-to-all-start = ((bf16[8,32,1024]{2,1,0:T(8,128)(2,1)}), bf16[8,32,1024]{2,1,0:T(8,128)(2,1)}, u32[]{:S(2)}, u32[]{:S(2)}) async-start(bf16[8,32,1024]{2,1,0:T(8,128)(2,1)} %copy.116), calls=%async_computation | async-start | bytes 1048576 | tf_op jit(solution)/shard_map/all_to_all | solution.py:288
  139.8 1.7 %fusion.24 = bf16[1,256,1024]{2,1,0:T(8,128)(2,1)S(1)} fusion(f32[256,4096]{1,0:T(8,128)} %copy-done.1, s32[]{:T(128)S(6)} %select_n.166, bf16[2,256,1024]{2,1,0:T(8,128)(2,1)} %copy-done.29), kind=kLoop, calls=%fused_computation.65 | loop fusion | flops 786432 | bytes 2097156 | tf_op jit(solution)/shard_map/convert_element_type | solution.py:105
  142.1 2.6 %fusion.3 = f32[256]{0:T(256)S(1)} fusion(f32[256,4096]{1,0:T(8,128)} %copy-done.1, f32[4096]{0:T(1024)S(1)} %copy-done.36, bf16[256,1024]{1,0:T(8,128)(2,1)S(1)} %copy-done.9, bf16[256,1024]{1,0:T(8,128)(2,1)S(1)} %copy-done.7, bf16[256,1024]{1,0:T(8,128)(2,1)S(1)} %copy-done.5, bf16[256,1024]{1,0:T(8,128)(2,1)S(1)} %copy-done.11), kind=kLoop, calls=%fused_computation.8 | loop fusion | flops 11534080 | bytes 6308864 | tf_op jit(solution)/shard_map/reduce_sum | solution.py:280
  144.8 1.1 collective-permute-done.15
  145.9 1.5 collective-permute-start.16
  147.7 7.8 %collective-permute-done.16 = f32[256]{0:T(256)S(1)} collective-permute-done((f32[256]{0:T(256)S(1)}, f32[256]{0:T(256)S(1)}, u32[]{:S(2)}, u32[]{:S(2)}) %collective-permute-start.16) | collective-permute-done | bytes 1056 | tf_op jit(solution)/shard_map/ppermute | solution.py:109
  155.6 2.6 %fusion.14 = bf16[256,1024]{1,0:T(8,128)(2,1)} fusion(bf16[256,1024]{1,0:T(8,128)(2,1)S(1)} %copy-done.3, f32[8,32,1024]{2,1,0:T(8,128)S(1)} %copy.117, f32[256,4096]{1,0:T(8,128)} %copy-done.1, s32[]{:T(128)} %select_n.163, bf16[1,256,1024]{2,1,0:T(8,128)(2,1)S(1)} %collective-permute-done.14, f32[256]{0:T(256)S(1)} %add_multiply_fusion, ...), kind=kLoop, calls=%fused_computation.36 | loop fusion | flops 3145728 | bytes 4201476 | tf_op jit(solution)/shard_map/convert_element_type | solution.py:298
  158.2 1.9 %copy.149 = bf16[256,1024]{1,0:T(8,128)(2,1)} copy(bf16[256,1024]{1,0:T(8,128)(2,1)} %bitcast.69) | data formatting | bytes 1048576
  (150 shorter events, 11.5 us)
Async XLA Ops:
  0.6 65.4 %copy-start = (bf16[4096,256]{1,0:T(8,128)(2,1)S(1)}, bf16[4096,256]{1,0:T(8,128)(2,1)}, u32[]{:S(2)}) copy-start(bf16[4096,256]{1,0:T(8,128)(2,1)} %param.14) | copy-start | bytes 6291460
  0.6 15.2 %collective-permute-start = (bf16[1,256,1024]{2,1,0:T(8,128)(2,1)}, bf16[1,256,1024]{2,1,0:T(8,128)(2,1)S(1)}, u32[]{:S(2)}, u32[]{:S(2)}) collective-permute-start(bf16[1,256,1024]{2,1,0:T(8,128)(2,1)} %bitcast.187), channel_id=1, source_target_pairs={{0,2},{1,3},{2,0},{3,1},{4,6},{5,7},{6,4},{7,5},{8,10},{9,11},{10,... | collective-permute-start | bytes 1572872 | tf_op jit(solution)/shard_map/ppermute | solution.py:70
  15.8 19.3 %copy-start.24 = (bf16[1,256,1024]{2,1,0:T(8,128)(2,1)}, bf16[1,256,1024]{2,1,0:T(8,128)(2,1)S(1)}, u32[]{:S(2)}) copy-start(bf16[1,256,1024]{2,1,0:T(8,128)(2,1)S(1)} %collective-permute-done) | copy-start | bytes 1572868
  17.1 8.3 %collective-permute-start.8 = (bf16[32,1024]{1,0:T(8,128)(2,1)S(1)}, bf16[32,1024]{1,0:T(8,128)(2,1)S(1)}, u32[]{:S(2)}, u32[]{:S(2)}) collective-permute-start(bf16[32,1024]{1,0:T(8,128)(2,1)S(1)} %get-tuple-element.48), channel_id=1, source_target_pairs={{0,28},{4,0},{8,4},{12,8},{16,12},{20,16},{24,20},{28,24},{1,29},{... | collective-permute-start | bytes 196616 | tf_op jit(solution)/shard_map/ppermute | solution.py:167
  21.9 5.3 %collective-permute-start.7 = (bf16[32,1024]{1,0:T(8,128)(2,1)S(1)}, bf16[32,1024]{1,0:T(8,128)(2,1)S(1)}, u32[]{:S(2)}, u32[]{:S(2)}) collective-permute-start(bf16[32,1024]{1,0:T(8,128)(2,1)S(1)} %get-tuple-element.49), channel_id=1, source_target_pairs={{0,24},{4,28},{8,0},{12,4},{16,8},{20,12},{24,16},{28,20},{1,25},{... | collective-permute-start | bytes 196616 | tf_op jit(solution)/shard_map/ppermute | solution.py:167
  22.4 7.5 %collective-permute-start.6 = (bf16[32,1024]{1,0:T(8,128)(2,1)S(1)}, bf16[32,1024]{1,0:T(8,128)(2,1)S(1)}, u32[]{:S(2)}, u32[]{:S(2)}) collective-permute-start(bf16[32,1024]{1,0:T(8,128)(2,1)S(1)} %get-tuple-element.50), channel_id=1, source_target_pairs={{0,20},{4,24},{8,28},{12,0},{16,4},{20,8},{24,12},{28,16},{1,21},{... | collective-permute-start | bytes 196616 | tf_op jit(solution)/shard_map/ppermute | solution.py:167
  22.4 8.9 %collective-permute-start.5 = (bf16[32,1024]{1,0:T(8,128)(2,1)S(1)}, bf16[32,1024]{1,0:T(8,128)(2,1)S(1)}, u32[]{:S(2)}, u32[]{:S(2)}) collective-permute-start(bf16[32,1024]{1,0:T(8,128)(2,1)S(1)} %get-tuple-element.51), channel_id=1, source_target_pairs={{0,16},{4,20},{8,24},{12,28},{16,0},{20,4},{24,8},{28,12},{1,17},{... | collective-permute-start | bytes 196616 | tf_op jit(solution)/shard_map/ppermute | solution.py:167
  25.4 9.7 %collective-permute-start.4 = (bf16[32,1024]{1,0:T(8,128)(2,1)S(1)}, bf16[32,1024]{1,0:T(8,128)(2,1)S(1)}, u32[]{:S(2)}, u32[]{:S(2)}) collective-permute-start(bf16[32,1024]{1,0:T(8,128)(2,1)S(1)} %get-tuple-element.52), channel_id=1, source_target_pairs={{0,12},{4,16},{8,20},{12,24},{16,28},{20,0},{24,4},{28,8},{1,13},{... | collective-permute-start | bytes 196616 | tf_op jit(solution)/shard_map/ppermute | solution.py:167
  25.4 9.8 %collective-permute-start.3 = (bf16[32,1024]{1,0:T(8,128)(2,1)S(1)}, bf16[32,1024]{1,0:T(8,128)(2,1)S(1)}, u32[]{:S(2)}, u32[]{:S(2)}) collective-permute-start(bf16[32,1024]{1,0:T(8,128)(2,1)S(1)} %get-tuple-element.53), channel_id=1, source_target_pairs={{0,8},{4,12},{8,16},{12,20},{16,24},{20,28},{24,0},{28,4},{1,9},{5... | collective-permute-start | bytes 196616 | tf_op jit(solution)/shard_map/ppermute | solution.py:167
  27.2 8.1 %collective-permute-start.2 = (bf16[32,1024]{1,0:T(8,128)(2,1)S(1)}, bf16[32,1024]{1,0:T(8,128)(2,1)S(1)}, u32[]{:S(2)}, u32[]{:S(2)}) collective-permute-start(bf16[32,1024]{1,0:T(8,128)(2,1)S(1)} %get-tuple-element.54), channel_id=1, source_target_pairs={{0,4},{4,8},{8,12},{12,16},{16,20},{20,24},{24,28},{28,0},{1,5},{5... | collective-permute-start | bytes 196616 | tf_op jit(solution)/shard_map/ppermute | solution.py:167
  35.1 8.6 %copy-start.3 = (bf16[256,1024]{1,0:T(8,128)(2,1)S(1)}, bf16[256,1024]{1,0:T(8,128)(2,1)}, u32[]{:S(2)}) copy-start(bf16[256,1024]{1,0:T(8,128)(2,1)} %param.11) | copy-start | bytes 1572868
  39.7 4.1 %copy-start.25 = (bf16[1,256,1024]{2,1,0:T(8,128)(2,1)S(1)}, bf16[1,256,1024]{2,1,0:T(8,128)(2,1)}, u32[]{:S(2)}) copy-start(bf16[1,256,1024]{2,1,0:T(8,128)(2,1)} %copy-done.24) | copy-start | bytes 1572868
  39.7 5.2 %copy-start.37 = (s32[4]{0:T(128)S(1)}, s32[4]{0:T(128)}, u32[]{:S(2)}) copy-start(s32[4]{0:T(128)} %constant.135.clone) | copy-start | bytes 52
  39.7 10.7 %copy-start.42 = (s32[1,2]{1,0:T(1,128)S(1)}, s32[1,2]{1,0:T(1,128)}, u32[]{:S(2)}) copy-start(s32[1,2]{1,0:T(1,128)} %param.18) | copy-start | bytes 28
  42.2 12.2 %collective-permute-start.9 = (bf16[1,256,1024]{2,1,0:T(8,128)(2,1)}, bf16[1,256,1024]{2,1,0:T(8,128)(2,1)}, u32[]{:S(2)}, u32[]{:S(2)}) collective-permute-start(bf16[1,256,1024]{2,1,0:T(8,128)(2,1)} %bitcast.39), channel_id=1, source_target_pairs={{0,2},{1,3},{2,0},{3,1},{4,6},{5,7},{6,4},{7,5},{8,10},{9,11},{10,... | collective-permute-start | bytes 1572872 | tf_op jit(solution)/shard_map/ppermute | solution.py:70
  44.8 12.4 %collective-permute-start.1 = (bf16[2,256,1024]{2,1,0:T(8,128)(2,1)}, bf16[2,256,1024]{2,1,0:T(8,128)(2,1)}, u32[]{:S(2)}, u32[]{:S(2)}) collective-permute-start(bf16[2,256,1024]{2,1,0:T(8,128)(2,1)} %pad_maximum_fusion.4), channel_id=1, source_target_pairs={{0,1},{1,0},{2,3},{3,2},{4,5},{5,4},{6,7},{7,6},{8,9},{9,8},{10,11... | collective-permute-start | bytes 3145736 | tf_op jit(solution)/shard_map/ppermute | solution.py:70
  53.0 4.2 %copy-start.26 = (bf16[1,256,1024]{2,1,0:T(8,128)(2,1)S(1)}, bf16[1,256,1024]{2,1,0:T(8,128)(2,1)}, u32[]{:S(2)}) copy-start(bf16[1,256,1024]{2,1,0:T(8,128)(2,1)} %copy-done.24) | copy-start | bytes 1572868
  55.7 2.9 %collective-permute-start.10 = (bf16[2,256,1024]{2,1,0:T(8,128)(2,1)S(1)}, bf16[2,256,1024]{2,1,0:T(8,128)(2,1)S(1)}, u32[]{:S(2)}, u32[]{:S(2)}) collective-permute-start(bf16[2,256,1024]{2,1,0:T(8,128)(2,1)S(1)} %pad_maximum_fusion.5), channel_id=1, source_target_pairs={{0,1},{1,0},{2,3},{3,2},{4,5},{5,4},{6,7},{7,6},{8,9},{9,8},{10,11... | collective-permute-start | bytes 3145736 | tf_op jit(solution)/shard_map/ppermute | solution.py:70
  60.1 2.8 %copy-start.36 = (f32[4096]{0:T(1024)S(1)}, f32[4096]{0:T(1024)}, u32[]{:S(2)}) copy-start(f32[4096]{0:T(1024)} %param.12) | copy-start | bytes 49156
  61.9 4.2 %copy-start.4 = (bf16[256,1024]{1,0:T(8,128)(2,1)}, bf16[256,1024]{1,0:T(8,128)(2,1)S(1)}, u32[]{:S(2)}) copy-start(bf16[256,1024]{1,0:T(8,128)(2,1)S(1)} %get-tuple-element.68) | copy-start | bytes 1572868
  61.9 4.2 %copy-start.6 = (bf16[256,1024]{1,0:T(8,128)(2,1)}, bf16[256,1024]{1,0:T(8,128)(2,1)S(1)}, u32[]{:S(2)}) copy-start(bf16[256,1024]{1,0:T(8,128)(2,1)S(1)} %get-tuple-element.69) | copy-start | bytes 1572868
  61.9 4.2 %copy-start.8 = (bf16[256,1024]{1,0:T(8,128)(2,1)}, bf16[256,1024]{1,0:T(8,128)(2,1)S(1)}, u32[]{:S(2)}) copy-start(bf16[256,1024]{1,0:T(8,128)(2,1)S(1)} %get-tuple-element.70) | copy-start | bytes 1572868
  61.9 4.2 %copy-start.10 = (bf16[256,1024]{1,0:T(8,128)(2,1)}, bf16[256,1024]{1,0:T(8,128)(2,1)S(1)}, u32[]{:S(2)}) copy-start(bf16[256,1024]{1,0:T(8,128)(2,1)S(1)} %get-tuple-element.71) | copy-start | bytes 1572868
  61.9 2.4 %copy-start.18 = (bf16[4096,256]{1,0:T(8,128)(2,1)S(1)}, bf16[4096,256]{1,0:T(8,128)(2,1)}, u32[]{:S(2)}) copy-start(bf16[4096,256]{1,0:T(8,128)(2,1)} %param.15) | copy-start | bytes 6291460
  62.9 3.1 %copy-start.39 = (f32[256]{0:T(256)}, f32[256]{0:T(256)S(1)}, u32[]{:S(2)}) copy-start(f32[256]{0:T(256)S(1)} %get-tuple-element.61) | copy-start | bytes 3076
  77.1 1.0 copy-start.28
  77.7 1.7 %copy-start.14 = (bf16[256,8,64]{2,0,1:T(8,128)(2,1)}, bf16[256,8,64]{2,0,1:T(8,128)(2,1)S(1)}, u32[]{:S(2)}) copy-start(bf16[256,8,64]{2,0,1:T(8,128)(2,1)S(1)} %copy.91) | copy-start | bytes 786436
  77.7 3.0 %slice-start = ((s8[8388608]{0:T(1024)(128)(4,1)}), s8[4194304]{0:T(1024)(128)(4,1)S(1)}, s32[]{:S(2)}) async-start(s8[8388608]{0:T(1024)(128)(4,1)} %bitcast.184), calls=%async_computation.1 | async-start | bytes 8388608
  78.1 1.2 copy-start.16
  78.1 1.5 copy-start.43
  78.2 2.1 %copy-start.31 = (bf16[256,2,64]{2,0,1:T(8,128)(2,1)}, bf16[256,2,64]{2,0,1:T(8,128)(2,1)S(1)}, u32[]{:S(2)}) copy-start(bf16[256,2,64]{2,0,1:T(8,128)(2,1)S(1)} %get-tuple-element.45) | copy-start | bytes 196612
  79.4 1.4 copy-start.44
  79.4 1.4 copy-start.46
  79.7 3.2 %slice-start.1 = ((s8[8388608]{0:T(1024)(128)(4,1)}), s8[4194304]{0:T(1024)(128)(4,1)S(1)}, s32[]{:S(2)}) async-start(s8[8388608]{0:T(1024)(128)(4,1)} %bitcast.184), calls=%async_computation.2 | async-start | bytes 8388608
  80.8 4.5 %copy-start.12 = (bf16[2,128,4,256]{3,1,2,0:T(8,128)(2,1)}, bf16[2,128,4,256]{3,1,2,0:T(8,128)(2,1)S(1)}, u32[]{:S(2)}) copy-start(bf16[2,128,4,256]{3,1,2,0:T(8,128)(2,1)S(1)} %convolution_convert_fusion.1) | copy-start | bytes 1572868
  82.8 2.4 %copy-start.20 = (bf16[256,1024]{1,0:T(8,128)(2,1)S(1)}, bf16[256,1024]{1,0:T(8,128)(2,1)}, u32[]{:S(2)}) copy-start(bf16[256,1024]{1,0:T(8,128)(2,1)} %get-tuple-element.32) | copy-start | bytes 1572868
  82.9 2.4 %copy-start.21 = (bf16[256,1024]{1,0:T(8,128)(2,1)S(1)}, bf16[256,1024]{1,0:T(8,128)(2,1)}, u32[]{:S(2)}) copy-start(bf16[256,1024]{1,0:T(8,128)(2,1)} %get-tuple-element.33) | copy-start | bytes 1572868
  82.9 2.4 %copy-start.22 = (bf16[256,1024]{1,0:T(8,128)(2,1)S(1)}, bf16[256,1024]{1,0:T(8,128)(2,1)}, u32[]{:S(2)}) copy-start(bf16[256,1024]{1,0:T(8,128)(2,1)} %get-tuple-element.34) | copy-start | bytes 1572868
  82.9 2.4 %copy-start.23 = (bf16[256,1024]{1,0:T(8,128)(2,1)S(1)}, bf16[256,1024]{1,0:T(8,128)(2,1)}, u32[]{:S(2)}) copy-start(bf16[256,1024]{1,0:T(8,128)(2,1)} %get-tuple-element.35) | copy-start | bytes 1572868
  85.3 2.8 %copy-start.2 = (f32[256,4096]{1,0:T(8,128)}, f32[256,4096]{1,0:T(8,128)S(1)}, u32[]{:S(2)}) copy-start(f32[256,4096]{1,0:T(8,128)S(1)} %fusion.56) | copy-start | bytes 12582916
  89.3 7.7 %collective-permute-start.11 = (bf16[2,256,1024]{2,1,0:T(8,128)(2,1)}, bf16[2,256,1024]{2,1,0:T(8,128)(2,1)}, u32[]{:S(2)}, u32[]{:S(2)}) collective-permute-start(bf16[2,256,1024]{2,1,0:T(8,128)(2,1)} %pad_maximum_fusion.6), channel_id=1, source_target_pairs={{0,1},{1,0},{2,3},{3,2},{4,5},{5,4},{6,7},{7,6},{8,9},{9,8},{10,11... | collective-permute-start | bytes 3145736 | tf_op jit(solution)/shard_map/ppermute | solution.py:107
  100.3 2.6 %copy-start.15 = (bf16[256,8,64]{2,0,1:T(8,128)(2,1)S(1)}, bf16[256,8,64]{2,0,1:T(8,128)(2,1)}, u32[]{:S(2)}) copy-start(bf16[256,8,64]{2,0,1:T(8,128)(2,1)} %copy-done.14) | copy-start | bytes 786436
  100.3 2.6 %copy-start.17 = (bf16[256,8,64]{2,0,1:T(8,128)(2,1)S(1)}, bf16[256,8,64]{2,0,1:T(8,128)(2,1)}, u32[]{:S(2)}) copy-start(bf16[256,8,64]{2,0,1:T(8,128)(2,1)} %copy-done.16) | copy-start | bytes 786436
  111.1 16.1 %collective-permute-start.12 = (bf16[1,256,1024]{2,1,0:T(8,128)(2,1)}, bf16[1,256,1024]{2,1,0:T(8,128)(2,1)}, u32[]{:S(2)}, u32[]{:S(2)}) collective-permute-start(bf16[1,256,1024]{2,1,0:T(8,128)(2,1)} %fusion.23), channel_id=1, source_target_pairs={{0,2},{1,3},{2,0},{3,1},{4,6},{5,7},{6,4},{7,5},{8,10},{9,11},{10,... | collective-permute-start | bytes 1572872 | tf_op jit(solution)/shard_map/ppermute | solution.py:107
  117.1 5.8 %copy-start.33 = (bf16[256,2,128]{0,2,1:T(8,128)(2,1)S(1)}, bf16[256,2,128]{0,2,1:T(8,128)(2,1)}, u32[]{:S(2)}) copy-start(bf16[256,2,128]{0,2,1:T(8,128)(2,1)} %copy.113) | copy-start | bytes 393220
  123.0 1.0 copy-start.13
  123.0 1.0 copy-start.35
  123.0 1.8 %copy-start.45 = (f32[2,256,256,4]{2,1,3,0:T(8,128)S(1)}, f32[2,256,256,4]{2,1,3,0:T(8,128)}, u32[]{:S(2)}) copy-start(f32[2,256,256,4]{2,1,3,0:T(8,128)} %copy-done.44) | copy-start | bytes 6291460
  123.0 1.8 %copy-start.47 = (f32[2,4,256]{2,1,0:T(4,128)S(1)}, f32[2,4,256]{2,1,0:T(4,128)}, u32[]{:S(2)}) copy-start(f32[2,4,256]{2,1,0:T(4,128)} %copy-done.46) | copy-start | bytes 24580
  124.8 1.6 copy-start.19
  127.1 3.5 %copy-start.1 = (f32[256,4096]{1,0:T(8,128)}, f32[256,4096]{1,0:T(8,128)S(1)}, u32[]{:S(2)}) copy-start(f32[256,4096]{1,0:T(8,128)S(1)} %convolution_add_fusion) | copy-start | bytes 12582916
  130.8 2.7 %collective-permute-start.13 = (bf16[2,256,1024]{2,1,0:T(8,128)(2,1)S(1)}, bf16[2,256,1024]{2,1,0:T(8,128)(2,1)S(1)}, u32[]{:S(2)}, u32[]{:S(2)}) collective-permute-start(bf16[2,256,1024]{2,1,0:T(8,128)(2,1)S(1)} %pad_maximum_fusion.7), channel_id=1, source_target_pairs={{0,1},{1,0},{2,3},{3,2},{4,5},{5,4},{6,7},{7,6},{8,9},{9,8},{10,11... | collective-permute-start | bytes 3145736 | tf_op jit(solution)/shard_map/ppermute | solution.py:109
  135.6 22.6 %all-to-all-start = ((bf16[8,32,1024]{2,1,0:T(8,128)(2,1)}), bf16[8,32,1024]{2,1,0:T(8,128)(2,1)}, u32[]{:S(2)}, u32[]{:S(2)}) async-start(bf16[8,32,1024]{2,1,0:T(8,128)(2,1)} %copy.116), calls=%async_computation | async-start | bytes 1048576 | tf_op jit(solution)/shard_map/all_to_all | solution.py:288
  139.7 2.3 %copy-start.5 = (bf16[256,1024]{1,0:T(8,128)(2,1)S(1)}, bf16[256,1024]{1,0:T(8,128)(2,1)}, u32[]{:S(2)}) copy-start(bf16[256,1024]{1,0:T(8,128)(2,1)} %copy-done.4) | copy-start | bytes 1572868
  139.8 2.3 %copy-start.7 = (bf16[256,1024]{1,0:T(8,128)(2,1)S(1)}, bf16[256,1024]{1,0:T(8,128)(2,1)}, u32[]{:S(2)}) copy-start(bf16[256,1024]{1,0:T(8,128)(2,1)} %copy-done.6) | copy-start | bytes 1572868
  139.8 2.3 %copy-start.9 = (bf16[256,1024]{1,0:T(8,128)(2,1)S(1)}, bf16[256,1024]{1,0:T(8,128)(2,1)}, u32[]{:S(2)}) copy-start(bf16[256,1024]{1,0:T(8,128)(2,1)} %copy-done.8) | copy-start | bytes 1572868
  139.8 2.3 %copy-start.11 = (bf16[256,1024]{1,0:T(8,128)(2,1)S(1)}, bf16[256,1024]{1,0:T(8,128)(2,1)}, u32[]{:S(2)}) copy-start(bf16[256,1024]{1,0:T(8,128)(2,1)} %copy-done.10) | copy-start | bytes 1572868
  141.4 14.1 %copy-start.30 = (bf16[2,256,1024]{2,1,0:T(8,128)(2,1)S(1)}, bf16[2,256,1024]{2,1,0:T(8,128)(2,1)}, u32[]{:S(2)}) copy-start(bf16[2,256,1024]{2,1,0:T(8,128)(2,1)} %copy-done.29) | copy-start | bytes 3145732
  141.5 14.1 %dynamic-slice-start = ((f32[4096]{0:T(1024)}, s32[]{:T(128)}), f32[1024]{0:T(1024)S(1)}, s32[]{:S(2)}) async-start(f32[4096]{0:T(1024)} %param.12, s32[]{:T(128)} %select_n.163), calls=%async_computation.3 | async-start | bytes 8704 | tf_op jit(solution)/shard_map/dynamic_slice | solution.py:147
  141.5 14.1 %copy-start.38 = (f32[256]{0:T(256)S(1)}, f32[256]{0:T(256)}, u32[]{:S(2)}) copy-start(f32[256]{0:T(256)} %get-tuple-element.60) | copy-start | bytes 3076
  141.5 14.1 %copy-start.40 = (f32[256]{0:T(256)S(1)}, f32[256]{0:T(256)}, u32[]{:S(2)}) copy-start(f32[256]{0:T(256)} %copy-done.39) | copy-start | bytes 3076
  141.5 14.1 %collective-permute-start.14 = (bf16[1,256,1024]{2,1,0:T(8,128)(2,1)S(1)}, bf16[1,256,1024]{2,1,0:T(8,128)(2,1)S(1)}, u32[]{:S(2)}, u32[]{:S(2)}) collective-permute-start(bf16[1,256,1024]{2,1,0:T(8,128)(2,1)S(1)} %fusion.24), channel_id=1, source_target_pairs={{0,2},{1,3},{2,0},{3,1},{4,6},{5,7},{6,4},{7,5},{8,10},{9,11},{10,... | collective-permute-start | bytes 1572872 | tf_op jit(solution)/shard_map/ppermute | solution.py:109
  144.7 1.2 collective-permute-start.15
  145.9 9.7 %collective-permute-start.16 = (f32[256]{0:T(256)S(1)}, f32[256]{0:T(256)S(1)}, u32[]{:S(2)}, u32[]{:S(2)}) collective-permute-start(f32[256]{0:T(256)S(1)} %add.253), channel_id=1, source_target_pairs={{0,2},{1,3},{2,0},{3,1},{4,6},{5,7},{6,4},{7,5},{8,10},{9,11},{10,... | collective-permute-start | bytes 3080 | tf_op jit(solution)/shard_map/ppermute | solution.py:109
  (5 other events, 4.3 us)

commit v21 on v12

--- a/solution.py
+++ b/solution.py
@@ -275,8 +275,13 @@
     outgoing = jnp.einsum(
         "dj,jrw->drw", send_table, home_blocks, preferred_element_type=jnp.float32
     ).astype(jnp.bfloat16)
-    normed_gradient, stat_sum, (outgoing,) = scatter_features(
-        normed_partial, "tensor", tensor_size, tensor_index, extra=stat_partial, ties=(outgoing,)
+    normed_gradient, stat_sum, (_, outgoing) = scatter_features(
+        normed_partial,
+        "tensor",
+        tensor_size,
+        tensor_index,
+        extra=stat_partial,
+        ties=(stat_partial, outgoing),
     )
     relaid = lax.all_to_all(outgoing, "dp", split_axis=0, concat_axis=0, tiled=True).reshape(
         token_row_count, width_part

time: 135 us -> 147 us (1.089)
  waiting for transfers between devices: 14.8 us -> 27.1 us
  other arithmetic: 22.8 us -> 19.2 us
  local copies, waits for them, and re-layouts: 25.4 us -> 28.1 us
    all_to_all x1, waiting for transfers between devices: 0.01 us -> 6.59 us  [per_device(): lax.all_to_all(outgoing, 'dp', split_axis=0, concat_axis=0, tiled=True)]
    ppermute x4, waiting for transfers between devices: 10.9 us -> 16.6 us  [scatter_features(): lax.ppermute((outgoing, extra), axis_name, _xor_pairs(size, bit))]
    unnamed x69 -> x73, local copies, waits for them, and re-layouts: 12 us -> 14.8 us
    reduce_sum x1, other arithmetic: 2.82 us -> 0.63 us  [per_device(): jnp.sum(normed_partial * norm_gain[None, :] * gathered_float, axis=1)]
    convert_element_type x2, other arithmetic: 3.97 us -> 2.45 us  [scatter_features(): outgoing = jnp.stack([held[i] for i in send]).astype(jnp.bfloat16)]
  transfers between devices with their start and end apart: 16 -> 16, of which waited for: 5 -> 7; matrix products, arithmetic and copies ran while one was open for 43% -> 37% of each run, Pallas kernels for 0% -> 0%
where the time goes in v21:
time: 147 us; the launch traced here: 146 us
  matrix products  34.6 us (24%)
  local copies, waits for them, and re-layouts  28.1 us (19%)
  waiting for transfers between devices  27.1 us (18%)
  starting transfers between devices  21.7 us (15%)
  other arithmetic  19.2 us (13%)
  between operations  14.8 us (10%)
    ppermute x4, waiting for transfers between devices, scatter_features(): lax.ppermute((outgoing, extra), axis_name, _xor_pairs(size, bit))  16.6 us
    unnamed x73, local copies, waits for them, and re-layouts  14.8 us
    ppermute x7, starting transfers between devices, per_device(): returned.append(lax.ppermute(piece, 'dp', pairs))  12.5 us
    dot_general x1, matrix products, per_device(): lax.dot_general(grad_full, w_out, (((1,), (1,)), ((), ())), preferred_ele...  7.42 us
    dot_general x1, matrix products, per_device(): jnp.dot(normed_input, w_query, preferred_element_type=jnp.float32)  6.67 us
    all_to_all x1, waiting for transfers between devices, per_device(): lax.all_to_all(outgoing, 'dp', split_axis=0, concat_axis=0, tiled=True)  6.59 us
    dot_general x1, matrix products, per_device(): lax.dot_general(grad_query.reshape(token_row_count, query_width), w_query...  5.75 us
    another operation x8, local copies, waits for them, and re-layouts, per_device(): returned = jnp.stack(returned)  5.59 us
  transfers between devices with their start and end apart: 16, of which 7 were waited for; matrix products, arithmetic and copies ran while one was open for 37% of the time, Pallas kernels for 0%

profile of v21, /device:TPU:0, one launch (start us, length us, event | category | flops | bytes accessed | tf_op | source)
XLA Modules:
  0.0 145.6 jit_solution(4724430834962134887)
XLA Ops:
  7.2 0.7 all-gather.3.cloned.1.call-update
  8.1 1.1 dynamic-slice_bitcast_fusion
  9.2 6.0 %collective-permute-start.6 = (bf16[32,1024]{1,0:T(8,128)(2,1)S(1)}, bf16[32,1024]{1,0:T(8,128)(2,1)S(1)}, u32[]{:S(2)}, u32[]{:S(2)}) collective-permute-start(bf16[32,1024]{1,0:T(8,128)(2,1)S(1)} %get-tuple-element.38), channel_id=1, source_target_pairs={{0,28},{4,0},{8,4},{12,8},{16,12},{20,16},{24,20},{28,24},{1,29},{... | collective-permute-start | bytes 196616 | tf_op jit(solution)/shard_map/ppermute | solution.py:159
  15.2 0.4 collective-permute-start.5
  15.7 3.0 %collective-permute-start.3 = (bf16[32,1024]{1,0:T(8,128)(2,1)S(1)}, bf16[32,1024]{1,0:T(8,128)(2,1)S(1)}, u32[]{:S(2)}, u32[]{:S(2)}) collective-permute-start(bf16[32,1024]{1,0:T(8,128)(2,1)S(1)} %get-tuple-element.41), channel_id=1, source_target_pairs={{0,16},{4,20},{8,24},{12,28},{16,0},{20,4},{24,8},{28,12},{1,17},{... | collective-permute-start | bytes 196616 | tf_op jit(solution)/shard_map/ppermute | solution.py:159
  18.7 0.8 reduce-window.8
  19.6 0.5 multiply_cosine_fusion
  20.2 0.7 fusion.31
  21.0 1.9 %collective-permute-start.1 = (bf16[32,1024]{1,0:T(8,128)(2,1)S(1)}, bf16[32,1024]{1,0:T(8,128)(2,1)S(1)}, u32[]{:S(2)}, u32[]{:S(2)}) collective-permute-start(bf16[32,1024]{1,0:T(8,128)(2,1)S(1)} %get-tuple-element.43), channel_id=1, source_target_pairs={{0,8},{4,12},{8,16},{12,20},{16,24},{20,28},{24,0},{28,4},{1,9},{5... | collective-permute-start | bytes 196616 | tf_op jit(solution)/shard_map/ppermute | solution.py:159
  22.9 1.1 collective-permute-start
  24.0 1.2 and_select_fusion
  25.7 2.9 %collective-permute-done.2 = bf16[32,1024]{1,0:T(8,128)(2,1)S(1)} collective-permute-done((bf16[32,1024]{1,0:T(8,128)(2,1)S(1)}, bf16[32,1024]{1,0:T(8,128)(2,1)S(1)}, u32[]{:S(2)}, u32[]{:S(2)}) %collective-permute-start.2) | collective-permute-done | bytes 65568 | tf_op jit(solution)/shard_map/ppermute | solution.py:159
  28.6 0.7 copy.93
  29.3 0.8 copy.92
  30.1 0.8 copy.91
  30.8 2.9 %stack.58 = bf16[8,32,1024]{2,0,1:T(8,128)(2,1)S(1)} concatenate(bf16[1,32,1024]{2,0,1:T(2,128)(2,1)S(1)} %copy.132, bf16[1,32,1024]{2,0,1:T(2,128)(2,1)} %copy.91, bf16[1,32,1024]{2,0,1:T(2,128)(2,1)} %copy.92, bf16[1,32,1024]{2,0,1:T(2,128)(2,1)} %copy.93, bf16[1,32,1024]{2,0,1:T(2,128)(2,1)S(1)} %copy.94, bf16[1,32,1024]{2,0,1:T(2,128)(2,1)S(1)} %copy.95, ...), dimensions={0} | concatenate | bytes 1048576 | tf_op jit(solution)/shard_map/stack | solution.py:160
  34.1 1.1 copy.98
  35.3 2.2 %fusion = f32[256]{0:T(256)S(1)} fusion(bf16[256,4096]{1,0:T(8,128)(2,1)} %all-gather.3.cloned.1.call-done), kind=kLoop, calls=%fused_computation.5 | loop fusion | flops 3145472 | bytes 2098176 | tf_op jit(solution)/shard_map/reduce_sum | solution.py:183
  37.5 0.6 multiply_multiply_fusion
  38.2 1.2 fusion.47
  39.6 6.7 %convolution_bitcast_fusion = f32[32,8,8,128]{3,1,2,0:T(8,128)S(1)} fusion(bf16[4096,1024]{1,0:T(8,128)(2,1)} %param.11, bf16[256,4096]{1,0:T(8,128)(2,1)} %all-gather.3.cloned.1.call-done, f32[4096]{0:T(1024)S(1)} %copy-done.21, f32[256]{0:T(256)S(1)} %get-tuple-element.51), kind=kOutput, calls=%fused_computation.16 | convolution fusion | flops 2151677952 | bytes 11551744 | tf_op jit(solution)/shard_map/dot_general | solution.py:185
  46.5 0.5 subtract_convert_fusion.1
  47.3 0.6 copy-done.9
  48.1 0.9 fusion.7
  49.1 0.7 copy-done.13
  49.8 1.2 convolution_convert_fusion.4
  51.2 0.7 convolution_convert_fusion.1
  51.8 1.0 slice-done
  52.8 1.4 slice-done.1
  54.3 4.5 %fusion.55 = f32[256,4096]{1,0:T(8,128)} fusion(bf16[256,1024]{0,1:T(8,128)(2,1)S(1)} %bitcast.167, bf16[1024,4096]{1,0:T(8,128)(2,1)S(1)} %bitcast.163), kind=kOutput, calls=%fused_computation.114 | convolution fusion | flops 2147483648 | bytes 13107200 | tf_op jit(solution)/shard_map/dot_general | solution.py:213
  59.1 1.7 %fusion.19 = (bf16[1,256,1024]{2,1,0:T(8,128)(2,1)S(1)}, bf16[1,256,1024]{2,1,0:T(8,128)(2,1)S(1)}) fusion(f32[256,4096]{1,0:T(8,128)} %fusion.55, s32[]{:T(128)S(6)} %select_n.111, s32[]{:T(128)S(6)} %select_n.112), kind=kLoop, calls=%fused_computation.54 | loop fusion | bytes 2097160 | tf_op jit(solution)/shard_map/stack | solution.py:100
  60.8 1.1 pad_maximum_fusion
  62.1 7.4 %convolution_convert_fusion = bf16[256,1024]{1,0:T(8,128)(2,1)} fusion(bf16[256,4096]{1,0:T(8,128)(2,1)} %all-gather.5.cloned.1.call-done, bf16[1024,4096]{1,0:T(8,128)(2,1)} %param.14), kind=kOutput, calls=%fused_computation.19 | convolution fusion | flops 2147745792 | bytes 11010048 | tf_op jit(solution)/shard_map/dot_general | solution.py:216
  69.6 1.2 copy.99
  71.0 2.5 %fusion.5 = bf16[2,4,256,256]{2,3,1,0:T(8,128)(2,1)S(1)} fusion(bf16[256,2,128,1]{0,2,3,1:T(8,128)(2,1)} %bitcast.191, bf16[256,2,4,128]{0,3,2,1:T(8,128)(2,1)S(1)} %bitcast.168, f32[2,4,256]{2,1,0:T(4,128)S(1)} %bitcast.187, f32[2,4,256]{2,1,0:T(4,128)} %copy-done.29, f32[2,256,256,4]{2,1,3,0:T(8,128)} %copy-done.27, pred[256,256]{0,1:T(8,128)(4,1)} %fusion.31), kind=kOutput, calls=%fused_computation.11 | convolution fusion | flops 137363456 | bytes 3883008 | tf_op jit(solution)/shard_map/qkgd,skd->kgqs/dot_general | solution.py:230
  73.5 0.5 fusion.9
  74.4 0.4 convolution_multiply_fusion
  74.9 1.1 fusion.53
  76.3 1.5 %copy.134 = f32[256,8,64]{2,1,0:T(8,128)S(1)} copy(f32[256,8,64]{0,2,1:T(8,128)} %get-tuple-element.32) | data formatting | bytes 1048576
  77.8 2.3 %fusion.23 = bf16[1,256,1024]{2,1,0:T(8,128)(2,1)} fusion(f32[256,4096]{1,0:T(8,128)} %fusion.55, s32[]{:T(128)S(6)} %select_n.113, bf16[2,256,1024]{2,1,0:T(8,128)(2,1)} %collective-permute-done.7), kind=kLoop, calls=%fused_computation.58 | loop fusion | flops 786432 | bytes 2097156 | tf_op jit(solution)/shard_map/convert_element_type | solution.py:100
  80.1 0.9 collective-permute-start.8
  81.0 2.4 %copy.133 = f32[256,8,64]{2,1,0:T(8,128)} copy(f32[256,8,64]{0,2,1:T(8,128)} %get-tuple-element.33) | data formatting | bytes 1048576
  83.4 1.5 %add_convert_fusion = (bf16[256,8,64]{2,1,0:T(8,128)(2,1)S(1)}, bf16[256,8,64]{2,1,0:T(8,128)(2,1)S(1)}) fusion(f32[256,8,64]{2,1,0:T(8,128)S(1)} %copy.134, f32[256,8,64]{2,1,0:T(8,128)} %copy.133, f32[256,64]{1,0:T(8,128)S(1)} %get-tuple-element.49, f32[256,64]{1,0:T(8,128)S(1)} %get-tuple-element.48), kind=kLoop, calls=%fused_computation.48 | loop fusion | flops 1048576 | bytes 1703936 | tf_op jit(solution)/shard_map/convert.12
  85.2 5.8 %fusion.25 = f32[256,4096]{1,0:T(8,128)S(1)} fusion(bf16[4096,1024]{1,0:T(8,128)(2,1)} %param.11, bf16[32,8,8,128]{3,2,1,0:T(8,128)(2,1)S(1)} %bitcast.175), kind=kOutput, calls=%fused_computation.60 | convolution fusion | flops 2147483648 | bytes 13107200 | tf_op jit(solution)/shard_map/dot_general | solution.py:253
  91.0 0.8 convolution_add_fusion.1
  92.0 0.7 copy-done.28
  92.7 0.6 fusion.10
  93.4 0.9 copy-done.14
  94.3 0.8 convolution_add_fusion
  95.4 3.1 %fusion.11 = bf16[256,1024]{1,0:T(8,128)(2,1)S(1)} fusion(bf16[256,1024]{1,0:T(8,128)(2,1)S(1)} %copy-done.6, f32[256,4096]{1,0:T(8,128)} %fusion.55, s32[]{:T(128)} %select_n.110, bf16[1,256,1024]{2,1,0:T(8,128)(2,1)} %collective-permute-done.8, bf16[2,256,1024]{2,1,0:T(8,128)(2,1)} %collective-permute-done.7), kind=kLoop, calls=%fused_computation.29 | loop fusion | flops 1835008 | bytes 3145732 | tf_op jit(solution)/shard_map/convert_element_type | solution.py:225
  99.1 1.0 copy-done.4
  100.1 0.6 fusion.3
  100.7 0.8 collective-permute-done.9
  101.7 1.2 collective-permute-start.10
  103.3 12.5 %collective-permute-done.10 = bf16[1,256,1024]{2,1,0:T(8,128)(2,1)S(1)} collective-permute-done((bf16[1,256,1024]{2,1,0:T(8,128)(2,1)S(1)}, bf16[1,256,1024]{2,1,0:T(8,128)(2,1)S(1)}, u32[]{:S(2)}, u32[]{:S(2)}) %collective-permute-start.10) | collective-permute-done | bytes 524320 | tf_op jit(solution)/shard_map/ppermute | solution.py:104
  115.8 0.8 copy-done.16
  116.6 1.1 copy.112
  117.7 5.1 %all-to-all-start = ((bf16[8,32,1024]{2,1,0:T(8,128)(2,1)}), bf16[8,32,1024]{2,1,0:T(8,128)(2,1)}, u32[]{:S(2)}, u32[]{:S(2)}) async-start(bf16[8,32,1024]{2,1,0:T(8,128)(2,1)} %copy.112), calls=%async_computation | async-start | bytes 1048576 | tf_op jit(solution)/shard_map/all_to_all | solution.py:286
  122.8 1.1 collective-permute-done.11
  123.9 1.5 %collective-permute-start.12 = (f32[256]{0:T(256)S(1)}, f32[256]{0:T(256)S(1)}, u32[]{:S(2)}, u32[]{:S(2)}) collective-permute-start(f32[256]{0:T(256)S(1)} %add.200), channel_id=1, source_target_pairs={{0,2},{1,3},{2,0},{3,1},{4,6},{5,7},{6,4},{7,5},{8,10},{9,11},{10,... | collective-permute-start | bytes 3080 | tf_op jit(solution)/shard_map/ppermute | solution.py:104
  125.4 2.1 %collective-permute-done.12 = f32[256]{0:T(256)S(1)} collective-permute-done((f32[256]{0:T(256)S(1)}, f32[256]{0:T(256)S(1)}, u32[]{:S(2)}, u32[]{:S(2)}) %collective-permute-start.12) | collective-permute-done | bytes 1056 | tf_op jit(solution)/shard_map/ppermute | solution.py:104
  127.5 2.8 %fusion.14 = bf16[256,1024]{1,0:T(8,128)(2,1)} fusion(bf16[256,1024]{1,0:T(8,128)(2,1)S(1)} %copy-done.6, f32[256,4096]{1,0:T(8,128)} %copy-done.1, s32[]{:T(128)} %select_n.110, bf16[1,256,1024]{2,1,0:T(8,128)(2,1)} %copy-done.16, f32[256]{0:T(256)S(1)} %add_multiply_fusion, f32[256]{0:T(256)S(1)} %copy-done.22, bf16[2,256,1024]{2,1,0:T(8,128)(2,1)} %copy-done.15, ...), kind=kLoop, calls=%fused_computation.32 | loop fusion | flops 3407872 | bytes 3677188 | tf_op jit(solution)/shard_map/convert_element_type | solution.py:296
  130.3 6.6 %all-to-all-done = bf16[8,32,1024]{2,1,0:T(8,128)(2,1)} async-done(((bf16[8,32,1024]{2,1,0:T(8,128)(2,1)}), bf16[8,32,1024]{2,1,0:T(8,128)(2,1)}, u32[]{:S(2)}, u32[]{:S(2)}) %all-to-all-start) | async-done | bytes 524320 | tf_op jit(solution)/shard_map/all_to_all | solution.py:286
  136.9 1.9 %copy.144 = bf16[256,1024]{1,0:T(8,128)(2,1)} copy(bf16[256,1024]{1,0:T(8,128)(2,1)} %bitcast.58) | data formatting | bytes 1048576
  (106 shorter events, 5.7 us)
Async XLA Ops:
  7.2 31.0 %copy-start = (bf16[4096,256]{1,0:T(8,128)(2,1)S(1)}, bf16[4096,256]{1,0:T(8,128)(2,1)}, u32[]{:S(2)}) copy-start(bf16[4096,256]{1,0:T(8,128)(2,1)} %param.12) | copy-start | bytes 6291460
  7.2 28.1 %all-gather.3.cloned.1.call-start = ((), (), s32[]{:S(2)}) async-start(), calls=%async_computation.1 | async-start | bytes 2621440 | tf_op jit(solution)/shard_map/all_gather | solution.py:181
  7.9 51.2 %all-gather.5.cloned.1.call-start = ((), (), s32[]{:S(2)}) async-start(), calls=%async_computation.2 | async-start | bytes 2621440 | tf_op jit(solution)/shard_map/all_gather | solution.py:214
  9.2 11.8 %collective-permute-start.6 = (bf16[32,1024]{1,0:T(8,128)(2,1)S(1)}, bf16[32,1024]{1,0:T(8,128)(2,1)S(1)}, u32[]{:S(2)}, u32[]{:S(2)}) collective-permute-start(bf16[32,1024]{1,0:T(8,128)(2,1)S(1)} %get-tuple-element.38), channel_id=1, source_target_pairs={{0,28},{4,0},{8,4},{12,8},{16,12},{20,16},{24,20},{28,24},{1,29},{... | collective-permute-start | bytes 196616 | tf_op jit(solution)/shard_map/ppermute | solution.py:159
  15.2 7.7 %collective-permute-start.5 = (bf16[32,1024]{1,0:T(8,128)(2,1)S(1)}, bf16[32,1024]{1,0:T(8,128)(2,1)S(1)}, u32[]{:S(2)}, u32[]{:S(2)}) collective-permute-start(bf16[32,1024]{1,0:T(8,128)(2,1)S(1)} %get-tuple-element.39), channel_id=1, source_target_pairs={{0,24},{4,28},{8,0},{12,4},{16,8},{20,12},{24,16},{28,20},{1,25},{... | collective-permute-start | bytes 196616 | tf_op jit(solution)/shard_map/ppermute | solution.py:159
  15.7 9.8 %collective-permute-start.4 = (bf16[32,1024]{1,0:T(8,128)(2,1)S(1)}, bf16[32,1024]{1,0:T(8,128)(2,1)S(1)}, u32[]{:S(2)}, u32[]{:S(2)}) collective-permute-start(bf16[32,1024]{1,0:T(8,128)(2,1)S(1)} %get-tuple-element.40), channel_id=1, source_target_pairs={{0,20},{4,24},{8,28},{12,0},{16,4},{20,8},{24,12},{28,16},{1,21},{... | collective-permute-start | bytes 196616 | tf_op jit(solution)/shard_map/ppermute | solution.py:159
  15.7 9.9 %collective-permute-start.3 = (bf16[32,1024]{1,0:T(8,128)(2,1)S(1)}, bf16[32,1024]{1,0:T(8,128)(2,1)S(1)}, u32[]{:S(2)}, u32[]{:S(2)}) collective-permute-start(bf16[32,1024]{1,0:T(8,128)(2,1)S(1)} %get-tuple-element.41), channel_id=1, source_target_pairs={{0,16},{4,20},{8,24},{12,28},{16,0},{20,4},{24,8},{28,12},{1,17},{... | collective-permute-start | bytes 196616 | tf_op jit(solution)/shard_map/ppermute | solution.py:159
  18.7 9.9 %collective-permute-start.2 = (bf16[32,1024]{1,0:T(8,128)(2,1)S(1)}, bf16[32,1024]{1,0:T(8,128)(2,1)S(1)}, u32[]{:S(2)}, u32[]{:S(2)}) collective-permute-start(bf16[32,1024]{1,0:T(8,128)(2,1)S(1)} %get-tuple-element.42), channel_id=1, source_target_pairs={{0,12},{4,16},{8,20},{12,24},{16,28},{20,0},{24,4},{28,8},{1,13},{... | collective-permute-start | bytes 196616 | tf_op jit(solution)/shard_map/ppermute | solution.py:159
  21.0 8.3 %collective-permute-start.1 = (bf16[32,1024]{1,0:T(8,128)(2,1)S(1)}, bf16[32,1024]{1,0:T(8,128)(2,1)S(1)}, u32[]{:S(2)}, u32[]{:S(2)}) collective-permute-start(bf16[32,1024]{1,0:T(8,128)(2,1)S(1)} %get-tuple-element.43), channel_id=1, source_target_pairs={{0,8},{4,12},{8,16},{12,20},{16,24},{20,28},{24,0},{28,4},{1,9},{5... | collective-permute-start | bytes 196616 | tf_op jit(solution)/shard_map/ppermute | solution.py:159
  22.9 7.2 %collective-permute-start = (bf16[32,1024]{1,0:T(8,128)(2,1)S(1)}, bf16[32,1024]{1,0:T(8,128)(2,1)S(1)}, u32[]{:S(2)}, u32[]{:S(2)}) collective-permute-start(bf16[32,1024]{1,0:T(8,128)(2,1)S(1)} %get-tuple-element.44), channel_id=1, source_target_pairs={{0,4},{4,8},{8,12},{12,16},{16,20},{20,24},{24,28},{28,0},{1,5},{5... | collective-permute-start | bytes 196616 | tf_op jit(solution)/shard_map/ppermute | solution.py:159
  34.1 4.0 %copy-start.21 = (f32[4096]{0:T(1024)S(1)}, f32[4096]{0:T(1024)}, u32[]{:S(2)}) copy-start(f32[4096]{0:T(1024)} %param.10) | copy-start | bytes 49156
  35.3 2.9 %copy-start.2 = (bf16[256,4096]{1,0:T(8,128)(2,1)S(1)}, bf16[256,4096]{1,0:T(8,128)(2,1)}, u32[]{:S(2)}) copy-start(bf16[256,4096]{1,0:T(8,128)(2,1)} %all-gather.3.cloned.1.call-done) | copy-start | bytes 6291460
  38.1 10.8 %copy-start.23 = (f32[256]{0:T(256)}, f32[256]{0:T(256)S(1)}, u32[]{:S(2)}) copy-start(f32[256]{0:T(256)S(1)} %get-tuple-element.51) | copy-start | bytes 3076
  47.0 1.1 copy-start.19
  47.1 0.8 copy-start.9
  47.2 0.9 copy-start.11
  47.2 1.9 %copy-start.3 = (bf16[256,4096]{1,0:T(8,128)(2,1)S(1)}, bf16[256,4096]{1,0:T(8,128)(2,1)}, u32[]{:S(2)}) copy-start(bf16[256,4096]{1,0:T(8,128)(2,1)} %all-gather.3.cloned.1.call-done) | copy-start | bytes 6291460
  47.2 2.6 %copy-start.13 = (bf16[4096,256]{1,0:T(8,128)(2,1)S(1)}, bf16[4096,256]{1,0:T(8,128)(2,1)}, u32[]{:S(2)}) copy-start(bf16[4096,256]{1,0:T(8,128)(2,1)} %param.13) | copy-start | bytes 6291460
  47.3 3.7 %copy-start.17 = (bf16[256,2,64]{2,0,1:T(8,128)(2,1)}, bf16[256,2,64]{2,0,1:T(8,128)(2,1)S(1)}, u32[]{:S(2)}) copy-start(bf16[256,2,64]{2,0,1:T(8,128)(2,1)S(1)} %get-tuple-element.35) | copy-start | bytes 196612
  49.8 1.4 copy-start.27
  49.8 1.4 copy-start.29
  49.8 3.0 %slice-start = ((s8[8388608]{0:T(1024)(128)(4,1)}), s8[4194304]{0:T(1024)(128)(4,1)S(1)}, s32[]{:S(2)}) async-start(s8[8388608]{0:T(1024)(128)(4,1)} %bitcast.162), calls=%async_computation.3 | async-start | bytes 8388608
  51.0 0.8 copy-start.26
  51.2 3.1 %slice-start.1 = ((s8[8388608]{0:T(1024)(128)(4,1)}), s8[4194304]{0:T(1024)(128)(4,1)S(1)}, s32[]{:S(2)}) async-start(s8[8388608]{0:T(1024)(128)(4,1)} %bitcast.162), calls=%async_computation.4 | async-start | bytes 8388608
  61.9 7.7 %collective-permute-start.7 = (bf16[2,256,1024]{2,1,0:T(8,128)(2,1)}, bf16[2,256,1024]{2,1,0:T(8,128)(2,1)}, u32[]{:S(2)}, u32[]{:S(2)}) collective-permute-start(bf16[2,256,1024]{2,1,0:T(8,128)(2,1)} %pad_maximum_fusion), channel_id=1, source_target_pairs={{0,1},{1,0},{2,3},{3,2},{4,5},{5,4},{6,7},{7,6},{8,9},{9,8},{10,11... | collective-permute-start | bytes 3145736 | tf_op jit(solution)/shard_map/ppermute | solution.py:102
  70.8 2.7 %copy-start.7 = (bf16[256,1024]{0,1:T(8,128)(2,1)}, bf16[256,1024]{0,1:T(8,128)(2,1)S(1)}, u32[]{:S(2)}) copy-start(bf16[256,1024]{0,1:T(8,128)(2,1)S(1)} %copy.99) | copy-start | bytes 1572868
  71.0 2.5 %copy-start.10 = (bf16[256,8,64]{2,0,1:T(8,128)(2,1)S(1)}, bf16[256,8,64]{2,0,1:T(8,128)(2,1)}, u32[]{:S(2)}) copy-start(bf16[256,8,64]{2,0,1:T(8,128)(2,1)} %copy-done.9) | copy-start | bytes 786436
  71.0 2.5 %copy-start.12 = (bf16[256,8,64]{2,0,1:T(8,128)(2,1)S(1)}, bf16[256,8,64]{2,0,1:T(8,128)(2,1)}, u32[]{:S(2)}) copy-start(bf16[256,8,64]{2,0,1:T(8,128)(2,1)} %copy-done.11) | copy-start | bytes 786436
  73.5 0.9 copy-start.18
  80.1 15.1 %collective-permute-start.8 = (bf16[1,256,1024]{2,1,0:T(8,128)(2,1)}, bf16[1,256,1024]{2,1,0:T(8,128)(2,1)}, u32[]{:S(2)}, u32[]{:S(2)}) collective-permute-start(bf16[1,256,1024]{2,1,0:T(8,128)(2,1)} %fusion.23), channel_id=1, source_target_pairs={{0,2},{1,3},{2,0},{3,1},{4,6},{5,7},{6,4},{7,5},{8,10},{9,11},{10,... | collective-permute-start | bytes 1572872 | tf_op jit(solution)/shard_map/ppermute | solution.py:102
  90.9 1.0 copy-start.8
  91.0 1.0 copy-start.20
  91.0 1.8 %copy-start.28 = (f32[2,256,256,4]{2,1,3,0:T(8,128)S(1)}, f32[2,256,256,4]{2,1,3,0:T(8,128)}, u32[]{:S(2)}) copy-start(f32[2,256,256,4]{2,1,3,0:T(8,128)} %copy-done.27) | copy-start | bytes 6291460
  91.0 1.8 %copy-start.30 = (f32[2,4,256]{2,1,0:T(4,128)S(1)}, f32[2,4,256]{2,1,0:T(4,128)}, u32[]{:S(2)}) copy-start(f32[2,4,256]{2,1,0:T(4,128)} %copy-done.29) | copy-start | bytes 24580
  92.7 1.6 %copy-start.14 = (bf16[4096,256]{1,0:T(8,128)(2,1)S(1)}, bf16[4096,256]{1,0:T(8,128)(2,1)}, u32[]{:S(2)}) copy-start(bf16[4096,256]{1,0:T(8,128)(2,1)} %param.13) | copy-start | bytes 6291460
  94.3 1.0 copy-start.6
  95.1 6.4 %copy-start.1 = (f32[256,4096]{1,0:T(8,128)}, f32[256,4096]{1,0:T(8,128)S(1)}, u32[]{:S(2)}) copy-start(f32[256,4096]{1,0:T(8,128)S(1)} %convolution_add_fusion) | copy-start | bytes 12582916
  98.5 1.6 %copy-start.4 = (bf16[256,4096]{1,0:T(8,128)(2,1)S(1)}, bf16[256,4096]{1,0:T(8,128)(2,1)}, u32[]{:S(2)}) copy-start(bf16[256,4096]{1,0:T(8,128)(2,1)} %all-gather.3.cloned.1.call-done) | copy-start | bytes 6291460
  98.8 2.7 %collective-permute-start.9 = (bf16[2,256,1024]{2,1,0:T(8,128)(2,1)S(1)}, bf16[2,256,1024]{2,1,0:T(8,128)(2,1)S(1)}, u32[]{:S(2)}, u32[]{:S(2)}) collective-permute-start(bf16[2,256,1024]{2,1,0:T(8,128)(2,1)S(1)} %pad_maximum_fusion.1), channel_id=1, source_target_pairs={{0,1},{1,0},{2,3},{3,2},{4,5},{5,4},{6,7},{7,6},{8,9},{9,8},{10,11... | collective-permute-start | bytes 3145736 | tf_op jit(solution)/shard_map/ppermute | solution.py:104
  100.7 2.2 %copy-start.25 = (s32[8]{0:T(128)S(1)}, s32[8]{0:T(128)}, u32[]{:S(2)}) copy-start(s32[8]{0:T(128)} %get-tuple-element.23) | copy-start | bytes 100
  101.5 1.8 %copy-start.15 = (bf16[2,256,1024]{2,1,0:T(8,128)(2,1)}, bf16[2,256,1024]{2,1,0:T(8,128)(2,1)S(1)}, u32[]{:S(2)}) copy-start(bf16[2,256,1024]{2,1,0:T(8,128)(2,1)S(1)} %collective-permute-done.9) | copy-start | bytes 3145732
  101.7 25.8 %copy-start.5 = (bf16[8,32,1024]{2,1,0:T(8,128)(2,1)S(1)}, bf16[8,32,1024]{2,1,0:T(8,128)(2,1)}, u32[]{:S(2)}) copy-start(bf16[8,32,1024]{2,1,0:T(8,128)(2,1)} %copy.98) | copy-start | bytes 1572868
  101.7 25.8 %dynamic-slice-start = ((f32[4096]{0:T(1024)}, s32[]{:T(128)}), f32[1024]{0:T(1024)S(1)}, s32[]{:S(2)}) async-start(f32[4096]{0:T(1024)} %param.10, s32[]{:T(128)} %select_n.110), calls=%async_computation.5 | async-start | bytes 8704 | tf_op jit(solution)/shard_map/dynamic_slice | solution.py:142
  101.7 25.8 %copy-start.22 = (f32[256]{0:T(256)S(1)}, f32[256]{0:T(256)}, u32[]{:S(2)}) copy-start(f32[256]{0:T(256)} %get-tuple-element.50) | copy-start | bytes 3076
  101.7 25.8 %copy-start.24 = (f32[256]{0:T(256)S(1)}, f32[256]{0:T(256)}, u32[]{:S(2)}) copy-start(f32[256]{0:T(256)} %copy-done.23) | copy-start | bytes 3076
  101.7 14.1 %collective-permute-start.10 = (bf16[1,256,1024]{2,1,0:T(8,128)(2,1)S(1)}, bf16[1,256,1024]{2,1,0:T(8,128)(2,1)S(1)}, u32[]{:S(2)}, u32[]{:S(2)}) collective-permute-start(bf16[1,256,1024]{2,1,0:T(8,128)(2,1)S(1)} %fusion.24), channel_id=1, source_target_pairs={{0,2},{1,3},{2,0},{3,1},{4,6},{5,7},{6,4},{7,5},{8,10},{9,11},{10,... | collective-permute-start | bytes 1572872 | tf_op jit(solution)/shard_map/ppermute | solution.py:104
  115.8 0.8 copy-start.16
  117.7 19.2 %all-to-all-start = ((bf16[8,32,1024]{2,1,0:T(8,128)(2,1)}), bf16[8,32,1024]{2,1,0:T(8,128)(2,1)}, u32[]{:S(2)}, u32[]{:S(2)}) async-start(bf16[8,32,1024]{2,1,0:T(8,128)(2,1)} %copy.112), calls=%async_computation | async-start | bytes 1048576 | tf_op jit(solution)/shard_map/all_to_all | solution.py:286
  122.8 1.1 collective-permute-start.11
  123.9 3.6 %collective-permute-start.12 = (f32[256]{0:T(256)S(1)}, f32[256]{0:T(256)S(1)}, u32[]{:S(2)}, u32[]{:S(2)}) collective-permute-start(f32[256]{0:T(256)S(1)} %add.200), channel_id=1, source_target_pairs={{0,2},{1,3},{2,0},{3,1},{4,6},{5,7},{6,4},{7,5},{8,10},{9,11},{10,... | collective-permute-start | bytes 3080 | tf_op jit(solution)/shard_map/ppermute | solution.py:104
Sparse Core Ops, SparseCore 0:
  9.6 25.2 all-gather.2
  36.5 22.5 all-gather.4

commit v22 on v12

--- a/solution.py
+++ b/solution.py
@@ -213,12 +213,16 @@
     mixed_partial = jnp.dot(attended_flat, w_out, preferred_element_type=jnp.float32)
     grad_full = lax.all_gather(grad_home, "tensor", axis=1, tiled=True)
     mixed_partial, grad_full = lax.optimization_barrier((mixed_partial, grad_full))
-    attended_gradient = lax.dot_general(
-        grad_full,
-        w_out,
-        (((1,), (1,)), ((), ())),
-        preferred_element_type=jnp.float32,
-    ).astype(jnp.bfloat16)
+    attended_gradient = (
+        lax.dot_general(
+            w_out,
+            grad_full,
+            (((1,), (1,)), ((), ())),
+            preferred_element_type=jnp.float32,
+        )
+        .astype(jnp.bfloat16)
+        .T
+    )
     mixed, _, (attended_gradient,) = scatter_features(
         mixed_partial, "tensor", tensor_size, tensor_index, ties=(attended_gradient,)
     )

time: 135 us -> 135 us (level)
  no operation moved by 1% of the time
where the time goes in v22:
time: 135 us; the launch traced here: 134 us
  matrix products  34.6 us (26%)
  local copies, waits for them, and re-layouts  25.4 us (19%)
  other arithmetic  22.8 us (17%)
  starting transfers between devices  21.3 us (16%)
  waiting for transfers between devices  14.8 us (11%)
  between operations  14.8 us (11%)
    ppermute x7, starting transfers between devices, per_device(): returned.append(lax.ppermute(piece, 'dp', pairs))  12.5 us
    unnamed x69, local copies, waits for them, and re-layouts  12 us
    ppermute x4, waiting for transfers between devices, scatter_features(): lax.ppermute((outgoing, extra), axis_name, _xor_pairs(size, bit))  10.9 us
    dot_general x1, matrix products, per_device(): lax.dot_general(w_out, grad_full, (((1,), (1,)), ((), ())), preferred_ele...  7.42 us
    dot_general x1, matrix products, per_device(): jnp.dot(normed_input, w_query, preferred_element_type=jnp.float32)  6.67 us
    dot_general x1, matrix products, per_device(): lax.dot_general(grad_query.reshape(token_row_count, query_width), w_query...  5.75 us
    another operation x8, local copies, waits for them, and re-layouts, per_device(): returned = jnp.stack(returned)  5.59 us
    all_to_all x1, starting transfers between devices, per_device(): lax.all_to_all(outgoing, 'dp', split_axis=0, concat_axis=0, tiled=True)  5.18 us
  transfers between devices with their start and end apart: 16, of which 5 were waited for; matrix products, arithmetic and copies ran while one was open for 43% of the time, Pallas kernels for 0%

profile of v22, /device:TPU:0, one launch (start us, length us, event | category | flops | bytes accessed | tf_op | source)
XLA Modules:
  0.0 133.7 jit_solution(13853256746741725114)
XLA Ops:
  7.2 0.7 all-gather.3.cloned.1.call-update
  8.1 1.1 dynamic-slice_bitcast_fusion
  9.2 6.0 %collective-permute-start.6 = (bf16[32,1024]{1,0:T(8,128)(2,1)S(1)}, bf16[32,1024]{1,0:T(8,128)(2,1)S(1)}, u32[]{:S(2)}, u32[]{:S(2)}) collective-permute-start(bf16[32,1024]{1,0:T(8,128)(2,1)S(1)} %get-tuple-element.36), channel_id=1, source_target_pairs={{0,28},{4,0},{8,4},{12,8},{16,12},{20,16},{24,20},{28,24},{1,29},{... | collective-permute-start | bytes 196616 | tf_op jit(solution)/shard_map/ppermute | solution.py:159
  15.2 0.4 collective-permute-start.5
  15.7 3.0 %collective-permute-start.3 = (bf16[32,1024]{1,0:T(8,128)(2,1)S(1)}, bf16[32,1024]{1,0:T(8,128)(2,1)S(1)}, u32[]{:S(2)}, u32[]{:S(2)}) collective-permute-start(bf16[32,1024]{1,0:T(8,128)(2,1)S(1)} %get-tuple-element.39), channel_id=1, source_target_pairs={{0,16},{4,20},{8,24},{12,28},{16,0},{20,4},{24,8},{28,12},{1,17},{... | collective-permute-start | bytes 196616 | tf_op jit(solution)/shard_map/ppermute | solution.py:159
  18.7 0.8 reduce-window.8
  19.6 0.5 multiply_cosine_fusion
  20.2 0.7 fusion.31
  21.0 1.9 %collective-permute-start.1 = (bf16[32,1024]{1,0:T(8,128)(2,1)S(1)}, bf16[32,1024]{1,0:T(8,128)(2,1)S(1)}, u32[]{:S(2)}, u32[]{:S(2)}) collective-permute-start(bf16[32,1024]{1,0:T(8,128)(2,1)S(1)} %get-tuple-element.41), channel_id=1, source_target_pairs={{0,8},{4,12},{8,16},{12,20},{16,24},{20,28},{24,0},{28,4},{1,9},{5... | collective-permute-start | bytes 196616 | tf_op jit(solution)/shard_map/ppermute | solution.py:159
  22.9 1.1 collective-permute-start
  24.0 1.3 and_select_fusion
  25.8 2.8 %collective-permute-done.2 = bf16[32,1024]{1,0:T(8,128)(2,1)S(1)} collective-permute-done((bf16[32,1024]{1,0:T(8,128)(2,1)S(1)}, bf16[32,1024]{1,0:T(8,128)(2,1)S(1)}, u32[]{:S(2)}, u32[]{:S(2)}) %collective-permute-start.2) | collective-permute-done | bytes 65568 | tf_op jit(solution)/shard_map/ppermute | solution.py:159
  28.6 0.8 copy.93
  29.3 0.8 copy.92
  30.1 0.8 copy.91
  30.8 2.9 %stack.58 = bf16[8,32,1024]{2,0,1:T(8,128)(2,1)S(1)} concatenate(bf16[1,32,1024]{2,0,1:T(2,128)(2,1)S(1)} %copy.132, bf16[1,32,1024]{2,0,1:T(2,128)(2,1)} %copy.91, bf16[1,32,1024]{2,0,1:T(2,128)(2,1)} %copy.92, bf16[1,32,1024]{2,0,1:T(2,128)(2,1)} %copy.93, bf16[1,32,1024]{2,0,1:T(2,128)(2,1)S(1)} %copy.94, bf16[1,32,1024]{2,0,1:T(2,128)(2,1)S(1)} %copy.95, ...), dimensions={0} | concatenate | bytes 1048576 | tf_op jit(solution)/shard_map/stack | solution.py:160
  33.8 0.4 convolution_convert_fusion.3
  34.1 1.1 copy.98
  35.3 2.2 %fusion = f32[256]{0:T(256)S(1)} fusion(bf16[256,4096]{1,0:T(8,128)(2,1)} %all-gather.3.cloned.1.call-done), kind=kLoop, calls=%fused_computation.5 | loop fusion | flops 3145472 | bytes 2098176 | tf_op jit(solution)/shard_map/reduce_sum | solution.py:183
  37.5 0.6 multiply_multiply_fusion
  38.1 1.2 fusion.47
  39.6 6.7 %convolution_bitcast_fusion = f32[32,8,8,128]{3,1,2,0:T(8,128)S(1)} fusion(bf16[4096,1024]{1,0:T(8,128)(2,1)} %param.11, bf16[256,4096]{1,0:T(8,128)(2,1)} %all-gather.3.cloned.1.call-done, f32[4096]{0:T(1024)S(1)} %copy-done.19, f32[256]{0:T(256)S(1)} %get-tuple-element.49), kind=kOutput, calls=%fused_computation.16 | convolution fusion | flops 2151677952 | bytes 11551744 | tf_op jit(solution)/shard_map/dot_general | solution.py:185
  46.5 0.5 subtract_convert_fusion.1
  47.3 0.6 copy-done.9
  48.0 0.9 fusion.7
  49.1 0.7 copy-done.13
  49.8 1.2 convolution_convert_fusion.4
  51.1 0.7 convolution_convert_fusion.1
  51.8 1.0 slice-done
  52.8 1.4 %slice-done.1 = s8[4194304]{0:T(1024)(128)(4,1)S(1)} async-done(((s8[8388608]{0:T(1024)(128)(4,1)}), s8[4194304]{0:T(1024)(128)(4,1)S(1)}, s32[]{:S(2)}) %slice-start.1) | async-done | bytes 4194328
  54.2 4.5 %fusion.55 = f32[256,4096]{1,0:T(8,128)} fusion(bf16[256,1024]{0,1:T(8,128)(2,1)S(1)} %bitcast.167, bf16[1024,4096]{1,0:T(8,128)(2,1)S(1)} %bitcast.163), kind=kOutput, calls=%fused_computation.114 | convolution fusion | flops 2147483648 | bytes 13107200 | tf_op jit(solution)/shard_map/dot_general | solution.py:213
  59.1 1.7 %fusion.19 = (bf16[1,256,1024]{2,1,0:T(8,128)(2,1)S(1)}, bf16[1,256,1024]{2,1,0:T(8,128)(2,1)S(1)}) fusion(f32[256,4096]{1,0:T(8,128)} %fusion.55, s32[]{:T(128)S(6)} %select_n.111, s32[]{:T(128)S(6)} %select_n.112), kind=kLoop, calls=%fused_computation.54 | loop fusion | bytes 2097160 | tf_op jit(solution)/shard_map/stack | solution.py:100
  60.8 1.1 pad_maximum_fusion
  62.1 7.4 %convolution_convert_fusion = bf16[256,1024]{1,0:T(8,128)(2,1)} fusion(bf16[256,4096]{1,0:T(8,128)(2,1)} %all-gather.5.cloned.1.call-done, bf16[1024,4096]{1,0:T(8,128)(2,1)} %param.14), kind=kOutput, calls=%fused_computation.19 | convolution fusion | flops 2147745792 | bytes 11010048 | tf_op jit(solution)/shard_map/dot_general | solution.py:217
  69.5 1.2 copy.99
  71.0 2.5 %fusion.5 = bf16[2,4,256,256]{2,3,1,0:T(8,128)(2,1)S(1)} fusion(bf16[256,2,128,1]{0,2,3,1:T(8,128)(2,1)} %bitcast.192, bf16[256,2,4,128]{0,3,2,1:T(8,128)(2,1)S(1)} %bitcast.168, f32[2,4,256]{2,1,0:T(4,128)S(1)} %bitcast.188, f32[2,4,256]{2,1,0:T(4,128)} %copy-done.27, f32[2,256,256,4]{2,1,3,0:T(8,128)} %copy-done.25, pred[256,256]{0,1:T(8,128)(4,1)} %fusion.31), kind=kOutput, calls=%fused_computation.11 | convolution fusion | flops 137363456 | bytes 3883008 | tf_op jit(solution)/shard_map/qkgd,skd->kgqs/dot_general | solution.py:234
  73.5 0.5 fusion.9
  74.1 0.4 copy-done.16
  74.4 0.4 convolution_multiply_fusion
  74.8 1.1 fusion.53
  76.3 1.5 %copy.134 = f32[256,8,64]{2,1,0:T(8,128)S(1)} copy(f32[256,8,64]{0,2,1:T(8,128)} %get-tuple-element.30) | data formatting | bytes 1048576
  77.8 2.3 %fusion.23 = bf16[1,256,1024]{2,1,0:T(8,128)(2,1)} fusion(f32[256,4096]{1,0:T(8,128)} %fusion.55, s32[]{:T(128)S(6)} %select_n.113, bf16[2,256,1024]{2,1,0:T(8,128)(2,1)} %collective-permute-done.7), kind=kLoop, calls=%fused_computation.58 | loop fusion | flops 786432 | bytes 2097156 | tf_op jit(solution)/shard_map/convert_element_type | solution.py:100
  80.1 0.9 collective-permute-start.8
  81.0 2.4 %copy.133 = f32[256,8,64]{2,1,0:T(8,128)} copy(f32[256,8,64]{0,2,1:T(8,128)} %get-tuple-element.31) | data formatting | bytes 1048576
  83.3 1.5 %add_convert_fusion = (bf16[256,8,64]{2,1,0:T(8,128)(2,1)S(1)}, bf16[256,8,64]{2,1,0:T(8,128)(2,1)S(1)}) fusion(f32[256,8,64]{2,1,0:T(8,128)S(1)} %copy.134, f32[256,8,64]{2,1,0:T(8,128)} %copy.133, f32[256,64]{1,0:T(8,128)S(1)} %get-tuple-element.47, f32[256,64]{1,0:T(8,128)S(1)} %get-tuple-element.46), kind=kLoop, calls=%fused_computation.48 | loop fusion | flops 1048576 | bytes 1703936 | tf_op jit(solution)/shard_map/convert.12
  85.1 5.8 %fusion.25 = f32[256,4096]{1,0:T(8,128)S(1)} fusion(bf16[4096,1024]{1,0:T(8,128)(2,1)} %param.11, bf16[32,8,8,128]{3,2,1,0:T(8,128)(2,1)S(1)} %bitcast.176), kind=kOutput, calls=%fused_computation.60 | convolution fusion | flops 2147483648 | bytes 13107200 | tf_op jit(solution)/shard_map/dot_general | solution.py:257
  90.9 0.8 convolution_add_fusion.1
  92.0 0.7 copy-done.26
  92.7 0.7 fusion.10
  93.4 0.9 copy-done.14
  94.3 0.8 convolution_add_fusion
  95.3 3.1 %fusion.11 = bf16[256,1024]{1,0:T(8,128)(2,1)S(1)} fusion(bf16[256,1024]{1,0:T(8,128)(2,1)S(1)} %copy-done.6, f32[256,4096]{1,0:T(8,128)} %fusion.55, s32[]{:T(128)} %select_n.110, bf16[1,256,1024]{2,1,0:T(8,128)(2,1)} %collective-permute-done.8, bf16[2,256,1024]{2,1,0:T(8,128)(2,1)} %collective-permute-done.7), kind=kLoop, calls=%fused_computation.29 | loop fusion | flops 1835008 | bytes 3145732 | tf_op jit(solution)/shard_map/convert_element_type | solution.py:229
  99.1 0.4 convolution_convert_fusion.2
  99.5 2.1 %collective-permute-done.9 = bf16[2,256,1024]{2,1,0:T(8,128)(2,1)} collective-permute-done((bf16[2,256,1024]{2,1,0:T(8,128)(2,1)S(1)}, bf16[2,256,1024]{2,1,0:T(8,128)(2,1)}, u32[]{:S(2)}, u32[]{:S(2)}) %collective-permute-start.9) | collective-permute-done | bytes 1048608 | tf_op jit(solution)/shard_map/ppermute | solution.py:104
  101.6 1.1 copy.112
  102.6 5.2 %all-to-all-start = ((bf16[8,32,1024]{2,1,0:T(8,128)(2,1)}), bf16[8,32,1024]{2,1,0:T(8,128)(2,1)S(1)}, u32[]{:S(2)}, u32[]{:S(2)}) async-start(bf16[8,32,1024]{2,1,0:T(8,128)(2,1)} %copy.112), calls=%async_computation | async-start | bytes 1048576 | tf_op jit(solution)/shard_map/all_to_all | solution.py:285
  107.8 1.7 %fusion.24 = bf16[1,256,1024]{2,1,0:T(8,128)(2,1)S(1)} fusion(f32[256,4096]{1,0:T(8,128)} %copy-done.1, s32[]{:T(128)S(6)} %select_n.113, bf16[2,256,1024]{2,1,0:T(8,128)(2,1)} %collective-permute-done.9), kind=kLoop, calls=%fused_computation.59 | loop fusion | flops 786432 | bytes 2097156 | tf_op jit(solution)/shard_map/convert_element_type | solution.py:100
  109.5 1.6 %collective-permute-start.10 = (bf16[1,256,1024]{2,1,0:T(8,128)(2,1)S(1)}, bf16[1,256,1024]{2,1,0:T(8,128)(2,1)S(1)}, u32[]{:S(2)}, u32[]{:S(2)}) collective-permute-start(bf16[1,256,1024]{2,1,0:T(8,128)(2,1)S(1)} %fusion.24), channel_id=1, source_target_pairs={{0,2},{1,3},{2,0},{3,1},{4,6},{5,7},{6,4},{7,5},{8,10},{9,11},{10,... | collective-permute-start | bytes 1572872 | tf_op jit(solution)/shard_map/ppermute | solution.py:104
  111.1 2.8 %fusion.3 = f32[256]{0:T(256)S(1)} fusion(bf16[256,4096]{1,0:T(8,128)(2,1)S(1)} %copy-done.4, f32[256,4096]{1,0:T(8,128)} %copy-done.1, f32[4096]{0:T(1024)S(1)} %copy-done.19), kind=kLoop, calls=%fused_computation.8 | loop fusion | flops 4194048 | bytes 6308864 | tf_op jit(solution)/shard_map/reduce_sum | solution.py:277
  114.0 1.1 collective-permute-done.11
  115.1 0.5 collective-permute-start.12
  115.7 7.7 %collective-permute-done.12 = f32[256]{0:T(256)S(1)} collective-permute-done((f32[256]{0:T(256)S(1)}, f32[256]{0:T(256)S(1)}, u32[]{:S(2)}, u32[]{:S(2)}) %collective-permute-start.12) | collective-permute-done | bytes 1056 | tf_op jit(solution)/shard_map/ppermute | solution.py:104
  123.4 2.6 %fusion.14 = bf16[256,1024]{1,0:T(8,128)(2,1)} fusion(bf16[256,1024]{1,0:T(8,128)(2,1)S(1)} %copy-done.6, f32[256,4096]{1,0:T(8,128)} %copy-done.1, s32[]{:T(128)} %select_n.110, bf16[1,256,1024]{2,1,0:T(8,128)(2,1)S(1)} %collective-permute-done.10, f32[256]{0:T(256)S(1)} %add_multiply_fusion, f32[256]{0:T(256)S(1)} %copy-done.20, ...), kind=kLoop, calls=%fused_computation.32 | loop fusion | flops 3407872 | bytes 3677188 | tf_op jit(solution)/shard_map/convert_element_type | solution.py:295
  126.0 0.8 copy.144
  (102 shorter events, 4.7 us)
Async XLA Ops:
  7.2 31.0 %copy-start = (bf16[4096,256]{1,0:T(8,128)(2,1)S(1)}, bf16[4096,256]{1,0:T(8,128)(2,1)}, u32[]{:S(2)}) copy-start(bf16[4096,256]{1,0:T(8,128)(2,1)} %param.12) | copy-start | bytes 6291460
  7.2 28.1 %all-gather.3.cloned.1.call-start = ((), (), s32[]{:S(2)}) async-start(), calls=%async_computation.1 | async-start | bytes 2621440 | tf_op jit(solution)/shard_map/all_gather | solution.py:181
  7.9 51.2 %all-gather.5.cloned.1.call-start = ((), (), s32[]{:S(2)}) async-start(), calls=%async_computation.2 | async-start | bytes 2621440 | tf_op jit(solution)/shard_map/all_gather | solution.py:214
  9.2 11.8 %collective-permute-start.6 = (bf16[32,1024]{1,0:T(8,128)(2,1)S(1)}, bf16[32,1024]{1,0:T(8,128)(2,1)S(1)}, u32[]{:S(2)}, u32[]{:S(2)}) collective-permute-start(bf16[32,1024]{1,0:T(8,128)(2,1)S(1)} %get-tuple-element.36), channel_id=1, source_target_pairs={{0,28},{4,0},{8,4},{12,8},{16,12},{20,16},{24,20},{28,24},{1,29},{... | collective-permute-start | bytes 196616 | tf_op jit(solution)/shard_map/ppermute | solution.py:159
  15.2 7.7 %collective-permute-start.5 = (bf16[32,1024]{1,0:T(8,128)(2,1)S(1)}, bf16[32,1024]{1,0:T(8,128)(2,1)S(1)}, u32[]{:S(2)}, u32[]{:S(2)}) collective-permute-start(bf16[32,1024]{1,0:T(8,128)(2,1)S(1)} %get-tuple-element.37), channel_id=1, source_target_pairs={{0,24},{4,28},{8,0},{12,4},{16,8},{20,12},{24,16},{28,20},{1,25},{... | collective-permute-start | bytes 196616 | tf_op jit(solution)/shard_map/ppermute | solution.py:159
  15.7 9.9 %collective-permute-start.4 = (bf16[32,1024]{1,0:T(8,128)(2,1)S(1)}, bf16[32,1024]{1,0:T(8,128)(2,1)S(1)}, u32[]{:S(2)}, u32[]{:S(2)}) collective-permute-start(bf16[32,1024]{1,0:T(8,128)(2,1)S(1)} %get-tuple-element.38), channel_id=1, source_target_pairs={{0,20},{4,24},{8,28},{12,0},{16,4},{20,8},{24,12},{28,16},{1,21},{... | collective-permute-start | bytes 196616 | tf_op jit(solution)/shard_map/ppermute | solution.py:159
  15.7 10.0 %collective-permute-start.3 = (bf16[32,1024]{1,0:T(8,128)(2,1)S(1)}, bf16[32,1024]{1,0:T(8,128)(2,1)S(1)}, u32[]{:S(2)}, u32[]{:S(2)}) collective-permute-start(bf16[32,1024]{1,0:T(8,128)(2,1)S(1)} %get-tuple-element.39), channel_id=1, source_target_pairs={{0,16},{4,20},{8,24},{12,28},{16,0},{20,4},{24,8},{28,12},{1,17},{... | collective-permute-start | bytes 196616 | tf_op jit(solution)/shard_map/ppermute | solution.py:159
  18.7 9.9 %collective-permute-start.2 = (bf16[32,1024]{1,0:T(8,128)(2,1)S(1)}, bf16[32,1024]{1,0:T(8,128)(2,1)S(1)}, u32[]{:S(2)}, u32[]{:S(2)}) collective-permute-start(bf16[32,1024]{1,0:T(8,128)(2,1)S(1)} %get-tuple-element.40), channel_id=1, source_target_pairs={{0,12},{4,16},{8,20},{12,24},{16,28},{20,0},{24,4},{28,8},{1,13},{... | collective-permute-start | bytes 196616 | tf_op jit(solution)/shard_map/ppermute | solution.py:159
  21.0 8.3 %collective-permute-start.1 = (bf16[32,1024]{1,0:T(8,128)(2,1)S(1)}, bf16[32,1024]{1,0:T(8,128)(2,1)S(1)}, u32[]{:S(2)}, u32[]{:S(2)}) collective-permute-start(bf16[32,1024]{1,0:T(8,128)(2,1)S(1)} %get-tuple-element.41), channel_id=1, source_target_pairs={{0,8},{4,12},{8,16},{12,20},{16,24},{20,28},{24,0},{28,4},{1,9},{5... | collective-permute-start | bytes 196616 | tf_op jit(solution)/shard_map/ppermute | solution.py:159
  22.9 7.2 %collective-permute-start = (bf16[32,1024]{1,0:T(8,128)(2,1)S(1)}, bf16[32,1024]{1,0:T(8,128)(2,1)S(1)}, u32[]{:S(2)}, u32[]{:S(2)}) collective-permute-start(bf16[32,1024]{1,0:T(8,128)(2,1)S(1)} %get-tuple-element.42), channel_id=1, source_target_pairs={{0,4},{4,8},{8,12},{12,16},{16,20},{20,24},{24,28},{28,0},{1,5},{5... | collective-permute-start | bytes 196616 | tf_op jit(solution)/shard_map/ppermute | solution.py:159
  34.1 4.0 %copy-start.19 = (f32[4096]{0:T(1024)S(1)}, f32[4096]{0:T(1024)}, u32[]{:S(2)}) copy-start(f32[4096]{0:T(1024)} %param.10) | copy-start | bytes 49156
  35.3 2.8 %copy-start.2 = (bf16[256,4096]{1,0:T(8,128)(2,1)S(1)}, bf16[256,4096]{1,0:T(8,128)(2,1)}, u32[]{:S(2)}) copy-start(bf16[256,4096]{1,0:T(8,128)(2,1)} %all-gather.3.cloned.1.call-done) | copy-start | bytes 6291460
  38.1 10.8 %copy-start.21 = (f32[256]{0:T(256)}, f32[256]{0:T(256)S(1)}, u32[]{:S(2)}) copy-start(f32[256]{0:T(256)S(1)} %get-tuple-element.49) | copy-start | bytes 3076
  47.0 1.1 copy-start.17
  47.1 0.8 copy-start.9
  47.2 0.9 copy-start.11
  47.2 1.9 %copy-start.3 = (bf16[256,4096]{1,0:T(8,128)(2,1)S(1)}, bf16[256,4096]{1,0:T(8,128)(2,1)}, u32[]{:S(2)}) copy-start(bf16[256,4096]{1,0:T(8,128)(2,1)} %all-gather.3.cloned.1.call-done) | copy-start | bytes 6291460
  47.2 2.6 %copy-start.13 = (bf16[4096,256]{1,0:T(8,128)(2,1)S(1)}, bf16[4096,256]{1,0:T(8,128)(2,1)}, u32[]{:S(2)}) copy-start(bf16[4096,256]{1,0:T(8,128)(2,1)} %param.13) | copy-start | bytes 6291460
  47.3 3.7 %copy-start.15 = (bf16[256,2,64]{2,0,1:T(8,128)(2,1)}, bf16[256,2,64]{2,0,1:T(8,128)(2,1)S(1)}, u32[]{:S(2)}) copy-start(bf16[256,2,64]{2,0,1:T(8,128)(2,1)S(1)} %get-tuple-element.33) | copy-start | bytes 196612
  49.8 1.4 %copy-start.25 = (f32[2,256,256,4]{2,1,3,0:T(8,128)}, f32[2,256,256,4]{2,1,3,0:T(8,128)S(1)}, u32[]{:S(2)}) copy-start(f32[2,256,256,4]{2,1,3,0:T(8,128)S(1)} %get-tuple-element.51) | copy-start | bytes 6291460
  49.8 1.4 %copy-start.27 = (f32[2,4,256]{2,1,0:T(4,128)}, f32[2,4,256]{2,1,0:T(4,128)S(1)}, u32[]{:S(2)}) copy-start(f32[2,4,256]{2,1,0:T(4,128)S(1)} %get-tuple-element.50) | copy-start | bytes 24580
  49.8 3.0 %slice-start = ((s8[8388608]{0:T(1024)(128)(4,1)}), s8[4194304]{0:T(1024)(128)(4,1)S(1)}, s32[]{:S(2)}) async-start(s8[8388608]{0:T(1024)(128)(4,1)} %bitcast.162), calls=%async_computation.3 | async-start | bytes 8388608
  51.0 0.8 copy-start.24
  51.1 3.1 %slice-start.1 = ((s8[8388608]{0:T(1024)(128)(4,1)}), s8[4194304]{0:T(1024)(128)(4,1)S(1)}, s32[]{:S(2)}) async-start(s8[8388608]{0:T(1024)(128)(4,1)} %bitcast.162), calls=%async_computation.4 | async-start | bytes 8388608
  61.9 7.7 %collective-permute-start.7 = (bf16[2,256,1024]{2,1,0:T(8,128)(2,1)}, bf16[2,256,1024]{2,1,0:T(8,128)(2,1)}, u32[]{:S(2)}, u32[]{:S(2)}) collective-permute-start(bf16[2,256,1024]{2,1,0:T(8,128)(2,1)} %pad_maximum_fusion), channel_id=1, source_target_pairs={{0,1},{1,0},{2,3},{3,2},{4,5},{5,4},{6,7},{7,6},{8,9},{9,8},{10,11... | collective-permute-start | bytes 3145736 | tf_op jit(solution)/shard_map/ppermute | solution.py:102
  70.8 2.7 %copy-start.7 = (bf16[256,1024]{0,1:T(8,128)(2,1)}, bf16[256,1024]{0,1:T(8,128)(2,1)S(1)}, u32[]{:S(2)}) copy-start(bf16[256,1024]{0,1:T(8,128)(2,1)S(1)} %copy.99) | copy-start | bytes 1572868
  71.0 2.5 %copy-start.10 = (bf16[256,8,64]{2,0,1:T(8,128)(2,1)S(1)}, bf16[256,8,64]{2,0,1:T(8,128)(2,1)}, u32[]{:S(2)}) copy-start(bf16[256,8,64]{2,0,1:T(8,128)(2,1)} %copy-done.9) | copy-start | bytes 786436
  71.0 2.5 %copy-start.12 = (bf16[256,8,64]{2,0,1:T(8,128)(2,1)S(1)}, bf16[256,8,64]{2,0,1:T(8,128)(2,1)}, u32[]{:S(2)}) copy-start(bf16[256,8,64]{2,0,1:T(8,128)(2,1)} %copy-done.11) | copy-start | bytes 786436
  73.5 0.9 copy-start.16
  80.1 15.0 %collective-permute-start.8 = (bf16[1,256,1024]{2,1,0:T(8,128)(2,1)}, bf16[1,256,1024]{2,1,0:T(8,128)(2,1)}, u32[]{:S(2)}, u32[]{:S(2)}) collective-permute-start(bf16[1,256,1024]{2,1,0:T(8,128)(2,1)} %fusion.23), channel_id=1, source_target_pairs={{0,2},{1,3},{2,0},{3,1},{4,6},{5,7},{6,4},{7,5},{8,10},{9,11},{10,... | collective-permute-start | bytes 1572872 | tf_op jit(solution)/shard_map/ppermute | solution.py:102
  90.9 1.0 copy-start.8
  90.9 1.0 copy-start.18
  90.9 1.8 %copy-start.26 = (f32[2,256,256,4]{2,1,3,0:T(8,128)S(1)}, f32[2,256,256,4]{2,1,3,0:T(8,128)}, u32[]{:S(2)}) copy-start(f32[2,256,256,4]{2,1,3,0:T(8,128)} %copy-done.25) | copy-start | bytes 6291460
  90.9 1.8 %copy-start.28 = (f32[2,4,256]{2,1,0:T(4,128)S(1)}, f32[2,4,256]{2,1,0:T(4,128)}, u32[]{:S(2)}) copy-start(f32[2,4,256]{2,1,0:T(4,128)} %copy-done.27) | copy-start | bytes 24580
  92.7 1.6 %copy-start.14 = (bf16[4096,256]{1,0:T(8,128)(2,1)S(1)}, bf16[4096,256]{1,0:T(8,128)(2,1)}, u32[]{:S(2)}) copy-start(bf16[4096,256]{1,0:T(8,128)(2,1)} %param.13) | copy-start | bytes 6291460
  94.3 1.0 copy-start.6
  95.1 3.5 %copy-start.1 = (f32[256,4096]{1,0:T(8,128)}, f32[256,4096]{1,0:T(8,128)S(1)}, u32[]{:S(2)}) copy-start(f32[256,4096]{1,0:T(8,128)S(1)} %convolution_add_fusion) | copy-start | bytes 12582916
  98.4 0.7 copy-start.23
  98.7 2.9 %collective-permute-start.9 = (bf16[2,256,1024]{2,1,0:T(8,128)(2,1)S(1)}, bf16[2,256,1024]{2,1,0:T(8,128)(2,1)}, u32[]{:S(2)}, u32[]{:S(2)}) collective-permute-start(bf16[2,256,1024]{2,1,0:T(8,128)(2,1)S(1)} %pad_maximum_fusion.1), channel_id=1, source_target_pairs={{0,1},{1,0},{2,3},{3,2},{4,5},{5,4},{6,7},{7,6},{8,9},{9,8},{10,11... | collective-permute-start | bytes 3145736 | tf_op jit(solution)/shard_map/ppermute | solution.py:104
  102.6 23.4 %all-to-all-start = ((bf16[8,32,1024]{2,1,0:T(8,128)(2,1)}), bf16[8,32,1024]{2,1,0:T(8,128)(2,1)S(1)}, u32[]{:S(2)}, u32[]{:S(2)}) async-start(bf16[8,32,1024]{2,1,0:T(8,128)(2,1)} %copy.112), calls=%async_computation | async-start | bytes 1048576 | tf_op jit(solution)/shard_map/all_to_all | solution.py:285
  107.8 3.3 %copy-start.4 = (bf16[256,4096]{1,0:T(8,128)(2,1)S(1)}, bf16[256,4096]{1,0:T(8,128)(2,1)}, u32[]{:S(2)}) copy-start(bf16[256,4096]{1,0:T(8,128)(2,1)} %all-gather.3.cloned.1.call-done) | copy-start | bytes 6291460
  109.5 13.9 %copy-start.5 = (bf16[8,32,1024]{2,1,0:T(8,128)(2,1)S(1)}, bf16[8,32,1024]{2,1,0:T(8,128)(2,1)}, u32[]{:S(2)}) copy-start(bf16[8,32,1024]{2,1,0:T(8,128)(2,1)} %copy.98) | copy-start | bytes 1572868
  109.5 13.9 %dynamic-slice-start = ((f32[4096]{0:T(1024)}, s32[]{:T(128)}), f32[1024]{0:T(1024)S(1)}, s32[]{:S(2)}) async-start(f32[4096]{0:T(1024)} %param.10, s32[]{:T(128)} %select_n.110), calls=%async_computation.5 | async-start | bytes 8704 | tf_op jit(solution)/shard_map/dynamic_slice | solution.py:142
  109.5 13.9 %copy-start.20 = (f32[256]{0:T(256)S(1)}, f32[256]{0:T(256)}, u32[]{:S(2)}) copy-start(f32[256]{0:T(256)} %get-tuple-element.48) | copy-start | bytes 3076
  109.5 13.9 %copy-start.22 = (f32[256]{0:T(256)S(1)}, f32[256]{0:T(256)}, u32[]{:S(2)}) copy-start(f32[256]{0:T(256)} %copy-done.21) | copy-start | bytes 3076
  109.5 13.8 %collective-permute-start.10 = (bf16[1,256,1024]{2,1,0:T(8,128)(2,1)S(1)}, bf16[1,256,1024]{2,1,0:T(8,128)(2,1)S(1)}, u32[]{:S(2)}, u32[]{:S(2)}) collective-permute-start(bf16[1,256,1024]{2,1,0:T(8,128)(2,1)S(1)} %fusion.24), channel_id=1, source_target_pairs={{0,2},{1,3},{2,0},{3,1},{4,6},{5,7},{6,4},{7,5},{8,10},{9,11},{10,... | collective-permute-start | bytes 1572872 | tf_op jit(solution)/shard_map/ppermute | solution.py:104
  113.9 1.2 collective-permute-start.11
  115.1 8.2 %collective-permute-start.12 = (f32[256]{0:T(256)S(1)}, f32[256]{0:T(256)S(1)}, u32[]{:S(2)}, u32[]{:S(2)}) collective-permute-start(f32[256]{0:T(256)S(1)} %add.200), channel_id=1, source_target_pairs={{0,2},{1,3},{2,0},{3,1},{4,6},{5,7},{6,4},{7,5},{8,10},{9,11},{10,... | collective-permute-start | bytes 3080 | tf_op jit(solution)/shard_map/ppermute | solution.py:104
Sparse Core Ops, SparseCore 0:
  9.6 25.2 all-gather.2
  36.5 22.5 all-gather.4

commit v23 on v22

--- a/solution.py
+++ b/solution.py
@@ -237,21 +237,37 @@
     grad_scores = (probs * (grad_probs - jnp.transpose(delta, (1, 2, 0))[..., None])).astype(
         jnp.bfloat16
     )
-    grad_query_rot = (
-        jnp.einsum("kgqs,skd->qkgd", grad_scores, keys, preferred_element_type=jnp.float32)
-        * scale_factor
-    )
-    grad_keys_rot = (
-        jnp.einsum("kgqs,qkgd->skd", grad_scores, grouped_query, preferred_element_type=jnp.float32)
-        * scale_factor
-    )
+    half = HEAD_SIZE // 2
+
+    def halves_product(spec, left, right):
+        return [
+            jnp.einsum(spec, left, piece, preferred_element_type=jnp.float32) * scale_factor
+            for piece in (right[..., :half], right[..., half:])
+        ]
+
+    query_former, query_latter = halves_product("kgqs,skd->qkgd", grad_scores, keys)
+    query_former = query_former.reshape(token_row_count, heads_local, half)
+    query_latter = query_latter.reshape(token_row_count, heads_local, half)
+    cos_part = cosine[:, None, :]
+    sin_part = sine_table[:, None, :]
+    grad_query = jnp.concatenate(
+        [
+            query_former * cos_part + query_latter * sin_part,
+            query_latter * cos_part - query_former * sin_part,
+        ],
+        axis=-1,
+    ).astype(jnp.bfloat16)
+    key_former, key_latter = halves_product("kgqs,qkgd->skd", grad_scores, grouped_query)
+    key_gradient = jnp.concatenate(
+        [
+            key_former * cos_part + key_latter * sin_part,
+            key_latter * cos_part - key_former * sin_part,
+        ],
+        axis=-1,
+    ).astype(jnp.bfloat16)
     value_gradient = jnp.einsum(
         "kgqs,qkgd->skd", probs_low, grouped_gradient, preferred_element_type=jnp.float32
     )
-    grad_query = unrotate(
-        grad_query_rot.reshape(token_row_count, heads_local, HEAD_SIZE), cosine, sine_table
-    ).astype(jnp.bfloat16)
-    key_gradient = unrotate(grad_keys_rot, cosine, sine_table).astype(jnp.bfloat16)
     contract_out = (((1,), (1,)), ((), ()))
     normed_partial = (
         lax.dot_general(

time: 135 us -> 134 us (level)
  matrix products: 34.6 us -> 38.5 us
  other arithmetic: 22.8 us -> 19.2 us
  waiting for transfers between devices: 14.8 us -> 17.3 us
  local copies, waits for them, and re-layouts: 25.4 us -> 23.3 us
  starting transfers between devices: 21.3 us -> 19.9 us
    unnamed x69 -> x64, local copies, waits for them, and re-layouts: 12 us -> 7.69 us
    ppermute x2, waiting for transfers between devices: 0.01 us -> 2.13 us  [scatter_features(): incoming = lax.ppermute(outgoing, axis_name, _xor_pairs(size, bit))]
    another operation x5 -> x3, other arithmetic: 3.06 us -> 1.13 us
    concatenate x1 -> x2, local copies, waits for them, and re-layouts: 0.11 us -> 2.01 us  [rotate(): jnp.concatenate([former * cos_part - latter * sin_part, latter * cos_part...]
    convert_element_type x1, other arithmetic: 3.06 us -> 1.35 us  [per_device(): output_home = (x_float + mixed).astype(jnp.bfloat16)]
    dot_general x1, matrix products: 0.85 us -> 2.55 us  [per_device(): jnp.einsum('qkgd,skd->kgqs', grouped_query, keys, preferred_element_type=...]
    all_to_all x1, starting transfers between devices: 5.18 us -> 3.49 us  [per_device(): lax.all_to_all(outgoing, 'dp', split_axis=0, concat_axis=0, tiled=True)]
    dot_general x1, matrix products: 6.67 us -> 8.16 us  [per_device(): jnp.dot(normed_input, w_query, preferred_element_type=jnp.float32)]
  transfers between devices with their start and end apart: 16 -> 16, of which waited for: 5 -> 6; matrix products, arithmetic and copies ran while one was open for 43% -> 45% of each run, Pallas kernels for 0% -> 0%
where the time goes in v23:
time: 134 us; the launch traced here: 133 us
  matrix products  38.5 us (29%)
  local copies, waits for them, and re-layouts  23.3 us (17%)
  starting transfers between devices  19.9 us (15%)
  other arithmetic  19.2 us (14%)
  waiting for transfers between devices  17.3 us (13%)
  between operations  14.8 us (11%)
    ppermute x7, starting transfers between devices, per_device(): returned.append(lax.ppermute(piece, 'dp', pairs))  12.5 us
    ppermute x4, waiting for transfers between devices, scatter_features(): lax.ppermute((outgoing, extra), axis_name, _xor_pairs(size, bit))  11.2 us
    dot_general x1, matrix products, per_device(): jnp.dot(normed_input, w_query, preferred_element_type=jnp.float32)  8.16 us
    unnamed x64, local copies, waits for them, and re-layouts  7.69 us
    dot_general x1, matrix products, per_device(): lax.dot_general(w_out, grad_full, (((1,), (1,)), ((), ())), preferred_ele...  7.42 us
    dot_general x1, matrix products, per_device(): lax.dot_general(grad_query.reshape(token_row_count, query_width), w_query...  5.81 us
    another operation x8, local copies, waits for them, and re-layouts, per_device(): returned = jnp.stack(returned)  4.91 us
    dot_general x1, matrix products, per_device(): jnp.dot(attended_flat, w_out, preferred_element_type=jnp.float32)  4.53 us
  transfers between devices with their start and end apart: 16, of which 6 were waited for; matrix products, arithmetic and copies ran while one was open for 45% of the time, Pallas kernels for 0%

profile of v23, /device:TPU:0, one launch (start us, length us, event | category | flops | bytes accessed | tf_op | source)
XLA Modules:
  0.0 133.0 jit_solution(4528214256355407275)
XLA Ops:
  7.2 0.7 all-gather.3.cloned.1.call-update
  8.1 1.1 dynamic-slice_bitcast_fusion
  9.2 6.0 %collective-permute-start.6 = (bf16[32,1024]{1,0:T(8,128)(2,1)S(1)}, bf16[32,1024]{1,0:T(8,128)(2,1)S(1)}, u32[]{:S(2)}, u32[]{:S(2)}) collective-permute-start(bf16[32,1024]{1,0:T(8,128)(2,1)S(1)} %get-tuple-element.32), channel_id=1, source_target_pairs={{0,28},{4,0},{8,4},{12,8},{16,12},{20,16},{24,20},{28,24},{1,29},{... | collective-permute-start | bytes 196616 | tf_op jit(solution)/shard_map/ppermute | solution.py:159
  15.2 0.4 collective-permute-start.5
  15.7 3.0 %collective-permute-start.3 = (bf16[32,1024]{1,0:T(8,128)(2,1)S(1)}, bf16[32,1024]{1,0:T(8,128)(2,1)S(1)}, u32[]{:S(2)}, u32[]{:S(2)}) collective-permute-start(bf16[32,1024]{1,0:T(8,128)(2,1)S(1)} %get-tuple-element.35), channel_id=1, source_target_pairs={{0,16},{4,20},{8,24},{12,28},{16,0},{20,4},{24,8},{28,12},{1,17},{... | collective-permute-start | bytes 196616 | tf_op jit(solution)/shard_map/ppermute | solution.py:159
  18.7 0.8 reduce-window.8
  19.6 1.0 broadcast_multiply_fusion.1
  20.6 0.7 fusion.34
  21.3 0.7 copy.141
  22.0 0.8 copy.139
  22.9 1.9 %collective-permute-start.1 = (bf16[32,1024]{1,0:T(8,128)(2,1)S(1)}, bf16[32,1024]{1,0:T(8,128)(2,1)S(1)}, u32[]{:S(2)}, u32[]{:S(2)}) collective-permute-start(bf16[32,1024]{1,0:T(8,128)(2,1)S(1)} %get-tuple-element.37), channel_id=1, source_target_pairs={{0,8},{4,12},{8,16},{12,20},{16,24},{20,28},{24,0},{28,4},{1,9},{5... | collective-permute-start | bytes 196616 | tf_op jit(solution)/shard_map/ppermute | solution.py:159
  24.8 1.1 collective-permute-start
  25.9 1.3 and_select_fusion
  27.8 2.2 %collective-permute-done.1 = bf16[32,1024]{1,0:T(8,128)(2,1)S(1)} collective-permute-done((bf16[32,1024]{1,0:T(8,128)(2,1)S(1)}, bf16[32,1024]{1,0:T(8,128)(2,1)S(1)}, u32[]{:S(2)}, u32[]{:S(2)}) %collective-permute-start.1) | collective-permute-done | bytes 65568 | tf_op jit(solution)/shard_map/ppermute | solution.py:159
  30.0 0.8 copy.148
  30.7 1.0 collective-permute-done
  31.8 0.8 copy.147
  32.5 2.9 %stack.58 = bf16[8,32,1024]{2,0,1:T(8,128)(2,1)S(1)} concatenate(bf16[1,32,1024]{2,0,1:T(2,128)(2,1)S(1)} %copy.191, bf16[1,32,1024]{2,0,1:T(2,128)(2,1)} %copy.147, bf16[1,32,1024]{2,0,1:T(2,128)(2,1)} %copy.148, bf16[1,32,1024]{2,0,1:T(2,128)(2,1)S(1)} %copy.149, bf16[1,32,1024]{2,0,1:T(2,128)(2,1)S(1)} %copy.150, bf16[1,32,1024]{2,0,1:T(2,128)(2,1)S(1)} %copy.151, ...), dimensions={0} | concatenate | bytes 1048576 | tf_op jit(solution)/shard_map/stack | solution.py:160
  35.4 0.4 convolution_convert_fusion.3
  35.8 1.1 copy.154
  37.0 2.2 %fusion = f32[256]{0:T(256)S(1)} fusion(bf16[256,4096]{1,0:T(8,128)(2,1)} %all-gather.3.cloned.1.call-done), kind=kLoop, calls=%fused_computation.5 | loop fusion | flops 3145472 | bytes 2098176 | tf_op jit(solution)/shard_map/reduce_sum | solution.py:183
  39.2 0.6 multiply_multiply_fusion
  39.8 1.2 fusion.52
  41.3 8.2 %fusion.50 = f32[256,1024]{0,1:T(8,128)S(1)} fusion(bf16[4096,1024]{1,0:T(8,128)(2,1)} %param.11, bf16[256,4096]{1,0:T(8,128)(2,1)} %all-gather.3.cloned.1.call-done, f32[4096]{0:T(1024)S(1)} %copy-done.20, f32[256]{0:T(256)S(1)} %get-tuple-element.49), kind=kOutput, calls=%fused_computation.119 | convolution fusion | flops 2151677952 | bytes 11551744 | tf_op jit(solution)/shard_map/dot_general | solution.py:185
  49.6 1.0 copy.144
  50.6 1.0 copy.143
  51.7 0.6 copy-done.13
  52.4 2.5 %fusion.7 = (f32[2,4,256]{2,1,0:T(4,128)S(1)}, f32[2,256,256,4]{2,1,3,0:T(8,128)S(1)}) fusion(pred[256,256]{0,1:T(8,128)(4,1)} %fusion.34, bf16[256,2,4,64]{3,0,2,1:T(8,128)(2,1)} %copy.144, bf16[256,2,4,64]{3,0,2,1:T(8,128)(2,1)} %copy.143, bf16[256,2,64]{2,0,1:T(8,128)(2,1)S(1)} %get-tuple-element.31, bf16[256,2,64]{2,0,1:T(8,128)(2,1)S(1)} %get-tuple-element.30), kind=kOutput, calls=%fused_computation.14 | convolution fusion | flops 137099264 | bytes 2826240 | tf_op jit(solution)/shard_map/qkgd,skd->kgqs/dot_general | solution.py:203
  55.0 1.2 convolution_convert_fusion.4
  56.3 0.7 convolution_convert_fusion.1
  57.0 1.0 slice-done
  58.0 1.4 %slice-done.1 = s8[4194304]{0:T(1024)(128)(4,1)S(1)} async-done(((s8[8388608]{0:T(1024)(128)(4,1)}), s8[4194304]{0:T(1024)(128)(4,1)S(1)}, s32[]{:S(2)}) %slice-start.1) | async-done | bytes 4194328
  59.4 4.5 %fusion.59 = f32[256,4096]{1,0:T(8,128)} fusion(bf16[256,1024]{0,1:T(8,128)(2,1)S(1)} %bitcast.192, bf16[1024,4096]{1,0:T(8,128)(2,1)S(1)} %bitcast.190), kind=kOutput, calls=%fused_computation.122 | convolution fusion | flops 2147483648 | bytes 13107200 | tf_op jit(solution)/shard_map/dot_general | solution.py:213
  64.0 1.7 %fusion.17 = (bf16[1,256,1024]{2,1,0:T(8,128)(2,1)S(1)}, bf16[1,256,1024]{2,1,0:T(8,128)(2,1)S(1)}) fusion(f32[256,4096]{1,0:T(8,128)} %fusion.59, s32[]{:T(128)S(6)} %select_n.111, s32[]{:T(128)S(6)} %select_n.112), kind=kLoop, calls=%fused_computation.49 | loop fusion | bytes 2097160 | tf_op jit(solution)/shard_map/stack | solution.py:100
  65.7 1.1 pad_maximum_fusion
  66.8 7.4 %convolution_convert_fusion = bf16[256,1024]{1,0:T(8,128)(2,1)} fusion(bf16[256,4096]{1,0:T(8,128)(2,1)} %all-gather.5.cloned.1.call-done, bf16[1024,4096]{1,0:T(8,128)(2,1)} %param.14), kind=kOutput, calls=%fused_computation.17 | convolution fusion | flops 2147745792 | bytes 11010048 | tf_op jit(solution)/shard_map/dot_general | solution.py:217
  74.2 2.0 %copy.155 = bf16[256,1024]{0,1:T(8,128)(2,1)} copy(bf16[256,1024]{1,0:T(8,128)(2,1)} %convolution_convert_fusion) | data formatting | bytes 1048576 | tf_op jit(solution)/shard_map/optimization_barrier | solution.py:107
  76.3 1.2 multiply_reduce_fusion
  77.5 2.5 %fusion.5 = bf16[2,4,256,256]{2,3,1,0:T(8,128)(2,1)S(1)} fusion(bf16[256,2,128,1]{0,2,3,1:T(8,128)(2,1)S(1)} %bitcast.218, bf16[256,2,4,128]{0,3,2,1:T(8,128)(2,1)} %bitcast.198, f32[2,4,256]{2,1,0:T(4,128)S(1)} %bitcast.214, f32[2,4,256]{2,1,0:T(4,128)S(1)} %get-tuple-element.50, f32[2,256,256,4]{2,1,3,0:T(8,128)} %copy-done.26, ...), kind=kOutput, calls=%fused_computation.11 | convolution fusion | flops 137363456 | bytes 3883008 | tf_op jit(solution)/shard_map/qkgd,skd->kgqs/dot_general | solution.py:234
  80.0 0.4 convolution_bitcast_fusion.2
  81.2 1.0 copy-done.2
  82.2 1.2 fusion.21
  83.4 1.6 %collective-permute-start.8 = (bf16[1,256,1024]{2,1,0:T(8,128)(2,1)S(1)}, bf16[1,256,1024]{2,1,0:T(8,128)(2,1)S(1)}, u32[]{:S(2)}, u32[]{:S(2)}) collective-permute-start(bf16[1,256,1024]{2,1,0:T(8,128)(2,1)S(1)} %fusion.21), channel_id=1, source_target_pairs={{0,2},{1,3},{2,0},{3,1},{4,6},{5,7},{6,4},{7,5},{8,10},{9,11},{10,... | collective-permute-start | bytes 1572872 | tf_op jit(solution)/shard_map/ppermute | solution.py:102
  85.2 5.8 %fusion.60 = f32[256,4096]{1,0:T(8,128)S(1)} fusion(bf16[256,1024]{0,1:T(8,128)(2,1)S(1)} %bitcast.203, bf16[4096,1024]{1,0:T(8,128)(2,1)} %param.11), kind=kOutput, calls=%fused_computation.123 | convolution fusion | flops 2147483648 | bytes 13107200 | tf_op jit(solution)/shard_map/dot_general | solution.py:273
  91.0 0.4 add_convert_fusion.2
  91.5 0.8 convolution_add_fusion.1
  92.5 0.7 copy-done.27
  93.3 0.7 fusion.8
  93.9 0.9 copy-done.10
  94.8 0.8 convolution_add_fusion
  95.7 2.1 %collective-permute-done.8 = bf16[1,256,1024]{2,1,0:T(8,128)(2,1)S(1)} collective-permute-done((bf16[1,256,1024]{2,1,0:T(8,128)(2,1)S(1)}, bf16[1,256,1024]{2,1,0:T(8,128)(2,1)S(1)}, u32[]{:S(2)}, u32[]{:S(2)}) %collective-permute-start.8) | collective-permute-done | bytes 524320 | tf_op jit(solution)/shard_map/ppermute | solution.py:102
  97.8 1.4 %fusion.9 = bf16[256,1024]{1,0:T(8,128)(2,1)S(1)} fusion(bf16[256,1024]{1,0:T(8,128)(2,1)S(1)} %copy-done.7, f32[256,4096]{1,0:T(8,128)S(1)} %copy-done.2, s32[]{:T(128)} %select_n.110, bf16[1,256,1024]{2,1,0:T(8,128)(2,1)S(1)} %collective-permute-done.8, bf16[2,256,1024]{2,1,0:T(8,128)(2,1)} %collective-permute-done.7), kind=kLoop, calls=%fused_computation.28 | loop fusion | flops 1835008 | bytes 3145732 | tf_op jit(solution)/shard_map/convert_element_type | solution.py:229
  99.8 0.4 convolution_convert_fusion.2
  100.2 2.1 %collective-permute-done.9 = bf16[2,256,1024]{2,1,0:T(8,128)(2,1)} collective-permute-done((bf16[2,256,1024]{2,1,0:T(8,128)(2,1)S(1)}, bf16[2,256,1024]{2,1,0:T(8,128)(2,1)}, u32[]{:S(2)}, u32[]{:S(2)}) %collective-permute-start.9) | collective-permute-done | bytes 1048608 | tf_op jit(solution)/shard_map/ppermute | solution.py:104
  102.3 1.1 copy.166
  103.4 3.5 %all-to-all-start = ((bf16[8,32,1024]{2,1,0:T(8,128)(2,1)}), bf16[8,32,1024]{2,1,0:T(8,128)(2,1)S(1)}, u32[]{:S(2)}, u32[]{:S(2)}) async-start(bf16[8,32,1024]{2,1,0:T(8,128)(2,1)} %copy.166), calls=%async_computation | async-start | bytes 1048576 | tf_op jit(solution)/shard_map/all_to_all | solution.py:301
  106.9 1.7 %fusion.22 = bf16[1,256,1024]{2,1,0:T(8,128)(2,1)S(1)} fusion(f32[256,4096]{1,0:T(8,128)} %copy-done.1, s32[]{:T(128)S(6)} %select_n.113, bf16[2,256,1024]{2,1,0:T(8,128)(2,1)} %collective-permute-done.9), kind=kLoop, calls=%fused_computation.54 | loop fusion | flops 786432 | bytes 2097156 | tf_op jit(solution)/shard_map/convert_element_type | solution.py:100
  108.6 1.6 %collective-permute-start.10 = (bf16[1,256,1024]{2,1,0:T(8,128)(2,1)S(1)}, bf16[1,256,1024]{2,1,0:T(8,128)(2,1)S(1)}, u32[]{:S(2)}, u32[]{:S(2)}) collective-permute-start(bf16[1,256,1024]{2,1,0:T(8,128)(2,1)S(1)} %fusion.22), channel_id=1, source_target_pairs={{0,2},{1,3},{2,0},{3,1},{4,6},{5,7},{6,4},{7,5},{8,10},{9,11},{10,... | collective-permute-start | bytes 1572872 | tf_op jit(solution)/shard_map/ppermute | solution.py:104
  110.2 2.8 %fusion.3 = f32[256]{0:T(256)S(1)} fusion(bf16[256,4096]{1,0:T(8,128)(2,1)S(1)} %copy-done.5, f32[256,4096]{1,0:T(8,128)} %copy-done.1, f32[4096]{0:T(1024)S(1)} %copy-done.20), kind=kLoop, calls=%fused_computation.8 | loop fusion | flops 4194048 | bytes 6308864 | tf_op jit(solution)/shard_map/reduce_sum | solution.py:293
  113.1 1.1 collective-permute-done.11
  114.2 0.5 collective-permute-start.12
  114.7 8.0 %collective-permute-done.12 = f32[256]{0:T(256)S(1)} collective-permute-done((f32[256]{0:T(256)S(1)}, f32[256]{0:T(256)S(1)}, u32[]{:S(2)}, u32[]{:S(2)}) %collective-permute-start.12) | collective-permute-done | bytes 1056 | tf_op jit(solution)/shard_map/ppermute | solution.py:104
  122.7 2.6 %fusion.12 = bf16[256,1024]{1,0:T(8,128)(2,1)} fusion(bf16[256,1024]{1,0:T(8,128)(2,1)S(1)} %copy-done.7, f32[256,4096]{1,0:T(8,128)} %copy-done.1, s32[]{:T(128)} %select_n.110, bf16[1,256,1024]{2,1,0:T(8,128)(2,1)S(1)} %collective-permute-done.10, f32[256]{0:T(256)S(1)} %add_multiply_fusion, f32[256]{0:T(256)S(1)} %copy-done.21, ...), kind=kLoop, calls=%fused_computation.31 | loop fusion | flops 3407872 | bytes 3677188 | tf_op jit(solution)/shard_map/convert_element_type | solution.py:311
  125.4 0.8 copy.195
  (98 shorter events, 3.4 us)
Async XLA Ops:
  7.2 32.6 %copy-start = (bf16[4096,256]{1,0:T(8,128)(2,1)S(1)}, bf16[4096,256]{1,0:T(8,128)(2,1)}, u32[]{:S(2)}) copy-start(bf16[4096,256]{1,0:T(8,128)(2,1)} %param.12) | copy-start | bytes 6291460
  7.2 29.8 %all-gather.3.cloned.1.call-start = ((), (), s32[]{:S(2)}) async-start(), calls=%async_computation.1 | async-start | bytes 2621440 | tf_op jit(solution)/shard_map/all_gather | solution.py:181
  7.9 56.1 %all-gather.5.cloned.1.call-start = ((), (), s32[]{:S(2)}) async-start(), calls=%async_computation.2 | async-start | bytes 2621440 | tf_op jit(solution)/shard_map/all_gather | solution.py:214
  9.2 13.7 %collective-permute-start.6 = (bf16[32,1024]{1,0:T(8,128)(2,1)S(1)}, bf16[32,1024]{1,0:T(8,128)(2,1)S(1)}, u32[]{:S(2)}, u32[]{:S(2)}) collective-permute-start(bf16[32,1024]{1,0:T(8,128)(2,1)S(1)} %get-tuple-element.32), channel_id=1, source_target_pairs={{0,28},{4,0},{8,4},{12,8},{16,12},{20,16},{24,20},{28,24},{1,29},{... | collective-permute-start | bytes 196616 | tf_op jit(solution)/shard_map/ppermute | solution.py:159
  15.2 9.6 %collective-permute-start.5 = (bf16[32,1024]{1,0:T(8,128)(2,1)S(1)}, bf16[32,1024]{1,0:T(8,128)(2,1)S(1)}, u32[]{:S(2)}, u32[]{:S(2)}) collective-permute-start(bf16[32,1024]{1,0:T(8,128)(2,1)S(1)} %get-tuple-element.33), channel_id=1, source_target_pairs={{0,24},{4,28},{8,0},{12,4},{16,8},{20,12},{24,16},{28,20},{1,25},{... | collective-permute-start | bytes 196616 | tf_op jit(solution)/shard_map/ppermute | solution.py:159
  15.7 11.8 %collective-permute-start.4 = (bf16[32,1024]{1,0:T(8,128)(2,1)S(1)}, bf16[32,1024]{1,0:T(8,128)(2,1)S(1)}, u32[]{:S(2)}, u32[]{:S(2)}) collective-permute-start(bf16[32,1024]{1,0:T(8,128)(2,1)S(1)} %get-tuple-element.34), channel_id=1, source_target_pairs={{0,20},{4,24},{8,28},{12,0},{16,4},{20,8},{24,12},{28,16},{1,21},{... | collective-permute-start | bytes 196616 | tf_op jit(solution)/shard_map/ppermute | solution.py:159
  15.7 11.9 %collective-permute-start.3 = (bf16[32,1024]{1,0:T(8,128)(2,1)S(1)}, bf16[32,1024]{1,0:T(8,128)(2,1)S(1)}, u32[]{:S(2)}, u32[]{:S(2)}) collective-permute-start(bf16[32,1024]{1,0:T(8,128)(2,1)S(1)} %get-tuple-element.35), channel_id=1, source_target_pairs={{0,16},{4,20},{8,24},{12,28},{16,0},{20,4},{24,8},{28,12},{1,17},{... | collective-permute-start | bytes 196616 | tf_op jit(solution)/shard_map/ppermute | solution.py:159
  18.7 9.0 %collective-permute-start.2 = (bf16[32,1024]{1,0:T(8,128)(2,1)S(1)}, bf16[32,1024]{1,0:T(8,128)(2,1)S(1)}, u32[]{:S(2)}, u32[]{:S(2)}) collective-permute-start(bf16[32,1024]{1,0:T(8,128)(2,1)S(1)} %get-tuple-element.36), channel_id=1, source_target_pairs={{0,12},{4,16},{8,20},{12,24},{16,28},{20,0},{24,4},{28,8},{1,13},{... | collective-permute-start | bytes 196616 | tf_op jit(solution)/shard_map/ppermute | solution.py:159
  22.9 7.1 %collective-permute-start.1 = (bf16[32,1024]{1,0:T(8,128)(2,1)S(1)}, bf16[32,1024]{1,0:T(8,128)(2,1)S(1)}, u32[]{:S(2)}, u32[]{:S(2)}) collective-permute-start(bf16[32,1024]{1,0:T(8,128)(2,1)S(1)} %get-tuple-element.37), channel_id=1, source_target_pairs={{0,8},{4,12},{8,16},{12,20},{16,24},{20,28},{24,0},{28,4},{1,9},{5... | collective-permute-start | bytes 196616 | tf_op jit(solution)/shard_map/ppermute | solution.py:159
  24.8 7.0 %collective-permute-start = (bf16[32,1024]{1,0:T(8,128)(2,1)S(1)}, bf16[32,1024]{1,0:T(8,128)(2,1)S(1)}, u32[]{:S(2)}, u32[]{:S(2)}) collective-permute-start(bf16[32,1024]{1,0:T(8,128)(2,1)S(1)} %get-tuple-element.38), channel_id=1, source_target_pairs={{0,4},{4,8},{8,12},{12,16},{16,20},{20,24},{24,28},{28,0},{1,5},{5... | collective-permute-start | bytes 196616 | tf_op jit(solution)/shard_map/ppermute | solution.py:159
  35.8 4.0 %copy-start.20 = (f32[4096]{0:T(1024)S(1)}, f32[4096]{0:T(1024)}, u32[]{:S(2)}) copy-start(f32[4096]{0:T(1024)} %param.10) | copy-start | bytes 49156
  36.9 2.8 %copy-start.3 = (bf16[256,4096]{1,0:T(8,128)(2,1)S(1)}, bf16[256,4096]{1,0:T(8,128)(2,1)}, u32[]{:S(2)}) copy-start(bf16[256,4096]{1,0:T(8,128)(2,1)} %all-gather.3.cloned.1.call-done) | copy-start | bytes 6291460
  39.8 1.5 %copy-start.22 = (f32[256]{0:T(256)}, f32[256]{0:T(256)S(1)}, u32[]{:S(2)}) copy-start(f32[256]{0:T(256)S(1)} %get-tuple-element.49) | copy-start | bytes 3076
  49.4 2.2 %copy-start.11 = (f32[256,64]{1,0:T(8,128)S(1)}, f32[256,64]{1,0:T(8,128)}, u32[]{:S(2)}) copy-start(f32[256,64]{1,0:T(8,128)} %copy.141) | copy-start | bytes 196612
  49.4 2.2 %copy-start.12 = (f32[256,64]{1,0:T(8,128)S(1)}, f32[256,64]{1,0:T(8,128)}, u32[]{:S(2)}) copy-start(f32[256,64]{1,0:T(8,128)} %copy.139) | copy-start | bytes 196612
  51.6 3.3 %copy-start.4 = (bf16[256,4096]{1,0:T(8,128)(2,1)S(1)}, bf16[256,4096]{1,0:T(8,128)(2,1)}, u32[]{:S(2)}) copy-start(bf16[256,4096]{1,0:T(8,128)(2,1)} %all-gather.3.cloned.1.call-done) | copy-start | bytes 6291460
  51.6 3.4 %copy-start.9 = (bf16[4096,256]{1,0:T(8,128)(2,1)S(1)}, bf16[4096,256]{1,0:T(8,128)(2,1)}, u32[]{:S(2)}) copy-start(bf16[4096,256]{1,0:T(8,128)(2,1)} %param.13) | copy-start | bytes 6291460
  51.6 3.4 %copy-start.23 = (f32[256]{0:T(256)S(1)}, f32[256]{0:T(256)}, u32[]{:S(2)}) copy-start(f32[256]{0:T(256)} %copy-done.22) | copy-start | bytes 3076
  51.7 0.6 copy-start.13
  51.7 0.7 copy-start.15
  55.0 1.3 copy-start.26
  55.0 1.3 copy-start.19
  55.0 3.0 %slice-start = ((s8[8388608]{0:T(1024)(128)(4,1)}), s8[4194304]{0:T(1024)(128)(4,1)S(1)}, s32[]{:S(2)}) async-start(s8[8388608]{0:T(1024)(128)(4,1)} %bitcast.189), calls=%async_computation.3 | async-start | bytes 8388608
  56.3 3.1 %slice-start.1 = ((s8[8388608]{0:T(1024)(128)(4,1)}), s8[4194304]{0:T(1024)(128)(4,1)S(1)}, s32[]{:S(2)}) async-start(s8[8388608]{0:T(1024)(128)(4,1)} %bitcast.189), calls=%async_computation.4 | async-start | bytes 8388608
  66.8 7.4 %collective-permute-start.7 = (bf16[2,256,1024]{2,1,0:T(8,128)(2,1)}, bf16[2,256,1024]{2,1,0:T(8,128)(2,1)}, u32[]{:S(2)}, u32[]{:S(2)}) collective-permute-start(bf16[2,256,1024]{2,1,0:T(8,128)(2,1)} %pad_maximum_fusion), channel_id=1, source_target_pairs={{0,1},{1,0},{2,3},{3,2},{4,5},{5,4},{6,7},{7,6},{8,9},{9,8},{10,11... | collective-permute-start | bytes 3145736 | tf_op jit(solution)/shard_map/ppermute | solution.py:102
  77.5 3.0 %copy-start.16 = (bf16[256,2,64]{2,0,1:T(8,128)(2,1)S(1)}, bf16[256,2,64]{2,0,1:T(8,128)(2,1)}, u32[]{:S(2)}) copy-start(bf16[256,2,64]{2,0,1:T(8,128)(2,1)} %copy-done.15) | copy-start | bytes 196612
  77.5 3.3 %copy-start.14 = (bf16[256,2,64]{2,0,1:T(8,128)(2,1)S(1)}, bf16[256,2,64]{2,0,1:T(8,128)(2,1)}, u32[]{:S(2)}) copy-start(bf16[256,2,64]{2,0,1:T(8,128)(2,1)} %copy-done.13) | copy-start | bytes 196612
  80.0 2.2 %copy-start.2 = (f32[256,4096]{1,0:T(8,128)S(1)}, f32[256,4096]{1,0:T(8,128)}, u32[]{:S(2)}) copy-start(f32[256,4096]{1,0:T(8,128)} %fusion.59) | copy-start | bytes 12582916
  83.4 14.4 %collective-permute-start.8 = (bf16[1,256,1024]{2,1,0:T(8,128)(2,1)S(1)}, bf16[1,256,1024]{2,1,0:T(8,128)(2,1)S(1)}, u32[]{:S(2)}, u32[]{:S(2)}) collective-permute-start(bf16[1,256,1024]{2,1,0:T(8,128)(2,1)S(1)} %fusion.21), channel_id=1, source_target_pairs={{0,2},{1,3},{2,0},{3,1},{4,6},{5,7},{6,4},{7,5},{8,10},{9,11},{10,... | collective-permute-start | bytes 1572872 | tf_op jit(solution)/shard_map/ppermute | solution.py:102
  85.2 5.8 %copy-start.17 = (f32[256,64]{0,1:T(8,128)S(1)}, f32[256,64]{0,1:T(8,128)}, u32[]{:S(2)}) copy-start(f32[256,64]{0,1:T(8,128)} %get-tuple-element.44) | copy-start | bytes 196612
  85.2 5.8 %copy-start.18 = (f32[256,64]{0,1:T(8,128)S(1)}, f32[256,64]{0,1:T(8,128)}, u32[]{:S(2)}) copy-start(f32[256,64]{0,1:T(8,128)} %get-tuple-element.45) | copy-start | bytes 196612
  91.5 1.0 copy-start.8
  91.5 1.8 %copy-start.27 = (f32[2,256,256,4]{2,1,3,0:T(8,128)S(1)}, f32[2,256,256,4]{2,1,3,0:T(8,128)}, u32[]{:S(2)}) copy-start(f32[2,256,256,4]{2,1,3,0:T(8,128)} %copy-done.26) | copy-start | bytes 6291460
  93.3 1.6 %copy-start.10 = (bf16[4096,256]{1,0:T(8,128)(2,1)S(1)}, bf16[4096,256]{1,0:T(8,128)(2,1)}, u32[]{:S(2)}) copy-start(bf16[4096,256]{1,0:T(8,128)(2,1)} %param.13) | copy-start | bytes 6291460
  94.8 3.0 %copy-start.7 = (bf16[256,1024]{1,0:T(8,128)(2,1)S(1)}, bf16[256,1024]{1,0:T(8,128)(2,1)}, u32[]{:S(2)}) copy-start(bf16[256,1024]{1,0:T(8,128)(2,1)} %param.9) | copy-start | bytes 1572868
  95.7 3.7 %copy-start.1 = (f32[256,4096]{1,0:T(8,128)}, f32[256,4096]{1,0:T(8,128)S(1)}, u32[]{:S(2)}) copy-start(f32[256,4096]{1,0:T(8,128)S(1)} %convolution_add_fusion) | copy-start | bytes 12582916
  99.2 0.7 copy-start.25
  99.5 2.9 %collective-permute-start.9 = (bf16[2,256,1024]{2,1,0:T(8,128)(2,1)S(1)}, bf16[2,256,1024]{2,1,0:T(8,128)(2,1)}, u32[]{:S(2)}, u32[]{:S(2)}) collective-permute-start(bf16[2,256,1024]{2,1,0:T(8,128)(2,1)S(1)} %pad_maximum_fusion.1), channel_id=1, source_target_pairs={{0,1},{1,0},{2,3},{3,2},{4,5},{5,4},{6,7},{7,6},{8,9},{9,8},{10,11... | collective-permute-start | bytes 3145736 | tf_op jit(solution)/shard_map/ppermute | solution.py:104
  103.4 22.0 %all-to-all-start = ((bf16[8,32,1024]{2,1,0:T(8,128)(2,1)}), bf16[8,32,1024]{2,1,0:T(8,128)(2,1)S(1)}, u32[]{:S(2)}, u32[]{:S(2)}) async-start(bf16[8,32,1024]{2,1,0:T(8,128)(2,1)} %copy.166), calls=%async_computation | async-start | bytes 1048576 | tf_op jit(solution)/shard_map/all_to_all | solution.py:301
  106.9 3.3 %copy-start.5 = (bf16[256,4096]{1,0:T(8,128)(2,1)S(1)}, bf16[256,4096]{1,0:T(8,128)(2,1)}, u32[]{:S(2)}) copy-start(bf16[256,4096]{1,0:T(8,128)(2,1)} %all-gather.3.cloned.1.call-done) | copy-start | bytes 6291460
  108.6 14.1 %copy-start.6 = (bf16[8,32,1024]{2,1,0:T(8,128)(2,1)S(1)}, bf16[8,32,1024]{2,1,0:T(8,128)(2,1)}, u32[]{:S(2)}) copy-start(bf16[8,32,1024]{2,1,0:T(8,128)(2,1)} %copy.154) | copy-start | bytes 1572868
  108.6 14.1 %dynamic-slice-start = ((f32[4096]{0:T(1024)}, s32[]{:T(128)}), f32[1024]{0:T(1024)S(1)}, s32[]{:S(2)}) async-start(f32[4096]{0:T(1024)} %param.10, s32[]{:T(128)} %select_n.110), calls=%async_computation.5 | async-start | bytes 8704 | tf_op jit(solution)/shard_map/dynamic_slice | solution.py:142
  108.6 14.1 %copy-start.21 = (f32[256]{0:T(256)S(1)}, f32[256]{0:T(256)}, u32[]{:S(2)}) copy-start(f32[256]{0:T(256)} %get-tuple-element.48) | copy-start | bytes 3076
  108.6 14.1 %copy-start.24 = (f32[256]{0:T(256)S(1)}, f32[256]{0:T(256)}, u32[]{:S(2)}) copy-start(f32[256]{0:T(256)} %copy-done.22) | copy-start | bytes 3076
  108.6 14.1 %collective-permute-start.10 = (bf16[1,256,1024]{2,1,0:T(8,128)(2,1)S(1)}, bf16[1,256,1024]{2,1,0:T(8,128)(2,1)S(1)}, u32[]{:S(2)}, u32[]{:S(2)}) collective-permute-start(bf16[1,256,1024]{2,1,0:T(8,128)(2,1)S(1)} %fusion.22), channel_id=1, source_target_pairs={{0,2},{1,3},{2,0},{3,1},{4,6},{5,7},{6,4},{7,5},{8,10},{9,11},{10,... | collective-permute-start | bytes 1572872 | tf_op jit(solution)/shard_map/ppermute | solution.py:104
  113.0 1.2 collective-permute-start.11
  114.2 8.5 %collective-permute-start.12 = (f32[256]{0:T(256)S(1)}, f32[256]{0:T(256)S(1)}, u32[]{:S(2)}, u32[]{:S(2)}) collective-permute-start(f32[256]{0:T(256)S(1)} %add.200), channel_id=1, source_target_pairs={{0,2},{1,3},{2,0},{3,1},{4,6},{5,7},{6,4},{7,5},{8,10},{9,11},{10,... | collective-permute-start | bytes 3080 | tf_op jit(solution)/shard_map/ppermute | solution.py:104
Sparse Core Ops, SparseCore 0:
  9.6 25.2 all-gather.2
  37.0 22.0 all-gather.4

commit v24 on v23

--- a/solution.py
+++ b/solution.py
@@ -103,6 +103,10 @@
         else:
             incoming, extra_in = lax.ppermute((outgoing, extra), axis_name, _xor_pairs(size, bit))
             extra = extra + extra_in
+            if ties and bit == 1:
+                extra, first = lax.optimization_barrier((extra, ties[0]))
+                ties = ties[1:]
+                done_ties.append(first)
         if ties:
             incoming, first = lax.optimization_barrier((incoming, ties[0]))
             ties = ties[1:]

time: 134 us -> 138 us (1.030)
  waiting for transfers between devices: 17.3 us -> 19.3 us
  local copies, waits for them, and re-layouts: 23.3 us -> 24.8 us
    reduce_sum x1, other arithmetic: 2.82 us -> 0.63 us  [per_device(): jnp.sum(normed_partial * norm_gain[None, :] * gathered_float, axis=1)]
    ppermute x4, waiting for transfers between devices: 11.2 us -> 13.2 us  [scatter_features(): lax.ppermute((outgoing, extra), axis_name, _xor_pairs(size, bit))]
    unnamed x64, local copies, waits for them, and re-layouts: 7.69 us -> 9.13 us
    optimization_barrier x2 -> x1, local copies, waits for them, and re-layouts: 3.13 us -> 2.04 us  [scatter_features(): incoming, first = lax.optimization_barrier((incoming, ties[0]))]
  transfers between devices with their start and end apart: 16 -> 16, of which waited for: 6 -> 5; matrix products, arithmetic and copies ran while one was open for 45% -> 42% of each run, Pallas kernels for 0% -> 0%
where the time goes in v24:
time: 138 us; the launch traced here: 137 us
  matrix products  38.5 us (28%)
  local copies, waits for them, and re-layouts  24.8 us (18%)
  starting transfers between devices  20.4 us (15%)
  waiting for transfers between devices  19.3 us (14%)
  other arithmetic  18.8 us (14%)
  between operations  14.8 us (11%)
    ppermute x4, waiting for transfers between devices, scatter_features(): lax.ppermute((outgoing, extra), axis_name, _xor_pairs(size, bit))  13.2 us
    ppermute x7, starting transfers between devices, per_device(): returned.append(lax.ppermute(piece, 'dp', pairs))  12.5 us
    unnamed x64, local copies, waits for them, and re-layouts  9.13 us
    dot_general x1, matrix products, per_device(): jnp.dot(normed_input, w_query, preferred_element_type=jnp.float32)  8.16 us
    dot_general x1, matrix products, per_device(): lax.dot_general(w_out, grad_full, (((1,), (1,)), ((), ())), preferred_ele...  7.42 us
    dot_general x1, matrix products, per_device(): lax.dot_general(grad_query.reshape(token_row_count, query_width), w_query...  5.81 us
    another operation x8, local copies, waits for them, and re-layouts, per_device(): returned = jnp.stack(returned)  4.91 us
    dot_general x1, matrix products, per_device(): jnp.dot(attended_flat, w_out, preferred_element_type=jnp.float32)  4.53 us
  transfers between devices with their start and end apart: 16, of which 5 were waited for; matrix products, arithmetic and copies ran while one was open for 42% of the time, Pallas kernels for 0%

profile of v24, /device:TPU:0, one launch (start us, length us, event | category | flops | bytes accessed | tf_op | source)
XLA Modules:
  0.0 136.5 jit_solution(1679282058693642639)
XLA Ops:
  7.2 0.7 all-gather.3.cloned.1.call-update
  8.1 1.1 dynamic-slice_bitcast_fusion
  9.2 6.0 %collective-permute-start.6 = (bf16[32,1024]{1,0:T(8,128)(2,1)S(1)}, bf16[32,1024]{1,0:T(8,128)(2,1)S(1)}, u32[]{:S(2)}, u32[]{:S(2)}) collective-permute-start(bf16[32,1024]{1,0:T(8,128)(2,1)S(1)} %get-tuple-element.32), channel_id=1, source_target_pairs={{0,28},{4,0},{8,4},{12,8},{16,12},{20,16},{24,20},{28,24},{1,29},{... | collective-permute-start | bytes 196616 | tf_op jit(solution)/shard_map/ppermute | solution.py:163
  15.2 0.4 collective-permute-start.5
  15.7 3.0 %collective-permute-start.3 = (bf16[32,1024]{1,0:T(8,128)(2,1)S(1)}, bf16[32,1024]{1,0:T(8,128)(2,1)S(1)}, u32[]{:S(2)}, u32[]{:S(2)}) collective-permute-start(bf16[32,1024]{1,0:T(8,128)(2,1)S(1)} %get-tuple-element.35), channel_id=1, source_target_pairs={{0,16},{4,20},{8,24},{12,28},{16,0},{20,4},{24,8},{28,12},{1,17},{... | collective-permute-start | bytes 196616 | tf_op jit(solution)/shard_map/ppermute | solution.py:163
  18.7 0.8 reduce-window.8
  19.6 1.0 broadcast_multiply_fusion.1
  20.6 0.7 fusion.34
  21.3 0.7 copy.141
  22.0 0.8 copy.139
  22.9 1.9 %collective-permute-start.1 = (bf16[32,1024]{1,0:T(8,128)(2,1)S(1)}, bf16[32,1024]{1,0:T(8,128)(2,1)S(1)}, u32[]{:S(2)}, u32[]{:S(2)}) collective-permute-start(bf16[32,1024]{1,0:T(8,128)(2,1)S(1)} %get-tuple-element.37), channel_id=1, source_target_pairs={{0,8},{4,12},{8,16},{12,20},{16,24},{20,28},{24,0},{28,4},{1,9},{5... | collective-permute-start | bytes 196616 | tf_op jit(solution)/shard_map/ppermute | solution.py:163
  24.8 1.1 collective-permute-start
  25.9 1.3 and_select_fusion
  27.8 2.2 %collective-permute-done.1 = bf16[32,1024]{1,0:T(8,128)(2,1)S(1)} collective-permute-done((bf16[32,1024]{1,0:T(8,128)(2,1)S(1)}, bf16[32,1024]{1,0:T(8,128)(2,1)S(1)}, u32[]{:S(2)}, u32[]{:S(2)}) %collective-permute-start.1) | collective-permute-done | bytes 65568 | tf_op jit(solution)/shard_map/ppermute | solution.py:163
  30.0 0.8 copy.148
  30.7 1.0 collective-permute-done
  31.8 0.8 copy.147
  32.5 2.9 %stack.58 = bf16[8,32,1024]{2,0,1:T(8,128)(2,1)S(1)} concatenate(bf16[1,32,1024]{2,0,1:T(2,128)(2,1)S(1)} %copy.191, bf16[1,32,1024]{2,0,1:T(2,128)(2,1)} %copy.147, bf16[1,32,1024]{2,0,1:T(2,128)(2,1)} %copy.148, bf16[1,32,1024]{2,0,1:T(2,128)(2,1)S(1)} %copy.149, bf16[1,32,1024]{2,0,1:T(2,128)(2,1)S(1)} %copy.150, bf16[1,32,1024]{2,0,1:T(2,128)(2,1)S(1)} %copy.151, ...), dimensions={0} | concatenate | bytes 1048576 | tf_op jit(solution)/shard_map/stack | solution.py:164
  35.8 1.1 copy.154
  37.0 2.2 %fusion = f32[256]{0:T(256)S(1)} fusion(bf16[256,4096]{1,0:T(8,128)(2,1)} %all-gather.3.cloned.1.call-done), kind=kLoop, calls=%fused_computation.5 | loop fusion | flops 3145472 | bytes 2098176 | tf_op jit(solution)/shard_map/reduce_sum | solution.py:187
  39.2 0.6 multiply_multiply_fusion
  39.8 1.2 fusion.52
  41.3 8.2 %fusion.50 = f32[256,1024]{0,1:T(8,128)S(1)} fusion(bf16[4096,1024]{1,0:T(8,128)(2,1)} %param.11, bf16[256,4096]{1,0:T(8,128)(2,1)} %all-gather.3.cloned.1.call-done, f32[4096]{0:T(1024)S(1)} %copy-done.20, f32[256]{0:T(256)S(1)} %get-tuple-element.49), kind=kOutput, calls=%fused_computation.121 | convolution fusion | flops 2151677952 | bytes 11551744 | tf_op jit(solution)/shard_map/dot_general | solution.py:189
  49.6 1.0 copy.144
  50.6 1.0 copy.143
  51.7 0.6 copy-done.13
  52.4 2.5 %fusion.7 = (f32[2,4,256]{2,1,0:T(4,128)S(1)}, f32[2,256,256,4]{2,1,3,0:T(8,128)S(1)}) fusion(pred[256,256]{0,1:T(8,128)(4,1)} %fusion.34, bf16[256,2,4,64]{3,0,2,1:T(8,128)(2,1)} %copy.144, bf16[256,2,4,64]{3,0,2,1:T(8,128)(2,1)} %copy.143, bf16[256,2,64]{2,0,1:T(8,128)(2,1)S(1)} %get-tuple-element.31, bf16[256,2,64]{2,0,1:T(8,128)(2,1)S(1)} %get-tuple-element.30), kind=kOutput, calls=%fused_computation.14 | convolution fusion | flops 137099264 | bytes 2826240 | tf_op jit(solution)/shard_map/qkgd,skd->kgqs/dot_general | solution.py:207
  55.0 1.2 convolution_convert_fusion.4
  56.3 0.7 convolution_convert_fusion.1
  57.0 1.0 slice-done
  58.0 1.4 %slice-done.1 = s8[4194304]{0:T(1024)(128)(4,1)S(1)} async-done(((s8[8388608]{0:T(1024)(128)(4,1)}), s8[4194304]{0:T(1024)(128)(4,1)S(1)}, s32[]{:S(2)}) %slice-start.1) | async-done | bytes 4194328
  59.4 4.5 %fusion.59 = f32[256,4096]{1,0:T(8,128)} fusion(bf16[256,1024]{0,1:T(8,128)(2,1)S(1)} %bitcast.196, bf16[1024,4096]{1,0:T(8,128)(2,1)S(1)} %bitcast.194), kind=kOutput, calls=%fused_computation.124 | convolution fusion | flops 2147483648 | bytes 13107200 | tf_op jit(solution)/shard_map/dot_general | solution.py:217
  64.0 1.7 %fusion.17 = (bf16[1,256,1024]{2,1,0:T(8,128)(2,1)S(1)}, bf16[1,256,1024]{2,1,0:T(8,128)(2,1)S(1)}) fusion(f32[256,4096]{1,0:T(8,128)} %fusion.59, s32[]{:T(128)S(6)} %select_n.111, s32[]{:T(128)S(6)} %select_n.112), kind=kLoop, calls=%fused_computation.49 | loop fusion | bytes 2097160 | tf_op jit(solution)/shard_map/stack | solution.py:100
  65.7 1.1 pad_maximum_fusion
  66.8 7.4 %convolution_convert_fusion = bf16[256,1024]{1,0:T(8,128)(2,1)} fusion(bf16[256,4096]{1,0:T(8,128)(2,1)} %all-gather.5.cloned.1.call-done, bf16[1024,4096]{1,0:T(8,128)(2,1)} %param.14), kind=kOutput, calls=%fused_computation.17 | convolution fusion | flops 2147745792 | bytes 11010048 | tf_op jit(solution)/shard_map/dot_general | solution.py:221
  74.2 2.0 %copy.155 = bf16[256,1024]{0,1:T(8,128)(2,1)} copy(bf16[256,1024]{1,0:T(8,128)(2,1)} %convolution_convert_fusion) | data formatting | bytes 1048576 | tf_op jit(solution)/shard_map/optimization_barrier | solution.py:111
  76.3 1.2 multiply_reduce_fusion
  77.5 2.5 %fusion.5 = bf16[2,4,256,256]{2,3,1,0:T(8,128)(2,1)S(1)} fusion(bf16[256,2,128,1]{0,2,3,1:T(8,128)(2,1)S(1)} %bitcast.221, bf16[256,2,4,128]{0,3,2,1:T(8,128)(2,1)} %bitcast.201, f32[2,4,256]{2,1,0:T(4,128)S(1)} %bitcast.217, f32[2,4,256]{2,1,0:T(4,128)S(1)} %get-tuple-element.50, f32[2,256,256,4]{2,1,3,0:T(8,128)} %copy-done.26, ...), kind=kOutput, calls=%fused_computation.11 | convolution fusion | flops 137363456 | bytes 3883008 | tf_op jit(solution)/shard_map/qkgd,skd->kgqs/dot_general | solution.py:238
  80.0 0.4 convolution_bitcast_fusion.2
  81.2 1.0 copy-done.2
  82.2 1.2 fusion.21
  83.4 1.6 %collective-permute-start.8 = (bf16[1,256,1024]{2,1,0:T(8,128)(2,1)S(1)}, bf16[1,256,1024]{2,1,0:T(8,128)(2,1)S(1)}, u32[]{:S(2)}, u32[]{:S(2)}) collective-permute-start(bf16[1,256,1024]{2,1,0:T(8,128)(2,1)S(1)} %fusion.21), channel_id=1, source_target_pairs={{0,2},{1,3},{2,0},{3,1},{4,6},{5,7},{6,4},{7,5},{8,10},{9,11},{10,... | collective-permute-start | bytes 1572872 | tf_op jit(solution)/shard_map/ppermute | solution.py:102
  85.2 5.8 %fusion.60 = f32[256,4096]{1,0:T(8,128)S(1)} fusion(bf16[256,1024]{0,1:T(8,128)(2,1)S(1)} %bitcast.206, bf16[4096,1024]{1,0:T(8,128)(2,1)} %param.11), kind=kOutput, calls=%fused_computation.125 | convolution fusion | flops 2147483648 | bytes 13107200 | tf_op jit(solution)/shard_map/dot_general | solution.py:277
  91.0 0.4 add_convert_fusion.2
  91.5 0.8 convolution_add_fusion.1
  92.5 0.7 copy-done.27
  93.3 0.6 fusion.8
  93.9 0.9 copy-done.10
  94.8 0.8 convolution_add_fusion
  95.6 2.2 %collective-permute-done.8 = bf16[1,256,1024]{2,1,0:T(8,128)(2,1)S(1)} collective-permute-done((bf16[1,256,1024]{2,1,0:T(8,128)(2,1)S(1)}, bf16[1,256,1024]{2,1,0:T(8,128)(2,1)S(1)}, u32[]{:S(2)}, u32[]{:S(2)}) %collective-permute-start.8) | collective-permute-done | bytes 524320 | tf_op jit(solution)/shard_map/ppermute | solution.py:102
  97.8 1.4 fusion.9
  99.3 1.1 pad_maximum_fusion.1
  100.5 0.6 copy-done.5
  101.1 0.6 fusion.3
  101.8 0.4 convolution_convert_fusion.2
  102.2 0.9 collective-permute-done.9
  103.1 1.1 copy.166
  104.2 4.1 %all-to-all-start = ((bf16[8,32,1024]{2,1,0:T(8,128)(2,1)}), bf16[8,32,1024]{2,1,0:T(8,128)(2,1)}, u32[]{:S(2)}, u32[]{:S(2)}) async-start(bf16[8,32,1024]{2,1,0:T(8,128)(2,1)} %copy.166), calls=%async_computation | async-start | bytes 1048576 | tf_op jit(solution)/shard_map/all_to_all | solution.py:305
  108.4 2.3 %fusion.22 = bf16[1,256,1024]{2,1,0:T(8,128)(2,1)} fusion(f32[256,4096]{1,0:T(8,128)} %copy-done.1, s32[]{:T(128)S(6)} %select_n.113, bf16[2,256,1024]{2,1,0:T(8,128)(2,1)} %collective-permute-done.10), kind=kLoop, calls=%fused_computation.54 | loop fusion | flops 786432 | bytes 2097156 | tf_op jit(solution)/shard_map/convert_element_type | solution.py:100
  110.7 1.5 %collective-permute-start.11 = (bf16[1,256,1024]{2,1,0:T(8,128)(2,1)}, bf16[1,256,1024]{2,1,0:T(8,128)(2,1)}, u32[]{:S(2)}, u32[]{:S(2)}) collective-permute-start(bf16[1,256,1024]{2,1,0:T(8,128)(2,1)} %fusion.22), channel_id=1, source_target_pairs={{0,2},{1,3},{2,0},{3,1},{4,6},{5,7},{6,4},{7,5},{8,10},{9,11},{10,... | collective-permute-start | bytes 1572872 | tf_op jit(solution)/shard_map/ppermute | solution.py:104
  112.2 0.5 collective-permute-start.12
  112.7 12.3 %collective-permute-done.12 = f32[256]{0:T(256)S(1)} collective-permute-done((f32[256]{0:T(256)S(1)}, f32[256]{0:T(256)S(1)}, u32[]{:S(2)}, u32[]{:S(2)}) %collective-permute-start.12) | collective-permute-done | bytes 1056 | tf_op jit(solution)/shard_map/ppermute | solution.py:104
  125.1 2.8 %fusion.12 = bf16[256,1024]{1,0:T(8,128)(2,1)} fusion(bf16[256,1024]{1,0:T(8,128)(2,1)S(1)} %copy-done.7, f32[256,4096]{1,0:T(8,128)} %copy-done.1, s32[]{:T(128)} %select_n.110, bf16[2,256,1024]{2,1,0:T(8,128)(2,1)} %collective-permute-done.10, bf16[1,256,1024]{2,1,0:T(8,128)(2,1)} %collective-permute-done.11, f32[256]{0:T(256)S(1)} %add_multiply_fusion, ...), kind=kLoop, calls=%fused_computation.31 | loop fusion | flops 3407872 | bytes 3677188 | tf_op jit(solution)/shard_map/convert_element_type | solution.py:315
  127.8 1.9 %copy.195 = bf16[256,1024]{1,0:T(8,128)(2,1)} copy(bf16[256,1024]{1,0:T(8,128)(2,1)} %bitcast.66) | data formatting | bytes 1048576
  (98 shorter events, 3.3 us)
Async XLA Ops:
  7.2 32.6 %copy-start = (bf16[4096,256]{1,0:T(8,128)(2,1)S(1)}, bf16[4096,256]{1,0:T(8,128)(2,1)}, u32[]{:S(2)}) copy-start(bf16[4096,256]{1,0:T(8,128)(2,1)} %param.12) | copy-start | bytes 6291460
  7.2 29.8 %all-gather.3.cloned.1.call-start = ((), (), s32[]{:S(2)}) async-start(), calls=%async_computation.1 | async-start | bytes 2621440 | tf_op jit(solution)/shard_map/all_gather | solution.py:185
  7.9 56.1 %all-gather.5.cloned.1.call-start = ((), (), s32[]{:S(2)}) async-start(), calls=%async_computation.2 | async-start | bytes 2621440 | tf_op jit(solution)/shard_map/all_gather | solution.py:218
  9.2 13.7 %collective-permute-start.6 = (bf16[32,1024]{1,0:T(8,128)(2,1)S(1)}, bf16[32,1024]{1,0:T(8,128)(2,1)S(1)}, u32[]{:S(2)}, u32[]{:S(2)}) collective-permute-start(bf16[32,1024]{1,0:T(8,128)(2,1)S(1)} %get-tuple-element.32), channel_id=1, source_target_pairs={{0,28},{4,0},{8,4},{12,8},{16,12},{20,16},{24,20},{28,24},{1,29},{... | collective-permute-start | bytes 196616 | tf_op jit(solution)/shard_map/ppermute | solution.py:163
  15.2 9.6 %collective-permute-start.5 = (bf16[32,1024]{1,0:T(8,128)(2,1)S(1)}, bf16[32,1024]{1,0:T(8,128)(2,1)S(1)}, u32[]{:S(2)}, u32[]{:S(2)}) collective-permute-start(bf16[32,1024]{1,0:T(8,128)(2,1)S(1)} %get-tuple-element.33), channel_id=1, source_target_pairs={{0,24},{4,28},{8,0},{12,4},{16,8},{20,12},{24,16},{28,20},{1,25},{... | collective-permute-start | bytes 196616 | tf_op jit(solution)/shard_map/ppermute | solution.py:163
  15.7 11.8 %collective-permute-start.4 = (bf16[32,1024]{1,0:T(8,128)(2,1)S(1)}, bf16[32,1024]{1,0:T(8,128)(2,1)S(1)}, u32[]{:S(2)}, u32[]{:S(2)}) collective-permute-start(bf16[32,1024]{1,0:T(8,128)(2,1)S(1)} %get-tuple-element.34), channel_id=1, source_target_pairs={{0,20},{4,24},{8,28},{12,0},{16,4},{20,8},{24,12},{28,16},{1,21},{... | collective-permute-start | bytes 196616 | tf_op jit(solution)/shard_map/ppermute | solution.py:163
  15.7 11.9 %collective-permute-start.3 = (bf16[32,1024]{1,0:T(8,128)(2,1)S(1)}, bf16[32,1024]{1,0:T(8,128)(2,1)S(1)}, u32[]{:S(2)}, u32[]{:S(2)}) collective-permute-start(bf16[32,1024]{1,0:T(8,128)(2,1)S(1)} %get-tuple-element.35), channel_id=1, source_target_pairs={{0,16},{4,20},{8,24},{12,28},{16,0},{20,4},{24,8},{28,12},{1,17},{... | collective-permute-start | bytes 196616 | tf_op jit(solution)/shard_map/ppermute | solution.py:163
  18.7 9.0 %collective-permute-start.2 = (bf16[32,1024]{1,0:T(8,128)(2,1)S(1)}, bf16[32,1024]{1,0:T(8,128)(2,1)S(1)}, u32[]{:S(2)}, u32[]{:S(2)}) collective-permute-start(bf16[32,1024]{1,0:T(8,128)(2,1)S(1)} %get-tuple-element.36), channel_id=1, source_target_pairs={{0,12},{4,16},{8,20},{12,24},{16,28},{20,0},{24,4},{28,8},{1,13},{... | collective-permute-start | bytes 196616 | tf_op jit(solution)/shard_map/ppermute | solution.py:163
  22.9 7.1 %collective-permute-start.1 = (bf16[32,1024]{1,0:T(8,128)(2,1)S(1)}, bf16[32,1024]{1,0:T(8,128)(2,1)S(1)}, u32[]{:S(2)}, u32[]{:S(2)}) collective-permute-start(bf16[32,1024]{1,0:T(8,128)(2,1)S(1)} %get-tuple-element.37), channel_id=1, source_target_pairs={{0,8},{4,12},{8,16},{12,20},{16,24},{20,28},{24,0},{28,4},{1,9},{5... | collective-permute-start | bytes 196616 | tf_op jit(solution)/shard_map/ppermute | solution.py:163
  24.8 7.0 %collective-permute-start = (bf16[32,1024]{1,0:T(8,128)(2,1)S(1)}, bf16[32,1024]{1,0:T(8,128)(2,1)S(1)}, u32[]{:S(2)}, u32[]{:S(2)}) collective-permute-start(bf16[32,1024]{1,0:T(8,128)(2,1)S(1)} %get-tuple-element.38), channel_id=1, source_target_pairs={{0,4},{4,8},{8,12},{12,16},{16,20},{20,24},{24,28},{28,0},{1,5},{5... | collective-permute-start | bytes 196616 | tf_op jit(solution)/shard_map/ppermute | solution.py:163
  35.8 4.0 %copy-start.20 = (f32[4096]{0:T(1024)S(1)}, f32[4096]{0:T(1024)}, u32[]{:S(2)}) copy-start(f32[4096]{0:T(1024)} %param.10) | copy-start | bytes 49156
  36.9 2.8 %copy-start.3 = (bf16[256,4096]{1,0:T(8,128)(2,1)S(1)}, bf16[256,4096]{1,0:T(8,128)(2,1)}, u32[]{:S(2)}) copy-start(bf16[256,4096]{1,0:T(8,128)(2,1)} %all-gather.3.cloned.1.call-done) | copy-start | bytes 6291460
  39.8 1.5 %copy-start.22 = (f32[256]{0:T(256)}, f32[256]{0:T(256)S(1)}, u32[]{:S(2)}) copy-start(f32[256]{0:T(256)S(1)} %get-tuple-element.49) | copy-start | bytes 3076
  49.4 2.2 %copy-start.11 = (f32[256,64]{1,0:T(8,128)S(1)}, f32[256,64]{1,0:T(8,128)}, u32[]{:S(2)}) copy-start(f32[256,64]{1,0:T(8,128)} %copy.141) | copy-start | bytes 196612
  49.4 2.2 %copy-start.12 = (f32[256,64]{1,0:T(8,128)S(1)}, f32[256,64]{1,0:T(8,128)}, u32[]{:S(2)}) copy-start(f32[256,64]{1,0:T(8,128)} %copy.139) | copy-start | bytes 196612
  51.6 3.3 %copy-start.4 = (bf16[256,4096]{1,0:T(8,128)(2,1)S(1)}, bf16[256,4096]{1,0:T(8,128)(2,1)}, u32[]{:S(2)}) copy-start(bf16[256,4096]{1,0:T(8,128)(2,1)} %all-gather.3.cloned.1.call-done) | copy-start | bytes 6291460
  51.6 3.4 %copy-start.9 = (bf16[4096,256]{1,0:T(8,128)(2,1)S(1)}, bf16[4096,256]{1,0:T(8,128)(2,1)}, u32[]{:S(2)}) copy-start(bf16[4096,256]{1,0:T(8,128)(2,1)} %param.13) | copy-start | bytes 6291460
  51.6 3.4 %copy-start.23 = (f32[256]{0:T(256)S(1)}, f32[256]{0:T(256)}, u32[]{:S(2)}) copy-start(f32[256]{0:T(256)} %copy-done.22) | copy-start | bytes 3076
  51.7 0.6 copy-start.13
  51.7 0.7 copy-start.15
  55.0 1.3 copy-start.26
  55.0 1.3 copy-start.19
  55.0 3.0 %slice-start = ((s8[8388608]{0:T(1024)(128)(4,1)}), s8[4194304]{0:T(1024)(128)(4,1)S(1)}, s32[]{:S(2)}) async-start(s8[8388608]{0:T(1024)(128)(4,1)} %bitcast.193), calls=%async_computation.3 | async-start | bytes 8388608
  56.3 3.1 %slice-start.1 = ((s8[8388608]{0:T(1024)(128)(4,1)}), s8[4194304]{0:T(1024)(128)(4,1)S(1)}, s32[]{:S(2)}) async-start(s8[8388608]{0:T(1024)(128)(4,1)} %bitcast.193), calls=%async_computation.4 | async-start | bytes 8388608
  66.8 7.4 %collective-permute-start.7 = (bf16[2,256,1024]{2,1,0:T(8,128)(2,1)}, bf16[2,256,1024]{2,1,0:T(8,128)(2,1)}, u32[]{:S(2)}, u32[]{:S(2)}) collective-permute-start(bf16[2,256,1024]{2,1,0:T(8,128)(2,1)} %pad_maximum_fusion), channel_id=1, source_target_pairs={{0,1},{1,0},{2,3},{3,2},{4,5},{5,4},{6,7},{7,6},{8,9},{9,8},{10,11... | collective-permute-start | bytes 3145736 | tf_op jit(solution)/shard_map/ppermute | solution.py:102
  77.5 3.0 %copy-start.16 = (bf16[256,2,64]{2,0,1:T(8,128)(2,1)S(1)}, bf16[256,2,64]{2,0,1:T(8,128)(2,1)}, u32[]{:S(2)}) copy-start(bf16[256,2,64]{2,0,1:T(8,128)(2,1)} %copy-done.15) | copy-start | bytes 196612
  77.5 3.3 %copy-start.14 = (bf16[256,2,64]{2,0,1:T(8,128)(2,1)S(1)}, bf16[256,2,64]{2,0,1:T(8,128)(2,1)}, u32[]{:S(2)}) copy-start(bf16[256,2,64]{2,0,1:T(8,128)(2,1)} %copy-done.13) | copy-start | bytes 196612
  80.0 2.2 %copy-start.2 = (f32[256,4096]{1,0:T(8,128)S(1)}, f32[256,4096]{1,0:T(8,128)}, u32[]{:S(2)}) copy-start(f32[256,4096]{1,0:T(8,128)} %fusion.59) | copy-start | bytes 12582916
  83.4 14.4 %collective-permute-start.8 = (bf16[1,256,1024]{2,1,0:T(8,128)(2,1)S(1)}, bf16[1,256,1024]{2,1,0:T(8,128)(2,1)S(1)}, u32[]{:S(2)}, u32[]{:S(2)}) collective-permute-start(bf16[1,256,1024]{2,1,0:T(8,128)(2,1)S(1)} %fusion.21), channel_id=1, source_target_pairs={{0,2},{1,3},{2,0},{3,1},{4,6},{5,7},{6,4},{7,5},{8,10},{9,11},{10,... | collective-permute-start | bytes 1572872 | tf_op jit(solution)/shard_map/ppermute | solution.py:102
  85.2 5.8 %copy-start.17 = (f32[256,64]{0,1:T(8,128)S(1)}, f32[256,64]{0,1:T(8,128)}, u32[]{:S(2)}) copy-start(f32[256,64]{0,1:T(8,128)} %get-tuple-element.44) | copy-start | bytes 196612
  85.2 5.8 %copy-start.18 = (f32[256,64]{0,1:T(8,128)S(1)}, f32[256,64]{0,1:T(8,128)}, u32[]{:S(2)}) copy-start(f32[256,64]{0,1:T(8,128)} %get-tuple-element.45) | copy-start | bytes 196612
  91.5 1.0 copy-start.8
  91.5 1.8 %copy-start.27 = (f32[2,256,256,4]{2,1,3,0:T(8,128)S(1)}, f32[2,256,256,4]{2,1,3,0:T(8,128)}, u32[]{:S(2)}) copy-start(f32[2,256,256,4]{2,1,3,0:T(8,128)} %copy-done.26) | copy-start | bytes 6291460
  93.3 1.6 %copy-start.10 = (bf16[4096,256]{1,0:T(8,128)(2,1)S(1)}, bf16[4096,256]{1,0:T(8,128)(2,1)}, u32[]{:S(2)}) copy-start(bf16[4096,256]{1,0:T(8,128)(2,1)} %param.13) | copy-start | bytes 6291460
  94.8 3.0 %copy-start.7 = (bf16[256,1024]{1,0:T(8,128)(2,1)S(1)}, bf16[256,1024]{1,0:T(8,128)(2,1)}, u32[]{:S(2)}) copy-start(bf16[256,1024]{1,0:T(8,128)(2,1)} %param.9) | copy-start | bytes 1572868
  95.6 4.9 %copy-start.1 = (f32[256,4096]{1,0:T(8,128)}, f32[256,4096]{1,0:T(8,128)S(1)}, u32[]{:S(2)}) copy-start(f32[256,4096]{1,0:T(8,128)S(1)} %convolution_add_fusion) | copy-start | bytes 12582916
  99.2 2.0 %copy-start.5 = (bf16[256,4096]{1,0:T(8,128)(2,1)S(1)}, bf16[256,4096]{1,0:T(8,128)(2,1)}, u32[]{:S(2)}) copy-start(bf16[256,4096]{1,0:T(8,128)(2,1)} %all-gather.3.cloned.1.call-done) | copy-start | bytes 6291460
  100.5 1.4 copy-start.25
  100.5 7.9 %collective-permute-start.10 = (bf16[2,256,1024]{2,1,0:T(8,128)(2,1)}, bf16[2,256,1024]{2,1,0:T(8,128)(2,1)}, u32[]{:S(2)}, u32[]{:S(2)}) collective-permute-start(bf16[2,256,1024]{2,1,0:T(8,128)(2,1)} %pad_maximum_fusion.1), channel_id=1, source_target_pairs={{0,1},{1,0},{2,3},{3,2},{4,5},{5,4},{6,7},{7,6},{8,9},{9,8},{10,11... | collective-permute-start | bytes 3145736 | tf_op jit(solution)/shard_map/ppermute | solution.py:104
  101.8 1.4 collective-permute-start.9
  103.1 21.9 %copy-start.6 = (bf16[8,32,1024]{2,1,0:T(8,128)(2,1)S(1)}, bf16[8,32,1024]{2,1,0:T(8,128)(2,1)}, u32[]{:S(2)}) copy-start(bf16[8,32,1024]{2,1,0:T(8,128)(2,1)} %copy.154) | copy-start | bytes 1572868
  103.1 21.9 %dynamic-slice-start = ((f32[4096]{0:T(1024)}, s32[]{:T(128)}), f32[1024]{0:T(1024)S(1)}, s32[]{:S(2)}) async-start(f32[4096]{0:T(1024)} %param.10, s32[]{:T(128)} %select_n.110), calls=%async_computation.5 | async-start | bytes 8704 | tf_op jit(solution)/shard_map/dynamic_slice | solution.py:146
  103.1 21.9 %copy-start.21 = (f32[256]{0:T(256)S(1)}, f32[256]{0:T(256)}, u32[]{:S(2)}) copy-start(f32[256]{0:T(256)} %get-tuple-element.48) | copy-start | bytes 3076
  103.1 21.9 %copy-start.24 = (f32[256]{0:T(256)S(1)}, f32[256]{0:T(256)}, u32[]{:S(2)}) copy-start(f32[256]{0:T(256)} %copy-done.22) | copy-start | bytes 3076
  104.2 20.8 %all-to-all-start = ((bf16[8,32,1024]{2,1,0:T(8,128)(2,1)}), bf16[8,32,1024]{2,1,0:T(8,128)(2,1)}, u32[]{:S(2)}, u32[]{:S(2)}) async-start(bf16[8,32,1024]{2,1,0:T(8,128)(2,1)} %copy.166), calls=%async_computation | async-start | bytes 1048576 | tf_op jit(solution)/shard_map/all_to_all | solution.py:305
  110.7 14.3 %collective-permute-start.11 = (bf16[1,256,1024]{2,1,0:T(8,128)(2,1)}, bf16[1,256,1024]{2,1,0:T(8,128)(2,1)}, u32[]{:S(2)}, u32[]{:S(2)}) collective-permute-start(bf16[1,256,1024]{2,1,0:T(8,128)(2,1)} %fusion.22), channel_id=1, source_target_pairs={{0,2},{1,3},{2,0},{3,1},{4,6},{5,7},{6,4},{7,5},{8,10},{9,11},{10,... | collective-permute-start | bytes 1572872 | tf_op jit(solution)/shard_map/ppermute | solution.py:104
  112.2 12.8 %collective-permute-start.12 = (f32[256]{0:T(256)S(1)}, f32[256]{0:T(256)S(1)}, u32[]{:S(2)}, u32[]{:S(2)}) collective-permute-start(f32[256]{0:T(256)S(1)} %add.196), channel_id=1, source_target_pairs={{0,2},{1,3},{2,0},{3,1},{4,6},{5,7},{6,4},{7,5},{8,10},{9,11},{10,... | collective-permute-start | bytes 3080 | tf_op jit(solution)/shard_map/ppermute | solution.py:104
Sparse Core Ops, SparseCore 0:
  9.6 25.2 all-gather.2
  37.0 22.0 all-gather.4

commit v25 on v23

--- a/solution.py
+++ b/solution.py
@@ -78,7 +78,7 @@
     return jnp.concatenate(blocks, axis=1)
 
 
-def scatter_features(partial, axis_name, size, position, extra=None, ties=()):
+def scatter_features(partial, axis_name, size, position, extra=None, ties=(), split_last=False):
     width = partial.shape[1] // size
     if not _is_pow2(size):
         summed = lax.psum_scatter(
@@ -86,7 +86,10 @@
         )
         if extra is not None:
             extra = lax.psum(extra, axis_name)
-        return summed.astype(jnp.float32), extra, ties
+        summed = summed.astype(jnp.float32)
+        if split_last:
+            summed = (summed, jnp.zeros(summed.shape, jnp.bfloat16))
+        return summed, extra, ties
     held = [
         lax.dynamic_slice_in_dim(partial, (position ^ m) * width, width, axis=1)
         for m in range(size)
@@ -108,6 +111,9 @@
             ties = ties[1:]
             done_ties.append(first)
         sent_masks = [masks[i] ^ bit for i in send]
+        if split_last and bit * 2 >= size:
+            own = held[keep[0]]
+            return (own, incoming[0]), extra, tuple(done_ties) + tuple(ties)
         held = [
             held[i] + incoming[sent_masks.index(masks[i])].astype(jnp.float32) for i in keep
         ]
@@ -296,16 +302,26 @@
         "dj,jrw->drw", send_table, home_blocks, preferred_element_type=jnp.float32
     ).astype(jnp.bfloat16)
     normed_gradient, stat_sum, (outgoing,) = scatter_features(
-        normed_partial, "tensor", tensor_size, tensor_index, extra=stat_partial, ties=(outgoing,)
+        normed_partial,
+        "tensor",
+        tensor_size,
+        tensor_index,
+        extra=stat_partial,
+        ties=(outgoing,),
+        split_last=True,
     )
     relaid = lax.all_to_all(outgoing, "dp", split_axis=0, concat_axis=0, tiled=True).reshape(
         token_row_count, width_part
     )
     stat = stat_sum / full_width
     cubed = inverse * inverse * inverse
+    own_part, last_part = normed_gradient
+    scale_rows = inverse[:, None] * gain_part[None, :]
+    base = grad_home.astype(jnp.float32) + scale_rows * own_part
+    base, last_part = lax.optimization_barrier((base, last_part))
     grad_x = (
-        grad_home.astype(jnp.float32)
-        + inverse[:, None] * gain_part[None, :] * normed_gradient
+        base
+        + scale_rows * last_part.astype(jnp.float32)
         - x_float * cubed[:, None] * stat[:, None]
     )
     return (relaid, grad_x.astype(jnp.bfloat16))

time: 134 us -> 136 us (1.015)
  local copies, waits for them, and re-layouts: 23.3 us -> 25.3 us
  other arithmetic: 19.2 us -> 17.8 us
    unnamed x64 -> x66, local copies, waits for them, and re-layouts: 7.69 us -> 9.69 us
    convert_element_type x1, other arithmetic: 2.62 us -> 1.16 us  [per_device(): return (relaid, grad_x.astype(jnp.bfloat16))]
  transfers between devices with their start and end apart: 16 -> 16, of which waited for: 6 -> 6; matrix products, arithmetic and copies ran while one was open for 45% -> 44% of each run, Pallas kernels for 0% -> 0%
where the time goes in v25:
time: 136 us; the launch traced here: 135 us
  matrix products  38.5 us (28%)
  local copies, waits for them, and re-layouts  25.3 us (19%)
  starting transfers between devices  20.7 us (15%)
  other arithmetic  17.8 us (13%)
  waiting for transfers between devices  17.6 us (13%)
  between operations  14.8 us (11%)
    ppermute x7, starting transfers between devices, per_device(): returned.append(lax.ppermute(piece, 'dp', pairs))  12.5 us
    ppermute x4, waiting for transfers between devices, scatter_features(): lax.ppermute((outgoing, extra), axis_name, _xor_pairs(size, bit))  11.5 us
    unnamed x66, local copies, waits for them, and re-layouts  9.69 us
    dot_general x1, matrix products, per_device(): jnp.dot(normed_input, w_query, preferred_element_type=jnp.float32)  8.16 us
    dot_general x1, matrix products, per_device(): lax.dot_general(w_out, grad_full, (((1,), (1,)), ((), ())), preferred_ele...  7.42 us
    dot_general x1, matrix products, per_device(): lax.dot_general(grad_query.reshape(token_row_count, query_width), w_query...  5.81 us
    another operation x8, local copies, waits for them, and re-layouts, per_device(): returned = jnp.stack(returned)  4.91 us
    dot_general x1, matrix products, per_device(): jnp.dot(attended_flat, w_out, preferred_element_type=jnp.float32)  4.53 us
  transfers between devices with their start and end apart: 16, of which 6 were waited for; matrix products, arithmetic and copies ran while one was open for 44% of the time, Pallas kernels for 0%

profile of v25, /device:TPU:0, one launch (start us, length us, event | category | flops | bytes accessed | tf_op | source)
XLA Modules:
  0.0 134.8 jit_solution(7492151522365478692)
XLA Ops:
  7.2 0.7 all-gather.3.cloned.1.call-update
  8.1 1.1 dynamic-slice_bitcast_fusion
  9.2 6.0 %collective-permute-start.6 = (bf16[32,1024]{1,0:T(8,128)(2,1)S(1)}, bf16[32,1024]{1,0:T(8,128)(2,1)S(1)}, u32[]{:S(2)}, u32[]{:S(2)}) collective-permute-start(bf16[32,1024]{1,0:T(8,128)(2,1)S(1)} %get-tuple-element.38), channel_id=1, source_target_pairs={{0,28},{4,0},{8,4},{12,8},{16,12},{20,16},{24,20},{28,24},{1,29},{... | collective-permute-start | bytes 196616 | tf_op jit(solution)/shard_map/ppermute | solution.py:165
  15.2 0.4 collective-permute-start.5
  15.7 3.0 %collective-permute-start.3 = (bf16[32,1024]{1,0:T(8,128)(2,1)S(1)}, bf16[32,1024]{1,0:T(8,128)(2,1)S(1)}, u32[]{:S(2)}, u32[]{:S(2)}) collective-permute-start(bf16[32,1024]{1,0:T(8,128)(2,1)S(1)} %get-tuple-element.41), channel_id=1, source_target_pairs={{0,16},{4,20},{8,24},{12,28},{16,0},{20,4},{24,8},{28,12},{1,17},{... | collective-permute-start | bytes 196616 | tf_op jit(solution)/shard_map/ppermute | solution.py:165
  18.7 0.8 reduce-window.8
  19.6 1.0 broadcast_multiply_fusion.1
  20.6 0.7 fusion.34
  21.3 0.7 copy.141
  22.0 0.8 copy.139
  22.9 1.9 %collective-permute-start.1 = (bf16[32,1024]{1,0:T(8,128)(2,1)S(1)}, bf16[32,1024]{1,0:T(8,128)(2,1)S(1)}, u32[]{:S(2)}, u32[]{:S(2)}) collective-permute-start(bf16[32,1024]{1,0:T(8,128)(2,1)S(1)} %get-tuple-element.43), channel_id=1, source_target_pairs={{0,8},{4,12},{8,16},{12,20},{16,24},{20,28},{24,0},{28,4},{1,9},{5... | collective-permute-start | bytes 196616 | tf_op jit(solution)/shard_map/ppermute | solution.py:165
  24.8 1.1 collective-permute-start
  25.9 1.3 and_select_fusion
  27.8 2.2 %collective-permute-done.1 = bf16[32,1024]{1,0:T(8,128)(2,1)S(1)} collective-permute-done((bf16[32,1024]{1,0:T(8,128)(2,1)S(1)}, bf16[32,1024]{1,0:T(8,128)(2,1)S(1)}, u32[]{:S(2)}, u32[]{:S(2)}) %collective-permute-start.1) | collective-permute-done | bytes 65568 | tf_op jit(solution)/shard_map/ppermute | solution.py:165
  30.0 0.8 copy.148
  30.7 1.0 collective-permute-done
  31.8 0.8 copy.147
  32.5 2.9 %stack.58 = bf16[8,32,1024]{2,0,1:T(8,128)(2,1)S(1)} concatenate(bf16[1,32,1024]{2,0,1:T(2,128)(2,1)S(1)} %copy.191, bf16[1,32,1024]{2,0,1:T(2,128)(2,1)} %copy.147, bf16[1,32,1024]{2,0,1:T(2,128)(2,1)} %copy.148, bf16[1,32,1024]{2,0,1:T(2,128)(2,1)S(1)} %copy.149, bf16[1,32,1024]{2,0,1:T(2,128)(2,1)S(1)} %copy.150, bf16[1,32,1024]{2,0,1:T(2,128)(2,1)S(1)} %copy.151, ...), dimensions={0} | concatenate | bytes 1048576 | tf_op jit(solution)/shard_map/stack | solution.py:166
  35.8 1.1 copy.154
  37.0 2.2 %fusion = f32[256]{0:T(256)S(1)} fusion(bf16[256,4096]{1,0:T(8,128)(2,1)} %all-gather.3.cloned.1.call-done), kind=kLoop, calls=%fused_computation.5 | loop fusion | flops 3145472 | bytes 2098176 | tf_op jit(solution)/shard_map/reduce_sum | solution.py:189
  39.2 0.6 multiply_multiply_fusion.2
  39.8 1.2 fusion.52
  41.3 8.2 %fusion.50 = f32[256,1024]{0,1:T(8,128)S(1)} fusion(bf16[4096,1024]{1,0:T(8,128)(2,1)} %param.11, bf16[256,4096]{1,0:T(8,128)(2,1)} %all-gather.3.cloned.1.call-done, f32[4096]{0:T(1024)S(1)} %copy-done.21, f32[256]{0:T(256)S(1)} %get-tuple-element.55), kind=kOutput, calls=%fused_computation.120 | convolution fusion | flops 2151677952 | bytes 11551744 | tf_op jit(solution)/shard_map/dot_general | solution.py:191
  49.6 1.0 copy.144
  50.6 1.0 copy.143
  51.7 0.6 copy-done.14
  52.4 2.5 %fusion.7 = (f32[2,4,256]{2,1,0:T(4,128)S(1)}, f32[2,256,256,4]{2,1,3,0:T(8,128)S(1)}) fusion(pred[256,256]{0,1:T(8,128)(4,1)} %fusion.34, bf16[256,2,4,64]{3,0,2,1:T(8,128)(2,1)} %copy.144, bf16[256,2,4,64]{3,0,2,1:T(8,128)(2,1)} %copy.143, bf16[256,2,64]{2,0,1:T(8,128)(2,1)S(1)} %get-tuple-element.37, bf16[256,2,64]{2,0,1:T(8,128)(2,1)S(1)} %get-tuple-element.36), kind=kOutput, calls=%fused_computation.14 | convolution fusion | flops 137099264 | bytes 2826240 | tf_op jit(solution)/shard_map/qkgd,skd->kgqs/dot_general | solution.py:209
  55.0 1.2 convolution_convert_fusion.4
  56.3 0.7 convolution_convert_fusion.1
  57.0 1.0 slice-done
  58.0 1.4 %slice-done.1 = s8[4194304]{0:T(1024)(128)(4,1)S(1)} async-done(((s8[8388608]{0:T(1024)(128)(4,1)}), s8[4194304]{0:T(1024)(128)(4,1)S(1)}, s32[]{:S(2)}) %slice-start.1) | async-done | bytes 4194328
  59.4 4.5 %fusion.59 = f32[256,4096]{1,0:T(8,128)} fusion(bf16[256,1024]{0,1:T(8,128)(2,1)S(1)} %bitcast.190, bf16[1024,4096]{1,0:T(8,128)(2,1)S(1)} %bitcast.188), kind=kOutput, calls=%fused_computation.123 | convolution fusion | flops 2147483648 | bytes 13107200 | tf_op jit(solution)/shard_map/dot_general | solution.py:219
  64.0 1.7 %fusion.17 = (bf16[1,256,1024]{2,1,0:T(8,128)(2,1)S(1)}, bf16[1,256,1024]{2,1,0:T(8,128)(2,1)S(1)}) fusion(f32[256,4096]{1,0:T(8,128)} %fusion.59, s32[]{:T(128)S(6)} %select_n.111, s32[]{:T(128)S(6)} %select_n.112), kind=kLoop, calls=%fused_computation.50 | loop fusion | bytes 2097160 | tf_op jit(solution)/shard_map/stack | solution.py:103
  65.7 1.1 pad_maximum_fusion
  66.8 7.4 %convolution_convert_fusion = bf16[256,1024]{1,0:T(8,128)(2,1)} fusion(bf16[256,4096]{1,0:T(8,128)(2,1)} %all-gather.5.cloned.1.call-done, bf16[1024,4096]{1,0:T(8,128)(2,1)} %param.14), kind=kOutput, calls=%fused_computation.19 | convolution fusion | flops 2147745792 | bytes 11010048 | tf_op jit(solution)/shard_map/dot_general | solution.py:223
  74.2 2.0 %copy.155 = bf16[256,1024]{0,1:T(8,128)(2,1)} copy(bf16[256,1024]{1,0:T(8,128)(2,1)} %convolution_convert_fusion) | data formatting | bytes 1048576 | tf_op jit(solution)/shard_map/optimization_barrier | solution.py:110
  76.3 1.2 multiply_reduce_fusion
  77.5 2.5 %fusion.5 = bf16[2,4,256,256]{2,3,1,0:T(8,128)(2,1)S(1)} fusion(bf16[256,2,128,1]{0,2,3,1:T(8,128)(2,1)S(1)} %bitcast.216, bf16[256,2,4,128]{0,3,2,1:T(8,128)(2,1)} %bitcast.195, f32[2,4,256]{2,1,0:T(4,128)S(1)} %bitcast.212, f32[2,4,256]{2,1,0:T(4,128)S(1)} %get-tuple-element.56, f32[2,256,256,4]{2,1,3,0:T(8,128)} %copy-done.27, ...), kind=kOutput, calls=%fused_computation.11 | convolution fusion | flops 137363456 | bytes 3883008 | tf_op jit(solution)/shard_map/qkgd,skd->kgqs/dot_general | solution.py:240
  80.0 0.4 convolution_bitcast_fusion.2
  81.2 1.0 copy-done.3
  82.2 1.2 fusion.21
  83.4 1.6 %collective-permute-start.8 = (bf16[1,256,1024]{2,1,0:T(8,128)(2,1)S(1)}, bf16[1,256,1024]{2,1,0:T(8,128)(2,1)S(1)}, u32[]{:S(2)}, u32[]{:S(2)}) collective-permute-start(bf16[1,256,1024]{2,1,0:T(8,128)(2,1)S(1)} %fusion.21), channel_id=1, source_target_pairs={{0,2},{1,3},{2,0},{3,1},{4,6},{5,7},{6,4},{7,5},{8,10},{9,11},{10,... | collective-permute-start | bytes 1572872 | tf_op jit(solution)/shard_map/ppermute | solution.py:105
  85.2 5.8 %fusion.60 = f32[256,4096]{1,0:T(8,128)S(1)} fusion(bf16[256,1024]{0,1:T(8,128)(2,1)S(1)} %bitcast.200, bf16[4096,1024]{1,0:T(8,128)(2,1)} %param.11), kind=kOutput, calls=%fused_computation.124 | convolution fusion | flops 2147483648 | bytes 13107200 | tf_op jit(solution)/shard_map/dot_general | solution.py:279
  91.0 0.4 add_convert_fusion.2
  91.5 0.8 convolution_add_fusion.1
  92.5 0.7 copy-done.28
  93.3 0.7 fusion.8
  93.9 0.9 copy-done.10
  94.8 0.8 convolution_add_fusion
  95.7 2.1 %collective-permute-done.8 = bf16[1,256,1024]{2,1,0:T(8,128)(2,1)S(1)} collective-permute-done((bf16[1,256,1024]{2,1,0:T(8,128)(2,1)S(1)}, bf16[1,256,1024]{2,1,0:T(8,128)(2,1)S(1)}, u32[]{:S(2)}, u32[]{:S(2)}) %collective-permute-start.8) | collective-permute-done | bytes 524320 | tf_op jit(solution)/shard_map/ppermute | solution.py:105
  97.8 1.4 %fusion.9 = bf16[256,1024]{1,0:T(8,128)(2,1)S(1)} fusion(bf16[256,1024]{1,0:T(8,128)(2,1)S(1)} %copy-done.6, f32[256,4096]{1,0:T(8,128)S(1)} %copy-done.3, s32[]{:T(128)S(6)} %select_n.110, bf16[1,256,1024]{2,1,0:T(8,128)(2,1)S(1)} %collective-permute-done.8, bf16[2,256,1024]{2,1,0:T(8,128)(2,1)} %collective-permute-done.7), kind=kLoop, calls=%fused_computation.30 | loop fusion | flops 1835008 | bytes 3145732 | tf_op jit(solution)/shard_map/convert_element_type | solution.py:235
  99.8 0.4 convolution_convert_fusion.2
  100.2 2.0 %collective-permute-done.9 = bf16[2,256,1024]{2,1,0:T(8,128)(2,1)S(1)} collective-permute-done((bf16[2,256,1024]{2,1,0:T(8,128)(2,1)S(1)}, bf16[2,256,1024]{2,1,0:T(8,128)(2,1)S(1)}, u32[]{:S(2)}, u32[]{:S(2)}) %collective-permute-start.9) | collective-permute-done | bytes 1048608 | tf_op jit(solution)/shard_map/ppermute | solution.py:107
  102.2 1.0 copy-done.11
  103.2 1.1 copy.166
  104.2 4.2 %all-to-all-start = ((bf16[8,32,1024]{2,1,0:T(8,128)(2,1)}), bf16[8,32,1024]{2,1,0:T(8,128)(2,1)}, u32[]{:S(2)}, u32[]{:S(2)}) async-start(bf16[8,32,1024]{2,1,0:T(8,128)(2,1)} %copy.166), calls=%async_computation | async-start | bytes 1048576 | tf_op jit(solution)/shard_map/all_to_all | solution.py:313
  108.4 2.4 %fusion.22 = (bf16[1,256,1024]{2,1,0:T(8,128)(2,1)S(1)}, f32[256,1024]{1,0:T(8,128)S(1)}) fusion(f32[256,4096]{1,0:T(8,128)} %copy-done.1, s32[]{:T(128)S(6)} %select_n.113, bf16[2,256,1024]{2,1,0:T(8,128)(2,1)} %copy-done.11, s32[]{:T(128)S(6)} %select_n.110, f32[1024]{0:T(1024)S(1)} %dynamic_slice.70, f32[256]{0:T(256)S(1)} %copy-done.24, ...), kind=kLoop, calls=%fused_computation.55 | loop fusion | flops 2359296 | bytes 5248008 | tf_op jit(solution)/shard_map/convert_element_type | solution.py:103
  110.8 1.6 %collective-permute-start.10 = (bf16[1,256,1024]{2,1,0:T(8,128)(2,1)S(1)}, bf16[1,256,1024]{2,1,0:T(8,128)(2,1)S(1)}, u32[]{:S(2)}, u32[]{:S(2)}) collective-permute-start(bf16[1,256,1024]{2,1,0:T(8,128)(2,1)S(1)} %get-tuple-element.26), channel_id=1, source_target_pairs={{0,2},{1,3},{2,0},{3,1},{4,6},{5,7},{6,4},{7,5},{8,10},{9,11},{10,... | collective-permute-start | bytes 1572872 | tf_op jit(solution)/shard_map/ppermute | solution.py:107
  112.4 2.2 %fusion.3 = f32[256]{0:T(256)S(1)} fusion(bf16[256,4096]{1,0:T(8,128)(2,1)} %all-gather.3.cloned.1.call-done, f32[256,4096]{1,0:T(8,128)S(1)} %copy-done.2, f32[4096]{0:T(1024)S(1)} %copy-done.21), kind=kLoop, calls=%fused_computation.8 | loop fusion | flops 4194048 | bytes 6308864 | tf_op jit(solution)/shard_map/reduce_sum | solution.py:299
  114.7 1.1 collective-permute-done.11
  115.8 0.7 collective-permute-start.12
  116.5 8.4 %collective-permute-done.12 = f32[256]{0:T(256)S(1)} collective-permute-done((f32[256]{0:T(256)S(1)}, f32[256]{0:T(256)S(1)}, u32[]{:S(2)}, u32[]{:S(2)}) %collective-permute-start.12) | collective-permute-done | bytes 1056 | tf_op jit(solution)/shard_map/ppermute | solution.py:107
  124.9 1.2 fusion.12
  126.1 1.9 %copy.195 = bf16[256,1024]{1,0:T(8,128)(2,1)} copy(bf16[256,1024]{1,0:T(8,128)(2,1)} %bitcast.68) | data formatting | bytes 1048576
  (99 shorter events, 3.8 us)
Async XLA Ops:
  7.2 32.6 %copy-start = (bf16[4096,256]{1,0:T(8,128)(2,1)S(1)}, bf16[4096,256]{1,0:T(8,128)(2,1)}, u32[]{:S(2)}) copy-start(bf16[4096,256]{1,0:T(8,128)(2,1)} %param.12) | copy-start | bytes 6291460
  7.2 29.8 %all-gather.3.cloned.1.call-start = ((), (), s32[]{:S(2)}) async-start(), calls=%async_computation.1 | async-start | bytes 2621440 | tf_op jit(solution)/shard_map/all_gather | solution.py:187
  7.9 56.1 %all-gather.5.cloned.1.call-start = ((), (), s32[]{:S(2)}) async-start(), calls=%async_computation.2 | async-start | bytes 2621440 | tf_op jit(solution)/shard_map/all_gather | solution.py:220
  9.2 13.7 %collective-permute-start.6 = (bf16[32,1024]{1,0:T(8,128)(2,1)S(1)}, bf16[32,1024]{1,0:T(8,128)(2,1)S(1)}, u32[]{:S(2)}, u32[]{:S(2)}) collective-permute-start(bf16[32,1024]{1,0:T(8,128)(2,1)S(1)} %get-tuple-element.38), channel_id=1, source_target_pairs={{0,28},{4,0},{8,4},{12,8},{16,12},{20,16},{24,20},{28,24},{1,29},{... | collective-permute-start | bytes 196616 | tf_op jit(solution)/shard_map/ppermute | solution.py:165
  15.2 9.6 %collective-permute-start.5 = (bf16[32,1024]{1,0:T(8,128)(2,1)S(1)}, bf16[32,1024]{1,0:T(8,128)(2,1)S(1)}, u32[]{:S(2)}, u32[]{:S(2)}) collective-permute-start(bf16[32,1024]{1,0:T(8,128)(2,1)S(1)} %get-tuple-element.39), channel_id=1, source_target_pairs={{0,24},{4,28},{8,0},{12,4},{16,8},{20,12},{24,16},{28,20},{1,25},{... | collective-permute-start | bytes 196616 | tf_op jit(solution)/shard_map/ppermute | solution.py:165
  15.7 11.8 %collective-permute-start.4 = (bf16[32,1024]{1,0:T(8,128)(2,1)S(1)}, bf16[32,1024]{1,0:T(8,128)(2,1)S(1)}, u32[]{:S(2)}, u32[]{:S(2)}) collective-permute-start(bf16[32,1024]{1,0:T(8,128)(2,1)S(1)} %get-tuple-element.40), channel_id=1, source_target_pairs={{0,20},{4,24},{8,28},{12,0},{16,4},{20,8},{24,12},{28,16},{1,21},{... | collective-permute-start | bytes 196616 | tf_op jit(solution)/shard_map/ppermute | solution.py:165
  15.7 11.9 %collective-permute-start.3 = (bf16[32,1024]{1,0:T(8,128)(2,1)S(1)}, bf16[32,1024]{1,0:T(8,128)(2,1)S(1)}, u32[]{:S(2)}, u32[]{:S(2)}) collective-permute-start(bf16[32,1024]{1,0:T(8,128)(2,1)S(1)} %get-tuple-element.41), channel_id=1, source_target_pairs={{0,16},{4,20},{8,24},{12,28},{16,0},{20,4},{24,8},{28,12},{1,17},{... | collective-permute-start | bytes 196616 | tf_op jit(solution)/shard_map/ppermute | solution.py:165
  18.7 9.0 %collective-permute-start.2 = (bf16[32,1024]{1,0:T(8,128)(2,1)S(1)}, bf16[32,1024]{1,0:T(8,128)(2,1)S(1)}, u32[]{:S(2)}, u32[]{:S(2)}) collective-permute-start(bf16[32,1024]{1,0:T(8,128)(2,1)S(1)} %get-tuple-element.42), channel_id=1, source_target_pairs={{0,12},{4,16},{8,20},{12,24},{16,28},{20,0},{24,4},{28,8},{1,13},{... | collective-permute-start | bytes 196616 | tf_op jit(solution)/shard_map/ppermute | solution.py:165
  22.9 7.1 %collective-permute-start.1 = (bf16[32,1024]{1,0:T(8,128)(2,1)S(1)}, bf16[32,1024]{1,0:T(8,128)(2,1)S(1)}, u32[]{:S(2)}, u32[]{:S(2)}) collective-permute-start(bf16[32,1024]{1,0:T(8,128)(2,1)S(1)} %get-tuple-element.43), channel_id=1, source_target_pairs={{0,8},{4,12},{8,16},{12,20},{16,24},{20,28},{24,0},{28,4},{1,9},{5... | collective-permute-start | bytes 196616 | tf_op jit(solution)/shard_map/ppermute | solution.py:165
  24.8 7.0 %collective-permute-start = (bf16[32,1024]{1,0:T(8,128)(2,1)S(1)}, bf16[32,1024]{1,0:T(8,128)(2,1)S(1)}, u32[]{:S(2)}, u32[]{:S(2)}) collective-permute-start(bf16[32,1024]{1,0:T(8,128)(2,1)S(1)} %get-tuple-element.44), channel_id=1, source_target_pairs={{0,4},{4,8},{8,12},{12,16},{16,20},{20,24},{24,28},{28,0},{1,5},{5... | collective-permute-start | bytes 196616 | tf_op jit(solution)/shard_map/ppermute | solution.py:165
  35.8 4.0 %copy-start.21 = (f32[4096]{0:T(1024)S(1)}, f32[4096]{0:T(1024)}, u32[]{:S(2)}) copy-start(f32[4096]{0:T(1024)} %param.10) | copy-start | bytes 49156
  36.9 2.8 %copy-start.4 = (bf16[256,4096]{1,0:T(8,128)(2,1)S(1)}, bf16[256,4096]{1,0:T(8,128)(2,1)}, u32[]{:S(2)}) copy-start(bf16[256,4096]{1,0:T(8,128)(2,1)} %all-gather.3.cloned.1.call-done) | copy-start | bytes 6291460
  39.8 1.5 %copy-start.22 = (f32[256]{0:T(256)}, f32[256]{0:T(256)S(1)}, u32[]{:S(2)}) copy-start(f32[256]{0:T(256)S(1)} %get-tuple-element.55) | copy-start | bytes 3076
  49.4 2.2 %copy-start.12 = (f32[256,64]{1,0:T(8,128)S(1)}, f32[256,64]{1,0:T(8,128)}, u32[]{:S(2)}) copy-start(f32[256,64]{1,0:T(8,128)} %copy.141) | copy-start | bytes 196612
  49.4 2.2 %copy-start.13 = (f32[256,64]{1,0:T(8,128)S(1)}, f32[256,64]{1,0:T(8,128)}, u32[]{:S(2)}) copy-start(f32[256,64]{1,0:T(8,128)} %copy.139) | copy-start | bytes 196612
  51.6 3.3 %copy-start.5 = (bf16[256,4096]{1,0:T(8,128)(2,1)S(1)}, bf16[256,4096]{1,0:T(8,128)(2,1)}, u32[]{:S(2)}) copy-start(bf16[256,4096]{1,0:T(8,128)(2,1)} %all-gather.3.cloned.1.call-done) | copy-start | bytes 6291460
  51.6 3.4 %copy-start.9 = (bf16[4096,256]{1,0:T(8,128)(2,1)S(1)}, bf16[4096,256]{1,0:T(8,128)(2,1)}, u32[]{:S(2)}) copy-start(bf16[4096,256]{1,0:T(8,128)(2,1)} %param.13) | copy-start | bytes 6291460
  51.6 3.4 %copy-start.23 = (f32[256]{0:T(256)S(1)}, f32[256]{0:T(256)}, u32[]{:S(2)}) copy-start(f32[256]{0:T(256)} %copy-done.22) | copy-start | bytes 3076
  51.7 0.6 copy-start.14
  51.7 0.7 copy-start.16
  55.0 1.3 copy-start.27
  55.0 1.3 copy-start.20
  55.0 3.0 %slice-start = ((s8[8388608]{0:T(1024)(128)(4,1)}), s8[4194304]{0:T(1024)(128)(4,1)S(1)}, s32[]{:S(2)}) async-start(s8[8388608]{0:T(1024)(128)(4,1)} %bitcast.187), calls=%async_computation.3 | async-start | bytes 8388608
  56.3 3.1 %slice-start.1 = ((s8[8388608]{0:T(1024)(128)(4,1)}), s8[4194304]{0:T(1024)(128)(4,1)S(1)}, s32[]{:S(2)}) async-start(s8[8388608]{0:T(1024)(128)(4,1)} %bitcast.187), calls=%async_computation.4 | async-start | bytes 8388608
  66.8 7.4 %collective-permute-start.7 = (bf16[2,256,1024]{2,1,0:T(8,128)(2,1)}, bf16[2,256,1024]{2,1,0:T(8,128)(2,1)}, u32[]{:S(2)}, u32[]{:S(2)}) collective-permute-start(bf16[2,256,1024]{2,1,0:T(8,128)(2,1)} %pad_maximum_fusion), channel_id=1, source_target_pairs={{0,1},{1,0},{2,3},{3,2},{4,5},{5,4},{6,7},{7,6},{8,9},{9,8},{10,11... | collective-permute-start | bytes 3145736 | tf_op jit(solution)/shard_map/ppermute | solution.py:105
  77.5 3.0 %copy-start.17 = (bf16[256,2,64]{2,0,1:T(8,128)(2,1)S(1)}, bf16[256,2,64]{2,0,1:T(8,128)(2,1)}, u32[]{:S(2)}) copy-start(bf16[256,2,64]{2,0,1:T(8,128)(2,1)} %copy-done.16) | copy-start | bytes 196612
  77.5 3.3 %copy-start.15 = (bf16[256,2,64]{2,0,1:T(8,128)(2,1)S(1)}, bf16[256,2,64]{2,0,1:T(8,128)(2,1)}, u32[]{:S(2)}) copy-start(bf16[256,2,64]{2,0,1:T(8,128)(2,1)} %copy-done.14) | copy-start | bytes 196612
  80.0 2.2 %copy-start.3 = (f32[256,4096]{1,0:T(8,128)S(1)}, f32[256,4096]{1,0:T(8,128)}, u32[]{:S(2)}) copy-start(f32[256,4096]{1,0:T(8,128)} %fusion.59) | copy-start | bytes 12582916
  83.4 14.4 %collective-permute-start.8 = (bf16[1,256,1024]{2,1,0:T(8,128)(2,1)S(1)}, bf16[1,256,1024]{2,1,0:T(8,128)(2,1)S(1)}, u32[]{:S(2)}, u32[]{:S(2)}) collective-permute-start(bf16[1,256,1024]{2,1,0:T(8,128)(2,1)S(1)} %fusion.21), channel_id=1, source_target_pairs={{0,2},{1,3},{2,0},{3,1},{4,6},{5,7},{6,4},{7,5},{8,10},{9,11},{10,... | collective-permute-start | bytes 1572872 | tf_op jit(solution)/shard_map/ppermute | solution.py:105
  85.2 5.8 %copy-start.18 = (f32[256,64]{0,1:T(8,128)S(1)}, f32[256,64]{0,1:T(8,128)}, u32[]{:S(2)}) copy-start(f32[256,64]{0,1:T(8,128)} %get-tuple-element.50) | copy-start | bytes 196612
  85.2 5.8 %copy-start.19 = (f32[256,64]{0,1:T(8,128)S(1)}, f32[256,64]{0,1:T(8,128)}, u32[]{:S(2)}) copy-start(f32[256,64]{0,1:T(8,128)} %get-tuple-element.51) | copy-start | bytes 196612
  91.5 1.0 copy-start.8
  91.5 1.8 %copy-start.28 = (f32[2,256,256,4]{2,1,3,0:T(8,128)S(1)}, f32[2,256,256,4]{2,1,3,0:T(8,128)}, u32[]{:S(2)}) copy-start(f32[2,256,256,4]{2,1,3,0:T(8,128)} %copy-done.27) | copy-start | bytes 6291460
  93.3 1.6 %copy-start.10 = (bf16[4096,256]{1,0:T(8,128)(2,1)S(1)}, bf16[4096,256]{1,0:T(8,128)(2,1)}, u32[]{:S(2)}) copy-start(bf16[4096,256]{1,0:T(8,128)(2,1)} %param.13) | copy-start | bytes 6291460
  94.8 3.0 %copy-start.6 = (bf16[256,1024]{1,0:T(8,128)(2,1)S(1)}, bf16[256,1024]{1,0:T(8,128)(2,1)}, u32[]{:S(2)}) copy-start(bf16[256,1024]{1,0:T(8,128)(2,1)} %param.9) | copy-start | bytes 1572868
  95.7 3.7 %copy-start.1 = (f32[256,4096]{1,0:T(8,128)}, f32[256,4096]{1,0:T(8,128)S(1)}, u32[]{:S(2)}) copy-start(f32[256,4096]{1,0:T(8,128)S(1)} %convolution_add_fusion) | copy-start | bytes 12582916
  99.2 0.7 copy-start.26
  99.5 9.0 %copy-start.7 = (bf16[8,32,1024]{2,1,0:T(8,128)(2,1)S(1)}, bf16[8,32,1024]{2,1,0:T(8,128)(2,1)}, u32[]{:S(2)}) copy-start(bf16[8,32,1024]{2,1,0:T(8,128)(2,1)} %copy.154) | copy-start | bytes 1572868
  99.5 9.0 %copy-start.24 = (f32[256]{0:T(256)S(1)}, f32[256]{0:T(256)}, u32[]{:S(2)}) copy-start(f32[256]{0:T(256)} %copy-done.22) | copy-start | bytes 3076
  99.5 2.7 %collective-permute-start.9 = (bf16[2,256,1024]{2,1,0:T(8,128)(2,1)S(1)}, bf16[2,256,1024]{2,1,0:T(8,128)(2,1)S(1)}, u32[]{:S(2)}, u32[]{:S(2)}) collective-permute-start(bf16[2,256,1024]{2,1,0:T(8,128)(2,1)S(1)} %pad_maximum_fusion.1), channel_id=1, source_target_pairs={{0,1},{1,0},{2,3},{3,2},{4,5},{5,4},{6,7},{7,6},{8,9},{9,8},{10,11... | collective-permute-start | bytes 3145736 | tf_op jit(solution)/shard_map/ppermute | solution.py:107
  102.2 1.0 copy-start.11
  104.2 21.8 %all-to-all-start = ((bf16[8,32,1024]{2,1,0:T(8,128)(2,1)}), bf16[8,32,1024]{2,1,0:T(8,128)(2,1)}, u32[]{:S(2)}, u32[]{:S(2)}) async-start(bf16[8,32,1024]{2,1,0:T(8,128)(2,1)} %copy.166), calls=%async_computation | async-start | bytes 1048576 | tf_op jit(solution)/shard_map/all_to_all | solution.py:313
  108.4 4.0 %copy-start.2 = (f32[256,4096]{1,0:T(8,128)S(1)}, f32[256,4096]{1,0:T(8,128)}, u32[]{:S(2)}) copy-start(f32[256,4096]{1,0:T(8,128)} %copy-done.1) | copy-start | bytes 12582916
  110.8 14.1 %copy-start.25 = (f32[256]{0:T(256)S(1)}, f32[256]{0:T(256)}, u32[]{:S(2)}) copy-start(f32[256]{0:T(256)} %get-tuple-element.54) | copy-start | bytes 3076
  110.8 14.1 %collective-permute-start.10 = (bf16[1,256,1024]{2,1,0:T(8,128)(2,1)S(1)}, bf16[1,256,1024]{2,1,0:T(8,128)(2,1)S(1)}, u32[]{:S(2)}, u32[]{:S(2)}) collective-permute-start(bf16[1,256,1024]{2,1,0:T(8,128)(2,1)S(1)} %get-tuple-element.26), channel_id=1, source_target_pairs={{0,2},{1,3},{2,0},{3,1},{4,6},{5,7},{6,4},{7,5},{8,10},{9,11},{10,... | collective-permute-start | bytes 1572872 | tf_op jit(solution)/shard_map/ppermute | solution.py:107
  114.6 1.2 collective-permute-start.11
  115.8 9.1 %collective-permute-start.12 = (f32[256]{0:T(256)S(1)}, f32[256]{0:T(256)S(1)}, u32[]{:S(2)}, u32[]{:S(2)}) collective-permute-start(f32[256]{0:T(256)S(1)} %add.200), channel_id=1, source_target_pairs={{0,2},{1,3},{2,0},{3,1},{4,6},{5,7},{6,4},{7,5},{8,10},{9,11},{10,... | collective-permute-start | bytes 3080 | tf_op jit(solution)/shard_map/ppermute | solution.py:107
Sparse Core Ops, SparseCore 0:
  9.6 25.2 all-gather.2
  37.0 22.0 all-gather.4

commit v26 on v23

--- a/solution.py
+++ b/solution.py
@@ -289,7 +289,6 @@
             preferred_element_type=jnp.float32,
         )
     )
-    output_home, normed_partial = lax.optimization_barrier((output_home, normed_partial))
     stat_partial = jnp.sum(normed_partial * norm_gain[None, :] * gathered_float, axis=1)
     home_blocks = output_home.reshape(block_count, home_rows, width_part)
     outgoing = jnp.einsum(

time: 134 us -> 134 us (level)
  waiting for transfers between devices: 17.3 us -> 20.1 us
  matrix products: 38.5 us -> 36.3 us
    dot_general x1, matrix products: 5.81 us -> 2.39 us  [per_device(): lax.dot_general(grad_query.reshape(token_row_count, query_width), w_query...]
    reduce_sum x1 -> x0, other arithmetic: 2.82 us -> none  [per_device(): jnp.sum(normed_partial * norm_gain[None, :] * gathered_float, axis=1)]
    ppermute x2, waiting for transfers between devices: 2.13 us -> 4.5 us  [scatter_features(): incoming = lax.ppermute(outgoing, axis_name, _xor_pairs(size, bit))]
    dot_general x1, matrix products: 0.66 us -> 2.55 us  [per_device(): jnp.einsum('kgqs,qkgd->skd', probs_low, grouped_gradient, preferred_eleme...]
    dot_general x1, matrix products: 2.52 us -> 0.73 us  [per_device(): jnp.einsum('qkgd,skd->kgqs', grouped_gradient, value_rows, preferred_elem...]
    dot_general x1, matrix products: 1.16 us -> 2.76 us  [per_device(): jnp.dot(normed_input, key_weight, preferred_element_type=jnp.float32)]
  transfers between devices with their start and end apart: 16 -> 16, of which waited for: 6 -> 5; matrix products, arithmetic and copies ran while one was open for 45% -> 43% of each run, Pallas kernels for 0% -> 0%
where the time goes in v26:
time: 134 us; the launch traced here: 133 us
  matrix products  36.3 us (27%)
  local copies, waits for them, and re-layouts  23.4 us (17%)
  starting transfers between devices  20.7 us (15%)
  waiting for transfers between devices  20.1 us (15%)
  other arithmetic  18 us (13%)
  between operations  14.8 us (11%)
    ppermute x7, starting transfers between devices, per_device(): returned.append(lax.ppermute(piece, 'dp', pairs))  12.5 us
    ppermute x4, waiting for transfers between devices, scatter_features(): lax.ppermute((outgoing, extra), axis_name, _xor_pairs(size, bit))  11.6 us
    dot_general x1, matrix products, per_device(): jnp.dot(normed_input, w_query, preferred_element_type=jnp.float32)  7.87 us
    unnamed x64, local copies, waits for them, and re-layouts  7.78 us
    dot_general x1, matrix products, per_device(): lax.dot_general(w_out, grad_full, (((1,), (1,)), ((), ())), preferred_ele...  7.41 us
    another operation x8, local copies, waits for them, and re-layouts, per_device(): returned = jnp.stack(returned)  4.91 us
    dot_general x1, matrix products, per_device(): jnp.dot(attended_flat, w_out, preferred_element_type=jnp.float32)  4.52 us
    ppermute x2, waiting for transfers between devices, scatter_features(): incoming = lax.ppermute(outgoing, axis_name, _xor_pairs(size, bit))  4.5 us
  transfers between devices with their start and end apart: 16, of which 5 were waited for; matrix products, arithmetic and copies ran while one was open for 43% of the time, Pallas kernels for 0%

profile of v26, /device:TPU:0, one launch (start us, length us, event | category | flops | bytes accessed | tf_op | source)
XLA Modules:
  0.0 133.4 jit_solution(4930974323154053371)
XLA Ops:
  7.2 0.7 all-gather.3.cloned.1.call-update
  8.1 1.1 dynamic-slice_bitcast_fusion
  9.2 6.0 %collective-permute-start.6 = (bf16[32,1024]{1,0:T(8,128)(2,1)S(1)}, bf16[32,1024]{1,0:T(8,128)(2,1)S(1)}, u32[]{:S(2)}, u32[]{:S(2)}) collective-permute-start(bf16[32,1024]{1,0:T(8,128)(2,1)S(1)} %get-tuple-element.28), channel_id=1, source_target_pairs={{0,28},{4,0},{8,4},{12,8},{16,12},{20,16},{24,20},{28,24},{1,29},{... | collective-permute-start | bytes 196616 | tf_op jit(solution)/shard_map/ppermute | solution.py:159
  15.2 0.4 collective-permute-start.5
  15.7 3.0 %collective-permute-start.3 = (bf16[32,1024]{1,0:T(8,128)(2,1)S(1)}, bf16[32,1024]{1,0:T(8,128)(2,1)S(1)}, u32[]{:S(2)}, u32[]{:S(2)}) collective-permute-start(bf16[32,1024]{1,0:T(8,128)(2,1)S(1)} %get-tuple-element.31), channel_id=1, source_target_pairs={{0,16},{4,20},{8,24},{12,28},{16,0},{20,4},{24,8},{28,12},{1,17},{... | collective-permute-start | bytes 196616 | tf_op jit(solution)/shard_map/ppermute | solution.py:159
  18.7 0.8 reduce-window.8
  19.6 1.0 broadcast_multiply_fusion.1
  20.6 0.7 fusion.34
  21.3 0.7 copy.141
  22.1 0.8 copy.139
  23.0 1.9 %collective-permute-start.1 = (bf16[32,1024]{1,0:T(8,128)(2,1)S(1)}, bf16[32,1024]{1,0:T(8,128)(2,1)S(1)}, u32[]{:S(2)}, u32[]{:S(2)}) collective-permute-start(bf16[32,1024]{1,0:T(8,128)(2,1)S(1)} %get-tuple-element.33), channel_id=1, source_target_pairs={{0,8},{4,12},{8,16},{12,20},{16,24},{20,28},{24,0},{28,4},{1,9},{5... | collective-permute-start | bytes 196616 | tf_op jit(solution)/shard_map/ppermute | solution.py:159
  24.8 1.1 collective-permute-start
  26.0 1.2 and_select_fusion
  27.8 2.2 %collective-permute-done.1 = bf16[32,1024]{1,0:T(8,128)(2,1)S(1)} collective-permute-done((bf16[32,1024]{1,0:T(8,128)(2,1)S(1)}, bf16[32,1024]{1,0:T(8,128)(2,1)S(1)}, u32[]{:S(2)}, u32[]{:S(2)}) %collective-permute-start.1) | collective-permute-done | bytes 65568 | tf_op jit(solution)/shard_map/ppermute | solution.py:159
  30.0 0.8 copy.148
  30.8 1.0 collective-permute-done
  31.8 0.8 copy.147
  32.6 2.9 %stack.58 = bf16[8,32,1024]{2,0,1:T(8,128)(2,1)S(1)} concatenate(bf16[1,32,1024]{2,0,1:T(2,128)(2,1)S(1)} %copy.191, bf16[1,32,1024]{2,0,1:T(2,128)(2,1)} %copy.147, bf16[1,32,1024]{2,0,1:T(2,128)(2,1)} %copy.148, bf16[1,32,1024]{2,0,1:T(2,128)(2,1)S(1)} %copy.149, bf16[1,32,1024]{2,0,1:T(2,128)(2,1)S(1)} %copy.150, bf16[1,32,1024]{2,0,1:T(2,128)(2,1)S(1)} %copy.151, ...), dimensions={0} | concatenate | bytes 1048576 | tf_op jit(solution)/shard_map/stack | solution.py:160
  35.5 0.4 convolution_convert_fusion.3
  35.8 1.1 copy.154
  37.0 2.2 %fusion = f32[256]{0:T(256)S(1)} fusion(bf16[256,4096]{1,0:T(8,128)(2,1)} %all-gather.3.cloned.1.call-done), kind=kLoop, calls=%fused_computation.5 | loop fusion | flops 3145472 | bytes 2098176 | tf_op jit(solution)/shard_map/reduce_sum | solution.py:183
  39.2 0.6 multiply_multiply_fusion
  39.8 2.8 %fusion.53 = f32[256,256]{0,1:T(8,128)S(1)} fusion(bf16[4096,256]{1,0:T(8,128)(2,1)} %param.12, bf16[256,4096]{1,0:T(8,128)(2,1)S(1)} %copy-done.2, f32[4096]{0:T(1024)S(1)} %copy-done.18, f32[256]{0:T(256)S(1)} %get-tuple-element.45), kind=kOutput, calls=%fused_computation.120 | convolution fusion | flops 541065216 | bytes 4473856 | tf_op jit(solution)/shard_map/dot_general | solution.py:186
  42.9 7.9 %fusion.51 = f32[256,1024]{0,1:T(8,128)S(1)} fusion(bf16[4096,1024]{1,0:T(8,128)(2,1)} %param.11, bf16[256,4096]{1,0:T(8,128)(2,1)} %all-gather.3.cloned.1.call-done, f32[4096]{0:T(1024)S(1)} %copy-done.18, f32[256]{0:T(256)S(1)} %get-tuple-element.45), kind=kOutput, calls=%fused_computation.119 | convolution fusion | flops 2151677952 | bytes 11551744 | tf_op jit(solution)/shard_map/dot_general | solution.py:185
  51.0 1.0 copy.144
  52.0 1.0 copy.143
  53.1 0.6 copy-done.11
  53.8 2.1 %fusion.7 = (f32[2,4,256]{2,1,0:T(4,128)S(1)}, f32[2,256,256,4]{2,1,3,0:T(8,128)S(1)}) fusion(pred[256,256]{0,1:T(8,128)(4,1)} %fusion.34, bf16[256,2,4,64]{3,0,2,1:T(8,128)(2,1)} %copy.144, bf16[256,2,4,64]{3,0,2,1:T(8,128)(2,1)} %copy.143, bf16[256,2,64]{2,0,1:T(8,128)(2,1)S(1)} %get-tuple-element.27, bf16[256,2,64]{2,0,1:T(8,128)(2,1)S(1)} %get-tuple-element.26), kind=kOutput, calls=%fused_computation.14 | convolution fusion | flops 137099264 | bytes 2826240 | tf_op jit(solution)/shard_map/qkgd,skd->kgqs/dot_general | solution.py:203
  55.9 1.2 convolution_convert_fusion.4
  57.2 0.7 convolution_convert_fusion.1
  57.9 1.0 slice-done
  58.9 1.4 %slice-done.1 = s8[4194304]{0:T(1024)(128)(4,1)S(1)} async-done(((s8[8388608]{0:T(1024)(128)(4,1)}), s8[4194304]{0:T(1024)(128)(4,1)S(1)}, s32[]{:S(2)}) %slice-start.1) | async-done | bytes 4194328
  60.3 4.5 %fusion.59 = f32[256,4096]{1,0:T(8,128)} fusion(bf16[256,1024]{0,1:T(8,128)(2,1)S(1)} %bitcast.192, bf16[1024,4096]{1,0:T(8,128)(2,1)S(1)} %bitcast.190), kind=kOutput, calls=%fused_computation.122 | convolution fusion | flops 2147483648 | bytes 13107200 | tf_op jit(solution)/shard_map/dot_general | solution.py:213
  64.8 1.7 %fusion.17 = (bf16[1,256,1024]{2,1,0:T(8,128)(2,1)S(1)}, bf16[1,256,1024]{2,1,0:T(8,128)(2,1)S(1)}) fusion(f32[256,4096]{1,0:T(8,128)} %fusion.59, s32[]{:T(128)S(6)} %select_n.110, s32[]{:T(128)S(6)} %select_n.111), kind=kLoop, calls=%fused_computation.49 | loop fusion | bytes 2097160 | tf_op jit(solution)/shard_map/stack | solution.py:100
  66.5 1.1 pad_maximum_fusion
  67.7 7.4 %convolution_convert_fusion = bf16[256,1024]{1,0:T(8,128)(2,1)} fusion(bf16[256,4096]{1,0:T(8,128)(2,1)} %all-gather.5.cloned.1.call-done, bf16[1024,4096]{1,0:T(8,128)(2,1)} %param.14), kind=kOutput, calls=%fused_computation.17 | convolution fusion | flops 2147745792 | bytes 11010048 | tf_op jit(solution)/shard_map/dot_general | solution.py:217
  75.1 2.0 %copy.155 = bf16[256,1024]{0,1:T(8,128)(2,1)} copy(bf16[256,1024]{1,0:T(8,128)(2,1)} %convolution_convert_fusion) | data formatting | bytes 1048576 | tf_op jit(solution)/shard_map/optimization_barrier | solution.py:107
  77.1 1.2 multiply_reduce_fusion
  78.4 2.5 %fusion.8 = bf16[2,128,256]{2,1,0:T(8,128)(2,1)S(1)} fusion(bf16[256,2,4,128]{0,3,2,1:T(8,128)(2,1)} %bitcast.197, f32[2,256,256,4]{2,1,3,0:T(8,128)} %copy-done.24, f32[2,4,256]{2,1,0:T(4,128)S(1)} %get-tuple-element.46, pred[256,256]{0,1:T(8,128)(4,1)S(1)} %copy-done.17), kind=kOutput, calls=%fused_computation.24 | convolution fusion | flops 136380416 | bytes 2826240 | tf_op jit(solution)/shard_map/kgqs,qkgd->skd/dot_general | solution.py:268
  81.0 0.7 fusion.5
  81.7 0.4 convolution_bitcast_fusion.2
  82.2 0.3 convolution_multiply_fusion
  82.5 0.3 copy-done.12
  83.2 1.5 %fusion.21 = bf16[1,256,1024]{2,1,0:T(8,128)(2,1)S(1)} fusion(f32[256,4096]{1,0:T(8,128)} %fusion.59, s32[]{:T(128)S(6)} %select_n.113, bf16[2,256,1024]{2,1,0:T(8,128)(2,1)} %collective-permute-done.7), kind=kLoop, calls=%fused_computation.53 | loop fusion | flops 786432 | bytes 2097156 | tf_op jit(solution)/shard_map/convert_element_type | solution.py:100
  84.7 1.6 %collective-permute-start.9 = (bf16[1,256,1024]{2,1,0:T(8,128)(2,1)S(1)}, bf16[1,256,1024]{2,1,0:T(8,128)(2,1)}, u32[]{:S(2)}, u32[]{:S(2)}) collective-permute-start(bf16[1,256,1024]{2,1,0:T(8,128)(2,1)S(1)} %fusion.21), channel_id=1, source_target_pairs={{0,2},{1,3},{2,0},{3,1},{4,6},{5,7},{6,4},{7,5},{8,10},{9,11},{10,... | collective-permute-start | bytes 1572872 | tf_op jit(solution)/shard_map/ppermute | solution.py:102
  86.6 2.4 %fusion.60 = f32[256,4096]{1,0:T(8,128)S(1)} fusion(bf16[256,1024]{0,1:T(8,128)(2,1)S(1)} %bitcast.202, bf16[4096,1024]{1,0:T(8,128)(2,1)S(1)} %bitcast.216), kind=kOutput, calls=%fused_computation.123 | convolution fusion | flops 2147483648 | bytes 13107200 | tf_op jit(solution)/shard_map/dot_general | solution.py:273
  89.0 0.5 add_convert_fusion.2
  89.5 0.8 convolution_add_fusion.1
  90.3 0.8 copy-done.4
  91.1 1.1 fusion.3
  92.3 1.1 pad_maximum_fusion.1
  93.4 1.1 copy-done.1
  94.7 4.5 %collective-permute-done.9 = bf16[1,256,1024]{2,1,0:T(8,128)(2,1)} collective-permute-done((bf16[1,256,1024]{2,1,0:T(8,128)(2,1)S(1)}, bf16[1,256,1024]{2,1,0:T(8,128)(2,1)}, u32[]{:S(2)}, u32[]{:S(2)}) %collective-permute-start.9) | collective-permute-done | bytes 524320 | tf_op jit(solution)/shard_map/ppermute | solution.py:102
  99.2 1.8 %fusion.9 = bf16[256,1024]{1,0:T(8,128)(2,1)S(1)} fusion(bf16[256,1024]{1,0:T(8,128)(2,1)S(1)} %copy-done.6, f32[256,4096]{1,0:T(8,128)} %fusion.59, s32[]{:T(128)} %select_n.112, bf16[1,256,1024]{2,1,0:T(8,128)(2,1)} %collective-permute-done.9, bf16[2,256,1024]{2,1,0:T(8,128)(2,1)} %collective-permute-done.7), kind=kLoop, calls=%fused_computation.28 | loop fusion | flops 1835008 | bytes 3145732 | tf_op jit(solution)/shard_map/convert_element_type | solution.py:229
  101.1 0.4 convolution_convert_fusion.2
  101.5 1.1 copy.166
  102.6 4.2 %all-to-all-start = ((bf16[8,32,1024]{2,1,0:T(8,128)(2,1)}), bf16[8,32,1024]{2,1,0:T(8,128)(2,1)}, u32[]{:S(2)}, u32[]{:S(2)}) async-start(bf16[8,32,1024]{2,1,0:T(8,128)(2,1)} %copy.166), calls=%async_computation | async-start | bytes 1048576 | tf_op jit(solution)/shard_map/all_to_all | solution.py:300
  106.8 1.5 %fusion.22 = bf16[1,256,1024]{2,1,0:T(8,128)(2,1)S(1)} fusion(f32[256,4096]{1,0:T(8,128)} %copy-done.1, s32[]{:T(128)S(6)} %select_n.113, bf16[2,256,1024]{2,1,0:T(8,128)(2,1)} %collective-permute-done.8), kind=kLoop, calls=%fused_computation.54 | loop fusion | flops 786432 | bytes 2097156 | tf_op jit(solution)/shard_map/convert_element_type | solution.py:100
  108.3 1.6 %collective-permute-start.10 = (bf16[1,256,1024]{2,1,0:T(8,128)(2,1)S(1)}, bf16[1,256,1024]{2,1,0:T(8,128)(2,1)S(1)}, u32[]{:S(2)}, u32[]{:S(2)}) collective-permute-start(bf16[1,256,1024]{2,1,0:T(8,128)(2,1)S(1)} %fusion.22), channel_id=1, source_target_pairs={{0,2},{1,3},{2,0},{3,1},{4,6},{5,7},{6,4},{7,5},{8,10},{9,11},{10,... | collective-permute-start | bytes 1572872 | tf_op jit(solution)/shard_map/ppermute | solution.py:104
  109.9 1.1 collective-permute-done.11
  111.1 0.5 collective-permute-start.12
  111.5 10.4 %collective-permute-done.12 = f32[256]{0:T(256)S(1)} collective-permute-done((f32[256]{0:T(256)S(1)}, f32[256]{0:T(256)S(1)}, u32[]{:S(2)}, u32[]{:S(2)}) %collective-permute-start.12) | collective-permute-done | bytes 1056 | tf_op jit(solution)/shard_map/ppermute | solution.py:104
  122.0 2.6 %fusion.12 = bf16[256,1024]{1,0:T(8,128)(2,1)} fusion(bf16[256,1024]{1,0:T(8,128)(2,1)S(1)} %copy-done.6, f32[256,4096]{1,0:T(8,128)} %copy-done.1, s32[]{:T(128)} %select_n.112, bf16[1,256,1024]{2,1,0:T(8,128)(2,1)S(1)} %collective-permute-done.10, f32[256]{0:T(256)S(1)} %add_multiply_fusion, f32[256]{0:T(256)S(1)} %copy-done.19, ...), kind=kLoop, calls=%fused_computation.31 | loop fusion | flops 3407872 | bytes 3677188 | tf_op jit(solution)/shard_map/convert_element_type | solution.py:310
  124.7 1.9 %copy.195 = bf16[256,1024]{1,0:T(8,128)(2,1)} copy(bf16[256,1024]{1,0:T(8,128)(2,1)} %bitcast.68) | data formatting | bytes 1048576
  (98 shorter events, 2.6 us)
Async XLA Ops:
  7.2 48.7 %copy-start = (bf16[4096,256]{1,0:T(8,128)(2,1)S(1)}, bf16[4096,256]{1,0:T(8,128)(2,1)}, u32[]{:S(2)}) copy-start(bf16[4096,256]{1,0:T(8,128)(2,1)} %param.13) | copy-start | bytes 6291460
  7.2 29.8 %all-gather.3.cloned.1.call-start = ((), (), s32[]{:S(2)}) async-start(), calls=%async_computation.1 | async-start | bytes 2621440 | tf_op jit(solution)/shard_map/all_gather | solution.py:181
  7.9 56.9 %all-gather.5.cloned.1.call-start = ((), (), s32[]{:S(2)}) async-start(), calls=%async_computation.2 | async-start | bytes 2621440 | tf_op jit(solution)/shard_map/all_gather | solution.py:214
  9.2 13.8 %collective-permute-start.6 = (bf16[32,1024]{1,0:T(8,128)(2,1)S(1)}, bf16[32,1024]{1,0:T(8,128)(2,1)S(1)}, u32[]{:S(2)}, u32[]{:S(2)}) collective-permute-start(bf16[32,1024]{1,0:T(8,128)(2,1)S(1)} %get-tuple-element.28), channel_id=1, source_target_pairs={{0,28},{4,0},{8,4},{12,8},{16,12},{20,16},{24,20},{28,24},{1,29},{... | collective-permute-start | bytes 196616 | tf_op jit(solution)/shard_map/ppermute | solution.py:159
  15.2 9.6 %collective-permute-start.5 = (bf16[32,1024]{1,0:T(8,128)(2,1)S(1)}, bf16[32,1024]{1,0:T(8,128)(2,1)S(1)}, u32[]{:S(2)}, u32[]{:S(2)}) collective-permute-start(bf16[32,1024]{1,0:T(8,128)(2,1)S(1)} %get-tuple-element.29), channel_id=1, source_target_pairs={{0,24},{4,28},{8,0},{12,4},{16,8},{20,12},{24,16},{28,20},{1,25},{... | collective-permute-start | bytes 196616 | tf_op jit(solution)/shard_map/ppermute | solution.py:159
  15.7 11.8 %collective-permute-start.4 = (bf16[32,1024]{1,0:T(8,128)(2,1)S(1)}, bf16[32,1024]{1,0:T(8,128)(2,1)S(1)}, u32[]{:S(2)}, u32[]{:S(2)}) collective-permute-start(bf16[32,1024]{1,0:T(8,128)(2,1)S(1)} %get-tuple-element.30), channel_id=1, source_target_pairs={{0,20},{4,24},{8,28},{12,0},{16,4},{20,8},{24,12},{28,16},{1,21},{... | collective-permute-start | bytes 196616 | tf_op jit(solution)/shard_map/ppermute | solution.py:159
  15.7 11.9 %collective-permute-start.3 = (bf16[32,1024]{1,0:T(8,128)(2,1)S(1)}, bf16[32,1024]{1,0:T(8,128)(2,1)S(1)}, u32[]{:S(2)}, u32[]{:S(2)}) collective-permute-start(bf16[32,1024]{1,0:T(8,128)(2,1)S(1)} %get-tuple-element.31), channel_id=1, source_target_pairs={{0,16},{4,20},{8,24},{12,28},{16,0},{20,4},{24,8},{28,12},{1,17},{... | collective-permute-start | bytes 196616 | tf_op jit(solution)/shard_map/ppermute | solution.py:159
  18.7 9.0 %collective-permute-start.2 = (bf16[32,1024]{1,0:T(8,128)(2,1)S(1)}, bf16[32,1024]{1,0:T(8,128)(2,1)S(1)}, u32[]{:S(2)}, u32[]{:S(2)}) collective-permute-start(bf16[32,1024]{1,0:T(8,128)(2,1)S(1)} %get-tuple-element.32), channel_id=1, source_target_pairs={{0,12},{4,16},{8,20},{12,24},{16,28},{20,0},{24,4},{28,8},{1,13},{... | collective-permute-start | bytes 196616 | tf_op jit(solution)/shard_map/ppermute | solution.py:159
  23.0 7.1 %collective-permute-start.1 = (bf16[32,1024]{1,0:T(8,128)(2,1)S(1)}, bf16[32,1024]{1,0:T(8,128)(2,1)S(1)}, u32[]{:S(2)}, u32[]{:S(2)}) collective-permute-start(bf16[32,1024]{1,0:T(8,128)(2,1)S(1)} %get-tuple-element.33), channel_id=1, source_target_pairs={{0,8},{4,12},{8,16},{12,20},{16,24},{20,28},{24,0},{28,4},{1,9},{5... | collective-permute-start | bytes 196616 | tf_op jit(solution)/shard_map/ppermute | solution.py:159
  24.8 7.0 %collective-permute-start = (bf16[32,1024]{1,0:T(8,128)(2,1)S(1)}, bf16[32,1024]{1,0:T(8,128)(2,1)S(1)}, u32[]{:S(2)}, u32[]{:S(2)}) collective-permute-start(bf16[32,1024]{1,0:T(8,128)(2,1)S(1)} %get-tuple-element.34), channel_id=1, source_target_pairs={{0,4},{4,8},{8,12},{12,16},{16,20},{20,24},{24,28},{28,0},{1,5},{5... | collective-permute-start | bytes 196616 | tf_op jit(solution)/shard_map/ppermute | solution.py:159
  35.8 4.0 %copy-start.18 = (f32[4096]{0:T(1024)S(1)}, f32[4096]{0:T(1024)}, u32[]{:S(2)}) copy-start(f32[4096]{0:T(1024)} %param.10) | copy-start | bytes 49156
  37.0 2.9 %copy-start.2 = (bf16[256,4096]{1,0:T(8,128)(2,1)S(1)}, bf16[256,4096]{1,0:T(8,128)(2,1)}, u32[]{:S(2)}) copy-start(bf16[256,4096]{1,0:T(8,128)(2,1)} %all-gather.3.cloned.1.call-done) | copy-start | bytes 6291460
  39.8 3.1 %copy-start.20 = (f32[256]{0:T(256)}, f32[256]{0:T(256)S(1)}, u32[]{:S(2)}) copy-start(f32[256]{0:T(256)S(1)} %get-tuple-element.45) | copy-start | bytes 3076
  50.8 2.2 %copy-start.9 = (f32[256,64]{1,0:T(8,128)S(1)}, f32[256,64]{1,0:T(8,128)}, u32[]{:S(2)}) copy-start(f32[256,64]{1,0:T(8,128)} %copy.141) | copy-start | bytes 196612
  50.8 2.2 %copy-start.10 = (f32[256,64]{1,0:T(8,128)S(1)}, f32[256,64]{1,0:T(8,128)}, u32[]{:S(2)}) copy-start(f32[256,64]{1,0:T(8,128)} %copy.139) | copy-start | bytes 196612
  53.0 2.9 %copy-start.3 = (bf16[256,4096]{1,0:T(8,128)(2,1)S(1)}, bf16[256,4096]{1,0:T(8,128)(2,1)}, u32[]{:S(2)}) copy-start(bf16[256,4096]{1,0:T(8,128)(2,1)} %all-gather.3.cloned.1.call-done) | copy-start | bytes 6291460
  53.0 2.9 %copy-start.21 = (f32[256]{0:T(256)S(1)}, f32[256]{0:T(256)}, u32[]{:S(2)}) copy-start(f32[256]{0:T(256)} %copy-done.20) | copy-start | bytes 3076
  53.1 0.6 copy-start.11
  53.1 0.7 copy-start.13
  55.9 1.3 copy-start.24
  55.9 1.3 copy-start.17
  55.9 3.0 %slice-start = ((s8[8388608]{0:T(1024)(128)(4,1)}), s8[4194304]{0:T(1024)(128)(4,1)S(1)}, s32[]{:S(2)}) async-start(s8[8388608]{0:T(1024)(128)(4,1)} %bitcast.189), calls=%async_computation.3 | async-start | bytes 8388608
  57.2 3.1 %slice-start.1 = ((s8[8388608]{0:T(1024)(128)(4,1)}), s8[4194304]{0:T(1024)(128)(4,1)S(1)}, s32[]{:S(2)}) async-start(s8[8388608]{0:T(1024)(128)(4,1)} %bitcast.189), calls=%async_computation.4 | async-start | bytes 8388608
  67.7 7.4 %collective-permute-start.7 = (bf16[2,256,1024]{2,1,0:T(8,128)(2,1)}, bf16[2,256,1024]{2,1,0:T(8,128)(2,1)}, u32[]{:S(2)}, u32[]{:S(2)}) collective-permute-start(bf16[2,256,1024]{2,1,0:T(8,128)(2,1)} %pad_maximum_fusion), channel_id=1, source_target_pairs={{0,1},{1,0},{2,3},{3,2},{4,5},{5,4},{6,7},{7,6},{8,9},{9,8},{10,11... | collective-permute-start | bytes 3145736 | tf_op jit(solution)/shard_map/ppermute | solution.py:102
  78.3 2.6 %copy-start.7 = (bf16[256,1024]{0,1:T(8,128)(2,1)S(1)}, bf16[256,1024]{0,1:T(8,128)(2,1)}, u32[]{:S(2)}) copy-start(bf16[256,1024]{0,1:T(8,128)(2,1)} %copy.155) | copy-start | bytes 1572868
  78.3 2.6 %copy-start.25 = (f32[2,256,256,4]{2,1,3,0:T(8,128)S(1)}, f32[2,256,256,4]{2,1,3,0:T(8,128)}, u32[]{:S(2)}) copy-start(f32[2,256,256,4]{2,1,3,0:T(8,128)} %copy-done.24) | copy-start | bytes 6291460
  78.4 8.2 %slice-start.2 = ((s8[8388608]{0:T(1024)(128)(4,1)}), s8[4194304]{0:T(1024)(128)(4,1)S(1)}, s32[]{:S(2)}) async-start(s8[8388608]{0:T(1024)(128)(4,1)} %bitcast.215), calls=%async_computation.6 | async-start | bytes 8388608
  80.9 1.2 copy-start.14
  81.0 5.6 %slice-start.3 = ((s8[8388608]{0:T(1024)(128)(4,1)}), s8[4194304]{0:T(1024)(128)(4,1)S(1)}, s32[]{:S(2)}) async-start(s8[8388608]{0:T(1024)(128)(4,1)} %bitcast.215), calls=%async_computation.7 | async-start | bytes 8388608
  81.7 1.1 copy-start.12
  84.7 14.5 %collective-permute-start.9 = (bf16[1,256,1024]{2,1,0:T(8,128)(2,1)S(1)}, bf16[1,256,1024]{2,1,0:T(8,128)(2,1)}, u32[]{:S(2)}, u32[]{:S(2)}) collective-permute-start(bf16[1,256,1024]{2,1,0:T(8,128)(2,1)S(1)} %fusion.21), channel_id=1, source_target_pairs={{0,2},{1,3},{2,0},{3,1},{4,6},{5,7},{6,4},{7,5},{8,10},{9,11},{10,... | collective-permute-start | bytes 1572872 | tf_op jit(solution)/shard_map/ppermute | solution.py:102
  86.6 2.4 %copy-start.15 = (f32[256,64]{0,1:T(8,128)S(1)}, f32[256,64]{0,1:T(8,128)}, u32[]{:S(2)}) copy-start(f32[256,64]{0,1:T(8,128)} %get-tuple-element.40) | copy-start | bytes 196612
  86.6 2.4 %copy-start.16 = (f32[256,64]{0,1:T(8,128)S(1)}, f32[256,64]{0,1:T(8,128)}, u32[]{:S(2)}) copy-start(f32[256,64]{0,1:T(8,128)} %get-tuple-element.41) | copy-start | bytes 196612
  86.6 2.9 %copy-start.8 = (bf16[4096,256]{1,0:T(8,128)(2,1)S(1)}, bf16[4096,256]{1,0:T(8,128)(2,1)}, u32[]{:S(2)}) copy-start(bf16[4096,256]{1,0:T(8,128)(2,1)} %param.12) | copy-start | bytes 6291460
  89.5 1.6 %copy-start.4 = (bf16[256,4096]{1,0:T(8,128)(2,1)S(1)}, bf16[256,4096]{1,0:T(8,128)(2,1)}, u32[]{:S(2)}) copy-start(bf16[256,4096]{1,0:T(8,128)(2,1)} %all-gather.3.cloned.1.call-done) | copy-start | bytes 6291460
  92.2 2.3 %copy-start.1 = (f32[256,4096]{1,0:T(8,128)}, f32[256,4096]{1,0:T(8,128)S(1)}, u32[]{:S(2)}) copy-start(f32[256,4096]{1,0:T(8,128)S(1)} %get-tuple-element.49) | copy-start | bytes 12582916
  92.2 7.1 %copy-start.6 = (bf16[256,1024]{1,0:T(8,128)(2,1)S(1)}, bf16[256,1024]{1,0:T(8,128)(2,1)}, u32[]{:S(2)}) copy-start(bf16[256,1024]{1,0:T(8,128)(2,1)} %param.9) | copy-start | bytes 1572868
  94.5 6.6 %copy-start.23 = (s32[8]{0:T(128)S(1)}, s32[8]{0:T(128)}, u32[]{:S(2)}) copy-start(s32[8]{0:T(128)} %get-tuple-element.17) | copy-start | bytes 100
  94.5 7.0 %collective-permute-start.8 = (bf16[2,256,1024]{2,1,0:T(8,128)(2,1)}, bf16[2,256,1024]{2,1,0:T(8,128)(2,1)}, u32[]{:S(2)}, u32[]{:S(2)}) collective-permute-start(bf16[2,256,1024]{2,1,0:T(8,128)(2,1)} %pad_maximum_fusion.1), channel_id=1, source_target_pairs={{0,1},{1,0},{2,3},{3,2},{4,5},{5,4},{6,7},{7,6},{8,9},{9,8},{10,11... | collective-permute-start | bytes 3145736 | tf_op jit(solution)/shard_map/ppermute | solution.py:104
  101.5 20.5 %copy-start.5 = (bf16[8,32,1024]{2,1,0:T(8,128)(2,1)S(1)}, bf16[8,32,1024]{2,1,0:T(8,128)(2,1)}, u32[]{:S(2)}) copy-start(bf16[8,32,1024]{2,1,0:T(8,128)(2,1)} %copy.154) | copy-start | bytes 1572868
  101.5 20.5 %dynamic-slice-start = ((f32[4096]{0:T(1024)}, s32[]{:T(128)}), f32[1024]{0:T(1024)S(1)}, s32[]{:S(2)}) async-start(f32[4096]{0:T(1024)} %param.10, s32[]{:T(128)} %select_n.112), calls=%async_computation.5 | async-start | bytes 8704 | tf_op jit(solution)/shard_map/dynamic_slice | solution.py:142
  101.5 20.5 %copy-start.19 = (f32[256]{0:T(256)S(1)}, f32[256]{0:T(256)}, u32[]{:S(2)}) copy-start(f32[256]{0:T(256)} %get-tuple-element.44) | copy-start | bytes 3076
  101.5 20.5 %copy-start.22 = (f32[256]{0:T(256)S(1)}, f32[256]{0:T(256)}, u32[]{:S(2)}) copy-start(f32[256]{0:T(256)} %copy-done.20) | copy-start | bytes 3076
  102.6 22.0 %all-to-all-start = ((bf16[8,32,1024]{2,1,0:T(8,128)(2,1)}), bf16[8,32,1024]{2,1,0:T(8,128)(2,1)}, u32[]{:S(2)}, u32[]{:S(2)}) async-start(bf16[8,32,1024]{2,1,0:T(8,128)(2,1)} %copy.166), calls=%async_computation | async-start | bytes 1048576 | tf_op jit(solution)/shard_map/all_to_all | solution.py:300
  108.3 13.7 %collective-permute-start.10 = (bf16[1,256,1024]{2,1,0:T(8,128)(2,1)S(1)}, bf16[1,256,1024]{2,1,0:T(8,128)(2,1)S(1)}, u32[]{:S(2)}, u32[]{:S(2)}) collective-permute-start(bf16[1,256,1024]{2,1,0:T(8,128)(2,1)S(1)} %fusion.22), channel_id=1, source_target_pairs={{0,2},{1,3},{2,0},{3,1},{4,6},{5,7},{6,4},{7,5},{8,10},{9,11},{10,... | collective-permute-start | bytes 1572872 | tf_op jit(solution)/shard_map/ppermute | solution.py:104
  109.9 1.1 collective-permute-start.11
  111.1 10.9 %collective-permute-start.12 = (f32[256]{0:T(256)S(1)}, f32[256]{0:T(256)S(1)}, u32[]{:S(2)}, u32[]{:S(2)}) collective-permute-start(f32[256]{0:T(256)S(1)} %add.200), channel_id=1, source_target_pairs={{0,2},{1,3},{2,0},{3,1},{4,6},{5,7},{6,4},{7,5},{8,10},{9,11},{10,... | collective-permute-start | bytes 3080 | tf_op jit(solution)/shard_map/ppermute | solution.py:104
Sparse Core Ops, SparseCore 0:
  9.6 25.2 all-gather.2
  37.1 21.9 all-gather.4
